TPU v7x, 32 devices: a whole 2x2x4 slice. The times are simulated.
32 devices in a mesh: group: 2 (over x), tm: 2 (over core), height: 8 (over z, y).
Axes of the slice: x: 2, y: 2, z: 4, core: 2. Of those that a mesh axis runs over, the one named last changes fastest.
Arguments:
- frames: bfloat16 [8, 16, 128, 384], P(('group', 'tm'), 'height'), parts along dimension 0, may hold values from -20 to 20
- earlier: int32 [8, 2], P(('group', 'tm')), parts along dimension 0, may hold values from -1 to 3, as said below
- gain_conv: float32 [384], replicated, may hold values from 0.1 to 1.9
- conv_weight: bfloat16 [3, 3, 3, 384, 384], replicated, may hold values from -0.0625 to 0.0625
- conv_bias: float32 [384], replicated, may hold values from -3 to 3
- gain_attn: float32 [384], replicated, may hold values from 0.1 to 1.9
- query_weight: bfloat16 [384, 384], replicated
- key_weight: bfloat16 [384, 384], replicated
- value_weight: bfloat16 [384, 384], replicated, may hold values from -0.3125 to 0.3125
- out_weight: bfloat16 [384, 384], replicated, may hold values from -0.3125 to 0.3125
Outputs:
- encoded: bfloat16 [8, 16, 128, 384], P(('group', 'tm'), 'height'), parts along dimension 0
There are 2 independent parts, one for each index of `group`. A program takes and returns all parts, laid end to end along the dimension named above; an argument that names none is the same for every part. Nothing has to cross between parts.
Inputs may be any that keep to these rules, and one draw needn't show every extreme that they name: Row i names the spans whose frames come two back and one back before span i's frame in the same clip, -1 where the clip has no such frame; spans of a clip may lie on either index of tm, in an order drawn from the seed. earlier[i, 0] is -1 whenever earlier[i, 1] is -1. Every span is named at most once in each column.
All inputs are finite; a program needn't handle non-finite values.
Results may differ from a plain program's by a relative error of at most 0.014.
Values may be sent and summed in bfloat16 or wider, within the bound.
No kernel may reach another device: no remote copies, remote signals or barrier semaphores. Data moves between devices by JAX's collectives and lax.ppermute only.
A program may use at most 128 MiB of HBM per device.

v0:
```python
import jax
import jax.numpy as jnp
from jax import lax
from jax.sharding import PartitionSpec as P


def padded_2(cells, sides, width):
    for axis, dim in sides:
        count = lax.axis_size(axis)
        ends = count - 1
        head = lax.slice_in_dim(cells, 0, width, axis=dim)
        tail = lax.slice_in_dim(cells, cells.shape[dim] - width, cells.shape[dim], axis=dim)
        cells = jnp.concatenate(
            [
                lax.ppermute(tail, axis, [(i, (i + 1) % count) for i in range(ends)]),
                cells,
                lax.ppermute(head, axis, [((i + 1) % count, i) for i in range(ends)]),
            ],
            axis=dim,
        )
    return cells


def rms_scaled(frames, gain):
    widened = frames.astype(jnp.float32)
    mean_square = jnp.mean(widened * widened, axis=-1, keepdims=True)
    return widened * lax.rsqrt(mean_square + 1e-06) * gain


def shards(
    frames,
    earlier,
    gain_conv,
    conv_weight,
    conv_bias,
    gain_attn,
    query_weight,
    key_weight,
    value_weight,
    out_weight,
):
    span_count, row_count, col_count, channels = frames.shape
    activated = jax.nn.silu(rms_scaled(frames, gain_conv)).astype(jnp.bfloat16)
    rimmed = padded_2(activated, (("height", 1),), 1)
    gathered = lax.all_gather(rimmed, "tm", axis=0, tiled=True)
    border = ((0, 0), (0, 0), (1, 1), (0, 0))
    padded = jnp.pad(rimmed, border)
    gathered = jnp.pad(gathered, border)
    back_two = jnp.take(gathered, jnp.maximum(earlier[:, 0], 0), axis=0)
    back_one = jnp.take(gathered, jnp.maximum(earlier[:, 1], 0), axis=0)
    present_two = (earlier[:, 0] >= 0)[:, None, None, None]
    present_one = (earlier[:, 1] >= 0)[:, None, None, None]
    back_two = jnp.where(present_two, back_two, jnp.zeros_like(back_two))
    back_one = jnp.where(present_one, back_one, jnp.zeros_like(back_one))
    window = jnp.stack([back_two, back_one, padded], axis=1)
    accum = jnp.zeros((span_count, row_count, col_count, channels), jnp.float32)
    for tap_t in range(3):
        for tap_y in range(3):
            for tap_x in range(3):
                sliced = window[:, tap_t, tap_y : tap_y + row_count, tap_x : tap_x + col_count]
                accum = accum + jnp.einsum(
                    "fhwc,cd->fhwd",
                    sliced,
                    conv_weight[tap_t, tap_y, tap_x],
                    preferred_element_type=jnp.float32,
                )
    mixed = (frames.astype(jnp.float32) + accum + conv_bias).astype(jnp.bfloat16)
    normed = rms_scaled(mixed, gain_attn).astype(jnp.bfloat16)
    tokens = normed.reshape(span_count, row_count * col_count, channels)
    queries = jnp.einsum(
        "ftc,cd->ftd", tokens, query_weight, preferred_element_type=jnp.float32
    ).astype(jnp.bfloat16)
    score_scale = 1.0 / channels**0.5
    query_rows = row_count * col_count
    keys_local = jnp.einsum(
        "ftc,cd->ftd", tokens, key_weight, preferred_element_type=jnp.float32
    ).astype(jnp.bfloat16)
    values_local = jnp.einsum(
        "ftc,cd->ftd", tokens, value_weight, preferred_element_type=jnp.float32
    ).astype(jnp.bfloat16)
    running = jnp.full((span_count, query_rows), -jnp.inf, jnp.float32)
    totals = jnp.zeros((span_count, query_rows), jnp.float32)
    summed = jnp.zeros((span_count, query_rows, channels), jnp.float32)
    scores = (
        jnp.einsum(
            "fqc,fkc->fqk",
            queries,
            lax.all_gather(keys_local, "height", axis=1, tiled=True),
            preferred_element_type=jnp.float32,
        )
        * score_scale
    )
    peak_new = jnp.max(scores, axis=-1)
    rescale = jnp.exp(running - peak_new)
    weights_exp = jnp.exp(scores - peak_new[:, :, None])
    totals = totals * rescale + jnp.sum(weights_exp, axis=-1)
    summed = summed * rescale[:, :, None] + jnp.einsum(
        "fqk,fkc->fqc",
        weights_exp.astype(jnp.bfloat16),
        lax.all_gather(values_local, "height", axis=1, tiled=True),
        preferred_element_type=jnp.float32,
    )
    attended = (summed / totals[:, :, None]).astype(jnp.bfloat16)
    projected = jnp.einsum("ftc,cd->ftd", attended, out_weight, preferred_element_type=jnp.float32)
    encoded = mixed.astype(jnp.float32) + projected.reshape(
        span_count, row_count, col_count, channels
    )
    return encoded.astype(jnp.bfloat16)


def solution(mesh):
    in_specs = (
        P(("group", "tm"), "height", None, None),
        P(("group", "tm"), None),
        P(),
        P(),
        P(),
        P(),
        P(),
        P(),
        P(),
        P(),
    )
    out_specs = P(("group", "tm"), "height", None, None)
    return jax.shard_map(shards, mesh=mesh, in_specs=in_specs, out_specs=out_specs, check_vma=False)
```

profile of v0, /device:TPU:0, one launch (start us, length us, event | category | flops | bytes accessed | tf_op | source)
XLA Modules:
  0.0 218.3 jit_solution(15502903867783971841)
XLA Ops:
  6.5 1.2 fusion.25
  7.7 1.3 fusion.32
  9.1 4.9 %collective-permute-start = (bf16[2,1,128,384]{3,2,1,0:T(8,128)(2,1)S(1)}, bf16[2,1,128,384]{3,2,1,0:T(8,128)(2,1)S(1)}, u32[]{:S(2)}, u32[]{:S(2)}) collective-permute-start(bf16[2,1,128,384]{3,2,1,0:T(8,128)(2,1)S(1)} %get-tuple-element.10), channel_id=1, source_target_pairs={{0,1},{1,2},{2,3},{3,4},{4,5},{5,6},{6,7},{8,9},{9,10},{10,11},{11... | collective-permute-start | bytes 589832 | tf_op jit(solution)/shard_map/ppermute | solution.py:15
  14.0 1.3 collective-permute-start.1
  15.3 2.9 %collective-permute-done = bf16[2,1,128,384]{3,2,1,0:T(8,128)(2,1)S(1)} collective-permute-done((bf16[2,1,128,384]{3,2,1,0:T(8,128)(2,1)S(1)}, bf16[2,1,128,384]{3,2,1,0:T(8,128)(2,1)S(1)}, u32[]{:S(2)}, u32[]{:S(2)}) %collective-permute-start) | collective-permute-done | bytes 196640 | tf_op jit(solution)/shard_map/ppermute | solution.py:15
  18.2 4.1 %collective-permute-done.1 = bf16[2,1,128,384]{3,2,1,0:T(8,128)(2,1)S(1)} collective-permute-done((bf16[2,1,128,384]{3,2,1,0:T(8,128)(2,1)S(1)}, bf16[2,1,128,384]{3,2,1,0:T(8,128)(2,1)S(1)}, u32[]{:S(2)}, u32[]{:S(2)}) %collective-permute-start.1) | collective-permute-done | bytes 196640 | tf_op jit(solution)/shard_map/ppermute | solution.py:17
  22.3 1.0 pad_maximum_fusion
  23.3 0.0 all-gather.4.cloned.1.call-update
  23.3 0.0 all-gather.6.cloned.1.call-start
  23.3 1.0 maximum_reduce_fusion
  24.3 1.0 compare_reduce_fusion
  25.3 1.3 pad_bitcast_fusion
  26.7 8.9 %all-gather.4.cloned.1.call-done = bf16[4,4,128,384]{3,2,1,0:T(8,128)(2,1)} async-done(((bf16[2,4,128,384]{3,2,1,0:T(8,128)(2,1)}), bf16[4,4,128,384]{3,2,1,0:T(8,128)(2,1)}) %all-gather.4.cloned.1.call-update) | async-done | bytes 1572880 | tf_op jit(solution)/shard_map/all_gather | solution.py:45
  35.5 1.9 pad.8
  37.5 1.6 gather_fusion
  39.1 1.3 fusion.24
  40.4 1.4 fusion.33
  41.8 1.4 convolution_add_fusion.25
  43.1 1.4 convolution_add_fusion.24
  44.5 1.4 convolution_add_fusion.23
  45.8 1.4 convolution_add_fusion.22
  47.2 1.4 convolution_add_fusion.21
  48.6 1.4 convolution_add_fusion.20
  49.9 1.4 convolution_add_fusion.19
  51.3 2.3 %convolution_add_fusion.18 = f32[2,2,128,384]{3,2,1,0:T(8,128)} fusion(f32[2,2,128,384]{3,2,1,0:T(8,128)S(1)} %convolution_add_fusion.19, bf16[2,1,4,130,384]{4,3,2,0,1:T(8,128)(2,1)S(1)} %fusion.24, bf16[3,3,3,384,384]{4,3,2,1,0:T(8,128)(2,1)} %param.15), kind=kOutput, calls=%fused_computation.27 | convolution fusion | flops 151191552 | bytes 2260992 | tf_op jit(solution)/shard_map/fhwc,cd->fhwd/dot_general | solution.py:61
  53.5 1.6 gather_fusion.1
  55.1 1.3 fusion.23
  56.5 1.6 convolution_add_fusion.17
  58.1 1.4 convolution_add_fusion.16
  59.5 1.4 convolution_add_fusion.15
  60.8 1.4 convolution_add_fusion.14
  62.2 1.4 convolution_add_fusion.13
  63.6 1.4 convolution_add_fusion.12
  64.9 1.4 convolution_add_fusion.11
  66.3 1.4 convolution_add_fusion.10
  67.7 1.4 convolution_add_fusion.9
  69.0 1.4 convolution_add_fusion.8
  70.4 0.0 copy-start.1
  70.4 0.0 copy-start.5
  70.4 1.4 convolution_add_fusion.7
  71.8 0.0 copy-start.4
  71.8 1.4 convolution_add_fusion.6
  73.2 0.0 copy-start.2
  73.2 0.0 copy-start.3
  73.2 1.4 convolution_add_fusion.5
  74.6 1.4 convolution_add_fusion.4
  76.0 1.4 convolution_add_fusion.3
  77.4 1.4 convolution_add_fusion.2
  78.7 1.4 convolution_add_fusion.1
  80.1 1.5 multiply_reduce_fusion.1
  81.6 0.0 copy-start.6
  81.6 0.1 multiply_convert_fusion
  81.8 0.0 copy-done.2
  81.8 1.3 convolution_convert_fusion.1
  83.1 0.0 all-gather.6.cloned.1.call-update
  83.2 0.0 all-gather.8.cloned.1.call-start
  83.2 1.1 convolution_convert_fusion
  84.3 0.0 all-gather.8.cloned.1.call-update
  84.4 60.6 %all-gather.6.cloned.1.call-done = bf16[2,2048,384]{2,1,0:T(8,128)(2,1)} async-done(((bf16[2,256,384]{2,1,0:T(8,128)(2,1)}), bf16[2,2048,384]{2,1,0:T(8,128)(2,1)}) %all-gather.6.cloned.1.call-update) | async-done | bytes 3145744 | tf_op jit(solution)/shard_map/all_gather | solution.py:88
  144.9 5.4 %multiply_reduce_fusion = (f32[2,256]{1,0:T(2,128)S(1)}, f32[2,256,2048]{2,1,0:T(8,128)}) fusion(bf16[2,2048,384]{2,1,0:T(8,128)(2,1)} %all-gather.6.cloned.1.call-done, bf16[2,256,384]{2,1,0:T(8,128)(2,1)S(1)} %bitcast.304, bf16[384,384]{1,0:T(8,128)(2,1)S(1)} %copy-done), kind=kOutput, calls=%fused_computation.3 | convolution fusion | flops 958594560 | bytes 8030208 | tf_op jit(solution)/shard_map/fqc,fkc->fqk/dot_general | solution.py:85
  150.3 3.0 %fusion = f32[2,256]{1,0:T(2,128)S(1)} fusion(f32[2,256,2048]{2,1,0:T(8,128)} %get-tuple-element.17, f32[2,256]{1,0:T(2,128)S(1)} %get-tuple-element.16), kind=kLoop, calls=%fused_computation.4 | loop fusion | flops 3145216 | bytes 4198400 | tf_op jit(solution)/shard_map/reduce_sum | solution.py:96
  153.3 52.9 %all-gather.8.cloned.1.call-done = bf16[2,2048,384]{2,1,0:T(8,128)(2,1)} async-done(((bf16[2,256,384]{2,1,0:T(8,128)(2,1)}), bf16[2,2048,384]{2,1,0:T(8,128)(2,1)}) %all-gather.8.cloned.1.call-update) | async-done | bytes 3145744 | tf_op jit(solution)/shard_map/all_gather | solution.py:100
  206.2 4.7 %fusion.21 = f32[2,256,384]{2,1,0:T(8,128)S(1)} fusion(bf16[2,2048,384]{2,1,0:T(8,128)(2,1)} %all-gather.8.cloned.1.call-done, f32[2,256,2048]{2,1,0:T(8,128)} %get-tuple-element.17, f32[2,256]{1,0:T(2,128)S(1)} %get-tuple-element.16, f32[2,256]{1,0:T(2,128)S(1)} %get-tuple-element.13, f32[2,256]{1,0:T(2,128)S(1)} %get-tuple-element.12, ...), kind=kOutput, calls=%fused_computation.48 | convolution fusion | flops 960036864 | bytes 8427520 | tf_op jit(solution)/shard_map/ftc,cd->ftd/dot_general | solution.py:104
  211.0 0.8 add_convert_fusion
  (16 shorter events, 0.1 us)
Async XLA Ops:
  6.5 138.4 %copy-start = (bf16[384,384]{1,0:T(8,128)(2,1)S(1)}, bf16[384,384]{1,0:T(8,128)(2,1)}, u32[]{:S(2)}) copy-start(bf16[384,384]{1,0:T(8,128)(2,1)} %param.18) | copy-start | bytes 884740
  6.5 29.0 %all-gather.4.cloned.1.call-start = ((), (), s32[]{:S(2)}) async-start(), calls=%async_computation | async-start | bytes 2359296 | tf_op jit(solution)/shard_map/all_gather | solution.py:45
  9.1 9.1 %collective-permute-start = (bf16[2,1,128,384]{3,2,1,0:T(8,128)(2,1)S(1)}, bf16[2,1,128,384]{3,2,1,0:T(8,128)(2,1)S(1)}, u32[]{:S(2)}, u32[]{:S(2)}) collective-permute-start(bf16[2,1,128,384]{3,2,1,0:T(8,128)(2,1)S(1)} %get-tuple-element.10), channel_id=1, source_target_pairs={{0,1},{1,2},{2,3},{3,4},{4,5},{5,6},{6,7},{8,9},{9,10},{10,11},{11... | collective-permute-start | bytes 589832 | tf_op jit(solution)/shard_map/ppermute | solution.py:15
  14.0 8.3 %collective-permute-start.1 = (bf16[2,1,128,384]{3,2,1,0:T(8,128)(2,1)S(1)}, bf16[2,1,128,384]{3,2,1,0:T(8,128)(2,1)S(1)}, u32[]{:S(2)}, u32[]{:S(2)}) collective-permute-start(bf16[2,1,128,384]{3,2,1,0:T(8,128)(2,1)S(1)} %get-tuple-element.11), channel_id=1, source_target_pairs={{1,0},{2,1},{3,2},{4,3},{5,4},{6,5},{7,6},{9,8},{10,9},{11,10},{12... | collective-permute-start | bytes 589832 | tf_op jit(solution)/shard_map/ppermute | solution.py:17
  23.3 121.7 %all-gather.6.cloned.1.call-start = ((), (), s32[]{:S(2)}) async-start(), calls=%async_computation.1 | async-start | bytes 3538944 | tf_op jit(solution)/shard_map/all_gather | solution.py:88
  70.4 9.7 %copy-start.1 = (bf16[2,2,128,384]{3,2,1,0:T(8,128)(2,1)S(1)}, bf16[2,2,128,384]{3,2,1,0:T(8,128)(2,1)}, u32[]{:S(2)}) copy-start(bf16[2,2,128,384]{3,2,1,0:T(8,128)(2,1)} %param.12) | copy-start | bytes 1179652
  70.4 9.7 %copy-start.5 = (f32[384]{0:T(512)S(1)}, f32[384]{0:T(512)}, u32[]{:S(2)}) copy-start(f32[384]{0:T(512)} %param.16) | copy-start | bytes 4612
  71.8 9.8 %copy-start.4 = (f32[384]{0:T(512)S(1)}, f32[384]{0:T(512)}, u32[]{:S(2)}) copy-start(f32[384]{0:T(512)} %param.17) | copy-start | bytes 4612
  73.2 8.6 %copy-start.2 = (bf16[384,384]{1,0:T(8,128)(2,1)S(1)}, bf16[384,384]{1,0:T(8,128)(2,1)}, u32[]{:S(2)}) copy-start(bf16[384,384]{1,0:T(8,128)(2,1)} %param.19) | copy-start | bytes 884740
  73.2 10.0 %copy-start.3 = (bf16[384,384]{1,0:T(8,128)(2,1)S(1)}, bf16[384,384]{1,0:T(8,128)(2,1)}, u32[]{:S(2)}) copy-start(bf16[384,384]{1,0:T(8,128)(2,1)} %param.20) | copy-start | bytes 884740
  81.6 124.6 %copy-start.6 = (bf16[384,384]{1,0:T(8,128)(2,1)S(1)}, bf16[384,384]{1,0:T(8,128)(2,1)}, u32[]{:S(2)}) copy-start(bf16[384,384]{1,0:T(8,128)(2,1)} %param.21) | copy-start | bytes 884740
  83.2 123.1 %all-gather.8.cloned.1.call-start = ((), (), s32[]{:S(2)}) async-start(), calls=%async_computation.2 | async-start | bytes 3538944 | tf_op jit(solution)/shard_map/all_gather | solution.py:100
Sparse Core Ops, SparseCore 0:
  23.4 12.0 all-gather.3
  83.3 61.6 all-gather.5
  147.1 59.0 all-gather.7
where the time goes:
time: 220 us; the launch traced here: 218 us
  waiting for transfers between devices  129 us (59%)
  matrix products  50.6 us (23%)
  between operations  13.5 us (6%)
  other arithmetic  12.1 us (6%)
  local copies, waits for them, and re-layouts  6.52 us (3%)
  starting transfers between devices  6.26 us (3%)
    all_gather x1, waiting for transfers between devices, shards(): lax.all_gather(keys_local, 'height', axis=1, tiled=True)  60.6 us
    all_gather x1, waiting for transfers between devices, shards(): lax.all_gather(values_local, 'height', axis=1, tiled=True)  52.9 us
    dot_general x27, matrix products, shards(): jnp.einsum('fhwc,cd->fhwd', sliced, conv_weight[tap_t, tap_y, tap_x], pre...  38 us
    all_gather x1, waiting for transfers between devices, shards(): gathered = lax.all_gather(rimmed, 'tm', axis=0, tiled=True)  8.85 us
    dot_general x1, matrix products, shards(): jnp.einsum('fqc,fkc->fqk', queries, lax.all_gather(keys_local, 'height',...  5.37 us
    ppermute x1, starting transfers between devices, padded_2(): lax.ppermute(tail, axis, [(i, (i + 1) % count) for i in range(ends)])  4.88 us
    dot_general x1, matrix products, shards(): jnp.einsum('ftc,cd->ftd', attended, out_weight, preferred_element_type=jn...  4.74 us
  transfers between devices with their start and end apart: 5, of which 5 were waited for; matrix products, arithmetic and copies ran while one was open for 6% of the time, Pallas kernels for 0%

commit v1 on v0

--- a/solution.py
+++ b/solution.py
@@ -71,33 +71,24 @@
         "ftc,cd->ftd", tokens, query_weight, preferred_element_type=jnp.float32
     ).astype(jnp.bfloat16)
     score_scale = 1.0 / channels**0.5
-    query_rows = row_count * col_count
-    keys_local = jnp.einsum(
-        "ftc,cd->ftd", tokens, key_weight, preferred_element_type=jnp.float32
+    tokens_all = lax.all_gather(tokens, "height", axis=1, tiled=True)
+    keys_all = jnp.einsum(
+        "ftc,cd->ftd", tokens_all, key_weight, preferred_element_type=jnp.float32
     ).astype(jnp.bfloat16)
-    values_local = jnp.einsum(
-        "ftc,cd->ftd", tokens, value_weight, preferred_element_type=jnp.float32
+    values_all = jnp.einsum(
+        "ftc,cd->ftd", tokens_all, value_weight, preferred_element_type=jnp.float32
     ).astype(jnp.bfloat16)
-    running = jnp.full((span_count, query_rows), -jnp.inf, jnp.float32)
-    totals = jnp.zeros((span_count, query_rows), jnp.float32)
-    summed = jnp.zeros((span_count, query_rows, channels), jnp.float32)
     scores = (
-        jnp.einsum(
-            "fqc,fkc->fqk",
-            queries,
-            lax.all_gather(keys_local, "height", axis=1, tiled=True),
-            preferred_element_type=jnp.float32,
-        )
+        jnp.einsum("fqc,fkc->fqk", queries, keys_all, preferred_element_type=jnp.float32)
         * score_scale
     )
-    peak_new = jnp.max(scores, axis=-1)
-    rescale = jnp.exp(running - peak_new)
-    weights_exp = jnp.exp(scores - peak_new[:, :, None])
-    totals = totals * rescale + jnp.sum(weights_exp, axis=-1)
-    summed = summed * rescale[:, :, None] + jnp.einsum(
+    peaks = jnp.max(scores, axis=-1, keepdims=True)
+    weights_exp = jnp.exp(scores - peaks)
+    totals = jnp.sum(weights_exp, axis=-1)
+    summed = jnp.einsum(
         "fqk,fkc->fqc",
         weights_exp.astype(jnp.bfloat16),
-        lax.all_gather(values_local, "height", axis=1, tiled=True),
+        values_all,
         preferred_element_type=jnp.float32,
     )
     attended = (summed / totals[:, :, None]).astype(jnp.bfloat16)

time: 220 us -> 147 us (0.67)
  waiting for transfers between devices: 129 us -> 76 us
  matrix products: 50.6 us -> 32.1 us
    all_gather x2 -> x1, waiting for transfers between devices: 113 us -> 60.2 us  [shards(): tokens_all = lax.all_gather(tokens, 'height', axis=1, tiled=True)]
    dot_general x27, matrix products: 38 us -> 16.7 us  [shards(): jnp.einsum('fhwc,cd->fhwd', sliced, conv_weight[tap_t, tap_y, tap_x], pre...]
    dot_general x3, matrix products: 7.84 us -> 15 us  [the longest x1 7 us: shards(): jnp.einsum('fqc,fkc->fqk', queries, keys_all, preferred_element_type=jnp....]
    dot_general x1, matrix products: 4.74 us -> 0.39 us  [shards(): jnp.einsum('ftc,cd->ftd', attended, out_weight, preferred_element_type=jn...]
  transfers between devices with their start and end apart: 5 -> 4, of which waited for: 5 -> 4; matrix products, arithmetic and copies ran while one was open for 6% -> 3% of each run, Pallas kernels for 0% -> 0%
where the time goes in v1:
time: 147 us
  waiting for transfers between devices  76 us (52%)
  matrix products  32.1 us (22%)
  between operations  13.8 us (9%)
  other arithmetic  11.9 us (8%)
  local copies, waits for them, and re-layouts  6.55 us (4%)
  starting transfers between devices  6.22 us (4%)
    all_gather x1, waiting for transfers between devices, shards(): tokens_all = lax.all_gather(tokens, 'height', axis=1, tiled=True)  60.2 us
    dot_general x27, matrix products, shards(): jnp.einsum('fhwc,cd->fhwd', sliced, conv_weight[tap_t, tap_y, tap_x], pre...  16.7 us
    all_gather x1, waiting for transfers between devices, shards(): gathered = lax.all_gather(rimmed, 'tm', axis=0, tiled=True)  8.85 us
    dot_general x1, matrix products, shards(): jnp.einsum('fqc,fkc->fqk', queries, keys_all, preferred_element_type=jnp....  7 us
    dot_general x1, matrix products, shards(): jnp.einsum('fqk,fkc->fqc', weights_exp.astype(jnp.bfloat16), values_all,...  6.4 us
    ppermute x1, starting transfers between devices, padded_2(): lax.ppermute(tail, axis, [(i, (i + 1) % count) for i in range(ends)])  4.88 us
    ppermute x1, waiting for transfers between devices, padded_2(): lax.ppermute(head, axis, [((i + 1) % count, i) for i in range(ends)])  4.07 us
    reduce_sum x1, other arithmetic, shards(): totals = jnp.sum(weights_exp, axis=-1)  3 us
  transfers between devices with their start and end apart: 4, of which 4 were waited for; matrix products, arithmetic and copies ran while one was open for 3% of the time, Pallas kernels for 0%

profile of v1, /device:TPU:0, one launch (start us, length us, event | category | flops | bytes accessed | tf_op | source)
XLA Modules:
  0.0 146.6 jit_solution(2470167891142109814)
XLA Ops:
  6.5 0.0 copy-start
  6.5 0.0 all-gather.3.cloned.1.call-start
  6.5 1.2 fusion.19
  7.7 1.3 fusion.26
  9.1 4.9 %collective-permute-start = (bf16[2,1,128,384]{3,2,1,0:T(8,128)(2,1)S(1)}, bf16[2,1,128,384]{3,2,1,0:T(8,128)(2,1)S(1)}, u32[]{:S(2)}, u32[]{:S(2)}) collective-permute-start(bf16[2,1,128,384]{3,2,1,0:T(8,128)(2,1)S(1)} %get-tuple-element.10), channel_id=1, source_target_pairs={{0,1},{1,2},{2,3},{3,4},{4,5},{5,6},{6,7},{8,9},{9,10},{10,11},{11... | collective-permute-start | bytes 589832 | tf_op jit(solution)/shard_map/ppermute | solution.py:15
  14.0 1.3 collective-permute-start.1
  15.3 2.9 %collective-permute-done = bf16[2,1,128,384]{3,2,1,0:T(8,128)(2,1)S(1)} collective-permute-done((bf16[2,1,128,384]{3,2,1,0:T(8,128)(2,1)S(1)}, bf16[2,1,128,384]{3,2,1,0:T(8,128)(2,1)S(1)}, u32[]{:S(2)}, u32[]{:S(2)}) %collective-permute-start) | collective-permute-done | bytes 196640 | tf_op jit(solution)/shard_map/ppermute | solution.py:15
  18.2 4.1 %collective-permute-done.1 = bf16[2,1,128,384]{3,2,1,0:T(8,128)(2,1)S(1)} collective-permute-done((bf16[2,1,128,384]{3,2,1,0:T(8,128)(2,1)S(1)}, bf16[2,1,128,384]{3,2,1,0:T(8,128)(2,1)S(1)}, u32[]{:S(2)}, u32[]{:S(2)}) %collective-permute-start.1) | collective-permute-done | bytes 196640 | tf_op jit(solution)/shard_map/ppermute | solution.py:17
  22.3 1.0 pad_maximum_fusion
  23.3 0.0 all-gather.3.cloned.1.call-update
  23.3 0.0 all-gather.5.cloned.1.call-start
  23.3 1.0 maximum_reduce_fusion
  24.4 1.0 compare_reduce_fusion
  25.3 1.3 pad_bitcast_fusion
  26.7 8.9 %all-gather.3.cloned.1.call-done = bf16[4,4,128,384]{3,2,1,0:T(8,128)(2,1)} async-done(((bf16[2,4,128,384]{3,2,1,0:T(8,128)(2,1)}), bf16[4,4,128,384]{3,2,1,0:T(8,128)(2,1)}) %all-gather.3.cloned.1.call-update) | async-done | bytes 1572880 | tf_op jit(solution)/shard_map/all_gather | solution.py:45
  35.5 1.9 %pad.8 = bf16[4,4,130,384]{3,2,1,0:T(8,128)(2,1)S(1)} pad(bf16[4,4,128,384]{3,2,1,0:T(8,128)(2,1)} %all-gather.3.cloned.1.call-done, bf16[]{:T(256)} %constant.14.clone.1), padding=0_0x0_0x1_1x0_0 | pad | bytes 3170306 | tf_op jit(solution)/shard_map/jit(_pad)/pad | solution.py:48
  37.5 1.6 %gather_fusion.1 = bf16[2,4,130,384]{3,2,1,0:T(8,128)(2,1)} fusion(bf16[4,4,130,384]{3,2,1,0:T(8,128)(2,1)S(1)} %pad.8, s32[1024]{0:T(1024)S(1)} %pad_clamp_fusion), kind=kCustom, calls=%fused_computation.1.clone | custom fusion | bytes 1597448 | tf_op jit(solution)/shard_map/jit(_take)/gather | solution.py:50
  39.1 1.6 %gather_fusion = bf16[2,4,130,384]{3,2,1,0:T(8,128)(2,1)} fusion(bf16[4,4,130,384]{3,2,1,0:T(8,128)(2,1)S(1)} %pad.8, s32[1024]{0:T(1024)S(1)} %pad_clamp_fusion.1), kind=kCustom, calls=%fused_computation.clone | custom fusion | bytes 1597448 | tf_op jit(solution)/shard_map/jit(_take)/gather | solution.py:49
  40.7 1.5 %fusion.18 = bf16[2,1,4,130,384]{4,3,2,0,1:T(8,128)(2,1)S(1)} fusion(bf16[2,4,130,384]{3,2,1,0:T(8,128)(2,1)} %gather_fusion, pred[2]{0:T(512)(128)(4,1)S(1)} %get-tuple-element.19, pred[2]{0:T(512)(128)(4,1)S(1)} %get-tuple-element.7), kind=kLoop, calls=%fused_computation.50 | loop fusion | flops 798720 | bytes 1597444 | tf_op jit(solution)/shard_map/stack | solution.py:55
  42.2 1.4 fusion.27
  43.5 1.4 convolution_add_fusion.25
  44.9 0.0 slice-start.1
  44.9 0.0 copy-start.2
  44.9 1.5 %convolution_add_fusion.24 = f32[2,2,128,384]{3,2,1,0:T(8,128)S(1)} fusion(f32[2,2,128,384]{3,2,1,0:T(8,128)S(1)} %convolution_add_fusion.25, bf16[2,1,4,130,384]{4,3,2,0,1:T(8,128)(2,1)S(1)} %fusion.18, bf16[3,3,3,384,384]{4,3,2,1,0:T(8,128)(2,1)} %param.15), kind=kOutput, calls=%fused_computation.36 | convolution fusion | flops 151191552 | bytes 2260992 | tf_op jit(solution)/shard_map/fhwc,cd->fhwd/dot_general | solution.py:61
  46.4 1.4 convolution_add_fusion.23
  47.8 1.4 convolution_add_fusion.22
  49.2 1.4 convolution_add_fusion.21
  50.5 0.0 slice-done
  50.6 0.4 convolution_add_fusion.20
  50.9 0.4 convolution_add_fusion.19
  51.3 0.4 convolution_add_fusion.18
  51.8 0.2 fusion.17
  52.0 0.4 convolution_add_fusion.17
  52.4 0.4 convolution_add_fusion.16
  52.8 0.4 convolution_add_fusion.15
  53.2 0.4 convolution_add_fusion.14
  53.6 0.4 convolution_add_fusion.13
  54.0 0.4 convolution_add_fusion.12
  54.4 0.4 convolution_add_fusion.11
  54.8 0.4 convolution_add_fusion.10
  55.2 0.4 convolution_add_fusion.9
  55.6 0.4 convolution_add_fusion.8
  56.0 0.0 copy-start.1
  56.0 0.0 copy-start.6
  56.0 0.4 convolution_add_fusion.7
  56.4 0.0 copy-start.5
  56.4 0.4 convolution_add_fusion.6
  56.8 0.0 copy-start.3
  56.8 0.4 convolution_add_fusion.5
  57.2 0.4 convolution_add_fusion.4
  57.6 0.4 convolution_add_fusion.3
  58.0 0.4 convolution_add_fusion.2
  58.4 0.4 convolution_add_fusion.1
  58.8 0.5 multiply_reduce_fusion.1
  59.4 0.9 multiply_convert_fusion
  60.3 0.0 all-gather.5.cloned.1.call-update
  60.3 1.6 %convolution_convert_fusion.2 = bf16[2,256,384]{2,1,0:T(8,128)(2,1)S(1)} fusion(bf16[2,256,384]{2,1,0:T(8,128)(2,1)} %bitcast.306, bf16[384,384]{1,0:T(8,128)(2,1)S(1)} %copy-done.3), kind=kOutput, calls=%fused_computation.42 | convolution fusion | flops 151191552 | bytes 1081344 | tf_op jit(solution)/shard_map/ftc,cd->ftd/dot_general | solution.py:70
  61.9 60.2 %all-gather.5.cloned.1.call-done = bf16[2,2048,384]{2,1,0:T(8,128)(2,1)} async-done(((bf16[2,256,384]{2,1,0:T(8,128)(2,1)}), bf16[2,2048,384]{2,1,0:T(8,128)(2,1)}) %all-gather.5.cloned.1.call-update) | async-done | bytes 3145744 | tf_op jit(solution)/shard_map/all_gather | solution.py:74
  122.1 7.0 %multiply_reduce_fusion = (f32[2,256]{1,0:T(2,128)S(1)}, f32[2,256,2048]{2,1,0:T(8,128)}) fusion(bf16[2,256,384]{2,1,0:T(8,128)(2,1)S(1)} %convolution_convert_fusion.2, bf16[2,2048,384]{2,1,0:T(8,128)(2,1)} %all-gather.5.cloned.1.call-done, bf16[384,384]{1,0:T(8,128)(2,1)S(1)} %copy-done), kind=kOutput, calls=%fused_computation.3 | convolution fusion | flops 2016935424 | bytes 8030208 | tf_op jit(solution)/shard_map/fqc,fkc->fqk/dot_general | solution.py:82
  129.1 3.0 %fusion = f32[2,256]{1,0:T(2,128)S(1)} fusion(f32[2,256,2048]{2,1,0:T(8,128)} %get-tuple-element.15, f32[2,256]{1,0:T(2,128)S(1)} %get-tuple-element.14), kind=kLoop, calls=%fused_computation.4 | loop fusion | flops 3145216 | bytes 4198400 | tf_op jit(solution)/shard_map/reduce_sum | solution.py:87
  132.1 0.0 copy-start.4
  132.1 6.4 %fusion.14 = bf16[2,256,384]{2,1,0:T(8,128)(2,1)S(1)} fusion(bf16[2,2048,384]{2,1,0:T(8,128)(2,1)} %all-gather.5.cloned.1.call-done, f32[2,256,2048]{2,1,0:T(8,128)} %get-tuple-element.15, f32[2,256]{1,0:T(2,128)S(1)} %get-tuple-element.14, f32[2,256]{1,0:T(2,128)S(1)} %fusion, bf16[384,384]{1,0:T(8,128)(2,1)S(1)} %copy-done.7), kind=kOutput, calls=%fused_computation.46 | convolution fusion | flops 2018377728 | bytes 8032256 | tf_op jit(solution)/shard_map/fqk,fkc->fqc/dot_general | solution.py:88
  138.5 0.4 fusion.55
  138.9 0.8 add_convert_fusion
  (19 shorter events, 0.1 us)
Async XLA Ops:
  6.5 115.6 %copy-start = (bf16[384,384]{1,0:T(8,128)(2,1)S(1)}, bf16[384,384]{1,0:T(8,128)(2,1)}, u32[]{:S(2)}) copy-start(bf16[384,384]{1,0:T(8,128)(2,1)} %param.19) | copy-start | bytes 884740
  6.5 29.0 %all-gather.3.cloned.1.call-start = ((), (), s32[]{:S(2)}) async-start(), calls=%async_computation | async-start | bytes 2359296 | tf_op jit(solution)/shard_map/all_gather | solution.py:45
  9.1 9.1 %collective-permute-start = (bf16[2,1,128,384]{3,2,1,0:T(8,128)(2,1)S(1)}, bf16[2,1,128,384]{3,2,1,0:T(8,128)(2,1)S(1)}, u32[]{:S(2)}, u32[]{:S(2)}) collective-permute-start(bf16[2,1,128,384]{3,2,1,0:T(8,128)(2,1)S(1)} %get-tuple-element.10), channel_id=1, source_target_pairs={{0,1},{1,2},{2,3},{3,4},{4,5},{5,6},{6,7},{8,9},{9,10},{10,11},{11... | collective-permute-start | bytes 589832 | tf_op jit(solution)/shard_map/ppermute | solution.py:15
  14.0 8.3 %collective-permute-start.1 = (bf16[2,1,128,384]{3,2,1,0:T(8,128)(2,1)S(1)}, bf16[2,1,128,384]{3,2,1,0:T(8,128)(2,1)S(1)}, u32[]{:S(2)}, u32[]{:S(2)}) collective-permute-start(bf16[2,1,128,384]{3,2,1,0:T(8,128)(2,1)S(1)} %get-tuple-element.11), channel_id=1, source_target_pairs={{1,0},{2,1},{3,2},{4,3},{5,4},{6,5},{7,6},{9,8},{10,9},{11,10},{12... | collective-permute-start | bytes 589832 | tf_op jit(solution)/shard_map/ppermute | solution.py:17
  23.3 98.8 %all-gather.5.cloned.1.call-start = ((), (), s32[]{:S(2)}) async-start(), calls=%async_computation.1 | async-start | bytes 3538944 | tf_op jit(solution)/shard_map/all_gather | solution.py:74
  40.7 9.9 %slice-start = ((s8[7962624]{0:T(1024)(128)(4,1)}), s8[4194304]{0:T(1024)(128)(4,1)S(1)}, s32[]{:S(2)}) async-start(s8[7962624]{0:T(1024)(128)(4,1)} %bitcast.303), calls=%async_computation.2 | async-start | bytes 8388608
  44.9 5.7 %slice-start.1 = ((s8[7962624]{0:T(1024)(128)(4,1)}), s8[3768320]{0:T(1024)(128)(4,1)S(1)}, s32[]{:S(2)}) async-start(s8[7962624]{0:T(1024)(128)(4,1)} %bitcast.303), calls=%async_computation.3 | async-start | bytes 7536640
  44.9 6.9 %copy-start.2 = (bf16[2,4,130,384]{3,2,1,0:T(8,128)(2,1)S(1)}, bf16[2,4,130,384]{3,2,1,0:T(8,128)(2,1)}, u32[]{:S(2)}) copy-start(bf16[2,4,130,384]{3,2,1,0:T(8,128)(2,1)} %gather_fusion.1) | copy-start | bytes 2396164
  56.0 2.8 %copy-start.1 = (bf16[2,2,128,384]{3,2,1,0:T(8,128)(2,1)S(1)}, bf16[2,2,128,384]{3,2,1,0:T(8,128)(2,1)}, u32[]{:S(2)}) copy-start(bf16[2,2,128,384]{3,2,1,0:T(8,128)(2,1)} %param.12) | copy-start | bytes 1179652
  56.0 2.8 %copy-start.6 = (f32[384]{0:T(512)S(1)}, f32[384]{0:T(512)}, u32[]{:S(2)}) copy-start(f32[384]{0:T(512)} %param.16) | copy-start | bytes 4612
  56.4 3.0 %copy-start.5 = (f32[384]{0:T(512)S(1)}, f32[384]{0:T(512)}, u32[]{:S(2)}) copy-start(f32[384]{0:T(512)} %param.17) | copy-start | bytes 4612
  56.8 3.5 %copy-start.3 = (bf16[384,384]{1,0:T(8,128)(2,1)S(1)}, bf16[384,384]{1,0:T(8,128)(2,1)}, u32[]{:S(2)}) copy-start(bf16[384,384]{1,0:T(8,128)(2,1)} %param.18) | copy-start | bytes 884740
  60.3 71.8 %copy-start.7 = (bf16[384,384]{1,0:T(8,128)(2,1)S(1)}, bf16[384,384]{1,0:T(8,128)(2,1)}, u32[]{:S(2)}) copy-start(bf16[384,384]{1,0:T(8,128)(2,1)} %param.20) | copy-start | bytes 884740
  132.1 6.4 %copy-start.4 = (bf16[384,384]{1,0:T(8,128)(2,1)S(1)}, bf16[384,384]{1,0:T(8,128)(2,1)}, u32[]{:S(2)}) copy-start(bf16[384,384]{1,0:T(8,128)(2,1)} %param.21) | copy-start | bytes 884740
Sparse Core Ops, SparseCore 0:
  23.4 12.0 all-gather.2
  60.4 61.6 all-gather.4

commit v2 on v1

v2 whole, which is shorter than its diff:
```python
import jax
import jax.numpy as jnp
from jax import lax
from jax.sharding import PartitionSpec as P


def padded_2(cells, sides, width):
    for axis, dim in sides:
        count = lax.axis_size(axis)
        ends = count - 1
        head = lax.slice_in_dim(cells, 0, width, axis=dim)
        tail = lax.slice_in_dim(cells, cells.shape[dim] - width, cells.shape[dim], axis=dim)
        cells = jnp.concatenate(
            [
                lax.ppermute(tail, axis, [(i, (i + 1) % count) for i in range(ends)]),
                cells,
                lax.ppermute(head, axis, [((i + 1) % count, i) for i in range(ends)]),
            ],
            axis=dim,
        )
    return cells


def rms_scaled(frames, gain):
    widened = frames.astype(jnp.float32)
    mean_square = jnp.mean(widened * widened, axis=-1, keepdims=True)
    return widened * lax.rsqrt(mean_square + 1e-06) * gain


def shards(
    frames,
    earlier,
    gain_conv,
    conv_weight,
    conv_bias,
    gain_attn,
    query_weight,
    key_weight,
    value_weight,
    out_weight,
):
    span_count, row_count, col_count, channels = frames.shape
    activated = jax.nn.silu(rms_scaled(frames, gain_conv)).astype(jnp.bfloat16)
    rimmed = padded_2(activated, (("height", 1),), 1)
    gathered = lax.all_gather(rimmed, "tm", axis=0, tiled=True)
    border = ((0, 0), (0, 0), (1, 1), (0, 0))
    padded = jnp.pad(rimmed, border)
    gathered = jnp.pad(gathered, border)
    back_two = jnp.take(gathered, jnp.maximum(earlier[:, 0], 0), axis=0)
    back_one = jnp.take(gathered, jnp.maximum(earlier[:, 1], 0), axis=0)
    present_two = (earlier[:, 0] >= 0)[:, None, None, None]
    present_one = (earlier[:, 1] >= 0)[:, None, None, None]
    back_two = jnp.where(present_two, back_two, jnp.zeros_like(back_two))
    back_one = jnp.where(present_one, back_one, jnp.zeros_like(back_one))
    window = jnp.stack([back_two, back_one, padded], axis=1)
    score_scale = 1.0 / channels**0.5

    def conv_span(span_window, span):
        accum = jnp.zeros((row_count, col_count, channels), jnp.float32)
        for tap_t in range(3):
            for tap_y in range(3):
                for tap_x in range(3):
                    sliced = span_window[tap_t, tap_y : tap_y + row_count, tap_x : tap_x + col_count]
                    accum = accum + jnp.einsum(
                        "hwc,cd->hwd",
                        sliced,
                        conv_weight[tap_t, tap_y, tap_x],
                        preferred_element_type=jnp.float32,
                    )
        mixed = (frames[span].astype(jnp.float32) + accum + conv_bias).astype(jnp.bfloat16)
        normed = rms_scaled(mixed, gain_attn).astype(jnp.bfloat16)
        return mixed, normed.reshape(row_count * col_count, channels)

    def attend_span(mixed, tokens, tokens_all):
        queries = jnp.dot(tokens, query_weight, preferred_element_type=jnp.float32).astype(
            jnp.bfloat16
        )
        keys_all = jnp.dot(tokens_all, key_weight, preferred_element_type=jnp.float32).astype(
            jnp.bfloat16
        )
        values_all = jnp.dot(
            tokens_all, value_weight, preferred_element_type=jnp.float32
        ).astype(jnp.bfloat16)
        scores = (
            jnp.einsum("qc,kc->qk", queries, keys_all, preferred_element_type=jnp.float32)
            * score_scale
        )
        peaks = jnp.max(scores, axis=-1, keepdims=True)
        weights_exp = jnp.exp(scores - peaks)
        totals = jnp.sum(weights_exp, axis=-1, keepdims=True)
        summed = jnp.dot(
            weights_exp.astype(jnp.bfloat16), values_all, preferred_element_type=jnp.float32
        )
        attended = (summed / totals).astype(jnp.bfloat16)
        projected = jnp.dot(attended, out_weight, preferred_element_type=jnp.float32)
        encoded = mixed.astype(jnp.float32) + projected.reshape(row_count, col_count, channels)
        return encoded.astype(jnp.bfloat16)

    outputs = []
    pending = None
    span_window = window[0]
    for span in range(span_count):
        mixed, tokens = conv_span(span_window, span)
        if span + 1 < span_count:
            tokens, span_window = lax.optimization_barrier((tokens, window[span + 1]))
        tokens_all = lax.all_gather(tokens, "height", axis=0, tiled=True)
        if pending is not None:
            mixed, tokens, pending = lax.optimization_barrier((mixed, tokens, pending))
            outputs.append(attend_span(*pending))
        pending = (mixed, tokens, tokens_all)
    outputs.append(attend_span(*pending))
    return jnp.stack(outputs, axis=0)


def solution(mesh):
    in_specs = (
        P(("group", "tm"), "height", None, None),
        P(("group", "tm"), None),
        P(),
        P(),
        P(),
        P(),
        P(),
        P(),
        P(),
        P(),
    )
    out_specs = P(("group", "tm"), "height", None, None)
    return jax.shard_map(shards, mesh=mesh, in_specs=in_specs, out_specs=out_specs, check_vma=False)
```

time: 147 us -> 185 us (1.26)
  matrix products: 32.1 us -> 59.4 us
  waiting for transfers between devices: 76 us -> 87.1 us
  other arithmetic: 11.9 us -> 9.3 us
    dot_general x31 -> x62, matrix products: 32.1 us -> 59.4 us  [the longest x54 43.3 us: conv_span(): jnp.einsum('hwc,cd->hwd', sliced, conv_weight[tap_t, tap_y, tap_x], prefe...]
    all_gather x1 -> x2, waiting for transfers between devices: 60.2 us -> 69.7 us  [shards(): tokens_all = lax.all_gather(tokens, 'height', axis=0, tiled=True)]
    reduce_sum x1 -> x2, other arithmetic: 3 us -> 0.87 us  [attend_span(): totals = jnp.sum(weights_exp, axis=-1, keepdims=True)]
  transfers between devices with their start and end apart: 4 -> 5, of which waited for: 4 -> 5; matrix products, arithmetic and copies ran while one was open for 3% -> 12% of each run, Pallas kernels for 0% -> 0%
where the time goes in v2:
time: 185 us; the launch traced here: 183 us
  waiting for transfers between devices  87.1 us (47%)
  matrix products  59.4 us (32%)
  between operations  13.8 us (7%)
  other arithmetic  9.3 us (5%)
  local copies, waits for them, and re-layouts  7.41 us (4%)
  starting transfers between devices  6.26 us (3%)
    all_gather x2, waiting for transfers between devices, shards(): tokens_all = lax.all_gather(tokens, 'height', axis=0, tiled=True)  69.7 us
    dot_general x54, matrix products, conv_span(): jnp.einsum('hwc,cd->hwd', sliced, conv_weight[tap_t, tap_y, tap_x], prefe...  43.3 us
    all_gather x1, waiting for transfers between devices, shards(): gathered = lax.all_gather(rimmed, 'tm', axis=0, tiled=True)  10.4 us
    dot_general x2, matrix products, attend_span(): jnp.dot(weights_exp.astype(jnp.bfloat16), values_all, preferred_element_t...  6.95 us
    dot_general x2, matrix products, attend_span(): jnp.einsum('qc,kc->qk', queries, keys_all, preferred_element_type=jnp.flo...  6.41 us
    ppermute x1, starting transfers between devices, padded_2(): lax.ppermute(tail, axis, [(i, (i + 1) % count) for i in range(ends)])  4.88 us
    ppermute x1, waiting for transfers between devices, padded_2(): lax.ppermute(head, axis, [((i + 1) % count, i) for i in range(ends)])  4.07 us
  transfers between devices with their start and end apart: 5, of which 5 were waited for; matrix products, arithmetic and copies ran while one was open for 12% of the time, Pallas kernels for 0%

profile of v2, /device:TPU:0, one launch (start us, length us, event | category | flops | bytes accessed | tf_op | source)
XLA Modules:
  0.0 183.2 jit_solution(11251715739805948440)
XLA Ops:
  6.5 1.2 fusion.22
  7.8 1.3 fusion.29
  9.1 4.9 %collective-permute-start = (bf16[2,1,128,384]{3,2,1,0:T(8,128)(2,1)S(1)}, bf16[2,1,128,384]{3,2,1,0:T(8,128)(2,1)S(1)}, u32[]{:S(2)}, u32[]{:S(2)}) collective-permute-start(bf16[2,1,128,384]{3,2,1,0:T(8,128)(2,1)S(1)} %get-tuple-element.26), channel_id=1, source_target_pairs={{0,1},{1,2},{2,3},{3,4},{4,5},{5,6},{6,7},{8,9},{9,10},{10,11},{11... | collective-permute-start | bytes 589832 | tf_op jit(solution)/shard_map/ppermute | solution.py:15
  14.0 1.3 collective-permute-start.1
  15.3 2.9 %collective-permute-done = bf16[2,1,128,384]{3,2,1,0:T(8,128)(2,1)S(1)} collective-permute-done((bf16[2,1,128,384]{3,2,1,0:T(8,128)(2,1)S(1)}, bf16[2,1,128,384]{3,2,1,0:T(8,128)(2,1)S(1)}, u32[]{:S(2)}, u32[]{:S(2)}) %collective-permute-start) | collective-permute-done | bytes 196640 | tf_op jit(solution)/shard_map/ppermute | solution.py:15
  18.2 4.1 %collective-permute-done.1 = bf16[2,1,128,384]{3,2,1,0:T(8,128)(2,1)S(1)} collective-permute-done((bf16[2,1,128,384]{3,2,1,0:T(8,128)(2,1)S(1)}, bf16[2,1,128,384]{3,2,1,0:T(8,128)(2,1)S(1)}, u32[]{:S(2)}, u32[]{:S(2)}) %collective-permute-start.1) | collective-permute-done | bytes 196640 | tf_op jit(solution)/shard_map/ppermute | solution.py:17
  22.3 1.0 pad_maximum_fusion.1
  23.8 1.3 pad_bitcast_fusion
  25.1 10.4 %all-gather.4.cloned.1.call-done = bf16[4,4,128,384]{3,2,1,0:T(8,128)(2,1)} async-done(((bf16[2,4,128,384]{3,2,1,0:T(8,128)(2,1)}), bf16[4,4,128,384]{3,2,1,0:T(8,128)(2,1)}) %all-gather.4.cloned.1.call-update) | async-done | bytes 1572880 | tf_op jit(solution)/shard_map/all_gather | solution.py:45
  35.5 1.9 %pad.8 = bf16[4,4,130,384]{3,2,1,0:T(8,128)(2,1)S(1)} pad(bf16[4,4,128,384]{3,2,1,0:T(8,128)(2,1)} %all-gather.4.cloned.1.call-done, bf16[]{:T(256)} %constant.9.clone.1), padding=0_0x0_0x1_1x0_0 | pad | bytes 3170306 | tf_op jit(solution)/shard_map/jit(_pad)/pad | solution.py:48
  37.5 1.6 gather_fusion.1
  39.0 1.6 gather_fusion
  40.6 1.5 fusion.20
  42.3 0.3 pad_maximum_fusion
  42.9 1.5 fusion.38
  44.5 1.2 convolution_add_fusion.51
  48.0 0.3 convolution_add_fusion.42
  48.3 0.3 convolution_add_fusion.41
  48.8 0.3 convolution_add_fusion.39
  49.7 0.3 convolution_add_fusion.36
  49.9 0.3 convolution_add_fusion.35
  51.6 0.3 convolution_add_fusion.29
  52.6 0.4 fusion.30
  53.0 0.8 fusion.32
  53.8 1.2 fusion.36
  55.1 1.2 convolution_add_fusion.25
  56.3 1.2 convolution_add_fusion.24
  57.6 1.2 convolution_add_fusion.23
  58.8 1.2 convolution_add_fusion.22
  60.0 1.2 convolution_add_fusion.21
  61.3 1.2 convolution_add_fusion.20
  62.5 1.2 convolution_add_fusion.19
  63.8 1.2 convolution_add_fusion.18
  65.0 1.2 convolution_add_fusion.17
  66.2 1.2 convolution_add_fusion.16
  67.5 1.2 convolution_add_fusion.15
  68.7 1.2 convolution_add_fusion.14
  69.9 1.2 convolution_add_fusion.13
  71.2 1.2 convolution_add_fusion.12
  72.4 1.2 convolution_add_fusion.11
  73.7 1.4 convolution_add_fusion.10
  75.1 1.2 convolution_add_fusion.9
  76.4 1.2 convolution_add_fusion.8
  77.6 1.2 convolution_add_fusion.7
  78.9 1.2 convolution_add_fusion.6
  80.1 1.2 convolution_add_fusion.5
  81.4 1.2 convolution_add_fusion.4
  82.6 1.2 convolution_add_fusion.3
  83.9 1.3 convolution_add_fusion.2
  85.2 1.2 convolution_add_fusion.1
  86.4 1.4 fusion.33
  87.8 0.8 fusion.35
  88.6 33.3 %all-gather.6.cloned.1.call-done = bf16[2048,384]{1,0:T(8,128)(2,1)} async-done(((bf16[256,384]{1,0:T(8,128)(2,1)}), bf16[2048,384]{1,0:T(8,128)(2,1)}) %all-gather.6.cloned.1.call-update) | async-done | bytes 1572880 | tf_op jit(solution)/shard_map/all_gather | solution.py:106
  122.2 3.1 %fusion.204 = (f32[256]{0:T(256)S(1)}, f32[256,2048]{1,0:T(8,128)S(1)}) fusion(bf16[256,384]{1,0:T(8,128)(2,1)S(1)} %convolution_convert_fusion.5, bf16[2048,384]{1,0:T(8,128)(2,1)} %all-gather.6.cloned.1.call-done, bf16[384,384]{1,0:T(8,128)(2,1)S(1)} %copy-done), kind=kOutput, calls=%fused_computation.322 | convolution fusion | flops 1008467712 | bytes 4162560 | tf_op jit(solution)/shard_map/qc,kc->qk/dot_general | solution.py:85
  125.3 0.4 fusion
  125.8 0.5 copy-done.3
  126.3 1.0 convolution_convert_fusion.4
  127.2 3.1 %fusion.15 = bf16[256,384]{1,0:T(8,128)(2,1)S(1)} fusion(bf16[2048,384]{1,0:T(8,128)(2,1)} %all-gather.6.cloned.1.call-done, bf16[384,384]{1,0:T(8,128)(2,1)} %param.20, f32[256,2048]{1,0:T(8,128)S(1)} %get-tuple-element.35, f32[256]{0:T(256)S(1)} %get-tuple-element.34, f32[256]{0:T(256)S(1)} %fusion), kind=kOutput, calls=%fused_computation.82 | convolution fusion | flops 1008664576 | bytes 4163584 | tf_op jit(solution)/shard_map/dot_general | solution.py:91
  130.7 36.5 %all-gather.8.cloned.1.call-done = bf16[2048,384]{1,0:T(8,128)(2,1)} async-done(((bf16[256,384]{1,0:T(8,128)(2,1)}), bf16[2048,384]{1,0:T(8,128)(2,1)}) %all-gather.8.cloned.1.call-update) | async-done | bytes 1572880 | tf_op jit(solution)/shard_map/all_gather | solution.py:106
  167.1 3.3 %fusion.203 = (f32[256]{0:T(256)S(1)}, f32[256,2048]{1,0:T(8,128)S(1)}) fusion(bf16[256,384]{1,0:T(8,128)(2,1)} %convolution_convert_fusion.4, bf16[2048,384]{1,0:T(8,128)(2,1)} %all-gather.8.cloned.1.call-done, bf16[384,384]{1,0:T(8,128)(2,1)S(1)} %copy-done), kind=kOutput, calls=%fused_computation.321 | convolution fusion | flops 1008467712 | bytes 4162560 | tf_op jit(solution)/shard_map/qc,kc->qk/dot_general | solution.py:85
  170.4 0.4 fusion.2
  170.8 3.8 %fusion.13 = bf16[256,384]{1,0:T(8,128)(2,1)} fusion(bf16[2048,384]{1,0:T(8,128)(2,1)} %all-gather.8.cloned.1.call-done, bf16[384,384]{1,0:T(8,128)(2,1)} %param.20, f32[256,2048]{1,0:T(8,128)S(1)} %get-tuple-element.33, f32[256]{0:T(256)S(1)} %get-tuple-element.32, f32[256]{0:T(256)S(1)} %fusion.2), kind=kOutput, calls=%fused_computation.80 | convolution fusion | flops 1008664576 | bytes 4163584 | tf_op jit(solution)/shard_map/dot_general | solution.py:91
  174.6 1.2 fusion.206
  175.9 0.8 pad_maximum_fusion.2
  (64 shorter events, 6.7 us)
Async XLA Ops:
  6.5 115.6 %copy-start = (bf16[384,384]{1,0:T(8,128)(2,1)S(1)}, bf16[384,384]{1,0:T(8,128)(2,1)}, u32[]{:S(2)}) copy-start(bf16[384,384]{1,0:T(8,128)(2,1)} %param.19) | copy-start | bytes 884740
  6.5 16.8 %copy-start.7 = (s32[2,2]{1,0:T(2,128)S(1)}, s32[2,2]{1,0:T(2,128)}, u32[]{:S(2)}) copy-start(s32[2,2]{1,0:T(2,128)} %param.13) | copy-start | bytes 52
  6.5 29.0 %all-gather.4.cloned.1.call-start = ((), (), s32[]{:S(2)}) async-start(), calls=%async_computation | async-start | bytes 2359296 | tf_op jit(solution)/shard_map/all_gather | solution.py:45
  9.1 9.1 %collective-permute-start = (bf16[2,1,128,384]{3,2,1,0:T(8,128)(2,1)S(1)}, bf16[2,1,128,384]{3,2,1,0:T(8,128)(2,1)S(1)}, u32[]{:S(2)}, u32[]{:S(2)}) collective-permute-start(bf16[2,1,128,384]{3,2,1,0:T(8,128)(2,1)S(1)} %get-tuple-element.26), channel_id=1, source_target_pairs={{0,1},{1,2},{2,3},{3,4},{4,5},{5,6},{6,7},{8,9},{9,10},{10,11},{11... | collective-permute-start | bytes 589832 | tf_op jit(solution)/shard_map/ppermute | solution.py:15
  14.0 8.3 %collective-permute-start.1 = (bf16[2,1,128,384]{3,2,1,0:T(8,128)(2,1)S(1)}, bf16[2,1,128,384]{3,2,1,0:T(8,128)(2,1)S(1)}, u32[]{:S(2)}, u32[]{:S(2)}) collective-permute-start(bf16[2,1,128,384]{3,2,1,0:T(8,128)(2,1)S(1)} %get-tuple-element.27), channel_id=1, source_target_pairs={{1,0},{2,1},{3,2},{4,3},{5,4},{6,5},{7,6},{9,8},{10,9},{11,10},{12... | collective-permute-start | bytes 589832 | tf_op jit(solution)/shard_map/ppermute | solution.py:17
  23.3 98.6 %all-gather.6.cloned.1.call-start = ((), (), s32[]{:S(2)}) async-start(), calls=%async_computation.1 | async-start | bytes 1769472 | tf_op jit(solution)/shard_map/all_gather | solution.py:106
  40.6 1.5 copy-start.1
  40.6 5.1 %slice-start = ((s8[7962624]{0:T(1024)(128)(4,1)}), s8[4194304]{0:T(1024)(128)(4,1)S(1)}, s32[]{:S(2)}) async-start(s8[7962624]{0:T(1024)(128)(4,1)} %bitcast.403), calls=%async_computation.3 | async-start | bytes 8388608
  42.3 3.4 %slice-start.1 = ((s8[7962624]{0:T(1024)(128)(4,1)}), s8[3768320]{0:T(1024)(128)(4,1)S(1)}, s32[]{:S(2)}) async-start(s8[7962624]{0:T(1024)(128)(4,1)} %bitcast.403), calls=%async_computation.4 | async-start | bytes 7536640
  51.6 1.0 copy-start.4
  51.6 1.0 copy-start.9
  51.9 1.1 copy-start.8
  76.4 90.8 %all-gather.8.cloned.1.call-start = ((), (), s32[]{:S(2)}) async-start(), calls=%async_computation.2 | async-start | bytes 1769472 | tf_op jit(solution)/shard_map/all_gather | solution.py:106
  83.8 38.1 %copy-start.2 = (bf16[2,128,384]{2,1,0:T(8,128)(2,1)S(1)}, bf16[2,128,384]{2,1,0:T(8,128)(2,1)}, u32[]{:S(2)}) copy-start(bf16[2,128,384]{2,1,0:T(8,128)(2,1)} %fusion.32) | copy-start | bytes 589828
  83.8 38.1 %copy-start.6 = (bf16[384,384]{1,0:T(8,128)(2,1)S(1)}, bf16[384,384]{1,0:T(8,128)(2,1)}, u32[]{:S(2)}) copy-start(bf16[384,384]{1,0:T(8,128)(2,1)} %param.18) | copy-start | bytes 884740
  125.3 0.9 copy-start.3
  127.2 3.2 %copy-start.5 = (bf16[384,384]{1,0:T(8,128)(2,1)S(1)}, bf16[384,384]{1,0:T(8,128)(2,1)}, u32[]{:S(2)}) copy-start(bf16[384,384]{1,0:T(8,128)(2,1)} %param.21) | copy-start | bytes 884740
Sparse Core Ops, SparseCore 0:
  23.4 12.0 all-gather.3
  76.5 45.3 all-gather.5
  124.1 42.9 all-gather.7

commit v3 on v1

--- a/solution.py
+++ b/solution.py
@@ -19,6 +19,23 @@
             axis=dim,
         )
     return cells
+
+
+def ring_gather(block, axis, dim):
+    count = lax.axis_size(axis)
+    ring = list(range(0, count, 2)) + list(range(count - 1 - count % 2, 0, -2))
+    ahead = [(ring[p], ring[(p + 1) % count]) for p in range(count)]
+    behind = [(ring[p], ring[(p - 1) % count]) for p in range(count)]
+    pieces = [block]
+    forward = block
+    backward = block
+    for step in range(count // 2):
+        forward = lax.ppermute(forward, axis, ahead)
+        pieces.append(forward)
+        if len(pieces) < count:
+            backward = lax.ppermute(backward, axis, behind)
+            pieces.append(backward)
+    return jnp.concatenate(pieces, axis=dim)
 
 
 def rms_scaled(frames, gain):
@@ -71,7 +88,7 @@
         "ftc,cd->ftd", tokens, query_weight, preferred_element_type=jnp.float32
     ).astype(jnp.bfloat16)
     score_scale = 1.0 / channels**0.5
-    tokens_all = lax.all_gather(tokens, "height", axis=1, tiled=True)
+    tokens_all = ring_gather(tokens, "height", 1)
     keys_all = jnp.einsum(
         "ftc,cd->ftd", tokens_all, key_weight, preferred_element_type=jnp.float32
     ).astype(jnp.bfloat16)

time: 147 us -> 148 us (level)
  waiting for transfers between devices: 76 us -> 43.7 us
  matrix products: 32.1 us -> 52.2 us
  starting transfers between devices: 6.22 us -> 14.1 us
  local copies, waits for them, and re-layouts: 6.55 us -> 12.9 us
    all_gather x1 -> x0, waiting for transfers between devices: 60.2 us -> none  [shards(): tokens_all = lax.all_gather(tokens, 'height', axis=1, tiled=True)]
    ppermute x0 -> x7, waiting for transfers between devices: none -> 26.3 us  [the longest x4 26.3 us: ring_gather(): forward = lax.ppermute(forward, axis, ahead)]
    dot_general x27, matrix products: 16.7 us -> 38 us  [shards(): jnp.einsum('fhwc,cd->fhwd', sliced, conv_weight[tap_t, tap_y, tap_x], pre...]
    ppermute x0 -> x7, starting transfers between devices: none -> 7.88 us  [the longest x4 7.04 us: ring_gather(): forward = lax.ppermute(forward, axis, ahead)]
    unnamed x20 -> x23, local copies, waits for them, and re-layouts: 0.06 us -> 5.57 us
    all_gather x1, waiting for transfers between devices: 8.85 us -> 10.4 us  [shards(): gathered = lax.all_gather(rimmed, 'tm', axis=0, tiled=True)]
  transfers between devices with their start and end apart: 4 -> 10, of which waited for: 4 -> 7; matrix products, arithmetic and copies ran while one was open for 3% -> 5% of each run, Pallas kernels for 0% -> 0%
where the time goes in v3:
time: 148 us; the launch traced here: 147 us
  matrix products  52.2 us (35%)
  waiting for transfers between devices  43.7 us (30%)
  starting transfers between devices  14.1 us (10%)
  between operations  13.8 us (9%)
  local copies, waits for them, and re-layouts  12.9 us (9%)
  other arithmetic  10.6 us (7%)
    dot_general x27, matrix products, shards(): jnp.einsum('fhwc,cd->fhwd', sliced, conv_weight[tap_t, tap_y, tap_x], pre...  38 us
    ppermute x4, waiting for transfers between devices, ring_gather(): forward = lax.ppermute(forward, axis, ahead)  26.3 us
    all_gather x1, waiting for transfers between devices, shards(): gathered = lax.all_gather(rimmed, 'tm', axis=0, tiled=True)  10.4 us
    ppermute x4, starting transfers between devices, ring_gather(): forward = lax.ppermute(forward, axis, ahead)  7.04 us
    dot_general x1, matrix products, shards(): jnp.einsum('fqc,fkc->fqk', queries, keys_all, preferred_element_type=jnp....  7 us
    dot_general x1, matrix products, shards(): jnp.einsum('fqk,fkc->fqc', weights_exp.astype(jnp.bfloat16), values_all,...  6.4 us
    unnamed x23, local copies, waits for them, and re-layouts  5.57 us
    ppermute x1, starting transfers between devices, padded_2(): lax.ppermute(tail, axis, [(i, (i + 1) % count) for i in range(ends)])  4.88 us
  transfers between devices with their start and end apart: 10, of which 7 were waited for; matrix products, arithmetic and copies ran while one was open for 5% of the time, Pallas kernels for 0%

profile of v3, /device:TPU:0, one launch (start us, length us, event | category | flops | bytes accessed | tf_op | source)
XLA Modules:
  0.0 147.2 jit_solution(3500945449126467119)
XLA Ops:
  6.5 1.2 fusion.19
  7.8 1.3 fusion.26
  9.1 4.9 %collective-permute-start = (bf16[2,1,128,384]{3,2,1,0:T(8,128)(2,1)S(1)}, bf16[2,1,128,384]{3,2,1,0:T(8,128)(2,1)S(1)}, u32[]{:S(2)}, u32[]{:S(2)}) collective-permute-start(bf16[2,1,128,384]{3,2,1,0:T(8,128)(2,1)S(1)} %get-tuple-element.10), channel_id=1, source_target_pairs={{0,1},{1,2},{2,3},{3,4},{4,5},{5,6},{6,7},{8,9},{9,10},{10,11},{11... | collective-permute-start | bytes 589832 | tf_op jit(solution)/shard_map/ppermute | solution.py:15
  14.0 1.3 collective-permute-start.1
  15.3 2.9 %collective-permute-done = bf16[2,1,128,384]{3,2,1,0:T(8,128)(2,1)S(1)} collective-permute-done((bf16[2,1,128,384]{3,2,1,0:T(8,128)(2,1)S(1)}, bf16[2,1,128,384]{3,2,1,0:T(8,128)(2,1)S(1)}, u32[]{:S(2)}, u32[]{:S(2)}) %collective-permute-start) | collective-permute-done | bytes 196640 | tf_op jit(solution)/shard_map/ppermute | solution.py:15
  18.2 4.1 %collective-permute-done.1 = bf16[2,1,128,384]{3,2,1,0:T(8,128)(2,1)S(1)} collective-permute-done((bf16[2,1,128,384]{3,2,1,0:T(8,128)(2,1)S(1)}, bf16[2,1,128,384]{3,2,1,0:T(8,128)(2,1)S(1)}, u32[]{:S(2)}, u32[]{:S(2)}) %collective-permute-start.1) | collective-permute-done | bytes 196640 | tf_op jit(solution)/shard_map/ppermute | solution.py:17
  22.3 1.0 pad_maximum_fusion
  23.7 1.3 pad_bitcast_fusion
  25.1 10.4 %all-gather.2.cloned.1.call-done = bf16[4,4,128,384]{3,2,1,0:T(8,128)(2,1)} async-done(((bf16[2,4,128,384]{3,2,1,0:T(8,128)(2,1)}), bf16[4,4,128,384]{3,2,1,0:T(8,128)(2,1)}) %all-gather.2.cloned.1.call-update) | async-done | bytes 1572880 | tf_op jit(solution)/shard_map/all_gather | solution.py:62
  35.5 1.9 %pad.8 = bf16[4,4,130,384]{3,2,1,0:T(8,128)(2,1)S(1)} pad(bf16[4,4,128,384]{3,2,1,0:T(8,128)(2,1)} %all-gather.2.cloned.1.call-done, bf16[]{:T(256)} %constant.14.clone.1), padding=0_0x0_0x1_1x0_0 | pad | bytes 3170306 | tf_op jit(solution)/shard_map/jit(_pad)/pad | solution.py:65
  37.5 1.6 %gather_fusion = bf16[2,4,130,384]{3,2,1,0:T(8,128)(2,1)} fusion(bf16[4,4,130,384]{3,2,1,0:T(8,128)(2,1)S(1)} %pad.8, s32[1024]{0:T(1024)S(1)} %pad_clamp_fusion.1), kind=kCustom, calls=%fused_computation.clone | custom fusion | bytes 1597448 | tf_op jit(solution)/shard_map/jit(_take)/gather | solution.py:66
  39.0 1.3 fusion.18
  40.4 1.4 fusion.27
  41.7 1.4 convolution_add_fusion.25
  43.1 1.4 convolution_add_fusion.24
  44.5 1.4 convolution_add_fusion.23
  45.8 1.4 convolution_add_fusion.22
  47.2 1.4 convolution_add_fusion.21
  48.6 1.4 convolution_add_fusion.20
  49.9 1.4 convolution_add_fusion.19
  51.3 2.3 %convolution_add_fusion.18 = f32[2,2,128,384]{3,2,1,0:T(8,128)} fusion(f32[2,2,128,384]{3,2,1,0:T(8,128)S(1)} %convolution_add_fusion.19, bf16[2,1,4,130,384]{4,3,2,0,1:T(8,128)(2,1)S(1)} %fusion.18, bf16[3,3,3,384,384]{4,3,2,1,0:T(8,128)(2,1)} %param.15), kind=kOutput, calls=%fused_computation.30 | convolution fusion | flops 151191552 | bytes 2260992 | tf_op jit(solution)/shard_map/fhwc,cd->fhwd/dot_general | solution.py:78
  53.5 1.6 %gather_fusion.1 = bf16[2,4,130,384]{3,2,1,0:T(8,128)(2,1)} fusion(bf16[4,4,130,384]{3,2,1,0:T(8,128)(2,1)S(1)} %pad.8, s32[1024]{0:T(1024)S(1)} %pad_clamp_fusion), kind=kCustom, calls=%fused_computation.1.clone | custom fusion | bytes 1597448 | tf_op jit(solution)/shard_map/jit(_take)/gather | solution.py:67
  55.1 1.3 fusion.17
  56.4 1.6 %convolution_add_fusion.17 = f32[2,2,128,384]{3,2,1,0:T(8,128)S(1)} fusion(f32[2,2,128,384]{3,2,1,0:T(8,128)} %convolution_add_fusion.18, bf16[2,1,4,130,384]{4,3,2,0,1:T(8,128)(2,1)S(1)} %fusion.17, bf16[3,3,3,384,384]{4,3,2,1,0:T(8,128)(2,1)} %param.15), kind=kOutput, calls=%fused_computation.29 | convolution fusion | flops 151191552 | bytes 2260992 | tf_op jit(solution)/shard_map/fhwc,cd->fhwd/dot_general | solution.py:78
  58.1 1.4 convolution_add_fusion.16
  59.5 1.4 convolution_add_fusion.15
  60.8 1.4 convolution_add_fusion.14
  62.2 1.4 convolution_add_fusion.13
  63.5 1.4 convolution_add_fusion.12
  64.9 1.4 convolution_add_fusion.11
  66.3 1.4 convolution_add_fusion.10
  67.6 1.4 convolution_add_fusion.9
  69.0 1.4 convolution_add_fusion.8
  70.4 1.4 convolution_add_fusion.7
  71.7 1.4 convolution_add_fusion.6
  73.1 1.4 convolution_add_fusion.5
  74.5 1.4 convolution_add_fusion.4
  75.9 1.4 convolution_add_fusion.3
  77.3 1.4 convolution_add_fusion.2
  78.7 1.4 convolution_add_fusion.1
  80.0 1.5 %multiply_reduce_fusion.1 = (f32[2,2,128]{2,1,0:T(2,128)S(1)}, f32[2,2,128,384]{3,2,1,0:T(8,128)S(1)}) fusion(f32[384]{0:T(512)S(1)} %copy-done.6, f32[2,2,128,384]{3,2,1,0:T(8,128)S(1)} %convolution_add_fusion.1, bf16[3,3,3,384,384]{4,3,2,1,0:T(8,128)(2,1)} %param.15, bf16[2,1,4,130,384]{4,3,2,0,1:T(8,128)(2,1)S(1)} %pad_bitcast_fusion, ...), kind=kOutput, calls=%fused_computation.63 | convolution fusion | flops 152567296 | bytes 2658304 | tf_op jit(solution)/shard_map/fhwc,cd->fhwd/dot_general | solution.py:78
  81.7 1.8 %collective-permute-start.2 = (bf16[2,256,384]{2,1,0:T(8,128)(2,1)S(1)}, bf16[2,256,384]{2,1,0:T(8,128)(2,1)S(1)}, u32[]{:S(2)}, u32[]{:S(2)}) collective-permute-start(bf16[2,256,384]{2,1,0:T(8,128)(2,1)S(1)} %bitcast.303), channel_id=1, source_target_pairs={{0,2},{2,4},{4,6},{6,7},{7,5},{5,3},{3,1},{1,0},{8,10},{10,12},{12... | collective-permute-start | bytes 1179656 | tf_op jit(solution)/shard_map/ppermute | solution.py:33
  83.5 0.3 collective-permute-start.3
  83.8 9.3 %collective-permute-done.2 = bf16[2,256,384]{2,1,0:T(8,128)(2,1)S(1)} collective-permute-done((bf16[2,256,384]{2,1,0:T(8,128)(2,1)S(1)}, bf16[2,256,384]{2,1,0:T(8,128)(2,1)S(1)}, u32[]{:S(2)}, u32[]{:S(2)}) %collective-permute-start.2) | collective-permute-done | bytes 393248 | tf_op jit(solution)/shard_map/ppermute | solution.py:33
  93.1 1.7 %collective-permute-start.4 = (bf16[2,256,384]{2,1,0:T(8,128)(2,1)S(1)}, bf16[2,256,384]{2,1,0:T(8,128)(2,1)S(1)}, u32[]{:S(2)}, u32[]{:S(2)}) collective-permute-start(bf16[2,256,384]{2,1,0:T(8,128)(2,1)S(1)} %collective-permute-done.2), channel_id=1, source_target_pairs={{0,2},{2,4},{4,6},{6,7},{7,5},{5,3},{3,1},{1,0},{8,10},{10,12},{12... | collective-permute-start | bytes 1179656 | tf_op jit(solution)/shard_map/ppermute | solution.py:33
  95.1 8.5 %collective-permute-done.4 = bf16[2,256,384]{2,1,0:T(8,128)(2,1)S(1)} collective-permute-done((bf16[2,256,384]{2,1,0:T(8,128)(2,1)S(1)}, bf16[2,256,384]{2,1,0:T(8,128)(2,1)S(1)}, u32[]{:S(2)}, u32[]{:S(2)}) %collective-permute-start.4) | collective-permute-done | bytes 393248 | tf_op jit(solution)/shard_map/ppermute | solution.py:33
  103.6 1.7 %collective-permute-start.6 = (bf16[2,256,384]{2,1,0:T(8,128)(2,1)S(1)}, bf16[2,256,384]{2,1,0:T(8,128)(2,1)S(1)}, u32[]{:S(2)}, u32[]{:S(2)}) collective-permute-start(bf16[2,256,384]{2,1,0:T(8,128)(2,1)S(1)} %collective-permute-done.4), channel_id=1, source_target_pairs={{0,2},{2,4},{4,6},{6,7},{7,5},{5,3},{3,1},{1,0},{8,10},{10,12},{12... | collective-permute-start | bytes 1179656 | tf_op jit(solution)/shard_map/ppermute | solution.py:33
  105.3 0.4 convolution_convert_fusion.2
  105.7 0.8 constant_dynamic-update-slice_fusion.7
  106.6 0.8 constant_dynamic-update-slice_fusion.6
  107.6 0.8 constant_dynamic-update-slice_fusion.5
  108.4 4.8 %collective-permute-done.6 = bf16[2,256,384]{2,1,0:T(8,128)(2,1)S(1)} collective-permute-done((bf16[2,256,384]{2,1,0:T(8,128)(2,1)S(1)}, bf16[2,256,384]{2,1,0:T(8,128)(2,1)S(1)}, u32[]{:S(2)}, u32[]{:S(2)}) %collective-permute-start.6) | collective-permute-done | bytes 393248 | tf_op jit(solution)/shard_map/ppermute | solution.py:33
  113.2 1.7 %collective-permute-start.8 = (bf16[2,256,384]{2,1,0:T(8,128)(2,1)S(1)}, bf16[2,256,384]{2,1,0:T(8,128)(2,1)S(1)}, u32[]{:S(2)}, u32[]{:S(2)}) collective-permute-start(bf16[2,256,384]{2,1,0:T(8,128)(2,1)S(1)} %collective-permute-done.6), channel_id=1, source_target_pairs={{0,2},{2,4},{4,6},{6,7},{7,5},{5,3},{3,1},{1,0},{8,10},{10,12},{12... | collective-permute-start | bytes 1179656 | tf_op jit(solution)/shard_map/ppermute | solution.py:33
  114.9 0.8 constant_dynamic-update-slice_fusion.4
  115.7 0.8 constant_dynamic-update-slice_fusion.3
  116.5 0.8 constant_dynamic-update-slice_fusion.2
  117.3 0.8 constant_dynamic-update-slice_fusion.1
  118.1 3.8 %collective-permute-done.8 = bf16[2,256,384]{2,1,0:T(8,128)(2,1)S(1)} collective-permute-done((bf16[2,256,384]{2,1,0:T(8,128)(2,1)S(1)}, bf16[2,256,384]{2,1,0:T(8,128)(2,1)S(1)}, u32[]{:S(2)}, u32[]{:S(2)}) %collective-permute-start.8) | collective-permute-done | bytes 393248 | tf_op jit(solution)/shard_map/ppermute | solution.py:33
  121.9 0.8 constant_dynamic-update-slice_fusion
  122.7 7.0 %multiply_reduce_fusion = (f32[2,256]{1,0:T(2,128)S(1)}, f32[2,256,2048]{2,1,0:T(8,128)}) fusion(bf16[2,256,384]{2,1,0:T(8,128)(2,1)S(1)} %convolution_convert_fusion.2, bf16[2,2048,384]{2,1,0:T(8,128)(2,1)} %constant_dynamic-update-slice_fusion, bf16[384,384]{1,0:T(8,128)(2,1)S(1)} %copy-done), kind=kOutput, calls=%fused_computation.3 | convolution fusion | flops 2016935424 | bytes 8030208 | tf_op jit(solution)/shard_map/fqc,fkc->fqk/dot_general | solution.py:99
  129.7 3.0 %fusion = f32[2,256]{1,0:T(2,128)S(1)} fusion(f32[2,256,2048]{2,1,0:T(8,128)} %get-tuple-element.15, f32[2,256]{1,0:T(2,128)S(1)} %get-tuple-element.14), kind=kLoop, calls=%fused_computation.4 | loop fusion | flops 3145216 | bytes 4198400 | tf_op jit(solution)/shard_map/reduce_sum | solution.py:104
  132.7 6.4 %fusion.14 = bf16[2,256,384]{2,1,0:T(8,128)(2,1)S(1)} fusion(bf16[2,2048,384]{2,1,0:T(8,128)(2,1)} %constant_dynamic-update-slice_fusion, f32[2,256,2048]{2,1,0:T(8,128)} %get-tuple-element.15, f32[2,256]{1,0:T(2,128)S(1)} %get-tuple-element.14, f32[2,256]{1,0:T(2,128)S(1)} %fusion, bf16[384,384]{1,0:T(8,128)(2,1)S(1)} %copy-done.7), kind=kOutput, calls=%fused_computation.46 | convolution fusion | flops 2018377728 | bytes 8032256 | tf_op jit(solution)/shard_map/fqk,fkc->fqc/dot_general | solution.py:105
  139.1 0.4 fusion.55
  139.5 0.8 add_convert_fusion
  (33 shorter events, 1.2 us)
Async XLA Ops:
  6.5 116.1 %copy-start = (bf16[384,384]{1,0:T(8,128)(2,1)S(1)}, bf16[384,384]{1,0:T(8,128)(2,1)}, u32[]{:S(2)}) copy-start(bf16[384,384]{1,0:T(8,128)(2,1)} %param.19) | copy-start | bytes 884740
  6.5 16.8 %copy-start.4 = (s32[2,2]{1,0:T(2,128)S(1)}, s32[2,2]{1,0:T(2,128)}, u32[]{:S(2)}) copy-start(s32[2,2]{1,0:T(2,128)} %param.13) | copy-start | bytes 52
  6.5 29.0 %all-gather.2.cloned.1.call-start = ((), (), s32[]{:S(2)}) async-start(), calls=%async_computation | async-start | bytes 2359296 | tf_op jit(solution)/shard_map/all_gather | solution.py:62
  9.1 9.1 %collective-permute-start = (bf16[2,1,128,384]{3,2,1,0:T(8,128)(2,1)S(1)}, bf16[2,1,128,384]{3,2,1,0:T(8,128)(2,1)S(1)}, u32[]{:S(2)}, u32[]{:S(2)}) collective-permute-start(bf16[2,1,128,384]{3,2,1,0:T(8,128)(2,1)S(1)} %get-tuple-element.10), channel_id=1, source_target_pairs={{0,1},{1,2},{2,3},{3,4},{4,5},{5,6},{6,7},{8,9},{9,10},{10,11},{11... | collective-permute-start | bytes 589832 | tf_op jit(solution)/shard_map/ppermute | solution.py:15
  14.0 8.3 %collective-permute-start.1 = (bf16[2,1,128,384]{3,2,1,0:T(8,128)(2,1)S(1)}, bf16[2,1,128,384]{3,2,1,0:T(8,128)(2,1)S(1)}, u32[]{:S(2)}, u32[]{:S(2)}) collective-permute-start(bf16[2,1,128,384]{3,2,1,0:T(8,128)(2,1)S(1)} %get-tuple-element.11), channel_id=1, source_target_pairs={{1,0},{2,1},{3,2},{4,3},{5,4},{6,5},{7,6},{9,8},{10,9},{11,10},{12... | collective-permute-start | bytes 589832 | tf_op jit(solution)/shard_map/ppermute | solution.py:17
  74.4 5.6 %copy-start.1 = (bf16[2,2,128,384]{3,2,1,0:T(8,128)(2,1)S(1)}, bf16[2,2,128,384]{3,2,1,0:T(8,128)(2,1)}, u32[]{:S(2)}) copy-start(bf16[2,2,128,384]{3,2,1,0:T(8,128)(2,1)} %param.12) | copy-start | bytes 1179652
  74.4 5.6 %copy-start.6 = (f32[384]{0:T(512)S(1)}, f32[384]{0:T(512)}, u32[]{:S(2)}) copy-start(f32[384]{0:T(512)} %param.16) | copy-start | bytes 4612
  75.9 5.7 %copy-start.5 = (f32[384]{0:T(512)S(1)}, f32[384]{0:T(512)}, u32[]{:S(2)}) copy-start(f32[384]{0:T(512)} %param.17) | copy-start | bytes 4612
  77.2 28.1 %copy-start.2 = (bf16[384,384]{1,0:T(8,128)(2,1)S(1)}, bf16[384,384]{1,0:T(8,128)(2,1)}, u32[]{:S(2)}) copy-start(bf16[384,384]{1,0:T(8,128)(2,1)} %param.18) | copy-start | bytes 884740
  81.7 11.4 %collective-permute-start.2 = (bf16[2,256,384]{2,1,0:T(8,128)(2,1)S(1)}, bf16[2,256,384]{2,1,0:T(8,128)(2,1)S(1)}, u32[]{:S(2)}, u32[]{:S(2)}) collective-permute-start(bf16[2,256,384]{2,1,0:T(8,128)(2,1)S(1)} %bitcast.303), channel_id=1, source_target_pairs={{0,2},{2,4},{4,6},{6,7},{7,5},{5,3},{3,1},{1,0},{8,10},{10,12},{12... | collective-permute-start | bytes 1179656 | tf_op jit(solution)/shard_map/ppermute | solution.py:33
  83.5 11.3 %collective-permute-start.3 = (bf16[2,256,384]{2,1,0:T(8,128)(2,1)S(1)}, bf16[2,256,384]{2,1,0:T(8,128)(2,1)S(1)}, u32[]{:S(2)}, u32[]{:S(2)}) collective-permute-start(bf16[2,256,384]{2,1,0:T(8,128)(2,1)S(1)} %bitcast.304), channel_id=1, source_target_pairs={{0,1},{2,0},{4,2},{6,4},{7,6},{5,7},{3,5},{1,3},{8,9},{10,8},{12,1... | collective-permute-start | bytes 1179656 | tf_op jit(solution)/shard_map/ppermute | solution.py:36
  93.1 10.5 %collective-permute-start.4 = (bf16[2,256,384]{2,1,0:T(8,128)(2,1)S(1)}, bf16[2,256,384]{2,1,0:T(8,128)(2,1)S(1)}, u32[]{:S(2)}, u32[]{:S(2)}) collective-permute-start(bf16[2,256,384]{2,1,0:T(8,128)(2,1)S(1)} %collective-permute-done.2), channel_id=1, source_target_pairs={{0,2},{2,4},{4,6},{6,7},{7,5},{5,3},{3,1},{1,0},{8,10},{10,12},{12... | collective-permute-start | bytes 1179656 | tf_op jit(solution)/shard_map/ppermute | solution.py:33
  94.8 12.5 %collective-permute-start.5 = (bf16[2,256,384]{2,1,0:T(8,128)(2,1)S(1)}, bf16[2,256,384]{2,1,0:T(8,128)(2,1)S(1)}, u32[]{:S(2)}, u32[]{:S(2)}) collective-permute-start(bf16[2,256,384]{2,1,0:T(8,128)(2,1)S(1)} %collective-permute-done.3), channel_id=1, source_target_pairs={{0,1},{2,0},{4,2},{6,4},{7,6},{5,7},{3,5},{1,3},{8,9},{10,8},{12,1... | collective-permute-start | bytes 1179656 | tf_op jit(solution)/shard_map/ppermute | solution.py:36
  103.6 9.6 %collective-permute-start.6 = (bf16[2,256,384]{2,1,0:T(8,128)(2,1)S(1)}, bf16[2,256,384]{2,1,0:T(8,128)(2,1)S(1)}, u32[]{:S(2)}, u32[]{:S(2)}) collective-permute-start(bf16[2,256,384]{2,1,0:T(8,128)(2,1)S(1)} %collective-permute-done.4), channel_id=1, source_target_pairs={{0,2},{2,4},{4,6},{6,7},{7,5},{5,3},{3,1},{1,0},{8,10},{10,12},{12... | collective-permute-start | bytes 1179656 | tf_op jit(solution)/shard_map/ppermute | solution.py:33
  107.3 10.0 %collective-permute-start.7 = (bf16[2,256,384]{2,1,0:T(8,128)(2,1)S(1)}, bf16[2,256,384]{2,1,0:T(8,128)(2,1)S(1)}, u32[]{:S(2)}, u32[]{:S(2)}) collective-permute-start(bf16[2,256,384]{2,1,0:T(8,128)(2,1)S(1)} %collective-permute-done.5), channel_id=1, source_target_pairs={{0,1},{2,0},{4,2},{6,4},{7,6},{5,7},{3,5},{1,3},{8,9},{10,8},{12,1... | collective-permute-start | bytes 1179656 | tf_op jit(solution)/shard_map/ppermute | solution.py:36
  113.2 8.7 %collective-permute-start.8 = (bf16[2,256,384]{2,1,0:T(8,128)(2,1)S(1)}, bf16[2,256,384]{2,1,0:T(8,128)(2,1)S(1)}, u32[]{:S(2)}, u32[]{:S(2)}) collective-permute-start(bf16[2,256,384]{2,1,0:T(8,128)(2,1)S(1)} %collective-permute-done.6), channel_id=1, source_target_pairs={{0,2},{2,4},{4,6},{6,7},{7,5},{5,3},{3,1},{1,0},{8,10},{10,12},{12... | collective-permute-start | bytes 1179656 | tf_op jit(solution)/shard_map/ppermute | solution.py:33
  129.7 3.1 %copy-start.7 = (bf16[384,384]{1,0:T(8,128)(2,1)S(1)}, bf16[384,384]{1,0:T(8,128)(2,1)}, u32[]{:S(2)}) copy-start(bf16[384,384]{1,0:T(8,128)(2,1)} %param.20) | copy-start | bytes 884740
  132.7 6.4 %copy-start.3 = (bf16[384,384]{1,0:T(8,128)(2,1)S(1)}, bf16[384,384]{1,0:T(8,128)(2,1)}, u32[]{:S(2)}) copy-start(bf16[384,384]{1,0:T(8,128)(2,1)} %param.21) | copy-start | bytes 884740
Sparse Core Ops, SparseCore 0:
  23.4 12.0 all-gather.1

commit v4 on v3

--- a/solution.py
+++ b/solution.py
@@ -70,17 +70,14 @@
     back_two = jnp.where(present_two, back_two, jnp.zeros_like(back_two))
     back_one = jnp.where(present_one, back_one, jnp.zeros_like(back_one))
     window = jnp.stack([back_two, back_one, padded], axis=1)
-    accum = jnp.zeros((span_count, row_count, col_count, channels), jnp.float32)
-    for tap_t in range(3):
-        for tap_y in range(3):
-            for tap_x in range(3):
-                sliced = window[:, tap_t, tap_y : tap_y + row_count, tap_x : tap_x + col_count]
-                accum = accum + jnp.einsum(
-                    "fhwc,cd->fhwd",
-                    sliced,
-                    conv_weight[tap_t, tap_y, tap_x],
-                    preferred_element_type=jnp.float32,
-                )
+    accum = lax.conv_general_dilated(
+        window,
+        conv_weight,
+        window_strides=(1, 1, 1),
+        padding="VALID",
+        dimension_numbers=("NDHWC", "DHWIO", "NDHWC"),
+        preferred_element_type=jnp.float32,
+    )[:, 0]
     mixed = (frames.astype(jnp.float32) + accum + conv_bias).astype(jnp.bfloat16)
     normed = rms_scaled(mixed, gain_attn).astype(jnp.bfloat16)
     tokens = normed.reshape(span_count, row_count * col_count, channels)

time: 148 us -> 123 us (0.83)
  matrix products: 52.2 us -> 20.2 us
  local copies, waits for them, and re-layouts: 12.9 us -> 20.2 us
    dot_general x27 -> x0, matrix products: 38 us -> none  [shards(): jnp.einsum('fhwc,cd->fhwd', sliced, conv_weight[tap_t, tap_y, tap_x], pre...]
    conv_general_dilated x0 -> x1, matrix products: none -> 5.99 us  [shards(): lax.conv_general_dilated(window, conv_weight, window_strides=(1, 1, 1), p...]
    unnamed x23 -> x32, local copies, waits for them, and re-layouts: 5.57 us -> 8.43 us
    conv_general_dilated x0 -> x1, other arithmetic: none -> 2.81 us  [shards(): lax.conv_general_dilated(window, conv_weight, window_strides=(1, 1, 1), p...]
    another operation x1 -> x2, local copies, waits for them, and re-layouts: 1.34 us -> 4.09 us  [shards(): window = jnp.stack([back_two, back_one, padded], axis=1)]
    all_gather x0 -> x1, local copies, waits for them, and re-layouts: none -> 2.62 us  [shards(): gathered = lax.all_gather(rimmed, 'tm', axis=0, tiled=True)]
    another operation x2 -> x3, other arithmetic: 2.68 us -> 0.78 us  [shards(): window = jnp.stack([back_two, back_one, padded], axis=1)]
  transfers between devices with their start and end apart: 10 -> 10, of which waited for: 7 -> 7; matrix products, arithmetic and copies ran while one was open for 5% -> 7% of each run, Pallas kernels for 0% -> 0%
where the time goes in v4:
time: 123 us
  waiting for transfers between devices  42.8 us (35%)
  local copies, waits for them, and re-layouts  20.2 us (16%)
  matrix products  20.2 us (16%)
  starting transfers between devices  14.1 us (11%)
  between operations  13.7 us (11%)
  other arithmetic  11.7 us (10%)
    ppermute x4, waiting for transfers between devices, ring_gather(): forward = lax.ppermute(forward, axis, ahead)  26.3 us
    all_gather x1, waiting for transfers between devices, shards(): gathered = lax.all_gather(rimmed, 'tm', axis=0, tiled=True)  9.54 us
    unnamed x32, local copies, waits for them, and re-layouts  8.43 us
    ppermute x4, starting transfers between devices, ring_gather(): forward = lax.ppermute(forward, axis, ahead)  7.05 us
    dot_general x1, matrix products, shards(): jnp.einsum('fqc,fkc->fqk', queries, keys_all, preferred_element_type=jnp....  7 us
    dot_general x1, matrix products, shards(): jnp.einsum('fqk,fkc->fqc', weights_exp.astype(jnp.bfloat16), values_all,...  6.4 us
    conv_general_dilated x1, matrix products, shards(): lax.conv_general_dilated(window, conv_weight, window_strides=(1, 1, 1), p...  5.99 us
    ppermute x1, starting transfers between devices, padded_2(): lax.ppermute(tail, axis, [(i, (i + 1) % count) for i in range(ends)])  4.88 us
  transfers between devices with their start and end apart: 10, of which 7 were waited for; matrix products, arithmetic and copies ran while one was open for 7% of the time, Pallas kernels for 0%

profile of v4, /device:TPU:0, one launch (start us, length us, event | category | flops | bytes accessed | tf_op | source)
XLA Modules:
  0.0 122.7 jit_solution(2787281488282797866)
XLA Ops:
  6.5 1.2 fusion.24
  7.8 1.3 %fusion.31 = bf16[2,2,128,384]{3,2,1,0:T(8,128)(2,1)S(1)} fusion(bf16[2,2,128,384]{3,2,1,0:T(8,128)(2,1)} %param.12, f32[384]{0:T(512)} %param.14, f32[2,2,128]{2,1,0:T(2,128)S(1)} %add_rsqrt_fusion.1), kind=kLoop, calls=%fused_computation.42 | loop fusion | flops 1572864 | bytes 790016 | tf_op jit(solution)/shard_map/convert_element_type | solution.py:60
  9.1 4.9 %collective-permute-start = (bf16[2,1,128,384]{3,2,1,0:T(8,128)(2,1)S(1)}, bf16[2,1,128,384]{3,2,1,0:T(8,128)(2,1)S(1)}, u32[]{:S(2)}, u32[]{:S(2)}) collective-permute-start(bf16[2,1,128,384]{3,2,1,0:T(8,128)(2,1)S(1)} %get-tuple-element.12), channel_id=1, source_target_pairs={{0,1},{1,2},{2,3},{3,4},{4,5},{5,6},{6,7},{8,9},{9,10},{10,11},{11... | collective-permute-start | bytes 589832 | tf_op jit(solution)/shard_map/ppermute | solution.py:15
  14.0 1.3 %collective-permute-start.1 = (bf16[2,1,128,384]{3,2,1,0:T(8,128)(2,1)S(1)}, bf16[2,1,128,384]{3,2,1,0:T(8,128)(2,1)S(1)}, u32[]{:S(2)}, u32[]{:S(2)}) collective-permute-start(bf16[2,1,128,384]{3,2,1,0:T(8,128)(2,1)S(1)} %get-tuple-element.13), channel_id=1, source_target_pairs={{1,0},{2,1},{3,2},{4,3},{5,4},{6,5},{7,6},{9,8},{10,9},{11,10},{12... | collective-permute-start | bytes 589832 | tf_op jit(solution)/shard_map/ppermute | solution.py:17
  15.3 2.9 %collective-permute-done = bf16[2,1,128,384]{3,2,1,0:T(8,128)(2,1)S(1)} collective-permute-done((bf16[2,1,128,384]{3,2,1,0:T(8,128)(2,1)S(1)}, bf16[2,1,128,384]{3,2,1,0:T(8,128)(2,1)S(1)}, u32[]{:S(2)}, u32[]{:S(2)}) %collective-permute-start) | collective-permute-done | bytes 196640 | tf_op jit(solution)/shard_map/ppermute | solution.py:15
  18.2 4.1 %collective-permute-done.1 = bf16[2,1,128,384]{3,2,1,0:T(8,128)(2,1)S(1)} collective-permute-done((bf16[2,1,128,384]{3,2,1,0:T(8,128)(2,1)S(1)}, bf16[2,1,128,384]{3,2,1,0:T(8,128)(2,1)S(1)}, u32[]{:S(2)}, u32[]{:S(2)}) %collective-permute-start.1) | collective-permute-done | bytes 196640 | tf_op jit(solution)/shard_map/ppermute | solution.py:17
  22.3 1.0 pad_maximum_fusion
  23.3 0.0 all-gather.2.cloned.1.call-update
  23.3 0.2 maximum_reduce_fusion.1
  23.5 0.2 compare_reduce_fusion.1
  23.7 2.2 %pad_bitcast_fusion = bf16[2,1,4,130,384]{4,3,2,0,1:T(8,128)(2,1)} fusion(bf16[2,4,128,384]{3,2,1,0:T(8,128)(2,1)} %pad_maximum_fusion), kind=kLoop, calls=%fused_computation.34 | loop fusion | bytes 1585152 | tf_op jit(solution)/shard_map/stack | solution.py:72
  26.0 9.5 %all-gather.2.cloned.1.call-done = bf16[4,4,128,384]{3,2,1,0:T(8,128)(2,1)} async-done(((bf16[2,4,128,384]{3,2,1,0:T(8,128)(2,1)}), bf16[4,4,128,384]{3,2,1,0:T(8,128)(2,1)}) %all-gather.2.cloned.1.call-update) | async-done | bytes 1572880 | tf_op jit(solution)/shard_map/all_gather | solution.py:62
  35.5 2.6 %copy.43 = bf16[4,4,128,384]{3,1,2,0:T(4,128)(2,1)S(1)} copy(bf16[4,4,128,384]{3,2,1,0:T(8,128)(2,1)} %all-gather.2.cloned.1.call-done) | data formatting | bytes 3145728 | tf_op jit(solution)/shard_map/all_gather | solution.py:62
  38.1 0.6 pad.8
  38.7 1.3 %gather_fusion.1 = bf16[2,4,130,384]{3,1,2,0:T(4,128)(2,1)S(1)} fusion(bf16[4,4,130,384]{3,1,2,0:T(4,128)(2,1)S(1)} %pad.8, s32[1024]{0:T(1024)S(1)} %pad_clamp_fusion), kind=kCustom, calls=%fused_computation.1.clone | custom fusion | bytes 1597448 | tf_op jit(solution)/shard_map/jit(_take)/gather | solution.py:67
  40.1 1.3 %gather_fusion = bf16[2,4,130,384]{3,1,2,0:T(4,128)(2,1)S(1)} fusion(bf16[4,4,130,384]{3,1,2,0:T(4,128)(2,1)S(1)} %pad.8, s32[1024]{0:T(1024)S(1)} %pad_clamp_fusion.1), kind=kCustom, calls=%fused_computation.clone | custom fusion | bytes 1597448 | tf_op jit(solution)/shard_map/jit(_take)/gather | solution.py:66
  41.5 0.2 fusion.21
  41.7 0.2 fusion.23
  41.9 0.7 copy-done.2
  42.6 0.3 maximum_bitcast_fusion
  43.0 0.0 slice-start
  43.0 1.8 %copy.51 = bf16[3,4,2,130,384]{4,2,3,1,0:T(2,128)(2,1)S(1)} copy(bf16[3,4,2,130,384]{4,3,1,2,0:T(8,128)(2,1)S(1)} %maximum_bitcast_fusion) | data formatting | bytes 4792320
  44.8 0.0 slice-start.1
  44.8 1.9 %pad.10.clone = bf16[3,4,2,136,384]{4,2,3,1,0:T(2,128)(2,1)S(1)} pad(bf16[3,4,2,130,384]{4,2,3,1,0:T(2,128)(2,1)S(1)} %copy.51, bf16[]{:T(256)} %constant.14.clone.1), padding=0_0x0_0x0_0x0_6x0_0 | pad | bytes 4902914 | tf_op jit(solution)/shard_map/stack | solution.py:72
  46.7 0.0 copy-start.9
  46.7 0.2 slice.26
  46.9 2.8 %fusion.2 = bf16[3,4,2,8,19,384]{5,2,4,3,1,0:T(2,128)(2,1)S(1)} fusion(bf16[3,4,2,7,2,384]{5,2,4,3,1,0:T(2,128)(2,1)S(1)} %slice.26, bf16[3,4,2,8,17,384]{5,2,4,3,1,0:T(2,128)(2,1)S(1)} %bitcast.47), kind=kLoop, calls=%fused_computation.9 | loop fusion | flops 8404992 | bytes 5566464 | tf_op jit(solution)/shard_map/conv_general_dilated | solution.py:73
  49.7 6.0 %fusion.11 = f32[1,2,16,17,384]{4,2,3,1,0:T(8,128)S(1)} fusion(bf16[3,3,3,384,384]{4,3,2,1,0:T(8,128)(2,1)S(1)} %bitcast.55, bf16[3,4,2,8,19,384]{5,2,4,3,1,0:T(2,128)(2,1)S(1)} %fusion.2, pred[16,17]{0,1:T(8,128)(4,1)S(1)} %copy-done.9), kind=kOutput, calls=%fused_computation.18 | convolution fusion | flops 4331876352 | bytes 11600144 | tf_op jit(solution)/shard_map/conv_general_dilated | solution.py:73
  55.7 0.0 copy-start.1
  55.8 0.0 copy-start.6
  55.8 0.0 copy-start.7
  55.8 0.0 copy-start.3
  55.8 0.4 copy.48
  56.2 0.3 slice.27
  56.5 0.2 copy-done.1
  56.7 0.2 fusion.34
  57.0 0.2 fusion.36
  57.2 1.8 %collective-permute-start.2 = (bf16[2,256,384]{2,1,0:T(8,128)(2,1)S(1)}, bf16[2,256,384]{2,1,0:T(8,128)(2,1)S(1)}, u32[]{:S(2)}, u32[]{:S(2)}) collective-permute-start(bf16[2,256,384]{2,1,0:T(8,128)(2,1)S(1)} %bitcast.48), channel_id=1, source_target_pairs={{0,2},{2,4},{4,6},{6,7},{7,5},{5,3},{3,1},{1,0},{8,10},{10,12},{12... | collective-permute-start | bytes 1179656 | tf_op jit(solution)/shard_map/ppermute | solution.py:33
  59.0 0.3 collective-permute-start.3
  59.2 9.3 %collective-permute-done.2 = bf16[2,256,384]{2,1,0:T(8,128)(2,1)S(1)} collective-permute-done((bf16[2,256,384]{2,1,0:T(8,128)(2,1)S(1)}, bf16[2,256,384]{2,1,0:T(8,128)(2,1)S(1)}, u32[]{:S(2)}, u32[]{:S(2)}) %collective-permute-start.2) | collective-permute-done | bytes 393248 | tf_op jit(solution)/shard_map/ppermute | solution.py:33
  68.5 1.8 %collective-permute-start.4 = (bf16[2,256,384]{2,1,0:T(8,128)(2,1)S(1)}, bf16[2,256,384]{2,1,0:T(8,128)(2,1)S(1)}, u32[]{:S(2)}, u32[]{:S(2)}) collective-permute-start(bf16[2,256,384]{2,1,0:T(8,128)(2,1)S(1)} %collective-permute-done.2), channel_id=1, source_target_pairs={{0,2},{2,4},{4,6},{6,7},{7,5},{5,3},{3,1},{1,0},{8,10},{10,12},{12... | collective-permute-start | bytes 1179656 | tf_op jit(solution)/shard_map/ppermute | solution.py:33
  70.3 0.3 collective-permute-start.5
  70.6 8.5 %collective-permute-done.4 = bf16[2,256,384]{2,1,0:T(8,128)(2,1)S(1)} collective-permute-done((bf16[2,256,384]{2,1,0:T(8,128)(2,1)S(1)}, bf16[2,256,384]{2,1,0:T(8,128)(2,1)S(1)}, u32[]{:S(2)}, u32[]{:S(2)}) %collective-permute-start.4) | collective-permute-done | bytes 393248 | tf_op jit(solution)/shard_map/ppermute | solution.py:33
  79.0 1.8 %collective-permute-start.6 = (bf16[2,256,384]{2,1,0:T(8,128)(2,1)S(1)}, bf16[2,256,384]{2,1,0:T(8,128)(2,1)S(1)}, u32[]{:S(2)}, u32[]{:S(2)}) collective-permute-start(bf16[2,256,384]{2,1,0:T(8,128)(2,1)S(1)} %collective-permute-done.4), channel_id=1, source_target_pairs={{0,2},{2,4},{4,6},{6,7},{7,5},{5,3},{3,1},{1,0},{8,10},{10,12},{12... | collective-permute-start | bytes 1179656 | tf_op jit(solution)/shard_map/ppermute | solution.py:33
  80.8 0.4 convolution_convert_fusion.2
  81.2 0.8 constant_dynamic-update-slice_fusion.7
  82.0 0.8 constant_dynamic-update-slice_fusion.6
  82.8 0.0 collective-permute-done.5
  82.8 0.3 collective-permute-start.7
  83.0 0.8 constant_dynamic-update-slice_fusion.5
  83.8 4.8 %collective-permute-done.6 = bf16[2,256,384]{2,1,0:T(8,128)(2,1)S(1)} collective-permute-done((bf16[2,256,384]{2,1,0:T(8,128)(2,1)S(1)}, bf16[2,256,384]{2,1,0:T(8,128)(2,1)S(1)}, u32[]{:S(2)}, u32[]{:S(2)}) %collective-permute-start.6) | collective-permute-done | bytes 393248 | tf_op jit(solution)/shard_map/ppermute | solution.py:33
  88.6 1.8 %collective-permute-start.8 = (bf16[2,256,384]{2,1,0:T(8,128)(2,1)S(1)}, bf16[2,256,384]{2,1,0:T(8,128)(2,1)S(1)}, u32[]{:S(2)}, u32[]{:S(2)}) collective-permute-start(bf16[2,256,384]{2,1,0:T(8,128)(2,1)S(1)} %collective-permute-done.6), channel_id=1, source_target_pairs={{0,2},{2,4},{4,6},{6,7},{7,5},{5,3},{3,1},{1,0},{8,10},{10,12},{12... | collective-permute-start | bytes 1179656 | tf_op jit(solution)/shard_map/ppermute | solution.py:33
  90.4 0.8 constant_dynamic-update-slice_fusion.4
  91.2 0.8 constant_dynamic-update-slice_fusion.3
  92.0 0.8 constant_dynamic-update-slice_fusion.2
  92.8 0.8 constant_dynamic-update-slice_fusion.1
  93.6 3.7 %collective-permute-done.8 = bf16[2,256,384]{2,1,0:T(8,128)(2,1)S(1)} collective-permute-done((bf16[2,256,384]{2,1,0:T(8,128)(2,1)S(1)}, bf16[2,256,384]{2,1,0:T(8,128)(2,1)S(1)}, u32[]{:S(2)}, u32[]{:S(2)}) %collective-permute-start.8) | collective-permute-done | bytes 393248 | tf_op jit(solution)/shard_map/ppermute | solution.py:33
  97.3 0.8 constant_dynamic-update-slice_fusion
  98.1 7.0 %multiply_reduce_fusion = (f32[2,256]{1,0:T(2,128)S(1)}, f32[2,256,2048]{2,1,0:T(8,128)}) fusion(bf16[2,256,384]{2,1,0:T(8,128)(2,1)S(1)} %convolution_convert_fusion.2, bf16[2,2048,384]{2,1,0:T(8,128)(2,1)} %constant_dynamic-update-slice_fusion, bf16[384,384]{1,0:T(8,128)(2,1)S(1)} %copy-done), kind=kOutput, calls=%fused_computation.4 | convolution fusion | flops 2016935424 | bytes 8030208 | tf_op jit(solution)/shard_map/fqc,fkc->fqk/dot_general | solution.py:96
  105.1 3.0 %fusion = f32[2,256]{1,0:T(2,128)S(1)} fusion(f32[2,256,2048]{2,1,0:T(8,128)} %get-tuple-element.15, f32[2,256]{1,0:T(2,128)S(1)} %get-tuple-element.14), kind=kLoop, calls=%fused_computation.5 | loop fusion | flops 3145216 | bytes 4198400 | tf_op jit(solution)/shard_map/reduce_sum | solution.py:101
  108.2 0.0 copy-start.4
  108.2 6.4 %fusion.17 = bf16[2,256,384]{2,1,0:T(8,128)(2,1)S(1)} fusion(bf16[2,2048,384]{2,1,0:T(8,128)(2,1)} %constant_dynamic-update-slice_fusion, f32[2,256,2048]{2,1,0:T(8,128)} %get-tuple-element.15, f32[2,256]{1,0:T(2,128)S(1)} %get-tuple-element.14, f32[2,256]{1,0:T(2,128)S(1)} %fusion, bf16[384,384]{1,0:T(8,128)(2,1)S(1)} %copy-done.8), kind=kOutput, calls=%fused_computation.27 | convolution fusion | flops 2018377728 | bytes 8032256 | tf_op jit(solution)/shard_map/fqk,fkc->fqc/dot_general | solution.py:102
  114.6 0.4 fusion.38
  115.0 0.8 fusion.37
  (25 shorter events, 0.1 us)
Async XLA Ops:
  6.5 91.6 %copy-start = (bf16[384,384]{1,0:T(8,128)(2,1)S(1)}, bf16[384,384]{1,0:T(8,128)(2,1)}, u32[]{:S(2)}) copy-start(bf16[384,384]{1,0:T(8,128)(2,1)} %param.19) | copy-start | bytes 884740
  6.5 16.8 %copy-start.5 = (s32[2,2]{1,0:T(2,128)S(1)}, s32[2,2]{1,0:T(2,128)}, u32[]{:S(2)}) copy-start(s32[2,2]{1,0:T(2,128)} %param.13) | copy-start | bytes 52
  6.5 29.0 %all-gather.2.cloned.1.call-start = ((), (), s32[]{:S(2)}) async-start(), calls=%async_computation | async-start | bytes 2359296 | tf_op jit(solution)/shard_map/all_gather | solution.py:62
  9.1 9.1 %collective-permute-start = (bf16[2,1,128,384]{3,2,1,0:T(8,128)(2,1)S(1)}, bf16[2,1,128,384]{3,2,1,0:T(8,128)(2,1)S(1)}, u32[]{:S(2)}, u32[]{:S(2)}) collective-permute-start(bf16[2,1,128,384]{3,2,1,0:T(8,128)(2,1)S(1)} %get-tuple-element.12), channel_id=1, source_target_pairs={{0,1},{1,2},{2,3},{3,4},{4,5},{5,6},{6,7},{8,9},{9,10},{10,11},{11... | collective-permute-start | bytes 589832 | tf_op jit(solution)/shard_map/ppermute | solution.py:15
  14.0 8.3 %collective-permute-start.1 = (bf16[2,1,128,384]{3,2,1,0:T(8,128)(2,1)S(1)}, bf16[2,1,128,384]{3,2,1,0:T(8,128)(2,1)S(1)}, u32[]{:S(2)}, u32[]{:S(2)}) collective-permute-start(bf16[2,1,128,384]{3,2,1,0:T(8,128)(2,1)S(1)} %get-tuple-element.13), channel_id=1, source_target_pairs={{1,0},{2,1},{3,2},{4,3},{5,4},{6,5},{7,6},{9,8},{10,9},{11,10},{12... | collective-permute-start | bytes 589832 | tf_op jit(solution)/shard_map/ppermute | solution.py:17
  41.5 1.2 copy-start.2
  43.0 6.8 %slice-start = ((s8[7962624]{0:T(1024)(128)(4,1)}), s8[4194304]{0:T(1024)(128)(4,1)S(1)}, s32[]{:S(2)}) async-start(s8[7962624]{0:T(1024)(128)(4,1)} %bitcast.54), calls=%async_computation.1 | async-start | bytes 8388608
  44.8 4.9 %slice-start.1 = ((s8[7962624]{0:T(1024)(128)(4,1)}), s8[3768320]{0:T(1024)(128)(4,1)S(1)}, s32[]{:S(2)}) async-start(s8[7962624]{0:T(1024)(128)(4,1)} %bitcast.54), calls=%async_computation.2 | async-start | bytes 7536640
  46.7 3.0 %copy-start.9 = (pred[16,17]{0,1:T(8,128)(4,1)S(1)}, pred[16,17]{0,1:T(8,128)(4,1)}, u32[]{:S(2)}) copy-start(pred[16,17]{0,1:T(8,128)(4,1)} %constant.41) | copy-start | bytes 820
  55.7 1.0 copy-start.1
  55.8 1.0 copy-start.6
  55.8 1.2 copy-start.7
  55.8 25.0 %copy-start.3 = (bf16[384,384]{1,0:T(8,128)(2,1)S(1)}, bf16[384,384]{1,0:T(8,128)(2,1)}, u32[]{:S(2)}) copy-start(bf16[384,384]{1,0:T(8,128)(2,1)} %param.18) | copy-start | bytes 884740
  57.2 11.4 %collective-permute-start.2 = (bf16[2,256,384]{2,1,0:T(8,128)(2,1)S(1)}, bf16[2,256,384]{2,1,0:T(8,128)(2,1)S(1)}, u32[]{:S(2)}, u32[]{:S(2)}) collective-permute-start(bf16[2,256,384]{2,1,0:T(8,128)(2,1)S(1)} %bitcast.48), channel_id=1, source_target_pairs={{0,2},{2,4},{4,6},{6,7},{7,5},{5,3},{3,1},{1,0},{8,10},{10,12},{12... | collective-permute-start | bytes 1179656 | tf_op jit(solution)/shard_map/ppermute | solution.py:33
  59.0 11.3 %collective-permute-start.3 = (bf16[2,256,384]{2,1,0:T(8,128)(2,1)S(1)}, bf16[2,256,384]{2,1,0:T(8,128)(2,1)S(1)}, u32[]{:S(2)}, u32[]{:S(2)}) collective-permute-start(bf16[2,256,384]{2,1,0:T(8,128)(2,1)S(1)} %bitcast.49), channel_id=1, source_target_pairs={{0,1},{2,0},{4,2},{6,4},{7,6},{5,7},{3,5},{1,3},{8,9},{10,8},{12,1... | collective-permute-start | bytes 1179656 | tf_op jit(solution)/shard_map/ppermute | solution.py:36
  68.5 10.5 %collective-permute-start.4 = (bf16[2,256,384]{2,1,0:T(8,128)(2,1)S(1)}, bf16[2,256,384]{2,1,0:T(8,128)(2,1)S(1)}, u32[]{:S(2)}, u32[]{:S(2)}) collective-permute-start(bf16[2,256,384]{2,1,0:T(8,128)(2,1)S(1)} %collective-permute-done.2), channel_id=1, source_target_pairs={{0,2},{2,4},{4,6},{6,7},{7,5},{5,3},{3,1},{1,0},{8,10},{10,12},{12... | collective-permute-start | bytes 1179656 | tf_op jit(solution)/shard_map/ppermute | solution.py:33
  70.3 12.5 %collective-permute-start.5 = (bf16[2,256,384]{2,1,0:T(8,128)(2,1)S(1)}, bf16[2,256,384]{2,1,0:T(8,128)(2,1)S(1)}, u32[]{:S(2)}, u32[]{:S(2)}) collective-permute-start(bf16[2,256,384]{2,1,0:T(8,128)(2,1)S(1)} %collective-permute-done.3), channel_id=1, source_target_pairs={{0,1},{2,0},{4,2},{6,4},{7,6},{5,7},{3,5},{1,3},{8,9},{10,8},{12,1... | collective-permute-start | bytes 1179656 | tf_op jit(solution)/shard_map/ppermute | solution.py:36
  79.0 9.6 %collective-permute-start.6 = (bf16[2,256,384]{2,1,0:T(8,128)(2,1)S(1)}, bf16[2,256,384]{2,1,0:T(8,128)(2,1)S(1)}, u32[]{:S(2)}, u32[]{:S(2)}) collective-permute-start(bf16[2,256,384]{2,1,0:T(8,128)(2,1)S(1)} %collective-permute-done.4), channel_id=1, source_target_pairs={{0,2},{2,4},{4,6},{6,7},{7,5},{5,3},{3,1},{1,0},{8,10},{10,12},{12... | collective-permute-start | bytes 1179656 | tf_op jit(solution)/shard_map/ppermute | solution.py:33
  82.8 10.0 %collective-permute-start.7 = (bf16[2,256,384]{2,1,0:T(8,128)(2,1)S(1)}, bf16[2,256,384]{2,1,0:T(8,128)(2,1)S(1)}, u32[]{:S(2)}, u32[]{:S(2)}) collective-permute-start(bf16[2,256,384]{2,1,0:T(8,128)(2,1)S(1)} %collective-permute-done.5), channel_id=1, source_target_pairs={{0,1},{2,0},{4,2},{6,4},{7,6},{5,7},{3,5},{1,3},{8,9},{10,8},{12,1... | collective-permute-start | bytes 1179656 | tf_op jit(solution)/shard_map/ppermute | solution.py:36
  88.6 8.7 %collective-permute-start.8 = (bf16[2,256,384]{2,1,0:T(8,128)(2,1)S(1)}, bf16[2,256,384]{2,1,0:T(8,128)(2,1)S(1)}, u32[]{:S(2)}, u32[]{:S(2)}) collective-permute-start(bf16[2,256,384]{2,1,0:T(8,128)(2,1)S(1)} %collective-permute-done.6), channel_id=1, source_target_pairs={{0,2},{2,4},{4,6},{6,7},{7,5},{5,3},{3,1},{1,0},{8,10},{10,12},{12... | collective-permute-start | bytes 1179656 | tf_op jit(solution)/shard_map/ppermute | solution.py:33
  105.1 3.1 %copy-start.8 = (bf16[384,384]{1,0:T(8,128)(2,1)S(1)}, bf16[384,384]{1,0:T(8,128)(2,1)}, u32[]{:S(2)}) copy-start(bf16[384,384]{1,0:T(8,128)(2,1)} %param.20) | copy-start | bytes 884740
  108.2 6.4 %copy-start.4 = (bf16[384,384]{1,0:T(8,128)(2,1)S(1)}, bf16[384,384]{1,0:T(8,128)(2,1)}, u32[]{:S(2)}) copy-start(bf16[384,384]{1,0:T(8,128)(2,1)} %param.21) | copy-start | bytes 884740
Sparse Core Ops, SparseCore 0:
  23.4 12.0 all-gather.1

commit v5 on v4

--- a/solution.py
+++ b/solution.py
@@ -29,12 +29,17 @@
     pieces = [block]
     forward = block
     backward = block
-    for step in range(count // 2):
+    for step in range((count - 1) // 2):
         forward = lax.ppermute(forward, axis, ahead)
-        pieces.append(forward)
-        if len(pieces) < count:
-            backward = lax.ppermute(backward, axis, behind)
-            pieces.append(backward)
+        backward = lax.ppermute(backward, axis, behind)
+        pieces += [forward, backward]
+    if count % 2 == 0 and count > 1:
+        half = block.shape[dim] // 2
+        front = lax.ppermute(lax.slice_in_dim(forward, 0, half, axis=dim), axis, ahead)
+        back = lax.ppermute(
+            lax.slice_in_dim(backward, half, block.shape[dim], axis=dim), axis, behind
+        )
+        pieces += [front, back]
     return jnp.concatenate(pieces, axis=dim)
 
 

time: 123 us -> 122 us (level)
  waiting for transfers between devices: 42.8 us -> 40.5 us
    ppermute x4 -> x3, waiting for transfers between devices: 26.3 us -> 20.9 us  [ring_gather(): forward = lax.ppermute(forward, axis, ahead)]
    ppermute x0 -> x2, waiting for transfers between devices: none -> 3.05 us  [the longest x1 1.71 us: ring_gather(): lax.ppermute(lax.slice_in_dim(forward, 0, half, axis=dim), axis, ahead)]
    ppermute x0 -> x2, starting transfers between devices: none -> 2.35 us  [the longest x1 1.81 us: ring_gather(): lax.ppermute(lax.slice_in_dim(forward, 0, half, axis=dim), axis, ahead)]
    ppermute x4 -> x3, starting transfers between devices: 7.05 us -> 5.3 us  [ring_gather(): forward = lax.ppermute(forward, axis, ahead)]
    unnamed x32 -> x33, local copies, waits for them, and re-layouts: 8.43 us -> 9.18 us
  transfers between devices with their start and end apart: 10 -> 11, of which waited for: 7 -> 8; matrix products, arithmetic and copies ran while one was open for 7% -> 8% of each run, Pallas kernels for 0% -> 0%
where the time goes in v5:
time: 122 us
  waiting for transfers between devices  40.5 us (33%)
  local copies, waits for them, and re-layouts  20.9 us (17%)
  matrix products  20.2 us (17%)
  starting transfers between devices  14.7 us (12%)
  between operations  13.8 us (11%)
  other arithmetic  11.7 us (10%)
    ppermute x3, waiting for transfers between devices, ring_gather(): forward = lax.ppermute(forward, axis, ahead)  20.9 us
    all_gather x1, waiting for transfers between devices, shards(): gathered = lax.all_gather(rimmed, 'tm', axis=0, tiled=True)  9.55 us
    unnamed x33, local copies, waits for them, and re-layouts  9.18 us
    dot_general x1, matrix products, shards(): jnp.einsum('fqc,fkc->fqk', queries, keys_all, preferred_element_type=jnp....  7 us
    dot_general x1, matrix products, shards(): jnp.einsum('fqk,fkc->fqc', weights_exp.astype(jnp.bfloat16), values_all,...  6.39 us
    conv_general_dilated x1, matrix products, shards(): lax.conv_general_dilated(window, conv_weight, window_strides=(1, 1, 1), p...  5.99 us
    ppermute x3, starting transfers between devices, ring_gather(): forward = lax.ppermute(forward, axis, ahead)  5.3 us
    ppermute x1, starting transfers between devices, padded_2(): lax.ppermute(tail, axis, [(i, (i + 1) % count) for i in range(ends)])  4.88 us
  transfers between devices with their start and end apart: 11, of which 8 were waited for; matrix products, arithmetic and copies ran while one was open for 8% of the time, Pallas kernels for 0%

profile of v5, /device:TPU:0, one launch (start us, length us, event | category | flops | bytes accessed | tf_op | source)
XLA Modules:
  0.0 121.7 jit_solution(383259964494615124)
XLA Ops:
  6.5 1.2 fusion.24
  7.8 1.3 %fusion.31 = bf16[2,2,128,384]{3,2,1,0:T(8,128)(2,1)S(1)} fusion(bf16[2,2,128,384]{3,2,1,0:T(8,128)(2,1)} %param.12, f32[384]{0:T(512)} %param.14, f32[2,2,128]{2,1,0:T(2,128)S(1)} %add_rsqrt_fusion.1), kind=kLoop, calls=%fused_computation.42 | loop fusion | flops 1572864 | bytes 790016 | tf_op jit(solution)/shard_map/convert_element_type | solution.py:65
  9.1 4.9 %collective-permute-start = (bf16[2,1,128,384]{3,2,1,0:T(8,128)(2,1)S(1)}, bf16[2,1,128,384]{3,2,1,0:T(8,128)(2,1)S(1)}, u32[]{:S(2)}, u32[]{:S(2)}) collective-permute-start(bf16[2,1,128,384]{3,2,1,0:T(8,128)(2,1)S(1)} %get-tuple-element.12), channel_id=1, source_target_pairs={{0,1},{1,2},{2,3},{3,4},{4,5},{5,6},{6,7},{8,9},{9,10},{10,11},{11... | collective-permute-start | bytes 589832 | tf_op jit(solution)/shard_map/ppermute | solution.py:15
  14.0 1.3 %collective-permute-start.1 = (bf16[2,1,128,384]{3,2,1,0:T(8,128)(2,1)S(1)}, bf16[2,1,128,384]{3,2,1,0:T(8,128)(2,1)S(1)}, u32[]{:S(2)}, u32[]{:S(2)}) collective-permute-start(bf16[2,1,128,384]{3,2,1,0:T(8,128)(2,1)S(1)} %get-tuple-element.13), channel_id=1, source_target_pairs={{1,0},{2,1},{3,2},{4,3},{5,4},{6,5},{7,6},{9,8},{10,9},{11,10},{12... | collective-permute-start | bytes 589832 | tf_op jit(solution)/shard_map/ppermute | solution.py:17
  15.3 2.9 %collective-permute-done = bf16[2,1,128,384]{3,2,1,0:T(8,128)(2,1)S(1)} collective-permute-done((bf16[2,1,128,384]{3,2,1,0:T(8,128)(2,1)S(1)}, bf16[2,1,128,384]{3,2,1,0:T(8,128)(2,1)S(1)}, u32[]{:S(2)}, u32[]{:S(2)}) %collective-permute-start) | collective-permute-done | bytes 196640 | tf_op jit(solution)/shard_map/ppermute | solution.py:15
  18.2 4.1 %collective-permute-done.1 = bf16[2,1,128,384]{3,2,1,0:T(8,128)(2,1)S(1)} collective-permute-done((bf16[2,1,128,384]{3,2,1,0:T(8,128)(2,1)S(1)}, bf16[2,1,128,384]{3,2,1,0:T(8,128)(2,1)S(1)}, u32[]{:S(2)}, u32[]{:S(2)}) %collective-permute-start.1) | collective-permute-done | bytes 196640 | tf_op jit(solution)/shard_map/ppermute | solution.py:17
  22.3 1.0 pad_maximum_fusion
  23.3 0.0 all-gather.2.cloned.1.call-update
  23.3 0.2 maximum_reduce_fusion.1
  23.5 0.2 compare_reduce_fusion.1
  23.7 2.2 %pad_bitcast_fusion = bf16[2,1,4,130,384]{4,3,2,0,1:T(8,128)(2,1)} fusion(bf16[2,4,128,384]{3,2,1,0:T(8,128)(2,1)} %pad_maximum_fusion), kind=kLoop, calls=%fused_computation.34 | loop fusion | bytes 1585152 | tf_op jit(solution)/shard_map/stack | solution.py:77
  25.9 9.5 %all-gather.2.cloned.1.call-done = bf16[4,4,128,384]{3,2,1,0:T(8,128)(2,1)} async-done(((bf16[2,4,128,384]{3,2,1,0:T(8,128)(2,1)}), bf16[4,4,128,384]{3,2,1,0:T(8,128)(2,1)}) %all-gather.2.cloned.1.call-update) | async-done | bytes 1572880 | tf_op jit(solution)/shard_map/all_gather | solution.py:67
  35.5 2.6 %copy.43 = bf16[4,4,128,384]{3,1,2,0:T(4,128)(2,1)S(1)} copy(bf16[4,4,128,384]{3,2,1,0:T(8,128)(2,1)} %all-gather.2.cloned.1.call-done) | data formatting | bytes 3145728 | tf_op jit(solution)/shard_map/all_gather | solution.py:67
  38.1 0.6 pad.8
  38.7 1.3 %gather_fusion.1 = bf16[2,4,130,384]{3,1,2,0:T(4,128)(2,1)S(1)} fusion(bf16[4,4,130,384]{3,1,2,0:T(4,128)(2,1)S(1)} %pad.8, s32[1024]{0:T(1024)S(1)} %pad_clamp_fusion), kind=kCustom, calls=%fused_computation.1.clone | custom fusion | bytes 1597448 | tf_op jit(solution)/shard_map/jit(_take)/gather | solution.py:72
  40.1 1.3 %gather_fusion = bf16[2,4,130,384]{3,1,2,0:T(4,128)(2,1)S(1)} fusion(bf16[4,4,130,384]{3,1,2,0:T(4,128)(2,1)S(1)} %pad.8, s32[1024]{0:T(1024)S(1)} %pad_clamp_fusion.1), kind=kCustom, calls=%fused_computation.clone | custom fusion | bytes 1597448 | tf_op jit(solution)/shard_map/jit(_take)/gather | solution.py:71
  41.5 0.2 fusion.21
  41.7 0.2 fusion.23
  41.9 0.7 copy-done.2
  42.6 0.3 maximum_bitcast_fusion
  42.9 0.0 slice-start
  43.0 1.8 %copy.51 = bf16[3,4,2,130,384]{4,2,3,1,0:T(2,128)(2,1)S(1)} copy(bf16[3,4,2,130,384]{4,3,1,2,0:T(8,128)(2,1)S(1)} %maximum_bitcast_fusion) | data formatting | bytes 4792320
  44.8 0.0 slice-start.1
  44.8 1.9 %pad.10.clone = bf16[3,4,2,136,384]{4,2,3,1,0:T(2,128)(2,1)S(1)} pad(bf16[3,4,2,130,384]{4,2,3,1,0:T(2,128)(2,1)S(1)} %copy.51, bf16[]{:T(256)} %constant.14.clone.1), padding=0_0x0_0x0_0x0_6x0_0 | pad | bytes 4902914 | tf_op jit(solution)/shard_map/stack | solution.py:77
  46.7 0.0 copy-start.9
  46.7 0.2 slice.34
  46.9 2.8 %fusion.2 = bf16[3,4,2,8,19,384]{5,2,4,3,1,0:T(2,128)(2,1)S(1)} fusion(bf16[3,4,2,7,2,384]{5,2,4,3,1,0:T(2,128)(2,1)S(1)} %slice.34, bf16[3,4,2,8,17,384]{5,2,4,3,1,0:T(2,128)(2,1)S(1)} %bitcast.47), kind=kLoop, calls=%fused_computation.9 | loop fusion | flops 8404992 | bytes 5566464 | tf_op jit(solution)/shard_map/conv_general_dilated | solution.py:78
  49.7 6.0 %fusion.11 = f32[1,2,16,17,384]{4,2,3,1,0:T(8,128)S(1)} fusion(bf16[3,3,3,384,384]{4,3,2,1,0:T(8,128)(2,1)S(1)} %bitcast.55, bf16[3,4,2,8,19,384]{5,2,4,3,1,0:T(2,128)(2,1)S(1)} %fusion.2, pred[16,17]{0,1:T(8,128)(4,1)S(1)} %copy-done.9), kind=kOutput, calls=%fused_computation.18 | convolution fusion | flops 4331876352 | bytes 11600144 | tf_op jit(solution)/shard_map/conv_general_dilated | solution.py:78
  55.7 0.0 copy-start.1
  55.8 0.0 copy-start.6
  55.8 0.0 copy-start.3
  55.8 0.4 copy.48
  56.2 0.3 slice.35
  56.5 0.2 copy-done.1
  56.7 0.2 fusion.34
  57.0 0.2 fusion.36
  57.2 1.8 %collective-permute-start.2 = (bf16[2,256,384]{2,1,0:T(8,128)(2,1)S(1)}, bf16[2,256,384]{2,1,0:T(8,128)(2,1)S(1)}, u32[]{:S(2)}, u32[]{:S(2)}) collective-permute-start(bf16[2,256,384]{2,1,0:T(8,128)(2,1)S(1)} %bitcast.48), channel_id=1, source_target_pairs={{0,2},{2,4},{4,6},{6,7},{7,5},{5,3},{3,1},{1,0},{8,10},{10,12},{12... | collective-permute-start | bytes 1179656 | tf_op jit(solution)/shard_map/ppermute | solution.py:33
  59.0 0.3 collective-permute-start.3
  59.2 9.3 %collective-permute-done.2 = bf16[2,256,384]{2,1,0:T(8,128)(2,1)S(1)} collective-permute-done((bf16[2,256,384]{2,1,0:T(8,128)(2,1)S(1)}, bf16[2,256,384]{2,1,0:T(8,128)(2,1)S(1)}, u32[]{:S(2)}, u32[]{:S(2)}) %collective-permute-start.2) | collective-permute-done | bytes 393248 | tf_op jit(solution)/shard_map/ppermute | solution.py:33
  68.5 1.8 %collective-permute-start.4 = (bf16[2,256,384]{2,1,0:T(8,128)(2,1)S(1)}, bf16[2,256,384]{2,1,0:T(8,128)(2,1)S(1)}, u32[]{:S(2)}, u32[]{:S(2)}) collective-permute-start(bf16[2,256,384]{2,1,0:T(8,128)(2,1)S(1)} %collective-permute-done.2), channel_id=1, source_target_pairs={{0,2},{2,4},{4,6},{6,7},{7,5},{5,3},{3,1},{1,0},{8,10},{10,12},{12... | collective-permute-start | bytes 1179656 | tf_op jit(solution)/shard_map/ppermute | solution.py:33
  70.3 0.3 collective-permute-start.5
  70.6 0.8 constant_dynamic-update-slice_fusion.8
  71.3 0.4 convolution_convert_fusion.2
  71.7 7.3 %collective-permute-done.4 = bf16[2,256,384]{2,1,0:T(8,128)(2,1)S(1)} collective-permute-done((bf16[2,256,384]{2,1,0:T(8,128)(2,1)S(1)}, bf16[2,256,384]{2,1,0:T(8,128)(2,1)S(1)}, u32[]{:S(2)}, u32[]{:S(2)}) %collective-permute-start.4) | collective-permute-done | bytes 393248 | tf_op jit(solution)/shard_map/ppermute | solution.py:33
  79.0 1.8 %collective-permute-start.6 = (bf16[2,256,384]{2,1,0:T(8,128)(2,1)S(1)}, bf16[2,256,384]{2,1,0:T(8,128)(2,1)S(1)}, u32[]{:S(2)}, u32[]{:S(2)}) collective-permute-start(bf16[2,256,384]{2,1,0:T(8,128)(2,1)S(1)} %collective-permute-done.4), channel_id=1, source_target_pairs={{0,2},{2,4},{4,6},{6,7},{7,5},{5,3},{3,1},{1,0},{8,10},{10,12},{12... | collective-permute-start | bytes 1179656 | tf_op jit(solution)/shard_map/ppermute | solution.py:33
  80.8 0.3 collective-permute-start.7
  81.1 0.8 constant_dynamic-update-slice_fusion.7
  81.9 0.8 constant_dynamic-update-slice_fusion.6
  82.7 0.8 constant_dynamic-update-slice_fusion.5
  83.4 0.8 constant_dynamic-update-slice_fusion.4
  84.3 4.4 %collective-permute-done.6 = bf16[2,256,384]{2,1,0:T(8,128)(2,1)S(1)} collective-permute-done((bf16[2,256,384]{2,1,0:T(8,128)(2,1)S(1)}, bf16[2,256,384]{2,1,0:T(8,128)(2,1)S(1)}, u32[]{:S(2)}, u32[]{:S(2)}) %collective-permute-start.6) | collective-permute-done | bytes 393248 | tf_op jit(solution)/shard_map/ppermute | solution.py:33
  88.7 1.8 %collective-permute-start.8 = (bf16[2,128,384]{2,1,0:T(8,128)(2,1)S(1)}, bf16[2,128,384]{2,1,0:T(8,128)(2,1)S(1)}, u32[]{:S(2)}, u32[]{:S(2)}) collective-permute-start(bf16[2,128,384]{2,1,0:T(8,128)(2,1)S(1)} %slice.36), channel_id=1, source_target_pairs={{0,2},{2,4},{4,6},{6,7},{7,5},{5,3},{3,1},{1,0},{8,10},{10,12},{12... | collective-permute-start | bytes 589832 | tf_op jit(solution)/shard_map/ppermute | solution.py:38
  90.5 0.5 collective-permute-start.9
  91.0 0.8 constant_dynamic-update-slice_fusion.3
  91.8 0.8 constant_dynamic-update-slice_fusion.2
  92.7 1.7 %collective-permute-done.8 = bf16[2,128,384]{2,1,0:T(8,128)(2,1)S(1)} collective-permute-done((bf16[2,128,384]{2,1,0:T(8,128)(2,1)S(1)}, bf16[2,128,384]{2,1,0:T(8,128)(2,1)S(1)}, u32[]{:S(2)}, u32[]{:S(2)}) %collective-permute-start.8) | collective-permute-done | bytes 196640 | tf_op jit(solution)/shard_map/ppermute | solution.py:38
  94.4 0.7 constant_dynamic-update-slice_fusion.1
  95.1 1.3 %collective-permute-done.9 = bf16[2,128,384]{2,1,0:T(8,128)(2,1)S(1)} collective-permute-done((bf16[2,128,384]{2,1,0:T(8,128)(2,1)S(1)}, bf16[2,128,384]{2,1,0:T(8,128)(2,1)S(1)}, u32[]{:S(2)}, u32[]{:S(2)}) %collective-permute-start.9) | collective-permute-done | bytes 196640 | tf_op jit(solution)/shard_map/ppermute | solution.py:39
  96.4 0.7 constant_dynamic-update-slice_fusion
  97.1 7.0 %multiply_reduce_fusion = (f32[2,256]{1,0:T(2,128)S(1)}, f32[2,256,2048]{2,1,0:T(8,128)}) fusion(bf16[2,256,384]{2,1,0:T(8,128)(2,1)S(1)} %convolution_convert_fusion.2, bf16[2,2048,384]{2,1,0:T(8,128)(2,1)} %constant_dynamic-update-slice_fusion, bf16[384,384]{1,0:T(8,128)(2,1)S(1)} %copy-done), kind=kOutput, calls=%fused_computation.4 | convolution fusion | flops 2016935424 | bytes 8030208 | tf_op jit(solution)/shard_map/fqc,fkc->fqk/dot_general | solution.py:101
  104.2 3.0 %fusion = f32[2,256]{1,0:T(2,128)S(1)} fusion(f32[2,256,2048]{2,1,0:T(8,128)} %get-tuple-element.15, f32[2,256]{1,0:T(2,128)S(1)} %get-tuple-element.14), kind=kLoop, calls=%fused_computation.5 | loop fusion | flops 3145216 | bytes 4198400 | tf_op jit(solution)/shard_map/reduce_sum | solution.py:106
  107.2 6.4 %fusion.17 = bf16[2,256,384]{2,1,0:T(8,128)(2,1)S(1)} fusion(bf16[2,2048,384]{2,1,0:T(8,128)(2,1)} %constant_dynamic-update-slice_fusion, f32[2,256,2048]{2,1,0:T(8,128)} %get-tuple-element.15, f32[2,256]{1,0:T(2,128)S(1)} %get-tuple-element.14, f32[2,256]{1,0:T(2,128)S(1)} %fusion, bf16[384,384]{1,0:T(8,128)(2,1)S(1)} %copy-done.8), kind=kOutput, calls=%fused_computation.27 | convolution fusion | flops 2018377728 | bytes 8032256 | tf_op jit(solution)/shard_map/fqk,fkc->fqc/dot_general | solution.py:107
  113.6 0.4 fusion.38
  114.0 0.8 fusion.37
  (30 shorter events, 0.2 us)
Async XLA Ops:
  6.5 90.6 %copy-start = (bf16[384,384]{1,0:T(8,128)(2,1)S(1)}, bf16[384,384]{1,0:T(8,128)(2,1)}, u32[]{:S(2)}) copy-start(bf16[384,384]{1,0:T(8,128)(2,1)} %param.19) | copy-start | bytes 884740
  6.5 16.8 %copy-start.5 = (s32[2,2]{1,0:T(2,128)S(1)}, s32[2,2]{1,0:T(2,128)}, u32[]{:S(2)}) copy-start(s32[2,2]{1,0:T(2,128)} %param.13) | copy-start | bytes 52
  6.5 29.0 %all-gather.2.cloned.1.call-start = ((), (), s32[]{:S(2)}) async-start(), calls=%async_computation | async-start | bytes 2359296 | tf_op jit(solution)/shard_map/all_gather | solution.py:67
  9.1 9.1 %collective-permute-start = (bf16[2,1,128,384]{3,2,1,0:T(8,128)(2,1)S(1)}, bf16[2,1,128,384]{3,2,1,0:T(8,128)(2,1)S(1)}, u32[]{:S(2)}, u32[]{:S(2)}) collective-permute-start(bf16[2,1,128,384]{3,2,1,0:T(8,128)(2,1)S(1)} %get-tuple-element.12), channel_id=1, source_target_pairs={{0,1},{1,2},{2,3},{3,4},{4,5},{5,6},{6,7},{8,9},{9,10},{10,11},{11... | collective-permute-start | bytes 589832 | tf_op jit(solution)/shard_map/ppermute | solution.py:15
  14.0 8.3 %collective-permute-start.1 = (bf16[2,1,128,384]{3,2,1,0:T(8,128)(2,1)S(1)}, bf16[2,1,128,384]{3,2,1,0:T(8,128)(2,1)S(1)}, u32[]{:S(2)}, u32[]{:S(2)}) collective-permute-start(bf16[2,1,128,384]{3,2,1,0:T(8,128)(2,1)S(1)} %get-tuple-element.13), channel_id=1, source_target_pairs={{1,0},{2,1},{3,2},{4,3},{5,4},{6,5},{7,6},{9,8},{10,9},{11,10},{12... | collective-permute-start | bytes 589832 | tf_op jit(solution)/shard_map/ppermute | solution.py:17
  41.4 1.2 copy-start.2
  42.9 6.8 %slice-start = ((s8[7962624]{0:T(1024)(128)(4,1)}), s8[4194304]{0:T(1024)(128)(4,1)S(1)}, s32[]{:S(2)}) async-start(s8[7962624]{0:T(1024)(128)(4,1)} %bitcast.54), calls=%async_computation.1 | async-start | bytes 8388608
  44.8 4.9 %slice-start.1 = ((s8[7962624]{0:T(1024)(128)(4,1)}), s8[3768320]{0:T(1024)(128)(4,1)S(1)}, s32[]{:S(2)}) async-start(s8[7962624]{0:T(1024)(128)(4,1)} %bitcast.54), calls=%async_computation.2 | async-start | bytes 7536640
  46.7 3.0 %copy-start.9 = (pred[16,17]{0,1:T(8,128)(4,1)S(1)}, pred[16,17]{0,1:T(8,128)(4,1)}, u32[]{:S(2)}) copy-start(pred[16,17]{0,1:T(8,128)(4,1)} %constant.41) | copy-start | bytes 820
  55.7 1.0 copy-start.1
  55.8 1.0 copy-start.6
  55.8 1.2 copy-start.7
  55.8 15.6 %copy-start.3 = (bf16[384,384]{1,0:T(8,128)(2,1)S(1)}, bf16[384,384]{1,0:T(8,128)(2,1)}, u32[]{:S(2)}) copy-start(bf16[384,384]{1,0:T(8,128)(2,1)} %param.18) | copy-start | bytes 884740
  57.2 11.4 %collective-permute-start.2 = (bf16[2,256,384]{2,1,0:T(8,128)(2,1)S(1)}, bf16[2,256,384]{2,1,0:T(8,128)(2,1)S(1)}, u32[]{:S(2)}, u32[]{:S(2)}) collective-permute-start(bf16[2,256,384]{2,1,0:T(8,128)(2,1)S(1)} %bitcast.48), channel_id=1, source_target_pairs={{0,2},{2,4},{4,6},{6,7},{7,5},{5,3},{3,1},{1,0},{8,10},{10,12},{12... | collective-permute-start | bytes 1179656 | tf_op jit(solution)/shard_map/ppermute | solution.py:33
  59.0 11.3 %collective-permute-start.3 = (bf16[2,256,384]{2,1,0:T(8,128)(2,1)S(1)}, bf16[2,256,384]{2,1,0:T(8,128)(2,1)S(1)}, u32[]{:S(2)}, u32[]{:S(2)}) collective-permute-start(bf16[2,256,384]{2,1,0:T(8,128)(2,1)S(1)} %bitcast.49), channel_id=1, source_target_pairs={{0,1},{2,0},{4,2},{6,4},{7,6},{5,7},{3,5},{1,3},{8,9},{10,8},{12,1... | collective-permute-start | bytes 1179656 | tf_op jit(solution)/shard_map/ppermute | solution.py:34
  68.5 10.5 %collective-permute-start.4 = (bf16[2,256,384]{2,1,0:T(8,128)(2,1)S(1)}, bf16[2,256,384]{2,1,0:T(8,128)(2,1)S(1)}, u32[]{:S(2)}, u32[]{:S(2)}) collective-permute-start(bf16[2,256,384]{2,1,0:T(8,128)(2,1)S(1)} %collective-permute-done.2), channel_id=1, source_target_pairs={{0,2},{2,4},{4,6},{6,7},{7,5},{5,3},{3,1},{1,0},{8,10},{10,12},{12... | collective-permute-start | bytes 1179656 | tf_op jit(solution)/shard_map/ppermute | solution.py:33
  70.3 10.5 %collective-permute-start.5 = (bf16[2,256,384]{2,1,0:T(8,128)(2,1)S(1)}, bf16[2,256,384]{2,1,0:T(8,128)(2,1)S(1)}, u32[]{:S(2)}, u32[]{:S(2)}) collective-permute-start(bf16[2,256,384]{2,1,0:T(8,128)(2,1)S(1)} %collective-permute-done.3), channel_id=1, source_target_pairs={{0,1},{2,0},{4,2},{6,4},{7,6},{5,7},{3,5},{1,3},{8,9},{10,8},{12,1... | collective-permute-start | bytes 1179656 | tf_op jit(solution)/shard_map/ppermute | solution.py:34
  79.0 9.6 %collective-permute-start.6 = (bf16[2,256,384]{2,1,0:T(8,128)(2,1)S(1)}, bf16[2,256,384]{2,1,0:T(8,128)(2,1)S(1)}, u32[]{:S(2)}, u32[]{:S(2)}) collective-permute-start(bf16[2,256,384]{2,1,0:T(8,128)(2,1)S(1)} %collective-permute-done.4), channel_id=1, source_target_pairs={{0,2},{2,4},{4,6},{6,7},{7,5},{5,3},{3,1},{1,0},{8,10},{10,12},{12... | collective-permute-start | bytes 1179656 | tf_op jit(solution)/shard_map/ppermute | solution.py:33
  80.8 9.7 %collective-permute-start.7 = (bf16[2,256,384]{2,1,0:T(8,128)(2,1)S(1)}, bf16[2,256,384]{2,1,0:T(8,128)(2,1)S(1)}, u32[]{:S(2)}, u32[]{:S(2)}) collective-permute-start(bf16[2,256,384]{2,1,0:T(8,128)(2,1)S(1)} %collective-permute-done.5), channel_id=1, source_target_pairs={{0,1},{2,0},{4,2},{6,4},{7,6},{5,7},{3,5},{1,3},{8,9},{10,8},{12,1... | collective-permute-start | bytes 1179656 | tf_op jit(solution)/shard_map/ppermute | solution.py:34
  88.7 5.7 %collective-permute-start.8 = (bf16[2,128,384]{2,1,0:T(8,128)(2,1)S(1)}, bf16[2,128,384]{2,1,0:T(8,128)(2,1)S(1)}, u32[]{:S(2)}, u32[]{:S(2)}) collective-permute-start(bf16[2,128,384]{2,1,0:T(8,128)(2,1)S(1)} %slice.36), channel_id=1, source_target_pairs={{0,2},{2,4},{4,6},{6,7},{7,5},{5,3},{3,1},{1,0},{8,10},{10,12},{12... | collective-permute-start | bytes 589832 | tf_op jit(solution)/shard_map/ppermute | solution.py:38
  90.5 5.9 %collective-permute-start.9 = (bf16[2,128,384]{2,1,0:T(8,128)(2,1)S(1)}, bf16[2,128,384]{2,1,0:T(8,128)(2,1)S(1)}, u32[]{:S(2)}, u32[]{:S(2)}) collective-permute-start(bf16[2,128,384]{2,1,0:T(8,128)(2,1)S(1)} %slice.37), channel_id=1, source_target_pairs={{0,1},{2,0},{4,2},{6,4},{7,6},{5,7},{3,5},{1,3},{8,9},{10,8},{12,1... | collective-permute-start | bytes 589832 | tf_op jit(solution)/shard_map/ppermute | solution.py:39
  104.1 3.1 %copy-start.8 = (bf16[384,384]{1,0:T(8,128)(2,1)S(1)}, bf16[384,384]{1,0:T(8,128)(2,1)}, u32[]{:S(2)}) copy-start(bf16[384,384]{1,0:T(8,128)(2,1)} %param.20) | copy-start | bytes 884740
  107.2 6.4 %copy-start.4 = (bf16[384,384]{1,0:T(8,128)(2,1)S(1)}, bf16[384,384]{1,0:T(8,128)(2,1)}, u32[]{:S(2)}) copy-start(bf16[384,384]{1,0:T(8,128)(2,1)} %param.21) | copy-start | bytes 884740
Sparse Core Ops, SparseCore 0:
  23.4 12.0 all-gather.1

commit v6 on v5

--- a/solution.py
+++ b/solution.py
@@ -63,18 +63,28 @@
 ):
     span_count, row_count, col_count, channels = frames.shape
     activated = jax.nn.silu(rms_scaled(frames, gain_conv)).astype(jnp.bfloat16)
+    activated = jnp.pad(activated, ((0, 0), (0, 0), (1, 1), (0, 0)))
     rimmed = padded_2(activated, (("height", 1),), 1)
-    gathered = lax.all_gather(rimmed, "tm", axis=0, tiled=True)
-    border = ((0, 0), (0, 0), (1, 1), (0, 0))
-    padded = jnp.pad(rimmed, border)
-    gathered = jnp.pad(gathered, border)
-    back_two = jnp.take(gathered, jnp.maximum(earlier[:, 0], 0), axis=0)
-    back_one = jnp.take(gathered, jnp.maximum(earlier[:, 1], 0), axis=0)
-    present_two = (earlier[:, 0] >= 0)[:, None, None, None]
-    present_one = (earlier[:, 1] >= 0)[:, None, None, None]
-    back_two = jnp.where(present_two, back_two, jnp.zeros_like(back_two))
-    back_one = jnp.where(present_one, back_one, jnp.zeros_like(back_one))
-    window = jnp.stack([back_two, back_one, padded], axis=1)
+    ways = lax.axis_size("tm")
+    mine = lax.axis_index("tm")
+    pieces = [rimmed]
+    for shift in range(1, ways):
+        pieces.append(
+            lax.ppermute(rimmed, "tm", [(i, (i + shift) % ways) for i in range(ways)])
+        )
+    pieces.append(jnp.zeros_like(rimmed[:1]))
+    pool = jnp.concatenate(pieces, axis=0)
+    blank = ways * span_count
+
+    def slot(index):
+        place = ((mine - index // span_count) % ways) * span_count + index % span_count
+        return jnp.where(index >= 0, place, blank)
+
+    own = jnp.arange(span_count, dtype=earlier.dtype)
+    picks = jnp.stack([slot(earlier[:, 0]), slot(earlier[:, 1]), own], axis=1)
+    window = jnp.take(pool, picks.reshape(-1), axis=0).reshape(
+        (span_count, 3) + rimmed.shape[1:]
+    )
     accum = lax.conv_general_dilated(
         window,
         conv_weight,

time: 122 us -> 98 us (0.80)
  between operations: 13.8 us -> 0.32 us
  waiting for transfers between devices: 40.5 us -> 32.1 us
  local copies, waits for them, and re-layouts: 20.9 us -> 13.4 us
  other arithmetic: 11.7 us -> 14.6 us
  starting transfers between devices: 14.7 us -> 17.2 us
    all_gather x1 -> x0, waiting for transfers between devices: 9.55 us -> none  [shards(): gathered = lax.all_gather(rimmed, 'tm', axis=0, tiled=True)]
    ppermute x1, waiting for transfers between devices: 2.89 us -> 7.49 us  [padded_2(): lax.ppermute(tail, axis, [(i, (i + 1) % count) for i in range(ends)])]
    select_n x1 -> x3, other arithmetic: 0.01 us -> 4.45 us  [the longest x2 4.36 us: shards(): jnp.take(pool, picks.reshape(-1), axis=0)]
    another operation x2 -> x0, local copies, waits for them, and re-layouts: 4.08 us -> none  [shards(): window = jnp.stack([back_two, back_one, padded], axis=1)]
    ppermute x1, waiting for transfers between devices: 4.07 us -> 0.01 us  [padded_2(): lax.ppermute(head, axis, [((i + 1) % count, i) for i in range(ends)])]
    ppermute x3, starting transfers between devices: 5.3 us -> 8.31 us  [ring_gather(): forward = lax.ppermute(forward, axis, ahead)]
    unnamed x33 -> x30, local copies, waits for them, and re-layouts: 9.18 us -> 6.53 us
    all_gather x1 -> x0, local copies, waits for them, and re-layouts: 2.62 us -> none  [shards(): gathered = lax.all_gather(rimmed, 'tm', axis=0, tiled=True)]
  transfers between devices with their start and end apart: 11 -> 11, of which waited for: 8 -> 7; matrix products, arithmetic and copies ran while one was open for 8% -> 7% of each run, Pallas kernels for 0% -> 0%
where the time goes in v6:
time: 98 us; the launch traced here: 97.8 us
  waiting for transfers between devices  32.1 us (33%)
  matrix products  20.2 us (21%)
  starting transfers between devices  17.2 us (18%)
  other arithmetic  14.6 us (15%)
  local copies, waits for them, and re-layouts  13.4 us (14%)
    ppermute x3, waiting for transfers between devices, ring_gather(): forward = lax.ppermute(forward, axis, ahead)  19.4 us
    ppermute x3, starting transfers between devices, ring_gather(): forward = lax.ppermute(forward, axis, ahead)  8.31 us
    ppermute x1, waiting for transfers between devices, padded_2(): lax.ppermute(tail, axis, [(i, (i + 1) % count) for i in range(ends)])  7.49 us
    dot_general x1, matrix products, shards(): jnp.einsum('fqc,fkc->fqk', queries, keys_all, preferred_element_type=jnp....  7.02 us
    unnamed x30, local copies, waits for them, and re-layouts  6.53 us
    dot_general x1, matrix products, shards(): jnp.einsum('fqk,fkc->fqc', weights_exp.astype(jnp.bfloat16), values_all,...  6.39 us
    conv_general_dilated x1, matrix products, shards(): lax.conv_general_dilated(window, conv_weight, window_strides=(1, 1, 1), p...  5.99 us
    ppermute x1, starting transfers between devices, padded_2(): lax.ppermute(tail, axis, [(i, (i + 1) % count) for i in range(ends)])  4.88 us
  transfers between devices with their start and end apart: 11, of which 7 were waited for; matrix products, arithmetic and copies ran while one was open for 7% of the time, Pallas kernels for 0%

profile of v6, /device:TPU:0, one launch (start us, length us, event | category | flops | bytes accessed | tf_op | source)
XLA Modules:
  0.0 97.8 jit_solution(6618781209624784087)
XLA Ops:
  0.0 1.2 %fusion.21 = f32[2,2,128]{2,1,0:T(2,128)S(1)} fusion(bf16[2,2,128,384]{3,2,1,0:T(8,128)(2,1)} %param.10), kind=kLoop, calls=%fused_computation.30 | loop fusion | flops 589312 | bytes 395264 | tf_op jit(solution)/shard_map/reduce_sum | solution.py:48
  1.2 1.3 %fusion.28 = bf16[2,2,128,384]{3,2,1,0:T(8,128)(2,1)S(1)} fusion(bf16[2,2,128,384]{3,2,1,0:T(8,128)(2,1)} %param.10, f32[384]{0:T(512)} %param.12, f32[2,2,128]{2,1,0:T(2,128)S(1)} %add_rsqrt_fusion.1), kind=kLoop, calls=%fused_computation.37 | loop fusion | flops 1572864 | bytes 790016 | tf_op jit(solution)/shard_map/convert_element_type | solution.py:65
  2.5 0.1 pad_slice_fusion.1
  2.6 4.9 %collective-permute-start = (bf16[2,1,130,384]{3,2,1,0:T(8,128)(2,1)S(1)}, bf16[2,1,130,384]{3,2,1,0:T(8,128)(2,1)S(1)}, u32[]{:S(2)}, u32[]{:S(2)}) collective-permute-start(bf16[2,1,130,384]{3,2,1,0:T(8,128)(2,1)S(1)} %get-tuple-element.9), channel_id=1, source_target_pairs={{0,1},{1,2},{2,3},{3,4},{4,5},{5,6},{6,7},{8,9},{9,10},{10,11},{11... | collective-permute-start | bytes 599048 | tf_op jit(solution)/shard_map/ppermute | solution.py:15
  7.5 1.3 %collective-permute-start.1 = (bf16[2,1,130,384]{3,2,1,0:T(8,128)(2,1)S(1)}, bf16[2,1,130,384]{3,2,1,0:T(8,128)(2,1)S(1)}, u32[]{:S(2)}, u32[]{:S(2)}) collective-permute-start(bf16[2,1,130,384]{3,2,1,0:T(8,128)(2,1)S(1)} %get-tuple-element.10), channel_id=1, source_target_pairs={{1,0},{2,1},{3,2},{4,3},{5,4},{6,5},{7,6},{9,8},{10,9},{11,10},{12... | collective-permute-start | bytes 599048 | tf_op jit(solution)/shard_map/ppermute | solution.py:17
  8.8 0.1 pad.4
  8.9 7.5 %collective-permute-done = bf16[2,1,130,384]{3,2,1,0:T(8,128)(2,1)S(1)} collective-permute-done((bf16[2,1,130,384]{3,2,1,0:T(8,128)(2,1)S(1)}, bf16[2,1,130,384]{3,2,1,0:T(8,128)(2,1)S(1)}, u32[]{:S(2)}, u32[]{:S(2)}) %collective-permute-start) | collective-permute-done | bytes 199712 | tf_op jit(solution)/shard_map/ppermute | solution.py:15
  16.4 0.0 collective-permute-done.1
  16.4 0.1 pad_maximum_fusion
  16.6 0.3 copy.32
  16.9 0.1 collective-permute-start.2
  17.0 0.1 compare_select_fusion.8
  17.1 0.1 compare_and_fusion
  17.2 0.1 reshape.67
  17.2 0.1 copy.31
  17.4 0.1 pad.13.clone
  17.4 1.8 %collective-permute-done.2 = bf16[2,4,130,384]{3,1,2,0:T(4,128)(2,1)S(1)} collective-permute-done((bf16[2,4,130,384]{3,1,2,0:T(4,128)(2,1)S(1)}, bf16[2,4,130,384]{3,1,2,0:T(4,128)(2,1)S(1)}, u32[]{:S(2)}, u32[]{:S(2)}) %collective-permute-start.2) | collective-permute-done | bytes 798752 | tf_op jit(solution)/shard_map/ppermute | solution.py:73
  19.3 0.1 copy.33
  19.4 0.4 maximum_maximum_fusion
  19.7 2.5 %gather_fusion = bf16[6,4,130,384]{3,2,1,0:T(8,128)(2,1)} fusion(bf16[5,4,130,384]{3,2,1,0:T(8,128)(2,1)S(1)} %maximum_maximum_fusion, s32[1024]{0:T(1024)S(1)} %pad_clamp_fusion), kind=kCustom, calls=%fused_computation | custom fusion | bytes 4792344 | tf_op jit(solution)/shard_map/jit(_take)/gather | solution.py:85
  22.3 4.4 %fusion.6 = bf16[3,4,2,130,384]{4,2,3,1,0:T(2,128)(2,1)S(1)} fusion(pred[2,3]{0,1:T(4,128)(4,1)S(1)} %copy.31, bf16[2,3,4,130,384]{4,3,2,1,0:T(8,128)(2,1)} %bitcast.46), kind=kLoop, calls=%fused_computation.13 | loop fusion | flops 1198080 | bytes 4792326 | tf_op jit(solution)/shard_map/jit(_take)/select_n | solution.py:85
  26.6 0.0 slice-start.1
  26.6 1.9 %pad.5 = bf16[3,4,2,136,384]{4,2,3,1,0:T(2,128)(2,1)S(1)} pad(bf16[3,4,2,130,384]{4,2,3,1,0:T(2,128)(2,1)S(1)} %fusion.6, bf16[]{:T(256)} %constant.87.clone.1), padding=0_0x0_0x0_0x0_6x0_0 | pad | bytes 4902914 | tf_op jit(solution)/shard_map/jit(_take)/select_n | solution.py:85
  28.5 0.0 copy-start.8
  28.5 0.2 slice.28
  28.7 2.8 %fusion.2 = bf16[3,4,2,8,19,384]{5,2,4,3,1,0:T(2,128)(2,1)S(1)} fusion(bf16[3,4,2,7,2,384]{5,2,4,3,1,0:T(2,128)(2,1)S(1)} %slice.28, bf16[3,4,2,8,17,384]{5,2,4,3,1,0:T(2,128)(2,1)S(1)} %bitcast.45), kind=kLoop, calls=%fused_computation.9 | loop fusion | flops 8404992 | bytes 5566464 | tf_op jit(solution)/shard_map/conv_general_dilated | solution.py:88
  31.5 6.0 %fusion.12 = f32[1,2,16,17,384]{4,2,3,1,0:T(8,128)S(1)} fusion(bf16[3,3,3,384,384]{4,3,2,1,0:T(8,128)(2,1)S(1)} %bitcast.54, bf16[3,4,2,8,19,384]{5,2,4,3,1,0:T(2,128)(2,1)S(1)} %fusion.2, pred[16,17]{0,1:T(8,128)(4,1)S(1)} %copy-done.8), kind=kOutput, calls=%fused_computation.19 | convolution fusion | flops 4331876352 | bytes 11600144 | tf_op jit(solution)/shard_map/conv_general_dilated | solution.py:88
  37.5 0.0 copy-start.1
  37.6 0.0 copy-start.5
  37.6 0.0 copy-start.6
  37.6 0.0 copy-start.2
  37.6 0.4 copy.36
  38.0 0.3 slice.29
  38.3 0.2 copy-done.1
  38.5 0.2 fusion.31
  38.8 0.2 fusion.33
  39.0 3.5 %collective-permute-start.3 = (bf16[2,256,384]{2,1,0:T(8,128)(2,1)S(1)}, bf16[2,256,384]{2,1,0:T(8,128)(2,1)S(1)}, u32[]{:S(2)}, u32[]{:S(2)}) collective-permute-start(bf16[2,256,384]{2,1,0:T(8,128)(2,1)S(1)} %bitcast.47), channel_id=1, source_target_pairs={{0,2},{2,4},{4,6},{6,7},{7,5},{5,3},{3,1},{1,0},{8,10},{10,12},{12... | collective-permute-start | bytes 1179656 | tf_op jit(solution)/shard_map/ppermute | solution.py:33
  42.4 8.7 %collective-permute-done.3 = bf16[2,256,384]{2,1,0:T(8,128)(2,1)S(1)} collective-permute-done((bf16[2,256,384]{2,1,0:T(8,128)(2,1)S(1)}, bf16[2,256,384]{2,1,0:T(8,128)(2,1)S(1)}, u32[]{:S(2)}, u32[]{:S(2)}) %collective-permute-start.3) | collective-permute-done | bytes 393248 | tf_op jit(solution)/shard_map/ppermute | solution.py:33
  51.1 2.5 %collective-permute-start.5 = (bf16[2,256,384]{2,1,0:T(8,128)(2,1)S(1)}, bf16[2,256,384]{2,1,0:T(8,128)(2,1)S(1)}, u32[]{:S(2)}, u32[]{:S(2)}) collective-permute-start(bf16[2,256,384]{2,1,0:T(8,128)(2,1)S(1)} %collective-permute-done.3), channel_id=1, source_target_pairs={{0,2},{2,4},{4,6},{6,7},{7,5},{5,3},{3,1},{1,0},{8,10},{10,12},{12... | collective-permute-start | bytes 1179656 | tf_op jit(solution)/shard_map/ppermute | solution.py:33
  53.6 0.0 collective-permute-done.4
  53.6 0.8 constant_dynamic-update-slice_fusion.8
  54.4 0.4 convolution_convert_fusion.2
  54.8 6.7 %collective-permute-done.5 = bf16[2,256,384]{2,1,0:T(8,128)(2,1)S(1)} collective-permute-done((bf16[2,256,384]{2,1,0:T(8,128)(2,1)S(1)}, bf16[2,256,384]{2,1,0:T(8,128)(2,1)S(1)}, u32[]{:S(2)}, u32[]{:S(2)}) %collective-permute-start.5) | collective-permute-done | bytes 393248 | tf_op jit(solution)/shard_map/ppermute | solution.py:33
  61.5 2.4 %collective-permute-start.7 = (bf16[2,256,384]{2,1,0:T(8,128)(2,1)S(1)}, bf16[2,256,384]{2,1,0:T(8,128)(2,1)S(1)}, u32[]{:S(2)}, u32[]{:S(2)}) collective-permute-start(bf16[2,256,384]{2,1,0:T(8,128)(2,1)S(1)} %collective-permute-done.5), channel_id=1, source_target_pairs={{0,2},{2,4},{4,6},{6,7},{7,5},{5,3},{3,1},{1,0},{8,10},{10,12},{12... | collective-permute-start | bytes 1179656 | tf_op jit(solution)/shard_map/ppermute | solution.py:33
  63.9 0.0 collective-permute-start.8
  63.9 0.8 constant_dynamic-update-slice_fusion.7
  64.7 0.8 constant_dynamic-update-slice_fusion.6
  65.5 0.8 constant_dynamic-update-slice_fusion.5
  66.3 0.8 constant_dynamic-update-slice_fusion.4
  67.1 4.0 %collective-permute-done.7 = bf16[2,256,384]{2,1,0:T(8,128)(2,1)S(1)} collective-permute-done((bf16[2,256,384]{2,1,0:T(8,128)(2,1)S(1)}, bf16[2,256,384]{2,1,0:T(8,128)(2,1)S(1)}, u32[]{:S(2)}, u32[]{:S(2)}) %collective-permute-start.7) | collective-permute-done | bytes 393248 | tf_op jit(solution)/shard_map/ppermute | solution.py:33
  71.1 2.3 %collective-permute-start.9 = (bf16[2,128,384]{2,1,0:T(8,128)(2,1)S(1)}, bf16[2,128,384]{2,1,0:T(8,128)(2,1)S(1)}, u32[]{:S(2)}, u32[]{:S(2)}) collective-permute-start(bf16[2,128,384]{2,1,0:T(8,128)(2,1)S(1)} %slice.30), channel_id=1, source_target_pairs={{0,2},{2,4},{4,6},{6,7},{7,5},{5,3},{3,1},{1,0},{8,10},{10,12},{12... | collective-permute-start | bytes 589832 | tf_op jit(solution)/shard_map/ppermute | solution.py:38
  73.4 0.3 collective-permute-start.10
  73.7 0.8 constant_dynamic-update-slice_fusion.3
  74.5 0.8 constant_dynamic-update-slice_fusion.2
  75.3 1.5 %collective-permute-done.9 = bf16[2,128,384]{2,1,0:T(8,128)(2,1)S(1)} collective-permute-done((bf16[2,128,384]{2,1,0:T(8,128)(2,1)S(1)}, bf16[2,128,384]{2,1,0:T(8,128)(2,1)S(1)}, u32[]{:S(2)}, u32[]{:S(2)}) %collective-permute-start.9) | collective-permute-done | bytes 196640 | tf_op jit(solution)/shard_map/ppermute | solution.py:38
  76.8 0.7 constant_dynamic-update-slice_fusion.1
  77.5 1.9 %collective-permute-done.10 = bf16[2,128,384]{2,1,0:T(8,128)(2,1)S(1)} collective-permute-done((bf16[2,128,384]{2,1,0:T(8,128)(2,1)S(1)}, bf16[2,128,384]{2,1,0:T(8,128)(2,1)S(1)}, u32[]{:S(2)}, u32[]{:S(2)}) %collective-permute-start.10) | collective-permute-done | bytes 196640 | tf_op jit(solution)/shard_map/ppermute | solution.py:39
  79.4 0.7 constant_dynamic-update-slice_fusion
  80.0 7.0 %multiply_reduce_fusion = (f32[2,256]{1,0:T(2,128)S(1)}, f32[2,256,2048]{2,1,0:T(8,128)}) fusion(bf16[2,256,384]{2,1,0:T(8,128)(2,1)S(1)} %convolution_convert_fusion.2, bf16[2,2048,384]{2,1,0:T(8,128)(2,1)} %constant_dynamic-update-slice_fusion, bf16[384,384]{1,0:T(8,128)(2,1)S(1)} %copy-done), kind=kOutput, calls=%fused_computation.4 | convolution fusion | flops 2016935424 | bytes 8030208 | tf_op jit(solution)/shard_map/fqc,fkc->fqk/dot_general | solution.py:111
  87.1 3.0 %fusion = f32[2,256]{1,0:T(2,128)S(1)} fusion(f32[2,256,2048]{2,1,0:T(8,128)} %get-tuple-element.14, f32[2,256]{1,0:T(2,128)S(1)} %get-tuple-element.13), kind=kLoop, calls=%fused_computation.5 | loop fusion | flops 3145216 | bytes 4198400 | tf_op jit(solution)/shard_map/reduce_sum | solution.py:116
  90.1 0.0 copy-start.3
  90.1 6.4 %fusion.18 = bf16[2,256,384]{2,1,0:T(8,128)(2,1)S(1)} fusion(bf16[2,2048,384]{2,1,0:T(8,128)(2,1)} %constant_dynamic-update-slice_fusion, f32[2,256,2048]{2,1,0:T(8,128)} %get-tuple-element.14, f32[2,256]{1,0:T(2,128)S(1)} %get-tuple-element.13, f32[2,256]{1,0:T(2,128)S(1)} %fusion, bf16[384,384]{1,0:T(8,128)(2,1)S(1)} %copy-done.7), kind=kOutput, calls=%fused_computation.28 | convolution fusion | flops 2018377728 | bytes 8032256 | tf_op jit(solution)/shard_map/fqk,fkc->fqc/dot_general | solution.py:117
  96.5 0.4 fusion.35
  96.9 0.8 fusion.34
  (26 shorter events, 0.1 us)
Async XLA Ops:
  0.0 80.0 %copy-start = (bf16[384,384]{1,0:T(8,128)(2,1)S(1)}, bf16[384,384]{1,0:T(8,128)(2,1)}, u32[]{:S(2)}) copy-start(bf16[384,384]{1,0:T(8,128)(2,1)} %param.17) | copy-start | bytes 884740
  0.0 17.0 %copy-start.4 = (s32[2,2]{1,0:T(2,128)S(1)}, s32[2,2]{1,0:T(2,128)}, u32[]{:S(2)}) copy-start(s32[2,2]{1,0:T(2,128)} %param.11) | copy-start | bytes 52
  2.6 13.8 %collective-permute-start = (bf16[2,1,130,384]{3,2,1,0:T(8,128)(2,1)S(1)}, bf16[2,1,130,384]{3,2,1,0:T(8,128)(2,1)S(1)}, u32[]{:S(2)}, u32[]{:S(2)}) collective-permute-start(bf16[2,1,130,384]{3,2,1,0:T(8,128)(2,1)S(1)} %get-tuple-element.9), channel_id=1, source_target_pairs={{0,1},{1,2},{2,3},{3,4},{4,5},{5,6},{6,7},{8,9},{9,10},{10,11},{11... | collective-permute-start | bytes 599048 | tf_op jit(solution)/shard_map/ppermute | solution.py:15
  7.5 8.9 %collective-permute-start.1 = (bf16[2,1,130,384]{3,2,1,0:T(8,128)(2,1)S(1)}, bf16[2,1,130,384]{3,2,1,0:T(8,128)(2,1)S(1)}, u32[]{:S(2)}, u32[]{:S(2)}) collective-permute-start(bf16[2,1,130,384]{3,2,1,0:T(8,128)(2,1)S(1)} %get-tuple-element.10), channel_id=1, source_target_pairs={{1,0},{2,1},{3,2},{4,3},{5,4},{6,5},{7,6},{9,8},{10,9},{11,10},{12... | collective-permute-start | bytes 599048 | tf_op jit(solution)/shard_map/ppermute | solution.py:17
  16.9 2.4 %collective-permute-start.2 = (bf16[2,4,130,384]{3,1,2,0:T(4,128)(2,1)S(1)}, bf16[2,4,130,384]{3,1,2,0:T(4,128)(2,1)S(1)}, u32[]{:S(2)}, u32[]{:S(2)}) collective-permute-start(bf16[2,4,130,384]{3,1,2,0:T(4,128)(2,1)S(1)} %copy.32), channel_id=1, source_target_pairs={{0,8},{8,0},{1,9},{9,1},{2,10},{10,2},{3,11},{11,3},{4,12},{12,4},... | collective-permute-start | bytes 2396168 | tf_op jit(solution)/shard_map/ppermute | solution.py:73
  22.3 9.3 %slice-start = ((s8[7962624]{0:T(1024)(128)(4,1)}), s8[4194304]{0:T(1024)(128)(4,1)S(1)}, s32[]{:S(2)}) async-start(s8[7962624]{0:T(1024)(128)(4,1)} %bitcast.53), calls=%async_computation | async-start | bytes 8388608
  26.6 4.9 %slice-start.1 = ((s8[7962624]{0:T(1024)(128)(4,1)}), s8[3768320]{0:T(1024)(128)(4,1)S(1)}, s32[]{:S(2)}) async-start(s8[7962624]{0:T(1024)(128)(4,1)} %bitcast.53), calls=%async_computation.1 | async-start | bytes 7536640
  28.5 3.0 %copy-start.8 = (pred[16,17]{0,1:T(8,128)(4,1)S(1)}, pred[16,17]{0,1:T(8,128)(4,1)}, u32[]{:S(2)}) copy-start(pred[16,17]{0,1:T(8,128)(4,1)} %constant.99) | copy-start | bytes 820
  37.5 1.0 %copy-start.1 = (bf16[2,2,128,384]{3,2,1,0:T(8,128)(2,1)S(1)}, bf16[2,2,128,384]{3,2,1,0:T(8,128)(2,1)}, u32[]{:S(2)}) copy-start(bf16[2,2,128,384]{3,2,1,0:T(8,128)(2,1)} %param.10) | copy-start | bytes 1179652
  37.6 1.0 %copy-start.5 = (f32[384]{0:T(512)S(1)}, f32[384]{0:T(512)}, u32[]{:S(2)}) copy-start(f32[384]{0:T(512)} %param.14) | copy-start | bytes 4612
  37.6 1.2 %copy-start.6 = (f32[384]{0:T(512)S(1)}, f32[384]{0:T(512)}, u32[]{:S(2)}) copy-start(f32[384]{0:T(512)} %param.15) | copy-start | bytes 4612
  37.6 16.8 %copy-start.2 = (bf16[384,384]{1,0:T(8,128)(2,1)S(1)}, bf16[384,384]{1,0:T(8,128)(2,1)}, u32[]{:S(2)}) copy-start(bf16[384,384]{1,0:T(8,128)(2,1)} %param.16) | copy-start | bytes 884740
  39.0 12.1 %collective-permute-start.3 = (bf16[2,256,384]{2,1,0:T(8,128)(2,1)S(1)}, bf16[2,256,384]{2,1,0:T(8,128)(2,1)S(1)}, u32[]{:S(2)}, u32[]{:S(2)}) collective-permute-start(bf16[2,256,384]{2,1,0:T(8,128)(2,1)S(1)} %bitcast.47), channel_id=1, source_target_pairs={{0,2},{2,4},{4,6},{6,7},{7,5},{5,3},{3,1},{1,0},{8,10},{10,12},{12... | collective-permute-start | bytes 1179656 | tf_op jit(solution)/shard_map/ppermute | solution.py:33
  42.4 11.2 %collective-permute-start.4 = (bf16[2,256,384]{2,1,0:T(8,128)(2,1)S(1)}, bf16[2,256,384]{2,1,0:T(8,128)(2,1)S(1)}, u32[]{:S(2)}, u32[]{:S(2)}) collective-permute-start(bf16[2,256,384]{2,1,0:T(8,128)(2,1)S(1)} %bitcast.48), channel_id=1, source_target_pairs={{0,1},{2,0},{4,2},{6,4},{7,6},{5,7},{3,5},{1,3},{8,9},{10,8},{12,1... | collective-permute-start | bytes 1179656 | tf_op jit(solution)/shard_map/ppermute | solution.py:34
  51.1 10.4 %collective-permute-start.5 = (bf16[2,256,384]{2,1,0:T(8,128)(2,1)S(1)}, bf16[2,256,384]{2,1,0:T(8,128)(2,1)S(1)}, u32[]{:S(2)}, u32[]{:S(2)}) collective-permute-start(bf16[2,256,384]{2,1,0:T(8,128)(2,1)S(1)} %collective-permute-done.3), channel_id=1, source_target_pairs={{0,2},{2,4},{4,6},{6,7},{7,5},{5,3},{3,1},{1,0},{8,10},{10,12},{12... | collective-permute-start | bytes 1179656 | tf_op jit(solution)/shard_map/ppermute | solution.py:33
  53.6 10.3 %collective-permute-start.6 = (bf16[2,256,384]{2,1,0:T(8,128)(2,1)S(1)}, bf16[2,256,384]{2,1,0:T(8,128)(2,1)S(1)}, u32[]{:S(2)}, u32[]{:S(2)}) collective-permute-start(bf16[2,256,384]{2,1,0:T(8,128)(2,1)S(1)} %collective-permute-done.4), channel_id=1, source_target_pairs={{0,1},{2,0},{4,2},{6,4},{7,6},{5,7},{3,5},{1,3},{8,9},{10,8},{12,1... | collective-permute-start | bytes 1179656 | tf_op jit(solution)/shard_map/ppermute | solution.py:34
  61.5 9.5 %collective-permute-start.7 = (bf16[2,256,384]{2,1,0:T(8,128)(2,1)S(1)}, bf16[2,256,384]{2,1,0:T(8,128)(2,1)S(1)}, u32[]{:S(2)}, u32[]{:S(2)}) collective-permute-start(bf16[2,256,384]{2,1,0:T(8,128)(2,1)S(1)} %collective-permute-done.5), channel_id=1, source_target_pairs={{0,2},{2,4},{4,6},{6,7},{7,5},{5,3},{3,1},{1,0},{8,10},{10,12},{12... | collective-permute-start | bytes 1179656 | tf_op jit(solution)/shard_map/ppermute | solution.py:33
  63.9 9.5 %collective-permute-start.8 = (bf16[2,256,384]{2,1,0:T(8,128)(2,1)S(1)}, bf16[2,256,384]{2,1,0:T(8,128)(2,1)S(1)}, u32[]{:S(2)}, u32[]{:S(2)}) collective-permute-start(bf16[2,256,384]{2,1,0:T(8,128)(2,1)S(1)} %collective-permute-done.6), channel_id=1, source_target_pairs={{0,1},{2,0},{4,2},{6,4},{7,6},{5,7},{3,5},{1,3},{8,9},{10,8},{12,1... | collective-permute-start | bytes 1179656 | tf_op jit(solution)/shard_map/ppermute | solution.py:34
  71.1 5.7 %collective-permute-start.9 = (bf16[2,128,384]{2,1,0:T(8,128)(2,1)S(1)}, bf16[2,128,384]{2,1,0:T(8,128)(2,1)S(1)}, u32[]{:S(2)}, u32[]{:S(2)}) collective-permute-start(bf16[2,128,384]{2,1,0:T(8,128)(2,1)S(1)} %slice.30), channel_id=1, source_target_pairs={{0,2},{2,4},{4,6},{6,7},{7,5},{5,3},{3,1},{1,0},{8,10},{10,12},{12... | collective-permute-start | bytes 589832 | tf_op jit(solution)/shard_map/ppermute | solution.py:38
  73.4 5.9 %collective-permute-start.10 = (bf16[2,128,384]{2,1,0:T(8,128)(2,1)S(1)}, bf16[2,128,384]{2,1,0:T(8,128)(2,1)S(1)}, u32[]{:S(2)}, u32[]{:S(2)}) collective-permute-start(bf16[2,128,384]{2,1,0:T(8,128)(2,1)S(1)} %slice.31), channel_id=1, source_target_pairs={{0,1},{2,0},{4,2},{6,4},{7,6},{5,7},{3,5},{1,3},{8,9},{10,8},{12,1... | collective-permute-start | bytes 589832 | tf_op jit(solution)/shard_map/ppermute | solution.py:39
  87.1 3.1 %copy-start.7 = (bf16[384,384]{1,0:T(8,128)(2,1)S(1)}, bf16[384,384]{1,0:T(8,128)(2,1)}, u32[]{:S(2)}) copy-start(bf16[384,384]{1,0:T(8,128)(2,1)} %param.18) | copy-start | bytes 884740
  90.1 6.4 %copy-start.3 = (bf16[384,384]{1,0:T(8,128)(2,1)S(1)}, bf16[384,384]{1,0:T(8,128)(2,1)}, u32[]{:S(2)}) copy-start(bf16[384,384]{1,0:T(8,128)(2,1)} %param.19) | copy-start | bytes 884740

commit v7 on v6

--- a/solution.py
+++ b/solution.py
@@ -40,7 +40,7 @@
             lax.slice_in_dim(backward, half, block.shape[dim], axis=dim), axis, behind
         )
         pieces += [front, back]
-    return jnp.concatenate(pieces, axis=dim)
+    return pieces
 
 
 def rms_scaled(frames, gain):
@@ -100,26 +100,36 @@
         "ftc,cd->ftd", tokens, query_weight, preferred_element_type=jnp.float32
     ).astype(jnp.bfloat16)
     score_scale = 1.0 / channels**0.5
-    tokens_all = ring_gather(tokens, "height", 1)
-    keys_all = jnp.einsum(
-        "ftc,cd->ftd", tokens_all, key_weight, preferred_element_type=jnp.float32
-    ).astype(jnp.bfloat16)
-    values_all = jnp.einsum(
-        "ftc,cd->ftd", tokens_all, value_weight, preferred_element_type=jnp.float32
-    ).astype(jnp.bfloat16)
-    scores = (
-        jnp.einsum("fqc,fkc->fqk", queries, keys_all, preferred_element_type=jnp.float32)
-        * score_scale
-    )
-    peaks = jnp.max(scores, axis=-1, keepdims=True)
-    weights_exp = jnp.exp(scores - peaks)
-    totals = jnp.sum(weights_exp, axis=-1)
-    summed = jnp.einsum(
-        "fqk,fkc->fqc",
-        weights_exp.astype(jnp.bfloat16),
-        values_all,
-        preferred_element_type=jnp.float32,
-    )
+    pieces = ring_gather(tokens, "height", 1)
+    scored = []
+    for piece in pieces:
+        keys = jnp.einsum(
+            "ftc,cd->ftd", piece, key_weight, preferred_element_type=jnp.float32
+        ).astype(jnp.bfloat16)
+        values = jnp.einsum(
+            "ftc,cd->ftd", piece, value_weight, preferred_element_type=jnp.float32
+        ).astype(jnp.bfloat16)
+        scores = (
+            jnp.einsum("fqc,fkc->fqk", queries, keys, preferred_element_type=jnp.float32)
+            * score_scale
+        )
+        scored.append((scores, values))
+    peaks = scored[0][0].max(axis=-1, keepdims=True)
+    for scores, _ in scored[1:]:
+        peaks = jnp.maximum(peaks, scores.max(axis=-1, keepdims=True))
+    totals = None
+    summed = None
+    for scores, values in scored:
+        weights_exp = jnp.exp(scores - peaks)
+        part_total = jnp.sum(weights_exp, axis=-1)
+        part_sum = jnp.einsum(
+            "fqk,fkc->fqc",
+            weights_exp.astype(jnp.bfloat16),
+            values,
+            preferred_element_type=jnp.float32,
+        )
+        totals = part_total if totals is None else totals + part_total
+        summed = part_sum if summed is None else summed + part_sum
     attended = (summed / totals[:, :, None]).astype(jnp.bfloat16)
     projected = jnp.einsum("ftc,cd->ftd", attended, out_weight, preferred_element_type=jnp.float32)
     encoded = mixed.astype(jnp.float32) + projected.reshape(

time: 98 us -> 105 us (1.071)
  matrix products: 20.2 us -> 40.6 us
  waiting for transfers between devices: 32.1 us -> 22.5 us
  local copies, waits for them, and re-layouts: 13.4 us -> 9.5 us
    dot_general x2 -> x18, matrix products: 13.4 us -> 33.9 us  [the longest x9 17.7 us: shards(): jnp.einsum('fqc,fkc->fqk', queries, keys, preferred_element_type=jnp.floa...]
    ppermute x3, waiting for transfers between devices: 19.4 us -> 12.7 us  [ring_gather(): forward = lax.ppermute(forward, axis, ahead)]
    unnamed x30 -> x42, local copies, waits for them, and re-layouts: 6.53 us -> 1 us
    slice x1, local copies, waits for them, and re-layouts: 0.02 us -> 1.62 us  [ring_gather(): lax.slice_in_dim(backward, half, block.shape[dim], axis=dim)]
    ppermute x1, waiting for transfers between devices: 1.51 us -> 0.01 us  [ring_gather(): lax.ppermute(lax.slice_in_dim(forward, 0, half, axis=dim), axis, ahead)]
    ppermute x1, waiting for transfers between devices: 1.87 us -> 0.5 us  [ring_gather(): lax.ppermute(lax.slice_in_dim(backward, half, block.shape[dim], axis=dim)...]
    reduce_sum x1 -> x2, other arithmetic: 3.05 us -> 2.32 us  [shards(): part_total = jnp.sum(weights_exp, axis=-1)]
  transfers between devices with their start and end apart: 11 -> 11, of which waited for: 7 -> 6; matrix products, arithmetic and copies ran while one was open for 7% -> 19% of each run, Pallas kernels for 0% -> 0%
where the time goes in v7:
time: 105 us
  matrix products  40.6 us (39%)
  waiting for transfers between devices  22.5 us (21%)
  starting transfers between devices  17.1 us (16%)
  other arithmetic  14.6 us (14%)
  local copies, waits for them, and re-layouts  9.5 us (9%)
    dot_general x9, matrix products, shards(): jnp.einsum('fqc,fkc->fqk', queries, keys, preferred_element_type=jnp.floa...  17.7 us
    dot_general x9, matrix products, shards(): jnp.einsum('fqk,fkc->fqc', weights_exp.astype(jnp.bfloat16), values, pref...  16.1 us
    ppermute x3, waiting for transfers between devices, ring_gather(): forward = lax.ppermute(forward, axis, ahead)  12.7 us
    ppermute x3, starting transfers between devices, ring_gather(): forward = lax.ppermute(forward, axis, ahead)  8.31 us
    ppermute x1, waiting for transfers between devices, padded_2(): lax.ppermute(tail, axis, [(i, (i + 1) % count) for i in range(ends)])  7.49 us
    conv_general_dilated x1, matrix products, shards(): lax.conv_general_dilated(window, conv_weight, window_strides=(1, 1, 1), p...  5.99 us
    ppermute x1, starting transfers between devices, padded_2(): lax.ppermute(tail, axis, [(i, (i + 1) % count) for i in range(ends)])  4.88 us
    select_n x2, other arithmetic, shards(): jnp.take(pool, picks.reshape(-1), axis=0)  4.36 us
  transfers between devices with their start and end apart: 11, of which 6 were waited for; matrix products, arithmetic and copies ran while one was open for 19% of the time, Pallas kernels for 0%

profile of v7, /device:TPU:0, one launch (start us, length us, event | category | flops | bytes accessed | tf_op | source)
XLA Modules:
  0.0 104.8 jit_solution(13088461618118776422)
XLA Ops:
  0.0 1.2 %fusion.15 = f32[2,2,128]{2,1,0:T(2,128)S(1)} fusion(bf16[2,2,128,384]{3,2,1,0:T(8,128)(2,1)} %param.10), kind=kLoop, calls=%fused_computation.58 | loop fusion | flops 589312 | bytes 395264 | tf_op jit(solution)/shard_map/reduce_sum | solution.py:48
  1.2 1.3 %fusion.22 = bf16[2,2,128,384]{3,2,1,0:T(8,128)(2,1)S(1)} fusion(bf16[2,2,128,384]{3,2,1,0:T(8,128)(2,1)} %param.10, f32[384]{0:T(512)} %param.12, f32[2,2,128]{2,1,0:T(2,128)S(1)} %add_rsqrt_fusion.1), kind=kLoop, calls=%fused_computation.65 | loop fusion | flops 1572864 | bytes 790016 | tf_op jit(solution)/shard_map/convert_element_type | solution.py:65
  2.5 0.1 pad_slice_fusion.1
  2.6 4.9 %collective-permute-start = (bf16[2,1,130,384]{3,2,1,0:T(8,128)(2,1)S(1)}, bf16[2,1,130,384]{3,2,1,0:T(8,128)(2,1)S(1)}, u32[]{:S(2)}, u32[]{:S(2)}) collective-permute-start(bf16[2,1,130,384]{3,2,1,0:T(8,128)(2,1)S(1)} %get-tuple-element.18), channel_id=1, source_target_pairs={{0,1},{1,2},{2,3},{3,4},{4,5},{5,6},{6,7},{8,9},{9,10},{10,11},{11... | collective-permute-start | bytes 599048 | tf_op jit(solution)/shard_map/ppermute | solution.py:15
  7.5 1.3 %collective-permute-start.1 = (bf16[2,1,130,384]{3,2,1,0:T(8,128)(2,1)S(1)}, bf16[2,1,130,384]{3,2,1,0:T(8,128)(2,1)S(1)}, u32[]{:S(2)}, u32[]{:S(2)}) collective-permute-start(bf16[2,1,130,384]{3,2,1,0:T(8,128)(2,1)S(1)} %get-tuple-element.19), channel_id=1, source_target_pairs={{1,0},{2,1},{3,2},{4,3},{5,4},{6,5},{7,6},{9,8},{10,9},{11,10},{12... | collective-permute-start | bytes 599048 | tf_op jit(solution)/shard_map/ppermute | solution.py:17
  8.8 0.1 pad.4
  8.9 7.5 %collective-permute-done = bf16[2,1,130,384]{3,2,1,0:T(8,128)(2,1)S(1)} collective-permute-done((bf16[2,1,130,384]{3,2,1,0:T(8,128)(2,1)S(1)}, bf16[2,1,130,384]{3,2,1,0:T(8,128)(2,1)S(1)}, u32[]{:S(2)}, u32[]{:S(2)}) %collective-permute-start) | collective-permute-done | bytes 199712 | tf_op jit(solution)/shard_map/ppermute | solution.py:15
  16.4 0.7 copy-done.6
  17.1 0.1 pad_maximum_fusion
  17.3 0.3 copy.50
  17.7 0.1 compare_select_fusion.8
  17.8 0.1 compare_and_fusion
  17.9 0.1 reshape.125
  17.9 0.1 copy.49
  18.1 1.8 %collective-permute-done.2 = bf16[2,4,130,384]{3,1,2,0:T(4,128)(2,1)S(1)} collective-permute-done((bf16[2,4,130,384]{3,1,2,0:T(4,128)(2,1)S(1)}, bf16[2,4,130,384]{3,1,2,0:T(4,128)(2,1)S(1)}, u32[]{:S(2)}, u32[]{:S(2)}) %collective-permute-start.2) | collective-permute-done | bytes 798752 | tf_op jit(solution)/shard_map/ppermute | solution.py:73
  19.9 0.1 copy.51
  20.1 0.4 maximum_maximum_fusion
  20.4 2.5 %gather_fusion = bf16[6,4,130,384]{3,2,1,0:T(8,128)(2,1)} fusion(bf16[5,4,130,384]{3,2,1,0:T(8,128)(2,1)S(1)} %maximum_maximum_fusion, s32[1024]{0:T(1024)S(1)} %pad_clamp_fusion), kind=kCustom, calls=%fused_computation | custom fusion | bytes 4792344 | tf_op jit(solution)/shard_map/jit(_take)/gather | solution.py:85
  22.9 4.4 %fusion.4 = bf16[3,4,2,130,384]{4,2,3,1,0:T(2,128)(2,1)S(1)} fusion(pred[2,3]{0,1:T(4,128)(4,1)S(1)} %copy.49, bf16[2,3,4,130,384]{4,3,2,1,0:T(8,128)(2,1)} %bitcast.134), kind=kLoop, calls=%fused_computation.7 | loop fusion | flops 1198080 | bytes 4792326 | tf_op jit(solution)/shard_map/jit(_take)/select_n | solution.py:85
  27.3 1.9 %pad.5 = bf16[3,4,2,136,384]{4,2,3,1,0:T(2,128)(2,1)S(1)} pad(bf16[3,4,2,130,384]{4,2,3,1,0:T(2,128)(2,1)S(1)} %fusion.4, bf16[]{:T(256)} %constant.88.clone.1), padding=0_0x0_0x0_0x0_6x0_0 | pad | bytes 4902914 | tf_op jit(solution)/shard_map/jit(_take)/select_n | solution.py:85
  29.2 0.2 slice.28
  29.4 2.8 %fusion = bf16[3,4,2,8,19,384]{5,2,4,3,1,0:T(2,128)(2,1)S(1)} fusion(bf16[3,4,2,7,2,384]{5,2,4,3,1,0:T(2,128)(2,1)S(1)} %slice.28, bf16[3,4,2,8,17,384]{5,2,4,3,1,0:T(2,128)(2,1)S(1)} %bitcast.133), kind=kLoop, calls=%fused_computation.3 | loop fusion | flops 8404992 | bytes 5566464 | tf_op jit(solution)/shard_map/conv_general_dilated | solution.py:88
  32.2 6.0 %fusion.8 = f32[1,2,16,17,384]{4,2,3,1,0:T(8,128)S(1)} fusion(bf16[3,3,3,384,384]{4,3,2,1,0:T(8,128)(2,1)S(1)} %bitcast.143, bf16[3,4,2,8,19,384]{5,2,4,3,1,0:T(2,128)(2,1)S(1)} %fusion, pred[16,17]{0,1:T(8,128)(4,1)S(1)} %copy-done.18), kind=kOutput, calls=%fused_computation.18 | convolution fusion | flops 4331876352 | bytes 11600144 | tf_op jit(solution)/shard_map/conv_general_dilated | solution.py:88
  38.3 0.4 copy.54
  38.7 0.3 slice.29
  39.0 0.2 copy-done.1
  39.2 0.2 fusion.25
  39.5 0.2 fusion.27
  39.6 3.5 %collective-permute-start.3 = (bf16[2,256,384]{2,1,0:T(8,128)(2,1)S(1)}, bf16[2,256,384]{2,1,0:T(8,128)(2,1)S(1)}, u32[]{:S(2)}, u32[]{:S(2)}) collective-permute-start(bf16[2,256,384]{2,1,0:T(8,128)(2,1)S(1)} %bitcast.135), channel_id=1, source_target_pairs={{0,2},{2,4},{4,6},{6,7},{7,5},{5,3},{3,1},{1,0},{8,10},{10,12},{12... | collective-permute-start | bytes 1179656 | tf_op jit(solution)/shard_map/ppermute | solution.py:33
  43.1 0.4 convolution_convert_fusion.14
  43.5 0.6 fusion.133
  44.1 7.6 %collective-permute-done.3 = bf16[2,256,384]{2,1,0:T(8,128)(2,1)S(1)} collective-permute-done((bf16[2,256,384]{2,1,0:T(8,128)(2,1)S(1)}, bf16[2,256,384]{2,1,0:T(8,128)(2,1)S(1)}, u32[]{:S(2)}, u32[]{:S(2)}) %collective-permute-start.3) | collective-permute-done | bytes 393248 | tf_op jit(solution)/shard_map/ppermute | solution.py:33
  51.8 2.5 %collective-permute-start.5 = (bf16[2,256,384]{2,1,0:T(8,128)(2,1)S(1)}, bf16[2,256,384]{2,1,0:T(8,128)(2,1)}, u32[]{:S(2)}, u32[]{:S(2)}) collective-permute-start(bf16[2,256,384]{2,1,0:T(8,128)(2,1)S(1)} %collective-permute-done.3), channel_id=1, source_target_pairs={{0,2},{2,4},{4,6},{6,7},{7,5},{5,3},{3,1},{1,0},{8,10},{10,12},{12... | collective-permute-start | bytes 1179656 | tf_op jit(solution)/shard_map/ppermute | solution.py:33
  54.2 0.1 collective-permute-start.6
  54.3 2.0 %fusion.136 = (f32[2,256]{1,0:T(2,128)}, f32[2,256,256]{1,2,0:T(8,128)}) fusion(bf16[2,256,384]{2,1,0:T(8,128)(2,1)S(1)} %convolution_convert_fusion.14, bf16[2,256,384]{2,1,0:T(8,128)(2,1)S(1)} %collective-permute-done.3, bf16[384,384]{1,0:T(8,128)(2,1)S(1)} %copy-done.4), kind=kOutput, calls=%fused_computation.174 | convolution fusion | flops 252116480 | bytes 1607680 | tf_op jit(solution)/shard_map/fqc,fkc->fqk/dot_general | solution.py:113
  56.4 2.2 %fusion.130 = (f32[2,256]{1,0:T(2,128)}, f32[2,256,256]{1,2,0:T(8,128)S(1)}) fusion(bf16[2,256,384]{2,1,0:T(8,128)(2,1)S(1)} %convolution_convert_fusion.14, bf16[2,256,384]{2,1,0:T(8,128)(2,1)} %collective-permute-done.4, bf16[384,384]{1,0:T(8,128)(2,1)S(1)} %copy-done.4), kind=kOutput, calls=%fused_computation.172 | convolution fusion | flops 252116480 | bytes 1607680 | tf_op jit(solution)/shard_map/fqc,fkc->fqk/dot_general | solution.py:113
  58.6 3.8 %collective-permute-done.5 = bf16[2,256,384]{2,1,0:T(8,128)(2,1)} collective-permute-done((bf16[2,256,384]{2,1,0:T(8,128)(2,1)S(1)}, bf16[2,256,384]{2,1,0:T(8,128)(2,1)}, u32[]{:S(2)}, u32[]{:S(2)}) %collective-permute-start.5) | collective-permute-done | bytes 393248 | tf_op jit(solution)/shard_map/ppermute | solution.py:33
  62.4 2.4 %collective-permute-start.7 = (bf16[2,256,384]{2,1,0:T(8,128)(2,1)}, bf16[2,256,384]{2,1,0:T(8,128)(2,1)S(1)}, u32[]{:S(2)}, u32[]{:S(2)}) collective-permute-start(bf16[2,256,384]{2,1,0:T(8,128)(2,1)} %collective-permute-done.5), channel_id=1, source_target_pairs={{0,2},{2,4},{4,6},{6,7},{7,5},{5,3},{3,1},{1,0},{8,10},{10,12},{12... | collective-permute-start | bytes 1179656 | tf_op jit(solution)/shard_map/ppermute | solution.py:33
  64.8 0.2 collective-permute-start.8
  65.0 3.0 %fusion.127 = (f32[2,256]{1,0:T(2,128)}, f32[2,256,256]{1,2,0:T(8,128)}) fusion(bf16[2,256,384]{2,1,0:T(8,128)(2,1)S(1)} %convolution_convert_fusion.14, bf16[2,256,384]{2,1,0:T(8,128)(2,1)} %collective-permute-done.5, bf16[384,384]{1,0:T(8,128)(2,1)S(1)} %copy-done.4), kind=kOutput, calls=%fused_computation.171 | convolution fusion | flops 252116480 | bytes 1607680 | tf_op jit(solution)/shard_map/fqc,fkc->fqk/dot_general | solution.py:113
  68.0 3.0 %fusion.124 = (f32[2,256]{1,0:T(2,128)}, f32[2,256,256]{1,2,0:T(8,128)}) fusion(bf16[2,256,384]{2,1,0:T(8,128)(2,1)S(1)} %convolution_convert_fusion.14, bf16[2,256,384]{2,1,0:T(8,128)(2,1)} %collective-permute-done.6, bf16[384,384]{1,0:T(8,128)(2,1)S(1)} %copy-done.4), kind=kOutput, calls=%fused_computation.170 | convolution fusion | flops 252116480 | bytes 1607680 | tf_op jit(solution)/shard_map/fqc,fkc->fqk/dot_general | solution.py:113
  71.0 1.2 %collective-permute-done.7 = bf16[2,256,384]{2,1,0:T(8,128)(2,1)S(1)} collective-permute-done((bf16[2,256,384]{2,1,0:T(8,128)(2,1)}, bf16[2,256,384]{2,1,0:T(8,128)(2,1)S(1)}, u32[]{:S(2)}, u32[]{:S(2)}) %collective-permute-start.7) | collective-permute-done | bytes 393248 | tf_op jit(solution)/shard_map/ppermute | solution.py:33
  72.2 0.8 slice.30
  73.0 2.3 %collective-permute-start.9 = (bf16[2,128,384]{2,1,0:T(8,128)(2,1)}, bf16[2,128,384]{2,1,0:T(8,128)(2,1)S(1)}, u32[]{:S(2)}, u32[]{:S(2)}) collective-permute-start(bf16[2,128,384]{2,1,0:T(8,128)(2,1)} %slice.30), channel_id=1, source_target_pairs={{0,2},{2,4},{4,6},{6,7},{7,5},{5,3},{3,1},{1,0},{8,10},{10,12},{12... | collective-permute-start | bytes 589832 | tf_op jit(solution)/shard_map/ppermute | solution.py:38
  75.3 1.6 %slice.31 = bf16[2,128,384]{2,1,0:T(8,128)(2,1)} slice(bf16[2,256,384]{2,1,0:T(8,128)(2,1)} %collective-permute-done.8), slice={[0:2], [128:256], [0:384]} | slice | bytes 393216 | tf_op jit(solution)/shard_map/slice | solution.py:40
  76.9 2.0 %fusion.121 = (f32[2,256]{1,0:T(2,128)}, f32[2,256,256]{1,2,0:T(8,128)}) fusion(bf16[2,256,384]{2,1,0:T(8,128)(2,1)S(1)} %convolution_convert_fusion.14, bf16[2,256,384]{2,1,0:T(8,128)(2,1)S(1)} %collective-permute-done.7, bf16[384,384]{1,0:T(8,128)(2,1)S(1)} %copy-done.4), kind=kOutput, calls=%fused_computation.169 | convolution fusion | flops 252116480 | bytes 1607680 | tf_op jit(solution)/shard_map/fqc,fkc->fqk/dot_general | solution.py:113
  78.9 3.0 %fusion.118 = (f32[2,256]{1,0:T(2,128)}, f32[2,256,256]{1,2,0:T(8,128)}) fusion(bf16[2,256,384]{2,1,0:T(8,128)(2,1)S(1)} %convolution_convert_fusion.14, bf16[2,256,384]{2,1,0:T(8,128)(2,1)} %collective-permute-done.8, bf16[384,384]{1,0:T(8,128)(2,1)S(1)} %copy-done.4), kind=kOutput, calls=%fused_computation.168 | convolution fusion | flops 252116480 | bytes 1607680 | tf_op jit(solution)/shard_map/fqc,fkc->fqk/dot_general | solution.py:113
  81.9 0.5 fusion.115
  82.4 0.5 collective-permute-done.10
  82.9 1.4 %fusion.112 = (f32[2,256]{1,0:T(2,128)S(1)}, f32[2,256,128]{1,2,0:T(8,128)S(1)}) fusion(bf16[2,256,384]{2,1,0:T(8,128)(2,1)S(1)} %convolution_convert_fusion.14, bf16[2,128,384]{2,1,0:T(8,128)(2,1)} %collective-permute-done.10, bf16[384,384]{1,0:T(8,128)(2,1)S(1)} %copy-done.4), kind=kOutput, calls=%fused_computation.166 | convolution fusion | flops 126057984 | bytes 1148928 | tf_op jit(solution)/shard_map/fqc,fkc->fqk/dot_general | solution.py:113
  84.2 0.7 maximum_maximum_fusion.1
  85.0 0.1 fusion.96
  85.1 0.6 fusion.12
  85.7 2.2 %fusion.31 = (f32[2,256]{1,0:T(2,128)S(1)}, f32[2,256]{1,0:T(2,128)S(1)}, f32[2,256]{1,0:T(2,128)S(1)}, f32[2,256]{1,0:T(2,128)S(1)}, f32[2,256]{1,0:T(2,128)S(1...) fusion(f32[2,256,256]{1,2,0:T(8,128)} %get-tuple-element.39, f32[2,256]{1,0:T(2,128)S(1)} %maximum_maximum_fusion.1, ...), kind=kLoop, calls=%fused_computation.82 | loop fusion | flops 1831424 | bytes 3686400 | tf_op jit(solution)/shard_map/reduce_sum | solution.py:124
  88.0 1.4 %fusion.13 = f32[2,256,384]{2,1,0:T(8,128)} fusion(bf16[2,128,384]{2,1,0:T(8,128)(2,1)S(1)} %copy-done.9, bf16[384,384]{1,0:T(8,128)(2,1)S(1)} %copy-done, f32[2,256,128]{1,2,0:T(8,128)S(1)} %get-tuple-element.25, f32[2,256]{1,0:T(2,128)S(1)} %maximum_maximum_fusion.1), kind=kOutput, calls=%fused_computation.55 | convolution fusion | flops 126058496 | bytes 1542144 | tf_op jit(solution)/shard_map/fqk,fkc->fqc/dot_general | solution.py:125
  89.4 2.3 %fusion.14 = f32[2,256,384]{2,1,0:T(8,128)} fusion(bf16[2,128,384]{2,1,0:T(8,128)(2,1)} %collective-permute-done.10, bf16[384,384]{1,0:T(8,128)(2,1)S(1)} %copy-done, f32[2,256,128]{1,2,0:T(8,128)S(1)} %get-tuple-element.23, f32[2,256]{1,0:T(2,128)S(1)} %maximum_maximum_fusion.1), kind=kOutput, calls=%fused_computation.56 | convolution fusion | flops 126058496 | bytes 1542144 | tf_op jit(solution)/shard_map/fqk,fkc->fqc/dot_general | solution.py:125
  91.7 1.8 %convolution_add_fusion.5 = f32[2,256,384]{2,1,0:T(8,128)S(1)} fusion(f32[2,256,384]{2,1,0:T(8,128)S(1)} %fusion.12, bf16[2,256,384]{2,1,0:T(8,128)(2,1)} %copy-done.12, bf16[384,384]{1,0:T(8,128)(2,1)S(1)} %copy-done, f32[2,256,256]{1,2,0:T(8,128)} %get-tuple-element.39, f32[2,256]{1,0:T(2,128)S(1)} %maximum_maximum_fusion.1), kind=kOutput, calls=%fused_computation.14 | convolution fusion | flops 252313600 | bytes 2787328 | tf_op jit(solution)/shard_map/fqk,fkc->fqc/dot_general | solution.py:125
  93.5 1.7 %convolution_add_fusion.4 = f32[2,256,384]{2,1,0:T(8,128)S(1)} fusion(f32[2,256,384]{2,1,0:T(8,128)S(1)} %convolution_add_fusion.5, bf16[2,256,384]{2,1,0:T(8,128)(2,1)} %collective-permute-done.4, bf16[384,384]{1,0:T(8,128)(2,1)S(1)} %copy-done, f32[2,256,256]{1,2,0:T(8,128)S(1)} %get-tuple-element.35, f32[2,256]{1,0:T(2,128)S(1)} %maximum_maximum_fusion.1), kind=kOutput, calls=%fused_computation.13 | convolution fusion | flops 252313600 | bytes 2787328 | tf_op jit(solution)/shard_map/fqk,fkc->fqc/dot_general | solution.py:125
  95.2 1.8 %convolution_add_fusion.3 = f32[2,256,384]{2,1,0:T(8,128)S(1)} fusion(f32[2,256,384]{2,1,0:T(8,128)S(1)} %convolution_add_fusion.4, bf16[2,256,384]{2,1,0:T(8,128)(2,1)} %collective-permute-done.5, bf16[384,384]{1,0:T(8,128)(2,1)S(1)} %copy-done, f32[2,256,256]{1,2,0:T(8,128)} %get-tuple-element.33, f32[2,256]{1,0:T(2,128)S(1)} %maximum_maximum_fusion.1), kind=kOutput, calls=%fused_computation.12 | convolution fusion | flops 252313600 | bytes 2787328 | tf_op jit(solution)/shard_map/fqk,fkc->fqc/dot_general | solution.py:125
  97.0 1.7 %convolution_add_fusion.2 = f32[2,256,384]{2,1,0:T(8,128)S(1)} fusion(f32[2,256,384]{2,1,0:T(8,128)S(1)} %convolution_add_fusion.3, bf16[2,256,384]{2,1,0:T(8,128)(2,1)} %collective-permute-done.6, bf16[384,384]{1,0:T(8,128)(2,1)S(1)} %copy-done, f32[2,256,256]{1,2,0:T(8,128)S(1)} %copy-done.2, f32[2,256]{1,0:T(2,128)S(1)} %maximum_maximum_fusion.1), kind=kOutput, calls=%fused_computation.11 | convolution fusion | flops 252313600 | bytes 2787328 | tf_op jit(solution)/shard_map/fqk,fkc->fqc/dot_general | solution.py:125
  98.8 2.6 %convolution_add_fusion.1 = f32[2,256,384]{2,1,0:T(8,128)} fusion(f32[2,256,384]{2,1,0:T(8,128)S(1)} %convolution_add_fusion.2, bf16[2,256,384]{2,1,0:T(8,128)(2,1)} %copy-done.5, bf16[384,384]{1,0:T(8,128)(2,1)S(1)} %copy-done, f32[2,256,256]{1,2,0:T(8,128)S(1)} %copy-done.3, f32[2,256]{1,0:T(2,128)S(1)} %maximum_maximum_fusion.1), kind=kOutput, calls=%fused_computation.10 | convolution fusion | flops 252313600 | bytes 2787328 | tf_op jit(solution)/shard_map/fqk,fkc->fqc/dot_general | solution.py:125
  101.4 2.2 %fusion.11 = bf16[2,256,384]{2,1,0:T(8,128)(2,1)S(1)} fusion(f32[2,256,384]{2,1,0:T(8,128)} %fusion.14, f32[2,256,384]{2,1,0:T(8,128)S(1)} %copy-done.10, f32[2,256,384]{2,1,0:T(8,128)} %convolution_add_fusion.1, bf16[2,256,384]{2,1,0:T(8,128)(2,1)} %collective-permute-done.8, f32[2,256]{1,0:T(2,128)S(1)} %add_add_fusion, bf16[384,384]{1,0:T(8,128)(2,1)S(1)} %copy-done, ...), kind=kOutput, calls=%fused_computation.19 | convolution fusion | flops 253100032 | bytes 3969024 | tf_op jit(solution)/shard_map/fqk,fkc->fqc/dot_general | solution.py:125
  103.6 0.4 fusion.43
  104.0 0.8 fusion.28
  (56 shorter events, 0.3 us)
Async XLA Ops:
  0.0 85.1 %copy-start = (bf16[384,384]{1,0:T(8,128)(2,1)S(1)}, bf16[384,384]{1,0:T(8,128)(2,1)}, u32[]{:S(2)}) copy-start(bf16[384,384]{1,0:T(8,128)(2,1)} %param.18) | copy-start | bytes 884740
  2.5 15.1 %copy-start.15 = (s32[2,2]{1,0:T(2,128)S(1)}, s32[2,2]{1,0:T(2,128)}, u32[]{:S(2)}) copy-start(s32[2,2]{1,0:T(2,128)} %param.11) | copy-start | bytes 52
  2.6 13.8 %collective-permute-start = (bf16[2,1,130,384]{3,2,1,0:T(8,128)(2,1)S(1)}, bf16[2,1,130,384]{3,2,1,0:T(8,128)(2,1)S(1)}, u32[]{:S(2)}, u32[]{:S(2)}) collective-permute-start(bf16[2,1,130,384]{3,2,1,0:T(8,128)(2,1)S(1)} %get-tuple-element.18), channel_id=1, source_target_pairs={{0,1},{1,2},{2,3},{3,4},{4,5},{5,6},{6,7},{8,9},{9,10},{10,11},{11... | collective-permute-start | bytes 599048 | tf_op jit(solution)/shard_map/ppermute | solution.py:15
  7.5 8.9 %collective-permute-start.1 = (bf16[2,1,130,384]{3,2,1,0:T(8,128)(2,1)S(1)}, bf16[2,1,130,384]{3,2,1,0:T(8,128)(2,1)S(1)}, u32[]{:S(2)}, u32[]{:S(2)}) collective-permute-start(bf16[2,1,130,384]{3,2,1,0:T(8,128)(2,1)S(1)} %get-tuple-element.19), channel_id=1, source_target_pairs={{1,0},{2,1},{3,2},{4,3},{5,4},{6,5},{7,6},{9,8},{10,9},{11,10},{12... | collective-permute-start | bytes 599048 | tf_op jit(solution)/shard_map/ppermute | solution.py:17
  16.4 0.7 copy-start.6
  17.2 2.8 %copy-start.7 = (bf16[2,1,130,384]{3,2,1,0:T(8,128)(2,1)S(1)}, bf16[2,1,130,384]{3,2,1,0:T(8,128)(2,1)}, u32[]{:S(2)}) copy-start(bf16[2,1,130,384]{3,2,1,0:T(8,128)(2,1)} %copy-done.6) | copy-start | bytes 599044
  17.6 2.4 %collective-permute-start.2 = (bf16[2,4,130,384]{3,1,2,0:T(4,128)(2,1)S(1)}, bf16[2,4,130,384]{3,1,2,0:T(4,128)(2,1)S(1)}, u32[]{:S(2)}, u32[]{:S(2)}) collective-permute-start(bf16[2,4,130,384]{3,1,2,0:T(4,128)(2,1)S(1)} %copy.50), channel_id=1, source_target_pairs={{0,8},{8,0},{1,9},{9,1},{2,10},{10,2},{3,11},{11,3},{4,12},{12,4},... | collective-permute-start | bytes 2396168 | tf_op jit(solution)/shard_map/ppermute | solution.py:73
  22.9 9.3 %slice-start = ((s8[7962624]{0:T(1024)(128)(4,1)}), s8[4194304]{0:T(1024)(128)(4,1)S(1)}, s32[]{:S(2)}) async-start(s8[7962624]{0:T(1024)(128)(4,1)} %bitcast.142), calls=%async_computation | async-start | bytes 8388608
  27.3 4.9 %slice-start.1 = ((s8[7962624]{0:T(1024)(128)(4,1)}), s8[3768320]{0:T(1024)(128)(4,1)S(1)}, s32[]{:S(2)}) async-start(s8[7962624]{0:T(1024)(128)(4,1)} %bitcast.142), calls=%async_computation.1 | async-start | bytes 7536640
  29.4 2.8 %copy-start.18 = (pred[16,17]{0,1:T(8,128)(4,1)S(1)}, pred[16,17]{0,1:T(8,128)(4,1)}, u32[]{:S(2)}) copy-start(pred[16,17]{0,1:T(8,128)(4,1)} %constant.100) | copy-start | bytes 820
  38.2 1.0 copy-start.1
  38.2 1.0 copy-start.16
  38.2 1.2 %copy-start.17 = (f32[384]{0:T(512)S(1)}, f32[384]{0:T(512)}, u32[]{:S(2)}) copy-start(f32[384]{0:T(512)} %param.15) | copy-start | bytes 4612
  38.3 4.8 %copy-start.13 = (bf16[384,384]{1,0:T(8,128)(2,1)S(1)}, bf16[384,384]{1,0:T(8,128)(2,1)}, u32[]{:S(2)}) copy-start(bf16[384,384]{1,0:T(8,128)(2,1)} %param.16) | copy-start | bytes 884740
  38.7 4.8 %copy-start.4 = (bf16[384,384]{1,0:T(8,128)(2,1)S(1)}, bf16[384,384]{1,0:T(8,128)(2,1)}, u32[]{:S(2)}) copy-start(bf16[384,384]{1,0:T(8,128)(2,1)} %param.17) | copy-start | bytes 884740
  39.6 12.1 %collective-permute-start.3 = (bf16[2,256,384]{2,1,0:T(8,128)(2,1)S(1)}, bf16[2,256,384]{2,1,0:T(8,128)(2,1)S(1)}, u32[]{:S(2)}, u32[]{:S(2)}) collective-permute-start(bf16[2,256,384]{2,1,0:T(8,128)(2,1)S(1)} %bitcast.135), channel_id=1, source_target_pairs={{0,2},{2,4},{4,6},{6,7},{7,5},{5,3},{3,1},{1,0},{8,10},{10,12},{12... | collective-permute-start | bytes 1179656 | tf_op jit(solution)/shard_map/ppermute | solution.py:33
  43.1 11.2 %collective-permute-start.4 = (bf16[2,256,384]{2,1,0:T(8,128)(2,1)S(1)}, bf16[2,256,384]{2,1,0:T(8,128)(2,1)}, u32[]{:S(2)}, u32[]{:S(2)}) collective-permute-start(bf16[2,256,384]{2,1,0:T(8,128)(2,1)S(1)} %bitcast.136), channel_id=1, source_target_pairs={{0,1},{2,0},{4,2},{6,4},{7,6},{5,7},{3,5},{1,3},{8,9},{10,8},{12,1... | collective-permute-start | bytes 1179656 | tf_op jit(solution)/shard_map/ppermute | solution.py:34
  51.8 6.8 %copy-start.12 = (bf16[2,256,384]{2,1,0:T(8,128)(2,1)}, bf16[2,256,384]{2,1,0:T(8,128)(2,1)S(1)}, u32[]{:S(2)}) copy-start(bf16[2,256,384]{2,1,0:T(8,128)(2,1)S(1)} %collective-permute-done.3) | copy-start | bytes 1179652
  51.8 10.6 %collective-permute-start.5 = (bf16[2,256,384]{2,1,0:T(8,128)(2,1)S(1)}, bf16[2,256,384]{2,1,0:T(8,128)(2,1)}, u32[]{:S(2)}, u32[]{:S(2)}) collective-permute-start(bf16[2,256,384]{2,1,0:T(8,128)(2,1)S(1)} %collective-permute-done.3), channel_id=1, source_target_pairs={{0,2},{2,4},{4,6},{6,7},{7,5},{5,3},{3,1},{1,0},{8,10},{10,12},{12... | collective-permute-start | bytes 1179656 | tf_op jit(solution)/shard_map/ppermute | solution.py:33
  54.2 10.5 %collective-permute-start.6 = (bf16[2,256,384]{2,1,0:T(8,128)(2,1)}, bf16[2,256,384]{2,1,0:T(8,128)(2,1)}, u32[]{:S(2)}, u32[]{:S(2)}) collective-permute-start(bf16[2,256,384]{2,1,0:T(8,128)(2,1)} %collective-permute-done.4), channel_id=1, source_target_pairs={{0,1},{2,0},{4,2},{6,4},{7,6},{5,7},{3,5},{1,3},{8,9},{10,8},{12,1... | collective-permute-start | bytes 1179656 | tf_op jit(solution)/shard_map/ppermute | solution.py:34
  62.4 9.8 %collective-permute-start.7 = (bf16[2,256,384]{2,1,0:T(8,128)(2,1)}, bf16[2,256,384]{2,1,0:T(8,128)(2,1)S(1)}, u32[]{:S(2)}, u32[]{:S(2)}) collective-permute-start(bf16[2,256,384]{2,1,0:T(8,128)(2,1)} %collective-permute-done.5), channel_id=1, source_target_pairs={{0,2},{2,4},{4,6},{6,7},{7,5},{5,3},{3,1},{1,0},{8,10},{10,12},{12... | collective-permute-start | bytes 1179656 | tf_op jit(solution)/shard_map/ppermute | solution.py:33
  64.8 10.5 %collective-permute-start.8 = (bf16[2,256,384]{2,1,0:T(8,128)(2,1)}, bf16[2,256,384]{2,1,0:T(8,128)(2,1)}, u32[]{:S(2)}, u32[]{:S(2)}) collective-permute-start(bf16[2,256,384]{2,1,0:T(8,128)(2,1)} %collective-permute-done.6), channel_id=1, source_target_pairs={{0,1},{2,0},{4,2},{6,4},{7,6},{5,7},{3,5},{1,3},{8,9},{10,8},{12,1... | collective-permute-start | bytes 1179656 | tf_op jit(solution)/shard_map/ppermute | solution.py:34
  72.2 9.7 %copy-start.5 = (bf16[2,256,384]{2,1,0:T(8,128)(2,1)}, bf16[2,256,384]{2,1,0:T(8,128)(2,1)S(1)}, u32[]{:S(2)}) copy-start(bf16[2,256,384]{2,1,0:T(8,128)(2,1)S(1)} %collective-permute-done.7) | copy-start | bytes 1179652
  73.0 8.9 %collective-permute-start.9 = (bf16[2,128,384]{2,1,0:T(8,128)(2,1)}, bf16[2,128,384]{2,1,0:T(8,128)(2,1)S(1)}, u32[]{:S(2)}, u32[]{:S(2)}) collective-permute-start(bf16[2,128,384]{2,1,0:T(8,128)(2,1)} %slice.30), channel_id=1, source_target_pairs={{0,2},{2,4},{4,6},{6,7},{7,5},{5,3},{3,1},{1,0},{8,10},{10,12},{12... | collective-permute-start | bytes 589832 | tf_op jit(solution)/shard_map/ppermute | solution.py:38
  76.9 6.0 %collective-permute-start.10 = (bf16[2,128,384]{2,1,0:T(8,128)(2,1)}, bf16[2,128,384]{2,1,0:T(8,128)(2,1)}, u32[]{:S(2)}, u32[]{:S(2)}) collective-permute-start(bf16[2,128,384]{2,1,0:T(8,128)(2,1)} %slice.31), channel_id=1, source_target_pairs={{0,1},{2,0},{4,2},{6,4},{7,6},{5,7},{3,5},{1,3},{8,9},{10,8},{12,1... | collective-permute-start | bytes 589832 | tf_op jit(solution)/shard_map/ppermute | solution.py:39
  81.9 3.2 %copy-start.8 = (bf16[2,128,384]{2,1,0:T(8,128)(2,1)}, bf16[2,128,384]{2,1,0:T(8,128)(2,1)S(1)}, u32[]{:S(2)}) copy-start(bf16[2,128,384]{2,1,0:T(8,128)(2,1)S(1)} %collective-permute-done.9) | copy-start | bytes 589828
  85.7 2.3 %copy-start.9 = (bf16[2,128,384]{2,1,0:T(8,128)(2,1)S(1)}, bf16[2,128,384]{2,1,0:T(8,128)(2,1)}, u32[]{:S(2)}) copy-start(bf16[2,128,384]{2,1,0:T(8,128)(2,1)} %copy-done.8) | copy-start | bytes 589828
  93.5 3.5 %copy-start.2 = (f32[2,256,256]{1,2,0:T(8,128)S(1)}, f32[2,256,256]{1,2,0:T(8,128)}, u32[]{:S(2)}) copy-start(f32[2,256,256]{1,2,0:T(8,128)} %get-tuple-element.31) | copy-start | bytes 1572868
  97.0 1.7 %copy-start.3 = (f32[2,256,256]{1,2,0:T(8,128)S(1)}, f32[2,256,256]{1,2,0:T(8,128)}, u32[]{:S(2)}) copy-start(f32[2,256,256]{1,2,0:T(8,128)} %get-tuple-element.29) | copy-start | bytes 1572868
  98.7 2.7 %copy-start.10 = (f32[2,256,384]{2,1,0:T(8,128)S(1)}, f32[2,256,384]{2,1,0:T(8,128)}, u32[]{:S(2)}) copy-start(f32[2,256,384]{2,1,0:T(8,128)} %fusion.13) | copy-start | bytes 2359300
  98.8 2.6 %copy-start.11 = (f32[2,256,256]{1,2,0:T(8,128)S(1)}, f32[2,256,256]{1,2,0:T(8,128)}, u32[]{:S(2)}) copy-start(f32[2,256,256]{1,2,0:T(8,128)} %get-tuple-element.27) | copy-start | bytes 1572868
  101.4 2.2 %copy-start.14 = (bf16[384,384]{1,0:T(8,128)(2,1)S(1)}, bf16[384,384]{1,0:T(8,128)(2,1)}, u32[]{:S(2)}) copy-start(bf16[384,384]{1,0:T(8,128)(2,1)} %param.19) | copy-start | bytes 884740

commit v8 on v6

--- a/solution.py
+++ b/solution.py
@@ -1,6 +1,7 @@
 import jax
 import jax.numpy as jnp
 from jax import lax
+from jax.experimental import pallas as pl
 from jax.sharding import PartitionSpec as P
 
 
@@ -41,6 +42,43 @@
         )
         pieces += [front, back]
     return jnp.concatenate(pieces, axis=dim)
+
+
+def attend_kernel(query_ref, key_ref, value_ref, out_ref, *, scale):
+    scores = (
+        lax.dot_general(
+            query_ref[0],
+            key_ref[0],
+            (((1,), (1,)), ((), ())),
+            preferred_element_type=jnp.float32,
+        )
+        * scale
+    )
+    peaks = jnp.max(scores, axis=-1, keepdims=True)
+    weights_exp = jnp.exp(scores - peaks)
+    totals = jnp.sum(weights_exp, axis=-1, keepdims=True)
+    summed = jnp.dot(
+        weights_exp.astype(jnp.bfloat16), value_ref[0], preferred_element_type=jnp.float32
+    )
+    out_ref[0] = (summed / totals).astype(out_ref.dtype)
+
+
+def attend(queries, keys_all, values_all, scale):
+    spans, query_rows, channels = queries.shape
+    key_rows = keys_all.shape[1]
+    block = 128 if query_rows % 128 == 0 else query_rows
+    kernel = lambda *refs: attend_kernel(*refs, scale=scale)
+    return pl.pallas_call(
+        kernel,
+        grid=(spans, query_rows // block),
+        in_specs=[
+            pl.BlockSpec((1, block, channels), lambda f, q: (f, q, 0)),
+            pl.BlockSpec((1, key_rows, channels), lambda f, q: (f, 0, 0)),
+            pl.BlockSpec((1, key_rows, channels), lambda f, q: (f, 0, 0)),
+        ],
+        out_specs=pl.BlockSpec((1, block, channels), lambda f, q: (f, q, 0)),
+        out_shape=jax.ShapeDtypeStruct(queries.shape, jnp.bfloat16),
+    )(queries, keys_all, values_all)
 
 
 def rms_scaled(frames, gain):
@@ -107,20 +145,7 @@
     values_all = jnp.einsum(
         "ftc,cd->ftd", tokens_all, value_weight, preferred_element_type=jnp.float32
     ).astype(jnp.bfloat16)
-    scores = (
-        jnp.einsum("fqc,fkc->fqk", queries, keys_all, preferred_element_type=jnp.float32)
-        * score_scale
-    )
-    peaks = jnp.max(scores, axis=-1, keepdims=True)
-    weights_exp = jnp.exp(scores - peaks)
-    totals = jnp.sum(weights_exp, axis=-1)
-    summed = jnp.einsum(
-        "fqk,fkc->fqc",
-        weights_exp.astype(jnp.bfloat16),
-        values_all,
-        preferred_element_type=jnp.float32,
-    )
-    attended = (summed / totals[:, :, None]).astype(jnp.bfloat16)
+    attended = attend(queries, keys_all, values_all, score_scale)
     projected = jnp.einsum("ftc,cd->ftd", attended, out_weight, preferred_element_type=jnp.float32)
     encoded = mixed.astype(jnp.float32) + projected.reshape(
         span_count, row_count, col_count, channels

time: 98 us -> 102 us (1.041)
  other arithmetic: 14.6 us -> 4.75 us
  Pallas kernels: 0 us -> 8.25 us
  matrix products: 20.2 us -> 26.4 us
  waiting for transfers between devices: 32.1 us -> 37.4 us
  local copies, waits for them, and re-layouts: 13.4 us -> 8.42 us
    ppermute x3, waiting for transfers between devices: 0.01 us -> 24.2 us  [ring_gather(): backward = lax.ppermute(backward, axis, behind)]
    ppermute x3, waiting for transfers between devices: 19.4 us -> 0.01 us  [ring_gather(): forward = lax.ppermute(forward, axis, ahead)]
    conv_general_dilated x1, matrix products: 5.99 us -> 16.3 us  [shards(): lax.conv_general_dilated(window, conv_weight, window_strides=(1, 1, 1), p...]
    pallas_call x0 -> x1, Pallas kernels: none -> 8.25 us  [attend(): pl.pallas_call(kernel, grid=(spans, query_rows // block), in_specs=[pl.Bl...]
    unnamed x30 -> x24, local copies, waits for them, and re-layouts: 6.53 us -> 0.5 us
    dot_general x2, matrix products: 13.4 us -> 7.51 us  [the longest x1 3.77 us: shards(): jnp.einsum('ftc,cd->ftd', tokens_all, value_weight, preferred_element_typ...]
    ppermute x3, starting transfers between devices: 8.31 us -> 3.81 us  [ring_gather(): forward = lax.ppermute(forward, axis, ahead)]
    select_n x2, other arithmetic: 4.36 us -> 0.35 us  [shards(): jnp.take(pool, picks.reshape(-1), axis=0)]
  transfers between devices with their start and end apart: 11 -> 11, of which waited for: 7 -> 6; matrix products, arithmetic and copies ran while one was open for 7% -> 2% of each run, Pallas kernels for 0% -> 0%
where the time goes in v8:
time: 102 us
  waiting for transfers between devices  37.4 us (37%)
  matrix products  26.4 us (26%)
  starting transfers between devices  16.2 us (16%)
  local copies, waits for them, and re-layouts  8.42 us (8%)
  Pallas kernels  8.25 us (8%)
  other arithmetic  4.75 us (5%)
    ppermute x3, waiting for transfers between devices, ring_gather(): backward = lax.ppermute(backward, axis, behind)  24.2 us
    conv_general_dilated x1, matrix products, shards(): lax.conv_general_dilated(window, conv_weight, window_strides=(1, 1, 1), p...  16.3 us
    pallas_call x1, Pallas kernels, attend(): pl.pallas_call(kernel, grid=(spans, query_rows // block), in_specs=[pl.Bl...  8.25 us
    ppermute x1, waiting for transfers between devices, padded_2(): lax.ppermute(tail, axis, [(i, (i + 1) % count) for i in range(ends)])  7.49 us
    gather x2, local copies, waits for them, and re-layouts, shards(): jnp.take(pool, picks.reshape(-1), axis=0)  6.3 us
    ppermute x1, starting transfers between devices, padded_2(): lax.ppermute(tail, axis, [(i, (i + 1) % count) for i in range(ends)])  4.88 us
    ppermute x3, starting transfers between devices, ring_gather(): forward = lax.ppermute(forward, axis, ahead)  3.81 us
    ppermute x1, waiting for transfers between devices, ring_gather(): lax.ppermute(lax.slice_in_dim(forward, 0, half, axis=dim), axis, ahead)  3.79 us
  transfers between devices with their start and end apart: 11, of which 6 were waited for; matrix products, arithmetic and copies ran while one was open for 2% of the time, Pallas kernels for 0%

profile of v8, /device:TPU:0, one launch (start us, length us, event | category | flops | bytes accessed | tf_op | source)
XLA Modules:
  0.0 101.7 jit_solution(2658314618164100041)
XLA Ops:
  0.0 0.0 copy-start
  0.0 1.2 %fusion.2 = f32[2,2,128]{2,1,0:T(2,128)S(1)} fusion(bf16[2,2,128,384]{3,2,1,0:T(8,128)(2,1)} %param.10), kind=kLoop, calls=%fused_computation.15 | loop fusion | flops 589312 | bytes 395264 | tf_op jit(solution)/shard_map/reduce_sum | solution.py:86
  1.2 1.3 %fusion.9 = bf16[2,2,128,384]{3,2,1,0:T(8,128)(2,1)S(1)} fusion(bf16[2,2,128,384]{3,2,1,0:T(8,128)(2,1)} %param.10, f32[384]{0:T(512)} %param.12, f32[2,2,128]{2,1,0:T(2,128)S(1)} %add_rsqrt_fusion.1), kind=kLoop, calls=%fused_computation.22 | loop fusion | flops 1572864 | bytes 790016 | tf_op jit(solution)/shard_map/convert_element_type | solution.py:103
  2.5 0.1 pad_slice_fusion.1
  2.6 4.9 %collective-permute-start = (bf16[2,1,130,384]{3,2,1,0:T(8,128)(2,1)S(1)}, bf16[2,1,130,384]{3,2,1,0:T(8,128)(2,1)S(1)}, u32[]{:S(2)}, u32[]{:S(2)}) collective-permute-start(bf16[2,1,130,384]{3,2,1,0:T(8,128)(2,1)S(1)} %get-tuple-element.9), channel_id=1, source_target_pairs={{0,1},{1,2},{2,3},{3,4},{4,5},{5,6},{6,7},{8,9},{9,10},{10,11},{11... | collective-permute-start | bytes 599048 | tf_op jit(solution)/shard_map/ppermute | solution.py:16
  7.5 1.3 %collective-permute-start.1 = (bf16[2,1,130,384]{3,2,1,0:T(8,128)(2,1)S(1)}, bf16[2,1,130,384]{3,2,1,0:T(8,128)(2,1)S(1)}, u32[]{:S(2)}, u32[]{:S(2)}) collective-permute-start(bf16[2,1,130,384]{3,2,1,0:T(8,128)(2,1)S(1)} %get-tuple-element.10), channel_id=1, source_target_pairs={{1,0},{2,1},{3,2},{4,3},{5,4},{6,5},{7,6},{9,8},{10,9},{11,10},{12... | collective-permute-start | bytes 599048 | tf_op jit(solution)/shard_map/ppermute | solution.py:18
  8.8 0.1 pad.4
  8.9 7.5 %collective-permute-done = bf16[2,1,130,384]{3,2,1,0:T(8,128)(2,1)S(1)} collective-permute-done((bf16[2,1,130,384]{3,2,1,0:T(8,128)(2,1)S(1)}, bf16[2,1,130,384]{3,2,1,0:T(8,128)(2,1)S(1)}, u32[]{:S(2)}, u32[]{:S(2)}) %collective-permute-start) | collective-permute-done | bytes 199712 | tf_op jit(solution)/shard_map/ppermute | solution.py:16
  16.4 0.0 collective-permute-done.1
  16.4 0.1 pad_maximum_fusion
  16.6 0.3 copy.26
  16.9 0.1 collective-permute-start.2
  17.0 0.0 copy-done.5
  17.0 0.1 compare_select_fusion.7
  17.1 0.1 compare_and_fusion
  17.2 0.1 reshape.65
  17.2 0.1 pad.9.clone
  17.3 1.9 %collective-permute-done.2 = bf16[2,4,130,384]{3,1,2,0:T(4,128)(2,1)S(1)} collective-permute-done((bf16[2,4,130,384]{3,1,2,0:T(4,128)(2,1)S(1)}, bf16[2,4,130,384]{3,1,2,0:T(4,128)(2,1)S(1)}, u32[]{:S(2)}, u32[]{:S(2)}) %collective-permute-start.2) | collective-permute-done | bytes 798752 | tf_op jit(solution)/shard_map/ppermute | solution.py:111
  19.3 0.1 copy.27
  19.4 0.4 maximum_maximum_fusion
  19.7 0.8 copy.28
  20.5 4.3 %gather_fusion = bf16[6,4,130,384]{3,1,2,0:T(4,128)(2,1)} fusion(bf16[5,4,130,384]{3,1,2,0:T(4,128)(2,1)S(1)} %copy.28, s32[1024]{0:T(1024)S(1)} %pad_clamp_fusion), kind=kCustom, calls=%fused_computation | custom fusion | bytes 4792344 | tf_op jit(solution)/shard_map/jit(_take)/gather | solution.py:123
  24.8 2.0 %copy.29 = bf16[6,4,130,384]{3,2,1,0:T(8,128)(2,1)S(1)} copy(bf16[6,4,130,384]{3,1,2,0:T(4,128)(2,1)} %gather_fusion) | data formatting | bytes 4792320 | tf_op jit(solution)/shard_map/jit(_take)/gather | solution.py:123
  26.8 0.3 broadcast_select_fusion
  27.2 0.0 copy-start.1
  27.2 0.0 copy-start.6
  27.2 0.0 copy-start.7
  27.2 16.3 %fusion = f32[2,1,2,128,384]{4,0,3,2,1:T(2,128)S(1)} fusion(bf16[3,3,3,384,384]{4,3,2,1,0:T(8,128)(2,1)} %param.13, bf16[2,3,4,130,384]{4,3,2,1,0:T(8,128)(2,1)S(1)} %broadcast_select_fusion), kind=kOutput, calls=%fused_computation.4 | convolution fusion | flops 4076863488 | bytes 11145216 | tf_op jit(solution)/shard_map/conv_general_dilated | solution.py:126
  43.5 0.0 copy-done.1
  43.6 0.0 copy-start.3
  43.6 0.2 fusion.12
  43.8 0.0 copy-done.7
  43.8 0.2 fusion.14
  44.0 2.5 %collective-permute-start.4 = (bf16[2,256,384]{2,1,0:T(8,128)(2,1)S(1)}, bf16[2,256,384]{2,1,0:T(8,128)(2,1)S(1)}, u32[]{:S(2)}, u32[]{:S(2)}) collective-permute-start(bf16[2,256,384]{2,1,0:T(8,128)(2,1)S(1)} %bitcast.27), channel_id=1, source_target_pairs={{0,1},{2,0},{4,2},{6,4},{7,6},{5,7},{3,5},{1,3},{8,9},{10,8},{12,1... | collective-permute-start | bytes 1179656 | tf_op jit(solution)/shard_map/ppermute | solution.py:35
  46.5 1.0 %collective-permute-start.3 = (bf16[2,256,384]{2,1,0:T(8,128)(2,1)S(1)}, bf16[2,256,384]{2,1,0:T(8,128)(2,1)S(1)}, u32[]{:S(2)}, u32[]{:S(2)}) collective-permute-start(bf16[2,256,384]{2,1,0:T(8,128)(2,1)S(1)} %bitcast.28), channel_id=1, source_target_pairs={{0,2},{2,4},{4,6},{6,7},{7,5},{5,3},{3,1},{1,0},{8,10},{10,12},{12... | collective-permute-start | bytes 1179656 | tf_op jit(solution)/shard_map/ppermute | solution.py:34
  47.5 9.3 %collective-permute-done.4 = bf16[2,256,384]{2,1,0:T(8,128)(2,1)S(1)} collective-permute-done((bf16[2,256,384]{2,1,0:T(8,128)(2,1)S(1)}, bf16[2,256,384]{2,1,0:T(8,128)(2,1)S(1)}, u32[]{:S(2)}, u32[]{:S(2)}) %collective-permute-start.4) | collective-permute-done | bytes 393248 | tf_op jit(solution)/shard_map/ppermute | solution.py:35
  56.9 0.8 collective-permute-start.6
  57.6 0.0 collective-permute-done.3
  57.6 1.2 %collective-permute-start.5 = (bf16[2,256,384]{2,1,0:T(8,128)(2,1)S(1)}, bf16[2,256,384]{2,1,0:T(8,128)(2,1)S(1)}, u32[]{:S(2)}, u32[]{:S(2)}) collective-permute-start(bf16[2,256,384]{2,1,0:T(8,128)(2,1)S(1)} %collective-permute-done.3), channel_id=1, source_target_pairs={{0,2},{2,4},{4,6},{6,7},{7,5},{5,3},{3,1},{1,0},{8,10},{10,12},{12... | collective-permute-start | bytes 1179656 | tf_op jit(solution)/shard_map/ppermute | solution.py:34
  58.9 0.0 copy-done.3
  58.9 1.1 %convolution_convert_fusion.2.refs_0_ = bf16[2,256,384]{2,1,0:T(8,128)(2,1)} fusion(bf16[2,256,384]{2,1,0:T(8,128)(2,1)S(1)} %bitcast.30, bf16[384,384]{1,0:T(8,128)(2,1)S(1)} %copy-done.3), kind=kOutput, calls=%fused_computation.7 | convolution fusion | flops 151191552 | bytes 1081344 | tf_op jit(solution)/shard_map/ftc,cd->ftd/dot_general | solution.py:137
  60.1 7.4 %collective-permute-done.6 = bf16[2,256,384]{2,1,0:T(8,128)(2,1)S(1)} collective-permute-done((bf16[2,256,384]{2,1,0:T(8,128)(2,1)S(1)}, bf16[2,256,384]{2,1,0:T(8,128)(2,1)S(1)}, u32[]{:S(2)}, u32[]{:S(2)}) %collective-permute-start.6) | collective-permute-done | bytes 393248 | tf_op jit(solution)/shard_map/ppermute | solution.py:35
  67.5 0.5 collective-permute-start.8
  68.0 0.0 collective-permute-done.5
  68.0 1.6 %collective-permute-start.7 = (bf16[2,256,384]{2,1,0:T(8,128)(2,1)S(1)}, bf16[2,256,384]{2,1,0:T(8,128)(2,1)S(1)}, u32[]{:S(2)}, u32[]{:S(2)}) collective-permute-start(bf16[2,256,384]{2,1,0:T(8,128)(2,1)S(1)} %collective-permute-done.5), channel_id=1, source_target_pairs={{0,2},{2,4},{4,6},{6,7},{7,5},{5,3},{3,1},{1,0},{8,10},{10,12},{12... | collective-permute-start | bytes 1179656 | tf_op jit(solution)/shard_map/ppermute | solution.py:34
  69.5 0.1 constant_dynamic-update-slice_fusion.7
  69.6 0.1 constant_dynamic-update-slice_fusion.6
  69.7 0.1 constant_dynamic-update-slice_fusion.5
  69.7 0.1 constant_dynamic-update-slice_fusion.4
  69.8 7.4 %collective-permute-done.8 = bf16[2,256,384]{2,1,0:T(8,128)(2,1)S(1)} collective-permute-done((bf16[2,256,384]{2,1,0:T(8,128)(2,1)S(1)}, bf16[2,256,384]{2,1,0:T(8,128)(2,1)S(1)}, u32[]{:S(2)}, u32[]{:S(2)}) %collective-permute-start.8) | collective-permute-done | bytes 393248 | tf_op jit(solution)/shard_map/ppermute | solution.py:35
  77.3 0.3 collective-permute-start.10
  77.6 0.0 collective-permute-done.7
  77.6 2.0 %collective-permute-start.9 = (bf16[2,128,384]{2,1,0:T(8,128)(2,1)S(1)}, bf16[2,128,384]{2,1,0:T(8,128)(2,1)S(1)}, u32[]{:S(2)}, u32[]{:S(2)}) collective-permute-start(bf16[2,128,384]{2,1,0:T(8,128)(2,1)S(1)} %slice.26), channel_id=1, source_target_pairs={{0,2},{2,4},{4,6},{6,7},{7,5},{5,3},{3,1},{1,0},{8,10},{10,12},{12... | collective-permute-start | bytes 589832 | tf_op jit(solution)/shard_map/ppermute | solution.py:39
  79.6 0.1 constant_dynamic-update-slice_fusion.3
  79.7 0.1 constant_dynamic-update-slice_fusion.2
  79.8 3.8 %collective-permute-done.9 = bf16[2,128,384]{2,1,0:T(8,128)(2,1)S(1)} collective-permute-done((bf16[2,128,384]{2,1,0:T(8,128)(2,1)S(1)}, bf16[2,128,384]{2,1,0:T(8,128)(2,1)S(1)}, u32[]{:S(2)}, u32[]{:S(2)}) %collective-permute-start.9) | collective-permute-done | bytes 196640 | tf_op jit(solution)/shard_map/ppermute | solution.py:39
  83.6 0.0 collective-permute-done.10
  83.7 0.0 copy-done
  83.7 0.0 copy-start.2
  83.7 3.8 %convolution_convert_fusion.refs_2_ = bf16[2,2048,384]{2,1,0:T(8,128)(2,1)} fusion(bf16[2,2048,384]{2,1,0:T(8,128)(2,1)S(1)} %constant_dynamic-update-slice_fusion, bf16[384,384]{1,0:T(8,128)(2,1)S(1)} %copy-done), kind=kOutput, calls=%fused_computation.1 | convolution fusion | flops 1209532416 | bytes 6586368 | tf_op jit(solution)/shard_map/ftc,cd->ftd/dot_general | solution.py:145
  87.5 3.7 %convolution_convert_fusion.1.refs_1_ = bf16[2,2048,384]{2,1,0:T(8,128)(2,1)} fusion(bf16[2,2048,384]{2,1,0:T(8,128)(2,1)S(1)} %constant_dynamic-update-slice_fusion, bf16[384,384]{1,0:T(8,128)(2,1)S(1)} %copy-done.2), kind=kOutput, calls=%fused_computation.2 | convolution fusion | flops 1209532416 | bytes 6586368 | tf_op jit(solution)/shard_map/ftc,cd->ftd/dot_general | solution.py:142
  91.2 8.2 %shard_map.100 = bf16[2,256,384]{2,1,0:T(8,128)(2,1)} custom-call(bf16[2,256,384]{2,1,0:T(8,128)(2,1)} %convolution_convert_fusion.2.refs_0_, bf16[2,2048,384]{2,1,0:T(8,128)(2,1)} %convolution_convert_fusion.1.refs_1_, bf16[2,2048,384]{2,1,0:T(8,128)(2,1)} %convolution_convert_fusion.refs_2_), custom_call_target="tpu_custom_call" | custom-call | tf_op jit(solution)/shard_map/pallas_call | solution.py:71
  99.4 1.4 %fusion.16 = f32[2,256,384]{2,1,0:T(8,128)S(1)} fusion(bf16[2,256,384]{2,1,0:T(8,128)(2,1)} %shard_map.100, bf16[384,384]{1,0:T(8,128)(2,1)S(1)} %copy-done.4), kind=kOutput, calls=%fused_computation.29 | convolution fusion | flops 150994944 | bytes 1474560 | tf_op jit(solution)/shard_map/ftc,cd->ftd/dot_general | solution.py:149
  100.8 0.8 fusion.15
  (15 shorter events, 0.2 us)
Async XLA Ops:
  0.0 83.7 %copy-start = (bf16[384,384]{1,0:T(8,128)(2,1)S(1)}, bf16[384,384]{1,0:T(8,128)(2,1)}, u32[]{:S(2)}) copy-start(bf16[384,384]{1,0:T(8,128)(2,1)} %param.18) | copy-start | bytes 884740
  0.0 17.0 %copy-start.5 = (s32[2,2]{1,0:T(2,128)S(1)}, s32[2,2]{1,0:T(2,128)}, u32[]{:S(2)}) copy-start(s32[2,2]{1,0:T(2,128)} %param.11) | copy-start | bytes 52
  2.6 13.8 %collective-permute-start = (bf16[2,1,130,384]{3,2,1,0:T(8,128)(2,1)S(1)}, bf16[2,1,130,384]{3,2,1,0:T(8,128)(2,1)S(1)}, u32[]{:S(2)}, u32[]{:S(2)}) collective-permute-start(bf16[2,1,130,384]{3,2,1,0:T(8,128)(2,1)S(1)} %get-tuple-element.9), channel_id=1, source_target_pairs={{0,1},{1,2},{2,3},{3,4},{4,5},{5,6},{6,7},{8,9},{9,10},{10,11},{11... | collective-permute-start | bytes 599048 | tf_op jit(solution)/shard_map/ppermute | solution.py:16
  7.5 8.9 %collective-permute-start.1 = (bf16[2,1,130,384]{3,2,1,0:T(8,128)(2,1)S(1)}, bf16[2,1,130,384]{3,2,1,0:T(8,128)(2,1)S(1)}, u32[]{:S(2)}, u32[]{:S(2)}) collective-permute-start(bf16[2,1,130,384]{3,2,1,0:T(8,128)(2,1)S(1)} %get-tuple-element.10), channel_id=1, source_target_pairs={{1,0},{2,1},{3,2},{4,3},{5,4},{6,5},{7,6},{9,8},{10,9},{11,10},{12... | collective-permute-start | bytes 599048 | tf_op jit(solution)/shard_map/ppermute | solution.py:18
  16.9 2.4 %collective-permute-start.2 = (bf16[2,4,130,384]{3,1,2,0:T(4,128)(2,1)S(1)}, bf16[2,4,130,384]{3,1,2,0:T(4,128)(2,1)S(1)}, u32[]{:S(2)}, u32[]{:S(2)}) collective-permute-start(bf16[2,4,130,384]{3,1,2,0:T(4,128)(2,1)S(1)} %copy.26), channel_id=1, source_target_pairs={{0,8},{8,0},{1,9},{9,1},{2,10},{10,2},{3,11},{11,3},{4,12},{12,4},... | collective-permute-start | bytes 2396168 | tf_op jit(solution)/shard_map/ppermute | solution.py:111
  27.2 16.4 %copy-start.1 = (bf16[2,2,128,384]{3,2,1,0:T(8,128)(2,1)S(1)}, bf16[2,2,128,384]{3,2,1,0:T(8,128)(2,1)}, u32[]{:S(2)}) copy-start(bf16[2,2,128,384]{3,2,1,0:T(8,128)(2,1)} %param.10) | copy-start | bytes 1179652
  27.2 16.4 %copy-start.6 = (f32[384]{0:T(512)S(1)}, f32[384]{0:T(512)}, u32[]{:S(2)}) copy-start(f32[384]{0:T(512)} %param.14) | copy-start | bytes 4612
  27.2 16.6 %copy-start.7 = (f32[384]{0:T(512)S(1)}, f32[384]{0:T(512)}, u32[]{:S(2)}) copy-start(f32[384]{0:T(512)} %param.15) | copy-start | bytes 4612
  43.6 15.4 %copy-start.3 = (bf16[384,384]{1,0:T(8,128)(2,1)S(1)}, bf16[384,384]{1,0:T(8,128)(2,1)}, u32[]{:S(2)}) copy-start(bf16[384,384]{1,0:T(8,128)(2,1)} %param.16) | copy-start | bytes 884740
  44.0 12.9 %collective-permute-start.4 = (bf16[2,256,384]{2,1,0:T(8,128)(2,1)S(1)}, bf16[2,256,384]{2,1,0:T(8,128)(2,1)S(1)}, u32[]{:S(2)}, u32[]{:S(2)}) collective-permute-start(bf16[2,256,384]{2,1,0:T(8,128)(2,1)S(1)} %bitcast.27), channel_id=1, source_target_pairs={{0,1},{2,0},{4,2},{6,4},{7,6},{5,7},{3,5},{1,3},{8,9},{10,8},{12,1... | collective-permute-start | bytes 1179656 | tf_op jit(solution)/shard_map/ppermute | solution.py:35
  46.5 11.2 %collective-permute-start.3 = (bf16[2,256,384]{2,1,0:T(8,128)(2,1)S(1)}, bf16[2,256,384]{2,1,0:T(8,128)(2,1)S(1)}, u32[]{:S(2)}, u32[]{:S(2)}) collective-permute-start(bf16[2,256,384]{2,1,0:T(8,128)(2,1)S(1)} %bitcast.28), channel_id=1, source_target_pairs={{0,2},{2,4},{4,6},{6,7},{7,5},{5,3},{3,1},{1,0},{8,10},{10,12},{12... | collective-permute-start | bytes 1179656 | tf_op jit(solution)/shard_map/ppermute | solution.py:34
  56.9 10.6 %collective-permute-start.6 = (bf16[2,256,384]{2,1,0:T(8,128)(2,1)S(1)}, bf16[2,256,384]{2,1,0:T(8,128)(2,1)S(1)}, u32[]{:S(2)}, u32[]{:S(2)}) collective-permute-start(bf16[2,256,384]{2,1,0:T(8,128)(2,1)S(1)} %collective-permute-done.4), channel_id=1, source_target_pairs={{0,1},{2,0},{4,2},{6,4},{7,6},{5,7},{3,5},{1,3},{8,9},{10,8},{12,1... | collective-permute-start | bytes 1179656 | tf_op jit(solution)/shard_map/ppermute | solution.py:35
  57.6 10.3 %collective-permute-start.5 = (bf16[2,256,384]{2,1,0:T(8,128)(2,1)S(1)}, bf16[2,256,384]{2,1,0:T(8,128)(2,1)S(1)}, u32[]{:S(2)}, u32[]{:S(2)}) collective-permute-start(bf16[2,256,384]{2,1,0:T(8,128)(2,1)S(1)} %collective-permute-done.3), channel_id=1, source_target_pairs={{0,2},{2,4},{4,6},{6,7},{7,5},{5,3},{3,1},{1,0},{8,10},{10,12},{12... | collective-permute-start | bytes 1179656 | tf_op jit(solution)/shard_map/ppermute | solution.py:34
  67.5 9.7 %collective-permute-start.8 = (bf16[2,256,384]{2,1,0:T(8,128)(2,1)S(1)}, bf16[2,256,384]{2,1,0:T(8,128)(2,1)S(1)}, u32[]{:S(2)}, u32[]{:S(2)}) collective-permute-start(bf16[2,256,384]{2,1,0:T(8,128)(2,1)S(1)} %collective-permute-done.6), channel_id=1, source_target_pairs={{0,1},{2,0},{4,2},{6,4},{7,6},{5,7},{3,5},{1,3},{8,9},{10,8},{12,1... | collective-permute-start | bytes 1179656 | tf_op jit(solution)/shard_map/ppermute | solution.py:35
  68.0 9.6 %collective-permute-start.7 = (bf16[2,256,384]{2,1,0:T(8,128)(2,1)S(1)}, bf16[2,256,384]{2,1,0:T(8,128)(2,1)S(1)}, u32[]{:S(2)}, u32[]{:S(2)}) collective-permute-start(bf16[2,256,384]{2,1,0:T(8,128)(2,1)S(1)} %collective-permute-done.5), channel_id=1, source_target_pairs={{0,2},{2,4},{4,6},{6,7},{7,5},{5,3},{3,1},{1,0},{8,10},{10,12},{12... | collective-permute-start | bytes 1179656 | tf_op jit(solution)/shard_map/ppermute | solution.py:34
  77.3 6.3 %collective-permute-start.10 = (bf16[2,128,384]{2,1,0:T(8,128)(2,1)S(1)}, bf16[2,128,384]{2,1,0:T(8,128)(2,1)S(1)}, u32[]{:S(2)}, u32[]{:S(2)}) collective-permute-start(bf16[2,128,384]{2,1,0:T(8,128)(2,1)S(1)} %slice.27), channel_id=1, source_target_pairs={{0,1},{2,0},{4,2},{6,4},{7,6},{5,7},{3,5},{1,3},{8,9},{10,8},{12,1... | collective-permute-start | bytes 589832 | tf_op jit(solution)/shard_map/ppermute | solution.py:40
  77.6 5.9 %collective-permute-start.9 = (bf16[2,128,384]{2,1,0:T(8,128)(2,1)S(1)}, bf16[2,128,384]{2,1,0:T(8,128)(2,1)S(1)}, u32[]{:S(2)}, u32[]{:S(2)}) collective-permute-start(bf16[2,128,384]{2,1,0:T(8,128)(2,1)S(1)} %slice.26), channel_id=1, source_target_pairs={{0,2},{2,4},{4,6},{6,7},{7,5},{5,3},{3,1},{1,0},{8,10},{10,12},{12... | collective-permute-start | bytes 589832 | tf_op jit(solution)/shard_map/ppermute | solution.py:39
  83.7 3.8 %copy-start.2 = (bf16[384,384]{1,0:T(8,128)(2,1)S(1)}, bf16[384,384]{1,0:T(8,128)(2,1)}, u32[]{:S(2)}) copy-start(bf16[384,384]{1,0:T(8,128)(2,1)} %param.17) | copy-start | bytes 884740
  91.2 8.3 %copy-start.4 = (bf16[384,384]{1,0:T(8,128)(2,1)S(1)}, bf16[384,384]{1,0:T(8,128)(2,1)}, u32[]{:S(2)}) copy-start(bf16[384,384]{1,0:T(8,128)(2,1)} %param.19) | copy-start | bytes 884740

commit v9 on v6

--- a/solution.py
+++ b/solution.py
@@ -1,6 +1,7 @@
 import jax
 import jax.numpy as jnp
 from jax import lax
+from jax.experimental import pallas as pl
 from jax.sharding import PartitionSpec as P
 
 
@@ -40,7 +41,76 @@
             lax.slice_in_dim(backward, half, block.shape[dim], axis=dim), axis, behind
         )
         pieces += [front, back]
-    return jnp.concatenate(pieces, axis=dim)
+    return pieces
+
+
+def update_kernel(*refs, scale, first):
+    if first:
+        piece_ref, query_ref, key_w_ref, value_w_ref, peak_out, total_out, acc_out = refs
+    else:
+        (piece_ref, query_ref, key_w_ref, value_w_ref, peak_ref, total_ref, acc_ref,
+         peak_out, total_out, acc_out) = refs
+    piece = piece_ref[0]
+    keys = jnp.dot(piece, key_w_ref[...], preferred_element_type=jnp.float32).astype(
+        jnp.bfloat16
+    )
+    values = jnp.dot(piece, value_w_ref[...], preferred_element_type=jnp.float32).astype(
+        jnp.bfloat16
+    )
+    scores = (
+        lax.dot_general(
+            query_ref[0], keys, (((1,), (1,)), ((), ())), preferred_element_type=jnp.float32
+        )
+        * scale
+    )
+    peak = jnp.max(scores, axis=-1, keepdims=True)
+    if not first:
+        peak = jnp.maximum(peak_ref[0], peak)
+    weights_exp = jnp.exp(scores - peak)
+    total = jnp.sum(weights_exp, axis=-1, keepdims=True)
+    summed = jnp.dot(weights_exp.astype(jnp.bfloat16), values, preferred_element_type=jnp.float32)
+    if not first:
+        rescale = jnp.exp(peak_ref[0] - peak)
+        total = total + total_ref[0] * rescale
+        summed = summed + acc_ref[0] * rescale
+    peak_out[0] = peak
+    total_out[0] = total
+    acc_out[0] = summed
+
+
+def attend_update(piece, queries, key_weight, value_weight, state, scale):
+    spans, query_rows, channels = queries.shape
+    piece_rows = piece.shape[1]
+    first = state is None
+    kernel = lambda *refs: update_kernel(*refs, scale=scale, first=first)
+    stat_spec = pl.BlockSpec((1, query_rows, 1), lambda f: (f, 0, 0))
+    acc_spec = pl.BlockSpec((1, query_rows, channels), lambda f: (f, 0, 0))
+    weight_spec = pl.BlockSpec((channels, channels), lambda f: (0, 0))
+    in_specs = [
+        pl.BlockSpec((1, piece_rows, channels), lambda f: (f, 0, 0)),
+        pl.BlockSpec((1, query_rows, channels), lambda f: (f, 0, 0)),
+        weight_spec,
+        weight_spec,
+    ]
+    operands = [piece, queries, key_weight, value_weight]
+    aliases = {}
+    if not first:
+        in_specs += [stat_spec, stat_spec, acc_spec]
+        operands += list(state)
+        aliases = {4: 0, 5: 1, 6: 2}
+    stat_shape = jax.ShapeDtypeStruct((spans, query_rows, 1), jnp.float32)
+    return pl.pallas_call(
+        kernel,
+        grid=(spans,),
+        in_specs=in_specs,
+        out_specs=[stat_spec, stat_spec, acc_spec],
+        out_shape=[
+            stat_shape,
+            stat_shape,
+            jax.ShapeDtypeStruct((spans, query_rows, channels), jnp.float32),
+        ],
+        input_output_aliases=aliases,
+    )(*operands)
 
 
 def rms_scaled(frames, gain):
@@ -100,26 +170,11 @@
         "ftc,cd->ftd", tokens, query_weight, preferred_element_type=jnp.float32
     ).astype(jnp.bfloat16)
     score_scale = 1.0 / channels**0.5
-    tokens_all = ring_gather(tokens, "height", 1)
-    keys_all = jnp.einsum(
-        "ftc,cd->ftd", tokens_all, key_weight, preferred_element_type=jnp.float32
-    ).astype(jnp.bfloat16)
-    values_all = jnp.einsum(
-        "ftc,cd->ftd", tokens_all, value_weight, preferred_element_type=jnp.float32
-    ).astype(jnp.bfloat16)
-    scores = (
-        jnp.einsum("fqc,fkc->fqk", queries, keys_all, preferred_element_type=jnp.float32)
-        * score_scale
-    )
-    peaks = jnp.max(scores, axis=-1, keepdims=True)
-    weights_exp = jnp.exp(scores - peaks)
-    totals = jnp.sum(weights_exp, axis=-1)
-    summed = jnp.einsum(
-        "fqk,fkc->fqc",
-        weights_exp.astype(jnp.bfloat16),
-        values_all,
-        preferred_element_type=jnp.float32,
-    )
+    state = None
+    for piece in ring_gather(tokens, "height", 1):
+        state = attend_update(piece, queries, key_weight, value_weight, state, score_scale)
+    _, totals, summed = state
+    totals = totals[:, :, 0]
     attended = (summed / totals[:, :, None]).astype(jnp.bfloat16)
     projected = jnp.einsum("ftc,cd->ftd", attended, out_weight, preferred_element_type=jnp.float32)
     encoded = mixed.astype(jnp.float32) + projected.reshape(

time: 98 us -> 123 us (1.26)
  Pallas kernels: 0 us -> 38.2 us
  other arithmetic: 14.6 us -> 5.82 us
  local copies, waits for them, and re-layouts: 13.4 us -> 9.43 us
    pallas_call x0 -> x9, Pallas kernels: none -> 38.2 us  [attend_update(): pl.pallas_call(kernel, grid=(spans,), in_specs=in_specs, out_specs=[stat_...]
    dot_general x2 -> x0, matrix products: 13.4 us -> none  [the longest x1 7.02 us: shards(): jnp.einsum('fqc,fkc->fqk', queries, keys_all, preferred_element_type=jnp....]
    conv_general_dilated x1, matrix products: 5.99 us -> 16.3 us  [shards(): lax.conv_general_dilated(window, conv_weight, window_strides=(1, 1, 1), p...]
    unnamed x30 -> x26, local copies, waits for them, and re-layouts: 6.53 us -> 0.06 us
    ppermute x3, waiting for transfers between devices: 19.4 us -> 23.7 us  [ring_gather(): forward = lax.ppermute(forward, axis, ahead)]
    select_n x2, other arithmetic: 4.36 us -> 0.35 us  [shards(): jnp.take(pool, picks.reshape(-1), axis=0)]
    gather x1 -> x2, local copies, waits for them, and re-layouts: 2.53 us -> 6.3 us  [shards(): jnp.take(pool, picks.reshape(-1), axis=0)]
    reduce_sum x1 -> x0, other arithmetic: 3.05 us -> none  [shards(): totals = jnp.sum(weights_exp, axis=-1)]
  transfers between devices with their start and end apart: 11 -> 11, of which waited for: 7 -> 5; matrix products, arithmetic and copies ran while one was open for 7% -> 3% of each run, Pallas kernels for 0% -> 28%
where the time goes in v9:
time: 123 us
  Pallas kernels  38.2 us (31%)
  waiting for transfers between devices  33.2 us (27%)
  matrix products  19.1 us (16%)
  starting transfers between devices  16.8 us (14%)
  local copies, waits for them, and re-layouts  9.43 us (8%)
  other arithmetic  5.82 us (5%)
    pallas_call x9, Pallas kernels, attend_update(): pl.pallas_call(kernel, grid=(spans,), in_specs=in_specs, out_specs=[stat_...  38.2 us
    ppermute x3, waiting for transfers between devices, ring_gather(): forward = lax.ppermute(forward, axis, ahead)  23.7 us
    conv_general_dilated x1, matrix products, shards(): lax.conv_general_dilated(window, conv_weight, window_strides=(1, 1, 1), p...  16.3 us
    ppermute x3, starting transfers between devices, ring_gather(): forward = lax.ppermute(forward, axis, ahead)  8.3 us
    ppermute x1, waiting for transfers between devices, padded_2(): lax.ppermute(tail, axis, [(i, (i + 1) % count) for i in range(ends)])  7.49 us
    gather x2, local copies, waits for them, and re-layouts, shards(): jnp.take(pool, picks.reshape(-1), axis=0)  6.3 us
    ppermute x1, starting transfers between devices, padded_2(): lax.ppermute(tail, axis, [(i, (i + 1) % count) for i in range(ends)])  4.88 us
  transfers between devices with their start and end apart: 11, of which 5 were waited for; matrix products, arithmetic and copies ran while one was open for 3% of the time, Pallas kernels for 28%

profile of v9, /device:TPU:0, one launch (start us, length us, event | category | flops | bytes accessed | tf_op | source)
XLA Modules:
  0.0 122.8 jit_solution(16849071299620840889)
XLA Ops:
  0.0 0.0 copy-start
  0.0 1.2 fusion.2
  1.2 1.3 %fusion.9 = bf16[2,2,128,384]{3,2,1,0:T(8,128)(2,1)S(1)} fusion(bf16[2,2,128,384]{3,2,1,0:T(8,128)(2,1)} %param.10, f32[384]{0:T(512)} %param.12, f32[2,2,128]{2,1,0:T(2,128)S(1)} %add_rsqrt_fusion.1), kind=kLoop, calls=%fused_computation.20 | loop fusion | flops 1572864 | bytes 790016 | tf_op jit(solution)/shard_map/convert_element_type | solution.py:135
  2.5 0.0 copy-start.9
  2.5 0.1 pad_slice_fusion.1
  2.6 4.9 %collective-permute-start = (bf16[2,1,130,384]{3,2,1,0:T(8,128)(2,1)S(1)}, bf16[2,1,130,384]{3,2,1,0:T(8,128)(2,1)S(1)}, u32[]{:S(2)}, u32[]{:S(2)}) collective-permute-start(bf16[2,1,130,384]{3,2,1,0:T(8,128)(2,1)S(1)} %get-tuple-element.61), channel_id=1, source_target_pairs={{0,1},{1,2},{2,3},{3,4},{4,5},{5,6},{6,7},{8,9},{9,10},{10,11},{11... | collective-permute-start | bytes 599048 | tf_op jit(solution)/shard_map/ppermute | solution.py:16
  7.5 1.3 %collective-permute-start.1 = (bf16[2,1,130,384]{3,2,1,0:T(8,128)(2,1)S(1)}, bf16[2,1,130,384]{3,2,1,0:T(8,128)(2,1)S(1)}, u32[]{:S(2)}, u32[]{:S(2)}) collective-permute-start(bf16[2,1,130,384]{3,2,1,0:T(8,128)(2,1)S(1)} %get-tuple-element.62), channel_id=1, source_target_pairs={{1,0},{2,1},{3,2},{4,3},{5,4},{6,5},{7,6},{9,8},{10,9},{11,10},{12... | collective-permute-start | bytes 599048 | tf_op jit(solution)/shard_map/ppermute | solution.py:18
  8.8 0.1 pad.4
  8.9 7.5 %collective-permute-done = bf16[2,1,130,384]{3,2,1,0:T(8,128)(2,1)S(1)} collective-permute-done((bf16[2,1,130,384]{3,2,1,0:T(8,128)(2,1)S(1)}, bf16[2,1,130,384]{3,2,1,0:T(8,128)(2,1)S(1)}, u32[]{:S(2)}, u32[]{:S(2)}) %collective-permute-start) | collective-permute-done | bytes 199712 | tf_op jit(solution)/shard_map/ppermute | solution.py:16
  16.4 0.0 collective-permute-done.1
  16.4 0.1 pad_maximum_fusion
  16.6 0.3 copy.52
  16.9 0.1 collective-permute-start.2
  17.0 0.0 copy-done.9
  17.0 0.1 compare_select_fusion.7
  17.1 0.1 compare_and_fusion
  17.2 0.1 reshape.65
  17.2 0.1 pad.9.clone
  17.3 1.9 %collective-permute-done.2 = bf16[2,4,130,384]{3,1,2,0:T(4,128)(2,1)S(1)} collective-permute-done((bf16[2,4,130,384]{3,1,2,0:T(4,128)(2,1)S(1)}, bf16[2,4,130,384]{3,1,2,0:T(4,128)(2,1)S(1)}, u32[]{:S(2)}, u32[]{:S(2)}) %collective-permute-start.2) | collective-permute-done | bytes 798752 | tf_op jit(solution)/shard_map/ppermute | solution.py:143
  19.3 0.1 copy.53
  19.4 0.4 maximum_maximum_fusion
  19.7 0.8 copy.54
  20.5 4.3 %gather_fusion = bf16[6,4,130,384]{3,1,2,0:T(4,128)(2,1)} fusion(bf16[5,4,130,384]{3,1,2,0:T(4,128)(2,1)S(1)} %copy.54, s32[1024]{0:T(1024)S(1)} %pad_clamp_fusion), kind=kCustom, calls=%fused_computation | custom fusion | bytes 4792344 | tf_op jit(solution)/shard_map/jit(_take)/gather | solution.py:155
  24.8 2.0 %copy.55 = bf16[6,4,130,384]{3,2,1,0:T(8,128)(2,1)S(1)} copy(bf16[6,4,130,384]{3,1,2,0:T(4,128)(2,1)} %gather_fusion) | data formatting | bytes 4792320 | tf_op jit(solution)/shard_map/jit(_take)/gather | solution.py:155
  26.8 0.3 broadcast_select_fusion
  27.2 0.0 copy-start.1
  27.2 0.0 copy-start.10
  27.2 0.0 copy-start.11
  27.2 16.3 %fusion = f32[2,1,2,128,384]{4,0,3,2,1:T(2,128)S(1)} fusion(bf16[3,3,3,384,384]{4,3,2,1,0:T(8,128)(2,1)} %param.13, bf16[2,3,4,130,384]{4,3,2,1,0:T(8,128)(2,1)S(1)} %broadcast_select_fusion), kind=kOutput, calls=%fused_computation.2 | convolution fusion | flops 4076863488 | bytes 11145216 | tf_op jit(solution)/shard_map/conv_general_dilated | solution.py:158
  43.6 0.2 fusion.12
  43.8 0.2 fusion.14
  44.0 3.5 %collective-permute-start.7 = (bf16[2,256,384]{2,1,0:T(8,128)(2,1)S(1)}, bf16[2,256,384]{2,1,0:T(8,128)(2,1)S(1)}, u32[]{:S(2)}, u32[]{:S(2)}) collective-permute-start(bf16[2,256,384]{2,1,0:T(8,128)(2,1)S(1)} %bitcast.18), channel_id=1, source_target_pairs={{0,2},{2,4},{4,6},{6,7},{7,5},{5,3},{3,1},{1,0},{8,10},{10,12},{12... | collective-permute-start | bytes 1179656 | tf_op jit(solution)/shard_map/ppermute | solution.py:34
  47.4 0.0 collective-permute-start.3
  47.4 8.7 %collective-permute-done.7.refs_0_ = bf16[2,256,384]{2,1,0:T(8,128)(2,1)S(1)} collective-permute-done((bf16[2,256,384]{2,1,0:T(8,128)(2,1)S(1)}, bf16[2,256,384]{2,1,0:T(8,128)(2,1)S(1)}, u32[]{:S(2)}, u32[]{:S(2)}) %collective-permute-start.7) | collective-permute-done | bytes 393248 | tf_op jit(solution)/shard_map/ppermute | solution.py:34
  56.1 2.5 %collective-permute-start.8 = (bf16[2,256,384]{2,1,0:T(8,128)(2,1)S(1)}, bf16[2,256,384]{2,1,0:T(8,128)(2,1)S(1)}, u32[]{:S(2)}, u32[]{:S(2)}) collective-permute-start(bf16[2,256,384]{2,1,0:T(8,128)(2,1)S(1)} %collective-permute-done.7.refs_0_), channel_id=1, source_target_pairs={{0,2},{2,4},{4,6},{6,7},{7,5},{5,3},{3,1},{1,0},{8,10},{10,12},{12... | collective-permute-start | bytes 1179656 | tf_op jit(solution)/shard_map/ppermute | solution.py:34
  58.6 0.0 collective-permute-done.3.refs_0_
  58.6 0.0 collective-permute-start.4
  58.6 7.9 %collective-permute-done.8.refs_0_ = bf16[2,256,384]{2,1,0:T(8,128)(2,1)S(1)} collective-permute-done((bf16[2,256,384]{2,1,0:T(8,128)(2,1)S(1)}, bf16[2,256,384]{2,1,0:T(8,128)(2,1)S(1)}, u32[]{:S(2)}, u32[]{:S(2)}) %collective-permute-start.8) | collective-permute-done | bytes 393248 | tf_op jit(solution)/shard_map/ppermute | solution.py:34
  66.6 2.4 %collective-permute-start.9 = (bf16[2,256,384]{2,1,0:T(8,128)(2,1)S(1)}, bf16[2,256,384]{2,1,0:T(8,128)(2,1)S(1)}, u32[]{:S(2)}, u32[]{:S(2)}) collective-permute-start(bf16[2,256,384]{2,1,0:T(8,128)(2,1)S(1)} %collective-permute-done.8.refs_0_), channel_id=1, source_target_pairs={{0,2},{2,4},{4,6},{6,7},{7,5},{5,3},{3,1},{1,0},{8,10},{10,12},{12... | collective-permute-start | bytes 1179656 | tf_op jit(solution)/shard_map/ppermute | solution.py:34
  68.9 0.0 collective-permute-done.4.refs_0_
  68.9 0.0 collective-permute-start.5
  68.9 7.1 %collective-permute-done.9.refs_0_ = bf16[2,256,384]{2,1,0:T(8,128)(2,1)S(1)} collective-permute-done((bf16[2,256,384]{2,1,0:T(8,128)(2,1)S(1)}, bf16[2,256,384]{2,1,0:T(8,128)(2,1)S(1)}, u32[]{:S(2)}, u32[]{:S(2)}) %collective-permute-start.9) | collective-permute-done | bytes 393248 | tf_op jit(solution)/shard_map/ppermute | solution.py:34
  76.1 0.7 slice.27
  76.8 2.3 %collective-permute-start.10 = (bf16[2,128,384]{2,1,0:T(8,128)(2,1)}, bf16[2,128,384]{2,1,0:T(8,128)(2,1)}, u32[]{:S(2)}, u32[]{:S(2)}) collective-permute-start(bf16[2,128,384]{2,1,0:T(8,128)(2,1)} %slice.27), channel_id=1, source_target_pairs={{0,2},{2,4},{4,6},{6,7},{7,5},{5,3},{3,1},{1,0},{8,10},{10,12},{12... | collective-permute-start | bytes 589832 | tf_op jit(solution)/shard_map/ppermute | solution.py:39
  79.1 0.0 collective-permute-done.5.refs_0_
  79.1 0.8 slice.26
  79.8 0.0 collective-permute-start.6
  79.9 1.1 convolution_convert_fusion.refs_1_
  81.0 3.7 %shard_map.100 = (f32[2,256,1]{2,1,0:T(8,128)}, f32[2,256,1]{2,1,0:T(8,128)}, f32[2,256,384]{2,1,0:T(8,128)}) custom-call(bf16[2,256,384]{2,1,0:T(8,128)(2,1)} %bitcast.21, bf16[2,256,384]{2,1,0:T(8,128)(2,1)} %convolution_convert_fusion.refs_1_, bf16[384,384]{1,0:T(8,128)(2,1)} %refs_2_.17, bf16[384,384]{1,0:T(8,128)(2,1)} %refs_3_.17), custom_call_target="tpu_custom_call" | custom-call | tf_op jit(solution)/shard_map/pallas_call | solution.py:102
  84.7 4.5 %shard_map.101 = (f32[2,256,1]{2,1,0:T(8,128)}, f32[2,256,1]{2,1,0:T(8,128)}, f32[2,256,384]{2,1,0:T(8,128)}) custom-call(bf16[2,256,384]{2,1,0:T(8,128)(2,1)} %copy-done.8, bf16[2,256,384]{2,1,0:T(8,128)(2,1)} %convolution_convert_fusion.refs_1_, bf16[384,384]{1,0:T(8,128)(2,1)} %refs_2_.17, ...), custom_call_target="tpu_custom_call", output_to_operand_aliasing={{0}: (4, {}), {1}: (5, {}), {2}: (6, {})} | custom-call | tf_op jit(solution)/shard_map/pallas_call | solution.py:102
  89.1 0.0 copy-done.7
  89.2 4.5 %shard_map.102 = (f32[2,256,1]{2,1,0:T(8,128)}, f32[2,256,1]{2,1,0:T(8,128)}, f32[2,256,384]{2,1,0:T(8,128)}) custom-call(bf16[2,256,384]{2,1,0:T(8,128)(2,1)} %copy-done.7, bf16[2,256,384]{2,1,0:T(8,128)(2,1)} %convolution_convert_fusion.refs_1_, bf16[384,384]{1,0:T(8,128)(2,1)} %refs_2_.17, ...), custom_call_target="tpu_custom_call", output_to_operand_aliasing={{0}: (4, {}), {1}: (5, {}), {2}: (6, {})} | custom-call | tf_op jit(solution)/shard_map/pallas_call | solution.py:102
  93.6 4.5 %shard_map.103 = (f32[2,256,1]{2,1,0:T(8,128)}, f32[2,256,1]{2,1,0:T(8,128)}, f32[2,256,384]{2,1,0:T(8,128)}) custom-call(bf16[2,256,384]{2,1,0:T(8,128)(2,1)} %copy-done.6, bf16[2,256,384]{2,1,0:T(8,128)(2,1)} %convolution_convert_fusion.refs_1_, bf16[384,384]{1,0:T(8,128)(2,1)} %refs_2_.17, ...), custom_call_target="tpu_custom_call", output_to_operand_aliasing={{0}: (4, {}), {1}: (5, {}), {2}: (6, {})} | custom-call | tf_op jit(solution)/shard_map/pallas_call | solution.py:102
  98.1 4.5 %shard_map.104 = (f32[2,256,1]{2,1,0:T(8,128)}, f32[2,256,1]{2,1,0:T(8,128)}, f32[2,256,384]{2,1,0:T(8,128)}) custom-call(bf16[2,256,384]{2,1,0:T(8,128)(2,1)} %copy-done.5, bf16[2,256,384]{2,1,0:T(8,128)(2,1)} %convolution_convert_fusion.refs_1_, bf16[384,384]{1,0:T(8,128)(2,1)} %refs_2_.17, ...), custom_call_target="tpu_custom_call", output_to_operand_aliasing={{0}: (4, {}), {1}: (5, {}), {2}: (6, {})} | custom-call | tf_op jit(solution)/shard_map/pallas_call | solution.py:102
  102.5 4.5 %shard_map.105 = (f32[2,256,1]{2,1,0:T(8,128)}, f32[2,256,1]{2,1,0:T(8,128)}, f32[2,256,384]{2,1,0:T(8,128)}) custom-call(bf16[2,256,384]{2,1,0:T(8,128)(2,1)} %copy-done.4, bf16[2,256,384]{2,1,0:T(8,128)(2,1)} %convolution_convert_fusion.refs_1_, bf16[384,384]{1,0:T(8,128)(2,1)} %refs_2_.17, ...), custom_call_target="tpu_custom_call", output_to_operand_aliasing={{0}: (4, {}), {1}: (5, {}), {2}: (6, {})} | custom-call | tf_op jit(solution)/shard_map/pallas_call | solution.py:102
  107.0 4.5 %shard_map.106 = (f32[2,256,1]{2,1,0:T(8,128)}, f32[2,256,1]{2,1,0:T(8,128)}, f32[2,256,384]{2,1,0:T(8,128)}) custom-call(bf16[2,256,384]{2,1,0:T(8,128)(2,1)} %copy-done.3, bf16[2,256,384]{2,1,0:T(8,128)(2,1)} %convolution_convert_fusion.refs_1_, bf16[384,384]{1,0:T(8,128)(2,1)} %refs_2_.17, ...), custom_call_target="tpu_custom_call", output_to_operand_aliasing={{0}: (4, {}), {1}: (5, {}), {2}: (6, {})} | custom-call | tf_op jit(solution)/shard_map/pallas_call | solution.py:102
  111.5 0.0 collective-permute-done.10.refs_0_
  111.5 0.0 copy-start.12
  111.5 3.9 %shard_map.107 = (f32[2,256,1]{2,1,0:T(8,128)}, f32[2,256,1]{2,1,0:T(8,128)}, f32[2,256,384]{2,1,0:T(8,128)}) custom-call(bf16[2,128,384]{2,1,0:T(8,128)(2,1)} %collective-permute-done.10.refs_0_, bf16[2,256,384]{2,1,0:T(8,128)(2,1)} %convolution_convert_fusion.refs_1_, ...), custom_call_target="tpu_custom_call", output_to_operand_aliasing={{0}: (4, {}), {1}: (5, {}), {2}: (6, {})} | custom-call | tf_op jit(solution)/shard_map/pallas_call | solution.py:102
  115.4 0.0 collective-permute-done.6.refs_0_
  115.4 3.9 %shard_map.108 = (f32[2,256,1]{2,1,0:T(8,128)}, f32[2,256,1]{2,1,0:T(8,128)}, f32[2,256,384]{2,1,0:T(8,128)}) custom-call(bf16[2,128,384]{2,1,0:T(8,128)(2,1)} %collective-permute-done.6.refs_0_, bf16[2,256,384]{2,1,0:T(8,128)(2,1)} %convolution_convert_fusion.refs_1_, ...), custom_call_target="tpu_custom_call", output_to_operand_aliasing={{0}: (4, {}), {1}: (5, {}), {2}: (6, {})} | custom-call | tf_op jit(solution)/shard_map/pallas_call | solution.py:102
  119.3 1.1 reduce
  120.4 1.6 %fusion.16 = f32[2,256,384]{2,1,0:T(8,128)S(1)} fusion(f32[2,256,384]{2,1,0:T(8,128)} %get-tuple-element.55, f32[2,256]{1,0:T(2,128)S(1)} %reduce, bf16[384,384]{1,0:T(8,128)(2,1)S(1)} %copy-done.12), kind=kOutput, calls=%fused_computation.28 | convolution fusion | flops 151388160 | bytes 1869824 | tf_op jit(solution)/shard_map/ftc,cd->ftd/dot_general | solution.py:179
  122.0 0.8 fusion.15
  (23 shorter events, 0.1 us)
Async XLA Ops:
  0.0 79.8 %copy-start = (bf16[384,384]{1,0:T(8,128)(2,1)S(1)}, bf16[384,384]{1,0:T(8,128)(2,1)}, u32[]{:S(2)}) copy-start(bf16[384,384]{1,0:T(8,128)(2,1)} %param.16) | copy-start | bytes 884740
  2.5 14.4 %copy-start.9 = (s32[2,2]{1,0:T(2,128)S(1)}, s32[2,2]{1,0:T(2,128)}, u32[]{:S(2)}) copy-start(s32[2,2]{1,0:T(2,128)} %param.11) | copy-start | bytes 52
  2.6 13.8 %collective-permute-start = (bf16[2,1,130,384]{3,2,1,0:T(8,128)(2,1)S(1)}, bf16[2,1,130,384]{3,2,1,0:T(8,128)(2,1)S(1)}, u32[]{:S(2)}, u32[]{:S(2)}) collective-permute-start(bf16[2,1,130,384]{3,2,1,0:T(8,128)(2,1)S(1)} %get-tuple-element.61), channel_id=1, source_target_pairs={{0,1},{1,2},{2,3},{3,4},{4,5},{5,6},{6,7},{8,9},{9,10},{10,11},{11... | collective-permute-start | bytes 599048 | tf_op jit(solution)/shard_map/ppermute | solution.py:16
  7.5 8.9 %collective-permute-start.1 = (bf16[2,1,130,384]{3,2,1,0:T(8,128)(2,1)S(1)}, bf16[2,1,130,384]{3,2,1,0:T(8,128)(2,1)S(1)}, u32[]{:S(2)}, u32[]{:S(2)}) collective-permute-start(bf16[2,1,130,384]{3,2,1,0:T(8,128)(2,1)S(1)} %get-tuple-element.62), channel_id=1, source_target_pairs={{1,0},{2,1},{3,2},{4,3},{5,4},{6,5},{7,6},{9,8},{10,9},{11,10},{12... | collective-permute-start | bytes 599048 | tf_op jit(solution)/shard_map/ppermute | solution.py:18
  16.9 2.4 %collective-permute-start.2 = (bf16[2,4,130,384]{3,1,2,0:T(4,128)(2,1)S(1)}, bf16[2,4,130,384]{3,1,2,0:T(4,128)(2,1)S(1)}, u32[]{:S(2)}, u32[]{:S(2)}) collective-permute-start(bf16[2,4,130,384]{3,1,2,0:T(4,128)(2,1)S(1)} %copy.52), channel_id=1, source_target_pairs={{0,8},{8,0},{1,9},{9,1},{2,10},{10,2},{3,11},{11,3},{4,12},{12,4},... | collective-permute-start | bytes 2396168 | tf_op jit(solution)/shard_map/ppermute | solution.py:143
  27.2 16.4 %copy-start.1 = (bf16[2,2,128,384]{3,2,1,0:T(8,128)(2,1)S(1)}, bf16[2,2,128,384]{3,2,1,0:T(8,128)(2,1)}, u32[]{:S(2)}) copy-start(bf16[2,2,128,384]{3,2,1,0:T(8,128)(2,1)} %param.10) | copy-start | bytes 1179652
  27.2 16.4 %copy-start.10 = (f32[384]{0:T(512)S(1)}, f32[384]{0:T(512)}, u32[]{:S(2)}) copy-start(f32[384]{0:T(512)} %param.14) | copy-start | bytes 4612
  27.2 16.6 %copy-start.11 = (f32[384]{0:T(512)S(1)}, f32[384]{0:T(512)}, u32[]{:S(2)}) copy-start(f32[384]{0:T(512)} %param.15) | copy-start | bytes 4612
  44.0 37.0 %copy-start.2 = (bf16[2,2,128,384]{3,2,1,0:T(8,128)(2,1)}, bf16[2,2,128,384]{3,2,1,0:T(8,128)(2,1)S(1)}, u32[]{:S(2)}) copy-start(bf16[2,2,128,384]{3,2,1,0:T(8,128)(2,1)S(1)} %fusion.14) | copy-start | bytes 1179652
  44.0 12.1 %collective-permute-start.7 = (bf16[2,256,384]{2,1,0:T(8,128)(2,1)S(1)}, bf16[2,256,384]{2,1,0:T(8,128)(2,1)S(1)}, u32[]{:S(2)}, u32[]{:S(2)}) collective-permute-start(bf16[2,256,384]{2,1,0:T(8,128)(2,1)S(1)} %bitcast.18), channel_id=1, source_target_pairs={{0,2},{2,4},{4,6},{6,7},{7,5},{5,3},{3,1},{1,0},{8,10},{10,12},{12... | collective-permute-start | bytes 1179656 | tf_op jit(solution)/shard_map/ppermute | solution.py:34
  47.4 11.2 %collective-permute-start.3 = (bf16[2,256,384]{2,1,0:T(8,128)(2,1)S(1)}, bf16[2,256,384]{2,1,0:T(8,128)(2,1)S(1)}, u32[]{:S(2)}, u32[]{:S(2)}) collective-permute-start(bf16[2,256,384]{2,1,0:T(8,128)(2,1)S(1)} %bitcast.19), channel_id=1, source_target_pairs={{0,1},{2,0},{4,2},{6,4},{7,6},{5,7},{3,5},{1,3},{8,9},{10,8},{12,1... | collective-permute-start | bytes 1179656 | tf_op jit(solution)/shard_map/ppermute | solution.py:35
  56.1 28.6 %copy-start.8 = (bf16[2,256,384]{2,1,0:T(8,128)(2,1)}, bf16[2,256,384]{2,1,0:T(8,128)(2,1)S(1)}, u32[]{:S(2)}) copy-start(bf16[2,256,384]{2,1,0:T(8,128)(2,1)S(1)} %collective-permute-done.7.refs_0_) | copy-start | bytes 1179652
  56.1 10.4 %collective-permute-start.8 = (bf16[2,256,384]{2,1,0:T(8,128)(2,1)S(1)}, bf16[2,256,384]{2,1,0:T(8,128)(2,1)S(1)}, u32[]{:S(2)}, u32[]{:S(2)}) collective-permute-start(bf16[2,256,384]{2,1,0:T(8,128)(2,1)S(1)} %collective-permute-done.7.refs_0_), channel_id=1, source_target_pairs={{0,2},{2,4},{4,6},{6,7},{7,5},{5,3},{3,1},{1,0},{8,10},{10,12},{12... | collective-permute-start | bytes 1179656 | tf_op jit(solution)/shard_map/ppermute | solution.py:34
  58.6 30.5 %copy-start.7 = (bf16[2,256,384]{2,1,0:T(8,128)(2,1)}, bf16[2,256,384]{2,1,0:T(8,128)(2,1)S(1)}, u32[]{:S(2)}) copy-start(bf16[2,256,384]{2,1,0:T(8,128)(2,1)S(1)} %collective-permute-done.3.refs_0_) | copy-start | bytes 1179652
  58.6 10.3 %collective-permute-start.4 = (bf16[2,256,384]{2,1,0:T(8,128)(2,1)S(1)}, bf16[2,256,384]{2,1,0:T(8,128)(2,1)S(1)}, u32[]{:S(2)}, u32[]{:S(2)}) collective-permute-start(bf16[2,256,384]{2,1,0:T(8,128)(2,1)S(1)} %collective-permute-done.3.refs_0_), channel_id=1, source_target_pairs={{0,1},{2,0},{4,2},{6,4},{7,6},{5,7},{3,5},{1,3},{8,9},{10,8},{12,1... | collective-permute-start | bytes 1179656 | tf_op jit(solution)/shard_map/ppermute | solution.py:35
  66.5 22.6 %copy-start.6 = (bf16[2,256,384]{2,1,0:T(8,128)(2,1)}, bf16[2,256,384]{2,1,0:T(8,128)(2,1)S(1)}, u32[]{:S(2)}) copy-start(bf16[2,256,384]{2,1,0:T(8,128)(2,1)S(1)} %collective-permute-done.8.refs_0_) | copy-start | bytes 1179652
  66.6 9.5 %collective-permute-start.9 = (bf16[2,256,384]{2,1,0:T(8,128)(2,1)S(1)}, bf16[2,256,384]{2,1,0:T(8,128)(2,1)S(1)}, u32[]{:S(2)}, u32[]{:S(2)}) collective-permute-start(bf16[2,256,384]{2,1,0:T(8,128)(2,1)S(1)} %collective-permute-done.8.refs_0_), channel_id=1, source_target_pairs={{0,2},{2,4},{4,6},{6,7},{7,5},{5,3},{3,1},{1,0},{8,10},{10,12},{12... | collective-permute-start | bytes 1179656 | tf_op jit(solution)/shard_map/ppermute | solution.py:34
  68.9 20.2 %copy-start.5 = (bf16[2,256,384]{2,1,0:T(8,128)(2,1)}, bf16[2,256,384]{2,1,0:T(8,128)(2,1)S(1)}, u32[]{:S(2)}) copy-start(bf16[2,256,384]{2,1,0:T(8,128)(2,1)S(1)} %collective-permute-done.4.refs_0_) | copy-start | bytes 1179652
  68.9 10.1 %collective-permute-start.5 = (bf16[2,256,384]{2,1,0:T(8,128)(2,1)S(1)}, bf16[2,256,384]{2,1,0:T(8,128)(2,1)S(1)}, u32[]{:S(2)}, u32[]{:S(2)}) collective-permute-start(bf16[2,256,384]{2,1,0:T(8,128)(2,1)S(1)} %collective-permute-done.4.refs_0_), channel_id=1, source_target_pairs={{0,1},{2,0},{4,2},{6,4},{7,6},{5,7},{3,5},{1,3},{8,9},{10,8},{12,1... | collective-permute-start | bytes 1179656 | tf_op jit(solution)/shard_map/ppermute | solution.py:35
  76.1 13.1 %copy-start.4 = (bf16[2,256,384]{2,1,0:T(8,128)(2,1)}, bf16[2,256,384]{2,1,0:T(8,128)(2,1)S(1)}, u32[]{:S(2)}) copy-start(bf16[2,256,384]{2,1,0:T(8,128)(2,1)S(1)} %collective-permute-done.9.refs_0_) | copy-start | bytes 1179652
  76.8 34.6 %collective-permute-start.10 = (bf16[2,128,384]{2,1,0:T(8,128)(2,1)}, bf16[2,128,384]{2,1,0:T(8,128)(2,1)}, u32[]{:S(2)}, u32[]{:S(2)}) collective-permute-start(bf16[2,128,384]{2,1,0:T(8,128)(2,1)} %slice.27), channel_id=1, source_target_pairs={{0,2},{2,4},{4,6},{6,7},{7,5},{5,3},{3,1},{1,0},{8,10},{10,12},{12... | collective-permute-start | bytes 589832 | tf_op jit(solution)/shard_map/ppermute | solution.py:39
  79.1 10.1 %copy-start.3 = (bf16[2,256,384]{2,1,0:T(8,128)(2,1)}, bf16[2,256,384]{2,1,0:T(8,128)(2,1)S(1)}, u32[]{:S(2)}) copy-start(bf16[2,256,384]{2,1,0:T(8,128)(2,1)S(1)} %collective-permute-done.5.refs_0_) | copy-start | bytes 1179652
  79.8 35.6 %collective-permute-start.6 = (bf16[2,128,384]{2,1,0:T(8,128)(2,1)}, bf16[2,128,384]{2,1,0:T(8,128)(2,1)}, u32[]{:S(2)}, u32[]{:S(2)}) collective-permute-start(bf16[2,128,384]{2,1,0:T(8,128)(2,1)} %slice.26), channel_id=1, source_target_pairs={{0,1},{2,0},{4,2},{6,4},{7,6},{5,7},{3,5},{1,3},{8,9},{10,8},{12,1... | collective-permute-start | bytes 589832 | tf_op jit(solution)/shard_map/ppermute | solution.py:40
  111.5 8.9 %copy-start.12 = (bf16[384,384]{1,0:T(8,128)(2,1)S(1)}, bf16[384,384]{1,0:T(8,128)(2,1)}, u32[]{:S(2)}) copy-start(bf16[384,384]{1,0:T(8,128)(2,1)} %param.19) | copy-start | bytes 884740

commit v10 on v6

--- a/solution.py
+++ b/solution.py
@@ -40,7 +40,7 @@
             lax.slice_in_dim(backward, half, block.shape[dim], axis=dim), axis, behind
         )
         pieces += [front, back]
-    return jnp.concatenate(pieces, axis=dim)
+    return pieces
 
 
 def rms_scaled(frames, gain):
@@ -100,13 +100,20 @@
         "ftc,cd->ftd", tokens, query_weight, preferred_element_type=jnp.float32
     ).astype(jnp.bfloat16)
     score_scale = 1.0 / channels**0.5
-    tokens_all = ring_gather(tokens, "height", 1)
-    keys_all = jnp.einsum(
-        "ftc,cd->ftd", tokens_all, key_weight, preferred_element_type=jnp.float32
-    ).astype(jnp.bfloat16)
-    values_all = jnp.einsum(
-        "ftc,cd->ftd", tokens_all, value_weight, preferred_element_type=jnp.float32
-    ).astype(jnp.bfloat16)
+    key_parts = []
+    value_parts = []
+    for piece in ring_gather(tokens, "height", 1):
+        keys = jnp.einsum(
+            "ftc,cd->ftd", piece, key_weight, preferred_element_type=jnp.float32
+        ).astype(jnp.bfloat16)
+        values = jnp.einsum(
+            "ftc,cd->ftd", piece, value_weight, preferred_element_type=jnp.float32
+        ).astype(jnp.bfloat16)
+        keys, values = lax.optimization_barrier((keys, values))
+        key_parts.append(keys)
+        value_parts.append(values)
+    keys_all = jnp.concatenate(key_parts, axis=1)
+    values_all = jnp.concatenate(value_parts, axis=1)
     scores = (
         jnp.einsum("fqc,fkc->fqk", queries, keys_all, preferred_element_type=jnp.float32)
         * score_scale

time: 98 us -> 102 us (1.041)
  matrix products: 20.2 us -> 22.7 us
  local copies, waits for them, and re-layouts: 13.4 us -> 15.1 us
  starting transfers between devices: 17.2 us -> 16.1 us
    dot_general x1, matrix products: 0.39 us -> 4.74 us  [shards(): jnp.einsum('ftc,cd->ftd', attended, out_weight, preferred_element_type=jn...]
    ppermute x3, starting transfers between devices: 8.31 us -> 4.55 us  [ring_gather(): forward = lax.ppermute(forward, axis, ahead)]
    ppermute x1, waiting for transfers between devices: 0.01 us -> 3.1 us  [padded_2(): lax.ppermute(head, axis, [((i + 1) % count, i) for i in range(ends)])]
    ppermute x1, waiting for transfers between devices: 7.49 us -> 4.63 us  [padded_2(): lax.ppermute(tail, axis, [(i, (i + 1) % count) for i in range(ends)])]
    ppermute x3, starting transfers between devices: 0.01 us -> 2.31 us  [ring_gather(): backward = lax.ppermute(backward, axis, behind)]
    dot_general x1, matrix products: 7.02 us -> 5.39 us  [shards(): jnp.einsum('fqc,fkc->fqk', queries, keys_all, preferred_element_type=jnp....]
    unnamed x30 -> x39, local copies, waits for them, and re-layouts: 6.53 us -> 8.14 us
    ppermute x1, starting transfers between devices: 2.31 us -> 1.28 us  [ring_gather(): lax.ppermute(lax.slice_in_dim(forward, 0, half, axis=dim), axis, ahead)]
  transfers between devices with their start and end apart: 11 -> 11, of which waited for: 7 -> 8; matrix products, arithmetic and copies ran while one was open for 7% -> 10% of each run, Pallas kernels for 0% -> 0%
where the time goes in v10:
time: 102 us
  waiting for transfers between devices  32.5 us (32%)
  matrix products  22.7 us (22%)
  starting transfers between devices  16.1 us (16%)
  local copies, waits for them, and re-layouts  15.1 us (15%)
  other arithmetic  14.6 us (14%)
    ppermute x3, waiting for transfers between devices, ring_gather(): forward = lax.ppermute(forward, axis, ahead)  20.4 us
    unnamed x39, local copies, waits for them, and re-layouts  8.14 us
    conv_general_dilated x1, matrix products, shards(): lax.conv_general_dilated(window, conv_weight, window_strides=(1, 1, 1), p...  5.99 us
    ppermute x1, starting transfers between devices, padded_2(): lax.ppermute(tail, axis, [(i, (i + 1) % count) for i in range(ends)])  5.51 us
    dot_general x1, matrix products, shards(): jnp.einsum('fqc,fkc->fqk', queries, keys_all, preferred_element_type=jnp....  5.39 us
    dot_general x1, matrix products, shards(): jnp.einsum('ftc,cd->ftd', attended, out_weight, preferred_element_type=jn...  4.74 us
    ppermute x1, waiting for transfers between devices, padded_2(): lax.ppermute(tail, axis, [(i, (i + 1) % count) for i in range(ends)])  4.63 us
    ppermute x3, starting transfers between devices, ring_gather(): forward = lax.ppermute(forward, axis, ahead)  4.55 us
  transfers between devices with their start and end apart: 11, of which 8 were waited for; matrix products, arithmetic and copies ran while one was open for 10% of the time, Pallas kernels for 0%

profile of v10, /device:TPU:0, one launch (start us, length us, event | category | flops | bytes accessed | tf_op | source)
XLA Modules:
  0.0 101.5 jit_solution(17771024662525078657)
XLA Ops:
  0.0 1.2 %fusion.24 = f32[2,2,128]{2,1,0:T(2,128)S(1)} fusion(bf16[2,2,128,384]{3,2,1,0:T(8,128)(2,1)} %param.10), kind=kLoop, calls=%fused_computation.47 | loop fusion | flops 589312 | bytes 395264 | tf_op jit(solution)/shard_map/reduce_sum | solution.py:48
  1.2 1.3 %fusion.31 = bf16[2,2,128,384]{3,2,1,0:T(8,128)(2,1)S(1)} fusion(bf16[2,2,128,384]{3,2,1,0:T(8,128)(2,1)} %param.10, f32[384]{0:T(512)} %param.12, f32[2,2,128]{2,1,0:T(2,128)S(1)} %add_rsqrt_fusion.1), kind=kLoop, calls=%fused_computation.54 | loop fusion | flops 1572864 | bytes 790016 | tf_op jit(solution)/shard_map/convert_element_type | solution.py:65
  2.6 1.3 %collective-permute-start.1 = (bf16[2,1,130,384]{3,2,1,0:T(8,128)(2,1)S(1)}, bf16[2,1,130,384]{3,2,1,0:T(8,128)(2,1)S(1)}, u32[]{:S(2)}, u32[]{:S(2)}) collective-permute-start(bf16[2,1,130,384]{3,2,1,0:T(8,128)(2,1)S(1)} %get-tuple-element.46), channel_id=1, source_target_pairs={{1,0},{2,1},{3,2},{4,3},{5,4},{6,5},{7,6},{9,8},{10,9},{11,10},{12... | collective-permute-start | bytes 599048 | tf_op jit(solution)/shard_map/ppermute | solution.py:17
  3.9 5.5 %collective-permute-start = (bf16[2,1,130,384]{3,2,1,0:T(8,128)(2,1)S(1)}, bf16[2,1,130,384]{3,2,1,0:T(8,128)(2,1)S(1)}, u32[]{:S(2)}, u32[]{:S(2)}) collective-permute-start(bf16[2,1,130,384]{3,2,1,0:T(8,128)(2,1)S(1)} %get-tuple-element.45), channel_id=1, source_target_pairs={{0,1},{1,2},{2,3},{3,4},{4,5},{5,6},{6,7},{8,9},{9,10},{10,11},{11... | collective-permute-start | bytes 599048 | tf_op jit(solution)/shard_map/ppermute | solution.py:15
  9.6 3.1 %collective-permute-done.1 = bf16[2,1,130,384]{3,2,1,0:T(8,128)(2,1)S(1)} collective-permute-done((bf16[2,1,130,384]{3,2,1,0:T(8,128)(2,1)S(1)}, bf16[2,1,130,384]{3,2,1,0:T(8,128)(2,1)S(1)}, u32[]{:S(2)}, u32[]{:S(2)}) %collective-permute-start.1) | collective-permute-done | bytes 199712 | tf_op jit(solution)/shard_map/ppermute | solution.py:17
  12.7 4.6 %collective-permute-done = bf16[2,1,130,384]{3,2,1,0:T(8,128)(2,1)S(1)} collective-permute-done((bf16[2,1,130,384]{3,2,1,0:T(8,128)(2,1)S(1)}, bf16[2,1,130,384]{3,2,1,0:T(8,128)(2,1)S(1)}, u32[]{:S(2)}, u32[]{:S(2)}) %collective-permute-start) | collective-permute-done | bytes 199712 | tf_op jit(solution)/shard_map/ppermute | solution.py:15
  17.4 0.3 copy.25
  18.3 1.8 %collective-permute-done.2 = bf16[2,4,130,384]{3,1,2,0:T(4,128)(2,1)S(1)} collective-permute-done((bf16[2,4,130,384]{3,1,2,0:T(4,128)(2,1)S(1)}, bf16[2,4,130,384]{3,1,2,0:T(4,128)(2,1)S(1)}, u32[]{:S(2)}, u32[]{:S(2)}) %collective-permute-start.2) | collective-permute-done | bytes 798752 | tf_op jit(solution)/shard_map/ppermute | solution.py:73
  20.2 0.4 maximum_maximum_fusion
  20.6 2.6 %gather_fusion = bf16[6,4,130,384]{3,2,1,0:T(8,128)(2,1)} fusion(bf16[5,4,130,384]{3,2,1,0:T(8,128)(2,1)S(1)} %maximum_maximum_fusion, s32[1024]{0:T(1024)S(1)} %pad_clamp_fusion), kind=kCustom, calls=%fused_computation | custom fusion | bytes 4792344 | tf_op jit(solution)/shard_map/jit(_take)/gather | solution.py:85
  23.2 4.4 %fusion.6 = bf16[3,4,2,130,384]{4,2,3,1,0:T(2,128)(2,1)S(1)} fusion(pred[2,3]{0,1:T(4,128)(4,1)S(1)} %copy.24, bf16[2,3,4,130,384]{4,3,2,1,0:T(8,128)(2,1)} %bitcast.93), kind=kLoop, calls=%fused_computation.11 | loop fusion | flops 1198080 | bytes 4792326 | tf_op jit(solution)/shard_map/jit(_take)/select_n | solution.py:85
  27.5 1.9 %pad.5 = bf16[3,4,2,136,384]{4,2,3,1,0:T(2,128)(2,1)S(1)} pad(bf16[3,4,2,130,384]{4,2,3,1,0:T(2,128)(2,1)S(1)} %fusion.6, bf16[]{:T(256)} %constant.87.clone.1), padding=0_0x0_0x0_0x0_6x0_0 | pad | bytes 4902914 | tf_op jit(solution)/shard_map/jit(_take)/select_n | solution.py:85
  29.4 0.2 slice.28
  29.6 2.8 %fusion.2 = bf16[3,4,2,8,19,384]{5,2,4,3,1,0:T(2,128)(2,1)S(1)} fusion(bf16[3,4,2,7,2,384]{5,2,4,3,1,0:T(2,128)(2,1)S(1)} %slice.28, bf16[3,4,2,8,17,384]{5,2,4,3,1,0:T(2,128)(2,1)S(1)} %bitcast.92), kind=kLoop, calls=%fused_computation.7 | loop fusion | flops 8404992 | bytes 5566464 | tf_op jit(solution)/shard_map/conv_general_dilated | solution.py:88
  32.4 6.0 %fusion.11 = f32[1,2,16,17,384]{4,2,3,1,0:T(8,128)S(1)} fusion(bf16[3,3,3,384,384]{4,3,2,1,0:T(8,128)(2,1)S(1)} %bitcast.102, bf16[3,4,2,8,19,384]{5,2,4,3,1,0:T(2,128)(2,1)S(1)} %fusion.2, pred[16,17]{0,1:T(8,128)(4,1)S(1)} %copy-done.9), kind=kOutput, calls=%fused_computation.16 | convolution fusion | flops 4331876352 | bytes 11600144 | tf_op jit(solution)/shard_map/conv_general_dilated | solution.py:88
  38.5 0.4 copy.29
  38.9 0.3 slice.29
  39.2 0.2 copy-done.2
  39.4 0.2 fusion.34
  39.9 1.7 %collective-permute-start.3 = (bf16[2,256,384]{2,1,0:T(8,128)(2,1)S(1)}, bf16[2,256,384]{2,1,0:T(8,128)(2,1)S(1)}, u32[]{:S(2)}, u32[]{:S(2)}) collective-permute-start(bf16[2,256,384]{2,1,0:T(8,128)(2,1)S(1)} %bitcast.94), channel_id=1, source_target_pairs={{0,2},{2,4},{4,6},{6,7},{7,5},{5,3},{3,1},{1,0},{8,10},{10,12},{12... | collective-permute-start | bytes 1179656 | tf_op jit(solution)/shard_map/ppermute | solution.py:33
  41.6 0.9 collective-permute-start.4
  42.5 0.4 convolution_convert_fusion.13
  42.9 0.4 convolution_convert_fusion.12
  43.3 0.9 constant_dynamic-update-slice_fusion.8
  44.1 7.7 %collective-permute-done.3 = bf16[2,256,384]{2,1,0:T(8,128)(2,1)S(1)} collective-permute-done((bf16[2,256,384]{2,1,0:T(8,128)(2,1)S(1)}, bf16[2,256,384]{2,1,0:T(8,128)(2,1)S(1)}, u32[]{:S(2)}, u32[]{:S(2)}) %collective-permute-start.3) | collective-permute-done | bytes 393248 | tf_op jit(solution)/shard_map/ppermute | solution.py:33
  51.8 0.4 convolution_convert_fusion.11
  52.2 0.4 convolution_convert_fusion.10
  52.6 0.4 convolution_convert_fusion.9
  53.0 0.4 convolution_convert_fusion.8
  53.4 1.4 %collective-permute-start.5 = (bf16[2,256,384]{2,1,0:T(8,128)(2,1)S(1)}, bf16[2,256,384]{2,1,0:T(8,128)(2,1)S(1)}, u32[]{:S(2)}, u32[]{:S(2)}) collective-permute-start(bf16[2,256,384]{2,1,0:T(8,128)(2,1)S(1)} %collective-permute-done.3), channel_id=1, source_target_pairs={{0,2},{2,4},{4,6},{6,7},{7,5},{5,3},{3,1},{1,0},{8,10},{10,12},{12... | collective-permute-start | bytes 1179656 | tf_op jit(solution)/shard_map/ppermute | solution.py:33
  54.9 0.7 collective-permute-start.6
  55.7 0.8 constant_dynamic-update-slice_fusion.7
  56.5 0.8 constant_dynamic-update-slice_fusion.6
  57.3 6.8 %collective-permute-done.5 = bf16[2,256,384]{2,1,0:T(8,128)(2,1)S(1)} collective-permute-done((bf16[2,256,384]{2,1,0:T(8,128)(2,1)S(1)}, bf16[2,256,384]{2,1,0:T(8,128)(2,1)S(1)}, u32[]{:S(2)}, u32[]{:S(2)}) %collective-permute-start.5) | collective-permute-done | bytes 393248 | tf_op jit(solution)/shard_map/ppermute | solution.py:33
  64.1 0.4 convolution_convert_fusion.7
  64.5 0.4 convolution_convert_fusion.6
  64.9 0.4 convolution_convert_fusion.5
  65.3 0.4 convolution_convert_fusion.4
  65.7 1.4 %collective-permute-start.7 = (bf16[2,256,384]{2,1,0:T(8,128)(2,1)S(1)}, bf16[2,256,384]{2,1,0:T(8,128)(2,1)S(1)}, u32[]{:S(2)}, u32[]{:S(2)}) collective-permute-start(bf16[2,256,384]{2,1,0:T(8,128)(2,1)S(1)} %collective-permute-done.5), channel_id=1, source_target_pairs={{0,2},{2,4},{4,6},{6,7},{7,5},{5,3},{3,1},{1,0},{8,10},{10,12},{12... | collective-permute-start | bytes 1179656 | tf_op jit(solution)/shard_map/ppermute | solution.py:33
  67.2 0.7 collective-permute-start.8
  68.0 0.9 constant_dynamic-update-slice_fusion.5
  68.8 0.8 constant_dynamic-update-slice_fusion.4
  69.7 5.8 %collective-permute-done.7 = bf16[2,256,384]{2,1,0:T(8,128)(2,1)S(1)} collective-permute-done((bf16[2,256,384]{2,1,0:T(8,128)(2,1)S(1)}, bf16[2,256,384]{2,1,0:T(8,128)(2,1)S(1)}, u32[]{:S(2)}, u32[]{:S(2)}) %collective-permute-start.7) | collective-permute-done | bytes 393248 | tf_op jit(solution)/shard_map/ppermute | solution.py:33
  75.5 0.4 convolution_convert_fusion.3
  75.9 0.4 convolution_convert_fusion.2
  76.3 0.4 convolution_convert_fusion.1
  76.7 0.4 convolution_convert_fusion
  77.1 1.3 %collective-permute-start.9 = (bf16[2,128,384]{2,1,0:T(8,128)(2,1)S(1)}, bf16[2,128,384]{2,1,0:T(8,128)(2,1)S(1)}, u32[]{:S(2)}, u32[]{:S(2)}) collective-permute-start(bf16[2,128,384]{2,1,0:T(8,128)(2,1)S(1)} %slice.30), channel_id=1, source_target_pairs={{0,2},{2,4},{4,6},{6,7},{7,5},{5,3},{3,1},{1,0},{8,10},{10,12},{12... | collective-permute-start | bytes 589832 | tf_op jit(solution)/shard_map/ppermute | solution.py:38
  78.5 1.1 %collective-permute-start.10 = (bf16[2,128,384]{2,1,0:T(8,128)(2,1)S(1)}, bf16[2,128,384]{2,1,0:T(8,128)(2,1)S(1)}, u32[]{:S(2)}, u32[]{:S(2)}) collective-permute-start(bf16[2,128,384]{2,1,0:T(8,128)(2,1)S(1)} %slice.31), channel_id=1, source_target_pairs={{0,1},{2,0},{4,2},{6,4},{7,6},{5,7},{3,5},{1,3},{8,9},{10,8},{12,1... | collective-permute-start | bytes 589832 | tf_op jit(solution)/shard_map/ppermute | solution.py:39
  79.7 0.8 constant_dynamic-update-slice_fusion.3
  80.5 0.8 constant_dynamic-update-slice_fusion.2
  81.3 1.6 %collective-permute-done.9 = bf16[2,128,384]{2,1,0:T(8,128)(2,1)S(1)} collective-permute-done((bf16[2,128,384]{2,1,0:T(8,128)(2,1)S(1)}, bf16[2,128,384]{2,1,0:T(8,128)(2,1)S(1)}, u32[]{:S(2)}, u32[]{:S(2)}) %collective-permute-start.9) | collective-permute-done | bytes 196640 | tf_op jit(solution)/shard_map/ppermute | solution.py:38
  82.9 0.3 convolution_convert_fusion.18
  83.2 0.3 convolution_convert_fusion.17
  83.4 1.0 collective-permute-done.10
  84.4 0.3 convolution_convert_fusion.16
  84.7 0.3 convolution_convert_fusion.15
  85.0 0.8 constant_dynamic-update-slice_fusion.1
  85.8 1.0 copy-done.4
  86.8 0.7 constant_dynamic-update-slice_fusion
  87.5 5.4 %multiply_reduce_fusion = (f32[2,256]{1,0:T(2,128)S(1)}, f32[2,256,2048]{2,1,0:T(8,128)}) fusion(bf16[2,2048,384]{2,1,0:T(8,128)(2,1)} %constant_dynamic-update-slice_fusion, bf16[2,256,384]{2,1,0:T(8,128)(2,1)S(1)} %bitcast.98, bf16[384,384]{1,0:T(8,128)(2,1)S(1)} %copy-done.3), kind=kOutput, calls=%fused_computation.4 | convolution fusion | flops 958594560 | bytes 8030208 | tf_op jit(solution)/shard_map/fqc,fkc->fqk/dot_general | solution.py:118
  92.9 3.0 %fusion = f32[2,256]{1,0:T(2,128)S(1)} fusion(f32[2,256,2048]{2,1,0:T(8,128)} %get-tuple-element.50, f32[2,256]{1,0:T(2,128)S(1)} %get-tuple-element.49), kind=kLoop, calls=%fused_computation.5 | loop fusion | flops 3145216 | bytes 4198400 | tf_op jit(solution)/shard_map/reduce_sum | solution.py:123
  95.9 4.7 %fusion.22 = f32[2,256,384]{2,1,0:T(8,128)S(1)} fusion(bf16[2,2048,384]{2,1,0:T(8,128)(2,1)} %copy-done.4, f32[2,256,2048]{2,1,0:T(8,128)} %get-tuple-element.50, f32[2,256]{1,0:T(2,128)S(1)} %get-tuple-element.49, f32[2,256]{1,0:T(2,128)S(1)} %fusion, bf16[384,384]{1,0:T(8,128)(2,1)S(1)} %copy-done.8), kind=kOutput, calls=%fused_computation.45 | convolution fusion | flops 959840256 | bytes 8425472 | tf_op jit(solution)/shard_map/ftc,cd->ftd/dot_general | solution.py:131
  100.7 0.8 fusion.37
  (52 shorter events, 1.7 us)
Async XLA Ops:
  0.0 42.5 %copy-start = (bf16[384,384]{1,0:T(8,128)(2,1)S(1)}, bf16[384,384]{1,0:T(8,128)(2,1)}, u32[]{:S(2)}) copy-start(bf16[384,384]{1,0:T(8,128)(2,1)} %param.17) | copy-start | bytes 884740
  0.0 17.8 %copy-start.5 = (s32[2,2]{1,0:T(2,128)S(1)}, s32[2,2]{1,0:T(2,128)}, u32[]{:S(2)}) copy-start(s32[2,2]{1,0:T(2,128)} %param.11) | copy-start | bytes 52
  2.6 10.0 %collective-permute-start.1 = (bf16[2,1,130,384]{3,2,1,0:T(8,128)(2,1)S(1)}, bf16[2,1,130,384]{3,2,1,0:T(8,128)(2,1)S(1)}, u32[]{:S(2)}, u32[]{:S(2)}) collective-permute-start(bf16[2,1,130,384]{3,2,1,0:T(8,128)(2,1)S(1)} %get-tuple-element.46), channel_id=1, source_target_pairs={{1,0},{2,1},{3,2},{4,3},{5,4},{6,5},{7,6},{9,8},{10,9},{11,10},{12... | collective-permute-start | bytes 599048 | tf_op jit(solution)/shard_map/ppermute | solution.py:17
  3.9 13.4 %collective-permute-start = (bf16[2,1,130,384]{3,2,1,0:T(8,128)(2,1)S(1)}, bf16[2,1,130,384]{3,2,1,0:T(8,128)(2,1)S(1)}, u32[]{:S(2)}, u32[]{:S(2)}) collective-permute-start(bf16[2,1,130,384]{3,2,1,0:T(8,128)(2,1)S(1)} %get-tuple-element.45), channel_id=1, source_target_pairs={{0,1},{1,2},{2,3},{3,4},{4,5},{5,6},{6,7},{8,9},{9,10},{10,11},{11... | collective-permute-start | bytes 599048 | tf_op jit(solution)/shard_map/ppermute | solution.py:15
  17.7 2.4 %collective-permute-start.2 = (bf16[2,4,130,384]{3,1,2,0:T(4,128)(2,1)S(1)}, bf16[2,4,130,384]{3,1,2,0:T(4,128)(2,1)S(1)}, u32[]{:S(2)}, u32[]{:S(2)}) collective-permute-start(bf16[2,4,130,384]{3,1,2,0:T(4,128)(2,1)S(1)} %copy.25), channel_id=1, source_target_pairs={{0,8},{8,0},{1,9},{9,1},{2,10},{10,2},{3,11},{11,3},{4,12},{12,4},... | collective-permute-start | bytes 2396168 | tf_op jit(solution)/shard_map/ppermute | solution.py:73
  23.2 9.3 %slice-start = ((s8[7962624]{0:T(1024)(128)(4,1)}), s8[4194304]{0:T(1024)(128)(4,1)S(1)}, s32[]{:S(2)}) async-start(s8[7962624]{0:T(1024)(128)(4,1)} %bitcast.101), calls=%async_computation | async-start | bytes 8388608
  27.5 4.9 %slice-start.1 = ((s8[7962624]{0:T(1024)(128)(4,1)}), s8[3768320]{0:T(1024)(128)(4,1)S(1)}, s32[]{:S(2)}) async-start(s8[7962624]{0:T(1024)(128)(4,1)} %bitcast.101), calls=%async_computation.1 | async-start | bytes 7536640
  29.4 3.0 %copy-start.9 = (pred[16,17]{0,1:T(8,128)(4,1)S(1)}, pred[16,17]{0,1:T(8,128)(4,1)}, u32[]{:S(2)}) copy-start(pred[16,17]{0,1:T(8,128)(4,1)} %constant.99) | copy-start | bytes 820
  38.4 1.0 copy-start.2
  38.5 1.0 copy-start.6
  38.5 1.2 %copy-start.7 = (f32[384]{0:T(512)S(1)}, f32[384]{0:T(512)}, u32[]{:S(2)}) copy-start(f32[384]{0:T(512)} %param.15) | copy-start | bytes 4612
  38.5 4.4 %copy-start.1 = (bf16[384,384]{1,0:T(8,128)(2,1)S(1)}, bf16[384,384]{1,0:T(8,128)(2,1)}, u32[]{:S(2)}) copy-start(bf16[384,384]{1,0:T(8,128)(2,1)} %param.18) | copy-start | bytes 884740
  39.9 11.9 %collective-permute-start.3 = (bf16[2,256,384]{2,1,0:T(8,128)(2,1)S(1)}, bf16[2,256,384]{2,1,0:T(8,128)(2,1)S(1)}, u32[]{:S(2)}, u32[]{:S(2)}) collective-permute-start(bf16[2,256,384]{2,1,0:T(8,128)(2,1)S(1)} %bitcast.94), channel_id=1, source_target_pairs={{0,2},{2,4},{4,6},{6,7},{7,5},{5,3},{3,1},{1,0},{8,10},{10,12},{12... | collective-permute-start | bytes 1179656 | tf_op jit(solution)/shard_map/ppermute | solution.py:33
  41.6 11.1 %collective-permute-start.4 = (bf16[2,256,384]{2,1,0:T(8,128)(2,1)S(1)}, bf16[2,256,384]{2,1,0:T(8,128)(2,1)S(1)}, u32[]{:S(2)}, u32[]{:S(2)}) collective-permute-start(bf16[2,256,384]{2,1,0:T(8,128)(2,1)S(1)} %bitcast.95), channel_id=1, source_target_pairs={{0,1},{2,0},{4,2},{6,4},{7,6},{5,7},{3,5},{1,3},{8,9},{10,8},{12,1... | collective-permute-start | bytes 1179656 | tf_op jit(solution)/shard_map/ppermute | solution.py:34
  53.4 10.7 %collective-permute-start.5 = (bf16[2,256,384]{2,1,0:T(8,128)(2,1)S(1)}, bf16[2,256,384]{2,1,0:T(8,128)(2,1)S(1)}, u32[]{:S(2)}, u32[]{:S(2)}) collective-permute-start(bf16[2,256,384]{2,1,0:T(8,128)(2,1)S(1)} %collective-permute-done.3), channel_id=1, source_target_pairs={{0,2},{2,4},{4,6},{6,7},{7,5},{5,3},{3,1},{1,0},{8,10},{10,12},{12... | collective-permute-start | bytes 1179656 | tf_op jit(solution)/shard_map/ppermute | solution.py:33
  54.9 10.0 %collective-permute-start.6 = (bf16[2,256,384]{2,1,0:T(8,128)(2,1)S(1)}, bf16[2,256,384]{2,1,0:T(8,128)(2,1)S(1)}, u32[]{:S(2)}, u32[]{:S(2)}) collective-permute-start(bf16[2,256,384]{2,1,0:T(8,128)(2,1)S(1)} %collective-permute-done.4), channel_id=1, source_target_pairs={{0,1},{2,0},{4,2},{6,4},{7,6},{5,7},{3,5},{1,3},{8,9},{10,8},{12,1... | collective-permute-start | bytes 1179656 | tf_op jit(solution)/shard_map/ppermute | solution.py:34
  65.7 9.8 %collective-permute-start.7 = (bf16[2,256,384]{2,1,0:T(8,128)(2,1)S(1)}, bf16[2,256,384]{2,1,0:T(8,128)(2,1)S(1)}, u32[]{:S(2)}, u32[]{:S(2)}) collective-permute-start(bf16[2,256,384]{2,1,0:T(8,128)(2,1)S(1)} %collective-permute-done.5), channel_id=1, source_target_pairs={{0,2},{2,4},{4,6},{6,7},{7,5},{5,3},{3,1},{1,0},{8,10},{10,12},{12... | collective-permute-start | bytes 1179656 | tf_op jit(solution)/shard_map/ppermute | solution.py:33
  67.2 9.1 %collective-permute-start.8 = (bf16[2,256,384]{2,1,0:T(8,128)(2,1)S(1)}, bf16[2,256,384]{2,1,0:T(8,128)(2,1)S(1)}, u32[]{:S(2)}, u32[]{:S(2)}) collective-permute-start(bf16[2,256,384]{2,1,0:T(8,128)(2,1)S(1)} %collective-permute-done.6), channel_id=1, source_target_pairs={{0,1},{2,0},{4,2},{6,4},{7,6},{5,7},{3,5},{1,3},{8,9},{10,8},{12,1... | collective-permute-start | bytes 1179656 | tf_op jit(solution)/shard_map/ppermute | solution.py:34
  77.1 5.7 %collective-permute-start.9 = (bf16[2,128,384]{2,1,0:T(8,128)(2,1)S(1)}, bf16[2,128,384]{2,1,0:T(8,128)(2,1)S(1)}, u32[]{:S(2)}, u32[]{:S(2)}) collective-permute-start(bf16[2,128,384]{2,1,0:T(8,128)(2,1)S(1)} %slice.30), channel_id=1, source_target_pairs={{0,2},{2,4},{4,6},{6,7},{7,5},{5,3},{3,1},{1,0},{8,10},{10,12},{12... | collective-permute-start | bytes 589832 | tf_op jit(solution)/shard_map/ppermute | solution.py:38
  78.5 5.9 %collective-permute-start.10 = (bf16[2,128,384]{2,1,0:T(8,128)(2,1)S(1)}, bf16[2,128,384]{2,1,0:T(8,128)(2,1)S(1)}, u32[]{:S(2)}, u32[]{:S(2)}) collective-permute-start(bf16[2,128,384]{2,1,0:T(8,128)(2,1)S(1)} %slice.31), channel_id=1, source_target_pairs={{0,1},{2,0},{4,2},{6,4},{7,6},{5,7},{3,5},{1,3},{8,9},{10,8},{12,1... | collective-permute-start | bytes 589832 | tf_op jit(solution)/shard_map/ppermute | solution.py:39
  79.6 7.9 %copy-start.3 = (bf16[384,384]{1,0:T(8,128)(2,1)S(1)}, bf16[384,384]{1,0:T(8,128)(2,1)}, u32[]{:S(2)}) copy-start(bf16[384,384]{1,0:T(8,128)(2,1)} %param.16) | copy-start | bytes 884740
  85.0 1.7 %copy-start.4 = (bf16[2,2048,384]{2,1,0:T(8,128)(2,1)}, bf16[2,2048,384]{2,1,0:T(8,128)(2,1)S(1)}, u32[]{:S(2)}) copy-start(bf16[2,2048,384]{2,1,0:T(8,128)(2,1)S(1)} %constant_dynamic-update-slice_fusion.9) | copy-start | bytes 9437188
  92.9 3.1 %copy-start.8 = (bf16[384,384]{1,0:T(8,128)(2,1)S(1)}, bf16[384,384]{1,0:T(8,128)(2,1)}, u32[]{:S(2)}) copy-start(bf16[384,384]{1,0:T(8,128)(2,1)} %param.19) | copy-start | bytes 884740

commit v11 on v8

--- a/solution.py
+++ b/solution.py
@@ -45,15 +45,7 @@
 
 
 def attend_kernel(query_ref, key_ref, value_ref, out_ref, *, scale):
-    scores = (
-        lax.dot_general(
-            query_ref[0],
-            key_ref[0],
-            (((1,), (1,)), ((), ())),
-            preferred_element_type=jnp.float32,
-        )
-        * scale
-    )
+    scores = jnp.dot(query_ref[0], key_ref[0], preferred_element_type=jnp.float32) * scale
     peaks = jnp.max(scores, axis=-1, keepdims=True)
     weights_exp = jnp.exp(scores - peaks)
     totals = jnp.sum(weights_exp, axis=-1, keepdims=True)
@@ -65,15 +57,15 @@
 
 def attend(queries, keys_all, values_all, scale):
     spans, query_rows, channels = queries.shape
-    key_rows = keys_all.shape[1]
-    block = 128 if query_rows % 128 == 0 else query_rows
+    key_rows = keys_all.shape[2]
+    block = query_rows
     kernel = lambda *refs: attend_kernel(*refs, scale=scale)
     return pl.pallas_call(
         kernel,
         grid=(spans, query_rows // block),
         in_specs=[
             pl.BlockSpec((1, block, channels), lambda f, q: (f, q, 0)),
-            pl.BlockSpec((1, key_rows, channels), lambda f, q: (f, 0, 0)),
+            pl.BlockSpec((1, channels, key_rows), lambda f, q: (f, 0, 0)),
             pl.BlockSpec((1, key_rows, channels), lambda f, q: (f, 0, 0)),
         ],
         out_specs=pl.BlockSpec((1, block, channels), lambda f, q: (f, q, 0)),
@@ -140,7 +132,7 @@
     score_scale = 1.0 / channels**0.5
     tokens_all = ring_gather(tokens, "height", 1)
     keys_all = jnp.einsum(
-        "ftc,cd->ftd", tokens_all, key_weight, preferred_element_type=jnp.float32
+        "ftc,cd->fdt", tokens_all, key_weight, preferred_element_type=jnp.float32
     ).astype(jnp.bfloat16)
     values_all = jnp.einsum(
         "ftc,cd->ftd", tokens_all, value_weight, preferred_element_type=jnp.float32

time: 102 us -> 99.5 us (0.975)
  Pallas kernels: 8.25 us -> 6.1 us
    pallas_call x1, Pallas kernels: 8.25 us -> 6.1 us  [attend(): pl.pallas_call(kernel, grid=(spans, query_rows // block), in_specs=[pl.Bl...]
where the time goes in v11:
time: 99.5 us; the launch traced here: 99.3 us
  waiting for transfers between devices  37.4 us (38%)
  matrix products  26.2 us (26%)
  starting transfers between devices  16.2 us (16%)
  local copies, waits for them, and re-layouts  8.42 us (8%)
  Pallas kernels  6.1 us (6%)
  other arithmetic  4.75 us (5%)
    ppermute x3, waiting for transfers between devices, ring_gather(): backward = lax.ppermute(backward, axis, behind)  24.2 us
    conv_general_dilated x1, matrix products, shards(): lax.conv_general_dilated(window, conv_weight, window_strides=(1, 1, 1), p...  16.3 us
    ppermute x1, waiting for transfers between devices, padded_2(): lax.ppermute(tail, axis, [(i, (i + 1) % count) for i in range(ends)])  7.49 us
    gather x2, local copies, waits for them, and re-layouts, shards(): jnp.take(pool, picks.reshape(-1), axis=0)  6.3 us
    pallas_call x1, Pallas kernels, attend(): pl.pallas_call(kernel, grid=(spans, query_rows // block), in_specs=[pl.Bl...  6.1 us
    ppermute x1, starting transfers between devices, padded_2(): lax.ppermute(tail, axis, [(i, (i + 1) % count) for i in range(ends)])  4.88 us
    ppermute x3, starting transfers between devices, ring_gather(): forward = lax.ppermute(forward, axis, ahead)  3.81 us
    ppermute x1, waiting for transfers between devices, ring_gather(): lax.ppermute(lax.slice_in_dim(forward, 0, half, axis=dim), axis, ahead)  3.79 us
  transfers between devices with their start and end apart: 11, of which 6 were waited for; matrix products, arithmetic and copies ran while one was open for 2% of the time, Pallas kernels for 0%

profile of v11, /device:TPU:0, one launch (start us, length us, event | category | flops | bytes accessed | tf_op | source)
XLA Modules:
  0.0 99.3 jit_solution(18049889053526472332)
XLA Ops:
  0.0 0.0 copy-start
  0.0 1.2 %fusion.3 = f32[2,2,128]{2,1,0:T(2,128)S(1)} fusion(bf16[2,2,128,384]{3,2,1,0:T(8,128)(2,1)} %param.10), kind=kLoop, calls=%fused_computation.16 | loop fusion | flops 589312 | bytes 395264 | tf_op jit(solution)/shard_map/reduce_sum | solution.py:78
  1.2 1.3 %fusion.10 = bf16[2,2,128,384]{3,2,1,0:T(8,128)(2,1)S(1)} fusion(bf16[2,2,128,384]{3,2,1,0:T(8,128)(2,1)} %param.10, f32[384]{0:T(512)} %param.12, f32[2,2,128]{2,1,0:T(2,128)S(1)} %add_rsqrt_fusion.1), kind=kLoop, calls=%fused_computation.23 | loop fusion | flops 1572864 | bytes 790016 | tf_op jit(solution)/shard_map/convert_element_type | solution.py:95
  2.5 0.1 pad_slice_fusion.1
  2.6 4.9 %collective-permute-start = (bf16[2,1,130,384]{3,2,1,0:T(8,128)(2,1)S(1)}, bf16[2,1,130,384]{3,2,1,0:T(8,128)(2,1)S(1)}, u32[]{:S(2)}, u32[]{:S(2)}) collective-permute-start(bf16[2,1,130,384]{3,2,1,0:T(8,128)(2,1)S(1)} %get-tuple-element.9), channel_id=1, source_target_pairs={{0,1},{1,2},{2,3},{3,4},{4,5},{5,6},{6,7},{8,9},{9,10},{10,11},{11... | collective-permute-start | bytes 599048 | tf_op jit(solution)/shard_map/ppermute | solution.py:16
  7.5 1.3 %collective-permute-start.1 = (bf16[2,1,130,384]{3,2,1,0:T(8,128)(2,1)S(1)}, bf16[2,1,130,384]{3,2,1,0:T(8,128)(2,1)S(1)}, u32[]{:S(2)}, u32[]{:S(2)}) collective-permute-start(bf16[2,1,130,384]{3,2,1,0:T(8,128)(2,1)S(1)} %get-tuple-element.10), channel_id=1, source_target_pairs={{1,0},{2,1},{3,2},{4,3},{5,4},{6,5},{7,6},{9,8},{10,9},{11,10},{12... | collective-permute-start | bytes 599048 | tf_op jit(solution)/shard_map/ppermute | solution.py:18
  8.8 0.1 pad.4
  8.9 7.5 %collective-permute-done = bf16[2,1,130,384]{3,2,1,0:T(8,128)(2,1)S(1)} collective-permute-done((bf16[2,1,130,384]{3,2,1,0:T(8,128)(2,1)S(1)}, bf16[2,1,130,384]{3,2,1,0:T(8,128)(2,1)S(1)}, u32[]{:S(2)}, u32[]{:S(2)}) %collective-permute-start) | collective-permute-done | bytes 199712 | tf_op jit(solution)/shard_map/ppermute | solution.py:16
  16.4 0.0 collective-permute-done.1
  16.4 0.1 pad_maximum_fusion
  16.6 0.3 copy.27
  16.9 0.1 collective-permute-start.2
  17.0 0.0 copy-done.5
  17.0 0.1 compare_select_fusion.7
  17.1 0.1 compare_and_fusion
  17.2 0.1 reshape.65
  17.2 0.1 pad.9.clone
  17.3 1.9 %collective-permute-done.2 = bf16[2,4,130,384]{3,1,2,0:T(4,128)(2,1)S(1)} collective-permute-done((bf16[2,4,130,384]{3,1,2,0:T(4,128)(2,1)S(1)}, bf16[2,4,130,384]{3,1,2,0:T(4,128)(2,1)S(1)}, u32[]{:S(2)}, u32[]{:S(2)}) %collective-permute-start.2) | collective-permute-done | bytes 798752 | tf_op jit(solution)/shard_map/ppermute | solution.py:103
  19.3 0.1 copy.28
  19.4 0.4 maximum_maximum_fusion
  19.7 0.8 copy.29
  20.5 4.3 %gather_fusion = bf16[6,4,130,384]{3,1,2,0:T(4,128)(2,1)} fusion(bf16[5,4,130,384]{3,1,2,0:T(4,128)(2,1)S(1)} %copy.29, s32[1024]{0:T(1024)S(1)} %pad_clamp_fusion), kind=kCustom, calls=%fused_computation | custom fusion | bytes 4792344 | tf_op jit(solution)/shard_map/jit(_take)/gather | solution.py:115
  24.8 2.0 %copy.30 = bf16[6,4,130,384]{3,2,1,0:T(8,128)(2,1)S(1)} copy(bf16[6,4,130,384]{3,1,2,0:T(4,128)(2,1)} %gather_fusion) | data formatting | bytes 4792320 | tf_op jit(solution)/shard_map/jit(_take)/gather | solution.py:115
  26.8 0.3 broadcast_select_fusion
  27.2 0.0 copy-start.1
  27.2 0.0 copy-start.6
  27.2 0.0 copy-start.7
  27.2 16.3 %fusion.1 = f32[2,1,2,128,384]{4,0,3,2,1:T(2,128)S(1)} fusion(bf16[3,3,3,384,384]{4,3,2,1,0:T(8,128)(2,1)} %param.13, bf16[2,3,4,130,384]{4,3,2,1,0:T(8,128)(2,1)S(1)} %broadcast_select_fusion), kind=kOutput, calls=%fused_computation.5 | convolution fusion | flops 4076863488 | bytes 11145216 | tf_op jit(solution)/shard_map/conv_general_dilated | solution.py:118
  43.5 0.0 copy-done.1
  43.6 0.0 copy-done.6
  43.6 0.0 copy-start.3
  43.6 0.2 fusion.13
  43.8 0.0 copy-done.7
  43.8 0.2 fusion.15
  44.0 2.5 %collective-permute-start.4 = (bf16[2,256,384]{2,1,0:T(8,128)(2,1)S(1)}, bf16[2,256,384]{2,1,0:T(8,128)(2,1)S(1)}, u32[]{:S(2)}, u32[]{:S(2)}) collective-permute-start(bf16[2,256,384]{2,1,0:T(8,128)(2,1)S(1)} %bitcast.29), channel_id=1, source_target_pairs={{0,1},{2,0},{4,2},{6,4},{7,6},{5,7},{3,5},{1,3},{8,9},{10,8},{12,1... | collective-permute-start | bytes 1179656 | tf_op jit(solution)/shard_map/ppermute | solution.py:35
  46.5 1.0 %collective-permute-start.3 = (bf16[2,256,384]{2,1,0:T(8,128)(2,1)S(1)}, bf16[2,256,384]{2,1,0:T(8,128)(2,1)S(1)}, u32[]{:S(2)}, u32[]{:S(2)}) collective-permute-start(bf16[2,256,384]{2,1,0:T(8,128)(2,1)S(1)} %bitcast.30), channel_id=1, source_target_pairs={{0,2},{2,4},{4,6},{6,7},{7,5},{5,3},{3,1},{1,0},{8,10},{10,12},{12... | collective-permute-start | bytes 1179656 | tf_op jit(solution)/shard_map/ppermute | solution.py:34
  47.5 9.3 %collective-permute-done.4 = bf16[2,256,384]{2,1,0:T(8,128)(2,1)S(1)} collective-permute-done((bf16[2,256,384]{2,1,0:T(8,128)(2,1)S(1)}, bf16[2,256,384]{2,1,0:T(8,128)(2,1)S(1)}, u32[]{:S(2)}, u32[]{:S(2)}) %collective-permute-start.4) | collective-permute-done | bytes 393248 | tf_op jit(solution)/shard_map/ppermute | solution.py:35
  56.9 0.8 collective-permute-start.6
  57.6 0.0 collective-permute-done.3
  57.6 1.2 %collective-permute-start.5 = (bf16[2,256,384]{2,1,0:T(8,128)(2,1)S(1)}, bf16[2,256,384]{2,1,0:T(8,128)(2,1)S(1)}, u32[]{:S(2)}, u32[]{:S(2)}) collective-permute-start(bf16[2,256,384]{2,1,0:T(8,128)(2,1)S(1)} %collective-permute-done.3), channel_id=1, source_target_pairs={{0,2},{2,4},{4,6},{6,7},{7,5},{5,3},{3,1},{1,0},{8,10},{10,12},{12... | collective-permute-start | bytes 1179656 | tf_op jit(solution)/shard_map/ppermute | solution.py:34
  58.9 1.1 %convolution_convert_fusion.2.refs_0_ = bf16[2,256,384]{2,1,0:T(8,128)(2,1)} fusion(bf16[2,256,384]{2,1,0:T(8,128)(2,1)S(1)} %bitcast.32, bf16[384,384]{1,0:T(8,128)(2,1)S(1)} %copy-done.3), kind=kOutput, calls=%fused_computation.8 | convolution fusion | flops 151191552 | bytes 1081344 | tf_op jit(solution)/shard_map/ftc,cd->ftd/dot_general | solution.py:129
  60.1 7.4 %collective-permute-done.6 = bf16[2,256,384]{2,1,0:T(8,128)(2,1)S(1)} collective-permute-done((bf16[2,256,384]{2,1,0:T(8,128)(2,1)S(1)}, bf16[2,256,384]{2,1,0:T(8,128)(2,1)S(1)}, u32[]{:S(2)}, u32[]{:S(2)}) %collective-permute-start.6) | collective-permute-done | bytes 393248 | tf_op jit(solution)/shard_map/ppermute | solution.py:35
  67.5 0.5 collective-permute-start.8
  68.0 0.0 collective-permute-done.5
  68.0 1.6 %collective-permute-start.7 = (bf16[2,256,384]{2,1,0:T(8,128)(2,1)S(1)}, bf16[2,256,384]{2,1,0:T(8,128)(2,1)S(1)}, u32[]{:S(2)}, u32[]{:S(2)}) collective-permute-start(bf16[2,256,384]{2,1,0:T(8,128)(2,1)S(1)} %collective-permute-done.5), channel_id=1, source_target_pairs={{0,2},{2,4},{4,6},{6,7},{7,5},{5,3},{3,1},{1,0},{8,10},{10,12},{12... | collective-permute-start | bytes 1179656 | tf_op jit(solution)/shard_map/ppermute | solution.py:34
  69.5 0.1 constant_dynamic-update-slice_fusion.7
  69.6 0.1 constant_dynamic-update-slice_fusion.6
  69.7 0.1 constant_dynamic-update-slice_fusion.5
  69.7 0.1 constant_dynamic-update-slice_fusion.4
  69.8 7.4 %collective-permute-done.8 = bf16[2,256,384]{2,1,0:T(8,128)(2,1)S(1)} collective-permute-done((bf16[2,256,384]{2,1,0:T(8,128)(2,1)S(1)}, bf16[2,256,384]{2,1,0:T(8,128)(2,1)S(1)}, u32[]{:S(2)}, u32[]{:S(2)}) %collective-permute-start.8) | collective-permute-done | bytes 393248 | tf_op jit(solution)/shard_map/ppermute | solution.py:35
  77.3 0.3 collective-permute-start.10
  77.6 0.0 collective-permute-done.7
  77.6 2.0 %collective-permute-start.9 = (bf16[2,128,384]{2,1,0:T(8,128)(2,1)S(1)}, bf16[2,128,384]{2,1,0:T(8,128)(2,1)S(1)}, u32[]{:S(2)}, u32[]{:S(2)}) collective-permute-start(bf16[2,128,384]{2,1,0:T(8,128)(2,1)S(1)} %slice.26), channel_id=1, source_target_pairs={{0,2},{2,4},{4,6},{6,7},{7,5},{5,3},{3,1},{1,0},{8,10},{10,12},{12... | collective-permute-start | bytes 589832 | tf_op jit(solution)/shard_map/ppermute | solution.py:39
  79.6 0.1 constant_dynamic-update-slice_fusion.3
  79.7 0.1 constant_dynamic-update-slice_fusion.2
  79.8 3.8 %collective-permute-done.9 = bf16[2,128,384]{2,1,0:T(8,128)(2,1)S(1)} collective-permute-done((bf16[2,128,384]{2,1,0:T(8,128)(2,1)S(1)}, bf16[2,128,384]{2,1,0:T(8,128)(2,1)S(1)}, u32[]{:S(2)}, u32[]{:S(2)}) %collective-permute-start.9) | collective-permute-done | bytes 196640 | tf_op jit(solution)/shard_map/ppermute | solution.py:39
  83.6 0.0 collective-permute-done.10
  83.7 0.0 copy-start.2
  83.7 3.8 %convolution_convert_fusion.refs_2_ = bf16[2,2048,384]{2,1,0:T(8,128)(2,1)} fusion(bf16[2,2048,384]{2,1,0:T(8,128)(2,1)S(1)} %constant_dynamic-update-slice_fusion, bf16[384,384]{1,0:T(8,128)(2,1)S(1)} %copy-done), kind=kOutput, calls=%fused_computation.1 | convolution fusion | flops 1209532416 | bytes 6586368 | tf_op jit(solution)/shard_map/ftc,cd->ftd/dot_general | solution.py:137
  87.5 0.0 copy-done.2
  87.5 3.5 %fusion.refs_1_ = bf16[2,384,2048]{2,1,0:T(8,128)(2,1)} fusion(bf16[2,2048,384]{2,1,0:T(8,128)(2,1)S(1)} %constant_dynamic-update-slice_fusion, bf16[384,384]{1,0:T(8,128)(2,1)S(1)} %copy-done.2), kind=kOutput, calls=%fused_computation.3 | convolution fusion | flops 1209532416 | bytes 6586368 | tf_op jit(solution)/shard_map/ftc,cd->fdt/dot_general | solution.py:134
  91.0 6.1 %shard_map.100 = bf16[2,256,384]{2,1,0:T(8,128)(2,1)} custom-call(bf16[2,256,384]{2,1,0:T(8,128)(2,1)} %convolution_convert_fusion.2.refs_0_, bf16[2,384,2048]{2,1,0:T(8,128)(2,1)} %fusion.refs_1_, bf16[2,2048,384]{2,1,0:T(8,128)(2,1)} %convolution_convert_fusion.refs_2_), custom_call_target="tpu_custom_call" | custom-call | tf_op jit(solution)/shard_map/pallas_call | solution.py:63
  97.1 1.4 %fusion.17 = f32[2,256,384]{2,1,0:T(8,128)S(1)} fusion(bf16[2,256,384]{2,1,0:T(8,128)(2,1)} %shard_map.100, bf16[384,384]{1,0:T(8,128)(2,1)S(1)} %copy-done.4), kind=kOutput, calls=%fused_computation.30 | convolution fusion | flops 150994944 | bytes 1474560 | tf_op jit(solution)/shard_map/ftc,cd->ftd/dot_general | solution.py:141
  98.5 0.8 fusion.16
  (15 shorter events, 0.2 us)
Async XLA Ops:
  0.0 83.7 %copy-start = (bf16[384,384]{1,0:T(8,128)(2,1)S(1)}, bf16[384,384]{1,0:T(8,128)(2,1)}, u32[]{:S(2)}) copy-start(bf16[384,384]{1,0:T(8,128)(2,1)} %param.18) | copy-start | bytes 884740
  0.0 17.0 %copy-start.5 = (s32[2,2]{1,0:T(2,128)S(1)}, s32[2,2]{1,0:T(2,128)}, u32[]{:S(2)}) copy-start(s32[2,2]{1,0:T(2,128)} %param.11) | copy-start | bytes 52
  2.6 13.8 %collective-permute-start = (bf16[2,1,130,384]{3,2,1,0:T(8,128)(2,1)S(1)}, bf16[2,1,130,384]{3,2,1,0:T(8,128)(2,1)S(1)}, u32[]{:S(2)}, u32[]{:S(2)}) collective-permute-start(bf16[2,1,130,384]{3,2,1,0:T(8,128)(2,1)S(1)} %get-tuple-element.9), channel_id=1, source_target_pairs={{0,1},{1,2},{2,3},{3,4},{4,5},{5,6},{6,7},{8,9},{9,10},{10,11},{11... | collective-permute-start | bytes 599048 | tf_op jit(solution)/shard_map/ppermute | solution.py:16
  7.5 8.9 %collective-permute-start.1 = (bf16[2,1,130,384]{3,2,1,0:T(8,128)(2,1)S(1)}, bf16[2,1,130,384]{3,2,1,0:T(8,128)(2,1)S(1)}, u32[]{:S(2)}, u32[]{:S(2)}) collective-permute-start(bf16[2,1,130,384]{3,2,1,0:T(8,128)(2,1)S(1)} %get-tuple-element.10), channel_id=1, source_target_pairs={{1,0},{2,1},{3,2},{4,3},{5,4},{6,5},{7,6},{9,8},{10,9},{11,10},{12... | collective-permute-start | bytes 599048 | tf_op jit(solution)/shard_map/ppermute | solution.py:18
  16.9 2.4 %collective-permute-start.2 = (bf16[2,4,130,384]{3,1,2,0:T(4,128)(2,1)S(1)}, bf16[2,4,130,384]{3,1,2,0:T(4,128)(2,1)S(1)}, u32[]{:S(2)}, u32[]{:S(2)}) collective-permute-start(bf16[2,4,130,384]{3,1,2,0:T(4,128)(2,1)S(1)} %copy.27), channel_id=1, source_target_pairs={{0,8},{8,0},{1,9},{9,1},{2,10},{10,2},{3,11},{11,3},{4,12},{12,4},... | collective-permute-start | bytes 2396168 | tf_op jit(solution)/shard_map/ppermute | solution.py:103
  27.2 16.4 %copy-start.1 = (bf16[2,2,128,384]{3,2,1,0:T(8,128)(2,1)S(1)}, bf16[2,2,128,384]{3,2,1,0:T(8,128)(2,1)}, u32[]{:S(2)}) copy-start(bf16[2,2,128,384]{3,2,1,0:T(8,128)(2,1)} %param.10) | copy-start | bytes 1179652
  27.2 16.4 %copy-start.6 = (f32[384]{0:T(512)S(1)}, f32[384]{0:T(512)}, u32[]{:S(2)}) copy-start(f32[384]{0:T(512)} %param.14) | copy-start | bytes 4612
  27.2 16.6 %copy-start.7 = (f32[384]{0:T(512)S(1)}, f32[384]{0:T(512)}, u32[]{:S(2)}) copy-start(f32[384]{0:T(512)} %param.15) | copy-start | bytes 4612
  43.6 15.4 %copy-start.3 = (bf16[384,384]{1,0:T(8,128)(2,1)S(1)}, bf16[384,384]{1,0:T(8,128)(2,1)}, u32[]{:S(2)}) copy-start(bf16[384,384]{1,0:T(8,128)(2,1)} %param.16) | copy-start | bytes 884740
  44.0 12.9 %collective-permute-start.4 = (bf16[2,256,384]{2,1,0:T(8,128)(2,1)S(1)}, bf16[2,256,384]{2,1,0:T(8,128)(2,1)S(1)}, u32[]{:S(2)}, u32[]{:S(2)}) collective-permute-start(bf16[2,256,384]{2,1,0:T(8,128)(2,1)S(1)} %bitcast.29), channel_id=1, source_target_pairs={{0,1},{2,0},{4,2},{6,4},{7,6},{5,7},{3,5},{1,3},{8,9},{10,8},{12,1... | collective-permute-start | bytes 1179656 | tf_op jit(solution)/shard_map/ppermute | solution.py:35
  46.5 11.2 %collective-permute-start.3 = (bf16[2,256,384]{2,1,0:T(8,128)(2,1)S(1)}, bf16[2,256,384]{2,1,0:T(8,128)(2,1)S(1)}, u32[]{:S(2)}, u32[]{:S(2)}) collective-permute-start(bf16[2,256,384]{2,1,0:T(8,128)(2,1)S(1)} %bitcast.30), channel_id=1, source_target_pairs={{0,2},{2,4},{4,6},{6,7},{7,5},{5,3},{3,1},{1,0},{8,10},{10,12},{12... | collective-permute-start | bytes 1179656 | tf_op jit(solution)/shard_map/ppermute | solution.py:34
  56.9 10.6 %collective-permute-start.6 = (bf16[2,256,384]{2,1,0:T(8,128)(2,1)S(1)}, bf16[2,256,384]{2,1,0:T(8,128)(2,1)S(1)}, u32[]{:S(2)}, u32[]{:S(2)}) collective-permute-start(bf16[2,256,384]{2,1,0:T(8,128)(2,1)S(1)} %collective-permute-done.4), channel_id=1, source_target_pairs={{0,1},{2,0},{4,2},{6,4},{7,6},{5,7},{3,5},{1,3},{8,9},{10,8},{12,1... | collective-permute-start | bytes 1179656 | tf_op jit(solution)/shard_map/ppermute | solution.py:35
  57.6 10.3 %collective-permute-start.5 = (bf16[2,256,384]{2,1,0:T(8,128)(2,1)S(1)}, bf16[2,256,384]{2,1,0:T(8,128)(2,1)S(1)}, u32[]{:S(2)}, u32[]{:S(2)}) collective-permute-start(bf16[2,256,384]{2,1,0:T(8,128)(2,1)S(1)} %collective-permute-done.3), channel_id=1, source_target_pairs={{0,2},{2,4},{4,6},{6,7},{7,5},{5,3},{3,1},{1,0},{8,10},{10,12},{12... | collective-permute-start | bytes 1179656 | tf_op jit(solution)/shard_map/ppermute | solution.py:34
  67.5 9.7 %collective-permute-start.8 = (bf16[2,256,384]{2,1,0:T(8,128)(2,1)S(1)}, bf16[2,256,384]{2,1,0:T(8,128)(2,1)S(1)}, u32[]{:S(2)}, u32[]{:S(2)}) collective-permute-start(bf16[2,256,384]{2,1,0:T(8,128)(2,1)S(1)} %collective-permute-done.6), channel_id=1, source_target_pairs={{0,1},{2,0},{4,2},{6,4},{7,6},{5,7},{3,5},{1,3},{8,9},{10,8},{12,1... | collective-permute-start | bytes 1179656 | tf_op jit(solution)/shard_map/ppermute | solution.py:35
  68.0 9.6 %collective-permute-start.7 = (bf16[2,256,384]{2,1,0:T(8,128)(2,1)S(1)}, bf16[2,256,384]{2,1,0:T(8,128)(2,1)S(1)}, u32[]{:S(2)}, u32[]{:S(2)}) collective-permute-start(bf16[2,256,384]{2,1,0:T(8,128)(2,1)S(1)} %collective-permute-done.5), channel_id=1, source_target_pairs={{0,2},{2,4},{4,6},{6,7},{7,5},{5,3},{3,1},{1,0},{8,10},{10,12},{12... | collective-permute-start | bytes 1179656 | tf_op jit(solution)/shard_map/ppermute | solution.py:34
  77.3 6.3 %collective-permute-start.10 = (bf16[2,128,384]{2,1,0:T(8,128)(2,1)S(1)}, bf16[2,128,384]{2,1,0:T(8,128)(2,1)S(1)}, u32[]{:S(2)}, u32[]{:S(2)}) collective-permute-start(bf16[2,128,384]{2,1,0:T(8,128)(2,1)S(1)} %slice.27), channel_id=1, source_target_pairs={{0,1},{2,0},{4,2},{6,4},{7,6},{5,7},{3,5},{1,3},{8,9},{10,8},{12,1... | collective-permute-start | bytes 589832 | tf_op jit(solution)/shard_map/ppermute | solution.py:40
  77.6 5.9 %collective-permute-start.9 = (bf16[2,128,384]{2,1,0:T(8,128)(2,1)S(1)}, bf16[2,128,384]{2,1,0:T(8,128)(2,1)S(1)}, u32[]{:S(2)}, u32[]{:S(2)}) collective-permute-start(bf16[2,128,384]{2,1,0:T(8,128)(2,1)S(1)} %slice.26), channel_id=1, source_target_pairs={{0,2},{2,4},{4,6},{6,7},{7,5},{5,3},{3,1},{1,0},{8,10},{10,12},{12... | collective-permute-start | bytes 589832 | tf_op jit(solution)/shard_map/ppermute | solution.py:39
  83.7 3.8 %copy-start.2 = (bf16[384,384]{1,0:T(8,128)(2,1)S(1)}, bf16[384,384]{1,0:T(8,128)(2,1)}, u32[]{:S(2)}) copy-start(bf16[384,384]{1,0:T(8,128)(2,1)} %param.17) | copy-start | bytes 884740
  91.0 6.1 %copy-start.4 = (bf16[384,384]{1,0:T(8,128)(2,1)S(1)}, bf16[384,384]{1,0:T(8,128)(2,1)}, u32[]{:S(2)}) copy-start(bf16[384,384]{1,0:T(8,128)(2,1)} %param.19) | copy-start | bytes 884740

commit v12 on v8

--- a/solution.py
+++ b/solution.py
@@ -44,41 +44,44 @@
     return jnp.concatenate(pieces, axis=dim)
 
 
-def attend_kernel(query_ref, key_ref, value_ref, out_ref, *, scale):
+def attend_kernel(query_ref, token_ref, key_w_ref, value_w_ref, out_ref, *, scale):
+    tokens = token_ref[0]
+    keys = jnp.dot(tokens, key_w_ref[...], preferred_element_type=jnp.float32).astype(
+        jnp.bfloat16
+    )
+    values = jnp.dot(tokens, value_w_ref[...], preferred_element_type=jnp.float32).astype(
+        jnp.bfloat16
+    )
     scores = (
         lax.dot_general(
-            query_ref[0],
-            key_ref[0],
-            (((1,), (1,)), ((), ())),
-            preferred_element_type=jnp.float32,
+            query_ref[0], keys, (((1,), (1,)), ((), ())), preferred_element_type=jnp.float32
         )
         * scale
     )
     peaks = jnp.max(scores, axis=-1, keepdims=True)
     weights_exp = jnp.exp(scores - peaks)
     totals = jnp.sum(weights_exp, axis=-1, keepdims=True)
-    summed = jnp.dot(
-        weights_exp.astype(jnp.bfloat16), value_ref[0], preferred_element_type=jnp.float32
-    )
+    summed = jnp.dot(weights_exp.astype(jnp.bfloat16), values, preferred_element_type=jnp.float32)
     out_ref[0] = (summed / totals).astype(out_ref.dtype)
 
 
-def attend(queries, keys_all, values_all, scale):
+def attend(queries, tokens_all, key_weight, value_weight, scale):
     spans, query_rows, channels = queries.shape
-    key_rows = keys_all.shape[1]
-    block = 128 if query_rows % 128 == 0 else query_rows
+    key_rows = tokens_all.shape[1]
     kernel = lambda *refs: attend_kernel(*refs, scale=scale)
+    weight_spec = pl.BlockSpec((channels, channels), lambda f: (0, 0))
     return pl.pallas_call(
         kernel,
-        grid=(spans, query_rows // block),
+        grid=(spans,),
         in_specs=[
-            pl.BlockSpec((1, block, channels), lambda f, q: (f, q, 0)),
-            pl.BlockSpec((1, key_rows, channels), lambda f, q: (f, 0, 0)),
-            pl.BlockSpec((1, key_rows, channels), lambda f, q: (f, 0, 0)),
+            pl.BlockSpec((1, query_rows, channels), lambda f: (f, 0, 0)),
+            pl.BlockSpec((1, key_rows, channels), lambda f: (f, 0, 0)),
+            weight_spec,
+            weight_spec,
         ],
-        out_specs=pl.BlockSpec((1, block, channels), lambda f, q: (f, q, 0)),
+        out_specs=pl.BlockSpec((1, query_rows, channels), lambda f: (f, 0, 0)),
         out_shape=jax.ShapeDtypeStruct(queries.shape, jnp.bfloat16),
-    )(queries, keys_all, values_all)
+    )(queries, tokens_all, key_weight, value_weight)
 
 
 def rms_scaled(frames, gain):
@@ -139,13 +142,7 @@
     ).astype(jnp.bfloat16)
     score_scale = 1.0 / channels**0.5
     tokens_all = ring_gather(tokens, "height", 1)
-    keys_all = jnp.einsum(
-        "ftc,cd->ftd", tokens_all, key_weight, preferred_element_type=jnp.float32
-    ).astype(jnp.bfloat16)
-    values_all = jnp.einsum(
-        "ftc,cd->ftd", tokens_all, value_weight, preferred_element_type=jnp.float32
-    ).astype(jnp.bfloat16)
-    attended = attend(queries, keys_all, values_all, score_scale)
+    attended = attend(queries, tokens_all, key_weight, value_weight, score_scale)
     projected = jnp.einsum("ftc,cd->ftd", attended, out_weight, preferred_element_type=jnp.float32)
     encoded = mixed.astype(jnp.float32) + projected.reshape(
         span_count, row_count, col_count, channels

time: 102 us -> 98.7 us (0.968)
  matrix products: 26.4 us -> 18.6 us
  local copies, waits for them, and re-layouts: 8.42 us -> 10.1 us
  Pallas kernels: 8.25 us -> 9.59 us
    ppermute x3, waiting for transfers between devices: 24.2 us -> 0.01 us  [ring_gather(): backward = lax.ppermute(backward, axis, behind)]
    ppermute x3, waiting for transfers between devices: 0.01 us -> 22.2 us  [ring_gather(): forward = lax.ppermute(forward, axis, ahead)]
    dot_general x2 -> x0, matrix products: 7.51 us -> none  [the longest x1 3.77 us: shards(): jnp.einsum('ftc,cd->ftd', tokens_all, value_weight, preferred_element_typ...]
    ppermute x3, starting transfers between devices: 3.81 us -> 8.32 us  [ring_gather(): forward = lax.ppermute(forward, axis, ahead)]
    ppermute x3, starting transfers between devices: 3.76 us -> 0.01 us  [ring_gather(): backward = lax.ppermute(backward, axis, behind)]
    ppermute x1, waiting for transfers between devices: 0.01 us -> 2.34 us  [ring_gather(): lax.ppermute(lax.slice_in_dim(backward, half, block.shape[dim], axis=dim)...]
    unnamed x24 -> x22, local copies, waits for them, and re-layouts: 0.5 us -> 2.13 us
    pallas_call x1, Pallas kernels: 8.25 us -> 9.59 us  [attend(): pl.pallas_call(kernel, grid=(spans,), in_specs=[pl.BlockSpec((1, query_ro...]
  transfers between devices with their start and end apart: 11 -> 11, of which waited for: 6 -> 7; matrix products, arithmetic and copies ran while one was open for 2% -> 2% of each run, Pallas kernels for 0% -> 0%
where the time goes in v12:
time: 98.7 us; the launch traced here: 98.4 us
  waiting for transfers between devices  37.1 us (38%)
  matrix products  18.6 us (19%)
  starting transfers between devices  17 us (17%)
  local copies, waits for them, and re-layouts  10.1 us (10%)
  Pallas kernels  9.59 us (10%)
  other arithmetic  5.74 us (6%)
    ppermute x3, waiting for transfers between devices, ring_gather(): forward = lax.ppermute(forward, axis, ahead)  22.2 us
    conv_general_dilated x1, matrix products, shards(): lax.conv_general_dilated(window, conv_weight, window_strides=(1, 1, 1), p...  16 us
    pallas_call x1, Pallas kernels, attend(): pl.pallas_call(kernel, grid=(spans,), in_specs=[pl.BlockSpec((1, query_ro...  9.59 us
    ppermute x3, starting transfers between devices, ring_gather(): forward = lax.ppermute(forward, axis, ahead)  8.32 us
    ppermute x1, waiting for transfers between devices, padded_2(): lax.ppermute(tail, axis, [(i, (i + 1) % count) for i in range(ends)])  7.49 us
    gather x2, local copies, waits for them, and re-layouts, shards(): jnp.take(pool, picks.reshape(-1), axis=0)  6.3 us
    ppermute x1, starting transfers between devices, padded_2(): lax.ppermute(tail, axis, [(i, (i + 1) % count) for i in range(ends)])  4.88 us
    ppermute x1, waiting for transfers between devices, ring_gather(): lax.ppermute(lax.slice_in_dim(forward, 0, half, axis=dim), axis, ahead)  3.14 us
  transfers between devices with their start and end apart: 11, of which 7 were waited for; matrix products, arithmetic and copies ran while one was open for 2% of the time, Pallas kernels for 0%

profile of v12, /device:TPU:0, one launch (start us, length us, event | category | flops | bytes accessed | tf_op | source)
XLA Modules:
  0.0 98.4 jit_solution(13886759938282667143)
XLA Ops:
  0.0 0.0 copy-start
  0.0 0.0 copy-start.4
  0.0 1.2 %fusion.2 = f32[2,2,128]{2,1,0:T(2,128)S(1)} fusion(bf16[2,2,128,384]{3,2,1,0:T(8,128)(2,1)} %param.10), kind=kLoop, calls=%fused_computation.13 | loop fusion | flops 589312 | bytes 395264 | tf_op jit(solution)/shard_map/reduce_sum | solution.py:89
  1.2 1.3 %fusion.9 = bf16[2,2,128,384]{3,2,1,0:T(8,128)(2,1)S(1)} fusion(bf16[2,2,128,384]{3,2,1,0:T(8,128)(2,1)} %param.10, f32[384]{0:T(512)} %param.12, f32[2,2,128]{2,1,0:T(2,128)S(1)} %add_rsqrt_fusion.1), kind=kLoop, calls=%fused_computation.20 | loop fusion | flops 1572864 | bytes 790016 | tf_op jit(solution)/shard_map/convert_element_type | solution.py:106
  2.5 0.1 pad_slice_fusion.1
  2.6 4.9 %collective-permute-start = (bf16[2,1,130,384]{3,2,1,0:T(8,128)(2,1)S(1)}, bf16[2,1,130,384]{3,2,1,0:T(8,128)(2,1)S(1)}, u32[]{:S(2)}, u32[]{:S(2)}) collective-permute-start(bf16[2,1,130,384]{3,2,1,0:T(8,128)(2,1)S(1)} %get-tuple-element.9), channel_id=1, source_target_pairs={{0,1},{1,2},{2,3},{3,4},{4,5},{5,6},{6,7},{8,9},{9,10},{10,11},{11... | collective-permute-start | bytes 599048 | tf_op jit(solution)/shard_map/ppermute | solution.py:16
  7.5 1.3 %collective-permute-start.1 = (bf16[2,1,130,384]{3,2,1,0:T(8,128)(2,1)S(1)}, bf16[2,1,130,384]{3,2,1,0:T(8,128)(2,1)S(1)}, u32[]{:S(2)}, u32[]{:S(2)}) collective-permute-start(bf16[2,1,130,384]{3,2,1,0:T(8,128)(2,1)S(1)} %get-tuple-element.10), channel_id=1, source_target_pairs={{1,0},{2,1},{3,2},{4,3},{5,4},{6,5},{7,6},{9,8},{10,9},{11,10},{12... | collective-permute-start | bytes 599048 | tf_op jit(solution)/shard_map/ppermute | solution.py:18
  8.8 0.1 pad.4
  8.9 7.5 %collective-permute-done = bf16[2,1,130,384]{3,2,1,0:T(8,128)(2,1)S(1)} collective-permute-done((bf16[2,1,130,384]{3,2,1,0:T(8,128)(2,1)S(1)}, bf16[2,1,130,384]{3,2,1,0:T(8,128)(2,1)S(1)}, u32[]{:S(2)}, u32[]{:S(2)}) %collective-permute-start) | collective-permute-done | bytes 199712 | tf_op jit(solution)/shard_map/ppermute | solution.py:16
  16.4 0.0 collective-permute-done.1
  16.4 0.1 pad_maximum_fusion
  16.6 0.3 copy.28
  16.9 0.1 collective-permute-start.2
  17.0 0.0 copy-done.4
  17.0 0.1 compare_select_fusion.7
  17.1 0.1 compare_and_fusion
  17.2 0.1 reshape.65
  17.2 0.1 pad.9.clone
  17.3 1.9 %collective-permute-done.2 = bf16[2,4,130,384]{3,1,2,0:T(4,128)(2,1)S(1)} collective-permute-done((bf16[2,4,130,384]{3,1,2,0:T(4,128)(2,1)S(1)}, bf16[2,4,130,384]{3,1,2,0:T(4,128)(2,1)S(1)}, u32[]{:S(2)}, u32[]{:S(2)}) %collective-permute-start.2) | collective-permute-done | bytes 798752 | tf_op jit(solution)/shard_map/ppermute | solution.py:114
  19.3 0.1 copy.29
  19.4 0.4 maximum_maximum_fusion
  19.7 0.8 copy.30
  20.5 4.3 %gather_fusion = bf16[6,4,130,384]{3,1,2,0:T(4,128)(2,1)} fusion(bf16[5,4,130,384]{3,1,2,0:T(4,128)(2,1)S(1)} %copy.30, s32[1024]{0:T(1024)S(1)} %pad_clamp_fusion), kind=kCustom, calls=%fused_computation | custom fusion | bytes 4792344 | tf_op jit(solution)/shard_map/jit(_take)/gather | solution.py:126
  24.8 2.0 %copy.31 = bf16[6,4,130,384]{3,2,1,0:T(8,128)(2,1)S(1)} copy(bf16[6,4,130,384]{3,1,2,0:T(4,128)(2,1)} %gather_fusion) | data formatting | bytes 4792320 | tf_op jit(solution)/shard_map/jit(_take)/gather | solution.py:126
  26.8 0.3 broadcast_select_fusion
  27.2 0.0 copy-start.2
  27.2 0.0 copy-start.5
  27.2 0.0 copy-start.6
  27.2 16.0 %fusion = f32[2,1,2,128,384]{4,0,3,2,1:T(2,128)S(1)} fusion(bf16[3,3,3,384,384]{4,3,2,1,0:T(8,128)(2,1)} %param.13, bf16[2,3,4,130,384]{4,3,2,1,0:T(8,128)(2,1)S(1)} %broadcast_select_fusion), kind=kOutput, calls=%fused_computation.2 | convolution fusion | flops 4076863488 | bytes 11145216 | tf_op jit(solution)/shard_map/conv_general_dilated | solution.py:129
  43.2 0.0 copy-done.2
  43.2 0.0 copy-done.5
  43.3 0.2 fusion.12
  43.5 0.0 copy-done.6
  43.5 0.2 fusion.14
  43.7 3.5 %collective-permute-start.3 = (bf16[2,256,384]{2,1,0:T(8,128)(2,1)S(1)}, bf16[2,256,384]{2,1,0:T(8,128)(2,1)S(1)}, u32[]{:S(2)}, u32[]{:S(2)}) collective-permute-start(bf16[2,256,384]{2,1,0:T(8,128)(2,1)S(1)} %bitcast.19), channel_id=1, source_target_pairs={{0,2},{2,4},{4,6},{6,7},{7,5},{5,3},{3,1},{1,0},{8,10},{10,12},{12... | collective-permute-start | bytes 1179656 | tf_op jit(solution)/shard_map/ppermute | solution.py:34
  47.1 0.0 collective-permute-start.4
  47.1 8.7 %collective-permute-done.3 = bf16[2,256,384]{2,1,0:T(8,128)(2,1)S(1)} collective-permute-done((bf16[2,256,384]{2,1,0:T(8,128)(2,1)S(1)}, bf16[2,256,384]{2,1,0:T(8,128)(2,1)S(1)}, u32[]{:S(2)}, u32[]{:S(2)}) %collective-permute-start.3) | collective-permute-done | bytes 393248 | tf_op jit(solution)/shard_map/ppermute | solution.py:34
  55.8 2.5 %collective-permute-start.5 = (bf16[2,256,384]{2,1,0:T(8,128)(2,1)S(1)}, bf16[2,256,384]{2,1,0:T(8,128)(2,1)S(1)}, u32[]{:S(2)}, u32[]{:S(2)}) collective-permute-start(bf16[2,256,384]{2,1,0:T(8,128)(2,1)S(1)} %collective-permute-done.3), channel_id=1, source_target_pairs={{0,2},{2,4},{4,6},{6,7},{7,5},{5,3},{3,1},{1,0},{8,10},{10,12},{12... | collective-permute-start | bytes 1179656 | tf_op jit(solution)/shard_map/ppermute | solution.py:34
  58.3 0.0 collective-permute-done.4
  58.3 0.0 collective-permute-start.6
  58.3 0.0 copy-done
  58.4 1.1 %convolution_convert_fusion.refs_0_ = bf16[2,256,384]{2,1,0:T(8,128)(2,1)} fusion(bf16[2,256,384]{2,1,0:T(8,128)(2,1)S(1)} %bitcast.22, bf16[384,384]{1,0:T(8,128)(2,1)S(1)} %copy-done), kind=kOutput, calls=%fused_computation.5 | convolution fusion | flops 151191552 | bytes 1081344 | tf_op jit(solution)/shard_map/ftc,cd->ftd/dot_general | solution.py:140
  59.5 6.7 %collective-permute-done.5 = bf16[2,256,384]{2,1,0:T(8,128)(2,1)S(1)} collective-permute-done((bf16[2,256,384]{2,1,0:T(8,128)(2,1)S(1)}, bf16[2,256,384]{2,1,0:T(8,128)(2,1)S(1)}, u32[]{:S(2)}, u32[]{:S(2)}) %collective-permute-start.5) | collective-permute-done | bytes 393248 | tf_op jit(solution)/shard_map/ppermute | solution.py:34
  66.2 2.4 %collective-permute-start.7 = (bf16[2,256,384]{2,1,0:T(8,128)(2,1)S(1)}, bf16[2,256,384]{2,1,0:T(8,128)(2,1)S(1)}, u32[]{:S(2)}, u32[]{:S(2)}) collective-permute-start(bf16[2,256,384]{2,1,0:T(8,128)(2,1)S(1)} %collective-permute-done.5), channel_id=1, source_target_pairs={{0,2},{2,4},{4,6},{6,7},{7,5},{5,3},{3,1},{1,0},{8,10},{10,12},{12... | collective-permute-start | bytes 1179656 | tf_op jit(solution)/shard_map/ppermute | solution.py:34
  68.6 0.0 collective-permute-done.6
  68.6 0.0 collective-permute-start.8
  68.6 0.1 constant_dynamic-update-slice_fusion.7
  68.7 0.1 constant_dynamic-update-slice_fusion.6
  68.8 0.1 constant_dynamic-update-slice_fusion.5
  68.8 0.1 constant_dynamic-update-slice_fusion.4
  68.9 6.8 %collective-permute-done.7 = bf16[2,256,384]{2,1,0:T(8,128)(2,1)S(1)} collective-permute-done((bf16[2,256,384]{2,1,0:T(8,128)(2,1)S(1)}, bf16[2,256,384]{2,1,0:T(8,128)(2,1)S(1)}, u32[]{:S(2)}, u32[]{:S(2)}) %collective-permute-start.7) | collective-permute-done | bytes 393248 | tf_op jit(solution)/shard_map/ppermute | solution.py:34
  75.8 2.3 %collective-permute-start.9 = (bf16[2,128,384]{2,1,0:T(8,128)(2,1)S(1)}, bf16[2,128,384]{2,1,0:T(8,128)(2,1)S(1)}, u32[]{:S(2)}, u32[]{:S(2)}) collective-permute-start(bf16[2,128,384]{2,1,0:T(8,128)(2,1)S(1)} %slice.26), channel_id=1, source_target_pairs={{0,2},{2,4},{4,6},{6,7},{7,5},{5,3},{3,1},{1,0},{8,10},{10,12},{12... | collective-permute-start | bytes 589832 | tf_op jit(solution)/shard_map/ppermute | solution.py:39
  78.1 0.0 collective-permute-done.8
  78.1 0.0 copy-done.3
  78.1 0.1 collective-permute-start.10
  78.2 0.1 constant_dynamic-update-slice_fusion.3
  78.3 0.1 constant_dynamic-update-slice_fusion.2
  78.4 3.1 %collective-permute-done.9 = bf16[2,128,384]{2,1,0:T(8,128)(2,1)S(1)} collective-permute-done((bf16[2,128,384]{2,1,0:T(8,128)(2,1)S(1)}, bf16[2,128,384]{2,1,0:T(8,128)(2,1)S(1)}, u32[]{:S(2)}, u32[]{:S(2)}) %collective-permute-start.9) | collective-permute-done | bytes 196640 | tf_op jit(solution)/shard_map/ppermute | solution.py:39
  81.5 2.3 %collective-permute-done.10 = bf16[2,128,384]{2,1,0:T(8,128)(2,1)S(1)} collective-permute-done((bf16[2,128,384]{2,1,0:T(8,128)(2,1)S(1)}, bf16[2,128,384]{2,1,0:T(8,128)(2,1)S(1)}, u32[]{:S(2)}, u32[]{:S(2)}) %collective-permute-start.10) | collective-permute-done | bytes 196640 | tf_op jit(solution)/shard_map/ppermute | solution.py:40
  83.9 0.0 copy-start.1
  83.9 1.6 %copy-done.1 = bf16[2,2048,384]{2,1,0:T(8,128)(2,1)} copy-done((bf16[2,2048,384]{2,1,0:T(8,128)(2,1)}, bf16[2,2048,384]{2,1,0:T(8,128)(2,1)S(1)}, u32[]{:S(2)}) %copy-start.1) | copy-done | bytes 3145752
  85.6 9.6 %shard_map.100 = bf16[2,256,384]{2,1,0:T(8,128)(2,1)} custom-call(bf16[2,256,384]{2,1,0:T(8,128)(2,1)} %convolution_convert_fusion.refs_0_, bf16[2,2048,384]{2,1,0:T(8,128)(2,1)} %copy-done.1, bf16[384,384]{1,0:T(8,128)(2,1)} %refs_2_.1, bf16[384,384]{1,0:T(8,128)(2,1)} %refs_3_.1), custom_call_target="tpu_custom_call" | custom-call | tf_op jit(solution)/shard_map/pallas_call | solution.py:73
  95.1 1.5 %fusion.16 = f32[2,256,384]{2,1,0:T(8,128)S(1)} fusion(bf16[2,256,384]{2,1,0:T(8,128)(2,1)} %shard_map.100, bf16[384,384]{1,0:T(8,128)(2,1)} %param.19), kind=kOutput, calls=%fused_computation.27 | convolution fusion | flops 150994944 | bytes 1474560 | tf_op jit(solution)/shard_map/ftc,cd->ftd/dot_general | solution.py:146
  96.6 1.8 %fusion.15 = bf16[2,2,128,384]{3,2,1,0:T(8,128)(2,1)} fusion(f32[2,2,128,384]{3,2,1,0:T(8,128)S(1)} %bitcast.23, bf16[2,2,128,384]{3,2,1,0:T(8,128)(2,1)} %copy-done.3), kind=kLoop, calls=%fused_computation.26 | loop fusion | flops 589824 | bytes 1572864 | tf_op jit(solution)/shard_map/convert_element_type | solution.py:150
  (11 shorter events, 0.2 us)
Async XLA Ops:
  0.0 58.3 %copy-start = (bf16[384,384]{1,0:T(8,128)(2,1)S(1)}, bf16[384,384]{1,0:T(8,128)(2,1)}, u32[]{:S(2)}) copy-start(bf16[384,384]{1,0:T(8,128)(2,1)} %param.16) | copy-start | bytes 884740
  0.0 17.0 %copy-start.4 = (s32[2,2]{1,0:T(2,128)S(1)}, s32[2,2]{1,0:T(2,128)}, u32[]{:S(2)}) copy-start(s32[2,2]{1,0:T(2,128)} %param.11) | copy-start | bytes 52
  2.6 13.8 %collective-permute-start = (bf16[2,1,130,384]{3,2,1,0:T(8,128)(2,1)S(1)}, bf16[2,1,130,384]{3,2,1,0:T(8,128)(2,1)S(1)}, u32[]{:S(2)}, u32[]{:S(2)}) collective-permute-start(bf16[2,1,130,384]{3,2,1,0:T(8,128)(2,1)S(1)} %get-tuple-element.9), channel_id=1, source_target_pairs={{0,1},{1,2},{2,3},{3,4},{4,5},{5,6},{6,7},{8,9},{9,10},{10,11},{11... | collective-permute-start | bytes 599048 | tf_op jit(solution)/shard_map/ppermute | solution.py:16
  7.5 8.9 %collective-permute-start.1 = (bf16[2,1,130,384]{3,2,1,0:T(8,128)(2,1)S(1)}, bf16[2,1,130,384]{3,2,1,0:T(8,128)(2,1)S(1)}, u32[]{:S(2)}, u32[]{:S(2)}) collective-permute-start(bf16[2,1,130,384]{3,2,1,0:T(8,128)(2,1)S(1)} %get-tuple-element.10), channel_id=1, source_target_pairs={{1,0},{2,1},{3,2},{4,3},{5,4},{6,5},{7,6},{9,8},{10,9},{11,10},{12... | collective-permute-start | bytes 599048 | tf_op jit(solution)/shard_map/ppermute | solution.py:18
  16.9 2.4 %collective-permute-start.2 = (bf16[2,4,130,384]{3,1,2,0:T(4,128)(2,1)S(1)}, bf16[2,4,130,384]{3,1,2,0:T(4,128)(2,1)S(1)}, u32[]{:S(2)}, u32[]{:S(2)}) collective-permute-start(bf16[2,4,130,384]{3,1,2,0:T(4,128)(2,1)S(1)} %copy.28), channel_id=1, source_target_pairs={{0,8},{8,0},{1,9},{9,1},{2,10},{10,2},{3,11},{11,3},{4,12},{12,4},... | collective-permute-start | bytes 2396168 | tf_op jit(solution)/shard_map/ppermute | solution.py:114
  27.2 16.1 %copy-start.2 = (bf16[2,2,128,384]{3,2,1,0:T(8,128)(2,1)S(1)}, bf16[2,2,128,384]{3,2,1,0:T(8,128)(2,1)}, u32[]{:S(2)}) copy-start(bf16[2,2,128,384]{3,2,1,0:T(8,128)(2,1)} %param.10) | copy-start | bytes 1179652
  27.2 16.1 %copy-start.5 = (f32[384]{0:T(512)S(1)}, f32[384]{0:T(512)}, u32[]{:S(2)}) copy-start(f32[384]{0:T(512)} %param.14) | copy-start | bytes 4612
  27.2 16.3 %copy-start.6 = (f32[384]{0:T(512)S(1)}, f32[384]{0:T(512)}, u32[]{:S(2)}) copy-start(f32[384]{0:T(512)} %param.15) | copy-start | bytes 4612
  43.5 34.7 %copy-start.3 = (bf16[2,2,128,384]{3,2,1,0:T(8,128)(2,1)}, bf16[2,2,128,384]{3,2,1,0:T(8,128)(2,1)S(1)}, u32[]{:S(2)}) copy-start(bf16[2,2,128,384]{3,2,1,0:T(8,128)(2,1)S(1)} %get-tuple-element.6) | copy-start | bytes 1179652
  43.7 12.1 %collective-permute-start.3 = (bf16[2,256,384]{2,1,0:T(8,128)(2,1)S(1)}, bf16[2,256,384]{2,1,0:T(8,128)(2,1)S(1)}, u32[]{:S(2)}, u32[]{:S(2)}) collective-permute-start(bf16[2,256,384]{2,1,0:T(8,128)(2,1)S(1)} %bitcast.19), channel_id=1, source_target_pairs={{0,2},{2,4},{4,6},{6,7},{7,5},{5,3},{3,1},{1,0},{8,10},{10,12},{12... | collective-permute-start | bytes 1179656 | tf_op jit(solution)/shard_map/ppermute | solution.py:34
  47.1 11.2 %collective-permute-start.4 = (bf16[2,256,384]{2,1,0:T(8,128)(2,1)S(1)}, bf16[2,256,384]{2,1,0:T(8,128)(2,1)S(1)}, u32[]{:S(2)}, u32[]{:S(2)}) collective-permute-start(bf16[2,256,384]{2,1,0:T(8,128)(2,1)S(1)} %bitcast.20), channel_id=1, source_target_pairs={{0,1},{2,0},{4,2},{6,4},{7,6},{5,7},{3,5},{1,3},{8,9},{10,8},{12,1... | collective-permute-start | bytes 1179656 | tf_op jit(solution)/shard_map/ppermute | solution.py:35
  55.8 10.4 %collective-permute-start.5 = (bf16[2,256,384]{2,1,0:T(8,128)(2,1)S(1)}, bf16[2,256,384]{2,1,0:T(8,128)(2,1)S(1)}, u32[]{:S(2)}, u32[]{:S(2)}) collective-permute-start(bf16[2,256,384]{2,1,0:T(8,128)(2,1)S(1)} %collective-permute-done.3), channel_id=1, source_target_pairs={{0,2},{2,4},{4,6},{6,7},{7,5},{5,3},{3,1},{1,0},{8,10},{10,12},{12... | collective-permute-start | bytes 1179656 | tf_op jit(solution)/shard_map/ppermute | solution.py:34
  58.3 10.3 %collective-permute-start.6 = (bf16[2,256,384]{2,1,0:T(8,128)(2,1)S(1)}, bf16[2,256,384]{2,1,0:T(8,128)(2,1)S(1)}, u32[]{:S(2)}, u32[]{:S(2)}) collective-permute-start(bf16[2,256,384]{2,1,0:T(8,128)(2,1)S(1)} %collective-permute-done.4), channel_id=1, source_target_pairs={{0,1},{2,0},{4,2},{6,4},{7,6},{5,7},{3,5},{1,3},{8,9},{10,8},{12,1... | collective-permute-start | bytes 1179656 | tf_op jit(solution)/shard_map/ppermute | solution.py:35
  66.2 9.5 %collective-permute-start.7 = (bf16[2,256,384]{2,1,0:T(8,128)(2,1)S(1)}, bf16[2,256,384]{2,1,0:T(8,128)(2,1)S(1)}, u32[]{:S(2)}, u32[]{:S(2)}) collective-permute-start(bf16[2,256,384]{2,1,0:T(8,128)(2,1)S(1)} %collective-permute-done.5), channel_id=1, source_target_pairs={{0,2},{2,4},{4,6},{6,7},{7,5},{5,3},{3,1},{1,0},{8,10},{10,12},{12... | collective-permute-start | bytes 1179656 | tf_op jit(solution)/shard_map/ppermute | solution.py:34
  68.6 9.5 %collective-permute-start.8 = (bf16[2,256,384]{2,1,0:T(8,128)(2,1)S(1)}, bf16[2,256,384]{2,1,0:T(8,128)(2,1)S(1)}, u32[]{:S(2)}, u32[]{:S(2)}) collective-permute-start(bf16[2,256,384]{2,1,0:T(8,128)(2,1)S(1)} %collective-permute-done.6), channel_id=1, source_target_pairs={{0,1},{2,0},{4,2},{6,4},{7,6},{5,7},{3,5},{1,3},{8,9},{10,8},{12,1... | collective-permute-start | bytes 1179656 | tf_op jit(solution)/shard_map/ppermute | solution.py:35
  75.8 5.7 %collective-permute-start.9 = (bf16[2,128,384]{2,1,0:T(8,128)(2,1)S(1)}, bf16[2,128,384]{2,1,0:T(8,128)(2,1)S(1)}, u32[]{:S(2)}, u32[]{:S(2)}) collective-permute-start(bf16[2,128,384]{2,1,0:T(8,128)(2,1)S(1)} %slice.26), channel_id=1, source_target_pairs={{0,2},{2,4},{4,6},{6,7},{7,5},{5,3},{3,1},{1,0},{8,10},{10,12},{12... | collective-permute-start | bytes 589832 | tf_op jit(solution)/shard_map/ppermute | solution.py:39
  78.1 5.7 %collective-permute-start.10 = (bf16[2,128,384]{2,1,0:T(8,128)(2,1)S(1)}, bf16[2,128,384]{2,1,0:T(8,128)(2,1)S(1)}, u32[]{:S(2)}, u32[]{:S(2)}) collective-permute-start(bf16[2,128,384]{2,1,0:T(8,128)(2,1)S(1)} %slice.27), channel_id=1, source_target_pairs={{0,1},{2,0},{4,2},{6,4},{7,6},{5,7},{3,5},{1,3},{8,9},{10,8},{12,1... | collective-permute-start | bytes 589832 | tf_op jit(solution)/shard_map/ppermute | solution.py:40
  83.9 1.7 %copy-start.1 = (bf16[2,2048,384]{2,1,0:T(8,128)(2,1)}, bf16[2,2048,384]{2,1,0:T(8,128)(2,1)S(1)}, u32[]{:S(2)}) copy-start(bf16[2,2048,384]{2,1,0:T(8,128)(2,1)S(1)} %constant_dynamic-update-slice_fusion.refs_1_) | copy-start | bytes 9437188

commit v13 on v6

--- a/solution.py
+++ b/solution.py
@@ -64,35 +64,55 @@
     span_count, row_count, col_count, channels = frames.shape
     activated = jax.nn.silu(rms_scaled(frames, gain_conv)).astype(jnp.bfloat16)
     activated = jnp.pad(activated, ((0, 0), (0, 0), (1, 1), (0, 0)))
-    rimmed = padded_2(activated, (("height", 1),), 1)
+    heights = lax.axis_size("height")
+    last = heights - 1
+    top = lax.ppermute(activated[:, -1:], "height", [(i, i + 1) for i in range(last)])
+    bottom = lax.ppermute(activated[:, :1], "height", [(i + 1, i) for i in range(last)])
     ways = lax.axis_size("tm")
     mine = lax.axis_index("tm")
-    pieces = [rimmed]
-    for shift in range(1, ways):
-        pieces.append(
-            lax.ppermute(rimmed, "tm", [(i, (i + shift) % ways) for i in range(ways)])
-        )
-    pieces.append(jnp.zeros_like(rimmed[:1]))
-    pool = jnp.concatenate(pieces, axis=0)
     blank = ways * span_count
+
+    def pooled(block):
+        pieces = [block]
+        for shift in range(1, ways):
+            pieces.append(
+                lax.ppermute(block, "tm", [(i, (i + shift) % ways) for i in range(ways)])
+            )
+        pieces.append(jnp.zeros_like(block[:1]))
+        return jnp.concatenate(pieces, axis=0)
 
     def slot(index):
         place = ((mine - index // span_count) % ways) * span_count + index % span_count
         return jnp.where(index >= 0, place, blank)
 
     own = jnp.arange(span_count, dtype=earlier.dtype)
-    picks = jnp.stack([slot(earlier[:, 0]), slot(earlier[:, 1]), own], axis=1)
-    window = jnp.take(pool, picks.reshape(-1), axis=0).reshape(
-        (span_count, 3) + rimmed.shape[1:]
+    picks = jnp.stack([slot(earlier[:, 0]), slot(earlier[:, 1]), own], axis=1).reshape(-1)
+
+    def windowed(block):
+        taken = jnp.take(pooled(block), picks, axis=0)
+        return taken.reshape((span_count, 3) + block.shape[1:])
+
+    def conv(window, weight):
+        return lax.conv_general_dilated(
+            window,
+            weight,
+            window_strides=(1, 1, 1),
+            padding="VALID",
+            dimension_numbers=("NDHWC", "DHWIO", "NDHWC"),
+            preferred_element_type=jnp.float32,
+        )[:, 0]
+
+    core = conv(
+        jnp.pad(windowed(activated), ((0, 0), (0, 0), (1, 1), (0, 0), (0, 0))), conv_weight
     )
-    accum = lax.conv_general_dilated(
-        window,
-        conv_weight,
-        window_strides=(1, 1, 1),
-        padding="VALID",
-        dimension_numbers=("NDHWC", "DHWIO", "NDHWC"),
-        preferred_element_type=jnp.float32,
-    )[:, 0]
+    core, top, bottom = lax.optimization_barrier((core, top, bottom))
+    rims = windowed(jnp.concatenate([top, bottom], axis=1))
+    upper = conv(rims[:, :, :1], conv_weight[:, :1])
+    lower = conv(rims[:, :, 1:], conv_weight[:, 2:])
+    edges = jnp.concatenate(
+        [upper, jnp.zeros_like(core[:, : row_count - 2]), lower], axis=1
+    )
+    accum = core + edges
     mixed = (frames.astype(jnp.float32) + accum + conv_bias).astype(jnp.bfloat16)
     normed = rms_scaled(mixed, gain_attn).astype(jnp.bfloat16)
     tokens = normed.reshape(span_count, row_count * col_count, channels)

time: 98 us -> 103 us (1.051)
  matrix products: 20.2 us -> 31.4 us
  waiting for transfers between devices: 32.1 us -> 25.4 us
  local copies, waits for them, and re-layouts: 13.4 us -> 17.8 us
  other arithmetic: 14.6 us -> 11.4 us
    conv_general_dilated x1 -> x3, matrix products: 5.99 us -> 17.2 us  [conv(): lax.conv_general_dilated(window, weight, window_strides=(1, 1, 1), paddin...]
    ppermute x3 -> x4, waiting for transfers between devices: 9.31 us -> 1.55 us  [the longest x2 1.54 us: pooled(): lax.ppermute(block, 'tm', [(i, (i + shift) % ways) for i in range(ways)])]
    select_n x2 -> x3, other arithmetic: 4.36 us -> 0.43 us  [windowed(): taken = jnp.take(pooled(block), picks, axis=0)]
    reshape x1 -> x5, local copies, waits for them, and re-layouts: 0.08 us -> 3.79 us  [the longest x4 3.71 us: windowed(): return taken.reshape((span_count, 3) + block.shape[1:])]
    select_n x1 -> x0, local copies, waits for them, and re-layouts: 1.85 us -> none  [shards(): jnp.take(pool, picks.reshape(-1), axis=0)]
    ppermute x3, waiting for transfers between devices: 19.4 us -> 21.1 us  [ring_gather(): forward = lax.ppermute(forward, axis, ahead)]
    ppermute x3, starting transfers between devices: 8.31 us -> 6.74 us  [ring_gather(): forward = lax.ppermute(forward, axis, ahead)]
    conv_general_dilated x3 -> x8, local copies, waits for them, and re-layouts: 0.88 us -> 2.29 us  [conv(): lax.conv_general_dilated(window, weight, window_strides=(1, 1, 1), paddin...]
  transfers between devices with their start and end apart: 11 -> 12, of which waited for: 7 -> 6; matrix products, arithmetic and copies ran while one was open for 7% -> 24% of each run, Pallas kernels for 0% -> 0%
where the time goes in v13:
time: 103 us
  matrix products  31.4 us (30%)
  waiting for transfers between devices  25.4 us (25%)
  local copies, waits for them, and re-layouts  17.8 us (17%)
  starting transfers between devices  16.6 us (16%)
  other arithmetic  11.4 us (11%)
    ppermute x3, waiting for transfers between devices, ring_gather(): forward = lax.ppermute(forward, axis, ahead)  21.1 us
    conv_general_dilated x3, matrix products, conv(): lax.conv_general_dilated(window, weight, window_strides=(1, 1, 1), paddin...  17.2 us
    unnamed x26, local copies, waits for them, and re-layouts  7.27 us
    dot_general x1, matrix products, shards(): jnp.einsum('fqc,fkc->fqk', queries, keys_all, preferred_element_type=jnp....  7 us
    ppermute x3, starting transfers between devices, ring_gather(): forward = lax.ppermute(forward, axis, ahead)  6.74 us
    dot_general x1, matrix products, shards(): jnp.einsum('fqk,fkc->fqc', weights_exp.astype(jnp.bfloat16), values_all,...  6.39 us
    ppermute x1, starting transfers between devices, shards(): lax.ppermute(activated[:, -1:], 'height', [(i, i + 1) for i in range(last)])  5.11 us
    reshape x4, local copies, waits for them, and re-layouts, windowed(): return taken.reshape((span_count, 3) + block.shape[1:])  3.71 us
  transfers between devices with their start and end apart: 12, of which 6 were waited for; matrix products, arithmetic and copies ran while one was open for 24% of the time, Pallas kernels for 0%

profile of v13, /device:TPU:0, one launch (start us, length us, event | category | flops | bytes accessed | tf_op | source)
XLA Modules:
  0.0 103.0 jit_solution(6111532846490136225)
XLA Ops:
  0.0 1.2 %fusion.41 = f32[2,2,128]{2,1,0:T(2,128)S(1)} fusion(bf16[2,2,128,384]{3,2,1,0:T(8,128)(2,1)} %param.12), kind=kLoop, calls=%fused_computation.46 | loop fusion | flops 589312 | bytes 395264 | tf_op jit(solution)/shard_map/reduce_sum | solution.py:48
  1.2 1.3 %fusion.48 = bf16[2,2,128,384]{3,2,1,0:T(8,128)(2,1)S(1)} fusion(bf16[2,2,128,384]{3,2,1,0:T(8,128)(2,1)} %param.12, f32[384]{0:T(512)} %param.14, f32[2,2,128]{2,1,0:T(2,128)S(1)} %add_rsqrt_fusion.1), kind=kLoop, calls=%fused_computation.53 | loop fusion | flops 1572864 | bytes 790016 | tf_op jit(solution)/shard_map/convert_element_type | solution.py:65
  2.5 0.1 pad.6
  2.6 0.5 collective-permute-start
  3.1 0.9 pad_slice_fusion
  4.0 5.1 %collective-permute-start.1 = (bf16[2,1,130,384]{3,2,1,0:T(8,128)(2,1)}, bf16[2,1,130,384]{3,2,1,0:T(8,128)(2,1)}, u32[]{:S(2)}, u32[]{:S(2)}) collective-permute-start(bf16[2,1,130,384]{3,2,1,0:T(8,128)(2,1)} %get-tuple-element.15), channel_id=1, source_target_pairs={{0,1},{1,2},{2,3},{3,4},{4,5},{5,6},{6,7},{8,9},{9,10},{10,11},{11... | collective-permute-start | bytes 599048 | tf_op jit(solution)/shard_map/ppermute | solution.py:69
  9.1 1.3 %collective-permute-start.2 = (bf16[2,1,130,384]{3,2,1,0:T(8,128)(2,1)}, bf16[2,1,130,384]{3,2,1,0:T(8,128)(2,1)}, u32[]{:S(2)}, u32[]{:S(2)}) collective-permute-start(bf16[2,1,130,384]{3,2,1,0:T(8,128)(2,1)} %get-tuple-element.14), channel_id=1, source_target_pairs={{1,0},{2,1},{3,2},{4,3},{5,4},{6,5},{7,6},{9,8},{10,9},{11,10},{12... | collective-permute-start | bytes 599048 | tf_op jit(solution)/shard_map/ppermute | solution.py:70
  10.4 0.8 compare_select_fusion.6
  11.3 0.1 reshape.41
  11.5 0.2 maximum_maximum_fusion
  11.7 0.8 gather_fusion
  12.6 0.2 broadcast_select_fusion.1
  12.8 0.9 copy.73
  13.7 0.9 pad.7
  14.7 0.1 slice.44
  14.8 1.5 %fusion.13 = bf16[3,2,2,8,19,384]{5,2,4,3,1,0:T(2,128)(2,1)S(1)} fusion(bf16[3,2,2,7,2,384]{5,2,4,3,1,0:T(2,128)(2,1)S(1)} %slice.44, bf16[3,2,2,8,17,384]{5,2,4,3,1,0:T(2,128)(2,1)S(1)} %bitcast.64), kind=kLoop, calls=%fused_computation.19 | loop fusion | flops 4202496 | bytes 2783232 | tf_op jit(solution)/shard_map/conv_general_dilated | solution.py:96
  16.3 11.0 %fusion.20 = f32[1,2,16,17,384]{4,2,3,1,0:T(8,128)S(1)} fusion(bf16[3,3,3,384,384]{4,3,2,1,0:T(8,128)(2,1)} %param.15, bf16[3,2,2,8,19,384]{5,2,4,3,1,0:T(2,128)(2,1)S(1)} %fusion.13, pred[16,17]{0,1:T(8,128)(4,1)S(1)} %copy-done.4), kind=kOutput, calls=%fused_computation.26 | convolution fusion | flops 2887987200 | bytes 10199312 | tf_op jit(solution)/shard_map/conv_general_dilated | solution.py:96
  27.3 0.4 copy.38
  27.8 0.3 slice.45
  28.1 1.0 constant_dynamic-update-slice_fusion.1
  29.1 1.0 constant_dynamic-update-slice_fusion
  30.1 0.3 collective-permute-start.3
  30.3 1.5 %collective-permute-done.3 = bf16[2,2,130,384]{3,2,1,0:T(8,128)(2,1)S(1)} collective-permute-done((bf16[2,2,130,384]{3,2,1,0:T(8,128)(2,1)S(1)}, bf16[2,2,130,384]{3,2,1,0:T(8,128)(2,1)S(1)}, u32[]{:S(2)}, u32[]{:S(2)}) %collective-permute-start.3) | collective-permute-done | bytes 399392 | tf_op jit(solution)/shard_map/ppermute | solution.py:79
  31.9 0.2 maximum_maximum_fusion.1
  32.1 0.8 gather_fusion.1
  32.9 0.2 broadcast_select_fusion
  33.1 0.9 copy.72
  34.1 0.9 pad.9
  35.0 0.1 slice.46
  35.1 1.3 %fusion.14 = bf16[3,2,2,8,19,384]{5,2,4,3,1,0:T(2,128)(2,1)S(1)} fusion(bf16[3,2,2,7,2,384]{5,2,4,3,1,0:T(2,128)(2,1)S(1)} %slice.46, bf16[3,2,2,8,17,384]{5,2,4,3,1,0:T(2,128)(2,1)S(1)} %bitcast.62), kind=kLoop, calls=%fused_computation.20 | loop fusion | flops 4202496 | bytes 2783232 | tf_op jit(solution)/shard_map/conv_general_dilated | solution.py:96
  36.4 3.1 %fusion.25 = f32[1,1,16,17,384]{4,2,3,1,0:T(8,128)S(1)} fusion(bf16[3,3,3,384,384]{4,3,2,1,0:T(8,128)(2,1)} %param.15, bf16[3,2,2,8,19,384]{5,2,4,3,1,0:T(2,128)(2,1)S(1)} %fusion.14, pred[16,17]{0,1:T(8,128)(4,1)S(1)} %copy-done.4), kind=kOutput, calls=%fused_computation.40 | convolution fusion | flops 722049024 | bytes 4473104 | tf_op jit(solution)/shard_map/conv_general_dilated | solution.py:96
  39.5 3.1 %fusion.30 = f32[1,1,16,17,384]{4,2,3,1,0:T(8,128)S(1)} fusion(bf16[3,3,3,384,384]{4,3,2,1,0:T(8,128)(2,1)} %param.15, bf16[3,2,2,8,19,384]{5,2,4,3,1,0:T(2,128)(2,1)S(1)} %fusion.14, pred[16,17]{0,1:T(8,128)(4,1)S(1)} %copy-done.4), kind=kOutput, calls=%fused_computation.41 | convolution fusion | flops 722049024 | bytes 4473104 | tf_op jit(solution)/shard_map/conv_general_dilated | solution.py:96
  42.6 0.4 copy.42
  43.1 0.3 slice.47
  43.4 0.4 copy.44
  43.8 0.3 slice.48
  44.2 0.3 fusion.51
  44.5 0.2 fusion.53
  44.7 3.0 %collective-permute-start.4 = (bf16[2,256,384]{2,1,0:T(8,128)(2,1)S(1)}, bf16[2,256,384]{2,1,0:T(8,128)(2,1)S(1)}, u32[]{:S(2)}, u32[]{:S(2)}) collective-permute-start(bf16[2,256,384]{2,1,0:T(8,128)(2,1)S(1)} %bitcast.69), channel_id=1, source_target_pairs={{0,2},{2,4},{4,6},{6,7},{7,5},{5,3},{3,1},{1,0},{8,10},{10,12},{12... | collective-permute-start | bytes 1179656 | tf_op jit(solution)/shard_map/ppermute | solution.py:33
  47.6 9.1 %collective-permute-done.4 = bf16[2,256,384]{2,1,0:T(8,128)(2,1)S(1)} collective-permute-done((bf16[2,256,384]{2,1,0:T(8,128)(2,1)S(1)}, bf16[2,256,384]{2,1,0:T(8,128)(2,1)S(1)}, u32[]{:S(2)}, u32[]{:S(2)}) %collective-permute-start.4) | collective-permute-done | bytes 393248 | tf_op jit(solution)/shard_map/ppermute | solution.py:33
  56.8 2.0 %collective-permute-start.6 = (bf16[2,256,384]{2,1,0:T(8,128)(2,1)S(1)}, bf16[2,256,384]{2,1,0:T(8,128)(2,1)S(1)}, u32[]{:S(2)}, u32[]{:S(2)}) collective-permute-start(bf16[2,256,384]{2,1,0:T(8,128)(2,1)S(1)} %collective-permute-done.4), channel_id=1, source_target_pairs={{0,2},{2,4},{4,6},{6,7},{7,5},{5,3},{3,1},{1,0},{8,10},{10,12},{12... | collective-permute-start | bytes 1179656 | tf_op jit(solution)/shard_map/ppermute | solution.py:33
  58.8 0.8 constant_dynamic-update-slice_fusion.10
  59.6 0.4 convolution_convert_fusion.2
  60.0 7.4 %collective-permute-done.6 = bf16[2,256,384]{2,1,0:T(8,128)(2,1)S(1)} collective-permute-done((bf16[2,256,384]{2,1,0:T(8,128)(2,1)S(1)}, bf16[2,256,384]{2,1,0:T(8,128)(2,1)S(1)}, u32[]{:S(2)}, u32[]{:S(2)}) %collective-permute-start.6) | collective-permute-done | bytes 393248 | tf_op jit(solution)/shard_map/ppermute | solution.py:33
  67.4 1.7 %collective-permute-start.8 = (bf16[2,256,384]{2,1,0:T(8,128)(2,1)S(1)}, bf16[2,256,384]{2,1,0:T(8,128)(2,1)S(1)}, u32[]{:S(2)}, u32[]{:S(2)}) collective-permute-start(bf16[2,256,384]{2,1,0:T(8,128)(2,1)S(1)} %collective-permute-done.6), channel_id=1, source_target_pairs={{0,2},{2,4},{4,6},{6,7},{7,5},{5,3},{3,1},{1,0},{8,10},{10,12},{12... | collective-permute-start | bytes 1179656 | tf_op jit(solution)/shard_map/ppermute | solution.py:33
  69.1 0.3 collective-permute-start.9
  69.4 0.8 constant_dynamic-update-slice_fusion.9
  70.2 0.8 constant_dynamic-update-slice_fusion.8
  71.0 0.8 constant_dynamic-update-slice_fusion.7
  71.8 0.8 constant_dynamic-update-slice_fusion.6
  72.6 4.6 %collective-permute-done.8 = bf16[2,256,384]{2,1,0:T(8,128)(2,1)S(1)} collective-permute-done((bf16[2,256,384]{2,1,0:T(8,128)(2,1)S(1)}, bf16[2,256,384]{2,1,0:T(8,128)(2,1)S(1)}, u32[]{:S(2)}, u32[]{:S(2)}) %collective-permute-start.8) | collective-permute-done | bytes 393248 | tf_op jit(solution)/shard_map/ppermute | solution.py:33
  77.2 1.4 %collective-permute-start.10 = (bf16[2,128,384]{2,1,0:T(8,128)(2,1)S(1)}, bf16[2,128,384]{2,1,0:T(8,128)(2,1)S(1)}, u32[]{:S(2)}, u32[]{:S(2)}) collective-permute-start(bf16[2,128,384]{2,1,0:T(8,128)(2,1)S(1)} %slice.49), channel_id=1, source_target_pairs={{0,2},{2,4},{4,6},{6,7},{7,5},{5,3},{3,1},{1,0},{8,10},{10,12},{12... | collective-permute-start | bytes 589832 | tf_op jit(solution)/shard_map/ppermute | solution.py:38
  78.6 0.9 collective-permute-start.11
  79.6 0.8 constant_dynamic-update-slice_fusion.5
  80.3 0.8 constant_dynamic-update-slice_fusion.4
  81.1 1.8 %collective-permute-done.10 = bf16[2,128,384]{2,1,0:T(8,128)(2,1)S(1)} collective-permute-done((bf16[2,128,384]{2,1,0:T(8,128)(2,1)S(1)}, bf16[2,128,384]{2,1,0:T(8,128)(2,1)S(1)}, u32[]{:S(2)}, u32[]{:S(2)}) %collective-permute-start.10) | collective-permute-done | bytes 196640 | tf_op jit(solution)/shard_map/ppermute | solution.py:38
  82.9 0.7 constant_dynamic-update-slice_fusion.3
  83.6 1.0 collective-permute-done.11
  84.6 0.7 constant_dynamic-update-slice_fusion.2
  85.3 7.0 %multiply_reduce_fusion = (f32[2,256]{1,0:T(2,128)S(1)}, f32[2,256,2048]{2,1,0:T(8,128)}) fusion(bf16[2,256,384]{2,1,0:T(8,128)(2,1)S(1)} %convolution_convert_fusion.2, bf16[2,2048,384]{2,1,0:T(8,128)(2,1)} %constant_dynamic-update-slice_fusion.2, bf16[384,384]{1,0:T(8,128)(2,1)S(1)} %copy-done), kind=kOutput, calls=%fused_computation.3 | convolution fusion | flops 2016935424 | bytes 8030208 | tf_op jit(solution)/shard_map/fqc,fkc->fqk/dot_general | solution.py:131
  92.3 3.0 %fusion = f32[2,256]{1,0:T(2,128)S(1)} fusion(f32[2,256,2048]{2,1,0:T(8,128)} %get-tuple-element.19, f32[2,256]{1,0:T(2,128)S(1)} %get-tuple-element.18), kind=kLoop, calls=%fused_computation.4 | loop fusion | flops 3145216 | bytes 4198400 | tf_op jit(solution)/shard_map/reduce_sum | solution.py:136
  95.4 6.4 %fusion.38 = bf16[2,256,384]{2,1,0:T(8,128)(2,1)S(1)} fusion(bf16[2,2048,384]{2,1,0:T(8,128)(2,1)} %constant_dynamic-update-slice_fusion.2, f32[2,256,2048]{2,1,0:T(8,128)} %get-tuple-element.19, f32[2,256]{1,0:T(2,128)S(1)} %get-tuple-element.18, f32[2,256]{1,0:T(2,128)S(1)} %fusion, bf16[384,384]{1,0:T(8,128)(2,1)S(1)} %copy-done.7), kind=kOutput, calls=%fused_computation.43 | convolution fusion | flops 2018377728 | bytes 8032256 | tf_op jit(solution)/shard_map/fqk,fkc->fqc/dot_general | solution.py:137
  101.8 0.4 fusion.55
  102.2 0.8 fusion.54
  (36 shorter events, 0.4 us)
Async XLA Ops:
  0.0 85.3 %copy-start = (bf16[384,384]{1,0:T(8,128)(2,1)S(1)}, bf16[384,384]{1,0:T(8,128)(2,1)}, u32[]{:S(2)}) copy-start(bf16[384,384]{1,0:T(8,128)(2,1)} %param.19) | copy-start | bytes 884740
  2.6 8.9 %collective-permute-start = (bf16[2,2,130,384]{3,2,1,0:T(8,128)(2,1)S(1)}, bf16[2,2,130,384]{3,2,1,0:T(8,128)(2,1)S(1)}, u32[]{:S(2)}, u32[]{:S(2)}) collective-permute-start(bf16[2,2,130,384]{3,2,1,0:T(8,128)(2,1)S(1)} %pad.6), channel_id=1, source_target_pairs={{0,8},{8,0},{1,9},{9,1},{2,10},{10,2},{3,11},{11,3},{4,12},{12,4},... | collective-permute-start | bytes 1198088 | tf_op jit(solution)/shard_map/ppermute | solution.py:79
  4.0 24.1 %collective-permute-start.1 = (bf16[2,1,130,384]{3,2,1,0:T(8,128)(2,1)}, bf16[2,1,130,384]{3,2,1,0:T(8,128)(2,1)}, u32[]{:S(2)}, u32[]{:S(2)}) collective-permute-start(bf16[2,1,130,384]{3,2,1,0:T(8,128)(2,1)} %get-tuple-element.15), channel_id=1, source_target_pairs={{0,1},{1,2},{2,3},{3,4},{4,5},{5,6},{6,7},{8,9},{9,10},{10,11},{11... | collective-permute-start | bytes 599048 | tf_op jit(solution)/shard_map/ppermute | solution.py:69
  9.1 19.0 %collective-permute-start.2 = (bf16[2,1,130,384]{3,2,1,0:T(8,128)(2,1)}, bf16[2,1,130,384]{3,2,1,0:T(8,128)(2,1)}, u32[]{:S(2)}, u32[]{:S(2)}) collective-permute-start(bf16[2,1,130,384]{3,2,1,0:T(8,128)(2,1)} %get-tuple-element.14), channel_id=1, source_target_pairs={{1,0},{2,1},{3,2},{4,3},{5,4},{6,5},{7,6},{9,8},{10,9},{11,10},{12... | collective-permute-start | bytes 599048 | tf_op jit(solution)/shard_map/ppermute | solution.py:70
  13.7 2.6 %copy-start.4 = (pred[16,17]{0,1:T(8,128)(4,1)S(1)}, pred[16,17]{0,1:T(8,128)(4,1)}, u32[]{:S(2)}) copy-start(pred[16,17]{0,1:T(8,128)(4,1)} %constant.103) | copy-start | bytes 820
  30.1 1.8 %collective-permute-start.3 = (bf16[2,2,130,384]{3,2,1,0:T(8,128)(2,1)S(1)}, bf16[2,2,130,384]{3,2,1,0:T(8,128)(2,1)S(1)}, u32[]{:S(2)}, u32[]{:S(2)}) collective-permute-start(bf16[2,2,130,384]{3,2,1,0:T(8,128)(2,1)S(1)} %constant_dynamic-update-slice_fusion), channel_id=1, source_target_pairs={{0,8},{8,0},{1,9},{9,1},{2,10},{10,2},{3,11},{11,3},{4,12},{12,4},... | collective-permute-start | bytes 1198088 | tf_op jit(solution)/shard_map/ppermute | solution.py:79
  42.6 1.5 %copy-start.1 = (bf16[2,2,128,384]{3,2,1,0:T(8,128)(2,1)S(1)}, bf16[2,2,128,384]{3,2,1,0:T(8,128)(2,1)}, u32[]{:S(2)}) copy-start(bf16[2,2,128,384]{3,2,1,0:T(8,128)(2,1)} %param.12) | copy-start | bytes 1179652
  42.6 1.5 %copy-start.5 = (f32[384]{0:T(512)S(1)}, f32[384]{0:T(512)}, u32[]{:S(2)}) copy-start(f32[384]{0:T(512)} %param.16) | copy-start | bytes 4612
  43.1 1.4 %copy-start.6 = (f32[384]{0:T(512)S(1)}, f32[384]{0:T(512)}, u32[]{:S(2)}) copy-start(f32[384]{0:T(512)} %param.17) | copy-start | bytes 4612
  43.8 15.8 %copy-start.2 = (bf16[384,384]{1,0:T(8,128)(2,1)S(1)}, bf16[384,384]{1,0:T(8,128)(2,1)}, u32[]{:S(2)}) copy-start(bf16[384,384]{1,0:T(8,128)(2,1)} %param.18) | copy-start | bytes 884740
  44.7 12.1 %collective-permute-start.4 = (bf16[2,256,384]{2,1,0:T(8,128)(2,1)S(1)}, bf16[2,256,384]{2,1,0:T(8,128)(2,1)S(1)}, u32[]{:S(2)}, u32[]{:S(2)}) collective-permute-start(bf16[2,256,384]{2,1,0:T(8,128)(2,1)S(1)} %bitcast.69), channel_id=1, source_target_pairs={{0,2},{2,4},{4,6},{6,7},{7,5},{5,3},{3,1},{1,0},{8,10},{10,12},{12... | collective-permute-start | bytes 1179656 | tf_op jit(solution)/shard_map/ppermute | solution.py:33
  47.6 11.2 %collective-permute-start.5 = (bf16[2,256,384]{2,1,0:T(8,128)(2,1)S(1)}, bf16[2,256,384]{2,1,0:T(8,128)(2,1)S(1)}, u32[]{:S(2)}, u32[]{:S(2)}) collective-permute-start(bf16[2,256,384]{2,1,0:T(8,128)(2,1)S(1)} %bitcast.70), channel_id=1, source_target_pairs={{0,1},{2,0},{4,2},{6,4},{7,6},{5,7},{3,5},{1,3},{8,9},{10,8},{12,1... | collective-permute-start | bytes 1179656 | tf_op jit(solution)/shard_map/ppermute | solution.py:34
  56.8 10.6 %collective-permute-start.6 = (bf16[2,256,384]{2,1,0:T(8,128)(2,1)S(1)}, bf16[2,256,384]{2,1,0:T(8,128)(2,1)S(1)}, u32[]{:S(2)}, u32[]{:S(2)}) collective-permute-start(bf16[2,256,384]{2,1,0:T(8,128)(2,1)S(1)} %collective-permute-done.4), channel_id=1, source_target_pairs={{0,2},{2,4},{4,6},{6,7},{7,5},{5,3},{3,1},{1,0},{8,10},{10,12},{12... | collective-permute-start | bytes 1179656 | tf_op jit(solution)/shard_map/ppermute | solution.py:33
  58.8 10.3 %collective-permute-start.7 = (bf16[2,256,384]{2,1,0:T(8,128)(2,1)S(1)}, bf16[2,256,384]{2,1,0:T(8,128)(2,1)S(1)}, u32[]{:S(2)}, u32[]{:S(2)}) collective-permute-start(bf16[2,256,384]{2,1,0:T(8,128)(2,1)S(1)} %collective-permute-done.5), channel_id=1, source_target_pairs={{0,1},{2,0},{4,2},{6,4},{7,6},{5,7},{3,5},{1,3},{8,9},{10,8},{12,1... | collective-permute-start | bytes 1179656 | tf_op jit(solution)/shard_map/ppermute | solution.py:34
  67.4 9.7 %collective-permute-start.8 = (bf16[2,256,384]{2,1,0:T(8,128)(2,1)S(1)}, bf16[2,256,384]{2,1,0:T(8,128)(2,1)S(1)}, u32[]{:S(2)}, u32[]{:S(2)}) collective-permute-start(bf16[2,256,384]{2,1,0:T(8,128)(2,1)S(1)} %collective-permute-done.6), channel_id=1, source_target_pairs={{0,2},{2,4},{4,6},{6,7},{7,5},{5,3},{3,1},{1,0},{8,10},{10,12},{12... | collective-permute-start | bytes 1179656 | tf_op jit(solution)/shard_map/ppermute | solution.py:33
  69.1 9.5 %collective-permute-start.9 = (bf16[2,256,384]{2,1,0:T(8,128)(2,1)S(1)}, bf16[2,256,384]{2,1,0:T(8,128)(2,1)S(1)}, u32[]{:S(2)}, u32[]{:S(2)}) collective-permute-start(bf16[2,256,384]{2,1,0:T(8,128)(2,1)S(1)} %collective-permute-done.7), channel_id=1, source_target_pairs={{0,1},{2,0},{4,2},{6,4},{7,6},{5,7},{3,5},{1,3},{8,9},{10,8},{12,1... | collective-permute-start | bytes 1179656 | tf_op jit(solution)/shard_map/ppermute | solution.py:34
  77.2 5.7 %collective-permute-start.10 = (bf16[2,128,384]{2,1,0:T(8,128)(2,1)S(1)}, bf16[2,128,384]{2,1,0:T(8,128)(2,1)S(1)}, u32[]{:S(2)}, u32[]{:S(2)}) collective-permute-start(bf16[2,128,384]{2,1,0:T(8,128)(2,1)S(1)} %slice.49), channel_id=1, source_target_pairs={{0,2},{2,4},{4,6},{6,7},{7,5},{5,3},{3,1},{1,0},{8,10},{10,12},{12... | collective-permute-start | bytes 589832 | tf_op jit(solution)/shard_map/ppermute | solution.py:38
  78.6 5.9 %collective-permute-start.11 = (bf16[2,128,384]{2,1,0:T(8,128)(2,1)S(1)}, bf16[2,128,384]{2,1,0:T(8,128)(2,1)S(1)}, u32[]{:S(2)}, u32[]{:S(2)}) collective-permute-start(bf16[2,128,384]{2,1,0:T(8,128)(2,1)S(1)} %slice.50), channel_id=1, source_target_pairs={{0,1},{2,0},{4,2},{6,4},{7,6},{5,7},{3,5},{1,3},{8,9},{10,8},{12,1... | collective-permute-start | bytes 589832 | tf_op jit(solution)/shard_map/ppermute | solution.py:39
  92.3 3.1 %copy-start.7 = (bf16[384,384]{1,0:T(8,128)(2,1)S(1)}, bf16[384,384]{1,0:T(8,128)(2,1)}, u32[]{:S(2)}) copy-start(bf16[384,384]{1,0:T(8,128)(2,1)} %param.20) | copy-start | bytes 884740
  95.3 6.4 %copy-start.3 = (bf16[384,384]{1,0:T(8,128)(2,1)S(1)}, bf16[384,384]{1,0:T(8,128)(2,1)}, u32[]{:S(2)}) copy-start(bf16[384,384]{1,0:T(8,128)(2,1)} %param.21) | copy-start | bytes 884740

commit v14 on v6

--- a/solution.py
+++ b/solution.py
@@ -62,9 +62,12 @@
     out_weight,
 ):
     span_count, row_count, col_count, channels = frames.shape
+    rims = padded_2(frames, (("height", 1),), 1)
+    rims = jnp.concatenate([rims[:, :1], rims[:, -1:]], axis=1)
     activated = jax.nn.silu(rms_scaled(frames, gain_conv)).astype(jnp.bfloat16)
-    activated = jnp.pad(activated, ((0, 0), (0, 0), (1, 1), (0, 0)))
-    rimmed = padded_2(activated, (("height", 1),), 1)
+    rims = jax.nn.silu(rms_scaled(rims, gain_conv)).astype(jnp.bfloat16)
+    rimmed = jnp.concatenate([rims[:, :1], activated, rims[:, 1:]], axis=1)
+    rimmed = jnp.pad(rimmed, ((0, 0), (0, 0), (1, 1), (0, 0)))
     ways = lax.axis_size("tm")
     mine = lax.axis_index("tm")
     pieces = [rimmed]

time: 98 us -> 97.8 us (level)
  waiting for transfers between devices: 32.1 us -> 30.3 us
  local copies, waits for them, and re-layouts: 13.4 us -> 14.4 us
    ppermute x1, waiting for transfers between devices: 7.49 us -> 1.72 us  [padded_2(): lax.ppermute(tail, axis, [(i, (i + 1) % count) for i in range(ends)])]
    ppermute x1, waiting for transfers between devices: 0.01 us -> 4.07 us  [padded_2(): lax.ppermute(head, axis, [((i + 1) % count, i) for i in range(ends)])]
    slice x1, local copies, waits for them, and re-layouts: 0.1 us -> 1.11 us  [padded_2(): lax.slice_in_dim(cells, cells.shape[dim] - width, cells.shape[dim], axis=...]
  transfers between devices with their start and end apart: 11 -> 11, of which waited for: 7 -> 8; matrix products, arithmetic and copies ran while one was open for 7% -> 9% of each run, Pallas kernels for 0% -> 0%
where the time goes in v14:
time: 97.8 us; the launch traced here: 97.5 us
  waiting for transfers between devices  30.3 us (31%)
  matrix products  20.2 us (21%)
  starting transfers between devices  17.3 us (18%)
  other arithmetic  15 us (15%)
  local copies, waits for them, and re-layouts  14.4 us (15%)
    ppermute x3, waiting for transfers between devices, ring_gather(): forward = lax.ppermute(forward, axis, ahead)  19.3 us
    ppermute x3, starting transfers between devices, ring_gather(): forward = lax.ppermute(forward, axis, ahead)  8.43 us
    dot_general x1, matrix products, shards(): jnp.einsum('fqc,fkc->fqk', queries, keys_all, preferred_element_type=jnp....  7.02 us
    unnamed x30, local copies, waits for them, and re-layouts  6.61 us
    dot_general x1, matrix products, shards(): jnp.einsum('fqk,fkc->fqc', weights_exp.astype(jnp.bfloat16), values_all,...  6.4 us
    conv_general_dilated x1, matrix products, shards(): lax.conv_general_dilated(window, conv_weight, window_strides=(1, 1, 1), p...  5.99 us
    ppermute x1, starting transfers between devices, padded_2(): lax.ppermute(tail, axis, [(i, (i + 1) % count) for i in range(ends)])  4.88 us
    select_n x2, other arithmetic, shards(): jnp.take(pool, picks.reshape(-1), axis=0)  4.36 us
  transfers between devices with their start and end apart: 11, of which 8 were waited for; matrix products, arithmetic and copies ran while one was open for 9% of the time, Pallas kernels for 0%

profile of v14, /device:TPU:0, one launch (start us, length us, event | category | flops | bytes accessed | tf_op | source)
XLA Modules:
  0.0 97.5 jit_solution(10874695117014105938)
XLA Ops:
  0.0 1.1 %fusion.66 = (bf16[2,1,128,384]{3,2,1,0:T(8,128)(2,1)S(1)}, bf16[2,1,128,384]{3,2,1,0:T(8,128)(2,1)S(1)}) fusion(bf16[2,2,128,384]{3,2,1,0:T(8,128)(2,1)} %param.10), kind=kLoop, calls=%fused_computation.112 | loop fusion | bytes 786432 | tf_op jit(solution)/shard_map/slice | solution.py:12
  1.1 4.9 %collective-permute-start = (bf16[2,1,128,384]{3,2,1,0:T(8,128)(2,1)S(1)}, bf16[2,1,128,384]{3,2,1,0:T(8,128)(2,1)S(1)}, u32[]{:S(2)}, u32[]{:S(2)}) collective-permute-start(bf16[2,1,128,384]{3,2,1,0:T(8,128)(2,1)S(1)} %get-tuple-element.11), channel_id=1, source_target_pairs={{0,1},{1,2},{2,3},{3,4},{4,5},{5,6},{6,7},{8,9},{9,10},{10,11},{11... | collective-permute-start | bytes 589832 | tf_op jit(solution)/shard_map/ppermute | solution.py:15
  6.0 0.0 copy-start.4
  6.0 1.3 %collective-permute-start.1 = (bf16[2,1,128,384]{3,2,1,0:T(8,128)(2,1)S(1)}, bf16[2,1,128,384]{3,2,1,0:T(8,128)(2,1)S(1)}, u32[]{:S(2)}, u32[]{:S(2)}) collective-permute-start(bf16[2,1,128,384]{3,2,1,0:T(8,128)(2,1)S(1)} %get-tuple-element.12), channel_id=1, source_target_pairs={{1,0},{2,1},{3,2},{4,3},{5,4},{6,5},{7,6},{9,8},{10,9},{11,10},{12... | collective-permute-start | bytes 589832 | tf_op jit(solution)/shard_map/ppermute | solution.py:17
  7.3 1.1 %fusion.35 = f32[2,2,128]{2,1,0:T(2,128)S(1)} fusion(bf16[2,2,128,384]{3,2,1,0:T(8,128)(2,1)} %param.10), kind=kLoop, calls=%fused_computation.47 | loop fusion | flops 589312 | bytes 395264 | tf_op jit(solution)/shard_map/reduce_sum | solution.py:48
  8.5 1.7 %collective-permute-done = bf16[2,1,128,384]{3,2,1,0:T(8,128)(2,1)S(1)} collective-permute-done((bf16[2,1,128,384]{3,2,1,0:T(8,128)(2,1)S(1)}, bf16[2,1,128,384]{3,2,1,0:T(8,128)(2,1)S(1)}, u32[]{:S(2)}, u32[]{:S(2)}) %collective-permute-start) | collective-permute-done | bytes 196640 | tf_op jit(solution)/shard_map/ppermute | solution.py:15
  10.2 4.1 %collective-permute-done.1 = bf16[2,1,128,384]{3,2,1,0:T(8,128)(2,1)S(1)} collective-permute-done((bf16[2,1,128,384]{3,2,1,0:T(8,128)(2,1)S(1)}, bf16[2,1,128,384]{3,2,1,0:T(8,128)(2,1)S(1)}, u32[]{:S(2)}, u32[]{:S(2)}) %collective-permute-start.1) | collective-permute-done | bytes 196640 | tf_op jit(solution)/shard_map/ppermute | solution.py:17
  14.3 0.2 fusion.27
  14.4 1.5 %fusion.42 = (bf16[2,2,128,384]{3,2,1,0:T(8,128)(2,1)S(1)}, bf16[2,2,128,384]{3,2,1,0:T(8,128)(2,1)S(1)}) fusion(bf16[2,2,128,384]{3,2,1,0:T(8,128)(2,1)} %param.10, f32[2,2,128]{2,1,0:T(2,128)S(1)} %add_rsqrt_fusion.1, f32[384]{0:T(512)} %param.12, f32[2,2,128]{2,1,0:T(2,128)S(1)} %add_rsqrt_fusion.2, ...), kind=kLoop, calls=%fused_computation.54 | loop fusion | flops 3342336 | bytes 1578496 | tf_op jit(solution)/shard_map/convert_element_type | solution.py:67
  16.0 0.2 fusion.26
  16.3 0.3 copy.36
  16.6 0.1 collective-permute-start.2
  16.7 0.1 compare_select_fusion.8
  16.8 0.1 compare_and_fusion
  16.8 0.1 reshape.75
  16.9 0.1 copy.35
  17.0 0.1 pad.11.clone
  17.1 1.8 %collective-permute-done.2 = bf16[2,4,130,384]{3,1,2,0:T(4,128)(2,1)S(1)} collective-permute-done((bf16[2,4,130,384]{3,1,2,0:T(4,128)(2,1)S(1)}, bf16[2,4,130,384]{3,1,2,0:T(4,128)(2,1)S(1)}, u32[]{:S(2)}, u32[]{:S(2)}) %collective-permute-start.2) | collective-permute-done | bytes 798752 | tf_op jit(solution)/shard_map/ppermute | solution.py:76
  18.9 0.1 copy.37
  19.1 0.3 maximum_maximum_fusion
  19.4 2.5 %gather_fusion = bf16[6,4,130,384]{3,2,1,0:T(8,128)(2,1)} fusion(bf16[5,4,130,384]{3,2,1,0:T(8,128)(2,1)S(1)} %maximum_maximum_fusion, s32[1024]{0:T(1024)S(1)} %pad_clamp_fusion), kind=kCustom, calls=%fused_computation | custom fusion | bytes 4792344 | tf_op jit(solution)/shard_map/jit(_take)/gather | solution.py:88
  21.9 4.4 %fusion.6 = bf16[3,4,2,130,384]{4,2,3,1,0:T(2,128)(2,1)S(1)} fusion(pred[2,3]{0,1:T(4,128)(4,1)S(1)} %copy.35, bf16[2,3,4,130,384]{4,3,2,1,0:T(8,128)(2,1)} %bitcast.46), kind=kLoop, calls=%fused_computation.15 | loop fusion | flops 1198080 | bytes 4792326 | tf_op jit(solution)/shard_map/jit(_take)/select_n | solution.py:88
  26.3 0.0 slice-start.1
  26.3 1.9 %pad.5 = bf16[3,4,2,136,384]{4,2,3,1,0:T(2,128)(2,1)S(1)} pad(bf16[3,4,2,130,384]{4,2,3,1,0:T(2,128)(2,1)S(1)} %fusion.6, bf16[]{:T(256)} %constant.89.clone.1), padding=0_0x0_0x0_0x0_6x0_0 | pad | bytes 4902914 | tf_op jit(solution)/shard_map/jit(_take)/select_n | solution.py:88
  28.1 0.0 copy-start.8
  28.1 0.2 slice.38
  28.3 2.8 %fusion.2 = bf16[3,4,2,8,19,384]{5,2,4,3,1,0:T(2,128)(2,1)S(1)} fusion(bf16[3,4,2,7,2,384]{5,2,4,3,1,0:T(2,128)(2,1)S(1)} %slice.38, bf16[3,4,2,8,17,384]{5,2,4,3,1,0:T(2,128)(2,1)S(1)} %bitcast.45), kind=kLoop, calls=%fused_computation.9 | loop fusion | flops 8404992 | bytes 5566464 | tf_op jit(solution)/shard_map/conv_general_dilated | solution.py:91
  31.2 6.0 %fusion.13 = f32[1,2,16,17,384]{4,2,3,1,0:T(8,128)S(1)} fusion(bf16[3,3,3,384,384]{4,3,2,1,0:T(8,128)(2,1)S(1)} %bitcast.54, bf16[3,4,2,8,19,384]{5,2,4,3,1,0:T(2,128)(2,1)S(1)} %fusion.2, pred[16,17]{0,1:T(8,128)(4,1)S(1)} %copy-done.8), kind=kOutput, calls=%fused_computation.22 | convolution fusion | flops 4331876352 | bytes 11600144 | tf_op jit(solution)/shard_map/conv_general_dilated | solution.py:91
  37.2 0.0 copy-start.1
  37.2 0.0 copy-start.5
  37.2 0.0 copy-start.6
  37.2 0.0 copy-start.2
  37.2 0.4 copy.40
  37.7 0.3 slice.39
  37.9 0.2 copy-done.1
  38.2 0.2 fusion.45
  38.4 0.2 fusion.47
  38.6 3.6 %collective-permute-start.3 = (bf16[2,256,384]{2,1,0:T(8,128)(2,1)S(1)}, bf16[2,256,384]{2,1,0:T(8,128)(2,1)S(1)}, u32[]{:S(2)}, u32[]{:S(2)}) collective-permute-start(bf16[2,256,384]{2,1,0:T(8,128)(2,1)S(1)} %bitcast.47), channel_id=1, source_target_pairs={{0,2},{2,4},{4,6},{6,7},{7,5},{5,3},{3,1},{1,0},{8,10},{10,12},{12... | collective-permute-start | bytes 1179656 | tf_op jit(solution)/shard_map/ppermute | solution.py:33
  42.2 8.7 %collective-permute-done.3 = bf16[2,256,384]{2,1,0:T(8,128)(2,1)S(1)} collective-permute-done((bf16[2,256,384]{2,1,0:T(8,128)(2,1)S(1)}, bf16[2,256,384]{2,1,0:T(8,128)(2,1)S(1)}, u32[]{:S(2)}, u32[]{:S(2)}) %collective-permute-start.3) | collective-permute-done | bytes 393248 | tf_op jit(solution)/shard_map/ppermute | solution.py:33
  50.8 2.5 %collective-permute-start.5 = (bf16[2,256,384]{2,1,0:T(8,128)(2,1)S(1)}, bf16[2,256,384]{2,1,0:T(8,128)(2,1)S(1)}, u32[]{:S(2)}, u32[]{:S(2)}) collective-permute-start(bf16[2,256,384]{2,1,0:T(8,128)(2,1)S(1)} %collective-permute-done.3), channel_id=1, source_target_pairs={{0,2},{2,4},{4,6},{6,7},{7,5},{5,3},{3,1},{1,0},{8,10},{10,12},{12... | collective-permute-start | bytes 1179656 | tf_op jit(solution)/shard_map/ppermute | solution.py:33
  53.3 0.8 constant_dynamic-update-slice_fusion.8
  54.1 0.4 convolution_convert_fusion.2
  54.5 6.7 %collective-permute-done.5 = bf16[2,256,384]{2,1,0:T(8,128)(2,1)S(1)} collective-permute-done((bf16[2,256,384]{2,1,0:T(8,128)(2,1)S(1)}, bf16[2,256,384]{2,1,0:T(8,128)(2,1)S(1)}, u32[]{:S(2)}, u32[]{:S(2)}) %collective-permute-start.5) | collective-permute-done | bytes 393248 | tf_op jit(solution)/shard_map/ppermute | solution.py:33
  61.3 2.4 %collective-permute-start.7 = (bf16[2,256,384]{2,1,0:T(8,128)(2,1)S(1)}, bf16[2,256,384]{2,1,0:T(8,128)(2,1)S(1)}, u32[]{:S(2)}, u32[]{:S(2)}) collective-permute-start(bf16[2,256,384]{2,1,0:T(8,128)(2,1)S(1)} %collective-permute-done.5), channel_id=1, source_target_pairs={{0,2},{2,4},{4,6},{6,7},{7,5},{5,3},{3,1},{1,0},{8,10},{10,12},{12... | collective-permute-start | bytes 1179656 | tf_op jit(solution)/shard_map/ppermute | solution.py:33
  63.6 0.0 collective-permute-start.8
  63.6 0.8 constant_dynamic-update-slice_fusion.7
  64.5 0.8 constant_dynamic-update-slice_fusion.6
  65.3 0.8 constant_dynamic-update-slice_fusion.5
  66.1 0.8 constant_dynamic-update-slice_fusion.4
  66.9 3.9 %collective-permute-done.7 = bf16[2,256,384]{2,1,0:T(8,128)(2,1)S(1)} collective-permute-done((bf16[2,256,384]{2,1,0:T(8,128)(2,1)S(1)}, bf16[2,256,384]{2,1,0:T(8,128)(2,1)S(1)}, u32[]{:S(2)}, u32[]{:S(2)}) %collective-permute-start.7) | collective-permute-done | bytes 393248 | tf_op jit(solution)/shard_map/ppermute | solution.py:33
  70.8 2.3 %collective-permute-start.9 = (bf16[2,128,384]{2,1,0:T(8,128)(2,1)S(1)}, bf16[2,128,384]{2,1,0:T(8,128)(2,1)S(1)}, u32[]{:S(2)}, u32[]{:S(2)}) collective-permute-start(bf16[2,128,384]{2,1,0:T(8,128)(2,1)S(1)} %slice.40), channel_id=1, source_target_pairs={{0,2},{2,4},{4,6},{6,7},{7,5},{5,3},{3,1},{1,0},{8,10},{10,12},{12... | collective-permute-start | bytes 589832 | tf_op jit(solution)/shard_map/ppermute | solution.py:38
  73.1 0.3 collective-permute-start.10
  73.4 0.8 constant_dynamic-update-slice_fusion.3
  74.2 0.8 constant_dynamic-update-slice_fusion.2
  75.0 1.5 %collective-permute-done.9 = bf16[2,128,384]{2,1,0:T(8,128)(2,1)S(1)} collective-permute-done((bf16[2,128,384]{2,1,0:T(8,128)(2,1)S(1)}, bf16[2,128,384]{2,1,0:T(8,128)(2,1)S(1)}, u32[]{:S(2)}, u32[]{:S(2)}) %collective-permute-start.9) | collective-permute-done | bytes 196640 | tf_op jit(solution)/shard_map/ppermute | solution.py:38
  76.5 0.7 constant_dynamic-update-slice_fusion.1
  77.2 1.9 %collective-permute-done.10 = bf16[2,128,384]{2,1,0:T(8,128)(2,1)S(1)} collective-permute-done((bf16[2,128,384]{2,1,0:T(8,128)(2,1)S(1)}, bf16[2,128,384]{2,1,0:T(8,128)(2,1)S(1)}, u32[]{:S(2)}, u32[]{:S(2)}) %collective-permute-start.10) | collective-permute-done | bytes 196640 | tf_op jit(solution)/shard_map/ppermute | solution.py:39
  79.1 0.7 constant_dynamic-update-slice_fusion
  79.8 7.0 %multiply_reduce_fusion = (f32[2,256]{1,0:T(2,128)S(1)}, f32[2,256,2048]{2,1,0:T(8,128)}) fusion(bf16[2,256,384]{2,1,0:T(8,128)(2,1)S(1)} %convolution_convert_fusion.2, bf16[2,2048,384]{2,1,0:T(8,128)(2,1)} %constant_dynamic-update-slice_fusion, bf16[384,384]{1,0:T(8,128)(2,1)S(1)} %copy-done), kind=kOutput, calls=%fused_computation.4 | convolution fusion | flops 2016935424 | bytes 8030208 | tf_op jit(solution)/shard_map/fqc,fkc->fqk/dot_general | solution.py:114
  86.8 3.0 %fusion = f32[2,256]{1,0:T(2,128)S(1)} fusion(f32[2,256,2048]{2,1,0:T(8,128)} %get-tuple-element.18, f32[2,256]{1,0:T(2,128)S(1)} %get-tuple-element.17), kind=kLoop, calls=%fused_computation.5 | loop fusion | flops 3145216 | bytes 4198400 | tf_op jit(solution)/shard_map/reduce_sum | solution.py:119
  89.9 0.0 copy-start.3
  89.9 6.4 %fusion.19 = bf16[2,256,384]{2,1,0:T(8,128)(2,1)S(1)} fusion(bf16[2,2048,384]{2,1,0:T(8,128)(2,1)} %constant_dynamic-update-slice_fusion, f32[2,256,2048]{2,1,0:T(8,128)} %get-tuple-element.18, f32[2,256]{1,0:T(2,128)S(1)} %get-tuple-element.17, f32[2,256]{1,0:T(2,128)S(1)} %fusion, bf16[384,384]{1,0:T(8,128)(2,1)S(1)} %copy-done.7), kind=kOutput, calls=%fused_computation.31 | convolution fusion | flops 2018377728 | bytes 8032256 | tf_op jit(solution)/shard_map/fqk,fkc->fqc/dot_general | solution.py:120
  96.3 0.4 fusion.49
  96.7 0.8 fusion.48
  (28 shorter events, 0.2 us)
Async XLA Ops:
  0.0 79.8 %copy-start = (bf16[384,384]{1,0:T(8,128)(2,1)S(1)}, bf16[384,384]{1,0:T(8,128)(2,1)}, u32[]{:S(2)}) copy-start(bf16[384,384]{1,0:T(8,128)(2,1)} %param.17) | copy-start | bytes 884740
  1.1 9.1 %collective-permute-start = (bf16[2,1,128,384]{3,2,1,0:T(8,128)(2,1)S(1)}, bf16[2,1,128,384]{3,2,1,0:T(8,128)(2,1)S(1)}, u32[]{:S(2)}, u32[]{:S(2)}) collective-permute-start(bf16[2,1,128,384]{3,2,1,0:T(8,128)(2,1)S(1)} %get-tuple-element.11), channel_id=1, source_target_pairs={{0,1},{1,2},{2,3},{3,4},{4,5},{5,6},{6,7},{8,9},{9,10},{10,11},{11... | collective-permute-start | bytes 589832 | tf_op jit(solution)/shard_map/ppermute | solution.py:15
  6.0 10.7 %copy-start.4 = (s32[2,2]{1,0:T(2,128)S(1)}, s32[2,2]{1,0:T(2,128)}, u32[]{:S(2)}) copy-start(s32[2,2]{1,0:T(2,128)} %param.11) | copy-start | bytes 52
  6.0 8.3 %collective-permute-start.1 = (bf16[2,1,128,384]{3,2,1,0:T(8,128)(2,1)S(1)}, bf16[2,1,128,384]{3,2,1,0:T(8,128)(2,1)S(1)}, u32[]{:S(2)}, u32[]{:S(2)}) collective-permute-start(bf16[2,1,128,384]{3,2,1,0:T(8,128)(2,1)S(1)} %get-tuple-element.12), channel_id=1, source_target_pairs={{1,0},{2,1},{3,2},{4,3},{5,4},{6,5},{7,6},{9,8},{10,9},{11,10},{12... | collective-permute-start | bytes 589832 | tf_op jit(solution)/shard_map/ppermute | solution.py:17
  16.6 2.4 %collective-permute-start.2 = (bf16[2,4,130,384]{3,1,2,0:T(4,128)(2,1)S(1)}, bf16[2,4,130,384]{3,1,2,0:T(4,128)(2,1)S(1)}, u32[]{:S(2)}, u32[]{:S(2)}) collective-permute-start(bf16[2,4,130,384]{3,1,2,0:T(4,128)(2,1)S(1)} %copy.36), channel_id=1, source_target_pairs={{0,8},{8,0},{1,9},{9,1},{2,10},{10,2},{3,11},{11,3},{4,12},{12,4},... | collective-permute-start | bytes 2396168 | tf_op jit(solution)/shard_map/ppermute | solution.py:76
  21.9 9.3 %slice-start = ((s8[7962624]{0:T(1024)(128)(4,1)}), s8[4194304]{0:T(1024)(128)(4,1)S(1)}, s32[]{:S(2)}) async-start(s8[7962624]{0:T(1024)(128)(4,1)} %bitcast.53), calls=%async_computation | async-start | bytes 8388608
  26.3 4.9 %slice-start.1 = ((s8[7962624]{0:T(1024)(128)(4,1)}), s8[3768320]{0:T(1024)(128)(4,1)S(1)}, s32[]{:S(2)}) async-start(s8[7962624]{0:T(1024)(128)(4,1)} %bitcast.53), calls=%async_computation.1 | async-start | bytes 7536640
  28.1 3.0 %copy-start.8 = (pred[16,17]{0,1:T(8,128)(4,1)S(1)}, pred[16,17]{0,1:T(8,128)(4,1)}, u32[]{:S(2)}) copy-start(pred[16,17]{0,1:T(8,128)(4,1)} %constant.101) | copy-start | bytes 820
  37.2 1.0 %copy-start.1 = (bf16[2,2,128,384]{3,2,1,0:T(8,128)(2,1)S(1)}, bf16[2,2,128,384]{3,2,1,0:T(8,128)(2,1)}, u32[]{:S(2)}) copy-start(bf16[2,2,128,384]{3,2,1,0:T(8,128)(2,1)} %param.10) | copy-start | bytes 1179652
  37.2 1.0 %copy-start.5 = (f32[384]{0:T(512)S(1)}, f32[384]{0:T(512)}, u32[]{:S(2)}) copy-start(f32[384]{0:T(512)} %param.14) | copy-start | bytes 4612
  37.2 1.2 %copy-start.6 = (f32[384]{0:T(512)S(1)}, f32[384]{0:T(512)}, u32[]{:S(2)}) copy-start(f32[384]{0:T(512)} %param.15) | copy-start | bytes 4612
  37.2 16.9 %copy-start.2 = (bf16[384,384]{1,0:T(8,128)(2,1)S(1)}, bf16[384,384]{1,0:T(8,128)(2,1)}, u32[]{:S(2)}) copy-start(bf16[384,384]{1,0:T(8,128)(2,1)} %param.16) | copy-start | bytes 884740
  38.6 12.2 %collective-permute-start.3 = (bf16[2,256,384]{2,1,0:T(8,128)(2,1)S(1)}, bf16[2,256,384]{2,1,0:T(8,128)(2,1)S(1)}, u32[]{:S(2)}, u32[]{:S(2)}) collective-permute-start(bf16[2,256,384]{2,1,0:T(8,128)(2,1)S(1)} %bitcast.47), channel_id=1, source_target_pairs={{0,2},{2,4},{4,6},{6,7},{7,5},{5,3},{3,1},{1,0},{8,10},{10,12},{12... | collective-permute-start | bytes 1179656 | tf_op jit(solution)/shard_map/ppermute | solution.py:33
  42.2 11.2 %collective-permute-start.4 = (bf16[2,256,384]{2,1,0:T(8,128)(2,1)S(1)}, bf16[2,256,384]{2,1,0:T(8,128)(2,1)S(1)}, u32[]{:S(2)}, u32[]{:S(2)}) collective-permute-start(bf16[2,256,384]{2,1,0:T(8,128)(2,1)S(1)} %bitcast.48), channel_id=1, source_target_pairs={{0,1},{2,0},{4,2},{6,4},{7,6},{5,7},{3,5},{1,3},{8,9},{10,8},{12,1... | collective-permute-start | bytes 1179656 | tf_op jit(solution)/shard_map/ppermute | solution.py:34
  50.8 10.4 %collective-permute-start.5 = (bf16[2,256,384]{2,1,0:T(8,128)(2,1)S(1)}, bf16[2,256,384]{2,1,0:T(8,128)(2,1)S(1)}, u32[]{:S(2)}, u32[]{:S(2)}) collective-permute-start(bf16[2,256,384]{2,1,0:T(8,128)(2,1)S(1)} %collective-permute-done.3), channel_id=1, source_target_pairs={{0,2},{2,4},{4,6},{6,7},{7,5},{5,3},{3,1},{1,0},{8,10},{10,12},{12... | collective-permute-start | bytes 1179656 | tf_op jit(solution)/shard_map/ppermute | solution.py:33
  53.3 10.3 %collective-permute-start.6 = (bf16[2,256,384]{2,1,0:T(8,128)(2,1)S(1)}, bf16[2,256,384]{2,1,0:T(8,128)(2,1)S(1)}, u32[]{:S(2)}, u32[]{:S(2)}) collective-permute-start(bf16[2,256,384]{2,1,0:T(8,128)(2,1)S(1)} %collective-permute-done.4), channel_id=1, source_target_pairs={{0,1},{2,0},{4,2},{6,4},{7,6},{5,7},{3,5},{1,3},{8,9},{10,8},{12,1... | collective-permute-start | bytes 1179656 | tf_op jit(solution)/shard_map/ppermute | solution.py:34
  61.3 9.5 %collective-permute-start.7 = (bf16[2,256,384]{2,1,0:T(8,128)(2,1)S(1)}, bf16[2,256,384]{2,1,0:T(8,128)(2,1)S(1)}, u32[]{:S(2)}, u32[]{:S(2)}) collective-permute-start(bf16[2,256,384]{2,1,0:T(8,128)(2,1)S(1)} %collective-permute-done.5), channel_id=1, source_target_pairs={{0,2},{2,4},{4,6},{6,7},{7,5},{5,3},{3,1},{1,0},{8,10},{10,12},{12... | collective-permute-start | bytes 1179656 | tf_op jit(solution)/shard_map/ppermute | solution.py:33
  63.6 9.5 %collective-permute-start.8 = (bf16[2,256,384]{2,1,0:T(8,128)(2,1)S(1)}, bf16[2,256,384]{2,1,0:T(8,128)(2,1)S(1)}, u32[]{:S(2)}, u32[]{:S(2)}) collective-permute-start(bf16[2,256,384]{2,1,0:T(8,128)(2,1)S(1)} %collective-permute-done.6), channel_id=1, source_target_pairs={{0,1},{2,0},{4,2},{6,4},{7,6},{5,7},{3,5},{1,3},{8,9},{10,8},{12,1... | collective-permute-start | bytes 1179656 | tf_op jit(solution)/shard_map/ppermute | solution.py:34
  70.8 5.7 %collective-permute-start.9 = (bf16[2,128,384]{2,1,0:T(8,128)(2,1)S(1)}, bf16[2,128,384]{2,1,0:T(8,128)(2,1)S(1)}, u32[]{:S(2)}, u32[]{:S(2)}) collective-permute-start(bf16[2,128,384]{2,1,0:T(8,128)(2,1)S(1)} %slice.40), channel_id=1, source_target_pairs={{0,2},{2,4},{4,6},{6,7},{7,5},{5,3},{3,1},{1,0},{8,10},{10,12},{12... | collective-permute-start | bytes 589832 | tf_op jit(solution)/shard_map/ppermute | solution.py:38
  73.1 5.9 %collective-permute-start.10 = (bf16[2,128,384]{2,1,0:T(8,128)(2,1)S(1)}, bf16[2,128,384]{2,1,0:T(8,128)(2,1)S(1)}, u32[]{:S(2)}, u32[]{:S(2)}) collective-permute-start(bf16[2,128,384]{2,1,0:T(8,128)(2,1)S(1)} %slice.41), channel_id=1, source_target_pairs={{0,1},{2,0},{4,2},{6,4},{7,6},{5,7},{3,5},{1,3},{8,9},{10,8},{12,1... | collective-permute-start | bytes 589832 | tf_op jit(solution)/shard_map/ppermute | solution.py:39
  86.8 3.1 %copy-start.7 = (bf16[384,384]{1,0:T(8,128)(2,1)S(1)}, bf16[384,384]{1,0:T(8,128)(2,1)}, u32[]{:S(2)}) copy-start(bf16[384,384]{1,0:T(8,128)(2,1)} %param.18) | copy-start | bytes 884740
  89.9 6.4 %copy-start.3 = (bf16[384,384]{1,0:T(8,128)(2,1)S(1)}, bf16[384,384]{1,0:T(8,128)(2,1)}, u32[]{:S(2)}) copy-start(bf16[384,384]{1,0:T(8,128)(2,1)} %param.19) | copy-start | bytes 884740

commit v15 on v7

--- a/solution.py
+++ b/solution.py
@@ -62,9 +62,12 @@
     out_weight,
 ):
     span_count, row_count, col_count, channels = frames.shape
+    rims = padded_2(frames, (("height", 1),), 1)
+    rims = jnp.concatenate([rims[:, :1], rims[:, -1:]], axis=1)
     activated = jax.nn.silu(rms_scaled(frames, gain_conv)).astype(jnp.bfloat16)
-    activated = jnp.pad(activated, ((0, 0), (0, 0), (1, 1), (0, 0)))
-    rimmed = padded_2(activated, (("height", 1),), 1)
+    rims = jax.nn.silu(rms_scaled(rims, gain_conv)).astype(jnp.bfloat16)
+    rimmed = jnp.concatenate([rims[:, :1], activated, rims[:, 1:]], axis=1)
+    rimmed = jnp.pad(rimmed, ((0, 0), (0, 0), (1, 1), (0, 0)))
     ways = lax.axis_size("tm")
     mine = lax.axis_index("tm")
     pieces = [rimmed]
@@ -85,57 +88,58 @@
     window = jnp.take(pool, picks.reshape(-1), axis=0).reshape(
         (span_count, 3) + rimmed.shape[1:]
     )
-    accum = lax.conv_general_dilated(
-        window,
-        conv_weight,
-        window_strides=(1, 1, 1),
-        padding="VALID",
-        dimension_numbers=("NDHWC", "DHWIO", "NDHWC"),
-        preferred_element_type=jnp.float32,
-    )[:, 0]
-    mixed = (frames.astype(jnp.float32) + accum + conv_bias).astype(jnp.bfloat16)
-    normed = rms_scaled(mixed, gain_attn).astype(jnp.bfloat16)
-    tokens = normed.reshape(span_count, row_count * col_count, channels)
-    queries = jnp.einsum(
-        "ftc,cd->ftd", tokens, query_weight, preferred_element_type=jnp.float32
-    ).astype(jnp.bfloat16)
     score_scale = 1.0 / channels**0.5
-    pieces = ring_gather(tokens, "height", 1)
-    scored = []
-    for piece in pieces:
-        keys = jnp.einsum(
-            "ftc,cd->ftd", piece, key_weight, preferred_element_type=jnp.float32
+    outputs = []
+    span_window = window[:1]
+    for span in range(span_count):
+        accum = lax.conv_general_dilated(
+            span_window,
+            conv_weight,
+            window_strides=(1, 1, 1),
+            padding="VALID",
+            dimension_numbers=("NDHWC", "DHWIO", "NDHWC"),
+            preferred_element_type=jnp.float32,
+        )[:, 0]
+        mixed = (frames[span : span + 1].astype(jnp.float32) + accum + conv_bias).astype(
+            jnp.bfloat16
+        )
+        normed = rms_scaled(mixed, gain_attn).astype(jnp.bfloat16)
+        tokens = normed.reshape(1, row_count * col_count, channels)
+        queries = jnp.einsum(
+            "ftc,cd->ftd", tokens, query_weight, preferred_element_type=jnp.float32
         ).astype(jnp.bfloat16)
-        values = jnp.einsum(
-            "ftc,cd->ftd", piece, value_weight, preferred_element_type=jnp.float32
+        pieces = ring_gather(tokens, "height", 1)
+        if span + 1 < span_count:
+            pieces[1], span_window = lax.optimization_barrier(
+                (pieces[1], window[span + 1 : span + 2])
+            )
+        tokens_all = jnp.concatenate(pieces, axis=1)
+        keys_all = jnp.einsum(
+            "ftc,cd->ftd", tokens_all, key_weight, preferred_element_type=jnp.float32
+        ).astype(jnp.bfloat16)
+        values_all = jnp.einsum(
+            "ftc,cd->ftd", tokens_all, value_weight, preferred_element_type=jnp.float32
         ).astype(jnp.bfloat16)
         scores = (
-            jnp.einsum("fqc,fkc->fqk", queries, keys, preferred_element_type=jnp.float32)
+            jnp.einsum("fqc,fkc->fqk", queries, keys_all, preferred_element_type=jnp.float32)
             * score_scale
         )
-        scored.append((scores, values))
-    peaks = scored[0][0].max(axis=-1, keepdims=True)
-    for scores, _ in scored[1:]:
-        peaks = jnp.maximum(peaks, scores.max(axis=-1, keepdims=True))
-    totals = None
-    summed = None
-    for scores, values in scored:
+        peaks = jnp.max(scores, axis=-1, keepdims=True)
         weights_exp = jnp.exp(scores - peaks)
-        part_total = jnp.sum(weights_exp, axis=-1)
-        part_sum = jnp.einsum(
+        totals = jnp.sum(weights_exp, axis=-1)
+        summed = jnp.einsum(
             "fqk,fkc->fqc",
             weights_exp.astype(jnp.bfloat16),
-            values,
+            values_all,
             preferred_element_type=jnp.float32,
         )
-        totals = part_total if totals is None else totals + part_total
-        summed = part_sum if summed is None else summed + part_sum
-    attended = (summed / totals[:, :, None]).astype(jnp.bfloat16)
-    projected = jnp.einsum("ftc,cd->ftd", attended, out_weight, preferred_element_type=jnp.float32)
-    encoded = mixed.astype(jnp.float32) + projected.reshape(
-        span_count, row_count, col_count, channels
-    )
-    return encoded.astype(jnp.bfloat16)
+        attended = (summed / totals[:, :, None]).astype(jnp.bfloat16)
+        projected = jnp.einsum(
+            "ftc,cd->ftd", attended, out_weight, preferred_element_type=jnp.float32
+        )
+        encoded = mixed.astype(jnp.float32) + projected.reshape(mixed.shape)
+        outputs.append(encoded.astype(jnp.bfloat16))
+    return jnp.concatenate(outputs, axis=0)
 
 
 def solution(mesh):

time: 105 us -> 96.8 us (0.922)
  matrix products: 40.6 us -> 20.8 us
  local copies, waits for them, and re-layouts: 9.5 us -> 23.3 us
  starting transfers between devices: 17.1 us -> 24.2 us
  other arithmetic: 14.6 us -> 8.4 us
  waiting for transfers between devices: 22.5 us -> 19 us
    dot_general x18 -> x4, matrix products: 33.9 us -> 12.7 us  [the longest x2 6.41 us: shards(): jnp.einsum('fqc,fkc->fqk', queries, keys_all, preferred_element_type=jnp....]
    unnamed x42 -> x44, local copies, waits for them, and re-layouts: 1 us -> 14 us
    ppermute x3 -> x6, starting transfers between devices: 0.32 us -> 6.87 us  [ring_gather(): backward = lax.ppermute(backward, axis, behind)]
    ppermute x1 -> x2, starting transfers between devices: 0.01 us -> 3.23 us  [ring_gather(): lax.ppermute(lax.slice_in_dim(backward, half, block.shape[dim], axis=dim)...]
    ppermute x1, waiting for transfers between devices: 7.49 us -> 4.36 us  [padded_2(): lax.ppermute(tail, axis, [(i, (i + 1) % count) for i in range(ends)])]
    conv_general_dilated x1 -> x0, other arithmetic: 2.81 us -> none  [shards(): lax.conv_general_dilated(window, conv_weight, window_strides=(1, 1, 1), p...]
    ppermute x3 -> x6, starting transfers between devices: 8.31 us -> 5.98 us  [ring_gather(): forward = lax.ppermute(forward, axis, ahead)]
    select_n x2, other arithmetic: 4.36 us -> 2.21 us  [shards(): jnp.take(pool, picks.reshape(-1), axis=0)]
  transfers between devices with their start and end apart: 11 -> 19, of which waited for: 6 -> 7; matrix products, arithmetic and copies ran while one was open for 19% -> 30% of each run, Pallas kernels for 0% -> 0%
where the time goes in v15:
time: 96.8 us; the launch traced here: 96.2 us
  starting transfers between devices  24.2 us (25%)
  local copies, waits for them, and re-layouts  23.3 us (24%)
  matrix products  20.8 us (21%)
  waiting for transfers between devices  19 us (20%)
  other arithmetic  8.4 us (9%)
    unnamed x44, local copies, waits for them, and re-layouts  14 us
    ppermute x6, waiting for transfers between devices, ring_gather(): forward = lax.ppermute(forward, axis, ahead)  11.3 us
    ppermute x6, starting transfers between devices, ring_gather(): backward = lax.ppermute(backward, axis, behind)  6.87 us
    dot_general x2, matrix products, shards(): jnp.einsum('fqc,fkc->fqk', queries, keys_all, preferred_element_type=jnp....  6.41 us
    conv_general_dilated x2, matrix products, shards(): lax.conv_general_dilated(span_window, conv_weight, window_strides=(1, 1,...  6.34 us
    dot_general x2, matrix products, shards(): jnp.einsum('fqk,fkc->fqc', weights_exp.astype(jnp.bfloat16), values_all,...  6.28 us
    ppermute x6, starting transfers between devices, ring_gather(): forward = lax.ppermute(forward, axis, ahead)  5.98 us
    ppermute x1, starting transfers between devices, padded_2(): lax.ppermute(tail, axis, [(i, (i + 1) % count) for i in range(ends)])  5.52 us
  transfers between devices with their start and end apart: 19, of which 7 were waited for; matrix products, arithmetic and copies ran while one was open for 30% of the time, Pallas kernels for 0%

profile of v15, /device:TPU:0, one launch (start us, length us, event | category | flops | bytes accessed | tf_op | source)
XLA Modules:
  0.0 96.2 jit_solution(17941834703001488397)
XLA Ops:
  0.0 1.1 %fusion.114 = (bf16[2,1,128,384]{3,2,1,0:T(8,128)(2,1)S(1)}, bf16[2,1,128,384]{3,2,1,0:T(8,128)(2,1)S(1)}) fusion(bf16[2,2,128,384]{3,2,1,0:T(8,128)(2,1)} %param.10), kind=kLoop, calls=%fused_computation.165 | loop fusion | bytes 786432 | tf_op jit(solution)/shard_map/slice | solution.py:12
  1.1 1.3 %collective-permute-start.1 = (bf16[2,1,128,384]{3,2,1,0:T(8,128)(2,1)S(1)}, bf16[2,1,128,384]{3,2,1,0:T(8,128)(2,1)S(1)}, u32[]{:S(2)}, u32[]{:S(2)}) collective-permute-start(bf16[2,1,128,384]{3,2,1,0:T(8,128)(2,1)S(1)} %get-tuple-element.18), channel_id=1, source_target_pairs={{1,0},{2,1},{3,2},{4,3},{5,4},{6,5},{7,6},{9,8},{10,9},{11,10},{12... | collective-permute-start | bytes 589832 | tf_op jit(solution)/shard_map/ppermute | solution.py:17
  2.4 5.5 %collective-permute-start = (bf16[2,1,128,384]{3,2,1,0:T(8,128)(2,1)S(1)}, bf16[2,1,128,384]{3,2,1,0:T(8,128)(2,1)S(1)}, u32[]{:S(2)}, u32[]{:S(2)}) collective-permute-start(bf16[2,1,128,384]{3,2,1,0:T(8,128)(2,1)S(1)} %get-tuple-element.17), channel_id=1, source_target_pairs={{0,1},{1,2},{2,3},{3,4},{4,5},{5,6},{6,7},{8,9},{9,10},{10,11},{11... | collective-permute-start | bytes 589832 | tf_op jit(solution)/shard_map/ppermute | solution.py:15
  8.0 1.1 %fusion.74 = f32[2,2,128]{2,1,0:T(2,128)S(1)} fusion(bf16[2,2,128,384]{3,2,1,0:T(8,128)(2,1)} %param.10), kind=kLoop, calls=%fused_computation.74 | loop fusion | flops 589312 | bytes 395264 | tf_op jit(solution)/shard_map/reduce_sum | solution.py:48
  9.1 1.8 %collective-permute-done.1 = bf16[2,1,128,384]{3,2,1,0:T(8,128)(2,1)S(1)} collective-permute-done((bf16[2,1,128,384]{3,2,1,0:T(8,128)(2,1)S(1)}, bf16[2,1,128,384]{3,2,1,0:T(8,128)(2,1)S(1)}, u32[]{:S(2)}, u32[]{:S(2)}) %collective-permute-start.1) | collective-permute-done | bytes 196640 | tf_op jit(solution)/shard_map/ppermute | solution.py:17
  10.9 4.4 %collective-permute-done = bf16[2,1,128,384]{3,2,1,0:T(8,128)(2,1)S(1)} collective-permute-done((bf16[2,1,128,384]{3,2,1,0:T(8,128)(2,1)S(1)}, bf16[2,1,128,384]{3,2,1,0:T(8,128)(2,1)S(1)}, u32[]{:S(2)}, u32[]{:S(2)}) %collective-permute-start) | collective-permute-done | bytes 196640 | tf_op jit(solution)/shard_map/ppermute | solution.py:15
  15.5 0.5 fusion.81
  17.2 1.6 %collective-permute-done.2 = bf16[2,4,130,384]{3,2,1,0:T(8,128)(2,1)} collective-permute-done((bf16[2,4,130,384]{3,2,1,0:T(8,128)(2,1)S(1)}, bf16[2,4,130,384]{3,2,1,0:T(8,128)(2,1)}, u32[]{:S(2)}, u32[]{:S(2)}) %collective-permute-start.2) | collective-permute-done | bytes 798752 | tf_op jit(solution)/shard_map/ppermute | solution.py:76
  18.9 1.7 %maximum_maximum_fusion = bf16[5,4,130,384]{3,2,1,0:T(8,128)(2,1)S(1)} fusion(bf16[2,4,130,384]{3,2,1,0:T(8,128)(2,1)} %collective-permute-done.2, bf16[2,4,130,384]{3,2,1,0:T(8,128)(2,1)} %copy-done.2, bf16[5]{0:T(256)(128)(2,1)S(1)} %pad.17.clone), kind=kLoop, calls=%fused_computation.15 | loop fusion | flops 1996800 | bytes 3594250 | tf_op jit(solution)/shard_map/concatenate | solution.py:79
  20.6 2.5 %gather_fusion = bf16[6,4,130,384]{3,2,1,0:T(8,128)(2,1)} fusion(bf16[5,4,130,384]{3,2,1,0:T(8,128)(2,1)S(1)} %maximum_maximum_fusion, s32[1024]{0:T(1024)S(1)} %pad_clamp_fusion), kind=kCustom, calls=%fused_computation | custom fusion | bytes 4792344 | tf_op jit(solution)/shard_map/jit(_take)/gather | solution.py:88
  23.1 2.2 %broadcast_select_fusion = bf16[6,4,130,384]{3,2,1,0:T(8,128)(2,1)S(1)} fusion(bf16[6,4,130,384]{3,2,1,0:T(8,128)(2,1)} %gather_fusion, pred[6]{0:T(512)(128)(4,1)S(1)} %compare_and_fusion), kind=kLoop, calls=%fused_computation.12 | loop fusion | flops 1198080 | bytes 4792326 | tf_op jit(solution)/shard_map/jit(_take)/select_n | solution.py:88
  25.6 0.5 copy.23
  26.1 0.5 pad.5.clone
  26.8 0.8 slice-done.1
  27.6 3.2 %fusion.38 = f32[1,2,8,17,384]{4,2,3,1,0:T(8,128)S(1)} fusion(bf16[3,3,3,384,384]{4,3,2,1,0:T(8,128)(2,1)S(1)} %bitcast.123, bf16[3,4,1,7,2,384]{5,3,4,1,0,2:T(8,128)(2,1)S(1)} %slice.73, bf16[3,4,1,8,17,384]{5,3,4,1,0,2:T(8,128)(2,1)S(1)} %copy.13, pred[8,17]{0,1:T(8,128)(4,1)S(1)} %copy-done.10), kind=kOutput, calls=%fused_computation.44 | convolution fusion | flops 2170140672 | bytes 9762952 | tf_op jit(solution)/shard_map/conv_general_dilated | solution.py:95
  31.1 0.3 copy-done.6
  31.7 1.7 %collective-permute-start.3 = (bf16[1,256,384]{2,1,0:T(8,128)(2,1)S(1)}, bf16[1,256,384]{2,1,0:T(8,128)(2,1)S(1)}, u32[]{:S(2)}, u32[]{:S(2)}) collective-permute-start(bf16[1,256,384]{2,1,0:T(8,128)(2,1)S(1)} %bitcast.110), channel_id=1, source_target_pairs={{0,2},{2,4},{4,6},{6,7},{7,5},{5,3},{3,1},{1,0},{8,10},{10,12},{12... | collective-permute-start | bytes 589832 | tf_op jit(solution)/shard_map/ppermute | solution.py:33
  33.4 0.7 constant_dynamic-update-slice_fusion.8
  34.1 0.8 collective-permute-start.4
  35.2 4.2 %collective-permute-done.3 = bf16[1,256,384]{2,1,0:T(8,128)(2,1)S(1)} collective-permute-done((bf16[1,256,384]{2,1,0:T(8,128)(2,1)S(1)}, bf16[1,256,384]{2,1,0:T(8,128)(2,1)S(1)}, u32[]{:S(2)}, u32[]{:S(2)}) %collective-permute-start.3) | collective-permute-done | bytes 196640 | tf_op jit(solution)/shard_map/ppermute | solution.py:33
  39.5 0.5 copy.24
  39.9 0.5 pad.7.clone
  40.6 3.2 %fusion.35 = f32[1,2,8,17,384]{4,2,3,1,0:T(8,128)S(1)} fusion(bf16[3,3,3,384,384]{4,3,2,1,0:T(8,128)(2,1)S(1)} %bitcast.123, bf16[3,4,1,7,2,384]{5,3,4,1,0,2:T(8,128)(2,1)S(1)} %slice.78, bf16[3,4,1,8,17,384]{5,3,4,1,0,2:T(8,128)(2,1)S(1)} %copy.18, pred[8,17]{0,1:T(8,128)(4,1)S(1)} %copy-done.10), kind=kOutput, calls=%fused_computation.43 | convolution fusion | flops 2170140672 | bytes 9762952 | tf_op jit(solution)/shard_map/conv_general_dilated | solution.py:95
  44.4 1.0 collective-permute-start.11
  45.4 1.1 %collective-permute-start.12 = (bf16[1,256,384]{2,1,0:T(8,128)(2,1)S(1)}, bf16[1,256,384]{2,1,0:T(8,128)(2,1)S(1)}, u32[]{:S(2)}, u32[]{:S(2)}) collective-permute-start(bf16[1,256,384]{2,1,0:T(8,128)(2,1)S(1)} %bitcast.115), channel_id=1, source_target_pairs={{0,1},{2,0},{4,2},{6,4},{7,6},{5,7},{3,5},{1,3},{8,9},{10,8},{12,1... | collective-permute-start | bytes 589832 | tf_op jit(solution)/shard_map/ppermute | solution.py:34
  46.5 0.9 collective-permute-start.5
  47.4 0.7 constant_dynamic-update-slice_fusion.7
  48.1 1.1 %collective-permute-start.6 = (bf16[1,256,384]{2,1,0:T(8,128)(2,1)S(1)}, bf16[1,256,384]{2,1,0:T(8,128)(2,1)S(1)}, u32[]{:S(2)}, u32[]{:S(2)}) collective-permute-start(bf16[1,256,384]{2,1,0:T(8,128)(2,1)S(1)} %collective-permute-done.4), channel_id=1, source_target_pairs={{0,1},{2,0},{4,2},{6,4},{7,6},{5,7},{3,5},{1,3},{8,9},{10,8},{12,1... | collective-permute-start | bytes 589832 | tf_op jit(solution)/shard_map/ppermute | solution.py:34
  49.3 0.7 constant_dynamic-update-slice_fusion.6
  49.9 0.9 convolution_convert_fusion.4
  50.9 1.4 %collective-permute-done.11 = bf16[1,256,384]{2,1,0:T(8,128)(2,1)S(1)} collective-permute-done((bf16[1,256,384]{2,1,0:T(8,128)(2,1)S(1)}, bf16[1,256,384]{2,1,0:T(8,128)(2,1)S(1)}, u32[]{:S(2)}, u32[]{:S(2)}) %collective-permute-start.11) | collective-permute-done | bytes 196640 | tf_op jit(solution)/shard_map/ppermute | solution.py:33
  52.3 0.9 collective-permute-start.13
  53.2 1.1 %collective-permute-start.14 = (bf16[1,256,384]{2,1,0:T(8,128)(2,1)S(1)}, bf16[1,256,384]{2,1,0:T(8,128)(2,1)}, u32[]{:S(2)}, u32[]{:S(2)}) collective-permute-start(bf16[1,256,384]{2,1,0:T(8,128)(2,1)S(1)} %collective-permute-done.12), channel_id=1, source_target_pairs={{0,1},{2,0},{4,2},{6,4},{7,6},{5,7},{3,5},{1,3},{8,9},{10,8},{12,1... | collective-permute-start | bytes 589832 | tf_op jit(solution)/shard_map/ppermute | solution.py:34
  54.3 2.2 %collective-permute-done.5 = bf16[1,256,384]{2,1,0:T(8,128)(2,1)S(1)} collective-permute-done((bf16[1,256,384]{2,1,0:T(8,128)(2,1)S(1)}, bf16[1,256,384]{2,1,0:T(8,128)(2,1)S(1)}, u32[]{:S(2)}, u32[]{:S(2)}) %collective-permute-start.5) | collective-permute-done | bytes 196640 | tf_op jit(solution)/shard_map/ppermute | solution.py:33
  56.5 0.9 collective-permute-start.7
  57.5 1.2 %collective-permute-start.8 = (bf16[1,256,384]{2,1,0:T(8,128)(2,1)S(1)}, bf16[1,256,384]{2,1,0:T(8,128)(2,1)S(1)}, u32[]{:S(2)}, u32[]{:S(2)}) collective-permute-start(bf16[1,256,384]{2,1,0:T(8,128)(2,1)S(1)} %collective-permute-done.6), channel_id=1, source_target_pairs={{0,1},{2,0},{4,2},{6,4},{7,6},{5,7},{3,5},{1,3},{8,9},{10,8},{12,1... | collective-permute-start | bytes 589832 | tf_op jit(solution)/shard_map/ppermute | solution.py:34
  58.7 0.7 constant_dynamic-update-slice_fusion.5
  59.3 0.7 constant_dynamic-update-slice_fusion.4
  60.0 3.5 %collective-permute-done.7 = bf16[1,256,384]{2,1,0:T(8,128)(2,1)S(1)} collective-permute-done((bf16[1,256,384]{2,1,0:T(8,128)(2,1)S(1)}, bf16[1,256,384]{2,1,0:T(8,128)(2,1)S(1)}, u32[]{:S(2)}, u32[]{:S(2)}) %collective-permute-start.7) | collective-permute-done | bytes 196640 | tf_op jit(solution)/shard_map/ppermute | solution.py:33
  63.5 0.6 collective-permute-start.9
  64.2 1.5 %collective-permute-start.10 = (bf16[1,128,384]{2,1,0:T(8,128)(2,1)S(1)}, bf16[1,128,384]{2,1,0:T(8,128)(2,1)S(1)}, u32[]{:S(2)}, u32[]{:S(2)}) collective-permute-start(bf16[1,128,384]{2,1,0:T(8,128)(2,1)S(1)} %slice.77), channel_id=1, source_target_pairs={{0,1},{2,0},{4,2},{6,4},{7,6},{5,7},{3,5},{1,3},{8,9},{10,8},{12,1... | collective-permute-start | bytes 294920 | tf_op jit(solution)/shard_map/ppermute | solution.py:39
  65.7 0.6 collective-permute-start.15
  66.3 1.0 %constant_dynamic-update-slice_fusion.14 = bf16[1,2048,384]{2,1,0:T(8,128)(2,1)S(1)} fusion(bf16[1,2048,384]{2,1,0:T(8,128)(2,1)S(1)} %constant_dynamic-update-slice_fusion.15, bf16[1,256,384]{2,1,0:T(8,128)(2,1)} %collective-permute-done.13), kind=kLoop, calls=%fused_computation.120 | loop fusion | bytes 393216
  67.3 1.5 %collective-permute-start.16 = (bf16[1,256,384]{2,1,0:T(8,128)(2,1)}, bf16[1,256,384]{2,1,0:T(8,128)(2,1)}, u32[]{:S(2)}, u32[]{:S(2)}) collective-permute-start(bf16[1,256,384]{2,1,0:T(8,128)(2,1)} %collective-permute-done.14), channel_id=1, source_target_pairs={{0,1},{2,0},{4,2},{6,4},{7,6},{5,7},{3,5},{1,3},{8,9},{10,8},{12,1... | collective-permute-start | bytes 589832 | tf_op jit(solution)/shard_map/ppermute | solution.py:34
  68.8 1.0 %constant_dynamic-update-slice_fusion.13 = bf16[1,2048,384]{2,1,0:T(8,128)(2,1)S(1)} fusion(bf16[1,2048,384]{2,1,0:T(8,128)(2,1)S(1)} %constant_dynamic-update-slice_fusion.14, bf16[1,256,384]{2,1,0:T(8,128)(2,1)} %collective-permute-done.14), kind=kLoop, calls=%fused_computation.119 | loop fusion | bytes 393216
  69.8 0.8 constant_dynamic-update-slice_fusion.3
  70.5 0.7 constant_dynamic-update-slice_fusion.2
  71.3 0.6 constant_dynamic-update-slice_fusion.1
  71.9 0.6 constant_dynamic-update-slice_fusion
  72.5 3.1 %fusion.118 = (f32[256]{0:T(256)S(1)}, f32[256,2048]{1,0:T(8,128)S(1)}) fusion(bf16[256,384]{1,0:T(8,128)(2,1)S(1)} %convolution_convert_fusion.5, bf16[384,384]{1,0:T(8,128)(2,1)S(1)} %copy-done, bf16[1,2048,384]{2,1,0:T(8,128)(2,1)} %constant_dynamic-update-slice_fusion), kind=kOutput, calls=%fused_computation.167 | convolution fusion | flops 1008467712 | bytes 4162560 | tf_op jit(solution)/shard_map/fqc,fkc->fqk/dot_general | solution.py:124
  75.7 0.4 fusion.2
  76.1 3.2 %fusion.54 = bf16[256,384]{1,0:T(8,128)(2,1)S(1)} fusion(bf16[384,384]{1,0:T(8,128)(2,1)} %param.18, bf16[1,2048,384]{2,1,0:T(8,128)(2,1)} %constant_dynamic-update-slice_fusion, f32[256,2048]{1,0:T(8,128)S(1)} %get-tuple-element.26, f32[256]{0:T(256)S(1)} %get-tuple-element.25, f32[256]{0:T(256)S(1)} %fusion.2), kind=kOutput, calls=%fused_computation.54 | convolution fusion | flops 1008664576 | bytes 4163584 | tf_op jit(solution)/shard_map/fqk,fkc->fqc/dot_general | solution.py:130
  79.6 0.9 slice.80
  80.5 0.6 collective-permute-start.17
  81.1 0.9 slice.81
  82.0 1.7 %collective-permute-start.18 = (bf16[1,128,384]{2,1,0:T(8,128)(2,1)S(1)}, bf16[1,128,384]{2,1,0:T(8,128)(2,1)S(1)}, u32[]{:S(2)}, u32[]{:S(2)}) collective-permute-start(bf16[1,128,384]{2,1,0:T(8,128)(2,1)S(1)} %slice.81), channel_id=1, source_target_pairs={{0,1},{2,0},{4,2},{6,4},{7,6},{5,7},{3,5},{1,3},{8,9},{10,8},{12,1... | collective-permute-start | bytes 294920 | tf_op jit(solution)/shard_map/ppermute | solution.py:39
  83.8 1.6 %constant_dynamic-update-slice_fusion.12 = bf16[1,2048,384]{2,1,0:T(8,128)(2,1)} fusion(bf16[1,2048,384]{2,1,0:T(8,128)(2,1)} %copy-done.5, bf16[1,256,384]{2,1,0:T(8,128)(2,1)} %collective-permute-done.15), kind=kLoop, calls=%fused_computation.118 | loop fusion | bytes 393216
  85.4 1.6 %constant_dynamic-update-slice_fusion.11 = bf16[1,2048,384]{2,1,0:T(8,128)(2,1)} fusion(bf16[1,2048,384]{2,1,0:T(8,128)(2,1)} %constant_dynamic-update-slice_fusion.12, bf16[1,256,384]{2,1,0:T(8,128)(2,1)} %collective-permute-done.16), kind=kLoop, calls=%fused_computation.117 | loop fusion | bytes 393216
  87.0 0.6 constant_dynamic-update-slice_fusion.10
  87.7 0.7 constant_dynamic-update-slice_fusion.9
  88.3 3.3 %fusion.115 = (f32[256]{0:T(256)S(1)}, f32[256,2048]{1,0:T(8,128)S(1)}) fusion(bf16[256,384]{1,0:T(8,128)(2,1)} %convolution_convert_fusion.4, bf16[384,384]{1,0:T(8,128)(2,1)S(1)} %copy-done, bf16[1,2048,384]{2,1,0:T(8,128)(2,1)} %constant_dynamic-update-slice_fusion.9), kind=kOutput, calls=%fused_computation.166 | convolution fusion | flops 1008467712 | bytes 4162560 | tf_op jit(solution)/shard_map/fqc,fkc->fqk/dot_general | solution.py:124
  91.6 0.4 fusion.4
  92.0 3.1 %fusion.48 = bf16[256,384]{1,0:T(8,128)(2,1)S(1)} fusion(bf16[384,384]{1,0:T(8,128)(2,1)} %param.18, bf16[1,2048,384]{2,1,0:T(8,128)(2,1)} %constant_dynamic-update-slice_fusion.9, f32[256,2048]{1,0:T(8,128)S(1)} %get-tuple-element.24, f32[256]{0:T(256)S(1)} %get-tuple-element.23, f32[256]{0:T(256)S(1)} %fusion.4), kind=kOutput, calls=%fused_computation.52 | convolution fusion | flops 1008664576 | bytes 4163584 | tf_op jit(solution)/shard_map/fqk,fkc->fqc/dot_general | solution.py:130
  95.4 0.8 pad_maximum_fusion.1
  (75 shorter events, 4.2 us)
Async XLA Ops:
  0.0 72.5 %copy-start = (bf16[384,384]{1,0:T(8,128)(2,1)S(1)}, bf16[384,384]{1,0:T(8,128)(2,1)}, u32[]{:S(2)}) copy-start(bf16[384,384]{1,0:T(8,128)(2,1)} %param.17) | copy-start | bytes 884740
  0.0 15.4 %copy-start.1 = (bf16[2,2,128,384]{3,2,1,0:T(8,128)(2,1)S(1)}, bf16[2,2,128,384]{3,2,1,0:T(8,128)(2,1)}, u32[]{:S(2)}) copy-start(bf16[2,2,128,384]{3,2,1,0:T(8,128)(2,1)} %param.10) | copy-start | bytes 1179652
  0.0 15.5 %copy-start.9 = (f32[384]{0:T(512)S(1)}, f32[384]{0:T(512)}, u32[]{:S(2)}) copy-start(f32[384]{0:T(512)} %param.12) | copy-start | bytes 4612
  1.1 9.8 %collective-permute-start.1 = (bf16[2,1,128,384]{3,2,1,0:T(8,128)(2,1)S(1)}, bf16[2,1,128,384]{3,2,1,0:T(8,128)(2,1)S(1)}, u32[]{:S(2)}, u32[]{:S(2)}) collective-permute-start(bf16[2,1,128,384]{3,2,1,0:T(8,128)(2,1)S(1)} %get-tuple-element.18), channel_id=1, source_target_pairs={{1,0},{2,1},{3,2},{4,3},{5,4},{6,5},{7,6},{9,8},{10,9},{11,10},{12... | collective-permute-start | bytes 589832 | tf_op jit(solution)/shard_map/ppermute | solution.py:17
  2.4 12.8 %collective-permute-start = (bf16[2,1,128,384]{3,2,1,0:T(8,128)(2,1)S(1)}, bf16[2,1,128,384]{3,2,1,0:T(8,128)(2,1)S(1)}, u32[]{:S(2)}, u32[]{:S(2)}) collective-permute-start(bf16[2,1,128,384]{3,2,1,0:T(8,128)(2,1)S(1)} %get-tuple-element.17), channel_id=1, source_target_pairs={{0,1},{1,2},{2,3},{3,4},{4,5},{5,6},{6,7},{8,9},{9,10},{10,11},{11... | collective-permute-start | bytes 589832 | tf_op jit(solution)/shard_map/ppermute | solution.py:15
  16.0 0.7 copy-start.8
  16.3 0.9 copy-start.2
  16.3 2.6 %collective-permute-start.2 = (bf16[2,4,130,384]{3,2,1,0:T(8,128)(2,1)S(1)}, bf16[2,4,130,384]{3,2,1,0:T(8,128)(2,1)}, u32[]{:S(2)}, u32[]{:S(2)}) collective-permute-start(bf16[2,4,130,384]{3,2,1,0:T(8,128)(2,1)S(1)} %fusion.65), channel_id=1, source_target_pairs={{0,8},{8,0},{1,9},{9,1},{2,10},{10,2},{3,11},{11,3},{4,12},{12,4},... | collective-permute-start | bytes 2396168 | tf_op jit(solution)/shard_map/ppermute | solution.py:76
  23.1 3.7 %slice-start = ((s8[7962624]{0:T(1024)(128)(4,1)}), s8[4194304]{0:T(1024)(128)(4,1)S(1)}, s32[]{:S(2)}) async-start(s8[7962624]{0:T(1024)(128)(4,1)} %bitcast.122), calls=%async_computation | async-start | bytes 8388608
  25.3 2.3 %slice-start.1 = ((s8[7962624]{0:T(1024)(128)(4,1)}), s8[3768320]{0:T(1024)(128)(4,1)S(1)}, s32[]{:S(2)}) async-start(s8[7962624]{0:T(1024)(128)(4,1)} %bitcast.122), calls=%async_computation.1 | async-start | bytes 7536640
  26.5 1.0 %copy-start.10 = (pred[8,17]{0,1:T(8,128)(4,1)S(1)}, pred[8,17]{0,1:T(8,128)(4,1)}, u32[]{:S(2)}) copy-start(pred[8,17]{0,1:T(8,128)(4,1)} %constant.108) | copy-start | bytes 412
  30.7 0.7 copy-start.6
  30.7 0.8 copy-start.7
  30.8 4.2 %copy-start.4 = (bf16[384,384]{1,0:T(8,128)(2,1)S(1)}, bf16[384,384]{1,0:T(8,128)(2,1)}, u32[]{:S(2)}) copy-start(bf16[384,384]{1,0:T(8,128)(2,1)} %param.16) | copy-start | bytes 884740
  31.7 7.7 %collective-permute-start.3 = (bf16[1,256,384]{2,1,0:T(8,128)(2,1)S(1)}, bf16[1,256,384]{2,1,0:T(8,128)(2,1)S(1)}, u32[]{:S(2)}, u32[]{:S(2)}) collective-permute-start(bf16[1,256,384]{2,1,0:T(8,128)(2,1)S(1)} %bitcast.110), channel_id=1, source_target_pairs={{0,2},{2,4},{4,6},{6,7},{7,5},{5,3},{3,1},{1,0},{8,10},{10,12},{12... | collective-permute-start | bytes 589832 | tf_op jit(solution)/shard_map/ppermute | solution.py:33
  34.1 14.0 %collective-permute-start.4 = (bf16[1,256,384]{2,1,0:T(8,128)(2,1)S(1)}, bf16[1,256,384]{2,1,0:T(8,128)(2,1)S(1)}, u32[]{:S(2)}, u32[]{:S(2)}) collective-permute-start(bf16[1,256,384]{2,1,0:T(8,128)(2,1)S(1)} %bitcast.112), channel_id=1, source_target_pairs={{0,1},{2,0},{4,2},{6,4},{7,6},{5,7},{3,5},{1,3},{8,9},{10,8},{12,1... | collective-permute-start | bytes 589832 | tf_op jit(solution)/shard_map/ppermute | solution.py:34
  44.4 7.9 %collective-permute-start.11 = (bf16[1,256,384]{2,1,0:T(8,128)(2,1)S(1)}, bf16[1,256,384]{2,1,0:T(8,128)(2,1)S(1)}, u32[]{:S(2)}, u32[]{:S(2)}) collective-permute-start(bf16[1,256,384]{2,1,0:T(8,128)(2,1)S(1)} %bitcast.114), channel_id=1, source_target_pairs={{0,2},{2,4},{4,6},{6,7},{7,5},{5,3},{3,1},{1,0},{8,10},{10,12},{12... | collective-permute-start | bytes 589832 | tf_op jit(solution)/shard_map/ppermute | solution.py:33
  45.4 7.8 %collective-permute-start.12 = (bf16[1,256,384]{2,1,0:T(8,128)(2,1)S(1)}, bf16[1,256,384]{2,1,0:T(8,128)(2,1)S(1)}, u32[]{:S(2)}, u32[]{:S(2)}) collective-permute-start(bf16[1,256,384]{2,1,0:T(8,128)(2,1)S(1)} %bitcast.115), channel_id=1, source_target_pairs={{0,1},{2,0},{4,2},{6,4},{7,6},{5,7},{3,5},{1,3},{8,9},{10,8},{12,1... | collective-permute-start | bytes 589832 | tf_op jit(solution)/shard_map/ppermute | solution.py:34
  46.5 10.0 %collective-permute-start.5 = (bf16[1,256,384]{2,1,0:T(8,128)(2,1)S(1)}, bf16[1,256,384]{2,1,0:T(8,128)(2,1)S(1)}, u32[]{:S(2)}, u32[]{:S(2)}) collective-permute-start(bf16[1,256,384]{2,1,0:T(8,128)(2,1)S(1)} %collective-permute-done.3), channel_id=1, source_target_pairs={{0,2},{2,4},{4,6},{6,7},{7,5},{5,3},{3,1},{1,0},{8,10},{10,12},{12... | collective-permute-start | bytes 589832 | tf_op jit(solution)/shard_map/ppermute | solution.py:33
  48.1 9.4 %collective-permute-start.6 = (bf16[1,256,384]{2,1,0:T(8,128)(2,1)S(1)}, bf16[1,256,384]{2,1,0:T(8,128)(2,1)S(1)}, u32[]{:S(2)}, u32[]{:S(2)}) collective-permute-start(bf16[1,256,384]{2,1,0:T(8,128)(2,1)S(1)} %collective-permute-done.4), channel_id=1, source_target_pairs={{0,1},{2,0},{4,2},{6,4},{7,6},{5,7},{3,5},{1,3},{8,9},{10,8},{12,1... | collective-permute-start | bytes 589832 | tf_op jit(solution)/shard_map/ppermute | solution.py:34
  52.3 13.4 %collective-permute-start.13 = (bf16[1,256,384]{2,1,0:T(8,128)(2,1)S(1)}, bf16[1,256,384]{2,1,0:T(8,128)(2,1)}, u32[]{:S(2)}, u32[]{:S(2)}) collective-permute-start(bf16[1,256,384]{2,1,0:T(8,128)(2,1)S(1)} %collective-permute-done.11), channel_id=1, source_target_pairs={{0,2},{2,4},{4,6},{6,7},{7,5},{5,3},{3,1},{1,0},{8,10},{10,12},{12... | collective-permute-start | bytes 589832 | tf_op jit(solution)/shard_map/ppermute | solution.py:33
  53.2 14.1 %collective-permute-start.14 = (bf16[1,256,384]{2,1,0:T(8,128)(2,1)S(1)}, bf16[1,256,384]{2,1,0:T(8,128)(2,1)}, u32[]{:S(2)}, u32[]{:S(2)}) collective-permute-start(bf16[1,256,384]{2,1,0:T(8,128)(2,1)S(1)} %collective-permute-done.12), channel_id=1, source_target_pairs={{0,1},{2,0},{4,2},{6,4},{7,6},{5,7},{3,5},{1,3},{8,9},{10,8},{12,1... | collective-permute-start | bytes 589832 | tf_op jit(solution)/shard_map/ppermute | solution.py:34
  56.5 7.0 %collective-permute-start.7 = (bf16[1,256,384]{2,1,0:T(8,128)(2,1)S(1)}, bf16[1,256,384]{2,1,0:T(8,128)(2,1)S(1)}, u32[]{:S(2)}, u32[]{:S(2)}) collective-permute-start(bf16[1,256,384]{2,1,0:T(8,128)(2,1)S(1)} %collective-permute-done.5), channel_id=1, source_target_pairs={{0,2},{2,4},{4,6},{6,7},{7,5},{5,3},{3,1},{1,0},{8,10},{10,12},{12... | collective-permute-start | bytes 589832 | tf_op jit(solution)/shard_map/ppermute | solution.py:33
  57.5 6.7 %collective-permute-start.8 = (bf16[1,256,384]{2,1,0:T(8,128)(2,1)S(1)}, bf16[1,256,384]{2,1,0:T(8,128)(2,1)S(1)}, u32[]{:S(2)}, u32[]{:S(2)}) collective-permute-start(bf16[1,256,384]{2,1,0:T(8,128)(2,1)S(1)} %collective-permute-done.6), channel_id=1, source_target_pairs={{0,1},{2,0},{4,2},{6,4},{7,6},{5,7},{3,5},{1,3},{8,9},{10,8},{12,1... | collective-permute-start | bytes 589832 | tf_op jit(solution)/shard_map/ppermute | solution.py:34
  63.5 7.7 %collective-permute-start.9 = (bf16[1,128,384]{2,1,0:T(8,128)(2,1)S(1)}, bf16[1,128,384]{2,1,0:T(8,128)(2,1)S(1)}, u32[]{:S(2)}, u32[]{:S(2)}) collective-permute-start(bf16[1,128,384]{2,1,0:T(8,128)(2,1)S(1)} %slice.76), channel_id=1, source_target_pairs={{0,2},{2,4},{4,6},{6,7},{7,5},{5,3},{3,1},{1,0},{8,10},{10,12},{12... | collective-permute-start | bytes 294920 | tf_op jit(solution)/shard_map/ppermute | solution.py:38
  64.2 7.7 %collective-permute-start.10 = (bf16[1,128,384]{2,1,0:T(8,128)(2,1)S(1)}, bf16[1,128,384]{2,1,0:T(8,128)(2,1)S(1)}, u32[]{:S(2)}, u32[]{:S(2)}) collective-permute-start(bf16[1,128,384]{2,1,0:T(8,128)(2,1)S(1)} %slice.77), channel_id=1, source_target_pairs={{0,1},{2,0},{4,2},{6,4},{7,6},{5,7},{3,5},{1,3},{8,9},{10,8},{12,1... | collective-permute-start | bytes 294920 | tf_op jit(solution)/shard_map/ppermute | solution.py:39
  65.7 13.9 %collective-permute-start.15 = (bf16[1,256,384]{2,1,0:T(8,128)(2,1)}, bf16[1,256,384]{2,1,0:T(8,128)(2,1)}, u32[]{:S(2)}, u32[]{:S(2)}) collective-permute-start(bf16[1,256,384]{2,1,0:T(8,128)(2,1)} %collective-permute-done.13), channel_id=1, source_target_pairs={{0,2},{2,4},{4,6},{6,7},{7,5},{5,3},{3,1},{1,0},{8,10},{10,12},{12... | collective-permute-start | bytes 589832 | tf_op jit(solution)/shard_map/ppermute | solution.py:33
  67.3 13.9 %collective-permute-start.16 = (bf16[1,256,384]{2,1,0:T(8,128)(2,1)}, bf16[1,256,384]{2,1,0:T(8,128)(2,1)}, u32[]{:S(2)}, u32[]{:S(2)}) collective-permute-start(bf16[1,256,384]{2,1,0:T(8,128)(2,1)} %collective-permute-done.14), channel_id=1, source_target_pairs={{0,1},{2,0},{4,2},{6,4},{7,6},{5,7},{3,5},{1,3},{8,9},{10,8},{12,1... | collective-permute-start | bytes 589832 | tf_op jit(solution)/shard_map/ppermute | solution.py:34
  69.8 2.1 %copy-start.5 = (bf16[1,2048,384]{2,1,0:T(8,128)(2,1)}, bf16[1,2048,384]{2,1,0:T(8,128)(2,1)S(1)}, u32[]{:S(2)}) copy-start(bf16[1,2048,384]{2,1,0:T(8,128)(2,1)S(1)} %constant_dynamic-update-slice_fusion.13) | copy-start | bytes 4718596
  76.1 3.2 %copy-start.3 = (bf16[384,384]{1,0:T(8,128)(2,1)S(1)}, bf16[384,384]{1,0:T(8,128)(2,1)}, u32[]{:S(2)}) copy-start(bf16[384,384]{1,0:T(8,128)(2,1)} %param.19) | copy-start | bytes 884740
  80.5 6.5 %collective-permute-start.17 = (bf16[1,128,384]{2,1,0:T(8,128)(2,1)S(1)}, bf16[1,128,384]{2,1,0:T(8,128)(2,1)S(1)}, u32[]{:S(2)}, u32[]{:S(2)}) collective-permute-start(bf16[1,128,384]{2,1,0:T(8,128)(2,1)S(1)} %slice.80), channel_id=1, source_target_pairs={{0,2},{2,4},{4,6},{6,7},{7,5},{5,3},{3,1},{1,0},{8,10},{10,12},{12... | collective-permute-start | bytes 294920 | tf_op jit(solution)/shard_map/ppermute | solution.py:38
  82.0 5.6 %collective-permute-start.18 = (bf16[1,128,384]{2,1,0:T(8,128)(2,1)S(1)}, bf16[1,128,384]{2,1,0:T(8,128)(2,1)S(1)}, u32[]{:S(2)}, u32[]{:S(2)}) collective-permute-start(bf16[1,128,384]{2,1,0:T(8,128)(2,1)S(1)} %slice.81), channel_id=1, source_target_pairs={{0,1},{2,0},{4,2},{6,4},{7,6},{5,7},{3,5},{1,3},{8,9},{10,8},{12,1... | collective-permute-start | bytes 294920 | tf_op jit(solution)/shard_map/ppermute | solution.py:39

commit v16 on v15

--- a/solution.py
+++ b/solution.py
@@ -85,7 +85,7 @@
 
     own = jnp.arange(span_count, dtype=earlier.dtype)
     picks = jnp.stack([slot(earlier[:, 0]), slot(earlier[:, 1]), own], axis=1)
-    window = jnp.take(pool, picks.reshape(-1), axis=0).reshape(
+    window = jnp.take(pool, picks.reshape(-1), axis=0, mode="clip").reshape(
         (span_count, 3) + rimmed.shape[1:]
     )
     score_scale = 1.0 / channels**0.5

time: 96.8 us -> 99.4 us (1.027)
  matrix products: 20.8 us -> 25.9 us
  other arithmetic: 8.4 us -> 6.19 us
    conv_general_dilated x2, matrix products: 6.34 us -> 9.89 us  [shards(): lax.conv_general_dilated(span_window, conv_weight, window_strides=(1, 1,...]
    select_n x2 -> x0, other arithmetic: 2.21 us -> none  [shards(): jnp.take(pool, picks.reshape(-1), axis=0)]
    slice x1, local copies, waits for them, and re-layouts: 0.25 us -> 1.92 us  [shards(): window[span + 1:span + 2]]
    unnamed x44, local copies, waits for them, and re-layouts: 14 us -> 12.9 us
  transfers between devices with their start and end apart: 19 -> 19, of which waited for: 7 -> 8; matrix products, arithmetic and copies ran while one was open for 30% -> 29% of each run, Pallas kernels for 0% -> 0%
where the time goes in v16:
time: 99.4 us; the launch traced here: 98.9 us
  matrix products  25.9 us (26%)
  starting transfers between devices  24.2 us (24%)
  local copies, waits for them, and re-layouts  22.8 us (23%)
  waiting for transfers between devices  19.3 us (19%)
  other arithmetic  6.19 us (6%)
    unnamed x44, local copies, waits for them, and re-layouts  12.9 us
    ppermute x6, waiting for transfers between devices, ring_gather(): forward = lax.ppermute(forward, axis, ahead)  11.3 us
    conv_general_dilated x2, matrix products, shards(): lax.conv_general_dilated(span_window, conv_weight, window_strides=(1, 1,...  9.89 us
    dot_general x2, matrix products, shards(): jnp.einsum('fqk,fkc->fqc', weights_exp.astype(jnp.bfloat16), values_all,...  6.95 us
    ppermute x6, starting transfers between devices, ring_gather(): backward = lax.ppermute(backward, axis, behind)  6.87 us
    dot_general x2, matrix products, shards(): jnp.einsum('fqc,fkc->fqk', queries, keys_all, preferred_element_type=jnp....  6.42 us
    ppermute x6, starting transfers between devices, ring_gather(): forward = lax.ppermute(forward, axis, ahead)  5.99 us
    ppermute x1, starting transfers between devices, padded_2(): lax.ppermute(tail, axis, [(i, (i + 1) % count) for i in range(ends)])  5.52 us
  transfers between devices with their start and end apart: 19, of which 8 were waited for; matrix products, arithmetic and copies ran while one was open for 29% of the time, Pallas kernels for 0%

profile of v16, /device:TPU:0, one launch (start us, length us, event | category | flops | bytes accessed | tf_op | source)
XLA Modules:
  0.0 98.9 jit_solution(13712857574899168710)
XLA Ops:
  0.0 1.1 %fusion.113 = (bf16[2,1,128,384]{3,2,1,0:T(8,128)(2,1)S(1)}, bf16[2,1,128,384]{3,2,1,0:T(8,128)(2,1)S(1)}) fusion(bf16[2,2,128,384]{3,2,1,0:T(8,128)(2,1)} %param.10), kind=kLoop, calls=%fused_computation.160 | loop fusion | bytes 786432 | tf_op jit(solution)/shard_map/slice | solution.py:12
  1.1 1.3 %collective-permute-start.1 = (bf16[2,1,128,384]{3,2,1,0:T(8,128)(2,1)S(1)}, bf16[2,1,128,384]{3,2,1,0:T(8,128)(2,1)S(1)}, u32[]{:S(2)}, u32[]{:S(2)}) collective-permute-start(bf16[2,1,128,384]{3,2,1,0:T(8,128)(2,1)S(1)} %get-tuple-element.18), channel_id=1, source_target_pairs={{1,0},{2,1},{3,2},{4,3},{5,4},{6,5},{7,6},{9,8},{10,9},{11,10},{12... | collective-permute-start | bytes 589832 | tf_op jit(solution)/shard_map/ppermute | solution.py:17
  2.4 5.5 %collective-permute-start = (bf16[2,1,128,384]{3,2,1,0:T(8,128)(2,1)S(1)}, bf16[2,1,128,384]{3,2,1,0:T(8,128)(2,1)S(1)}, u32[]{:S(2)}, u32[]{:S(2)}) collective-permute-start(bf16[2,1,128,384]{3,2,1,0:T(8,128)(2,1)S(1)} %get-tuple-element.17), channel_id=1, source_target_pairs={{0,1},{1,2},{2,3},{3,4},{4,5},{5,6},{6,7},{8,9},{9,10},{10,11},{11... | collective-permute-start | bytes 589832 | tf_op jit(solution)/shard_map/ppermute | solution.py:15
  8.0 1.1 %fusion.74 = f32[2,2,128]{2,1,0:T(2,128)S(1)} fusion(bf16[2,2,128,384]{3,2,1,0:T(8,128)(2,1)} %param.10), kind=kLoop, calls=%fused_computation.73 | loop fusion | flops 589312 | bytes 395264 | tf_op jit(solution)/shard_map/reduce_sum | solution.py:48
  9.1 1.8 %collective-permute-done.1 = bf16[2,1,128,384]{3,2,1,0:T(8,128)(2,1)S(1)} collective-permute-done((bf16[2,1,128,384]{3,2,1,0:T(8,128)(2,1)S(1)}, bf16[2,1,128,384]{3,2,1,0:T(8,128)(2,1)S(1)}, u32[]{:S(2)}, u32[]{:S(2)}) %collective-permute-start.1) | collective-permute-done | bytes 196640 | tf_op jit(solution)/shard_map/ppermute | solution.py:17
  10.9 4.4 %collective-permute-done = bf16[2,1,128,384]{3,2,1,0:T(8,128)(2,1)S(1)} collective-permute-done((bf16[2,1,128,384]{3,2,1,0:T(8,128)(2,1)S(1)}, bf16[2,1,128,384]{3,2,1,0:T(8,128)(2,1)S(1)}, u32[]{:S(2)}, u32[]{:S(2)}) %collective-permute-start) | collective-permute-done | bytes 196640 | tf_op jit(solution)/shard_map/ppermute | solution.py:15
  15.5 0.5 fusion.81
  17.2 1.6 %collective-permute-done.2 = bf16[2,4,130,384]{3,2,1,0:T(8,128)(2,1)} collective-permute-done((bf16[2,4,130,384]{3,2,1,0:T(8,128)(2,1)S(1)}, bf16[2,4,130,384]{3,2,1,0:T(8,128)(2,1)}, u32[]{:S(2)}, u32[]{:S(2)}) %collective-permute-start.2) | collective-permute-done | bytes 798752 | tf_op jit(solution)/shard_map/ppermute | solution.py:76
  18.9 1.7 %maximum_maximum_fusion = bf16[5,4,130,384]{3,2,1,0:T(8,128)(2,1)S(1)} fusion(bf16[2,4,130,384]{3,2,1,0:T(8,128)(2,1)} %collective-permute-done.2, bf16[2,4,130,384]{3,2,1,0:T(8,128)(2,1)} %copy-done.2, bf16[5]{0:T(256)(128)(2,1)S(1)} %pad.20.clone), kind=kLoop, calls=%fused_computation.14 | loop fusion | flops 1996800 | bytes 3594250 | tf_op jit(solution)/shard_map/concatenate | solution.py:79
  20.6 2.5 %gather_fusion = bf16[6,4,130,384]{3,2,1,0:T(8,128)(2,1)} fusion(bf16[5,4,130,384]{3,2,1,0:T(8,128)(2,1)S(1)} %maximum_maximum_fusion, s32[1024]{0:T(1024)S(1)} %pad_clamp_fusion), kind=kCustom, calls=%fused_computation | custom fusion | bytes 4792344 | tf_op jit(solution)/shard_map/jit(_take)/gather | solution.py:88
  23.1 1.9 %slice_bitcast_fusion = (bf16[1,3,4,130,384]{4,3,2,1,0:T(8,128)(2,1)S(1)}, bf16[3,4,1,130,384]{4,3,1,0,2:T(8,128)(2,1)S(1)}) fusion(bf16[6,4,130,384]{3,2,1,0:T(8,128)(2,1)} %gather_fusion), kind=kLoop, calls=%fused_computation.38 | loop fusion | bytes 4792320 | tf_op jit(solution)/shard_map/slice | solution.py:114
  25.0 0.5 copy.23
  25.5 0.5 pad.5.clone
  26.2 0.4 copy-done.10
  26.7 6.7 %fusion.38 = f32[1,2,8,17,384]{4,2,3,1,0:T(8,128)S(1)} fusion(bf16[3,3,3,384,384]{4,3,2,1,0:T(8,128)(2,1)} %param.13, bf16[3,4,1,7,2,384]{5,3,4,1,0,2:T(8,128)(2,1)S(1)} %slice.73, bf16[3,4,1,8,17,384]{5,3,4,1,0,2:T(8,128)(2,1)S(1)} %copy.13, pred[8,17]{0,1:T(8,128)(4,1)S(1)} %copy-done.10), kind=kOutput, calls=%fused_computation.43 | convolution fusion | flops 2170140672 | bytes 9762952 | tf_op jit(solution)/shard_map/conv_general_dilated | solution.py:95
  33.7 0.3 copy-done.6
  34.4 1.7 %collective-permute-start.3 = (bf16[1,256,384]{2,1,0:T(8,128)(2,1)S(1)}, bf16[1,256,384]{2,1,0:T(8,128)(2,1)S(1)}, u32[]{:S(2)}, u32[]{:S(2)}) collective-permute-start(bf16[1,256,384]{2,1,0:T(8,128)(2,1)S(1)} %bitcast.108), channel_id=1, source_target_pairs={{0,2},{2,4},{4,6},{6,7},{7,5},{5,3},{3,1},{1,0},{8,10},{10,12},{12... | collective-permute-start | bytes 589832 | tf_op jit(solution)/shard_map/ppermute | solution.py:33
  36.1 0.7 constant_dynamic-update-slice_fusion.8
  36.8 0.9 collective-permute-start.4
  37.9 4.2 %collective-permute-done.3 = bf16[1,256,384]{2,1,0:T(8,128)(2,1)S(1)} collective-permute-done((bf16[1,256,384]{2,1,0:T(8,128)(2,1)S(1)}, bf16[1,256,384]{2,1,0:T(8,128)(2,1)S(1)}, u32[]{:S(2)}, u32[]{:S(2)}) %collective-permute-start.3) | collective-permute-done | bytes 196640 | tf_op jit(solution)/shard_map/ppermute | solution.py:33
  42.1 0.5 copy.24
  42.6 0.5 pad.7.clone
  43.3 3.2 %fusion.35 = f32[1,2,8,17,384]{4,2,3,1,0:T(8,128)S(1)} fusion(bf16[3,3,3,384,384]{4,3,2,1,0:T(8,128)(2,1)S(1)} %bitcast.121, bf16[3,4,1,7,2,384]{5,3,4,1,0,2:T(8,128)(2,1)S(1)} %slice.78, bf16[3,4,1,8,17,384]{5,3,4,1,0,2:T(8,128)(2,1)S(1)} %copy.18, pred[8,17]{0,1:T(8,128)(4,1)S(1)} %copy-done.10), kind=kOutput, calls=%fused_computation.42 | convolution fusion | flops 2170140672 | bytes 9762952 | tf_op jit(solution)/shard_map/conv_general_dilated | solution.py:95
  47.1 1.0 collective-permute-start.11
  48.0 1.1 %collective-permute-start.12 = (bf16[1,256,384]{2,1,0:T(8,128)(2,1)S(1)}, bf16[1,256,384]{2,1,0:T(8,128)(2,1)S(1)}, u32[]{:S(2)}, u32[]{:S(2)}) collective-permute-start(bf16[1,256,384]{2,1,0:T(8,128)(2,1)S(1)} %bitcast.113), channel_id=1, source_target_pairs={{0,1},{2,0},{4,2},{6,4},{7,6},{5,7},{3,5},{1,3},{8,9},{10,8},{12,1... | collective-permute-start | bytes 589832 | tf_op jit(solution)/shard_map/ppermute | solution.py:34
  49.2 0.9 collective-permute-start.5
  50.1 0.7 constant_dynamic-update-slice_fusion.7
  50.8 1.1 %collective-permute-start.6 = (bf16[1,256,384]{2,1,0:T(8,128)(2,1)S(1)}, bf16[1,256,384]{2,1,0:T(8,128)(2,1)S(1)}, u32[]{:S(2)}, u32[]{:S(2)}) collective-permute-start(bf16[1,256,384]{2,1,0:T(8,128)(2,1)S(1)} %collective-permute-done.4), channel_id=1, source_target_pairs={{0,1},{2,0},{4,2},{6,4},{7,6},{5,7},{3,5},{1,3},{8,9},{10,8},{12,1... | collective-permute-start | bytes 589832 | tf_op jit(solution)/shard_map/ppermute | solution.py:34
  51.9 0.7 constant_dynamic-update-slice_fusion.6
  52.6 1.0 convolution_convert_fusion.4
  53.6 1.4 %collective-permute-done.11 = bf16[1,256,384]{2,1,0:T(8,128)(2,1)S(1)} collective-permute-done((bf16[1,256,384]{2,1,0:T(8,128)(2,1)S(1)}, bf16[1,256,384]{2,1,0:T(8,128)(2,1)S(1)}, u32[]{:S(2)}, u32[]{:S(2)}) %collective-permute-start.11) | collective-permute-done | bytes 196640 | tf_op jit(solution)/shard_map/ppermute | solution.py:33
  55.0 0.9 collective-permute-start.13
  55.9 1.1 %collective-permute-start.14 = (bf16[1,256,384]{2,1,0:T(8,128)(2,1)S(1)}, bf16[1,256,384]{2,1,0:T(8,128)(2,1)}, u32[]{:S(2)}, u32[]{:S(2)}) collective-permute-start(bf16[1,256,384]{2,1,0:T(8,128)(2,1)S(1)} %collective-permute-done.12), channel_id=1, source_target_pairs={{0,1},{2,0},{4,2},{6,4},{7,6},{5,7},{3,5},{1,3},{8,9},{10,8},{12,1... | collective-permute-start | bytes 589832 | tf_op jit(solution)/shard_map/ppermute | solution.py:34
  57.0 2.2 %collective-permute-done.5 = bf16[1,256,384]{2,1,0:T(8,128)(2,1)S(1)} collective-permute-done((bf16[1,256,384]{2,1,0:T(8,128)(2,1)S(1)}, bf16[1,256,384]{2,1,0:T(8,128)(2,1)S(1)}, u32[]{:S(2)}, u32[]{:S(2)}) %collective-permute-start.5) | collective-permute-done | bytes 196640 | tf_op jit(solution)/shard_map/ppermute | solution.py:33
  59.2 0.9 collective-permute-start.7
  60.2 1.2 %collective-permute-start.8 = (bf16[1,256,384]{2,1,0:T(8,128)(2,1)S(1)}, bf16[1,256,384]{2,1,0:T(8,128)(2,1)S(1)}, u32[]{:S(2)}, u32[]{:S(2)}) collective-permute-start(bf16[1,256,384]{2,1,0:T(8,128)(2,1)S(1)} %collective-permute-done.6), channel_id=1, source_target_pairs={{0,1},{2,0},{4,2},{6,4},{7,6},{5,7},{3,5},{1,3},{8,9},{10,8},{12,1... | collective-permute-start | bytes 589832 | tf_op jit(solution)/shard_map/ppermute | solution.py:34
  61.3 0.7 constant_dynamic-update-slice_fusion.5
  62.0 0.7 constant_dynamic-update-slice_fusion.4
  62.7 3.5 %collective-permute-done.7 = bf16[1,256,384]{2,1,0:T(8,128)(2,1)S(1)} collective-permute-done((bf16[1,256,384]{2,1,0:T(8,128)(2,1)S(1)}, bf16[1,256,384]{2,1,0:T(8,128)(2,1)S(1)}, u32[]{:S(2)}, u32[]{:S(2)}) %collective-permute-start.7) | collective-permute-done | bytes 196640 | tf_op jit(solution)/shard_map/ppermute | solution.py:33
  66.2 0.6 collective-permute-start.9
  66.9 1.5 %collective-permute-start.10 = (bf16[1,128,384]{2,1,0:T(8,128)(2,1)S(1)}, bf16[1,128,384]{2,1,0:T(8,128)(2,1)S(1)}, u32[]{:S(2)}, u32[]{:S(2)}) collective-permute-start(bf16[1,128,384]{2,1,0:T(8,128)(2,1)S(1)} %slice.77), channel_id=1, source_target_pairs={{0,1},{2,0},{4,2},{6,4},{7,6},{5,7},{3,5},{1,3},{8,9},{10,8},{12,1... | collective-permute-start | bytes 294920 | tf_op jit(solution)/shard_map/ppermute | solution.py:39
  68.4 0.6 collective-permute-start.15
  69.0 1.0 %constant_dynamic-update-slice_fusion.14 = bf16[1,2048,384]{2,1,0:T(8,128)(2,1)S(1)} fusion(bf16[1,2048,384]{2,1,0:T(8,128)(2,1)S(1)} %constant_dynamic-update-slice_fusion.15, bf16[1,256,384]{2,1,0:T(8,128)(2,1)} %collective-permute-done.13), kind=kLoop, calls=%fused_computation.119 | loop fusion | bytes 393216
  70.0 1.5 %collective-permute-start.16 = (bf16[1,256,384]{2,1,0:T(8,128)(2,1)}, bf16[1,256,384]{2,1,0:T(8,128)(2,1)}, u32[]{:S(2)}, u32[]{:S(2)}) collective-permute-start(bf16[1,256,384]{2,1,0:T(8,128)(2,1)} %collective-permute-done.14), channel_id=1, source_target_pairs={{0,1},{2,0},{4,2},{6,4},{7,6},{5,7},{3,5},{1,3},{8,9},{10,8},{12,1... | collective-permute-start | bytes 589832 | tf_op jit(solution)/shard_map/ppermute | solution.py:34
  71.5 1.0 %constant_dynamic-update-slice_fusion.13 = bf16[1,2048,384]{2,1,0:T(8,128)(2,1)S(1)} fusion(bf16[1,2048,384]{2,1,0:T(8,128)(2,1)S(1)} %constant_dynamic-update-slice_fusion.14, bf16[1,256,384]{2,1,0:T(8,128)(2,1)} %collective-permute-done.14), kind=kLoop, calls=%fused_computation.118 | loop fusion | bytes 393216
  72.5 0.8 constant_dynamic-update-slice_fusion.3
  73.2 0.7 constant_dynamic-update-slice_fusion.2
  73.9 0.6 constant_dynamic-update-slice_fusion.1
  74.6 0.6 constant_dynamic-update-slice_fusion
  75.2 3.2 %fusion.117 = (f32[256]{0:T(256)S(1)}, f32[256,2048]{1,0:T(8,128)S(1)}) fusion(bf16[256,384]{1,0:T(8,128)(2,1)S(1)} %convolution_convert_fusion.5, bf16[384,384]{1,0:T(8,128)(2,1)S(1)} %copy-done, bf16[1,2048,384]{2,1,0:T(8,128)(2,1)} %constant_dynamic-update-slice_fusion), kind=kOutput, calls=%fused_computation.162 | convolution fusion | flops 1008467712 | bytes 4162560 | tf_op jit(solution)/shard_map/fqc,fkc->fqk/dot_general | solution.py:124
  78.4 0.4 fusion.2
  78.8 3.8 %fusion.54 = bf16[256,384]{1,0:T(8,128)(2,1)} fusion(bf16[384,384]{1,0:T(8,128)(2,1)} %param.18, bf16[1,2048,384]{2,1,0:T(8,128)(2,1)} %constant_dynamic-update-slice_fusion, f32[256,2048]{1,0:T(8,128)S(1)} %get-tuple-element.26, f32[256]{0:T(256)S(1)} %get-tuple-element.25, f32[256]{0:T(256)S(1)} %fusion.2), kind=kOutput, calls=%fused_computation.53 | convolution fusion | flops 1008664576 | bytes 4163584 | tf_op jit(solution)/shard_map/fqk,fkc->fqc/dot_general | solution.py:130
  82.7 1.2 %fusion.44 = bf16[1,2,128,384]{3,2,1,0:T(8,128)(2,1)S(1)} fusion(bf16[2,128,384]{2,1,0:T(8,128)(2,1)} %bitcast.118, bf16[1,2,128,384]{3,2,1,0:T(8,128)(2,1)S(1)} %get-tuple-element.12, bf16[384,384]{1,0:T(8,128)(2,1)S(1)} %copy-done.3), kind=kOutput, calls=%fused_computation.49 | convolution fusion | flops 75792384 | bytes 884736 | tf_op jit(solution)/shard_map/ftc,cd->ftd/dot_general | solution.py:137
  83.9 0.6 collective-permute-start.17
  84.5 0.9 slice.81
  85.4 1.7 %collective-permute-start.18 = (bf16[1,128,384]{2,1,0:T(8,128)(2,1)S(1)}, bf16[1,128,384]{2,1,0:T(8,128)(2,1)S(1)}, u32[]{:S(2)}, u32[]{:S(2)}) collective-permute-start(bf16[1,128,384]{2,1,0:T(8,128)(2,1)S(1)} %slice.81), channel_id=1, source_target_pairs={{0,1},{2,0},{4,2},{6,4},{7,6},{5,7},{3,5},{1,3},{8,9},{10,8},{12,1... | collective-permute-start | bytes 294920 | tf_op jit(solution)/shard_map/ppermute | solution.py:39
  87.2 0.7 constant_dynamic-update-slice_fusion.12
  87.9 1.6 %constant_dynamic-update-slice_fusion.11 = bf16[1,2048,384]{2,1,0:T(8,128)(2,1)} fusion(bf16[1,2048,384]{2,1,0:T(8,128)(2,1)} %constant_dynamic-update-slice_fusion.12, bf16[1,256,384]{2,1,0:T(8,128)(2,1)} %collective-permute-done.16), kind=kLoop, calls=%fused_computation.116 | loop fusion | bytes 393216
  89.5 0.6 constant_dynamic-update-slice_fusion.10
  90.3 0.7 constant_dynamic-update-slice_fusion.9
  91.0 3.3 %fusion.114 = (f32[256]{0:T(256)S(1)}, f32[256,2048]{1,0:T(8,128)S(1)}) fusion(bf16[256,384]{1,0:T(8,128)(2,1)} %convolution_convert_fusion.4, bf16[384,384]{1,0:T(8,128)(2,1)S(1)} %copy-done, bf16[1,2048,384]{2,1,0:T(8,128)(2,1)} %constant_dynamic-update-slice_fusion.9), kind=kOutput, calls=%fused_computation.161 | convolution fusion | flops 1008467712 | bytes 4162560 | tf_op jit(solution)/shard_map/fqc,fkc->fqk/dot_general | solution.py:124
  94.2 0.4 fusion.4
  94.7 3.1 %fusion.48 = bf16[256,384]{1,0:T(8,128)(2,1)S(1)} fusion(bf16[384,384]{1,0:T(8,128)(2,1)} %param.18, bf16[1,2048,384]{2,1,0:T(8,128)(2,1)} %constant_dynamic-update-slice_fusion.9, f32[256,2048]{1,0:T(8,128)S(1)} %get-tuple-element.24, f32[256]{0:T(256)S(1)} %get-tuple-element.23, f32[256]{0:T(256)S(1)} %fusion.4), kind=kOutput, calls=%fused_computation.51 | convolution fusion | flops 1008664576 | bytes 4163584 | tf_op jit(solution)/shard_map/fqk,fkc->fqc/dot_general | solution.py:130
  98.1 0.8 pad_maximum_fusion.1
  (71 shorter events, 3.9 us)
Async XLA Ops:
  0.0 75.2 %copy-start = (bf16[384,384]{1,0:T(8,128)(2,1)S(1)}, bf16[384,384]{1,0:T(8,128)(2,1)}, u32[]{:S(2)}) copy-start(bf16[384,384]{1,0:T(8,128)(2,1)} %param.17) | copy-start | bytes 884740
  0.0 15.4 %copy-start.1 = (bf16[2,2,128,384]{3,2,1,0:T(8,128)(2,1)S(1)}, bf16[2,2,128,384]{3,2,1,0:T(8,128)(2,1)}, u32[]{:S(2)}) copy-start(bf16[2,2,128,384]{3,2,1,0:T(8,128)(2,1)} %param.10) | copy-start | bytes 1179652
  0.0 15.5 %copy-start.9 = (f32[384]{0:T(512)S(1)}, f32[384]{0:T(512)}, u32[]{:S(2)}) copy-start(f32[384]{0:T(512)} %param.12) | copy-start | bytes 4612
  1.1 9.8 %collective-permute-start.1 = (bf16[2,1,128,384]{3,2,1,0:T(8,128)(2,1)S(1)}, bf16[2,1,128,384]{3,2,1,0:T(8,128)(2,1)S(1)}, u32[]{:S(2)}, u32[]{:S(2)}) collective-permute-start(bf16[2,1,128,384]{3,2,1,0:T(8,128)(2,1)S(1)} %get-tuple-element.18), channel_id=1, source_target_pairs={{1,0},{2,1},{3,2},{4,3},{5,4},{6,5},{7,6},{9,8},{10,9},{11,10},{12... | collective-permute-start | bytes 589832 | tf_op jit(solution)/shard_map/ppermute | solution.py:17
  2.4 12.8 %collective-permute-start = (bf16[2,1,128,384]{3,2,1,0:T(8,128)(2,1)S(1)}, bf16[2,1,128,384]{3,2,1,0:T(8,128)(2,1)S(1)}, u32[]{:S(2)}, u32[]{:S(2)}) collective-permute-start(bf16[2,1,128,384]{3,2,1,0:T(8,128)(2,1)S(1)} %get-tuple-element.17), channel_id=1, source_target_pairs={{0,1},{1,2},{2,3},{3,4},{4,5},{5,6},{6,7},{8,9},{9,10},{10,11},{11... | collective-permute-start | bytes 589832 | tf_op jit(solution)/shard_map/ppermute | solution.py:15
  16.0 0.7 copy-start.8
  16.3 0.9 copy-start.2
  16.3 2.6 %collective-permute-start.2 = (bf16[2,4,130,384]{3,2,1,0:T(8,128)(2,1)S(1)}, bf16[2,4,130,384]{3,2,1,0:T(8,128)(2,1)}, u32[]{:S(2)}, u32[]{:S(2)}) collective-permute-start(bf16[2,4,130,384]{3,2,1,0:T(8,128)(2,1)S(1)} %fusion.65), channel_id=1, source_target_pairs={{0,8},{8,0},{1,9},{9,1},{2,10},{10,2},{3,11},{11,3},{4,12},{12,4},... | collective-permute-start | bytes 2396168 | tf_op jit(solution)/shard_map/ppermute | solution.py:76
  26.0 0.7 copy-start.10
  26.0 17.3 %slice-start = ((s8[7962624]{0:T(1024)(128)(4,1)}), s8[4194304]{0:T(1024)(128)(4,1)S(1)}, s32[]{:S(2)}) async-start(s8[7962624]{0:T(1024)(128)(4,1)} %bitcast.120), calls=%async_computation | async-start | bytes 8388608
  26.7 16.6 %slice-start.1 = ((s8[7962624]{0:T(1024)(128)(4,1)}), s8[3768320]{0:T(1024)(128)(4,1)S(1)}, s32[]{:S(2)}) async-start(s8[7962624]{0:T(1024)(128)(4,1)} %bitcast.120), calls=%async_computation.1 | async-start | bytes 7536640
  33.4 0.7 copy-start.6
  33.4 0.8 copy-start.7
  33.4 4.2 %copy-start.4 = (bf16[384,384]{1,0:T(8,128)(2,1)S(1)}, bf16[384,384]{1,0:T(8,128)(2,1)}, u32[]{:S(2)}) copy-start(bf16[384,384]{1,0:T(8,128)(2,1)} %param.16) | copy-start | bytes 884740
  34.4 7.7 %collective-permute-start.3 = (bf16[1,256,384]{2,1,0:T(8,128)(2,1)S(1)}, bf16[1,256,384]{2,1,0:T(8,128)(2,1)S(1)}, u32[]{:S(2)}, u32[]{:S(2)}) collective-permute-start(bf16[1,256,384]{2,1,0:T(8,128)(2,1)S(1)} %bitcast.108), channel_id=1, source_target_pairs={{0,2},{2,4},{4,6},{6,7},{7,5},{5,3},{3,1},{1,0},{8,10},{10,12},{12... | collective-permute-start | bytes 589832 | tf_op jit(solution)/shard_map/ppermute | solution.py:33
  36.8 14.0 %collective-permute-start.4 = (bf16[1,256,384]{2,1,0:T(8,128)(2,1)S(1)}, bf16[1,256,384]{2,1,0:T(8,128)(2,1)S(1)}, u32[]{:S(2)}, u32[]{:S(2)}) collective-permute-start(bf16[1,256,384]{2,1,0:T(8,128)(2,1)S(1)} %bitcast.110), channel_id=1, source_target_pairs={{0,1},{2,0},{4,2},{6,4},{7,6},{5,7},{3,5},{1,3},{8,9},{10,8},{12,1... | collective-permute-start | bytes 589832 | tf_op jit(solution)/shard_map/ppermute | solution.py:34
  47.1 7.9 %collective-permute-start.11 = (bf16[1,256,384]{2,1,0:T(8,128)(2,1)S(1)}, bf16[1,256,384]{2,1,0:T(8,128)(2,1)S(1)}, u32[]{:S(2)}, u32[]{:S(2)}) collective-permute-start(bf16[1,256,384]{2,1,0:T(8,128)(2,1)S(1)} %bitcast.112), channel_id=1, source_target_pairs={{0,2},{2,4},{4,6},{6,7},{7,5},{5,3},{3,1},{1,0},{8,10},{10,12},{12... | collective-permute-start | bytes 589832 | tf_op jit(solution)/shard_map/ppermute | solution.py:33
  48.0 7.8 %collective-permute-start.12 = (bf16[1,256,384]{2,1,0:T(8,128)(2,1)S(1)}, bf16[1,256,384]{2,1,0:T(8,128)(2,1)S(1)}, u32[]{:S(2)}, u32[]{:S(2)}) collective-permute-start(bf16[1,256,384]{2,1,0:T(8,128)(2,1)S(1)} %bitcast.113), channel_id=1, source_target_pairs={{0,1},{2,0},{4,2},{6,4},{7,6},{5,7},{3,5},{1,3},{8,9},{10,8},{12,1... | collective-permute-start | bytes 589832 | tf_op jit(solution)/shard_map/ppermute | solution.py:34
  49.2 10.0 %collective-permute-start.5 = (bf16[1,256,384]{2,1,0:T(8,128)(2,1)S(1)}, bf16[1,256,384]{2,1,0:T(8,128)(2,1)S(1)}, u32[]{:S(2)}, u32[]{:S(2)}) collective-permute-start(bf16[1,256,384]{2,1,0:T(8,128)(2,1)S(1)} %collective-permute-done.3), channel_id=1, source_target_pairs={{0,2},{2,4},{4,6},{6,7},{7,5},{5,3},{3,1},{1,0},{8,10},{10,12},{12... | collective-permute-start | bytes 589832 | tf_op jit(solution)/shard_map/ppermute | solution.py:33
  50.8 9.4 %collective-permute-start.6 = (bf16[1,256,384]{2,1,0:T(8,128)(2,1)S(1)}, bf16[1,256,384]{2,1,0:T(8,128)(2,1)S(1)}, u32[]{:S(2)}, u32[]{:S(2)}) collective-permute-start(bf16[1,256,384]{2,1,0:T(8,128)(2,1)S(1)} %collective-permute-done.4), channel_id=1, source_target_pairs={{0,1},{2,0},{4,2},{6,4},{7,6},{5,7},{3,5},{1,3},{8,9},{10,8},{12,1... | collective-permute-start | bytes 589832 | tf_op jit(solution)/shard_map/ppermute | solution.py:34
  55.0 13.4 %collective-permute-start.13 = (bf16[1,256,384]{2,1,0:T(8,128)(2,1)S(1)}, bf16[1,256,384]{2,1,0:T(8,128)(2,1)}, u32[]{:S(2)}, u32[]{:S(2)}) collective-permute-start(bf16[1,256,384]{2,1,0:T(8,128)(2,1)S(1)} %collective-permute-done.11), channel_id=1, source_target_pairs={{0,2},{2,4},{4,6},{6,7},{7,5},{5,3},{3,1},{1,0},{8,10},{10,12},{12... | collective-permute-start | bytes 589832 | tf_op jit(solution)/shard_map/ppermute | solution.py:33
  55.9 14.1 %collective-permute-start.14 = (bf16[1,256,384]{2,1,0:T(8,128)(2,1)S(1)}, bf16[1,256,384]{2,1,0:T(8,128)(2,1)}, u32[]{:S(2)}, u32[]{:S(2)}) collective-permute-start(bf16[1,256,384]{2,1,0:T(8,128)(2,1)S(1)} %collective-permute-done.12), channel_id=1, source_target_pairs={{0,1},{2,0},{4,2},{6,4},{7,6},{5,7},{3,5},{1,3},{8,9},{10,8},{12,1... | collective-permute-start | bytes 589832 | tf_op jit(solution)/shard_map/ppermute | solution.py:34
  59.2 7.0 %collective-permute-start.7 = (bf16[1,256,384]{2,1,0:T(8,128)(2,1)S(1)}, bf16[1,256,384]{2,1,0:T(8,128)(2,1)S(1)}, u32[]{:S(2)}, u32[]{:S(2)}) collective-permute-start(bf16[1,256,384]{2,1,0:T(8,128)(2,1)S(1)} %collective-permute-done.5), channel_id=1, source_target_pairs={{0,2},{2,4},{4,6},{6,7},{7,5},{5,3},{3,1},{1,0},{8,10},{10,12},{12... | collective-permute-start | bytes 589832 | tf_op jit(solution)/shard_map/ppermute | solution.py:33
  60.2 6.7 %collective-permute-start.8 = (bf16[1,256,384]{2,1,0:T(8,128)(2,1)S(1)}, bf16[1,256,384]{2,1,0:T(8,128)(2,1)S(1)}, u32[]{:S(2)}, u32[]{:S(2)}) collective-permute-start(bf16[1,256,384]{2,1,0:T(8,128)(2,1)S(1)} %collective-permute-done.6), channel_id=1, source_target_pairs={{0,1},{2,0},{4,2},{6,4},{7,6},{5,7},{3,5},{1,3},{8,9},{10,8},{12,1... | collective-permute-start | bytes 589832 | tf_op jit(solution)/shard_map/ppermute | solution.py:34
  66.2 7.7 %collective-permute-start.9 = (bf16[1,128,384]{2,1,0:T(8,128)(2,1)S(1)}, bf16[1,128,384]{2,1,0:T(8,128)(2,1)S(1)}, u32[]{:S(2)}, u32[]{:S(2)}) collective-permute-start(bf16[1,128,384]{2,1,0:T(8,128)(2,1)S(1)} %slice.76), channel_id=1, source_target_pairs={{0,2},{2,4},{4,6},{6,7},{7,5},{5,3},{3,1},{1,0},{8,10},{10,12},{12... | collective-permute-start | bytes 294920 | tf_op jit(solution)/shard_map/ppermute | solution.py:38
  66.9 7.7 %collective-permute-start.10 = (bf16[1,128,384]{2,1,0:T(8,128)(2,1)S(1)}, bf16[1,128,384]{2,1,0:T(8,128)(2,1)S(1)}, u32[]{:S(2)}, u32[]{:S(2)}) collective-permute-start(bf16[1,128,384]{2,1,0:T(8,128)(2,1)S(1)} %slice.77), channel_id=1, source_target_pairs={{0,1},{2,0},{4,2},{6,4},{7,6},{5,7},{3,5},{1,3},{8,9},{10,8},{12,1... | collective-permute-start | bytes 294920 | tf_op jit(solution)/shard_map/ppermute | solution.py:39
  68.4 15.5 %collective-permute-start.15 = (bf16[1,256,384]{2,1,0:T(8,128)(2,1)}, bf16[1,256,384]{2,1,0:T(8,128)(2,1)S(1)}, u32[]{:S(2)}, u32[]{:S(2)}) collective-permute-start(bf16[1,256,384]{2,1,0:T(8,128)(2,1)} %collective-permute-done.13), channel_id=1, source_target_pairs={{0,2},{2,4},{4,6},{6,7},{7,5},{5,3},{3,1},{1,0},{8,10},{10,12},{12... | collective-permute-start | bytes 589832 | tf_op jit(solution)/shard_map/ppermute | solution.py:33
  70.0 14.6 %collective-permute-start.16 = (bf16[1,256,384]{2,1,0:T(8,128)(2,1)}, bf16[1,256,384]{2,1,0:T(8,128)(2,1)}, u32[]{:S(2)}, u32[]{:S(2)}) collective-permute-start(bf16[1,256,384]{2,1,0:T(8,128)(2,1)} %collective-permute-done.14), channel_id=1, source_target_pairs={{0,1},{2,0},{4,2},{6,4},{7,6},{5,7},{3,5},{1,3},{8,9},{10,8},{12,1... | collective-permute-start | bytes 589832 | tf_op jit(solution)/shard_map/ppermute | solution.py:34
  72.5 2.1 %copy-start.5 = (bf16[1,2048,384]{2,1,0:T(8,128)(2,1)}, bf16[1,2048,384]{2,1,0:T(8,128)(2,1)S(1)}, u32[]{:S(2)}) copy-start(bf16[1,2048,384]{2,1,0:T(8,128)(2,1)S(1)} %constant_dynamic-update-slice_fusion.13) | copy-start | bytes 4718596
  78.8 3.8 %copy-start.3 = (bf16[384,384]{1,0:T(8,128)(2,1)S(1)}, bf16[384,384]{1,0:T(8,128)(2,1)}, u32[]{:S(2)}) copy-start(bf16[384,384]{1,0:T(8,128)(2,1)} %param.19) | copy-start | bytes 884740
  83.9 5.6 %collective-permute-start.17 = (bf16[1,128,384]{2,1,0:T(8,128)(2,1)S(1)}, bf16[1,128,384]{2,1,0:T(8,128)(2,1)S(1)}, u32[]{:S(2)}, u32[]{:S(2)}) collective-permute-start(bf16[1,128,384]{2,1,0:T(8,128)(2,1)S(1)} %slice.80), channel_id=1, source_target_pairs={{0,2},{2,4},{4,6},{6,7},{7,5},{5,3},{3,1},{1,0},{8,10},{10,12},{12... | collective-permute-start | bytes 294920 | tf_op jit(solution)/shard_map/ppermute | solution.py:38
  85.4 4.9 %collective-permute-start.18 = (bf16[1,128,384]{2,1,0:T(8,128)(2,1)S(1)}, bf16[1,128,384]{2,1,0:T(8,128)(2,1)S(1)}, u32[]{:S(2)}, u32[]{:S(2)}) collective-permute-start(bf16[1,128,384]{2,1,0:T(8,128)(2,1)S(1)} %slice.81), channel_id=1, source_target_pairs={{0,1},{2,0},{4,2},{6,4},{7,6},{5,7},{3,5},{1,3},{8,9},{10,8},{12,1... | collective-permute-start | bytes 294920 | tf_op jit(solution)/shard_map/ppermute | solution.py:39

commit v17 on v16

--- a/solution.py
+++ b/solution.py
@@ -85,12 +85,13 @@
 
     own = jnp.arange(span_count, dtype=earlier.dtype)
     picks = jnp.stack([slot(earlier[:, 0]), slot(earlier[:, 1]), own], axis=1)
-    window = jnp.take(pool, picks.reshape(-1), axis=0, mode="clip").reshape(
-        (span_count, 3) + rimmed.shape[1:]
-    )
+
+    def span_window_of(source, span):
+        return jnp.take(source, picks[span], axis=0)[None]
+
     score_scale = 1.0 / channels**0.5
     outputs = []
-    span_window = window[:1]
+    span_window = span_window_of(pool, 0)
     for span in range(span_count):
         accum = lax.conv_general_dilated(
             span_window,
@@ -110,9 +111,8 @@
         ).astype(jnp.bfloat16)
         pieces = ring_gather(tokens, "height", 1)
         if span + 1 < span_count:
-            pieces[1], span_window = lax.optimization_barrier(
-                (pieces[1], window[span + 1 : span + 2])
-            )
+            pieces[1], tied = lax.optimization_barrier((pieces[1], pool))
+            span_window = span_window_of(tied, span + 1)
         tokens_all = jnp.concatenate(pieces, axis=1)
         keys_all = jnp.einsum(
             "ftc,cd->ftd", tokens_all, key_weight, preferred_element_type=jnp.float32

time: 99.4 us -> 105 us (1.056)
  other arithmetic: 6.19 us -> 9.22 us
  matrix products: 25.9 us -> 27.9 us
  local copies, waits for them, and re-layouts: 22.8 us -> 24.8 us
  waiting for transfers between devices: 19.3 us -> 17.5 us
    broadcast_in_dim x0 -> x2, other arithmetic: none -> 3.01 us  [span_window_of(): return jnp.take(source, picks[span], axis=0)[None]]
    conv_general_dilated x2, matrix products: 9.89 us -> 12.7 us  [shards(): lax.conv_general_dilated(span_window, conv_weight, window_strides=(1, 1,...]
    slice x2 -> x0, local copies, waits for them, and re-layouts: 2.39 us -> none  [the longest x1 1.92 us: shards(): window[span + 1:span + 2]]
    unnamed x44 -> x48, local copies, waits for them, and re-layouts: 12.9 us -> 14.8 us
    ppermute x6, waiting for transfers between devices: 11.3 us -> 9.7 us  [ring_gather(): forward = lax.ppermute(forward, axis, ahead)]
    gather x1 -> x2, local copies, waits for them, and re-layouts: 2.52 us -> 3.64 us  [span_window_of(): return jnp.take(source, picks[span], axis=0)[None]]
  transfers between devices with their start and end apart: 19 -> 19, of which waited for: 8 -> 7; matrix products, arithmetic and copies ran while one was open for 29% -> 35% of each run, Pallas kernels for 0% -> 0%
where the time goes in v17:
time: 105 us; the launch traced here: 104 us
  matrix products  27.9 us (27%)
  local copies, waits for them, and re-layouts  24.8 us (24%)
  starting transfers between devices  24.3 us (23%)
  waiting for transfers between devices  17.5 us (17%)
  other arithmetic  9.22 us (9%)
    unnamed x48, local copies, waits for them, and re-layouts  14.8 us
    conv_general_dilated x2, matrix products, shards(): lax.conv_general_dilated(span_window, conv_weight, window_strides=(1, 1,...  12.7 us
    ppermute x6, waiting for transfers between devices, ring_gather(): forward = lax.ppermute(forward, axis, ahead)  9.7 us
    ppermute x6, starting transfers between devices, ring_gather(): backward = lax.ppermute(backward, axis, behind)  6.9 us
    dot_general x2, matrix products, shards(): jnp.einsum('fqc,fkc->fqk', queries, keys_all, preferred_element_type=jnp....  6.42 us
    dot_general x2, matrix products, shards(): jnp.einsum('fqk,fkc->fqc', weights_exp.astype(jnp.bfloat16), values_all,...  6.27 us
    ppermute x6, starting transfers between devices, ring_gather(): forward = lax.ppermute(forward, axis, ahead)  5.96 us
    ppermute x1, starting transfers between devices, padded_2(): lax.ppermute(tail, axis, [(i, (i + 1) % count) for i in range(ends)])  5.52 us
  transfers between devices with their start and end apart: 19, of which 7 were waited for; matrix products, arithmetic and copies ran while one was open for 35% of the time, Pallas kernels for 0%

profile of v17, /device:TPU:0, one launch (start us, length us, event | category | flops | bytes accessed | tf_op | source)
XLA Modules:
  0.0 104.1 jit_solution(1093010522755222604)
XLA Ops:
  0.0 1.1 %fusion.113 = (bf16[2,1,128,384]{3,2,1,0:T(8,128)(2,1)S(1)}, bf16[2,1,128,384]{3,2,1,0:T(8,128)(2,1)S(1)}) fusion(bf16[2,2,128,384]{3,2,1,0:T(8,128)(2,1)} %param.12), kind=kLoop, calls=%fused_computation.166 | loop fusion | bytes 786432 | tf_op jit(solution)/shard_map/slice | solution.py:12
  1.1 1.3 %collective-permute-start.1 = (bf16[2,1,128,384]{3,2,1,0:T(8,128)(2,1)S(1)}, bf16[2,1,128,384]{3,2,1,0:T(8,128)(2,1)S(1)}, u32[]{:S(2)}, u32[]{:S(2)}) collective-permute-start(bf16[2,1,128,384]{3,2,1,0:T(8,128)(2,1)S(1)} %get-tuple-element.21), channel_id=1, source_target_pairs={{1,0},{2,1},{3,2},{4,3},{5,4},{6,5},{7,6},{9,8},{10,9},{11,10},{12... | collective-permute-start | bytes 589832 | tf_op jit(solution)/shard_map/ppermute | solution.py:17
  2.4 5.5 %collective-permute-start = (bf16[2,1,128,384]{3,2,1,0:T(8,128)(2,1)S(1)}, bf16[2,1,128,384]{3,2,1,0:T(8,128)(2,1)S(1)}, u32[]{:S(2)}, u32[]{:S(2)}) collective-permute-start(bf16[2,1,128,384]{3,2,1,0:T(8,128)(2,1)S(1)} %get-tuple-element.20), channel_id=1, source_target_pairs={{0,1},{1,2},{2,3},{3,4},{4,5},{5,6},{6,7},{8,9},{9,10},{10,11},{11... | collective-permute-start | bytes 589832 | tf_op jit(solution)/shard_map/ppermute | solution.py:15
  8.0 1.1 %fusion.74 = f32[2,2,128]{2,1,0:T(2,128)S(1)} fusion(bf16[2,2,128,384]{3,2,1,0:T(8,128)(2,1)} %param.12), kind=kLoop, calls=%fused_computation.74 | loop fusion | flops 589312 | bytes 395264 | tf_op jit(solution)/shard_map/reduce_sum | solution.py:48
  9.1 1.8 %collective-permute-done.1 = bf16[2,1,128,384]{3,2,1,0:T(8,128)(2,1)S(1)} collective-permute-done((bf16[2,1,128,384]{3,2,1,0:T(8,128)(2,1)S(1)}, bf16[2,1,128,384]{3,2,1,0:T(8,128)(2,1)S(1)}, u32[]{:S(2)}, u32[]{:S(2)}) %collective-permute-start.1) | collective-permute-done | bytes 196640 | tf_op jit(solution)/shard_map/ppermute | solution.py:17
  10.9 4.4 %collective-permute-done = bf16[2,1,128,384]{3,2,1,0:T(8,128)(2,1)S(1)} collective-permute-done((bf16[2,1,128,384]{3,2,1,0:T(8,128)(2,1)S(1)}, bf16[2,1,128,384]{3,2,1,0:T(8,128)(2,1)S(1)}, u32[]{:S(2)}, u32[]{:S(2)}) %collective-permute-start) | collective-permute-done | bytes 196640 | tf_op jit(solution)/shard_map/ppermute | solution.py:15
  15.5 0.5 fusion.81
  17.2 1.6 %collective-permute-done.2 = bf16[2,4,130,384]{3,2,1,0:T(8,128)(2,1)} collective-permute-done((bf16[2,4,130,384]{3,2,1,0:T(8,128)(2,1)S(1)}, bf16[2,4,130,384]{3,2,1,0:T(8,128)(2,1)}, u32[]{:S(2)}, u32[]{:S(2)}) %collective-permute-start.2) | collective-permute-done | bytes 798752 | tf_op jit(solution)/shard_map/ppermute | solution.py:76
  18.9 1.7 %maximum_maximum_fusion = bf16[5,4,130,384]{3,2,1,0:T(8,128)(2,1)S(1)} fusion(bf16[2,4,130,384]{3,2,1,0:T(8,128)(2,1)} %collective-permute-done.2, bf16[2,4,130,384]{3,2,1,0:T(8,128)(2,1)} %copy-done.2, bf16[5]{0:T(256)(128)(2,1)S(1)} %pad.17.clone), kind=kLoop, calls=%fused_computation.15 | loop fusion | flops 1996800 | bytes 3594250 | tf_op jit(solution)/shard_map/concatenate | solution.py:79
  20.6 1.8 %gather_fusion = bf16[3,4,130,384]{3,2,1,0:T(8,128)(2,1)} fusion(bf16[5,4,130,384]{3,2,1,0:T(8,128)(2,1)S(1)} %maximum_maximum_fusion, s32[1024]{0:T(1024)S(1)} %pad_clamp_fusion.1), kind=kCustom, calls=%fused_computation.clone | custom fusion | bytes 2396172 | tf_op jit(solution)/shard_map/jit(_take)/gather | solution.py:90
  22.4 1.5 %select_bitcast_fusion.1 = bf16[3,4,1,130,384]{4,3,1,0,2:T(8,128)(2,1)S(1)} fusion(bf16[3,4,130,384]{3,2,1,0:T(8,128)(2,1)} %gather_fusion, pred[3]{0:T(512)(128)(4,1)S(1)} %get-tuple-element.24), kind=kLoop, calls=%fused_computation.40 | loop fusion | flops 599040 | bytes 2396163 | tf_op jit(solution)/shard_map/broadcast_in_dim | solution.py:90
  23.9 0.5 copy.23
  24.4 0.5 pad.5.clone
  25.1 0.5 copy-done.14
  25.5 6.4 %fusion.38 = f32[1,2,8,17,384]{4,2,3,1,0:T(8,128)S(1)} fusion(bf16[3,3,3,384,384]{4,3,2,1,0:T(8,128)(2,1)} %param.15, bf16[3,4,1,7,2,384]{5,3,4,1,0,2:T(8,128)(2,1)S(1)} %slice.66, bf16[3,4,1,8,17,384]{5,3,4,1,0,2:T(8,128)(2,1)S(1)} %copy.13, pred[8,17]{0,1:T(8,128)(4,1)S(1)} %copy-done.14), kind=kOutput, calls=%fused_computation.44 | convolution fusion | flops 2170140672 | bytes 9762952 | tf_op jit(solution)/shard_map/conv_general_dilated | solution.py:96
  32.9 1.7 %collective-permute-start.3 = (bf16[1,256,384]{2,1,0:T(8,128)(2,1)S(1)}, bf16[1,256,384]{2,1,0:T(8,128)(2,1)S(1)}, u32[]{:S(2)}, u32[]{:S(2)}) collective-permute-start(bf16[1,256,384]{2,1,0:T(8,128)(2,1)S(1)} %bitcast.112), channel_id=1, source_target_pairs={{0,2},{2,4},{4,6},{6,7},{7,5},{5,3},{3,1},{1,0},{8,10},{10,12},{12... | collective-permute-start | bytes 589832 | tf_op jit(solution)/shard_map/ppermute | solution.py:33
  34.6 0.7 constant_dynamic-update-slice_fusion.8
  35.3 0.9 collective-permute-start.4
  36.2 0.9 convolution_convert_fusion.5
  37.1 3.5 %collective-permute-done.3 = bf16[1,256,384]{2,1,0:T(8,128)(2,1)S(1)} collective-permute-done((bf16[1,256,384]{2,1,0:T(8,128)(2,1)S(1)}, bf16[1,256,384]{2,1,0:T(8,128)(2,1)S(1)}, u32[]{:S(2)}, u32[]{:S(2)}) %collective-permute-start.3) | collective-permute-done | bytes 196640 | tf_op jit(solution)/shard_map/ppermute | solution.py:33
  40.6 1.8 %gather_fusion.1 = bf16[3,4,130,384]{3,2,1,0:T(8,128)(2,1)} fusion(bf16[5,4,130,384]{3,2,1,0:T(8,128)(2,1)S(1)} %maximum_maximum_fusion, s32[1024]{0:T(1024)S(1)} %pad_clamp_fusion), kind=kCustom, calls=%fused_computation.1.clone | custom fusion | bytes 2396172 | tf_op jit(solution)/shard_map/jit(_take)/gather | solution.py:90
  42.5 1.5 %select_bitcast_fusion = bf16[3,4,1,130,384]{4,3,1,0,2:T(8,128)(2,1)S(1)} fusion(bf16[3,4,130,384]{3,2,1,0:T(8,128)(2,1)} %gather_fusion.1, pred[3]{0:T(512)(128)(4,1)S(1)} %get-tuple-element.12), kind=kLoop, calls=%fused_computation.39 | loop fusion | flops 599040 | bytes 2396163 | tf_op jit(solution)/shard_map/broadcast_in_dim | solution.py:90
  44.0 0.5 copy.24
  44.5 0.5 pad.7.clone
  45.1 6.4 %fusion.35 = f32[1,2,8,17,384]{4,2,3,1,0:T(8,128)S(1)} fusion(bf16[3,3,3,384,384]{4,3,2,1,0:T(8,128)(2,1)} %param.15, bf16[3,4,1,7,2,384]{5,3,4,1,0,2:T(8,128)(2,1)S(1)} %slice.70, bf16[3,4,1,8,17,384]{5,3,4,1,0,2:T(8,128)(2,1)S(1)} %copy.18, pred[8,17]{0,1:T(8,128)(4,1)S(1)} %copy-done.14), kind=kOutput, calls=%fused_computation.43 | convolution fusion | flops 2170140672 | bytes 9762952 | tf_op jit(solution)/shard_map/conv_general_dilated | solution.py:96
  52.2 1.0 collective-permute-start.11
  53.1 1.1 %collective-permute-start.12 = (bf16[1,256,384]{2,1,0:T(8,128)(2,1)S(1)}, bf16[1,256,384]{2,1,0:T(8,128)(2,1)S(1)}, u32[]{:S(2)}, u32[]{:S(2)}) collective-permute-start(bf16[1,256,384]{2,1,0:T(8,128)(2,1)S(1)} %bitcast.117), channel_id=1, source_target_pairs={{0,1},{2,0},{4,2},{6,4},{7,6},{5,7},{3,5},{1,3},{8,9},{10,8},{12,1... | collective-permute-start | bytes 589832 | tf_op jit(solution)/shard_map/ppermute | solution.py:34
  54.2 0.9 collective-permute-start.5
  55.2 0.7 constant_dynamic-update-slice_fusion.7
  55.9 1.1 %collective-permute-start.6 = (bf16[1,256,384]{2,1,0:T(8,128)(2,1)}, bf16[1,256,384]{2,1,0:T(8,128)(2,1)S(1)}, u32[]{:S(2)}, u32[]{:S(2)}) collective-permute-start(bf16[1,256,384]{2,1,0:T(8,128)(2,1)} %collective-permute-done.4), channel_id=1, source_target_pairs={{0,1},{2,0},{4,2},{6,4},{7,6},{5,7},{3,5},{1,3},{8,9},{10,8},{12,1... | collective-permute-start | bytes 589832 | tf_op jit(solution)/shard_map/ppermute | solution.py:34
  57.0 1.6 %constant_dynamic-update-slice_fusion.6 = bf16[1,2048,384]{2,1,0:T(8,128)(2,1)} fusion(bf16[1,2048,384]{2,1,0:T(8,128)(2,1)} %constant_dynamic-update-slice_fusion.7, bf16[1,256,384]{2,1,0:T(8,128)(2,1)} %collective-permute-done.4), kind=kLoop, calls=%fused_computation.112 | loop fusion | bytes 393216
  58.7 0.9 convolution_convert_fusion.4
  60.0 0.9 collective-permute-start.13
  61.0 1.1 %collective-permute-start.14 = (bf16[1,256,384]{2,1,0:T(8,128)(2,1)S(1)}, bf16[1,256,384]{2,1,0:T(8,128)(2,1)}, u32[]{:S(2)}, u32[]{:S(2)}) collective-permute-start(bf16[1,256,384]{2,1,0:T(8,128)(2,1)S(1)} %collective-permute-done.12), channel_id=1, source_target_pairs={{0,1},{2,0},{4,2},{6,4},{7,6},{5,7},{3,5},{1,3},{8,9},{10,8},{12,1... | collective-permute-start | bytes 589832 | tf_op jit(solution)/shard_map/ppermute | solution.py:34
  62.1 2.2 %collective-permute-done.5 = bf16[1,256,384]{2,1,0:T(8,128)(2,1)S(1)} collective-permute-done((bf16[1,256,384]{2,1,0:T(8,128)(2,1)S(1)}, bf16[1,256,384]{2,1,0:T(8,128)(2,1)S(1)}, u32[]{:S(2)}, u32[]{:S(2)}) %collective-permute-start.5) | collective-permute-done | bytes 196640 | tf_op jit(solution)/shard_map/ppermute | solution.py:33
  64.2 0.9 collective-permute-start.7
  65.3 1.1 %collective-permute-start.8 = (bf16[1,256,384]{2,1,0:T(8,128)(2,1)S(1)}, bf16[1,256,384]{2,1,0:T(8,128)(2,1)S(1)}, u32[]{:S(2)}, u32[]{:S(2)}) collective-permute-start(bf16[1,256,384]{2,1,0:T(8,128)(2,1)S(1)} %collective-permute-done.6), channel_id=1, source_target_pairs={{0,1},{2,0},{4,2},{6,4},{7,6},{5,7},{3,5},{1,3},{8,9},{10,8},{12,1... | collective-permute-start | bytes 589832 | tf_op jit(solution)/shard_map/ppermute | solution.py:34
  66.4 0.7 constant_dynamic-update-slice_fusion.5
  67.1 0.7 constant_dynamic-update-slice_fusion.4
  67.8 3.6 %collective-permute-done.7 = bf16[1,256,384]{2,1,0:T(8,128)(2,1)S(1)} collective-permute-done((bf16[1,256,384]{2,1,0:T(8,128)(2,1)S(1)}, bf16[1,256,384]{2,1,0:T(8,128)(2,1)S(1)}, u32[]{:S(2)}, u32[]{:S(2)}) %collective-permute-start.7) | collective-permute-done | bytes 196640 | tf_op jit(solution)/shard_map/ppermute | solution.py:33
  71.4 0.6 collective-permute-start.9
  72.1 1.5 %collective-permute-start.10 = (bf16[1,128,384]{2,1,0:T(8,128)(2,1)S(1)}, bf16[1,128,384]{2,1,0:T(8,128)(2,1)S(1)}, u32[]{:S(2)}, u32[]{:S(2)}) collective-permute-start(bf16[1,128,384]{2,1,0:T(8,128)(2,1)S(1)} %slice.69), channel_id=1, source_target_pairs={{0,1},{2,0},{4,2},{6,4},{7,6},{5,7},{3,5},{1,3},{8,9},{10,8},{12,1... | collective-permute-start | bytes 294920 | tf_op jit(solution)/shard_map/ppermute | solution.py:39
  73.6 0.5 collective-permute-start.15
  74.1 1.0 constant_dynamic-update-slice_fusion.14
  75.1 1.5 %collective-permute-start.16 = (bf16[1,256,384]{2,1,0:T(8,128)(2,1)}, bf16[1,256,384]{2,1,0:T(8,128)(2,1)}, u32[]{:S(2)}, u32[]{:S(2)}) collective-permute-start(bf16[1,256,384]{2,1,0:T(8,128)(2,1)} %collective-permute-done.14), channel_id=1, source_target_pairs={{0,1},{2,0},{4,2},{6,4},{7,6},{5,7},{3,5},{1,3},{8,9},{10,8},{12,1... | collective-permute-start | bytes 589832 | tf_op jit(solution)/shard_map/ppermute | solution.py:34
  76.7 1.0 constant_dynamic-update-slice_fusion.13
  77.7 0.8 constant_dynamic-update-slice_fusion.3
  78.4 0.7 constant_dynamic-update-slice_fusion.2
  79.1 0.6 constant_dynamic-update-slice_fusion.1
  79.8 0.6 constant_dynamic-update-slice_fusion
  80.4 3.2 %fusion.117 = (f32[256]{0:T(256)S(1)}, f32[256,2048]{1,0:T(8,128)S(1)}) fusion(bf16[256,384]{1,0:T(8,128)(2,1)S(1)} %copy-done.8, bf16[384,384]{1,0:T(8,128)(2,1)S(1)} %copy-done, bf16[1,2048,384]{2,1,0:T(8,128)(2,1)} %constant_dynamic-update-slice_fusion), kind=kOutput, calls=%fused_computation.168 | convolution fusion | flops 1008467712 | bytes 4162560 | tf_op jit(solution)/shard_map/fqc,fkc->fqk/dot_general | solution.py:124
  84.0 3.2 %fusion.54 = bf16[256,384]{1,0:T(8,128)(2,1)S(1)} fusion(bf16[384,384]{1,0:T(8,128)(2,1)} %param.20, bf16[1,2048,384]{2,1,0:T(8,128)(2,1)} %constant_dynamic-update-slice_fusion, f32[256,2048]{1,0:T(8,128)S(1)} %get-tuple-element.31, f32[256]{0:T(256)S(1)} %get-tuple-element.30, f32[256]{0:T(256)S(1)} %fusion.2), kind=kOutput, calls=%fused_computation.54 | convolution fusion | flops 1008664576 | bytes 4163584 | tf_op jit(solution)/shard_map/fqk,fkc->fqc/dot_general | solution.py:130
  87.5 0.9 slice.72
  88.4 0.6 collective-permute-start.17
  89.0 0.9 slice.73
  89.9 1.7 %collective-permute-start.18 = (bf16[1,128,384]{2,1,0:T(8,128)(2,1)S(1)}, bf16[1,128,384]{2,1,0:T(8,128)(2,1)S(1)}, u32[]{:S(2)}, u32[]{:S(2)}) collective-permute-start(bf16[1,128,384]{2,1,0:T(8,128)(2,1)S(1)} %slice.73), channel_id=1, source_target_pairs={{0,1},{2,0},{4,2},{6,4},{7,6},{5,7},{3,5},{1,3},{8,9},{10,8},{12,1... | collective-permute-start | bytes 294920 | tf_op jit(solution)/shard_map/ppermute | solution.py:39
  91.7 1.6 %constant_dynamic-update-slice_fusion.12 = bf16[1,2048,384]{2,1,0:T(8,128)(2,1)} fusion(bf16[1,2048,384]{2,1,0:T(8,128)(2,1)} %copy-done.9, bf16[1,256,384]{2,1,0:T(8,128)(2,1)} %collective-permute-done.15), kind=kLoop, calls=%fused_computation.118 | loop fusion | bytes 393216
  93.3 1.6 %constant_dynamic-update-slice_fusion.11 = bf16[1,2048,384]{2,1,0:T(8,128)(2,1)} fusion(bf16[1,2048,384]{2,1,0:T(8,128)(2,1)} %constant_dynamic-update-slice_fusion.12, bf16[1,256,384]{2,1,0:T(8,128)(2,1)} %collective-permute-done.16), kind=kLoop, calls=%fused_computation.117 | loop fusion | bytes 393216
  94.9 0.6 constant_dynamic-update-slice_fusion.10
  95.5 0.7 constant_dynamic-update-slice_fusion.9
  96.2 3.3 %fusion.114 = (f32[256]{0:T(256)S(1)}, f32[256,2048]{1,0:T(8,128)S(1)}) fusion(bf16[256,384]{1,0:T(8,128)(2,1)} %convolution_convert_fusion.4, bf16[384,384]{1,0:T(8,128)(2,1)S(1)} %copy-done, bf16[1,2048,384]{2,1,0:T(8,128)(2,1)} %constant_dynamic-update-slice_fusion.9), kind=kOutput, calls=%fused_computation.167 | convolution fusion | flops 1008467712 | bytes 4162560 | tf_op jit(solution)/shard_map/fqc,fkc->fqk/dot_general | solution.py:124
  99.5 0.4 fusion.4
  99.9 3.1 %fusion.48 = bf16[256,384]{1,0:T(8,128)(2,1)S(1)} fusion(bf16[384,384]{1,0:T(8,128)(2,1)} %param.20, bf16[1,2048,384]{2,1,0:T(8,128)(2,1)} %constant_dynamic-update-slice_fusion.9, f32[256,2048]{1,0:T(8,128)S(1)} %get-tuple-element.29, f32[256]{0:T(256)S(1)} %get-tuple-element.28, f32[256]{0:T(256)S(1)} %fusion.4), kind=kOutput, calls=%fused_computation.52 | convolution fusion | flops 1008664576 | bytes 4163584 | tf_op jit(solution)/shard_map/fqk,fkc->fqc/dot_general | solution.py:130
  103.3 0.8 pad_maximum_fusion.1
  (77 shorter events, 4.8 us)
Async XLA Ops:
  0.0 80.4 %copy-start = (bf16[384,384]{1,0:T(8,128)(2,1)S(1)}, bf16[384,384]{1,0:T(8,128)(2,1)}, u32[]{:S(2)}) copy-start(bf16[384,384]{1,0:T(8,128)(2,1)} %param.19) | copy-start | bytes 884740
  0.0 15.4 %copy-start.1 = (bf16[2,2,128,384]{3,2,1,0:T(8,128)(2,1)S(1)}, bf16[2,2,128,384]{3,2,1,0:T(8,128)(2,1)}, u32[]{:S(2)}) copy-start(bf16[2,2,128,384]{3,2,1,0:T(8,128)(2,1)} %param.12) | copy-start | bytes 1179652
  0.0 15.5 %copy-start.13 = (f32[384]{0:T(512)S(1)}, f32[384]{0:T(512)}, u32[]{:S(2)}) copy-start(f32[384]{0:T(512)} %param.14) | copy-start | bytes 4612
  1.1 9.8 %collective-permute-start.1 = (bf16[2,1,128,384]{3,2,1,0:T(8,128)(2,1)S(1)}, bf16[2,1,128,384]{3,2,1,0:T(8,128)(2,1)S(1)}, u32[]{:S(2)}, u32[]{:S(2)}) collective-permute-start(bf16[2,1,128,384]{3,2,1,0:T(8,128)(2,1)S(1)} %get-tuple-element.21), channel_id=1, source_target_pairs={{1,0},{2,1},{3,2},{4,3},{5,4},{6,5},{7,6},{9,8},{10,9},{11,10},{12... | collective-permute-start | bytes 589832 | tf_op jit(solution)/shard_map/ppermute | solution.py:17
  2.4 12.8 %collective-permute-start = (bf16[2,1,128,384]{3,2,1,0:T(8,128)(2,1)S(1)}, bf16[2,1,128,384]{3,2,1,0:T(8,128)(2,1)S(1)}, u32[]{:S(2)}, u32[]{:S(2)}) collective-permute-start(bf16[2,1,128,384]{3,2,1,0:T(8,128)(2,1)S(1)} %get-tuple-element.20), channel_id=1, source_target_pairs={{0,1},{1,2},{2,3},{3,4},{4,5},{5,6},{6,7},{8,9},{9,10},{10,11},{11... | collective-permute-start | bytes 589832 | tf_op jit(solution)/shard_map/ppermute | solution.py:15
  16.0 0.7 copy-start.12
  16.3 0.9 copy-start.2
  16.3 2.6 %collective-permute-start.2 = (bf16[2,4,130,384]{3,2,1,0:T(8,128)(2,1)S(1)}, bf16[2,4,130,384]{3,2,1,0:T(8,128)(2,1)}, u32[]{:S(2)}, u32[]{:S(2)}) collective-permute-start(bf16[2,4,130,384]{3,2,1,0:T(8,128)(2,1)S(1)} %fusion.65), channel_id=1, source_target_pairs={{0,8},{8,0},{1,9},{9,1},{2,10},{10,2},{3,11},{11,3},{4,12},{12,4},... | collective-permute-start | bytes 2396168 | tf_op jit(solution)/shard_map/ppermute | solution.py:76
  24.9 0.7 copy-start.14
  31.9 0.7 copy-start.10
  31.9 0.8 copy-start.11
  31.9 4.2 %copy-start.4 = (bf16[384,384]{1,0:T(8,128)(2,1)S(1)}, bf16[384,384]{1,0:T(8,128)(2,1)}, u32[]{:S(2)}) copy-start(bf16[384,384]{1,0:T(8,128)(2,1)} %param.18) | copy-start | bytes 884740
  32.9 7.7 %collective-permute-start.3 = (bf16[1,256,384]{2,1,0:T(8,128)(2,1)S(1)}, bf16[1,256,384]{2,1,0:T(8,128)(2,1)S(1)}, u32[]{:S(2)}, u32[]{:S(2)}) collective-permute-start(bf16[1,256,384]{2,1,0:T(8,128)(2,1)S(1)} %bitcast.112), channel_id=1, source_target_pairs={{0,2},{2,4},{4,6},{6,7},{7,5},{5,3},{3,1},{1,0},{8,10},{10,12},{12... | collective-permute-start | bytes 589832 | tf_op jit(solution)/shard_map/ppermute | solution.py:33
  35.3 20.6 %collective-permute-start.4 = (bf16[1,256,384]{2,1,0:T(8,128)(2,1)S(1)}, bf16[1,256,384]{2,1,0:T(8,128)(2,1)}, u32[]{:S(2)}, u32[]{:S(2)}) collective-permute-start(bf16[1,256,384]{2,1,0:T(8,128)(2,1)S(1)} %bitcast.114), channel_id=1, source_target_pairs={{0,1},{2,0},{4,2},{6,4},{7,6},{5,7},{3,5},{1,3},{8,9},{10,8},{12,1... | collective-permute-start | bytes 589832 | tf_op jit(solution)/shard_map/ppermute | solution.py:34
  40.6 3.3 %copy-start.6 = (bf16[1,256,384]{2,1,0:T(8,128)(2,1)}, bf16[1,256,384]{2,1,0:T(8,128)(2,1)S(1)}, u32[]{:S(2)}) copy-start(bf16[1,256,384]{2,1,0:T(8,128)(2,1)S(1)} %collective-permute-done.3) | copy-start | bytes 589828
  51.5 2.7 %copy-start.7 = (bf16[1,256,384]{2,1,0:T(8,128)(2,1)S(1)}, bf16[1,256,384]{2,1,0:T(8,128)(2,1)}, u32[]{:S(2)}) copy-start(bf16[1,256,384]{2,1,0:T(8,128)(2,1)} %copy-done.6) | copy-start | bytes 589828
  51.8 6.9 %copy-start.5 = (bf16[384,384]{1,0:T(8,128)(2,1)S(1)}, bf16[384,384]{1,0:T(8,128)(2,1)}, u32[]{:S(2)}) copy-start(bf16[384,384]{1,0:T(8,128)(2,1)} %param.18) | copy-start | bytes 884740
  52.2 7.9 %collective-permute-start.11 = (bf16[1,256,384]{2,1,0:T(8,128)(2,1)S(1)}, bf16[1,256,384]{2,1,0:T(8,128)(2,1)S(1)}, u32[]{:S(2)}, u32[]{:S(2)}) collective-permute-start(bf16[1,256,384]{2,1,0:T(8,128)(2,1)S(1)} %bitcast.116), channel_id=1, source_target_pairs={{0,2},{2,4},{4,6},{6,7},{7,5},{5,3},{3,1},{1,0},{8,10},{10,12},{12... | collective-permute-start | bytes 589832 | tf_op jit(solution)/shard_map/ppermute | solution.py:33
  53.1 7.8 %collective-permute-start.12 = (bf16[1,256,384]{2,1,0:T(8,128)(2,1)S(1)}, bf16[1,256,384]{2,1,0:T(8,128)(2,1)S(1)}, u32[]{:S(2)}, u32[]{:S(2)}) collective-permute-start(bf16[1,256,384]{2,1,0:T(8,128)(2,1)S(1)} %bitcast.117), channel_id=1, source_target_pairs={{0,1},{2,0},{4,2},{6,4},{7,6},{5,7},{3,5},{1,3},{8,9},{10,8},{12,1... | collective-permute-start | bytes 589832 | tf_op jit(solution)/shard_map/ppermute | solution.py:34
  54.2 10.0 %collective-permute-start.5 = (bf16[1,256,384]{2,1,0:T(8,128)(2,1)S(1)}, bf16[1,256,384]{2,1,0:T(8,128)(2,1)S(1)}, u32[]{:S(2)}, u32[]{:S(2)}) collective-permute-start(bf16[1,256,384]{2,1,0:T(8,128)(2,1)S(1)} %copy-done.7), channel_id=1, source_target_pairs={{0,2},{2,4},{4,6},{6,7},{7,5},{5,3},{3,1},{1,0},{8,10},{10,12},{12... | collective-permute-start | bytes 589832 | tf_op jit(solution)/shard_map/ppermute | solution.py:33
  55.9 9.4 %collective-permute-start.6 = (bf16[1,256,384]{2,1,0:T(8,128)(2,1)}, bf16[1,256,384]{2,1,0:T(8,128)(2,1)S(1)}, u32[]{:S(2)}, u32[]{:S(2)}) collective-permute-start(bf16[1,256,384]{2,1,0:T(8,128)(2,1)} %collective-permute-done.4), channel_id=1, source_target_pairs={{0,1},{2,0},{4,2},{6,4},{7,6},{5,7},{3,5},{1,3},{8,9},{10,8},{12,1... | collective-permute-start | bytes 589832 | tf_op jit(solution)/shard_map/ppermute | solution.py:34
  60.0 13.6 %collective-permute-start.13 = (bf16[1,256,384]{2,1,0:T(8,128)(2,1)S(1)}, bf16[1,256,384]{2,1,0:T(8,128)(2,1)}, u32[]{:S(2)}, u32[]{:S(2)}) collective-permute-start(bf16[1,256,384]{2,1,0:T(8,128)(2,1)S(1)} %collective-permute-done.11), channel_id=1, source_target_pairs={{0,2},{2,4},{4,6},{6,7},{7,5},{5,3},{3,1},{1,0},{8,10},{10,12},{12... | collective-permute-start | bytes 589832 | tf_op jit(solution)/shard_map/ppermute | solution.py:33
  61.0 14.2 %collective-permute-start.14 = (bf16[1,256,384]{2,1,0:T(8,128)(2,1)S(1)}, bf16[1,256,384]{2,1,0:T(8,128)(2,1)}, u32[]{:S(2)}, u32[]{:S(2)}) collective-permute-start(bf16[1,256,384]{2,1,0:T(8,128)(2,1)S(1)} %collective-permute-done.12), channel_id=1, source_target_pairs={{0,1},{2,0},{4,2},{6,4},{7,6},{5,7},{3,5},{1,3},{8,9},{10,8},{12,1... | collective-permute-start | bytes 589832 | tf_op jit(solution)/shard_map/ppermute | solution.py:34
  64.2 7.2 %collective-permute-start.7 = (bf16[1,256,384]{2,1,0:T(8,128)(2,1)S(1)}, bf16[1,256,384]{2,1,0:T(8,128)(2,1)S(1)}, u32[]{:S(2)}, u32[]{:S(2)}) collective-permute-start(bf16[1,256,384]{2,1,0:T(8,128)(2,1)S(1)} %collective-permute-done.5), channel_id=1, source_target_pairs={{0,2},{2,4},{4,6},{6,7},{7,5},{5,3},{3,1},{1,0},{8,10},{10,12},{12... | collective-permute-start | bytes 589832 | tf_op jit(solution)/shard_map/ppermute | solution.py:33
  65.2 15.2 %copy-start.8 = (bf16[256,384]{1,0:T(8,128)(2,1)S(1)}, bf16[256,384]{1,0:T(8,128)(2,1)}, u32[]{:S(2)}) copy-start(bf16[256,384]{1,0:T(8,128)(2,1)} %convolution_convert_fusion.5) | copy-start | bytes 589828
  65.3 6.8 %collective-permute-start.8 = (bf16[1,256,384]{2,1,0:T(8,128)(2,1)S(1)}, bf16[1,256,384]{2,1,0:T(8,128)(2,1)S(1)}, u32[]{:S(2)}, u32[]{:S(2)}) collective-permute-start(bf16[1,256,384]{2,1,0:T(8,128)(2,1)S(1)} %collective-permute-done.6), channel_id=1, source_target_pairs={{0,1},{2,0},{4,2},{6,4},{7,6},{5,7},{3,5},{1,3},{8,9},{10,8},{12,1... | collective-permute-start | bytes 589832 | tf_op jit(solution)/shard_map/ppermute | solution.py:34
  71.4 7.7 %collective-permute-start.9 = (bf16[1,128,384]{2,1,0:T(8,128)(2,1)S(1)}, bf16[1,128,384]{2,1,0:T(8,128)(2,1)S(1)}, u32[]{:S(2)}, u32[]{:S(2)}) collective-permute-start(bf16[1,128,384]{2,1,0:T(8,128)(2,1)S(1)} %slice.68), channel_id=1, source_target_pairs={{0,2},{2,4},{4,6},{6,7},{7,5},{5,3},{3,1},{1,0},{8,10},{10,12},{12... | collective-permute-start | bytes 294920 | tf_op jit(solution)/shard_map/ppermute | solution.py:38
  72.1 7.7 %collective-permute-start.10 = (bf16[1,128,384]{2,1,0:T(8,128)(2,1)S(1)}, bf16[1,128,384]{2,1,0:T(8,128)(2,1)S(1)}, u32[]{:S(2)}, u32[]{:S(2)}) collective-permute-start(bf16[1,128,384]{2,1,0:T(8,128)(2,1)S(1)} %slice.69), channel_id=1, source_target_pairs={{0,1},{2,0},{4,2},{6,4},{7,6},{5,7},{3,5},{1,3},{8,9},{10,8},{12,1... | collective-permute-start | bytes 294920 | tf_op jit(solution)/shard_map/ppermute | solution.py:39
  73.6 13.9 %collective-permute-start.15 = (bf16[1,256,384]{2,1,0:T(8,128)(2,1)}, bf16[1,256,384]{2,1,0:T(8,128)(2,1)}, u32[]{:S(2)}, u32[]{:S(2)}) collective-permute-start(bf16[1,256,384]{2,1,0:T(8,128)(2,1)} %collective-permute-done.13), channel_id=1, source_target_pairs={{0,2},{2,4},{4,6},{6,7},{7,5},{5,3},{3,1},{1,0},{8,10},{10,12},{12... | collective-permute-start | bytes 589832 | tf_op jit(solution)/shard_map/ppermute | solution.py:33
  75.1 13.9 %collective-permute-start.16 = (bf16[1,256,384]{2,1,0:T(8,128)(2,1)}, bf16[1,256,384]{2,1,0:T(8,128)(2,1)}, u32[]{:S(2)}, u32[]{:S(2)}) collective-permute-start(bf16[1,256,384]{2,1,0:T(8,128)(2,1)} %collective-permute-done.14), channel_id=1, source_target_pairs={{0,1},{2,0},{4,2},{6,4},{7,6},{5,7},{3,5},{1,3},{8,9},{10,8},{12,1... | collective-permute-start | bytes 589832 | tf_op jit(solution)/shard_map/ppermute | solution.py:34
  77.7 2.1 %copy-start.9 = (bf16[1,2048,384]{2,1,0:T(8,128)(2,1)}, bf16[1,2048,384]{2,1,0:T(8,128)(2,1)S(1)}, u32[]{:S(2)}) copy-start(bf16[1,2048,384]{2,1,0:T(8,128)(2,1)S(1)} %constant_dynamic-update-slice_fusion.13) | copy-start | bytes 4718596
  84.0 3.2 %copy-start.3 = (bf16[384,384]{1,0:T(8,128)(2,1)S(1)}, bf16[384,384]{1,0:T(8,128)(2,1)}, u32[]{:S(2)}) copy-start(bf16[384,384]{1,0:T(8,128)(2,1)} %param.21) | copy-start | bytes 884740
  88.4 6.5 %collective-permute-start.17 = (bf16[1,128,384]{2,1,0:T(8,128)(2,1)S(1)}, bf16[1,128,384]{2,1,0:T(8,128)(2,1)S(1)}, u32[]{:S(2)}, u32[]{:S(2)}) collective-permute-start(bf16[1,128,384]{2,1,0:T(8,128)(2,1)S(1)} %slice.72), channel_id=1, source_target_pairs={{0,2},{2,4},{4,6},{6,7},{7,5},{5,3},{3,1},{1,0},{8,10},{10,12},{12... | collective-permute-start | bytes 294920 | tf_op jit(solution)/shard_map/ppermute | solution.py:38
  89.9 5.6 %collective-permute-start.18 = (bf16[1,128,384]{2,1,0:T(8,128)(2,1)S(1)}, bf16[1,128,384]{2,1,0:T(8,128)(2,1)S(1)}, u32[]{:S(2)}, u32[]{:S(2)}) collective-permute-start(bf16[1,128,384]{2,1,0:T(8,128)(2,1)S(1)} %slice.73), channel_id=1, source_target_pairs={{0,1},{2,0},{4,2},{6,4},{7,6},{5,7},{3,5},{1,3},{8,9},{10,8},{12,1... | collective-permute-start | bytes 294920 | tf_op jit(solution)/shard_map/ppermute | solution.py:39

commit v18 on v15

--- a/solution.py
+++ b/solution.py
@@ -108,7 +108,10 @@
         queries = jnp.einsum(
             "ftc,cd->ftd", tokens, query_weight, preferred_element_type=jnp.float32
         ).astype(jnp.bfloat16)
+        if span > 0:
+            tokens, _ = lax.optimization_barrier((tokens, previous_tail))
         pieces = ring_gather(tokens, "height", 1)
+        previous_tail = pieces[-2:]
         if span + 1 < span_count:
             pieces[1], span_window = lax.optimization_barrier(
                 (pieces[1], window[span + 1 : span + 2])

time: 96.8 us -> 105 us (1.085)
  waiting for transfers between devices: 19 us -> 24.5 us
  starting transfers between devices: 24.2 us -> 26 us
  matrix products: 20.8 us -> 22.4 us
    ppermute x6, starting transfers between devices: 5.98 us -> 13.2 us  [ring_gather(): forward = lax.ppermute(forward, axis, ahead)]
    ppermute x6, starting transfers between devices: 6.87 us -> 1.57 us  [ring_gather(): backward = lax.ppermute(backward, axis, behind)]
    ppermute x2, waiting for transfers between devices: 0.01 us -> 3.7 us  [ring_gather(): lax.ppermute(lax.slice_in_dim(backward, half, block.shape[dim], axis=dim)...]
    ppermute x2, starting transfers between devices: 1.25 us -> 4.11 us  [ring_gather(): lax.ppermute(lax.slice_in_dim(forward, 0, half, axis=dim), axis, ahead)]
    ppermute x1, waiting for transfers between devices: 4.36 us -> 1.72 us  [padded_2(): lax.ppermute(tail, axis, [(i, (i + 1) % count) for i in range(ends)])]
    ppermute x2, starting transfers between devices: 3.23 us -> 0.83 us  [ring_gather(): lax.ppermute(lax.slice_in_dim(backward, half, block.shape[dim], axis=dim)...]
    ppermute x1, waiting for transfers between devices: 1.78 us -> 4.07 us  [padded_2(): lax.ppermute(head, axis, [((i + 1) % count, i) for i in range(ends)])]
    ppermute x2, waiting for transfers between devices: 0.01 us -> 1.57 us  [ring_gather(): lax.ppermute(lax.slice_in_dim(forward, 0, half, axis=dim), axis, ahead)]
  transfers between devices with their start and end apart: 19 -> 19, of which waited for: 7 -> 12; matrix products, arithmetic and copies ran while one was open for 30% -> 27% of each run, Pallas kernels for 0% -> 0%
where the time goes in v18:
time: 105 us
  starting transfers between devices  26 us (25%)
  waiting for transfers between devices  24.5 us (23%)
  local copies, waits for them, and re-layouts  23 us (22%)
  matrix products  22.4 us (21%)
  other arithmetic  8.39 us (8%)
    unnamed x42, local copies, waits for them, and re-layouts  15.5 us
    ppermute x6, starting transfers between devices, ring_gather(): forward = lax.ppermute(forward, axis, ahead)  13.2 us
    ppermute x6, waiting for transfers between devices, ring_gather(): forward = lax.ppermute(forward, axis, ahead)  11.8 us
    dot_general x2, matrix products, shards(): jnp.einsum('fqk,fkc->fqc', weights_exp.astype(jnp.bfloat16), values_all,...  6.95 us
    dot_general x2, matrix products, shards(): jnp.einsum('fqc,fkc->fqk', queries, keys_all, preferred_element_type=jnp....  6.42 us
    conv_general_dilated x2, matrix products, shards(): lax.conv_general_dilated(span_window, conv_weight, window_strides=(1, 1,...  6.33 us
    ppermute x1, starting transfers between devices, padded_2(): lax.ppermute(tail, axis, [(i, (i + 1) % count) for i in range(ends)])  4.89 us
    ppermute x2, starting transfers between devices, ring_gather(): lax.ppermute(lax.slice_in_dim(forward, 0, half, axis=dim), axis, ahead)  4.11 us
  transfers between devices with their start and end apart: 19, of which 12 were waited for; matrix products, arithmetic and copies ran while one was open for 27% of the time, Pallas kernels for 0%

profile of v18, /device:TPU:0, one launch (start us, length us, event | category | flops | bytes accessed | tf_op | source)
XLA Modules:
  0.0 104.6 jit_solution(14578193912312647664)
XLA Ops:
  0.0 1.1 %fusion.114 = (bf16[2,1,128,384]{3,2,1,0:T(8,128)(2,1)S(1)}, bf16[2,1,128,384]{3,2,1,0:T(8,128)(2,1)S(1)}) fusion(bf16[2,2,128,384]{3,2,1,0:T(8,128)(2,1)} %param.10), kind=kLoop, calls=%fused_computation.165 | loop fusion | bytes 786432 | tf_op jit(solution)/shard_map/slice | solution.py:12
  1.1 4.9 %collective-permute-start = (bf16[2,1,128,384]{3,2,1,0:T(8,128)(2,1)S(1)}, bf16[2,1,128,384]{3,2,1,0:T(8,128)(2,1)S(1)}, u32[]{:S(2)}, u32[]{:S(2)}) collective-permute-start(bf16[2,1,128,384]{3,2,1,0:T(8,128)(2,1)S(1)} %get-tuple-element.19), channel_id=1, source_target_pairs={{0,1},{1,2},{2,3},{3,4},{4,5},{5,6},{6,7},{8,9},{9,10},{10,11},{11... | collective-permute-start | bytes 589832 | tf_op jit(solution)/shard_map/ppermute | solution.py:15
  6.0 1.3 %collective-permute-start.1 = (bf16[2,1,128,384]{3,2,1,0:T(8,128)(2,1)S(1)}, bf16[2,1,128,384]{3,2,1,0:T(8,128)(2,1)S(1)}, u32[]{:S(2)}, u32[]{:S(2)}) collective-permute-start(bf16[2,1,128,384]{3,2,1,0:T(8,128)(2,1)S(1)} %get-tuple-element.20), channel_id=1, source_target_pairs={{1,0},{2,1},{3,2},{4,3},{5,4},{6,5},{7,6},{9,8},{10,9},{11,10},{12... | collective-permute-start | bytes 589832 | tf_op jit(solution)/shard_map/ppermute | solution.py:17
  7.3 1.1 %fusion.74 = f32[2,2,128]{2,1,0:T(2,128)S(1)} fusion(bf16[2,2,128,384]{3,2,1,0:T(8,128)(2,1)} %param.10), kind=kLoop, calls=%fused_computation.74 | loop fusion | flops 589312 | bytes 395264 | tf_op jit(solution)/shard_map/reduce_sum | solution.py:48
  8.5 1.7 %collective-permute-done = bf16[2,1,128,384]{3,2,1,0:T(8,128)(2,1)S(1)} collective-permute-done((bf16[2,1,128,384]{3,2,1,0:T(8,128)(2,1)S(1)}, bf16[2,1,128,384]{3,2,1,0:T(8,128)(2,1)S(1)}, u32[]{:S(2)}, u32[]{:S(2)}) %collective-permute-start) | collective-permute-done | bytes 196640 | tf_op jit(solution)/shard_map/ppermute | solution.py:15
  10.2 4.1 %collective-permute-done.1 = bf16[2,1,128,384]{3,2,1,0:T(8,128)(2,1)S(1)} collective-permute-done((bf16[2,1,128,384]{3,2,1,0:T(8,128)(2,1)S(1)}, bf16[2,1,128,384]{3,2,1,0:T(8,128)(2,1)S(1)}, u32[]{:S(2)}, u32[]{:S(2)}) %collective-permute-start.1) | collective-permute-done | bytes 196640 | tf_op jit(solution)/shard_map/ppermute | solution.py:17
  14.5 0.5 fusion.81
  16.2 1.6 %collective-permute-done.2 = bf16[2,4,130,384]{3,2,1,0:T(8,128)(2,1)} collective-permute-done((bf16[2,4,130,384]{3,2,1,0:T(8,128)(2,1)S(1)}, bf16[2,4,130,384]{3,2,1,0:T(8,128)(2,1)}, u32[]{:S(2)}, u32[]{:S(2)}) %collective-permute-start.2) | collective-permute-done | bytes 798752 | tf_op jit(solution)/shard_map/ppermute | solution.py:76
  17.9 1.7 %maximum_maximum_fusion = bf16[5,4,130,384]{3,2,1,0:T(8,128)(2,1)S(1)} fusion(bf16[2,4,130,384]{3,2,1,0:T(8,128)(2,1)} %collective-permute-done.2, bf16[2,4,130,384]{3,2,1,0:T(8,128)(2,1)} %copy-done.2, bf16[5]{0:T(256)(128)(2,1)S(1)} %pad.17.clone), kind=kLoop, calls=%fused_computation.15 | loop fusion | flops 1996800 | bytes 3594250 | tf_op jit(solution)/shard_map/concatenate | solution.py:79
  19.6 2.5 %gather_fusion = bf16[6,4,130,384]{3,2,1,0:T(8,128)(2,1)} fusion(bf16[5,4,130,384]{3,2,1,0:T(8,128)(2,1)S(1)} %maximum_maximum_fusion, s32[1024]{0:T(1024)S(1)} %pad_clamp_fusion), kind=kCustom, calls=%fused_computation | custom fusion | bytes 4792344 | tf_op jit(solution)/shard_map/jit(_take)/gather | solution.py:88
  22.1 2.2 %broadcast_select_fusion = bf16[6,4,130,384]{3,2,1,0:T(8,128)(2,1)S(1)} fusion(bf16[6,4,130,384]{3,2,1,0:T(8,128)(2,1)} %gather_fusion, pred[6]{0:T(512)(128)(4,1)S(1)} %compare_and_fusion), kind=kLoop, calls=%fused_computation.12 | loop fusion | flops 1198080 | bytes 4792326 | tf_op jit(solution)/shard_map/jit(_take)/select_n | solution.py:88
  24.6 0.5 copy.23
  25.1 0.5 pad.5.clone
  25.8 0.8 slice-done.1
  26.6 3.2 %fusion.38 = f32[1,2,8,17,384]{4,2,3,1,0:T(8,128)S(1)} fusion(bf16[3,3,3,384,384]{4,3,2,1,0:T(8,128)(2,1)S(1)} %bitcast.123, bf16[3,4,1,7,2,384]{5,3,4,1,0,2:T(8,128)(2,1)S(1)} %slice.73, bf16[3,4,1,8,17,384]{5,3,4,1,0,2:T(8,128)(2,1)S(1)} %copy.13, pred[8,17]{0,1:T(8,128)(4,1)S(1)} %copy-done.9), kind=kOutput, calls=%fused_computation.44 | convolution fusion | flops 2170140672 | bytes 9762952 | tf_op jit(solution)/shard_map/conv_general_dilated | solution.py:95
  30.7 0.7 constant_dynamic-update-slice_fusion.8
  31.4 3.5 %collective-permute-start.3 = (bf16[1,256,384]{2,1,0:T(8,128)(2,1)S(1)}, bf16[1,256,384]{2,1,0:T(8,128)(2,1)S(1)}, u32[]{:S(2)}, u32[]{:S(2)}) collective-permute-start(bf16[1,256,384]{2,1,0:T(8,128)(2,1)S(1)} %bitcast.115), channel_id=1, source_target_pairs={{0,2},{2,4},{4,6},{6,7},{7,5},{5,3},{3,1},{1,0},{8,10},{10,12},{12... | collective-permute-start | bytes 589832 | tf_op jit(solution)/shard_map/ppermute | solution.py:33
  35.3 4.2 %collective-permute-done.3 = bf16[1,256,384]{2,1,0:T(8,128)(2,1)S(1)} collective-permute-done((bf16[1,256,384]{2,1,0:T(8,128)(2,1)S(1)}, bf16[1,256,384]{2,1,0:T(8,128)(2,1)S(1)}, u32[]{:S(2)}, u32[]{:S(2)}) %collective-permute-start.3) | collective-permute-done | bytes 196640 | tf_op jit(solution)/shard_map/ppermute | solution.py:33
  39.4 0.5 copy.24
  39.9 0.5 pad.7.clone
  40.6 3.2 %fusion.35 = f32[1,2,8,17,384]{4,2,3,1,0:T(8,128)S(1)} fusion(bf16[3,3,3,384,384]{4,3,2,1,0:T(8,128)(2,1)S(1)} %bitcast.123, bf16[3,4,1,7,2,384]{5,3,4,1,0,2:T(8,128)(2,1)S(1)} %slice.78, bf16[3,4,1,8,17,384]{5,3,4,1,0,2:T(8,128)(2,1)S(1)} %copy.18, pred[8,17]{0,1:T(8,128)(4,1)S(1)} %copy-done.9), kind=kOutput, calls=%fused_computation.43 | convolution fusion | flops 2170140672 | bytes 9762952 | tf_op jit(solution)/shard_map/conv_general_dilated | solution.py:95
  44.3 0.7 constant_dynamic-update-slice_fusion.7
  45.0 2.5 %collective-permute-start.5 = (bf16[1,256,384]{2,1,0:T(8,128)(2,1)S(1)}, bf16[1,256,384]{2,1,0:T(8,128)(2,1)S(1)}, u32[]{:S(2)}, u32[]{:S(2)}) collective-permute-start(bf16[1,256,384]{2,1,0:T(8,128)(2,1)S(1)} %collective-permute-done.3), channel_id=1, source_target_pairs={{0,2},{2,4},{4,6},{6,7},{7,5},{5,3},{3,1},{1,0},{8,10},{10,12},{12... | collective-permute-start | bytes 589832 | tf_op jit(solution)/shard_map/ppermute | solution.py:33
  47.7 0.7 constant_dynamic-update-slice_fusion.6
  48.4 0.9 convolution_convert_fusion.4
  49.3 1.9 %collective-permute-done.5 = bf16[1,256,384]{2,1,0:T(8,128)(2,1)S(1)} collective-permute-done((bf16[1,256,384]{2,1,0:T(8,128)(2,1)S(1)}, bf16[1,256,384]{2,1,0:T(8,128)(2,1)S(1)}, u32[]{:S(2)}, u32[]{:S(2)}) %collective-permute-start.5) | collective-permute-done | bytes 196640 | tf_op jit(solution)/shard_map/ppermute | solution.py:33
  51.2 2.4 %collective-permute-start.7 = (bf16[1,256,384]{2,1,0:T(8,128)(2,1)S(1)}, bf16[1,256,384]{2,1,0:T(8,128)(2,1)S(1)}, u32[]{:S(2)}, u32[]{:S(2)}) collective-permute-start(bf16[1,256,384]{2,1,0:T(8,128)(2,1)S(1)} %collective-permute-done.5), channel_id=1, source_target_pairs={{0,2},{2,4},{4,6},{6,7},{7,5},{5,3},{3,1},{1,0},{8,10},{10,12},{12... | collective-permute-start | bytes 589832 | tf_op jit(solution)/shard_map/ppermute | solution.py:33
  53.8 0.7 constant_dynamic-update-slice_fusion.5
  54.5 0.7 constant_dynamic-update-slice_fusion.4
  55.2 1.7 %collective-permute-done.7 = bf16[1,256,384]{2,1,0:T(8,128)(2,1)S(1)} collective-permute-done((bf16[1,256,384]{2,1,0:T(8,128)(2,1)S(1)}, bf16[1,256,384]{2,1,0:T(8,128)(2,1)S(1)}, u32[]{:S(2)}, u32[]{:S(2)}) %collective-permute-start.7) | collective-permute-done | bytes 196640 | tf_op jit(solution)/shard_map/ppermute | solution.py:33
  56.9 2.5 %collective-permute-start.9 = (bf16[1,128,384]{2,1,0:T(8,128)(2,1)S(1)}, bf16[1,128,384]{2,1,0:T(8,128)(2,1)S(1)}, u32[]{:S(2)}, u32[]{:S(2)}) collective-permute-start(bf16[1,128,384]{2,1,0:T(8,128)(2,1)S(1)} %slice.76), channel_id=1, source_target_pairs={{0,2},{2,4},{4,6},{6,7},{7,5},{5,3},{3,1},{1,0},{8,10},{10,12},{12... | collective-permute-start | bytes 294920 | tf_op jit(solution)/shard_map/ppermute | solution.py:38
  59.5 0.7 constant_dynamic-update-slice_fusion.3
  60.2 0.7 constant_dynamic-update-slice_fusion.2
  60.9 0.7 collective-permute-done.9
  61.6 2.5 %collective-permute-done.10 = bf16[1,128,384]{2,1,0:T(8,128)(2,1)S(1)} collective-permute-done((bf16[1,128,384]{2,1,0:T(8,128)(2,1)S(1)}, bf16[1,128,384]{2,1,0:T(8,128)(2,1)S(1)}, u32[]{:S(2)}, u32[]{:S(2)}) %collective-permute-start.10) | collective-permute-done | bytes 98336 | tf_op jit(solution)/shard_map/ppermute | solution.py:39
  64.0 0.7 constant_dynamic-update-slice_fusion.17
  64.8 1.6 %collective-permute-start.11 = (bf16[1,256,384]{2,1,0:T(8,128)(2,1)S(1)}, bf16[1,256,384]{2,1,0:T(8,128)(2,1)}, u32[]{:S(2)}, u32[]{:S(2)}) collective-permute-start(bf16[1,256,384]{2,1,0:T(8,128)(2,1)S(1)} %bitcast.112), channel_id=1, source_target_pairs={{0,2},{2,4},{4,6},{6,7},{7,5},{5,3},{3,1},{1,0},{8,10},{10,12},{12... | collective-permute-start | bytes 589832 | tf_op jit(solution)/shard_map/ppermute | solution.py:33
  66.3 0.4 collective-permute-start.12
  66.8 0.7 constant_dynamic-update-slice_fusion.1
  67.4 0.6 constant_dynamic-update-slice_fusion
  68.1 3.2 %fusion.118 = (f32[256]{0:T(256)S(1)}, f32[256,2048]{1,0:T(8,128)S(1)}) fusion(bf16[256,384]{1,0:T(8,128)(2,1)S(1)} %convolution_convert_fusion.5, bf16[384,384]{1,0:T(8,128)(2,1)S(1)} %copy-done, bf16[1,2048,384]{2,1,0:T(8,128)(2,1)} %constant_dynamic-update-slice_fusion), kind=kOutput, calls=%fused_computation.167 | convolution fusion | flops 1008467712 | bytes 4162560 | tf_op jit(solution)/shard_map/fqc,fkc->fqk/dot_general | solution.py:127
  71.7 3.8 %fusion.54 = bf16[256,384]{1,0:T(8,128)(2,1)} fusion(bf16[384,384]{1,0:T(8,128)(2,1)} %param.18, bf16[1,2048,384]{2,1,0:T(8,128)(2,1)} %constant_dynamic-update-slice_fusion, f32[256,2048]{1,0:T(8,128)S(1)} %get-tuple-element.28, f32[256]{0:T(256)S(1)} %get-tuple-element.27, f32[256]{0:T(256)S(1)} %fusion.2), kind=kOutput, calls=%fused_computation.54 | convolution fusion | flops 1008664576 | bytes 4163584 | tf_op jit(solution)/shard_map/fqk,fkc->fqc/dot_general | solution.py:133
  75.5 1.2 %fusion.44 = bf16[1,2,128,384]{3,2,1,0:T(8,128)(2,1)S(1)} fusion(bf16[2,128,384]{2,1,0:T(8,128)(2,1)} %bitcast.120, bf16[1,2,128,384]{3,2,1,0:T(8,128)(2,1)S(1)} %get-tuple-element.14, bf16[384,384]{1,0:T(8,128)(2,1)S(1)} %copy-done.3), kind=kOutput, calls=%fused_computation.50 | convolution fusion | flops 75792384 | bytes 884736 | tf_op jit(solution)/shard_map/ftc,cd->ftd/dot_general | solution.py:140
  76.7 1.6 %collective-permute-start.13 = (bf16[1,256,384]{2,1,0:T(8,128)(2,1)}, bf16[1,256,384]{2,1,0:T(8,128)(2,1)S(1)}, u32[]{:S(2)}, u32[]{:S(2)}) collective-permute-start(bf16[1,256,384]{2,1,0:T(8,128)(2,1)} %collective-permute-done.11), channel_id=1, source_target_pairs={{0,2},{2,4},{4,6},{6,7},{7,5},{5,3},{3,1},{1,0},{8,10},{10,12},{12... | collective-permute-start | bytes 589832 | tf_op jit(solution)/shard_map/ppermute | solution.py:33
  78.4 0.4 collective-permute-start.14
  78.8 1.6 %constant_dynamic-update-slice_fusion.16 = bf16[1,2048,384]{2,1,0:T(8,128)(2,1)} fusion(bf16[1,2048,384]{2,1,0:T(8,128)(2,1)} %constant_dynamic-update-slice_fusion.17, bf16[1,256,384]{2,1,0:T(8,128)(2,1)} %collective-permute-done.11), kind=kLoop, calls=%fused_computation.122 | loop fusion | bytes 393216
  80.4 1.6 %constant_dynamic-update-slice_fusion.15 = bf16[1,2048,384]{2,1,0:T(8,128)(2,1)} fusion(bf16[1,2048,384]{2,1,0:T(8,128)(2,1)} %constant_dynamic-update-slice_fusion.16, bf16[1,256,384]{2,1,0:T(8,128)(2,1)} %collective-permute-done.12), kind=kLoop, calls=%fused_computation.121 | loop fusion | bytes 393216
  82.1 1.8 %collective-permute-done.13 = bf16[1,256,384]{2,1,0:T(8,128)(2,1)S(1)} collective-permute-done((bf16[1,256,384]{2,1,0:T(8,128)(2,1)}, bf16[1,256,384]{2,1,0:T(8,128)(2,1)S(1)}, u32[]{:S(2)}, u32[]{:S(2)}) %collective-permute-start.13) | collective-permute-done | bytes 196640 | tf_op jit(solution)/shard_map/ppermute | solution.py:33
  83.8 1.6 %collective-permute-start.15 = (bf16[1,256,384]{2,1,0:T(8,128)(2,1)S(1)}, bf16[1,256,384]{2,1,0:T(8,128)(2,1)S(1)}, u32[]{:S(2)}, u32[]{:S(2)}) collective-permute-start(bf16[1,256,384]{2,1,0:T(8,128)(2,1)S(1)} %collective-permute-done.13), channel_id=1, source_target_pairs={{0,2},{2,4},{4,6},{6,7},{7,5},{5,3},{3,1},{1,0},{8,10},{10,12},{12... | collective-permute-start | bytes 589832 | tf_op jit(solution)/shard_map/ppermute | solution.py:33
  85.9 0.7 constant_dynamic-update-slice_fusion.14
  86.6 0.7 constant_dynamic-update-slice_fusion.13
  87.3 2.2 %collective-permute-done.15 = bf16[1,256,384]{2,1,0:T(8,128)(2,1)S(1)} collective-permute-done((bf16[1,256,384]{2,1,0:T(8,128)(2,1)S(1)}, bf16[1,256,384]{2,1,0:T(8,128)(2,1)S(1)}, u32[]{:S(2)}, u32[]{:S(2)}) %collective-permute-start.15) | collective-permute-done | bytes 196640 | tf_op jit(solution)/shard_map/ppermute | solution.py:33
  89.5 1.6 %collective-permute-start.17 = (bf16[1,128,384]{2,1,0:T(8,128)(2,1)S(1)}, bf16[1,128,384]{2,1,0:T(8,128)(2,1)S(1)}, u32[]{:S(2)}, u32[]{:S(2)}) collective-permute-start(bf16[1,128,384]{2,1,0:T(8,128)(2,1)S(1)} %slice.80), channel_id=1, source_target_pairs={{0,2},{2,4},{4,6},{6,7},{7,5},{5,3},{3,1},{1,0},{8,10},{10,12},{12... | collective-permute-start | bytes 294920 | tf_op jit(solution)/shard_map/ppermute | solution.py:38
  91.2 0.7 collective-permute-start.18
  91.9 0.7 constant_dynamic-update-slice_fusion.12
  92.6 0.7 constant_dynamic-update-slice_fusion.11
  93.3 0.9 collective-permute-done.17
  94.2 0.7 constant_dynamic-update-slice_fusion.10
  94.8 1.2 %collective-permute-done.18 = bf16[1,128,384]{2,1,0:T(8,128)(2,1)S(1)} collective-permute-done((bf16[1,128,384]{2,1,0:T(8,128)(2,1)S(1)}, bf16[1,128,384]{2,1,0:T(8,128)(2,1)S(1)}, u32[]{:S(2)}, u32[]{:S(2)}) %collective-permute-start.18) | collective-permute-done | bytes 98336 | tf_op jit(solution)/shard_map/ppermute | solution.py:39
  96.1 0.6 constant_dynamic-update-slice_fusion.9
  96.7 3.3 %fusion.115 = (f32[256]{0:T(256)S(1)}, f32[256,2048]{1,0:T(8,128)S(1)}) fusion(bf16[256,384]{1,0:T(8,128)(2,1)} %convolution_convert_fusion.4, bf16[384,384]{1,0:T(8,128)(2,1)S(1)} %copy-done, bf16[1,2048,384]{2,1,0:T(8,128)(2,1)} %constant_dynamic-update-slice_fusion.9), kind=kOutput, calls=%fused_computation.166 | convolution fusion | flops 1008467712 | bytes 4162560 | tf_op jit(solution)/shard_map/fqc,fkc->fqk/dot_general | solution.py:127
  100.0 0.4 fusion.4
  100.4 3.1 %fusion.48 = bf16[256,384]{1,0:T(8,128)(2,1)S(1)} fusion(bf16[384,384]{1,0:T(8,128)(2,1)} %param.18, bf16[1,2048,384]{2,1,0:T(8,128)(2,1)} %constant_dynamic-update-slice_fusion.9, f32[256,2048]{1,0:T(8,128)S(1)} %get-tuple-element.26, f32[256]{0:T(256)S(1)} %get-tuple-element.25, f32[256]{0:T(256)S(1)} %fusion.4), kind=kOutput, calls=%fused_computation.52 | convolution fusion | flops 1008664576 | bytes 4163584 | tf_op jit(solution)/shard_map/fqk,fkc->fqc/dot_general | solution.py:133
  103.8 0.8 pad_maximum_fusion.1
  (73 shorter events, 5.4 us)
Async XLA Ops:
  0.0 68.1 %copy-start = (bf16[384,384]{1,0:T(8,128)(2,1)S(1)}, bf16[384,384]{1,0:T(8,128)(2,1)}, u32[]{:S(2)}) copy-start(bf16[384,384]{1,0:T(8,128)(2,1)} %param.17) | copy-start | bytes 884740
  0.0 14.5 %copy-start.1 = (bf16[2,2,128,384]{3,2,1,0:T(8,128)(2,1)S(1)}, bf16[2,2,128,384]{3,2,1,0:T(8,128)(2,1)}, u32[]{:S(2)}) copy-start(bf16[2,2,128,384]{3,2,1,0:T(8,128)(2,1)} %param.10) | copy-start | bytes 1179652
  0.0 14.5 %copy-start.8 = (f32[384]{0:T(512)S(1)}, f32[384]{0:T(512)}, u32[]{:S(2)}) copy-start(f32[384]{0:T(512)} %param.12) | copy-start | bytes 4612
  1.1 9.1 %collective-permute-start = (bf16[2,1,128,384]{3,2,1,0:T(8,128)(2,1)S(1)}, bf16[2,1,128,384]{3,2,1,0:T(8,128)(2,1)S(1)}, u32[]{:S(2)}, u32[]{:S(2)}) collective-permute-start(bf16[2,1,128,384]{3,2,1,0:T(8,128)(2,1)S(1)} %get-tuple-element.19), channel_id=1, source_target_pairs={{0,1},{1,2},{2,3},{3,4},{4,5},{5,6},{6,7},{8,9},{9,10},{10,11},{11... | collective-permute-start | bytes 589832 | tf_op jit(solution)/shard_map/ppermute | solution.py:15
  6.0 8.3 %collective-permute-start.1 = (bf16[2,1,128,384]{3,2,1,0:T(8,128)(2,1)S(1)}, bf16[2,1,128,384]{3,2,1,0:T(8,128)(2,1)S(1)}, u32[]{:S(2)}, u32[]{:S(2)}) collective-permute-start(bf16[2,1,128,384]{3,2,1,0:T(8,128)(2,1)S(1)} %get-tuple-element.20), channel_id=1, source_target_pairs={{1,0},{2,1},{3,2},{4,3},{5,4},{6,5},{7,6},{9,8},{10,9},{11,10},{12... | collective-permute-start | bytes 589832 | tf_op jit(solution)/shard_map/ppermute | solution.py:17
  15.0 0.7 copy-start.7
  15.3 0.9 copy-start.2
  15.3 2.6 %collective-permute-start.2 = (bf16[2,4,130,384]{3,2,1,0:T(8,128)(2,1)S(1)}, bf16[2,4,130,384]{3,2,1,0:T(8,128)(2,1)}, u32[]{:S(2)}, u32[]{:S(2)}) collective-permute-start(bf16[2,4,130,384]{3,2,1,0:T(8,128)(2,1)S(1)} %fusion.65), channel_id=1, source_target_pairs={{0,8},{8,0},{1,9},{9,1},{2,10},{10,2},{3,11},{11,3},{4,12},{12,4},... | collective-permute-start | bytes 2396168 | tf_op jit(solution)/shard_map/ppermute | solution.py:76
  22.1 3.7 %slice-start = ((s8[7962624]{0:T(1024)(128)(4,1)}), s8[4194304]{0:T(1024)(128)(4,1)S(1)}, s32[]{:S(2)}) async-start(s8[7962624]{0:T(1024)(128)(4,1)} %bitcast.122), calls=%async_computation | async-start | bytes 8388608
  24.3 2.3 %slice-start.1 = ((s8[7962624]{0:T(1024)(128)(4,1)}), s8[3768320]{0:T(1024)(128)(4,1)S(1)}, s32[]{:S(2)}) async-start(s8[7962624]{0:T(1024)(128)(4,1)} %bitcast.122), calls=%async_computation.1 | async-start | bytes 7536640
  25.5 1.0 copy-start.9
  29.8 0.7 copy-start.5
  29.8 0.8 copy-start.6
  29.8 5.2 %copy-start.4 = (bf16[384,384]{1,0:T(8,128)(2,1)S(1)}, bf16[384,384]{1,0:T(8,128)(2,1)}, u32[]{:S(2)}) copy-start(bf16[384,384]{1,0:T(8,128)(2,1)} %param.16) | copy-start | bytes 884740
  31.4 8.0 %collective-permute-start.3 = (bf16[1,256,384]{2,1,0:T(8,128)(2,1)S(1)}, bf16[1,256,384]{2,1,0:T(8,128)(2,1)S(1)}, u32[]{:S(2)}, u32[]{:S(2)}) collective-permute-start(bf16[1,256,384]{2,1,0:T(8,128)(2,1)S(1)} %bitcast.115), channel_id=1, source_target_pairs={{0,2},{2,4},{4,6},{6,7},{7,5},{5,3},{3,1},{1,0},{8,10},{10,12},{12... | collective-permute-start | bytes 589832 | tf_op jit(solution)/shard_map/ppermute | solution.py:33
  35.0 12.6 %collective-permute-start.4 = (bf16[1,256,384]{2,1,0:T(8,128)(2,1)S(1)}, bf16[1,256,384]{2,1,0:T(8,128)(2,1)S(1)}, u32[]{:S(2)}, u32[]{:S(2)}) collective-permute-start(bf16[1,256,384]{2,1,0:T(8,128)(2,1)S(1)} %bitcast.116), channel_id=1, source_target_pairs={{0,1},{2,0},{4,2},{6,4},{7,6},{5,7},{3,5},{1,3},{8,9},{10,8},{12,1... | collective-permute-start | bytes 589832 | tf_op jit(solution)/shard_map/ppermute | solution.py:34
  45.0 6.2 %collective-permute-start.5 = (bf16[1,256,384]{2,1,0:T(8,128)(2,1)S(1)}, bf16[1,256,384]{2,1,0:T(8,128)(2,1)S(1)}, u32[]{:S(2)}, u32[]{:S(2)}) collective-permute-start(bf16[1,256,384]{2,1,0:T(8,128)(2,1)S(1)} %collective-permute-done.3), channel_id=1, source_target_pairs={{0,2},{2,4},{4,6},{6,7},{7,5},{5,3},{3,1},{1,0},{8,10},{10,12},{12... | collective-permute-start | bytes 589832 | tf_op jit(solution)/shard_map/ppermute | solution.py:33
  47.6 6.0 %collective-permute-start.6 = (bf16[1,256,384]{2,1,0:T(8,128)(2,1)S(1)}, bf16[1,256,384]{2,1,0:T(8,128)(2,1)S(1)}, u32[]{:S(2)}, u32[]{:S(2)}) collective-permute-start(bf16[1,256,384]{2,1,0:T(8,128)(2,1)S(1)} %collective-permute-done.4), channel_id=1, source_target_pairs={{0,1},{2,0},{4,2},{6,4},{7,6},{5,7},{3,5},{1,3},{8,9},{10,8},{12,1... | collective-permute-start | bytes 589832 | tf_op jit(solution)/shard_map/ppermute | solution.py:34
  51.2 5.7 %collective-permute-start.7 = (bf16[1,256,384]{2,1,0:T(8,128)(2,1)S(1)}, bf16[1,256,384]{2,1,0:T(8,128)(2,1)S(1)}, u32[]{:S(2)}, u32[]{:S(2)}) collective-permute-start(bf16[1,256,384]{2,1,0:T(8,128)(2,1)S(1)} %collective-permute-done.5), channel_id=1, source_target_pairs={{0,2},{2,4},{4,6},{6,7},{7,5},{5,3},{3,1},{1,0},{8,10},{10,12},{12... | collective-permute-start | bytes 589832 | tf_op jit(solution)/shard_map/ppermute | solution.py:33
  53.6 5.8 %collective-permute-start.8 = (bf16[1,256,384]{2,1,0:T(8,128)(2,1)S(1)}, bf16[1,256,384]{2,1,0:T(8,128)(2,1)S(1)}, u32[]{:S(2)}, u32[]{:S(2)}) collective-permute-start(bf16[1,256,384]{2,1,0:T(8,128)(2,1)S(1)} %collective-permute-done.6), channel_id=1, source_target_pairs={{0,1},{2,0},{4,2},{6,4},{7,6},{5,7},{3,5},{1,3},{8,9},{10,8},{12,1... | collective-permute-start | bytes 589832 | tf_op jit(solution)/shard_map/ppermute | solution.py:34
  56.9 4.7 %collective-permute-start.9 = (bf16[1,128,384]{2,1,0:T(8,128)(2,1)S(1)}, bf16[1,128,384]{2,1,0:T(8,128)(2,1)S(1)}, u32[]{:S(2)}, u32[]{:S(2)}) collective-permute-start(bf16[1,128,384]{2,1,0:T(8,128)(2,1)S(1)} %slice.76), channel_id=1, source_target_pairs={{0,2},{2,4},{4,6},{6,7},{7,5},{5,3},{3,1},{1,0},{8,10},{10,12},{12... | collective-permute-start | bytes 294920 | tf_op jit(solution)/shard_map/ppermute | solution.py:38
  59.4 4.7 %collective-permute-start.10 = (bf16[1,128,384]{2,1,0:T(8,128)(2,1)S(1)}, bf16[1,128,384]{2,1,0:T(8,128)(2,1)S(1)}, u32[]{:S(2)}, u32[]{:S(2)}) collective-permute-start(bf16[1,128,384]{2,1,0:T(8,128)(2,1)S(1)} %slice.77), channel_id=1, source_target_pairs={{0,1},{2,0},{4,2},{6,4},{7,6},{5,7},{3,5},{1,3},{8,9},{10,8},{12,1... | collective-permute-start | bytes 294920 | tf_op jit(solution)/shard_map/ppermute | solution.py:39
  64.8 12.0 %collective-permute-start.11 = (bf16[1,256,384]{2,1,0:T(8,128)(2,1)S(1)}, bf16[1,256,384]{2,1,0:T(8,128)(2,1)}, u32[]{:S(2)}, u32[]{:S(2)}) collective-permute-start(bf16[1,256,384]{2,1,0:T(8,128)(2,1)S(1)} %bitcast.112), channel_id=1, source_target_pairs={{0,2},{2,4},{4,6},{6,7},{7,5},{5,3},{3,1},{1,0},{8,10},{10,12},{12... | collective-permute-start | bytes 589832 | tf_op jit(solution)/shard_map/ppermute | solution.py:33
  66.3 12.0 %collective-permute-start.12 = (bf16[1,256,384]{2,1,0:T(8,128)(2,1)S(1)}, bf16[1,256,384]{2,1,0:T(8,128)(2,1)}, u32[]{:S(2)}, u32[]{:S(2)}) collective-permute-start(bf16[1,256,384]{2,1,0:T(8,128)(2,1)S(1)} %bitcast.113), channel_id=1, source_target_pairs={{0,1},{2,0},{4,2},{6,4},{7,6},{5,7},{3,5},{1,3},{8,9},{10,8},{12,1... | collective-permute-start | bytes 589832 | tf_op jit(solution)/shard_map/ppermute | solution.py:34
  71.7 3.8 %copy-start.3 = (bf16[384,384]{1,0:T(8,128)(2,1)S(1)}, bf16[384,384]{1,0:T(8,128)(2,1)}, u32[]{:S(2)}) copy-start(bf16[384,384]{1,0:T(8,128)(2,1)} %param.19) | copy-start | bytes 884740
  76.7 7.1 %collective-permute-start.13 = (bf16[1,256,384]{2,1,0:T(8,128)(2,1)}, bf16[1,256,384]{2,1,0:T(8,128)(2,1)S(1)}, u32[]{:S(2)}, u32[]{:S(2)}) collective-permute-start(bf16[1,256,384]{2,1,0:T(8,128)(2,1)} %collective-permute-done.11), channel_id=1, source_target_pairs={{0,2},{2,4},{4,6},{6,7},{7,5},{5,3},{3,1},{1,0},{8,10},{10,12},{12... | collective-permute-start | bytes 589832 | tf_op jit(solution)/shard_map/ppermute | solution.py:33
  78.4 7.1 %collective-permute-start.14 = (bf16[1,256,384]{2,1,0:T(8,128)(2,1)}, bf16[1,256,384]{2,1,0:T(8,128)(2,1)S(1)}, u32[]{:S(2)}, u32[]{:S(2)}) collective-permute-start(bf16[1,256,384]{2,1,0:T(8,128)(2,1)} %collective-permute-done.12), channel_id=1, source_target_pairs={{0,1},{2,0},{4,2},{6,4},{7,6},{5,7},{3,5},{1,3},{8,9},{10,8},{12,1... | collective-permute-start | bytes 589832 | tf_op jit(solution)/shard_map/ppermute | solution.py:34
  83.8 5.7 %collective-permute-start.15 = (bf16[1,256,384]{2,1,0:T(8,128)(2,1)S(1)}, bf16[1,256,384]{2,1,0:T(8,128)(2,1)S(1)}, u32[]{:S(2)}, u32[]{:S(2)}) collective-permute-start(bf16[1,256,384]{2,1,0:T(8,128)(2,1)S(1)} %collective-permute-done.13), channel_id=1, source_target_pairs={{0,2},{2,4},{4,6},{6,7},{7,5},{5,3},{3,1},{1,0},{8,10},{10,12},{12... | collective-permute-start | bytes 589832 | tf_op jit(solution)/shard_map/ppermute | solution.py:33
  85.4 5.7 %collective-permute-start.16 = (bf16[1,256,384]{2,1,0:T(8,128)(2,1)S(1)}, bf16[1,256,384]{2,1,0:T(8,128)(2,1)S(1)}, u32[]{:S(2)}, u32[]{:S(2)}) collective-permute-start(bf16[1,256,384]{2,1,0:T(8,128)(2,1)S(1)} %collective-permute-done.14), channel_id=1, source_target_pairs={{0,1},{2,0},{4,2},{6,4},{7,6},{5,7},{3,5},{1,3},{8,9},{10,8},{12,1... | collective-permute-start | bytes 589832 | tf_op jit(solution)/shard_map/ppermute | solution.py:34
  89.5 4.7 %collective-permute-start.17 = (bf16[1,128,384]{2,1,0:T(8,128)(2,1)S(1)}, bf16[1,128,384]{2,1,0:T(8,128)(2,1)S(1)}, u32[]{:S(2)}, u32[]{:S(2)}) collective-permute-start(bf16[1,128,384]{2,1,0:T(8,128)(2,1)S(1)} %slice.80), channel_id=1, source_target_pairs={{0,2},{2,4},{4,6},{6,7},{7,5},{5,3},{3,1},{1,0},{8,10},{10,12},{12... | collective-permute-start | bytes 294920 | tf_op jit(solution)/shard_map/ppermute | solution.py:38
  91.2 4.9 %collective-permute-start.18 = (bf16[1,128,384]{2,1,0:T(8,128)(2,1)S(1)}, bf16[1,128,384]{2,1,0:T(8,128)(2,1)S(1)}, u32[]{:S(2)}, u32[]{:S(2)}) collective-permute-start(bf16[1,128,384]{2,1,0:T(8,128)(2,1)S(1)} %slice.81), channel_id=1, source_target_pairs={{0,1},{2,0},{4,2},{6,4},{7,6},{5,7},{3,5},{1,3},{8,9},{10,8},{12,1... | collective-permute-start | bytes 294920 | tf_op jit(solution)/shard_map/ppermute | solution.py:39

commit v19 on v15

--- a/solution.py
+++ b/solution.py
@@ -110,8 +110,9 @@
         ).astype(jnp.bfloat16)
         pieces = ring_gather(tokens, "height", 1)
         if span + 1 < span_count:
-            pieces[1], span_window = lax.optimization_barrier(
-                (pieces[1], window[span + 1 : span + 2])
+            tie = min(3, len(pieces) - 1)
+            pieces[tie], span_window = lax.optimization_barrier(
+                (pieces[tie], window[span + 1 : span + 2])
             )
         tokens_all = jnp.concatenate(pieces, axis=1)
         keys_all = jnp.einsum(

time: 96.8 us -> 99.8 us (1.031)
  waiting for transfers between devices: 19 us -> 20.9 us
  local copies, waits for them, and re-layouts: 23.3 us -> 24.8 us
    unnamed x44, local copies, waits for them, and re-layouts: 14 us -> 17.3 us
    ppermute x6, starting transfers between devices: 5.98 us -> 4.36 us  [ring_gather(): forward = lax.ppermute(forward, axis, ahead)]
    ppermute x6, starting transfers between devices: 6.87 us -> 8.38 us  [ring_gather(): backward = lax.ppermute(backward, axis, behind)]
  transfers between devices with their start and end apart: 19 -> 19, of which waited for: 7 -> 9; matrix products, arithmetic and copies ran while one was open for 30% -> 30% of each run, Pallas kernels for 0% -> 0%
where the time goes in v19:
time: 99.8 us; the launch traced here: 99.3 us
  local copies, waits for them, and re-layouts  24.8 us (25%)
  starting transfers between devices  24.1 us (24%)
  waiting for transfers between devices  20.9 us (21%)
  matrix products  20.7 us (21%)
  other arithmetic  8.4 us (8%)
    unnamed x44, local copies, waits for them, and re-layouts  17.3 us
    ppermute x6, waiting for transfers between devices, ring_gather(): forward = lax.ppermute(forward, axis, ahead)  11.8 us
    ppermute x6, starting transfers between devices, ring_gather(): backward = lax.ppermute(backward, axis, behind)  8.38 us
    conv_general_dilated x2, matrix products, shards(): lax.conv_general_dilated(span_window, conv_weight, window_strides=(1, 1,...  6.34 us
    dot_general x2, matrix products, shards(): jnp.einsum('fqc,fkc->fqk', queries, keys_all, preferred_element_type=jnp....  6.3 us
    dot_general x2, matrix products, shards(): jnp.einsum('fqk,fkc->fqc', weights_exp.astype(jnp.bfloat16), values_all,...  6.28 us
    ppermute x1, starting transfers between devices, padded_2(): lax.ppermute(tail, axis, [(i, (i + 1) % count) for i in range(ends)])  5.52 us
    ppermute x1, waiting for transfers between devices, padded_2(): lax.ppermute(tail, axis, [(i, (i + 1) % count) for i in range(ends)])  4.36 us
  transfers between devices with their start and end apart: 19, of which 9 were waited for; matrix products, arithmetic and copies ran while one was open for 30% of the time, Pallas kernels for 0%

profile of v19, /device:TPU:0, one launch (start us, length us, event | category | flops | bytes accessed | tf_op | source)
XLA Modules:
  0.0 99.3 jit_solution(12293062263654021964)
XLA Ops:
  0.0 1.1 %fusion.114 = (bf16[2,1,128,384]{3,2,1,0:T(8,128)(2,1)S(1)}, bf16[2,1,128,384]{3,2,1,0:T(8,128)(2,1)S(1)}) fusion(bf16[2,2,128,384]{3,2,1,0:T(8,128)(2,1)} %param.10), kind=kLoop, calls=%fused_computation.165 | loop fusion | bytes 786432 | tf_op jit(solution)/shard_map/slice | solution.py:12
  1.1 1.3 %collective-permute-start.1 = (bf16[2,1,128,384]{3,2,1,0:T(8,128)(2,1)S(1)}, bf16[2,1,128,384]{3,2,1,0:T(8,128)(2,1)S(1)}, u32[]{:S(2)}, u32[]{:S(2)}) collective-permute-start(bf16[2,1,128,384]{3,2,1,0:T(8,128)(2,1)S(1)} %get-tuple-element.18), channel_id=1, source_target_pairs={{1,0},{2,1},{3,2},{4,3},{5,4},{6,5},{7,6},{9,8},{10,9},{11,10},{12... | collective-permute-start | bytes 589832 | tf_op jit(solution)/shard_map/ppermute | solution.py:17
  2.4 5.5 %collective-permute-start = (bf16[2,1,128,384]{3,2,1,0:T(8,128)(2,1)S(1)}, bf16[2,1,128,384]{3,2,1,0:T(8,128)(2,1)S(1)}, u32[]{:S(2)}, u32[]{:S(2)}) collective-permute-start(bf16[2,1,128,384]{3,2,1,0:T(8,128)(2,1)S(1)} %get-tuple-element.17), channel_id=1, source_target_pairs={{0,1},{1,2},{2,3},{3,4},{4,5},{5,6},{6,7},{8,9},{9,10},{10,11},{11... | collective-permute-start | bytes 589832 | tf_op jit(solution)/shard_map/ppermute | solution.py:15
  8.0 1.1 %fusion.74 = f32[2,2,128]{2,1,0:T(2,128)S(1)} fusion(bf16[2,2,128,384]{3,2,1,0:T(8,128)(2,1)} %param.10), kind=kLoop, calls=%fused_computation.74 | loop fusion | flops 589312 | bytes 395264 | tf_op jit(solution)/shard_map/reduce_sum | solution.py:48
  9.1 1.8 %collective-permute-done.1 = bf16[2,1,128,384]{3,2,1,0:T(8,128)(2,1)S(1)} collective-permute-done((bf16[2,1,128,384]{3,2,1,0:T(8,128)(2,1)S(1)}, bf16[2,1,128,384]{3,2,1,0:T(8,128)(2,1)S(1)}, u32[]{:S(2)}, u32[]{:S(2)}) %collective-permute-start.1) | collective-permute-done | bytes 196640 | tf_op jit(solution)/shard_map/ppermute | solution.py:17
  10.9 4.4 %collective-permute-done = bf16[2,1,128,384]{3,2,1,0:T(8,128)(2,1)S(1)} collective-permute-done((bf16[2,1,128,384]{3,2,1,0:T(8,128)(2,1)S(1)}, bf16[2,1,128,384]{3,2,1,0:T(8,128)(2,1)S(1)}, u32[]{:S(2)}, u32[]{:S(2)}) %collective-permute-start) | collective-permute-done | bytes 196640 | tf_op jit(solution)/shard_map/ppermute | solution.py:15
  15.5 0.5 fusion.81
  17.2 1.6 %collective-permute-done.2 = bf16[2,4,130,384]{3,2,1,0:T(8,128)(2,1)} collective-permute-done((bf16[2,4,130,384]{3,2,1,0:T(8,128)(2,1)S(1)}, bf16[2,4,130,384]{3,2,1,0:T(8,128)(2,1)}, u32[]{:S(2)}, u32[]{:S(2)}) %collective-permute-start.2) | collective-permute-done | bytes 798752 | tf_op jit(solution)/shard_map/ppermute | solution.py:76
  18.9 1.7 %maximum_maximum_fusion = bf16[5,4,130,384]{3,2,1,0:T(8,128)(2,1)S(1)} fusion(bf16[2,4,130,384]{3,2,1,0:T(8,128)(2,1)} %collective-permute-done.2, bf16[2,4,130,384]{3,2,1,0:T(8,128)(2,1)} %copy-done.2, bf16[5]{0:T(256)(128)(2,1)S(1)} %pad.17.clone), kind=kLoop, calls=%fused_computation.15 | loop fusion | flops 1996800 | bytes 3594250 | tf_op jit(solution)/shard_map/concatenate | solution.py:79
  20.6 2.5 %gather_fusion = bf16[6,4,130,384]{3,2,1,0:T(8,128)(2,1)} fusion(bf16[5,4,130,384]{3,2,1,0:T(8,128)(2,1)S(1)} %maximum_maximum_fusion, s32[1024]{0:T(1024)S(1)} %pad_clamp_fusion), kind=kCustom, calls=%fused_computation | custom fusion | bytes 4792344 | tf_op jit(solution)/shard_map/jit(_take)/gather | solution.py:88
  23.1 2.2 %broadcast_select_fusion = bf16[6,4,130,384]{3,2,1,0:T(8,128)(2,1)S(1)} fusion(bf16[6,4,130,384]{3,2,1,0:T(8,128)(2,1)} %gather_fusion, pred[6]{0:T(512)(128)(4,1)S(1)} %compare_and_fusion), kind=kLoop, calls=%fused_computation.12 | loop fusion | flops 1198080 | bytes 4792326 | tf_op jit(solution)/shard_map/jit(_take)/select_n | solution.py:88
  25.6 0.5 copy.23
  26.1 0.5 pad.5.clone
  26.8 0.8 slice-done.1
  27.6 3.2 %fusion.38 = f32[1,2,8,17,384]{4,2,3,1,0:T(8,128)S(1)} fusion(bf16[3,3,3,384,384]{4,3,2,1,0:T(8,128)(2,1)S(1)} %bitcast.123, bf16[3,4,1,7,2,384]{5,3,4,1,0,2:T(8,128)(2,1)S(1)} %slice.73, bf16[3,4,1,8,17,384]{5,3,4,1,0,2:T(8,128)(2,1)S(1)} %copy.13, pred[8,17]{0,1:T(8,128)(4,1)S(1)} %copy-done.10), kind=kOutput, calls=%fused_computation.44 | convolution fusion | flops 2170140672 | bytes 9762952 | tf_op jit(solution)/shard_map/conv_general_dilated | solution.py:95
  31.7 1.7 %collective-permute-start.3 = (bf16[1,256,384]{2,1,0:T(8,128)(2,1)S(1)}, bf16[1,256,384]{2,1,0:T(8,128)(2,1)S(1)}, u32[]{:S(2)}, u32[]{:S(2)}) collective-permute-start(bf16[1,256,384]{2,1,0:T(8,128)(2,1)S(1)} %bitcast.114), channel_id=1, source_target_pairs={{0,2},{2,4},{4,6},{6,7},{7,5},{5,3},{3,1},{1,0},{8,10},{10,12},{12... | collective-permute-start | bytes 589832 | tf_op jit(solution)/shard_map/ppermute | solution.py:33
  33.4 0.7 constant_dynamic-update-slice_fusion.8
  34.1 0.8 collective-permute-start.4
  35.2 4.2 %collective-permute-done.3 = bf16[1,256,384]{2,1,0:T(8,128)(2,1)S(1)} collective-permute-done((bf16[1,256,384]{2,1,0:T(8,128)(2,1)S(1)}, bf16[1,256,384]{2,1,0:T(8,128)(2,1)S(1)}, u32[]{:S(2)}, u32[]{:S(2)}) %collective-permute-start.3) | collective-permute-done | bytes 196640 | tf_op jit(solution)/shard_map/ppermute | solution.py:33
  39.5 0.9 collective-permute-start.5
  40.4 0.4 collective-permute-done.4
  40.8 1.1 %collective-permute-start.6 = (bf16[1,256,384]{2,1,0:T(8,128)(2,1)S(1)}, bf16[1,256,384]{2,1,0:T(8,128)(2,1)S(1)}, u32[]{:S(2)}, u32[]{:S(2)}) collective-permute-start(bf16[1,256,384]{2,1,0:T(8,128)(2,1)S(1)} %collective-permute-done.4), channel_id=1, source_target_pairs={{0,1},{2,0},{4,2},{6,4},{7,6},{5,7},{3,5},{1,3},{8,9},{10,8},{12,1... | collective-permute-start | bytes 589832 | tf_op jit(solution)/shard_map/ppermute | solution.py:34
  41.9 0.7 constant_dynamic-update-slice_fusion.7
  42.6 0.7 constant_dynamic-update-slice_fusion.6
  43.3 2.6 %collective-permute-done.5 = bf16[1,256,384]{2,1,0:T(8,128)(2,1)S(1)} collective-permute-done((bf16[1,256,384]{2,1,0:T(8,128)(2,1)S(1)}, bf16[1,256,384]{2,1,0:T(8,128)(2,1)S(1)}, u32[]{:S(2)}, u32[]{:S(2)}) %collective-permute-start.5) | collective-permute-done | bytes 196640 | tf_op jit(solution)/shard_map/ppermute | solution.py:33
  45.9 0.5 copy.24
  46.4 0.5 pad.7.clone
  47.0 3.2 %fusion.35 = f32[1,2,8,17,384]{4,2,3,1,0:T(8,128)S(1)} fusion(bf16[3,3,3,384,384]{4,3,2,1,0:T(8,128)(2,1)S(1)} %bitcast.123, bf16[3,4,1,7,2,384]{5,3,4,1,0,2:T(8,128)(2,1)S(1)} %slice.78, bf16[3,4,1,8,17,384]{5,3,4,1,0,2:T(8,128)(2,1)S(1)} %copy.18, pred[8,17]{0,1:T(8,128)(4,1)S(1)} %copy-done.10), kind=kOutput, calls=%fused_computation.43 | convolution fusion | flops 2170140672 | bytes 9762952 | tf_op jit(solution)/shard_map/conv_general_dilated | solution.py:95
  50.8 0.7 constant_dynamic-update-slice_fusion.17
  51.5 0.6 collective-permute-start.11
  52.1 1.5 %collective-permute-start.12 = (bf16[1,256,384]{2,1,0:T(8,128)(2,1)S(1)}, bf16[1,256,384]{2,1,0:T(8,128)(2,1)}, u32[]{:S(2)}, u32[]{:S(2)}) collective-permute-start(bf16[1,256,384]{2,1,0:T(8,128)(2,1)S(1)} %bitcast.112), channel_id=1, source_target_pairs={{0,1},{2,0},{4,2},{6,4},{7,6},{5,7},{3,5},{1,3},{8,9},{10,8},{12,1... | collective-permute-start | bytes 589832 | tf_op jit(solution)/shard_map/ppermute | solution.py:34
  53.6 0.6 collective-permute-start.7
  54.1 0.9 convolution_convert_fusion.4
  55.1 1.5 %collective-permute-start.8 = (bf16[1,256,384]{2,1,0:T(8,128)(2,1)S(1)}, bf16[1,256,384]{2,1,0:T(8,128)(2,1)S(1)}, u32[]{:S(2)}, u32[]{:S(2)}) collective-permute-start(bf16[1,256,384]{2,1,0:T(8,128)(2,1)S(1)} %collective-permute-done.6), channel_id=1, source_target_pairs={{0,1},{2,0},{4,2},{6,4},{7,6},{5,7},{3,5},{1,3},{8,9},{10,8},{12,1... | collective-permute-start | bytes 589832 | tf_op jit(solution)/shard_map/ppermute | solution.py:34
  56.5 0.7 constant_dynamic-update-slice_fusion.5
  57.2 0.7 constant_dynamic-update-slice_fusion.4
  57.9 3.4 %collective-permute-done.7 = bf16[1,256,384]{2,1,0:T(8,128)(2,1)S(1)} collective-permute-done((bf16[1,256,384]{2,1,0:T(8,128)(2,1)S(1)}, bf16[1,256,384]{2,1,0:T(8,128)(2,1)S(1)}, u32[]{:S(2)}, u32[]{:S(2)}) %collective-permute-start.7) | collective-permute-done | bytes 196640 | tf_op jit(solution)/shard_map/ppermute | solution.py:33
  61.3 0.3 collective-permute-start.9
  61.7 1.8 %collective-permute-start.10 = (bf16[1,128,384]{2,1,0:T(8,128)(2,1)S(1)}, bf16[1,128,384]{2,1,0:T(8,128)(2,1)S(1)}, u32[]{:S(2)}, u32[]{:S(2)}) collective-permute-start(bf16[1,128,384]{2,1,0:T(8,128)(2,1)S(1)} %slice.77), channel_id=1, source_target_pairs={{0,1},{2,0},{4,2},{6,4},{7,6},{5,7},{3,5},{1,3},{8,9},{10,8},{12,1... | collective-permute-start | bytes 294920 | tf_op jit(solution)/shard_map/ppermute | solution.py:39
  63.7 1.7 %constant_dynamic-update-slice_fusion.16 = bf16[1,2048,384]{2,1,0:T(8,128)(2,1)} fusion(bf16[1,2048,384]{2,1,0:T(8,128)(2,1)} %constant_dynamic-update-slice_fusion.17, bf16[1,256,384]{2,1,0:T(8,128)(2,1)} %collective-permute-done.11), kind=kLoop, calls=%fused_computation.122 | loop fusion | bytes 393216
  65.4 1.7 %collective-permute-start.14 = (bf16[1,256,384]{2,1,0:T(8,128)(2,1)}, bf16[1,256,384]{2,1,0:T(8,128)(2,1)}, u32[]{:S(2)}, u32[]{:S(2)}) collective-permute-start(bf16[1,256,384]{2,1,0:T(8,128)(2,1)} %collective-permute-done.12), channel_id=1, source_target_pairs={{0,1},{2,0},{4,2},{6,4},{7,6},{5,7},{3,5},{1,3},{8,9},{10,8},{12,1... | collective-permute-start | bytes 589832 | tf_op jit(solution)/shard_map/ppermute | solution.py:34
  67.1 1.6 %constant_dynamic-update-slice_fusion.15 = bf16[1,2048,384]{2,1,0:T(8,128)(2,1)} fusion(bf16[1,2048,384]{2,1,0:T(8,128)(2,1)} %constant_dynamic-update-slice_fusion.16, bf16[1,256,384]{2,1,0:T(8,128)(2,1)} %collective-permute-done.12), kind=kLoop, calls=%fused_computation.121 | loop fusion | bytes 393216
  68.8 0.7 constant_dynamic-update-slice_fusion.3
  69.5 0.7 constant_dynamic-update-slice_fusion.2
  70.2 0.6 constant_dynamic-update-slice_fusion.1
  70.8 0.6 constant_dynamic-update-slice_fusion
  71.5 3.2 %fusion.118 = (f32[256]{0:T(256)S(1)}, f32[256,2048]{1,0:T(8,128)S(1)}) fusion(bf16[256,384]{1,0:T(8,128)(2,1)S(1)} %convolution_convert_fusion.5, bf16[384,384]{1,0:T(8,128)(2,1)S(1)} %copy-done, bf16[1,2048,384]{2,1,0:T(8,128)(2,1)} %constant_dynamic-update-slice_fusion), kind=kOutput, calls=%fused_computation.167 | convolution fusion | flops 1008467712 | bytes 4162560 | tf_op jit(solution)/shard_map/fqc,fkc->fqk/dot_general | solution.py:125
  74.6 0.4 fusion.2
  75.1 3.2 %fusion.54 = bf16[256,384]{1,0:T(8,128)(2,1)S(1)} fusion(bf16[384,384]{1,0:T(8,128)(2,1)} %param.18, bf16[1,2048,384]{2,1,0:T(8,128)(2,1)} %constant_dynamic-update-slice_fusion, f32[256,2048]{1,0:T(8,128)S(1)} %get-tuple-element.26, f32[256]{0:T(256)S(1)} %get-tuple-element.25, f32[256]{0:T(256)S(1)} %fusion.2), kind=kOutput, calls=%fused_computation.54 | convolution fusion | flops 1008664576 | bytes 4163584 | tf_op jit(solution)/shard_map/fqk,fkc->fqc/dot_general | solution.py:131
  78.6 0.3 collective-permute-start.15
  78.9 1.7 %collective-permute-start.16 = (bf16[1,256,384]{2,1,0:T(8,128)(2,1)}, bf16[1,256,384]{2,1,0:T(8,128)(2,1)S(1)}, u32[]{:S(2)}, u32[]{:S(2)}) collective-permute-start(bf16[1,256,384]{2,1,0:T(8,128)(2,1)} %collective-permute-done.14), channel_id=1, source_target_pairs={{0,1},{2,0},{4,2},{6,4},{7,6},{5,7},{3,5},{1,3},{8,9},{10,8},{12,1... | collective-permute-start | bytes 589832 | tf_op jit(solution)/shard_map/ppermute | solution.py:34
  80.6 1.6 %constant_dynamic-update-slice_fusion.14 = bf16[1,2048,384]{2,1,0:T(8,128)(2,1)} fusion(bf16[1,2048,384]{2,1,0:T(8,128)(2,1)} %constant_dynamic-update-slice_fusion.15, bf16[1,256,384]{2,1,0:T(8,128)(2,1)} %collective-permute-done.13), kind=kLoop, calls=%fused_computation.120 | loop fusion | bytes 393216
  82.3 1.6 %constant_dynamic-update-slice_fusion.13 = bf16[1,2048,384]{2,1,0:T(8,128)(2,1)} fusion(bf16[1,2048,384]{2,1,0:T(8,128)(2,1)} %constant_dynamic-update-slice_fusion.14, bf16[1,256,384]{2,1,0:T(8,128)(2,1)} %collective-permute-done.14), kind=kLoop, calls=%fused_computation.119 | loop fusion | bytes 393216
  83.9 1.7 %collective-permute-done.15 = bf16[1,256,384]{2,1,0:T(8,128)(2,1)S(1)} collective-permute-done((bf16[1,256,384]{2,1,0:T(8,128)(2,1)}, bf16[1,256,384]{2,1,0:T(8,128)(2,1)S(1)}, u32[]{:S(2)}, u32[]{:S(2)}) %collective-permute-start.15) | collective-permute-done | bytes 196640 | tf_op jit(solution)/shard_map/ppermute | solution.py:33
  85.9 2.0 %collective-permute-start.18 = (bf16[1,128,384]{2,1,0:T(8,128)(2,1)S(1)}, bf16[1,128,384]{2,1,0:T(8,128)(2,1)S(1)}, u32[]{:S(2)}, u32[]{:S(2)}) collective-permute-start(bf16[1,128,384]{2,1,0:T(8,128)(2,1)S(1)} %slice.81), channel_id=1, source_target_pairs={{0,1},{2,0},{4,2},{6,4},{7,6},{5,7},{3,5},{1,3},{8,9},{10,8},{12,1... | collective-permute-start | bytes 294920 | tf_op jit(solution)/shard_map/ppermute | solution.py:39
  87.9 0.7 constant_dynamic-update-slice_fusion.12
  88.6 0.7 constant_dynamic-update-slice_fusion.11
  89.3 0.9 collective-permute-done.17
  90.2 0.6 constant_dynamic-update-slice_fusion.10
  90.9 0.7 constant_dynamic-update-slice_fusion.9
  91.5 3.1 %fusion.115 = (f32[256]{0:T(256)S(1)}, f32[256,2048]{1,0:T(8,128)S(1)}) fusion(bf16[256,384]{1,0:T(8,128)(2,1)S(1)} %copy-done.5, bf16[384,384]{1,0:T(8,128)(2,1)S(1)} %copy-done, bf16[1,2048,384]{2,1,0:T(8,128)(2,1)} %constant_dynamic-update-slice_fusion.9), kind=kOutput, calls=%fused_computation.166 | convolution fusion | flops 1008467712 | bytes 4162560 | tf_op jit(solution)/shard_map/fqc,fkc->fqk/dot_general | solution.py:125
  94.7 0.4 fusion.4
  95.1 3.1 %fusion.48 = bf16[256,384]{1,0:T(8,128)(2,1)S(1)} fusion(bf16[384,384]{1,0:T(8,128)(2,1)} %param.18, bf16[1,2048,384]{2,1,0:T(8,128)(2,1)} %constant_dynamic-update-slice_fusion.9, f32[256,2048]{1,0:T(8,128)S(1)} %get-tuple-element.24, f32[256]{0:T(256)S(1)} %get-tuple-element.23, f32[256]{0:T(256)S(1)} %fusion.4), kind=kOutput, calls=%fused_computation.52 | convolution fusion | flops 1008664576 | bytes 4163584 | tf_op jit(solution)/shard_map/fqk,fkc->fqc/dot_general | solution.py:131
  98.5 0.8 pad_maximum_fusion.1
  (75 shorter events, 5.1 us)
Async XLA Ops:
  0.0 71.5 %copy-start = (bf16[384,384]{1,0:T(8,128)(2,1)S(1)}, bf16[384,384]{1,0:T(8,128)(2,1)}, u32[]{:S(2)}) copy-start(bf16[384,384]{1,0:T(8,128)(2,1)} %param.17) | copy-start | bytes 884740
  0.0 15.4 %copy-start.1 = (bf16[2,2,128,384]{3,2,1,0:T(8,128)(2,1)S(1)}, bf16[2,2,128,384]{3,2,1,0:T(8,128)(2,1)}, u32[]{:S(2)}) copy-start(bf16[2,2,128,384]{3,2,1,0:T(8,128)(2,1)} %param.10) | copy-start | bytes 1179652
  0.0 15.5 %copy-start.9 = (f32[384]{0:T(512)S(1)}, f32[384]{0:T(512)}, u32[]{:S(2)}) copy-start(f32[384]{0:T(512)} %param.12) | copy-start | bytes 4612
  1.1 9.8 %collective-permute-start.1 = (bf16[2,1,128,384]{3,2,1,0:T(8,128)(2,1)S(1)}, bf16[2,1,128,384]{3,2,1,0:T(8,128)(2,1)S(1)}, u32[]{:S(2)}, u32[]{:S(2)}) collective-permute-start(bf16[2,1,128,384]{3,2,1,0:T(8,128)(2,1)S(1)} %get-tuple-element.18), channel_id=1, source_target_pairs={{1,0},{2,1},{3,2},{4,3},{5,4},{6,5},{7,6},{9,8},{10,9},{11,10},{12... | collective-permute-start | bytes 589832 | tf_op jit(solution)/shard_map/ppermute | solution.py:17
  2.4 12.8 %collective-permute-start = (bf16[2,1,128,384]{3,2,1,0:T(8,128)(2,1)S(1)}, bf16[2,1,128,384]{3,2,1,0:T(8,128)(2,1)S(1)}, u32[]{:S(2)}, u32[]{:S(2)}) collective-permute-start(bf16[2,1,128,384]{3,2,1,0:T(8,128)(2,1)S(1)} %get-tuple-element.17), channel_id=1, source_target_pairs={{0,1},{1,2},{2,3},{3,4},{4,5},{5,6},{6,7},{8,9},{9,10},{10,11},{11... | collective-permute-start | bytes 589832 | tf_op jit(solution)/shard_map/ppermute | solution.py:15
  16.0 0.7 copy-start.8
  16.3 0.9 copy-start.2
  16.3 2.6 %collective-permute-start.2 = (bf16[2,4,130,384]{3,2,1,0:T(8,128)(2,1)S(1)}, bf16[2,4,130,384]{3,2,1,0:T(8,128)(2,1)}, u32[]{:S(2)}, u32[]{:S(2)}) collective-permute-start(bf16[2,4,130,384]{3,2,1,0:T(8,128)(2,1)S(1)} %fusion.65), channel_id=1, source_target_pairs={{0,8},{8,0},{1,9},{9,1},{2,10},{10,2},{3,11},{11,3},{4,12},{12,4},... | collective-permute-start | bytes 2396168 | tf_op jit(solution)/shard_map/ppermute | solution.py:76
  23.1 3.7 %slice-start = ((s8[7962624]{0:T(1024)(128)(4,1)}), s8[4194304]{0:T(1024)(128)(4,1)S(1)}, s32[]{:S(2)}) async-start(s8[7962624]{0:T(1024)(128)(4,1)} %bitcast.122), calls=%async_computation | async-start | bytes 8388608
  25.3 2.3 %slice-start.1 = ((s8[7962624]{0:T(1024)(128)(4,1)}), s8[3768320]{0:T(1024)(128)(4,1)S(1)}, s32[]{:S(2)}) async-start(s8[7962624]{0:T(1024)(128)(4,1)} %bitcast.122), calls=%async_computation.1 | async-start | bytes 7536640
  26.5 1.0 %copy-start.10 = (pred[8,17]{0,1:T(8,128)(4,1)S(1)}, pred[8,17]{0,1:T(8,128)(4,1)}, u32[]{:S(2)}) copy-start(pred[8,17]{0,1:T(8,128)(4,1)} %constant.108) | copy-start | bytes 412
  30.7 0.7 copy-start.6
  30.7 0.8 copy-start.7
  30.8 4.2 %copy-start.4 = (bf16[384,384]{1,0:T(8,128)(2,1)S(1)}, bf16[384,384]{1,0:T(8,128)(2,1)}, u32[]{:S(2)}) copy-start(bf16[384,384]{1,0:T(8,128)(2,1)} %param.16) | copy-start | bytes 884740
  31.7 7.7 %collective-permute-start.3 = (bf16[1,256,384]{2,1,0:T(8,128)(2,1)S(1)}, bf16[1,256,384]{2,1,0:T(8,128)(2,1)S(1)}, u32[]{:S(2)}, u32[]{:S(2)}) collective-permute-start(bf16[1,256,384]{2,1,0:T(8,128)(2,1)S(1)} %bitcast.114), channel_id=1, source_target_pairs={{0,2},{2,4},{4,6},{6,7},{7,5},{5,3},{3,1},{1,0},{8,10},{10,12},{12... | collective-permute-start | bytes 589832 | tf_op jit(solution)/shard_map/ppermute | solution.py:33
  34.1 6.7 %collective-permute-start.4 = (bf16[1,256,384]{2,1,0:T(8,128)(2,1)S(1)}, bf16[1,256,384]{2,1,0:T(8,128)(2,1)S(1)}, u32[]{:S(2)}, u32[]{:S(2)}) collective-permute-start(bf16[1,256,384]{2,1,0:T(8,128)(2,1)S(1)} %bitcast.116), channel_id=1, source_target_pairs={{0,1},{2,0},{4,2},{6,4},{7,6},{5,7},{3,5},{1,3},{8,9},{10,8},{12,1... | collective-permute-start | bytes 589832 | tf_op jit(solution)/shard_map/ppermute | solution.py:34
  39.5 6.4 %collective-permute-start.5 = (bf16[1,256,384]{2,1,0:T(8,128)(2,1)S(1)}, bf16[1,256,384]{2,1,0:T(8,128)(2,1)S(1)}, u32[]{:S(2)}, u32[]{:S(2)}) collective-permute-start(bf16[1,256,384]{2,1,0:T(8,128)(2,1)S(1)} %collective-permute-done.3), channel_id=1, source_target_pairs={{0,2},{2,4},{4,6},{6,7},{7,5},{5,3},{3,1},{1,0},{8,10},{10,12},{12... | collective-permute-start | bytes 589832 | tf_op jit(solution)/shard_map/ppermute | solution.py:33
  40.8 14.3 %collective-permute-start.6 = (bf16[1,256,384]{2,1,0:T(8,128)(2,1)S(1)}, bf16[1,256,384]{2,1,0:T(8,128)(2,1)S(1)}, u32[]{:S(2)}, u32[]{:S(2)}) collective-permute-start(bf16[1,256,384]{2,1,0:T(8,128)(2,1)S(1)} %collective-permute-done.4), channel_id=1, source_target_pairs={{0,1},{2,0},{4,2},{6,4},{7,6},{5,7},{3,5},{1,3},{8,9},{10,8},{12,1... | collective-permute-start | bytes 589832 | tf_op jit(solution)/shard_map/ppermute | solution.py:34
  51.5 11.9 %collective-permute-start.11 = (bf16[1,256,384]{2,1,0:T(8,128)(2,1)S(1)}, bf16[1,256,384]{2,1,0:T(8,128)(2,1)}, u32[]{:S(2)}, u32[]{:S(2)}) collective-permute-start(bf16[1,256,384]{2,1,0:T(8,128)(2,1)S(1)} %bitcast.111), channel_id=1, source_target_pairs={{0,2},{2,4},{4,6},{6,7},{7,5},{5,3},{3,1},{1,0},{8,10},{10,12},{12... | collective-permute-start | bytes 589832 | tf_op jit(solution)/shard_map/ppermute | solution.py:33
  52.1 13.3 %collective-permute-start.12 = (bf16[1,256,384]{2,1,0:T(8,128)(2,1)S(1)}, bf16[1,256,384]{2,1,0:T(8,128)(2,1)}, u32[]{:S(2)}, u32[]{:S(2)}) collective-permute-start(bf16[1,256,384]{2,1,0:T(8,128)(2,1)S(1)} %bitcast.112), channel_id=1, source_target_pairs={{0,1},{2,0},{4,2},{6,4},{7,6},{5,7},{3,5},{1,3},{8,9},{10,8},{12,1... | collective-permute-start | bytes 589832 | tf_op jit(solution)/shard_map/ppermute | solution.py:34
  53.6 7.7 %collective-permute-start.7 = (bf16[1,256,384]{2,1,0:T(8,128)(2,1)S(1)}, bf16[1,256,384]{2,1,0:T(8,128)(2,1)S(1)}, u32[]{:S(2)}, u32[]{:S(2)}) collective-permute-start(bf16[1,256,384]{2,1,0:T(8,128)(2,1)S(1)} %collective-permute-done.5), channel_id=1, source_target_pairs={{0,2},{2,4},{4,6},{6,7},{7,5},{5,3},{3,1},{1,0},{8,10},{10,12},{12... | collective-permute-start | bytes 589832 | tf_op jit(solution)/shard_map/ppermute | solution.py:33
  55.1 6.6 %collective-permute-start.8 = (bf16[1,256,384]{2,1,0:T(8,128)(2,1)S(1)}, bf16[1,256,384]{2,1,0:T(8,128)(2,1)S(1)}, u32[]{:S(2)}, u32[]{:S(2)}) collective-permute-start(bf16[1,256,384]{2,1,0:T(8,128)(2,1)S(1)} %collective-permute-done.6), channel_id=1, source_target_pairs={{0,1},{2,0},{4,2},{6,4},{7,6},{5,7},{3,5},{1,3},{8,9},{10,8},{12,1... | collective-permute-start | bytes 589832 | tf_op jit(solution)/shard_map/ppermute | solution.py:34
  61.3 8.9 %collective-permute-start.9 = (bf16[1,128,384]{2,1,0:T(8,128)(2,1)S(1)}, bf16[1,128,384]{2,1,0:T(8,128)(2,1)S(1)}, u32[]{:S(2)}, u32[]{:S(2)}) collective-permute-start(bf16[1,128,384]{2,1,0:T(8,128)(2,1)S(1)} %slice.76), channel_id=1, source_target_pairs={{0,2},{2,4},{4,6},{6,7},{7,5},{5,3},{3,1},{1,0},{8,10},{10,12},{12... | collective-permute-start | bytes 294920 | tf_op jit(solution)/shard_map/ppermute | solution.py:38
  61.7 9.2 %collective-permute-start.10 = (bf16[1,128,384]{2,1,0:T(8,128)(2,1)S(1)}, bf16[1,128,384]{2,1,0:T(8,128)(2,1)S(1)}, u32[]{:S(2)}, u32[]{:S(2)}) collective-permute-start(bf16[1,128,384]{2,1,0:T(8,128)(2,1)S(1)} %slice.77), channel_id=1, source_target_pairs={{0,1},{2,0},{4,2},{6,4},{7,6},{5,7},{3,5},{1,3},{8,9},{10,8},{12,1... | collective-permute-start | bytes 294920 | tf_op jit(solution)/shard_map/ppermute | solution.py:39
  63.5 15.1 %collective-permute-start.13 = (bf16[1,256,384]{2,1,0:T(8,128)(2,1)}, bf16[1,256,384]{2,1,0:T(8,128)(2,1)}, u32[]{:S(2)}, u32[]{:S(2)}) collective-permute-start(bf16[1,256,384]{2,1,0:T(8,128)(2,1)} %collective-permute-done.11), channel_id=1, source_target_pairs={{0,2},{2,4},{4,6},{6,7},{7,5},{5,3},{3,1},{1,0},{8,10},{10,12},{12... | collective-permute-start | bytes 589832 | tf_op jit(solution)/shard_map/ppermute | solution.py:33
  65.4 13.5 %collective-permute-start.14 = (bf16[1,256,384]{2,1,0:T(8,128)(2,1)}, bf16[1,256,384]{2,1,0:T(8,128)(2,1)}, u32[]{:S(2)}, u32[]{:S(2)}) collective-permute-start(bf16[1,256,384]{2,1,0:T(8,128)(2,1)} %collective-permute-done.12), channel_id=1, source_target_pairs={{0,1},{2,0},{4,2},{6,4},{7,6},{5,7},{3,5},{1,3},{8,9},{10,8},{12,1... | collective-permute-start | bytes 589832 | tf_op jit(solution)/shard_map/ppermute | solution.py:34
  75.1 3.2 %copy-start.3 = (bf16[384,384]{1,0:T(8,128)(2,1)S(1)}, bf16[384,384]{1,0:T(8,128)(2,1)}, u32[]{:S(2)}) copy-start(bf16[384,384]{1,0:T(8,128)(2,1)} %param.19) | copy-start | bytes 884740
  78.5 13.0 %copy-start.5 = (bf16[256,384]{1,0:T(8,128)(2,1)S(1)}, bf16[256,384]{1,0:T(8,128)(2,1)}, u32[]{:S(2)}) copy-start(bf16[256,384]{1,0:T(8,128)(2,1)} %convolution_convert_fusion.4) | copy-start | bytes 589828
  78.6 7.0 %collective-permute-start.15 = (bf16[1,256,384]{2,1,0:T(8,128)(2,1)}, bf16[1,256,384]{2,1,0:T(8,128)(2,1)S(1)}, u32[]{:S(2)}, u32[]{:S(2)}) collective-permute-start(bf16[1,256,384]{2,1,0:T(8,128)(2,1)} %collective-permute-done.13), channel_id=1, source_target_pairs={{0,2},{2,4},{4,6},{6,7},{7,5},{5,3},{3,1},{1,0},{8,10},{10,12},{12... | collective-permute-start | bytes 589832 | tf_op jit(solution)/shard_map/ppermute | solution.py:33
  78.9 7.0 %collective-permute-start.16 = (bf16[1,256,384]{2,1,0:T(8,128)(2,1)}, bf16[1,256,384]{2,1,0:T(8,128)(2,1)S(1)}, u32[]{:S(2)}, u32[]{:S(2)}) collective-permute-start(bf16[1,256,384]{2,1,0:T(8,128)(2,1)} %collective-permute-done.14), channel_id=1, source_target_pairs={{0,1},{2,0},{4,2},{6,4},{7,6},{5,7},{3,5},{1,3},{8,9},{10,8},{12,1... | collective-permute-start | bytes 589832 | tf_op jit(solution)/shard_map/ppermute | solution.py:34
  85.6 4.7 %collective-permute-start.17 = (bf16[1,128,384]{2,1,0:T(8,128)(2,1)S(1)}, bf16[1,128,384]{2,1,0:T(8,128)(2,1)S(1)}, u32[]{:S(2)}, u32[]{:S(2)}) collective-permute-start(bf16[1,128,384]{2,1,0:T(8,128)(2,1)S(1)} %slice.80), channel_id=1, source_target_pairs={{0,2},{2,4},{4,6},{6,7},{7,5},{5,3},{3,1},{1,0},{8,10},{10,12},{12... | collective-permute-start | bytes 294920 | tf_op jit(solution)/shard_map/ppermute | solution.py:38
  85.9 5.0 %collective-permute-start.18 = (bf16[1,128,384]{2,1,0:T(8,128)(2,1)S(1)}, bf16[1,128,384]{2,1,0:T(8,128)(2,1)S(1)}, u32[]{:S(2)}, u32[]{:S(2)}) collective-permute-start(bf16[1,128,384]{2,1,0:T(8,128)(2,1)S(1)} %slice.81), channel_id=1, source_target_pairs={{0,1},{2,0},{4,2},{6,4},{7,6},{5,7},{3,5},{1,3},{8,9},{10,8},{12,1... | collective-permute-start | bytes 294920 | tf_op jit(solution)/shard_map/ppermute | solution.py:39

commit v20 on v19

--- a/solution.py
+++ b/solution.py
@@ -110,7 +110,7 @@
         ).astype(jnp.bfloat16)
         pieces = ring_gather(tokens, "height", 1)
         if span + 1 < span_count:
-            tie = min(3, len(pieces) - 1)
+            tie = min(2, len(pieces) - 1)
             pieces[tie], span_window = lax.optimization_barrier(
                 (pieces[tie], window[span + 1 : span + 2])
             )

time: 99.8 us -> 96.4 us (0.966)
  waiting for transfers between devices: 20.9 us -> 18.2 us
  local copies, waits for them, and re-layouts: 24.8 us -> 23.3 us
    ppermute x6, waiting for transfers between devices: 11.8 us -> 6.96 us  [ring_gather(): forward = lax.ppermute(forward, axis, ahead)]
    unnamed x44, local copies, waits for them, and re-layouts: 17.3 us -> 14 us
    ppermute x6, waiting for transfers between devices: 0.44 us -> 3.49 us  [ring_gather(): backward = lax.ppermute(backward, axis, behind)]
    ppermute x6, starting transfers between devices: 4.36 us -> 5.7 us  [ring_gather(): forward = lax.ppermute(forward, axis, ahead)]
    ppermute x2, starting transfers between devices: 0.67 us -> 1.91 us  [ring_gather(): lax.ppermute(lax.slice_in_dim(forward, 0, half, axis=dim), axis, ahead)]
    ppermute x2, starting transfers between devices: 3.81 us -> 2.57 us  [ring_gather(): lax.ppermute(lax.slice_in_dim(backward, half, block.shape[dim], axis=dim)...]
  transfers between devices with their start and end apart: 19 -> 19, of which waited for: 9 -> 7; matrix products, arithmetic and copies ran while one was open for 30% -> 30% of each run, Pallas kernels for 0% -> 0%
where the time goes in v20:
time: 96.4 us; the launch traced here: 95.9 us
  starting transfers between devices  24.7 us (26%)
  local copies, waits for them, and re-layouts  23.3 us (24%)
  matrix products  20.8 us (22%)
  waiting for transfers between devices  18.2 us (19%)
  other arithmetic  8.4 us (9%)
    unnamed x44, local copies, waits for them, and re-layouts  14 us
    ppermute x6, starting transfers between devices, ring_gather(): backward = lax.ppermute(backward, axis, behind)  7.65 us
    ppermute x6, waiting for transfers between devices, ring_gather(): forward = lax.ppermute(forward, axis, ahead)  6.96 us
    dot_general x2, matrix products, shards(): jnp.einsum('fqc,fkc->fqk', queries, keys_all, preferred_element_type=jnp....  6.43 us
    conv_general_dilated x2, matrix products, shards(): lax.conv_general_dilated(span_window, conv_weight, window_strides=(1, 1,...  6.34 us
    dot_general x2, matrix products, shards(): jnp.einsum('fqk,fkc->fqc', weights_exp.astype(jnp.bfloat16), values_all,...  6.27 us
    ppermute x6, starting transfers between devices, ring_gather(): forward = lax.ppermute(forward, axis, ahead)  5.7 us
    ppermute x1, starting transfers between devices, padded_2(): lax.ppermute(tail, axis, [(i, (i + 1) % count) for i in range(ends)])  5.52 us
  transfers between devices with their start and end apart: 19, of which 7 were waited for; matrix products, arithmetic and copies ran while one was open for 30% of the time, Pallas kernels for 0%

profile of v20, /device:TPU:0, one launch (start us, length us, event | category | flops | bytes accessed | tf_op | source)
XLA Modules:
  0.0 95.9 jit_solution(17506331657647610148)
XLA Ops:
  0.0 1.1 %fusion.114 = (bf16[2,1,128,384]{3,2,1,0:T(8,128)(2,1)S(1)}, bf16[2,1,128,384]{3,2,1,0:T(8,128)(2,1)S(1)}) fusion(bf16[2,2,128,384]{3,2,1,0:T(8,128)(2,1)} %param.10), kind=kLoop, calls=%fused_computation.165 | loop fusion | bytes 786432 | tf_op jit(solution)/shard_map/slice | solution.py:12
  1.1 1.3 %collective-permute-start.1 = (bf16[2,1,128,384]{3,2,1,0:T(8,128)(2,1)S(1)}, bf16[2,1,128,384]{3,2,1,0:T(8,128)(2,1)S(1)}, u32[]{:S(2)}, u32[]{:S(2)}) collective-permute-start(bf16[2,1,128,384]{3,2,1,0:T(8,128)(2,1)S(1)} %get-tuple-element.18), channel_id=1, source_target_pairs={{1,0},{2,1},{3,2},{4,3},{5,4},{6,5},{7,6},{9,8},{10,9},{11,10},{12... | collective-permute-start | bytes 589832 | tf_op jit(solution)/shard_map/ppermute | solution.py:17
  2.4 5.5 %collective-permute-start = (bf16[2,1,128,384]{3,2,1,0:T(8,128)(2,1)S(1)}, bf16[2,1,128,384]{3,2,1,0:T(8,128)(2,1)S(1)}, u32[]{:S(2)}, u32[]{:S(2)}) collective-permute-start(bf16[2,1,128,384]{3,2,1,0:T(8,128)(2,1)S(1)} %get-tuple-element.17), channel_id=1, source_target_pairs={{0,1},{1,2},{2,3},{3,4},{4,5},{5,6},{6,7},{8,9},{9,10},{10,11},{11... | collective-permute-start | bytes 589832 | tf_op jit(solution)/shard_map/ppermute | solution.py:15
  8.0 1.1 %fusion.74 = f32[2,2,128]{2,1,0:T(2,128)S(1)} fusion(bf16[2,2,128,384]{3,2,1,0:T(8,128)(2,1)} %param.10), kind=kLoop, calls=%fused_computation.74 | loop fusion | flops 589312 | bytes 395264 | tf_op jit(solution)/shard_map/reduce_sum | solution.py:48
  9.1 1.8 %collective-permute-done.1 = bf16[2,1,128,384]{3,2,1,0:T(8,128)(2,1)S(1)} collective-permute-done((bf16[2,1,128,384]{3,2,1,0:T(8,128)(2,1)S(1)}, bf16[2,1,128,384]{3,2,1,0:T(8,128)(2,1)S(1)}, u32[]{:S(2)}, u32[]{:S(2)}) %collective-permute-start.1) | collective-permute-done | bytes 196640 | tf_op jit(solution)/shard_map/ppermute | solution.py:17
  10.9 4.4 %collective-permute-done = bf16[2,1,128,384]{3,2,1,0:T(8,128)(2,1)S(1)} collective-permute-done((bf16[2,1,128,384]{3,2,1,0:T(8,128)(2,1)S(1)}, bf16[2,1,128,384]{3,2,1,0:T(8,128)(2,1)S(1)}, u32[]{:S(2)}, u32[]{:S(2)}) %collective-permute-start) | collective-permute-done | bytes 196640 | tf_op jit(solution)/shard_map/ppermute | solution.py:15
  15.5 0.5 fusion.81
  16.4 0.3 copy-done.8
  17.2 1.6 %collective-permute-done.2 = bf16[2,4,130,384]{3,2,1,0:T(8,128)(2,1)} collective-permute-done((bf16[2,4,130,384]{3,2,1,0:T(8,128)(2,1)S(1)}, bf16[2,4,130,384]{3,2,1,0:T(8,128)(2,1)}, u32[]{:S(2)}, u32[]{:S(2)}) %collective-permute-start.2) | collective-permute-done | bytes 798752 | tf_op jit(solution)/shard_map/ppermute | solution.py:76
  18.9 1.7 %maximum_maximum_fusion = bf16[5,4,130,384]{3,2,1,0:T(8,128)(2,1)S(1)} fusion(bf16[2,4,130,384]{3,2,1,0:T(8,128)(2,1)} %collective-permute-done.2, bf16[2,4,130,384]{3,2,1,0:T(8,128)(2,1)} %copy-done.2, bf16[5]{0:T(256)(128)(2,1)S(1)} %pad.17.clone), kind=kLoop, calls=%fused_computation.15 | loop fusion | flops 1996800 | bytes 3594250 | tf_op jit(solution)/shard_map/concatenate | solution.py:79
  20.6 2.5 %gather_fusion = bf16[6,4,130,384]{3,2,1,0:T(8,128)(2,1)} fusion(bf16[5,4,130,384]{3,2,1,0:T(8,128)(2,1)S(1)} %maximum_maximum_fusion, s32[1024]{0:T(1024)S(1)} %pad_clamp_fusion), kind=kCustom, calls=%fused_computation | custom fusion | bytes 4792344 | tf_op jit(solution)/shard_map/jit(_take)/gather | solution.py:88
  23.1 2.2 %broadcast_select_fusion = bf16[6,4,130,384]{3,2,1,0:T(8,128)(2,1)S(1)} fusion(bf16[6,4,130,384]{3,2,1,0:T(8,128)(2,1)} %gather_fusion, pred[6]{0:T(512)(128)(4,1)S(1)} %compare_and_fusion), kind=kLoop, calls=%fused_computation.12 | loop fusion | flops 1198080 | bytes 4792326 | tf_op jit(solution)/shard_map/jit(_take)/select_n | solution.py:88
  25.6 0.5 copy.23
  26.1 0.5 pad.5.clone
  26.8 0.8 slice-done.1
  27.6 3.2 %fusion.38 = f32[1,2,8,17,384]{4,2,3,1,0:T(8,128)S(1)} fusion(bf16[3,3,3,384,384]{4,3,2,1,0:T(8,128)(2,1)S(1)} %bitcast.123, bf16[3,4,1,7,2,384]{5,3,4,1,0,2:T(8,128)(2,1)S(1)} %slice.73, bf16[3,4,1,8,17,384]{5,3,4,1,0,2:T(8,128)(2,1)S(1)} %copy.13, pred[8,17]{0,1:T(8,128)(4,1)S(1)} %copy-done.10), kind=kOutput, calls=%fused_computation.44 | convolution fusion | flops 2170140672 | bytes 9762952 | tf_op jit(solution)/shard_map/conv_general_dilated | solution.py:95
  31.1 0.3 copy-done.6
  31.7 2.5 %collective-permute-start.4 = (bf16[1,256,384]{2,1,0:T(8,128)(2,1)S(1)}, bf16[1,256,384]{2,1,0:T(8,128)(2,1)S(1)}, u32[]{:S(2)}, u32[]{:S(2)}) collective-permute-start(bf16[1,256,384]{2,1,0:T(8,128)(2,1)S(1)} %bitcast.110), channel_id=1, source_target_pairs={{0,1},{2,0},{4,2},{6,4},{7,6},{5,7},{3,5},{1,3},{8,9},{10,8},{12,1... | collective-permute-start | bytes 589832 | tf_op jit(solution)/shard_map/ppermute | solution.py:34
  34.2 0.7 constant_dynamic-update-slice_fusion.8
  35.2 3.5 %collective-permute-done.4 = bf16[1,256,384]{2,1,0:T(8,128)(2,1)S(1)} collective-permute-done((bf16[1,256,384]{2,1,0:T(8,128)(2,1)S(1)}, bf16[1,256,384]{2,1,0:T(8,128)(2,1)S(1)}, u32[]{:S(2)}, u32[]{:S(2)}) %collective-permute-start.4) | collective-permute-done | bytes 196640 | tf_op jit(solution)/shard_map/ppermute | solution.py:34
  38.7 0.5 copy.24
  39.2 0.5 pad.7.clone
  39.9 3.2 %fusion.35 = f32[1,2,8,17,384]{4,2,3,1,0:T(8,128)S(1)} fusion(bf16[3,3,3,384,384]{4,3,2,1,0:T(8,128)(2,1)S(1)} %bitcast.123, bf16[3,4,1,7,2,384]{5,3,4,1,0,2:T(8,128)(2,1)S(1)} %slice.78, bf16[3,4,1,8,17,384]{5,3,4,1,0,2:T(8,128)(2,1)S(1)} %copy.18, pred[8,17]{0,1:T(8,128)(4,1)S(1)} %copy-done.10), kind=kOutput, calls=%fused_computation.43 | convolution fusion | flops 2170140672 | bytes 9762952 | tf_op jit(solution)/shard_map/conv_general_dilated | solution.py:95
  43.7 1.7 %collective-permute-start.11 = (bf16[1,256,384]{2,1,0:T(8,128)(2,1)S(1)}, bf16[1,256,384]{2,1,0:T(8,128)(2,1)S(1)}, u32[]{:S(2)}, u32[]{:S(2)}) collective-permute-start(bf16[1,256,384]{2,1,0:T(8,128)(2,1)S(1)} %bitcast.114), channel_id=1, source_target_pairs={{0,2},{2,4},{4,6},{6,7},{7,5},{5,3},{3,1},{1,0},{8,10},{10,12},{12... | collective-permute-start | bytes 589832 | tf_op jit(solution)/shard_map/ppermute | solution.py:33
  45.4 0.9 collective-permute-start.12
  46.3 0.7 constant_dynamic-update-slice_fusion.7
  47.0 0.7 constant_dynamic-update-slice_fusion.6
  47.7 1.1 %collective-permute-start.5 = (bf16[1,256,384]{2,1,0:T(8,128)(2,1)S(1)}, bf16[1,256,384]{2,1,0:T(8,128)(2,1)S(1)}, u32[]{:S(2)}, u32[]{:S(2)}) collective-permute-start(bf16[1,256,384]{2,1,0:T(8,128)(2,1)S(1)} %collective-permute-done.3), channel_id=1, source_target_pairs={{0,2},{2,4},{4,6},{6,7},{7,5},{5,3},{3,1},{1,0},{8,10},{10,12},{12... | collective-permute-start | bytes 589832 | tf_op jit(solution)/shard_map/ppermute | solution.py:33
  48.8 0.9 collective-permute-start.6
  49.7 0.9 convolution_convert_fusion.4
  50.7 1.1 %collective-permute-done.11 = bf16[1,256,384]{2,1,0:T(8,128)(2,1)S(1)} collective-permute-done((bf16[1,256,384]{2,1,0:T(8,128)(2,1)S(1)}, bf16[1,256,384]{2,1,0:T(8,128)(2,1)S(1)}, u32[]{:S(2)}, u32[]{:S(2)}) %collective-permute-start.11) | collective-permute-done | bytes 196640 | tf_op jit(solution)/shard_map/ppermute | solution.py:33
  51.8 1.0 %collective-permute-start.13 = (bf16[1,256,384]{2,1,0:T(8,128)(2,1)S(1)}, bf16[1,256,384]{2,1,0:T(8,128)(2,1)}, u32[]{:S(2)}, u32[]{:S(2)}) collective-permute-start(bf16[1,256,384]{2,1,0:T(8,128)(2,1)S(1)} %collective-permute-done.11), channel_id=1, source_target_pairs={{0,2},{2,4},{4,6},{6,7},{7,5},{5,3},{3,1},{1,0},{8,10},{10,12},{12... | collective-permute-start | bytes 589832 | tf_op jit(solution)/shard_map/ppermute | solution.py:33
  52.8 1.0 %collective-permute-start.14 = (bf16[1,256,384]{2,1,0:T(8,128)(2,1)S(1)}, bf16[1,256,384]{2,1,0:T(8,128)(2,1)}, u32[]{:S(2)}, u32[]{:S(2)}) collective-permute-start(bf16[1,256,384]{2,1,0:T(8,128)(2,1)S(1)} %collective-permute-done.12), channel_id=1, source_target_pairs={{0,1},{2,0},{4,2},{6,4},{7,6},{5,7},{3,5},{1,3},{8,9},{10,8},{12,1... | collective-permute-start | bytes 589832 | tf_op jit(solution)/shard_map/ppermute | solution.py:34
  53.8 2.2 %collective-permute-done.5 = bf16[1,256,384]{2,1,0:T(8,128)(2,1)S(1)} collective-permute-done((bf16[1,256,384]{2,1,0:T(8,128)(2,1)S(1)}, bf16[1,256,384]{2,1,0:T(8,128)(2,1)S(1)}, u32[]{:S(2)}, u32[]{:S(2)}) %collective-permute-start.5) | collective-permute-done | bytes 196640 | tf_op jit(solution)/shard_map/ppermute | solution.py:33
  56.0 1.0 %collective-permute-start.7 = (bf16[1,256,384]{2,1,0:T(8,128)(2,1)S(1)}, bf16[1,256,384]{2,1,0:T(8,128)(2,1)S(1)}, u32[]{:S(2)}, u32[]{:S(2)}) collective-permute-start(bf16[1,256,384]{2,1,0:T(8,128)(2,1)S(1)} %collective-permute-done.5), channel_id=1, source_target_pairs={{0,2},{2,4},{4,6},{6,7},{7,5},{5,3},{3,1},{1,0},{8,10},{10,12},{12... | collective-permute-start | bytes 589832 | tf_op jit(solution)/shard_map/ppermute | solution.py:33
  57.1 1.1 %collective-permute-start.8 = (bf16[1,256,384]{2,1,0:T(8,128)(2,1)S(1)}, bf16[1,256,384]{2,1,0:T(8,128)(2,1)S(1)}, u32[]{:S(2)}, u32[]{:S(2)}) collective-permute-start(bf16[1,256,384]{2,1,0:T(8,128)(2,1)S(1)} %collective-permute-done.6), channel_id=1, source_target_pairs={{0,1},{2,0},{4,2},{6,4},{7,6},{5,7},{3,5},{1,3},{8,9},{10,8},{12,1... | collective-permute-start | bytes 589832 | tf_op jit(solution)/shard_map/ppermute | solution.py:34
  58.1 0.7 constant_dynamic-update-slice_fusion.5
  58.8 0.7 constant_dynamic-update-slice_fusion.4
  59.5 3.7 %collective-permute-done.7 = bf16[1,256,384]{2,1,0:T(8,128)(2,1)S(1)} collective-permute-done((bf16[1,256,384]{2,1,0:T(8,128)(2,1)S(1)}, bf16[1,256,384]{2,1,0:T(8,128)(2,1)S(1)}, u32[]{:S(2)}, u32[]{:S(2)}) %collective-permute-start.7) | collective-permute-done | bytes 196640 | tf_op jit(solution)/shard_map/ppermute | solution.py:33
  63.2 1.0 collective-permute-start.9
  64.2 1.2 %collective-permute-start.10 = (bf16[1,128,384]{2,1,0:T(8,128)(2,1)S(1)}, bf16[1,128,384]{2,1,0:T(8,128)(2,1)S(1)}, u32[]{:S(2)}, u32[]{:S(2)}) collective-permute-start(bf16[1,128,384]{2,1,0:T(8,128)(2,1)S(1)} %slice.77), channel_id=1, source_target_pairs={{0,1},{2,0},{4,2},{6,4},{7,6},{5,7},{3,5},{1,3},{8,9},{10,8},{12,1... | collective-permute-start | bytes 294920 | tf_op jit(solution)/shard_map/ppermute | solution.py:39
  65.4 0.9 collective-permute-start.15
  66.3 1.0 %constant_dynamic-update-slice_fusion.14 = bf16[1,2048,384]{2,1,0:T(8,128)(2,1)S(1)} fusion(bf16[1,2048,384]{2,1,0:T(8,128)(2,1)S(1)} %constant_dynamic-update-slice_fusion.15, bf16[1,256,384]{2,1,0:T(8,128)(2,1)} %collective-permute-done.13), kind=kLoop, calls=%fused_computation.120 | loop fusion | bytes 393216
  67.3 1.2 %collective-permute-start.16 = (bf16[1,256,384]{2,1,0:T(8,128)(2,1)}, bf16[1,256,384]{2,1,0:T(8,128)(2,1)}, u32[]{:S(2)}, u32[]{:S(2)}) collective-permute-start(bf16[1,256,384]{2,1,0:T(8,128)(2,1)} %collective-permute-done.14), channel_id=1, source_target_pairs={{0,1},{2,0},{4,2},{6,4},{7,6},{5,7},{3,5},{1,3},{8,9},{10,8},{12,1... | collective-permute-start | bytes 589832 | tf_op jit(solution)/shard_map/ppermute | solution.py:34
  68.5 1.0 %constant_dynamic-update-slice_fusion.13 = bf16[1,2048,384]{2,1,0:T(8,128)(2,1)S(1)} fusion(bf16[1,2048,384]{2,1,0:T(8,128)(2,1)S(1)} %constant_dynamic-update-slice_fusion.14, bf16[1,256,384]{2,1,0:T(8,128)(2,1)} %collective-permute-done.14), kind=kLoop, calls=%fused_computation.119 | loop fusion | bytes 393216
  69.5 0.8 constant_dynamic-update-slice_fusion.3
  70.2 0.7 constant_dynamic-update-slice_fusion.2
  70.9 0.6 constant_dynamic-update-slice_fusion.1
  71.6 0.6 constant_dynamic-update-slice_fusion
  72.2 3.2 %fusion.118 = (f32[256]{0:T(256)S(1)}, f32[256,2048]{1,0:T(8,128)S(1)}) fusion(bf16[256,384]{1,0:T(8,128)(2,1)S(1)} %convolution_convert_fusion.5, bf16[384,384]{1,0:T(8,128)(2,1)S(1)} %copy-done, bf16[1,2048,384]{2,1,0:T(8,128)(2,1)} %constant_dynamic-update-slice_fusion), kind=kOutput, calls=%fused_computation.167 | convolution fusion | flops 1008467712 | bytes 4162560 | tf_op jit(solution)/shard_map/fqc,fkc->fqk/dot_general | solution.py:125
  75.4 0.4 fusion.2
  75.8 3.2 %fusion.54 = bf16[256,384]{1,0:T(8,128)(2,1)S(1)} fusion(bf16[384,384]{1,0:T(8,128)(2,1)} %param.18, bf16[1,2048,384]{2,1,0:T(8,128)(2,1)} %constant_dynamic-update-slice_fusion, f32[256,2048]{1,0:T(8,128)S(1)} %get-tuple-element.26, f32[256]{0:T(256)S(1)} %get-tuple-element.25, f32[256]{0:T(256)S(1)} %fusion.2), kind=kOutput, calls=%fused_computation.54 | convolution fusion | flops 1008664576 | bytes 4163584 | tf_op jit(solution)/shard_map/fqk,fkc->fqc/dot_general | solution.py:131
  79.3 0.9 slice.80
  80.2 1.0 collective-permute-start.17
  81.2 0.9 slice.81
  82.1 1.4 %collective-permute-start.18 = (bf16[1,128,384]{2,1,0:T(8,128)(2,1)S(1)}, bf16[1,128,384]{2,1,0:T(8,128)(2,1)S(1)}, u32[]{:S(2)}, u32[]{:S(2)}) collective-permute-start(bf16[1,128,384]{2,1,0:T(8,128)(2,1)S(1)} %slice.81), channel_id=1, source_target_pairs={{0,1},{2,0},{4,2},{6,4},{7,6},{5,7},{3,5},{1,3},{8,9},{10,8},{12,1... | collective-permute-start | bytes 294920 | tf_op jit(solution)/shard_map/ppermute | solution.py:39
  83.5 1.6 %constant_dynamic-update-slice_fusion.12 = bf16[1,2048,384]{2,1,0:T(8,128)(2,1)} fusion(bf16[1,2048,384]{2,1,0:T(8,128)(2,1)} %copy-done.5, bf16[1,256,384]{2,1,0:T(8,128)(2,1)} %collective-permute-done.15), kind=kLoop, calls=%fused_computation.118 | loop fusion | bytes 393216
  85.1 1.6 %constant_dynamic-update-slice_fusion.11 = bf16[1,2048,384]{2,1,0:T(8,128)(2,1)} fusion(bf16[1,2048,384]{2,1,0:T(8,128)(2,1)} %constant_dynamic-update-slice_fusion.12, bf16[1,256,384]{2,1,0:T(8,128)(2,1)} %collective-permute-done.16), kind=kLoop, calls=%fused_computation.117 | loop fusion | bytes 393216
  86.7 0.6 constant_dynamic-update-slice_fusion.10
  87.3 0.7 constant_dynamic-update-slice_fusion.9
  88.0 3.3 %fusion.115 = (f32[256]{0:T(256)S(1)}, f32[256,2048]{1,0:T(8,128)S(1)}) fusion(bf16[256,384]{1,0:T(8,128)(2,1)} %convolution_convert_fusion.4, bf16[384,384]{1,0:T(8,128)(2,1)S(1)} %copy-done, bf16[1,2048,384]{2,1,0:T(8,128)(2,1)} %constant_dynamic-update-slice_fusion.9), kind=kOutput, calls=%fused_computation.166 | convolution fusion | flops 1008467712 | bytes 4162560 | tf_op jit(solution)/shard_map/fqc,fkc->fqk/dot_general | solution.py:125
  91.3 0.4 fusion.4
  91.7 3.1 %fusion.48 = bf16[256,384]{1,0:T(8,128)(2,1)S(1)} fusion(bf16[384,384]{1,0:T(8,128)(2,1)} %param.18, bf16[1,2048,384]{2,1,0:T(8,128)(2,1)} %constant_dynamic-update-slice_fusion.9, f32[256,2048]{1,0:T(8,128)S(1)} %get-tuple-element.24, f32[256]{0:T(256)S(1)} %get-tuple-element.23, f32[256]{0:T(256)S(1)} %fusion.4), kind=kOutput, calls=%fused_computation.52 | convolution fusion | flops 1008664576 | bytes 4163584 | tf_op jit(solution)/shard_map/fqk,fkc->fqc/dot_general | solution.py:131
  95.1 0.8 pad_maximum_fusion.1
  (75 shorter events, 3.9 us)
Async XLA Ops:
  0.0 72.2 %copy-start = (bf16[384,384]{1,0:T(8,128)(2,1)S(1)}, bf16[384,384]{1,0:T(8,128)(2,1)}, u32[]{:S(2)}) copy-start(bf16[384,384]{1,0:T(8,128)(2,1)} %param.17) | copy-start | bytes 884740
  0.0 15.4 %copy-start.1 = (bf16[2,2,128,384]{3,2,1,0:T(8,128)(2,1)S(1)}, bf16[2,2,128,384]{3,2,1,0:T(8,128)(2,1)}, u32[]{:S(2)}) copy-start(bf16[2,2,128,384]{3,2,1,0:T(8,128)(2,1)} %param.10) | copy-start | bytes 1179652
  0.0 15.5 %copy-start.9 = (f32[384]{0:T(512)S(1)}, f32[384]{0:T(512)}, u32[]{:S(2)}) copy-start(f32[384]{0:T(512)} %param.12) | copy-start | bytes 4612
  1.1 9.8 %collective-permute-start.1 = (bf16[2,1,128,384]{3,2,1,0:T(8,128)(2,1)S(1)}, bf16[2,1,128,384]{3,2,1,0:T(8,128)(2,1)S(1)}, u32[]{:S(2)}, u32[]{:S(2)}) collective-permute-start(bf16[2,1,128,384]{3,2,1,0:T(8,128)(2,1)S(1)} %get-tuple-element.18), channel_id=1, source_target_pairs={{1,0},{2,1},{3,2},{4,3},{5,4},{6,5},{7,6},{9,8},{10,9},{11,10},{12... | collective-permute-start | bytes 589832 | tf_op jit(solution)/shard_map/ppermute | solution.py:17
  2.4 12.8 %collective-permute-start = (bf16[2,1,128,384]{3,2,1,0:T(8,128)(2,1)S(1)}, bf16[2,1,128,384]{3,2,1,0:T(8,128)(2,1)S(1)}, u32[]{:S(2)}, u32[]{:S(2)}) collective-permute-start(bf16[2,1,128,384]{3,2,1,0:T(8,128)(2,1)S(1)} %get-tuple-element.17), channel_id=1, source_target_pairs={{0,1},{1,2},{2,3},{3,4},{4,5},{5,6},{6,7},{8,9},{9,10},{10,11},{11... | collective-permute-start | bytes 589832 | tf_op jit(solution)/shard_map/ppermute | solution.py:15
  16.0 0.7 copy-start.8
  16.3 0.9 copy-start.2
  16.3 2.6 %collective-permute-start.2 = (bf16[2,4,130,384]{3,2,1,0:T(8,128)(2,1)S(1)}, bf16[2,4,130,384]{3,2,1,0:T(8,128)(2,1)}, u32[]{:S(2)}, u32[]{:S(2)}) collective-permute-start(bf16[2,4,130,384]{3,2,1,0:T(8,128)(2,1)S(1)} %fusion.65), channel_id=1, source_target_pairs={{0,8},{8,0},{1,9},{9,1},{2,10},{10,2},{3,11},{11,3},{4,12},{12,4},... | collective-permute-start | bytes 2396168 | tf_op jit(solution)/shard_map/ppermute | solution.py:76
  23.1 3.7 %slice-start = ((s8[7962624]{0:T(1024)(128)(4,1)}), s8[4194304]{0:T(1024)(128)(4,1)S(1)}, s32[]{:S(2)}) async-start(s8[7962624]{0:T(1024)(128)(4,1)} %bitcast.122), calls=%async_computation | async-start | bytes 8388608
  25.3 2.3 %slice-start.1 = ((s8[7962624]{0:T(1024)(128)(4,1)}), s8[3768320]{0:T(1024)(128)(4,1)S(1)}, s32[]{:S(2)}) async-start(s8[7962624]{0:T(1024)(128)(4,1)} %bitcast.122), calls=%async_computation.1 | async-start | bytes 7536640
  26.5 1.0 %copy-start.10 = (pred[8,17]{0,1:T(8,128)(4,1)S(1)}, pred[8,17]{0,1:T(8,128)(4,1)}, u32[]{:S(2)}) copy-start(pred[8,17]{0,1:T(8,128)(4,1)} %constant.108) | copy-start | bytes 412
  30.7 0.7 copy-start.6
  30.7 0.8 copy-start.7
  30.8 4.2 %copy-start.4 = (bf16[384,384]{1,0:T(8,128)(2,1)S(1)}, bf16[384,384]{1,0:T(8,128)(2,1)}, u32[]{:S(2)}) copy-start(bf16[384,384]{1,0:T(8,128)(2,1)} %param.16) | copy-start | bytes 884740
  31.7 7.0 %collective-permute-start.4 = (bf16[1,256,384]{2,1,0:T(8,128)(2,1)S(1)}, bf16[1,256,384]{2,1,0:T(8,128)(2,1)S(1)}, u32[]{:S(2)}, u32[]{:S(2)}) collective-permute-start(bf16[1,256,384]{2,1,0:T(8,128)(2,1)S(1)} %bitcast.110), channel_id=1, source_target_pairs={{0,1},{2,0},{4,2},{6,4},{7,6},{5,7},{3,5},{1,3},{8,9},{10,8},{12,1... | collective-permute-start | bytes 589832 | tf_op jit(solution)/shard_map/ppermute | solution.py:34
  35.0 11.3 %collective-permute-start.3 = (bf16[1,256,384]{2,1,0:T(8,128)(2,1)S(1)}, bf16[1,256,384]{2,1,0:T(8,128)(2,1)S(1)}, u32[]{:S(2)}, u32[]{:S(2)}) collective-permute-start(bf16[1,256,384]{2,1,0:T(8,128)(2,1)S(1)} %bitcast.112), channel_id=1, source_target_pairs={{0,2},{2,4},{4,6},{6,7},{7,5},{5,3},{3,1},{1,0},{8,10},{10,12},{12... | collective-permute-start | bytes 589832 | tf_op jit(solution)/shard_map/ppermute | solution.py:33
  43.7 8.1 %collective-permute-start.11 = (bf16[1,256,384]{2,1,0:T(8,128)(2,1)S(1)}, bf16[1,256,384]{2,1,0:T(8,128)(2,1)S(1)}, u32[]{:S(2)}, u32[]{:S(2)}) collective-permute-start(bf16[1,256,384]{2,1,0:T(8,128)(2,1)S(1)} %bitcast.114), channel_id=1, source_target_pairs={{0,2},{2,4},{4,6},{6,7},{7,5},{5,3},{3,1},{1,0},{8,10},{10,12},{12... | collective-permute-start | bytes 589832 | tf_op jit(solution)/shard_map/ppermute | solution.py:33
  45.4 7.4 %collective-permute-start.12 = (bf16[1,256,384]{2,1,0:T(8,128)(2,1)S(1)}, bf16[1,256,384]{2,1,0:T(8,128)(2,1)S(1)}, u32[]{:S(2)}, u32[]{:S(2)}) collective-permute-start(bf16[1,256,384]{2,1,0:T(8,128)(2,1)S(1)} %bitcast.115), channel_id=1, source_target_pairs={{0,1},{2,0},{4,2},{6,4},{7,6},{5,7},{3,5},{1,3},{8,9},{10,8},{12,1... | collective-permute-start | bytes 589832 | tf_op jit(solution)/shard_map/ppermute | solution.py:34
  47.7 8.3 %collective-permute-start.5 = (bf16[1,256,384]{2,1,0:T(8,128)(2,1)S(1)}, bf16[1,256,384]{2,1,0:T(8,128)(2,1)S(1)}, u32[]{:S(2)}, u32[]{:S(2)}) collective-permute-start(bf16[1,256,384]{2,1,0:T(8,128)(2,1)S(1)} %collective-permute-done.3), channel_id=1, source_target_pairs={{0,2},{2,4},{4,6},{6,7},{7,5},{5,3},{3,1},{1,0},{8,10},{10,12},{12... | collective-permute-start | bytes 589832 | tf_op jit(solution)/shard_map/ppermute | solution.py:33
  48.8 8.2 %collective-permute-start.6 = (bf16[1,256,384]{2,1,0:T(8,128)(2,1)S(1)}, bf16[1,256,384]{2,1,0:T(8,128)(2,1)S(1)}, u32[]{:S(2)}, u32[]{:S(2)}) collective-permute-start(bf16[1,256,384]{2,1,0:T(8,128)(2,1)S(1)} %collective-permute-done.4), channel_id=1, source_target_pairs={{0,1},{2,0},{4,2},{6,4},{7,6},{5,7},{3,5},{1,3},{8,9},{10,8},{12,1... | collective-permute-start | bytes 589832 | tf_op jit(solution)/shard_map/ppermute | solution.py:34
  51.8 13.6 %collective-permute-start.13 = (bf16[1,256,384]{2,1,0:T(8,128)(2,1)S(1)}, bf16[1,256,384]{2,1,0:T(8,128)(2,1)}, u32[]{:S(2)}, u32[]{:S(2)}) collective-permute-start(bf16[1,256,384]{2,1,0:T(8,128)(2,1)S(1)} %collective-permute-done.11), channel_id=1, source_target_pairs={{0,2},{2,4},{4,6},{6,7},{7,5},{5,3},{3,1},{1,0},{8,10},{10,12},{12... | collective-permute-start | bytes 589832 | tf_op jit(solution)/shard_map/ppermute | solution.py:33
  52.8 14.5 %collective-permute-start.14 = (bf16[1,256,384]{2,1,0:T(8,128)(2,1)S(1)}, bf16[1,256,384]{2,1,0:T(8,128)(2,1)}, u32[]{:S(2)}, u32[]{:S(2)}) collective-permute-start(bf16[1,256,384]{2,1,0:T(8,128)(2,1)S(1)} %collective-permute-done.12), channel_id=1, source_target_pairs={{0,1},{2,0},{4,2},{6,4},{7,6},{5,7},{3,5},{1,3},{8,9},{10,8},{12,1... | collective-permute-start | bytes 589832 | tf_op jit(solution)/shard_map/ppermute | solution.py:34
  56.0 7.2 %collective-permute-start.7 = (bf16[1,256,384]{2,1,0:T(8,128)(2,1)S(1)}, bf16[1,256,384]{2,1,0:T(8,128)(2,1)S(1)}, u32[]{:S(2)}, u32[]{:S(2)}) collective-permute-start(bf16[1,256,384]{2,1,0:T(8,128)(2,1)S(1)} %collective-permute-done.5), channel_id=1, source_target_pairs={{0,2},{2,4},{4,6},{6,7},{7,5},{5,3},{3,1},{1,0},{8,10},{10,12},{12... | collective-permute-start | bytes 589832 | tf_op jit(solution)/shard_map/ppermute | solution.py:33
  57.1 7.1 %collective-permute-start.8 = (bf16[1,256,384]{2,1,0:T(8,128)(2,1)S(1)}, bf16[1,256,384]{2,1,0:T(8,128)(2,1)S(1)}, u32[]{:S(2)}, u32[]{:S(2)}) collective-permute-start(bf16[1,256,384]{2,1,0:T(8,128)(2,1)S(1)} %collective-permute-done.6), channel_id=1, source_target_pairs={{0,1},{2,0},{4,2},{6,4},{7,6},{5,7},{3,5},{1,3},{8,9},{10,8},{12,1... | collective-permute-start | bytes 589832 | tf_op jit(solution)/shard_map/ppermute | solution.py:34
  63.2 7.7 %collective-permute-start.9 = (bf16[1,128,384]{2,1,0:T(8,128)(2,1)S(1)}, bf16[1,128,384]{2,1,0:T(8,128)(2,1)S(1)}, u32[]{:S(2)}, u32[]{:S(2)}) collective-permute-start(bf16[1,128,384]{2,1,0:T(8,128)(2,1)S(1)} %slice.76), channel_id=1, source_target_pairs={{0,2},{2,4},{4,6},{6,7},{7,5},{5,3},{3,1},{1,0},{8,10},{10,12},{12... | collective-permute-start | bytes 294920 | tf_op jit(solution)/shard_map/ppermute | solution.py:38
  64.2 7.4 %collective-permute-start.10 = (bf16[1,128,384]{2,1,0:T(8,128)(2,1)S(1)}, bf16[1,128,384]{2,1,0:T(8,128)(2,1)S(1)}, u32[]{:S(2)}, u32[]{:S(2)}) collective-permute-start(bf16[1,128,384]{2,1,0:T(8,128)(2,1)S(1)} %slice.77), channel_id=1, source_target_pairs={{0,1},{2,0},{4,2},{6,4},{7,6},{5,7},{3,5},{1,3},{8,9},{10,8},{12,1... | collective-permute-start | bytes 294920 | tf_op jit(solution)/shard_map/ppermute | solution.py:39
  65.4 13.9 %collective-permute-start.15 = (bf16[1,256,384]{2,1,0:T(8,128)(2,1)}, bf16[1,256,384]{2,1,0:T(8,128)(2,1)}, u32[]{:S(2)}, u32[]{:S(2)}) collective-permute-start(bf16[1,256,384]{2,1,0:T(8,128)(2,1)} %collective-permute-done.13), channel_id=1, source_target_pairs={{0,2},{2,4},{4,6},{6,7},{7,5},{5,3},{3,1},{1,0},{8,10},{10,12},{12... | collective-permute-start | bytes 589832 | tf_op jit(solution)/shard_map/ppermute | solution.py:33
  67.3 13.9 %collective-permute-start.16 = (bf16[1,256,384]{2,1,0:T(8,128)(2,1)}, bf16[1,256,384]{2,1,0:T(8,128)(2,1)}, u32[]{:S(2)}, u32[]{:S(2)}) collective-permute-start(bf16[1,256,384]{2,1,0:T(8,128)(2,1)} %collective-permute-done.14), channel_id=1, source_target_pairs={{0,1},{2,0},{4,2},{6,4},{7,6},{5,7},{3,5},{1,3},{8,9},{10,8},{12,1... | collective-permute-start | bytes 589832 | tf_op jit(solution)/shard_map/ppermute | solution.py:34
  69.5 2.1 %copy-start.5 = (bf16[1,2048,384]{2,1,0:T(8,128)(2,1)}, bf16[1,2048,384]{2,1,0:T(8,128)(2,1)S(1)}, u32[]{:S(2)}) copy-start(bf16[1,2048,384]{2,1,0:T(8,128)(2,1)S(1)} %constant_dynamic-update-slice_fusion.13) | copy-start | bytes 4718596
  75.8 3.2 %copy-start.3 = (bf16[384,384]{1,0:T(8,128)(2,1)S(1)}, bf16[384,384]{1,0:T(8,128)(2,1)}, u32[]{:S(2)}) copy-start(bf16[384,384]{1,0:T(8,128)(2,1)} %param.19) | copy-start | bytes 884740
  80.2 6.5 %collective-permute-start.17 = (bf16[1,128,384]{2,1,0:T(8,128)(2,1)S(1)}, bf16[1,128,384]{2,1,0:T(8,128)(2,1)S(1)}, u32[]{:S(2)}, u32[]{:S(2)}) collective-permute-start(bf16[1,128,384]{2,1,0:T(8,128)(2,1)S(1)} %slice.80), channel_id=1, source_target_pairs={{0,2},{2,4},{4,6},{6,7},{7,5},{5,3},{3,1},{1,0},{8,10},{10,12},{12... | collective-permute-start | bytes 294920 | tf_op jit(solution)/shard_map/ppermute | solution.py:38
  82.1 5.3 %collective-permute-start.18 = (bf16[1,128,384]{2,1,0:T(8,128)(2,1)S(1)}, bf16[1,128,384]{2,1,0:T(8,128)(2,1)S(1)}, u32[]{:S(2)}, u32[]{:S(2)}) collective-permute-start(bf16[1,128,384]{2,1,0:T(8,128)(2,1)S(1)} %slice.81), channel_id=1, source_target_pairs={{0,1},{2,0},{4,2},{6,4},{7,6},{5,7},{3,5},{1,3},{8,9},{10,8},{12,1... | collective-permute-start | bytes 294920 | tf_op jit(solution)/shard_map/ppermute | solution.py:39

commit v21 on v20

--- a/solution.py
+++ b/solution.py
@@ -34,12 +34,7 @@
         backward = lax.ppermute(backward, axis, behind)
         pieces += [forward, backward]
     if count % 2 == 0 and count > 1:
-        half = block.shape[dim] // 2
-        front = lax.ppermute(lax.slice_in_dim(forward, 0, half, axis=dim), axis, ahead)
-        back = lax.ppermute(
-            lax.slice_in_dim(backward, half, block.shape[dim], axis=dim), axis, behind
-        )
-        pieces += [front, back]
+        pieces.append(lax.ppermute(forward, axis, ahead))
     return pieces
 
 

time: 96.4 us -> 94.4 us (0.979)
  waiting for transfers between devices: 18.2 us -> 21.7 us
  local copies, waits for them, and re-layouts: 23.3 us -> 20.3 us
  starting transfers between devices: 24.7 us -> 22.3 us
    ppermute x4 -> x2, waiting for transfers between devices: 0.01 us -> 5.29 us  [ring_gather(): pieces.append(lax.ppermute(forward, axis, ahead))]
    ppermute x4 -> x2, starting transfers between devices: 4.48 us -> 2.15 us  [ring_gather(): pieces.append(lax.ppermute(forward, axis, ahead))]
    slice x4 -> x0, local copies, waits for them, and re-layouts: 1.83 us -> none  [the longest x2 0.91 us: ring_gather(): lax.slice_in_dim(forward, 0, half, axis=dim)]
    ppermute x6, waiting for transfers between devices: 6.96 us -> 5.14 us  [ring_gather(): forward = lax.ppermute(forward, axis, ahead)]
    unnamed x44 -> x42, local copies, waits for them, and re-layouts: 14 us -> 12.7 us
  transfers between devices with their start and end apart: 19 -> 17, of which waited for: 7 -> 10; matrix products, arithmetic and copies ran while one was open for 30% -> 27% of each run, Pallas kernels for 0% -> 0%
where the time goes in v21:
time: 94.4 us; the launch traced here: 93.9 us
  starting transfers between devices  22.3 us (24%)
  waiting for transfers between devices  21.7 us (23%)
  matrix products  20.8 us (22%)
  local copies, waits for them, and re-layouts  20.3 us (22%)
  other arithmetic  8.4 us (9%)
    unnamed x42, local copies, waits for them, and re-layouts  12.7 us
    ppermute x6, starting transfers between devices, ring_gather(): backward = lax.ppermute(backward, axis, behind)  7.51 us
    dot_general x2, matrix products, shards(): jnp.einsum('fqc,fkc->fqk', queries, keys_all, preferred_element_type=jnp....  6.42 us
    conv_general_dilated x2, matrix products, shards(): lax.conv_general_dilated(span_window, conv_weight, window_strides=(1, 1,...  6.34 us
    dot_general x2, matrix products, shards(): jnp.einsum('fqk,fkc->fqc', weights_exp.astype(jnp.bfloat16), values_all,...  6.27 us
    ppermute x6, starting transfers between devices, ring_gather(): forward = lax.ppermute(forward, axis, ahead)  5.78 us
    ppermute x1, starting transfers between devices, padded_2(): lax.ppermute(tail, axis, [(i, (i + 1) % count) for i in range(ends)])  5.52 us
    ppermute x2, waiting for transfers between devices, ring_gather(): pieces.append(lax.ppermute(forward, axis, ahead))  5.29 us
  transfers between devices with their start and end apart: 17, of which 10 were waited for; matrix products, arithmetic and copies ran while one was open for 27% of the time, Pallas kernels for 0%

profile of v21, /device:TPU:0, one launch (start us, length us, event | category | flops | bytes accessed | tf_op | source)
XLA Modules:
  0.0 93.9 jit_solution(4354094506254429044)
XLA Ops:
  0.0 1.1 %fusion.114 = (bf16[2,1,128,384]{3,2,1,0:T(8,128)(2,1)S(1)}, bf16[2,1,128,384]{3,2,1,0:T(8,128)(2,1)S(1)}) fusion(bf16[2,2,128,384]{3,2,1,0:T(8,128)(2,1)} %param.10), kind=kLoop, calls=%fused_computation.163 | loop fusion | bytes 786432 | tf_op jit(solution)/shard_map/slice | solution.py:12
  1.1 1.3 %collective-permute-start.1 = (bf16[2,1,128,384]{3,2,1,0:T(8,128)(2,1)S(1)}, bf16[2,1,128,384]{3,2,1,0:T(8,128)(2,1)S(1)}, u32[]{:S(2)}, u32[]{:S(2)}) collective-permute-start(bf16[2,1,128,384]{3,2,1,0:T(8,128)(2,1)S(1)} %get-tuple-element.18), channel_id=1, source_target_pairs={{1,0},{2,1},{3,2},{4,3},{5,4},{6,5},{7,6},{9,8},{10,9},{11,10},{12... | collective-permute-start | bytes 589832 | tf_op jit(solution)/shard_map/ppermute | solution.py:17
  2.4 5.5 %collective-permute-start = (bf16[2,1,128,384]{3,2,1,0:T(8,128)(2,1)S(1)}, bf16[2,1,128,384]{3,2,1,0:T(8,128)(2,1)S(1)}, u32[]{:S(2)}, u32[]{:S(2)}) collective-permute-start(bf16[2,1,128,384]{3,2,1,0:T(8,128)(2,1)S(1)} %get-tuple-element.17), channel_id=1, source_target_pairs={{0,1},{1,2},{2,3},{3,4},{4,5},{5,6},{6,7},{8,9},{9,10},{10,11},{11... | collective-permute-start | bytes 589832 | tf_op jit(solution)/shard_map/ppermute | solution.py:15
  8.0 1.1 %fusion.74 = f32[2,2,128]{2,1,0:T(2,128)S(1)} fusion(bf16[2,2,128,384]{3,2,1,0:T(8,128)(2,1)} %param.10), kind=kLoop, calls=%fused_computation.74 | loop fusion | flops 589312 | bytes 395264 | tf_op jit(solution)/shard_map/reduce_sum | solution.py:43
  9.1 1.8 %collective-permute-done.1 = bf16[2,1,128,384]{3,2,1,0:T(8,128)(2,1)S(1)} collective-permute-done((bf16[2,1,128,384]{3,2,1,0:T(8,128)(2,1)S(1)}, bf16[2,1,128,384]{3,2,1,0:T(8,128)(2,1)S(1)}, u32[]{:S(2)}, u32[]{:S(2)}) %collective-permute-start.1) | collective-permute-done | bytes 196640 | tf_op jit(solution)/shard_map/ppermute | solution.py:17
  10.9 4.4 %collective-permute-done = bf16[2,1,128,384]{3,2,1,0:T(8,128)(2,1)S(1)} collective-permute-done((bf16[2,1,128,384]{3,2,1,0:T(8,128)(2,1)S(1)}, bf16[2,1,128,384]{3,2,1,0:T(8,128)(2,1)S(1)}, u32[]{:S(2)}, u32[]{:S(2)}) %collective-permute-start) | collective-permute-done | bytes 196640 | tf_op jit(solution)/shard_map/ppermute | solution.py:15
  15.5 0.5 fusion.81
  16.4 0.3 copy-done.8
  17.2 1.6 %collective-permute-done.2 = bf16[2,4,130,384]{3,2,1,0:T(8,128)(2,1)} collective-permute-done((bf16[2,4,130,384]{3,2,1,0:T(8,128)(2,1)S(1)}, bf16[2,4,130,384]{3,2,1,0:T(8,128)(2,1)}, u32[]{:S(2)}, u32[]{:S(2)}) %collective-permute-start.2) | collective-permute-done | bytes 798752 | tf_op jit(solution)/shard_map/ppermute | solution.py:71
  18.9 1.7 %maximum_maximum_fusion = bf16[5,4,130,384]{3,2,1,0:T(8,128)(2,1)S(1)} fusion(bf16[2,4,130,384]{3,2,1,0:T(8,128)(2,1)} %collective-permute-done.2, bf16[2,4,130,384]{3,2,1,0:T(8,128)(2,1)} %copy-done.2, bf16[5]{0:T(256)(128)(2,1)S(1)} %pad.17.clone), kind=kLoop, calls=%fused_computation.15 | loop fusion | flops 1996800 | bytes 3594250 | tf_op jit(solution)/shard_map/concatenate | solution.py:74
  20.6 2.5 %gather_fusion = bf16[6,4,130,384]{3,2,1,0:T(8,128)(2,1)} fusion(bf16[5,4,130,384]{3,2,1,0:T(8,128)(2,1)S(1)} %maximum_maximum_fusion, s32[1024]{0:T(1024)S(1)} %pad_clamp_fusion), kind=kCustom, calls=%fused_computation | custom fusion | bytes 4792344 | tf_op jit(solution)/shard_map/jit(_take)/gather | solution.py:83
  23.1 2.2 %broadcast_select_fusion = bf16[6,4,130,384]{3,2,1,0:T(8,128)(2,1)S(1)} fusion(bf16[6,4,130,384]{3,2,1,0:T(8,128)(2,1)} %gather_fusion, pred[6]{0:T(512)(128)(4,1)S(1)} %compare_and_fusion), kind=kLoop, calls=%fused_computation.12 | loop fusion | flops 1198080 | bytes 4792326 | tf_op jit(solution)/shard_map/jit(_take)/select_n | solution.py:83
  25.6 0.5 copy.23
  26.1 0.5 pad.5.clone
  26.8 0.8 slice-done.1
  27.6 3.2 %fusion.38 = f32[1,2,8,17,384]{4,2,3,1,0:T(8,128)S(1)} fusion(bf16[3,3,3,384,384]{4,3,2,1,0:T(8,128)(2,1)S(1)} %bitcast.123, bf16[3,4,1,7,2,384]{5,3,4,1,0,2:T(8,128)(2,1)S(1)} %slice.57, bf16[3,4,1,8,17,384]{5,3,4,1,0,2:T(8,128)(2,1)S(1)} %copy.13, pred[8,17]{0,1:T(8,128)(4,1)S(1)} %copy-done.10), kind=kOutput, calls=%fused_computation.44 | convolution fusion | flops 2170140672 | bytes 9762952 | tf_op jit(solution)/shard_map/conv_general_dilated | solution.py:90
  31.1 0.3 copy-done.6
  31.7 2.5 %collective-permute-start.4 = (bf16[1,256,384]{2,1,0:T(8,128)(2,1)S(1)}, bf16[1,256,384]{2,1,0:T(8,128)(2,1)S(1)}, u32[]{:S(2)}, u32[]{:S(2)}) collective-permute-start(bf16[1,256,384]{2,1,0:T(8,128)(2,1)S(1)} %bitcast.110), channel_id=1, source_target_pairs={{0,1},{2,0},{4,2},{6,4},{7,6},{5,7},{3,5},{1,3},{8,9},{10,8},{12,1... | collective-permute-start | bytes 589832 | tf_op jit(solution)/shard_map/ppermute | solution.py:34
  34.3 0.7 constant_dynamic-update-slice_fusion.7
  35.0 0.3 convolution_convert_fusion.5
  35.2 3.5 %collective-permute-done.4 = bf16[1,256,384]{2,1,0:T(8,128)(2,1)S(1)} collective-permute-done((bf16[1,256,384]{2,1,0:T(8,128)(2,1)S(1)}, bf16[1,256,384]{2,1,0:T(8,128)(2,1)S(1)}, u32[]{:S(2)}, u32[]{:S(2)}) %collective-permute-start.4) | collective-permute-done | bytes 196640 | tf_op jit(solution)/shard_map/ppermute | solution.py:34
  38.7 0.5 copy.24
  39.2 0.5 pad.7.clone
  39.9 3.2 %fusion.35 = f32[1,2,8,17,384]{4,2,3,1,0:T(8,128)S(1)} fusion(bf16[3,3,3,384,384]{4,3,2,1,0:T(8,128)(2,1)S(1)} %bitcast.123, bf16[3,4,1,7,2,384]{5,3,4,1,0,2:T(8,128)(2,1)S(1)} %slice.60, bf16[3,4,1,8,17,384]{5,3,4,1,0,2:T(8,128)(2,1)S(1)} %copy.18, pred[8,17]{0,1:T(8,128)(4,1)S(1)} %copy-done.10), kind=kOutput, calls=%fused_computation.43 | convolution fusion | flops 2170140672 | bytes 9762952 | tf_op jit(solution)/shard_map/conv_general_dilated | solution.py:90
  43.7 1.7 %collective-permute-start.10 = (bf16[1,256,384]{2,1,0:T(8,128)(2,1)S(1)}, bf16[1,256,384]{2,1,0:T(8,128)(2,1)S(1)}, u32[]{:S(2)}, u32[]{:S(2)}) collective-permute-start(bf16[1,256,384]{2,1,0:T(8,128)(2,1)S(1)} %bitcast.114), channel_id=1, source_target_pairs={{0,2},{2,4},{4,6},{6,7},{7,5},{5,3},{3,1},{1,0},{8,10},{10,12},{12... | collective-permute-start | bytes 589832 | tf_op jit(solution)/shard_map/ppermute | solution.py:33
  45.4 0.9 collective-permute-start.11
  46.3 0.7 constant_dynamic-update-slice_fusion.6
  47.0 0.7 constant_dynamic-update-slice_fusion.5
  47.7 1.1 %collective-permute-start.5 = (bf16[1,256,384]{2,1,0:T(8,128)(2,1)S(1)}, bf16[1,256,384]{2,1,0:T(8,128)(2,1)S(1)}, u32[]{:S(2)}, u32[]{:S(2)}) collective-permute-start(bf16[1,256,384]{2,1,0:T(8,128)(2,1)S(1)} %collective-permute-done.3), channel_id=1, source_target_pairs={{0,2},{2,4},{4,6},{6,7},{7,5},{5,3},{3,1},{1,0},{8,10},{10,12},{12... | collective-permute-start | bytes 589832 | tf_op jit(solution)/shard_map/ppermute | solution.py:33
  48.8 0.9 collective-permute-start.6
  49.7 0.9 %convolution_convert_fusion.4 = bf16[256,384]{1,0:T(8,128)(2,1)} fusion(bf16[256,384]{1,0:T(8,128)(2,1)S(1)} %bitcast.117, bf16[384,384]{1,0:T(8,128)(2,1)S(1)} %copy-done.4), kind=kOutput, calls=%fused_computation.47 | convolution fusion | flops 75595776 | bytes 688128 | tf_op jit(solution)/shard_map/ftc,cd->ftd/dot_general | solution.py:103
  50.7 1.1 %collective-permute-done.10 = bf16[1,256,384]{2,1,0:T(8,128)(2,1)S(1)} collective-permute-done((bf16[1,256,384]{2,1,0:T(8,128)(2,1)S(1)}, bf16[1,256,384]{2,1,0:T(8,128)(2,1)S(1)}, u32[]{:S(2)}, u32[]{:S(2)}) %collective-permute-start.10) | collective-permute-done | bytes 196640 | tf_op jit(solution)/shard_map/ppermute | solution.py:33
  51.8 1.0 %collective-permute-start.12 = (bf16[1,256,384]{2,1,0:T(8,128)(2,1)S(1)}, bf16[1,256,384]{2,1,0:T(8,128)(2,1)}, u32[]{:S(2)}, u32[]{:S(2)}) collective-permute-start(bf16[1,256,384]{2,1,0:T(8,128)(2,1)S(1)} %collective-permute-done.10), channel_id=1, source_target_pairs={{0,2},{2,4},{4,6},{6,7},{7,5},{5,3},{3,1},{1,0},{8,10},{10,12},{12... | collective-permute-start | bytes 589832 | tf_op jit(solution)/shard_map/ppermute | solution.py:33
  52.8 1.0 %collective-permute-start.13 = (bf16[1,256,384]{2,1,0:T(8,128)(2,1)S(1)}, bf16[1,256,384]{2,1,0:T(8,128)(2,1)}, u32[]{:S(2)}, u32[]{:S(2)}) collective-permute-start(bf16[1,256,384]{2,1,0:T(8,128)(2,1)S(1)} %collective-permute-done.11), channel_id=1, source_target_pairs={{0,1},{2,0},{4,2},{6,4},{7,6},{5,7},{3,5},{1,3},{8,9},{10,8},{12,1... | collective-permute-start | bytes 589832 | tf_op jit(solution)/shard_map/ppermute | solution.py:34
  53.8 2.2 %collective-permute-done.5 = bf16[1,256,384]{2,1,0:T(8,128)(2,1)S(1)} collective-permute-done((bf16[1,256,384]{2,1,0:T(8,128)(2,1)S(1)}, bf16[1,256,384]{2,1,0:T(8,128)(2,1)S(1)}, u32[]{:S(2)}, u32[]{:S(2)}) %collective-permute-start.5) | collective-permute-done | bytes 196640 | tf_op jit(solution)/shard_map/ppermute | solution.py:33
  56.0 1.0 %collective-permute-start.7 = (bf16[1,256,384]{2,1,0:T(8,128)(2,1)S(1)}, bf16[1,256,384]{2,1,0:T(8,128)(2,1)S(1)}, u32[]{:S(2)}, u32[]{:S(2)}) collective-permute-start(bf16[1,256,384]{2,1,0:T(8,128)(2,1)S(1)} %collective-permute-done.5), channel_id=1, source_target_pairs={{0,2},{2,4},{4,6},{6,7},{7,5},{5,3},{3,1},{1,0},{8,10},{10,12},{12... | collective-permute-start | bytes 589832 | tf_op jit(solution)/shard_map/ppermute | solution.py:33
  57.1 1.1 %collective-permute-start.8 = (bf16[1,256,384]{2,1,0:T(8,128)(2,1)S(1)}, bf16[1,256,384]{2,1,0:T(8,128)(2,1)S(1)}, u32[]{:S(2)}, u32[]{:S(2)}) collective-permute-start(bf16[1,256,384]{2,1,0:T(8,128)(2,1)S(1)} %collective-permute-done.6), channel_id=1, source_target_pairs={{0,1},{2,0},{4,2},{6,4},{7,6},{5,7},{3,5},{1,3},{8,9},{10,8},{12,1... | collective-permute-start | bytes 589832 | tf_op jit(solution)/shard_map/ppermute | solution.py:34
  58.1 0.7 constant_dynamic-update-slice_fusion.4
  58.9 0.7 constant_dynamic-update-slice_fusion.3
  59.5 0.8 collective-permute-done.12
  60.3 1.0 %collective-permute-start.14 = (bf16[1,256,384]{2,1,0:T(8,128)(2,1)}, bf16[1,256,384]{2,1,0:T(8,128)(2,1)}, u32[]{:S(2)}, u32[]{:S(2)}) collective-permute-start(bf16[1,256,384]{2,1,0:T(8,128)(2,1)} %collective-permute-done.12), channel_id=1, source_target_pairs={{0,2},{2,4},{4,6},{6,7},{7,5},{5,3},{3,1},{1,0},{8,10},{10,12},{12... | collective-permute-start | bytes 589832 | tf_op jit(solution)/shard_map/ppermute | solution.py:33
  61.3 1.0 %collective-permute-start.15 = (bf16[1,256,384]{2,1,0:T(8,128)(2,1)}, bf16[1,256,384]{2,1,0:T(8,128)(2,1)}, u32[]{:S(2)}, u32[]{:S(2)}) collective-permute-start(bf16[1,256,384]{2,1,0:T(8,128)(2,1)} %collective-permute-done.13), channel_id=1, source_target_pairs={{0,1},{2,0},{4,2},{6,4},{7,6},{5,7},{3,5},{1,3},{8,9},{10,8},{12,1... | collective-permute-start | bytes 589832 | tf_op jit(solution)/shard_map/ppermute | solution.py:34
  62.3 1.0 %constant_dynamic-update-slice_fusion.12 = bf16[1,2048,384]{2,1,0:T(8,128)(2,1)S(1)} fusion(bf16[1,2048,384]{2,1,0:T(8,128)(2,1)S(1)} %constant_dynamic-update-slice_fusion.13, bf16[1,256,384]{2,1,0:T(8,128)(2,1)} %collective-permute-done.12), kind=kLoop, calls=%fused_computation.118 | loop fusion | bytes 393216
  63.3 1.1 %collective-permute-done.7 = bf16[1,256,384]{2,1,0:T(8,128)(2,1)S(1)} collective-permute-done((bf16[1,256,384]{2,1,0:T(8,128)(2,1)S(1)}, bf16[1,256,384]{2,1,0:T(8,128)(2,1)S(1)}, u32[]{:S(2)}, u32[]{:S(2)}) %collective-permute-start.7) | collective-permute-done | bytes 196640 | tf_op jit(solution)/shard_map/ppermute | solution.py:33
  64.4 1.0 %collective-permute-start.9 = (bf16[1,256,384]{2,1,0:T(8,128)(2,1)S(1)}, bf16[1,256,384]{2,1,0:T(8,128)(2,1)S(1)}, u32[]{:S(2)}, u32[]{:S(2)}) collective-permute-start(bf16[1,256,384]{2,1,0:T(8,128)(2,1)S(1)} %collective-permute-done.7), channel_id=1, source_target_pairs={{0,2},{2,4},{4,6},{6,7},{7,5},{5,3},{3,1},{1,0},{8,10},{10,12},{12... | collective-permute-start | bytes 589832 | tf_op jit(solution)/shard_map/ppermute | solution.py:37
  65.4 1.0 %constant_dynamic-update-slice_fusion.11 = bf16[1,2048,384]{2,1,0:T(8,128)(2,1)S(1)} fusion(bf16[1,2048,384]{2,1,0:T(8,128)(2,1)S(1)} %constant_dynamic-update-slice_fusion.12, bf16[1,256,384]{2,1,0:T(8,128)(2,1)} %collective-permute-done.13), kind=kLoop, calls=%fused_computation.117 | loop fusion | bytes 393216
  66.4 0.8 constant_dynamic-update-slice_fusion.2
  67.1 0.7 constant_dynamic-update-slice_fusion.1
  67.8 3.8 %collective-permute-done.9 = bf16[1,256,384]{2,1,0:T(8,128)(2,1)S(1)} collective-permute-done((bf16[1,256,384]{2,1,0:T(8,128)(2,1)S(1)}, bf16[1,256,384]{2,1,0:T(8,128)(2,1)S(1)}, u32[]{:S(2)}, u32[]{:S(2)}) %collective-permute-start.9) | collective-permute-done | bytes 196640 | tf_op jit(solution)/shard_map/ppermute | solution.py:37
  71.7 0.7 constant_dynamic-update-slice_fusion
  72.4 3.2 %fusion.118 = (f32[256]{0:T(256)S(1)}, f32[256,2048]{1,0:T(8,128)S(1)}) fusion(bf16[256,384]{1,0:T(8,128)(2,1)S(1)} %convolution_convert_fusion.5, bf16[384,384]{1,0:T(8,128)(2,1)S(1)} %copy-done, bf16[1,2048,384]{2,1,0:T(8,128)(2,1)} %constant_dynamic-update-slice_fusion), kind=kOutput, calls=%fused_computation.165 | convolution fusion | flops 1008467712 | bytes 4162560 | tf_op jit(solution)/shard_map/fqc,fkc->fqk/dot_general | solution.py:120
  75.5 0.4 fusion.2
  76.0 3.2 %fusion.54 = bf16[256,384]{1,0:T(8,128)(2,1)S(1)} fusion(bf16[384,384]{1,0:T(8,128)(2,1)} %param.18, bf16[1,2048,384]{2,1,0:T(8,128)(2,1)} %constant_dynamic-update-slice_fusion, f32[256,2048]{1,0:T(8,128)S(1)} %get-tuple-element.26, f32[256]{0:T(256)S(1)} %get-tuple-element.25, f32[256]{0:T(256)S(1)} %fusion.2), kind=kOutput, calls=%fused_computation.54 | convolution fusion | flops 1008664576 | bytes 4163584 | tf_op jit(solution)/shard_map/fqk,fkc->fqc/dot_general | solution.py:126
  79.1 1.2 %collective-permute-start.16 = (bf16[1,256,384]{2,1,0:T(8,128)(2,1)}, bf16[1,256,384]{2,1,0:T(8,128)(2,1)S(1)}, u32[]{:S(2)}, u32[]{:S(2)}) collective-permute-start(bf16[1,256,384]{2,1,0:T(8,128)(2,1)} %collective-permute-done.14), channel_id=1, source_target_pairs={{0,2},{2,4},{4,6},{6,7},{7,5},{5,3},{3,1},{1,0},{8,10},{10,12},{12... | collective-permute-start | bytes 589832 | tf_op jit(solution)/shard_map/ppermute | solution.py:37
  80.3 1.7 %constant_dynamic-update-slice_fusion.10 = bf16[1,2048,384]{2,1,0:T(8,128)(2,1)} fusion(bf16[1,2048,384]{2,1,0:T(8,128)(2,1)} %copy-done.5, bf16[1,256,384]{2,1,0:T(8,128)(2,1)} %collective-permute-done.14), kind=kLoop, calls=%fused_computation.116 | loop fusion | bytes 393216
  82.0 1.6 %constant_dynamic-update-slice_fusion.9 = bf16[1,2048,384]{2,1,0:T(8,128)(2,1)} fusion(bf16[1,2048,384]{2,1,0:T(8,128)(2,1)} %constant_dynamic-update-slice_fusion.10, bf16[1,256,384]{2,1,0:T(8,128)(2,1)} %collective-permute-done.15), kind=kLoop, calls=%fused_computation.115 | loop fusion | bytes 393216
  83.6 0.3 fusion.44
  83.8 1.5 %collective-permute-done.16 = bf16[1,256,384]{2,1,0:T(8,128)(2,1)S(1)} collective-permute-done((bf16[1,256,384]{2,1,0:T(8,128)(2,1)}, bf16[1,256,384]{2,1,0:T(8,128)(2,1)S(1)}, u32[]{:S(2)}, u32[]{:S(2)}) %collective-permute-start.16) | collective-permute-done | bytes 196640 | tf_op jit(solution)/shard_map/ppermute | solution.py:37
  85.3 0.7 constant_dynamic-update-slice_fusion.8
  86.0 3.3 %fusion.115 = (f32[256]{0:T(256)S(1)}, f32[256,2048]{1,0:T(8,128)S(1)}) fusion(bf16[256,384]{1,0:T(8,128)(2,1)} %convolution_convert_fusion.4, bf16[384,384]{1,0:T(8,128)(2,1)S(1)} %copy-done, bf16[1,2048,384]{2,1,0:T(8,128)(2,1)} %constant_dynamic-update-slice_fusion.8), kind=kOutput, calls=%fused_computation.164 | convolution fusion | flops 1008467712 | bytes 4162560 | tf_op jit(solution)/shard_map/fqc,fkc->fqk/dot_general | solution.py:120
  89.3 0.4 fusion.4
  89.7 3.1 %fusion.48 = bf16[256,384]{1,0:T(8,128)(2,1)S(1)} fusion(bf16[384,384]{1,0:T(8,128)(2,1)} %param.18, bf16[1,2048,384]{2,1,0:T(8,128)(2,1)} %constant_dynamic-update-slice_fusion.8, f32[256,2048]{1,0:T(8,128)S(1)} %get-tuple-element.24, f32[256]{0:T(256)S(1)} %get-tuple-element.23, f32[256]{0:T(256)S(1)} %fusion.4), kind=kOutput, calls=%fused_computation.52 | convolution fusion | flops 1008664576 | bytes 4163584 | tf_op jit(solution)/shard_map/fqk,fkc->fqc/dot_general | solution.py:126
  92.9 0.3 fusion.43
  93.1 0.8 pad_maximum_fusion.1
  (65 shorter events, 3.0 us)
Async XLA Ops:
  0.0 72.4 %copy-start = (bf16[384,384]{1,0:T(8,128)(2,1)S(1)}, bf16[384,384]{1,0:T(8,128)(2,1)}, u32[]{:S(2)}) copy-start(bf16[384,384]{1,0:T(8,128)(2,1)} %param.17) | copy-start | bytes 884740
  0.0 15.4 %copy-start.1 = (bf16[2,2,128,384]{3,2,1,0:T(8,128)(2,1)S(1)}, bf16[2,2,128,384]{3,2,1,0:T(8,128)(2,1)}, u32[]{:S(2)}) copy-start(bf16[2,2,128,384]{3,2,1,0:T(8,128)(2,1)} %param.10) | copy-start | bytes 1179652
  0.0 15.5 %copy-start.9 = (f32[384]{0:T(512)S(1)}, f32[384]{0:T(512)}, u32[]{:S(2)}) copy-start(f32[384]{0:T(512)} %param.12) | copy-start | bytes 4612
  1.1 9.8 %collective-permute-start.1 = (bf16[2,1,128,384]{3,2,1,0:T(8,128)(2,1)S(1)}, bf16[2,1,128,384]{3,2,1,0:T(8,128)(2,1)S(1)}, u32[]{:S(2)}, u32[]{:S(2)}) collective-permute-start(bf16[2,1,128,384]{3,2,1,0:T(8,128)(2,1)S(1)} %get-tuple-element.18), channel_id=1, source_target_pairs={{1,0},{2,1},{3,2},{4,3},{5,4},{6,5},{7,6},{9,8},{10,9},{11,10},{12... | collective-permute-start | bytes 589832 | tf_op jit(solution)/shard_map/ppermute | solution.py:17
  2.4 12.8 %collective-permute-start = (bf16[2,1,128,384]{3,2,1,0:T(8,128)(2,1)S(1)}, bf16[2,1,128,384]{3,2,1,0:T(8,128)(2,1)S(1)}, u32[]{:S(2)}, u32[]{:S(2)}) collective-permute-start(bf16[2,1,128,384]{3,2,1,0:T(8,128)(2,1)S(1)} %get-tuple-element.17), channel_id=1, source_target_pairs={{0,1},{1,2},{2,3},{3,4},{4,5},{5,6},{6,7},{8,9},{9,10},{10,11},{11... | collective-permute-start | bytes 589832 | tf_op jit(solution)/shard_map/ppermute | solution.py:15
  16.0 0.7 copy-start.8
  16.3 0.9 copy-start.2
  16.3 2.6 %collective-permute-start.2 = (bf16[2,4,130,384]{3,2,1,0:T(8,128)(2,1)S(1)}, bf16[2,4,130,384]{3,2,1,0:T(8,128)(2,1)}, u32[]{:S(2)}, u32[]{:S(2)}) collective-permute-start(bf16[2,4,130,384]{3,2,1,0:T(8,128)(2,1)S(1)} %fusion.65), channel_id=1, source_target_pairs={{0,8},{8,0},{1,9},{9,1},{2,10},{10,2},{3,11},{11,3},{4,12},{12,4},... | collective-permute-start | bytes 2396168 | tf_op jit(solution)/shard_map/ppermute | solution.py:71
  23.1 3.7 %slice-start = ((s8[7962624]{0:T(1024)(128)(4,1)}), s8[4194304]{0:T(1024)(128)(4,1)S(1)}, s32[]{:S(2)}) async-start(s8[7962624]{0:T(1024)(128)(4,1)} %bitcast.122), calls=%async_computation | async-start | bytes 8388608
  25.3 2.3 %slice-start.1 = ((s8[7962624]{0:T(1024)(128)(4,1)}), s8[3768320]{0:T(1024)(128)(4,1)S(1)}, s32[]{:S(2)}) async-start(s8[7962624]{0:T(1024)(128)(4,1)} %bitcast.122), calls=%async_computation.1 | async-start | bytes 7536640
  26.5 1.0 %copy-start.10 = (pred[8,17]{0,1:T(8,128)(4,1)S(1)}, pred[8,17]{0,1:T(8,128)(4,1)}, u32[]{:S(2)}) copy-start(pred[8,17]{0,1:T(8,128)(4,1)} %constant.108) | copy-start | bytes 412
  30.7 0.7 copy-start.6
  30.8 0.8 copy-start.7
  30.8 4.2 %copy-start.4 = (bf16[384,384]{1,0:T(8,128)(2,1)S(1)}, bf16[384,384]{1,0:T(8,128)(2,1)}, u32[]{:S(2)}) copy-start(bf16[384,384]{1,0:T(8,128)(2,1)} %param.16) | copy-start | bytes 884740
  31.7 7.0 %collective-permute-start.4 = (bf16[1,256,384]{2,1,0:T(8,128)(2,1)S(1)}, bf16[1,256,384]{2,1,0:T(8,128)(2,1)S(1)}, u32[]{:S(2)}, u32[]{:S(2)}) collective-permute-start(bf16[1,256,384]{2,1,0:T(8,128)(2,1)S(1)} %bitcast.110), channel_id=1, source_target_pairs={{0,1},{2,0},{4,2},{6,4},{7,6},{5,7},{3,5},{1,3},{8,9},{10,8},{12,1... | collective-permute-start | bytes 589832 | tf_op jit(solution)/shard_map/ppermute | solution.py:34
  35.0 11.3 %collective-permute-start.3 = (bf16[1,256,384]{2,1,0:T(8,128)(2,1)S(1)}, bf16[1,256,384]{2,1,0:T(8,128)(2,1)S(1)}, u32[]{:S(2)}, u32[]{:S(2)}) collective-permute-start(bf16[1,256,384]{2,1,0:T(8,128)(2,1)S(1)} %bitcast.112), channel_id=1, source_target_pairs={{0,2},{2,4},{4,6},{6,7},{7,5},{5,3},{3,1},{1,0},{8,10},{10,12},{12... | collective-permute-start | bytes 589832 | tf_op jit(solution)/shard_map/ppermute | solution.py:33
  43.7 8.1 %collective-permute-start.10 = (bf16[1,256,384]{2,1,0:T(8,128)(2,1)S(1)}, bf16[1,256,384]{2,1,0:T(8,128)(2,1)S(1)}, u32[]{:S(2)}, u32[]{:S(2)}) collective-permute-start(bf16[1,256,384]{2,1,0:T(8,128)(2,1)S(1)} %bitcast.114), channel_id=1, source_target_pairs={{0,2},{2,4},{4,6},{6,7},{7,5},{5,3},{3,1},{1,0},{8,10},{10,12},{12... | collective-permute-start | bytes 589832 | tf_op jit(solution)/shard_map/ppermute | solution.py:33
  45.4 7.4 %collective-permute-start.11 = (bf16[1,256,384]{2,1,0:T(8,128)(2,1)S(1)}, bf16[1,256,384]{2,1,0:T(8,128)(2,1)S(1)}, u32[]{:S(2)}, u32[]{:S(2)}) collective-permute-start(bf16[1,256,384]{2,1,0:T(8,128)(2,1)S(1)} %bitcast.115), channel_id=1, source_target_pairs={{0,1},{2,0},{4,2},{6,4},{7,6},{5,7},{3,5},{1,3},{8,9},{10,8},{12,1... | collective-permute-start | bytes 589832 | tf_op jit(solution)/shard_map/ppermute | solution.py:34
  47.7 8.3 %collective-permute-start.5 = (bf16[1,256,384]{2,1,0:T(8,128)(2,1)S(1)}, bf16[1,256,384]{2,1,0:T(8,128)(2,1)S(1)}, u32[]{:S(2)}, u32[]{:S(2)}) collective-permute-start(bf16[1,256,384]{2,1,0:T(8,128)(2,1)S(1)} %collective-permute-done.3), channel_id=1, source_target_pairs={{0,2},{2,4},{4,6},{6,7},{7,5},{5,3},{3,1},{1,0},{8,10},{10,12},{12... | collective-permute-start | bytes 589832 | tf_op jit(solution)/shard_map/ppermute | solution.py:33
  48.8 8.2 %collective-permute-start.6 = (bf16[1,256,384]{2,1,0:T(8,128)(2,1)S(1)}, bf16[1,256,384]{2,1,0:T(8,128)(2,1)S(1)}, u32[]{:S(2)}, u32[]{:S(2)}) collective-permute-start(bf16[1,256,384]{2,1,0:T(8,128)(2,1)S(1)} %collective-permute-done.4), channel_id=1, source_target_pairs={{0,1},{2,0},{4,2},{6,4},{7,6},{5,7},{3,5},{1,3},{8,9},{10,8},{12,1... | collective-permute-start | bytes 589832 | tf_op jit(solution)/shard_map/ppermute | solution.py:34
  51.8 8.5 %collective-permute-start.12 = (bf16[1,256,384]{2,1,0:T(8,128)(2,1)S(1)}, bf16[1,256,384]{2,1,0:T(8,128)(2,1)}, u32[]{:S(2)}, u32[]{:S(2)}) collective-permute-start(bf16[1,256,384]{2,1,0:T(8,128)(2,1)S(1)} %collective-permute-done.10), channel_id=1, source_target_pairs={{0,2},{2,4},{4,6},{6,7},{7,5},{5,3},{3,1},{1,0},{8,10},{10,12},{12... | collective-permute-start | bytes 589832 | tf_op jit(solution)/shard_map/ppermute | solution.py:33
  52.8 8.5 %collective-permute-start.13 = (bf16[1,256,384]{2,1,0:T(8,128)(2,1)S(1)}, bf16[1,256,384]{2,1,0:T(8,128)(2,1)}, u32[]{:S(2)}, u32[]{:S(2)}) collective-permute-start(bf16[1,256,384]{2,1,0:T(8,128)(2,1)S(1)} %collective-permute-done.11), channel_id=1, source_target_pairs={{0,1},{2,0},{4,2},{6,4},{7,6},{5,7},{3,5},{1,3},{8,9},{10,8},{12,1... | collective-permute-start | bytes 589832 | tf_op jit(solution)/shard_map/ppermute | solution.py:34
  56.0 8.4 %collective-permute-start.7 = (bf16[1,256,384]{2,1,0:T(8,128)(2,1)S(1)}, bf16[1,256,384]{2,1,0:T(8,128)(2,1)S(1)}, u32[]{:S(2)}, u32[]{:S(2)}) collective-permute-start(bf16[1,256,384]{2,1,0:T(8,128)(2,1)S(1)} %collective-permute-done.5), channel_id=1, source_target_pairs={{0,2},{2,4},{4,6},{6,7},{7,5},{5,3},{3,1},{1,0},{8,10},{10,12},{12... | collective-permute-start | bytes 589832 | tf_op jit(solution)/shard_map/ppermute | solution.py:33
  57.1 10.1 %collective-permute-start.8 = (bf16[1,256,384]{2,1,0:T(8,128)(2,1)S(1)}, bf16[1,256,384]{2,1,0:T(8,128)(2,1)S(1)}, u32[]{:S(2)}, u32[]{:S(2)}) collective-permute-start(bf16[1,256,384]{2,1,0:T(8,128)(2,1)S(1)} %collective-permute-done.6), channel_id=1, source_target_pairs={{0,1},{2,0},{4,2},{6,4},{7,6},{5,7},{3,5},{1,3},{8,9},{10,8},{12,1... | collective-permute-start | bytes 589832 | tf_op jit(solution)/shard_map/ppermute | solution.py:34
  60.3 18.8 %collective-permute-start.14 = (bf16[1,256,384]{2,1,0:T(8,128)(2,1)}, bf16[1,256,384]{2,1,0:T(8,128)(2,1)}, u32[]{:S(2)}, u32[]{:S(2)}) collective-permute-start(bf16[1,256,384]{2,1,0:T(8,128)(2,1)} %collective-permute-done.12), channel_id=1, source_target_pairs={{0,2},{2,4},{4,6},{6,7},{7,5},{5,3},{3,1},{1,0},{8,10},{10,12},{12... | collective-permute-start | bytes 589832 | tf_op jit(solution)/shard_map/ppermute | solution.py:33
  61.3 20.7 %collective-permute-start.15 = (bf16[1,256,384]{2,1,0:T(8,128)(2,1)}, bf16[1,256,384]{2,1,0:T(8,128)(2,1)}, u32[]{:S(2)}, u32[]{:S(2)}) collective-permute-start(bf16[1,256,384]{2,1,0:T(8,128)(2,1)} %collective-permute-done.13), channel_id=1, source_target_pairs={{0,1},{2,0},{4,2},{6,4},{7,6},{5,7},{3,5},{1,3},{8,9},{10,8},{12,1... | collective-permute-start | bytes 589832 | tf_op jit(solution)/shard_map/ppermute | solution.py:34
  64.4 7.2 %collective-permute-start.9 = (bf16[1,256,384]{2,1,0:T(8,128)(2,1)S(1)}, bf16[1,256,384]{2,1,0:T(8,128)(2,1)S(1)}, u32[]{:S(2)}, u32[]{:S(2)}) collective-permute-start(bf16[1,256,384]{2,1,0:T(8,128)(2,1)S(1)} %collective-permute-done.7), channel_id=1, source_target_pairs={{0,2},{2,4},{4,6},{6,7},{7,5},{5,3},{3,1},{1,0},{8,10},{10,12},{12... | collective-permute-start | bytes 589832 | tf_op jit(solution)/shard_map/ppermute | solution.py:37
  66.4 5.3 %copy-start.5 = (bf16[1,2048,384]{2,1,0:T(8,128)(2,1)}, bf16[1,2048,384]{2,1,0:T(8,128)(2,1)S(1)}, u32[]{:S(2)}) copy-start(bf16[1,2048,384]{2,1,0:T(8,128)(2,1)S(1)} %constant_dynamic-update-slice_fusion.11) | copy-start | bytes 4718596
  75.9 7.6 %copy-start.3 = (bf16[384,384]{1,0:T(8,128)(2,1)S(1)}, bf16[384,384]{1,0:T(8,128)(2,1)}, u32[]{:S(2)}) copy-start(bf16[384,384]{1,0:T(8,128)(2,1)} %param.19) | copy-start | bytes 884740
  79.1 6.2 %collective-permute-start.16 = (bf16[1,256,384]{2,1,0:T(8,128)(2,1)}, bf16[1,256,384]{2,1,0:T(8,128)(2,1)S(1)}, u32[]{:S(2)}, u32[]{:S(2)}) collective-permute-start(bf16[1,256,384]{2,1,0:T(8,128)(2,1)} %collective-permute-done.14), channel_id=1, source_target_pairs={{0,2},{2,4},{4,6},{6,7},{7,5},{5,3},{3,1},{1,0},{8,10},{10,12},{12... | collective-permute-start | bytes 589832 | tf_op jit(solution)/shard_map/ppermute | solution.py:37

commit v22 on v21

--- a/solution.py
+++ b/solution.py
@@ -105,7 +105,7 @@
         ).astype(jnp.bfloat16)
         pieces = ring_gather(tokens, "height", 1)
         if span + 1 < span_count:
-            tie = min(2, len(pieces) - 1)
+            tie = min(1, len(pieces) - 1)
             pieces[tie], span_window = lax.optimization_barrier(
                 (pieces[tie], window[span + 1 : span + 2])
             )

time: 94.4 us -> 94.7 us (level)
  waiting for transfers between devices: 21.7 us -> 22.8 us
    ppermute x6, waiting for transfers between devices: 5.14 us -> 9.63 us  [ring_gather(): forward = lax.ppermute(forward, axis, ahead)]
    ppermute x6, waiting for transfers between devices: 3.49 us -> 0.02 us  [ring_gather(): backward = lax.ppermute(backward, axis, behind)]
    ppermute x6, starting transfers between devices: 7.51 us -> 6.47 us  [ring_gather(): backward = lax.ppermute(backward, axis, behind)]
where the time goes in v22:
time: 94.7 us; the launch traced here: 94.2 us
  waiting for transfers between devices  22.8 us (24%)
  starting transfers between devices  21.5 us (23%)
  matrix products  20.8 us (22%)
  local copies, waits for them, and re-layouts  20.3 us (21%)
  other arithmetic  8.4 us (9%)
    unnamed x42, local copies, waits for them, and re-layouts  12.7 us
    ppermute x6, waiting for transfers between devices, ring_gather(): forward = lax.ppermute(forward, axis, ahead)  9.63 us
    ppermute x6, starting transfers between devices, ring_gather(): backward = lax.ppermute(backward, axis, behind)  6.47 us
    dot_general x2, matrix products, shards(): jnp.einsum('fqc,fkc->fqk', queries, keys_all, preferred_element_type=jnp....  6.42 us
    ppermute x6, starting transfers between devices, ring_gather(): forward = lax.ppermute(forward, axis, ahead)  6.34 us
    conv_general_dilated x2, matrix products, shards(): lax.conv_general_dilated(span_window, conv_weight, window_strides=(1, 1,...  6.33 us
    dot_general x2, matrix products, shards(): jnp.einsum('fqk,fkc->fqc', weights_exp.astype(jnp.bfloat16), values_all,...  6.27 us
    ppermute x1, starting transfers between devices, padded_2(): lax.ppermute(tail, axis, [(i, (i + 1) % count) for i in range(ends)])  5.52 us
  transfers between devices with their start and end apart: 17, of which 10 were waited for; matrix products, arithmetic and copies ran while one was open for 27% of the time, Pallas kernels for 0%

profile of v22, /device:TPU:0, one launch (start us, length us, event | category | flops | bytes accessed | tf_op | source)
XLA Modules:
  0.0 94.2 jit_solution(17248623197066146203)
XLA Ops:
  0.0 1.1 %fusion.114 = (bf16[2,1,128,384]{3,2,1,0:T(8,128)(2,1)S(1)}, bf16[2,1,128,384]{3,2,1,0:T(8,128)(2,1)S(1)}) fusion(bf16[2,2,128,384]{3,2,1,0:T(8,128)(2,1)} %param.10), kind=kLoop, calls=%fused_computation.163 | loop fusion | bytes 786432 | tf_op jit(solution)/shard_map/slice | solution.py:12
  1.1 1.3 %collective-permute-start.1 = (bf16[2,1,128,384]{3,2,1,0:T(8,128)(2,1)S(1)}, bf16[2,1,128,384]{3,2,1,0:T(8,128)(2,1)S(1)}, u32[]{:S(2)}, u32[]{:S(2)}) collective-permute-start(bf16[2,1,128,384]{3,2,1,0:T(8,128)(2,1)S(1)} %get-tuple-element.18), channel_id=1, source_target_pairs={{1,0},{2,1},{3,2},{4,3},{5,4},{6,5},{7,6},{9,8},{10,9},{11,10},{12... | collective-permute-start | bytes 589832 | tf_op jit(solution)/shard_map/ppermute | solution.py:17
  2.4 5.5 %collective-permute-start = (bf16[2,1,128,384]{3,2,1,0:T(8,128)(2,1)S(1)}, bf16[2,1,128,384]{3,2,1,0:T(8,128)(2,1)S(1)}, u32[]{:S(2)}, u32[]{:S(2)}) collective-permute-start(bf16[2,1,128,384]{3,2,1,0:T(8,128)(2,1)S(1)} %get-tuple-element.17), channel_id=1, source_target_pairs={{0,1},{1,2},{2,3},{3,4},{4,5},{5,6},{6,7},{8,9},{9,10},{10,11},{11... | collective-permute-start | bytes 589832 | tf_op jit(solution)/shard_map/ppermute | solution.py:15
  8.0 1.1 %fusion.74 = f32[2,2,128]{2,1,0:T(2,128)S(1)} fusion(bf16[2,2,128,384]{3,2,1,0:T(8,128)(2,1)} %param.10), kind=kLoop, calls=%fused_computation.74 | loop fusion | flops 589312 | bytes 395264 | tf_op jit(solution)/shard_map/reduce_sum | solution.py:43
  9.1 1.8 %collective-permute-done.1 = bf16[2,1,128,384]{3,2,1,0:T(8,128)(2,1)S(1)} collective-permute-done((bf16[2,1,128,384]{3,2,1,0:T(8,128)(2,1)S(1)}, bf16[2,1,128,384]{3,2,1,0:T(8,128)(2,1)S(1)}, u32[]{:S(2)}, u32[]{:S(2)}) %collective-permute-start.1) | collective-permute-done | bytes 196640 | tf_op jit(solution)/shard_map/ppermute | solution.py:17
  10.9 4.4 %collective-permute-done = bf16[2,1,128,384]{3,2,1,0:T(8,128)(2,1)S(1)} collective-permute-done((bf16[2,1,128,384]{3,2,1,0:T(8,128)(2,1)S(1)}, bf16[2,1,128,384]{3,2,1,0:T(8,128)(2,1)S(1)}, u32[]{:S(2)}, u32[]{:S(2)}) %collective-permute-start) | collective-permute-done | bytes 196640 | tf_op jit(solution)/shard_map/ppermute | solution.py:15
  15.5 0.5 fusion.81
  16.4 0.3 copy-done.8
  17.2 1.6 %collective-permute-done.2 = bf16[2,4,130,384]{3,2,1,0:T(8,128)(2,1)} collective-permute-done((bf16[2,4,130,384]{3,2,1,0:T(8,128)(2,1)S(1)}, bf16[2,4,130,384]{3,2,1,0:T(8,128)(2,1)}, u32[]{:S(2)}, u32[]{:S(2)}) %collective-permute-start.2) | collective-permute-done | bytes 798752 | tf_op jit(solution)/shard_map/ppermute | solution.py:71
  18.9 1.7 %maximum_maximum_fusion = bf16[5,4,130,384]{3,2,1,0:T(8,128)(2,1)S(1)} fusion(bf16[2,4,130,384]{3,2,1,0:T(8,128)(2,1)} %collective-permute-done.2, bf16[2,4,130,384]{3,2,1,0:T(8,128)(2,1)} %copy-done.2, bf16[5]{0:T(256)(128)(2,1)S(1)} %pad.17.clone), kind=kLoop, calls=%fused_computation.15 | loop fusion | flops 1996800 | bytes 3594250 | tf_op jit(solution)/shard_map/concatenate | solution.py:74
  20.6 2.5 %gather_fusion = bf16[6,4,130,384]{3,2,1,0:T(8,128)(2,1)} fusion(bf16[5,4,130,384]{3,2,1,0:T(8,128)(2,1)S(1)} %maximum_maximum_fusion, s32[1024]{0:T(1024)S(1)} %pad_clamp_fusion), kind=kCustom, calls=%fused_computation | custom fusion | bytes 4792344 | tf_op jit(solution)/shard_map/jit(_take)/gather | solution.py:83
  23.1 2.2 %broadcast_select_fusion = bf16[6,4,130,384]{3,2,1,0:T(8,128)(2,1)S(1)} fusion(bf16[6,4,130,384]{3,2,1,0:T(8,128)(2,1)} %gather_fusion, pred[6]{0:T(512)(128)(4,1)S(1)} %compare_and_fusion), kind=kLoop, calls=%fused_computation.12 | loop fusion | flops 1198080 | bytes 4792326 | tf_op jit(solution)/shard_map/jit(_take)/select_n | solution.py:83
  25.6 0.5 copy.23
  26.1 0.5 pad.5.clone
  26.8 0.8 slice-done.1
  27.6 3.2 %fusion.38 = f32[1,2,8,17,384]{4,2,3,1,0:T(8,128)S(1)} fusion(bf16[3,3,3,384,384]{4,3,2,1,0:T(8,128)(2,1)S(1)} %bitcast.123, bf16[3,4,1,7,2,384]{5,3,4,1,0,2:T(8,128)(2,1)S(1)} %slice.57, bf16[3,4,1,8,17,384]{5,3,4,1,0,2:T(8,128)(2,1)S(1)} %copy.13, pred[8,17]{0,1:T(8,128)(4,1)S(1)} %copy-done.10), kind=kOutput, calls=%fused_computation.44 | convolution fusion | flops 2170140672 | bytes 9762952 | tf_op jit(solution)/shard_map/conv_general_dilated | solution.py:90
  31.1 0.3 copy-done.6
  31.7 1.7 %collective-permute-start.3 = (bf16[1,256,384]{2,1,0:T(8,128)(2,1)S(1)}, bf16[1,256,384]{2,1,0:T(8,128)(2,1)S(1)}, u32[]{:S(2)}, u32[]{:S(2)}) collective-permute-start(bf16[1,256,384]{2,1,0:T(8,128)(2,1)S(1)} %bitcast.110), channel_id=1, source_target_pairs={{0,2},{2,4},{4,6},{6,7},{7,5},{5,3},{3,1},{1,0},{8,10},{10,12},{12... | collective-permute-start | bytes 589832 | tf_op jit(solution)/shard_map/ppermute | solution.py:33
  33.4 0.7 constant_dynamic-update-slice_fusion.7
  34.1 0.8 collective-permute-start.4
  35.2 4.2 %collective-permute-done.3 = bf16[1,256,384]{2,1,0:T(8,128)(2,1)S(1)} collective-permute-done((bf16[1,256,384]{2,1,0:T(8,128)(2,1)S(1)}, bf16[1,256,384]{2,1,0:T(8,128)(2,1)S(1)}, u32[]{:S(2)}, u32[]{:S(2)}) %collective-permute-start.3) | collective-permute-done | bytes 196640 | tf_op jit(solution)/shard_map/ppermute | solution.py:33
  39.5 0.5 copy.24
  39.9 0.5 pad.7.clone
  40.6 3.2 %fusion.35 = f32[1,2,8,17,384]{4,2,3,1,0:T(8,128)S(1)} fusion(bf16[3,3,3,384,384]{4,3,2,1,0:T(8,128)(2,1)S(1)} %bitcast.123, bf16[3,4,1,7,2,384]{5,3,4,1,0,2:T(8,128)(2,1)S(1)} %slice.60, bf16[3,4,1,8,17,384]{5,3,4,1,0,2:T(8,128)(2,1)S(1)} %copy.18, pred[8,17]{0,1:T(8,128)(4,1)S(1)} %copy-done.10), kind=kOutput, calls=%fused_computation.43 | convolution fusion | flops 2170140672 | bytes 9762952 | tf_op jit(solution)/shard_map/conv_general_dilated | solution.py:90
  44.4 1.0 %collective-permute-start.10 = (bf16[1,256,384]{2,1,0:T(8,128)(2,1)S(1)}, bf16[1,256,384]{2,1,0:T(8,128)(2,1)S(1)}, u32[]{:S(2)}, u32[]{:S(2)}) collective-permute-start(bf16[1,256,384]{2,1,0:T(8,128)(2,1)S(1)} %bitcast.114), channel_id=1, source_target_pairs={{0,2},{2,4},{4,6},{6,7},{7,5},{5,3},{3,1},{1,0},{8,10},{10,12},{12... | collective-permute-start | bytes 589832 | tf_op jit(solution)/shard_map/ppermute | solution.py:33
  45.4 1.1 %collective-permute-start.11 = (bf16[1,256,384]{2,1,0:T(8,128)(2,1)S(1)}, bf16[1,256,384]{2,1,0:T(8,128)(2,1)S(1)}, u32[]{:S(2)}, u32[]{:S(2)}) collective-permute-start(bf16[1,256,384]{2,1,0:T(8,128)(2,1)S(1)} %bitcast.115), channel_id=1, source_target_pairs={{0,1},{2,0},{4,2},{6,4},{7,6},{5,7},{3,5},{1,3},{8,9},{10,8},{12,1... | collective-permute-start | bytes 589832 | tf_op jit(solution)/shard_map/ppermute | solution.py:34
  46.5 0.9 collective-permute-start.5
  47.4 0.7 constant_dynamic-update-slice_fusion.6
  48.1 1.1 %collective-permute-start.6 = (bf16[1,256,384]{2,1,0:T(8,128)(2,1)S(1)}, bf16[1,256,384]{2,1,0:T(8,128)(2,1)S(1)}, u32[]{:S(2)}, u32[]{:S(2)}) collective-permute-start(bf16[1,256,384]{2,1,0:T(8,128)(2,1)S(1)} %collective-permute-done.4), channel_id=1, source_target_pairs={{0,1},{2,0},{4,2},{6,4},{7,6},{5,7},{3,5},{1,3},{8,9},{10,8},{12,1... | collective-permute-start | bytes 589832 | tf_op jit(solution)/shard_map/ppermute | solution.py:34
  49.3 0.7 constant_dynamic-update-slice_fusion.5
  49.9 0.9 %convolution_convert_fusion.4 = bf16[256,384]{1,0:T(8,128)(2,1)} fusion(bf16[256,384]{1,0:T(8,128)(2,1)S(1)} %bitcast.117, bf16[384,384]{1,0:T(8,128)(2,1)S(1)} %copy-done.4), kind=kOutput, calls=%fused_computation.47 | convolution fusion | flops 75595776 | bytes 688128 | tf_op jit(solution)/shard_map/ftc,cd->ftd/dot_general | solution.py:103
  50.9 1.4 %collective-permute-done.10 = bf16[1,256,384]{2,1,0:T(8,128)(2,1)S(1)} collective-permute-done((bf16[1,256,384]{2,1,0:T(8,128)(2,1)S(1)}, bf16[1,256,384]{2,1,0:T(8,128)(2,1)S(1)}, u32[]{:S(2)}, u32[]{:S(2)}) %collective-permute-start.10) | collective-permute-done | bytes 196640 | tf_op jit(solution)/shard_map/ppermute | solution.py:33
  52.3 0.9 collective-permute-start.12
  53.2 1.1 %collective-permute-start.13 = (bf16[1,256,384]{2,1,0:T(8,128)(2,1)S(1)}, bf16[1,256,384]{2,1,0:T(8,128)(2,1)}, u32[]{:S(2)}, u32[]{:S(2)}) collective-permute-start(bf16[1,256,384]{2,1,0:T(8,128)(2,1)S(1)} %collective-permute-done.11), channel_id=1, source_target_pairs={{0,1},{2,0},{4,2},{6,4},{7,6},{5,7},{3,5},{1,3},{8,9},{10,8},{12,1... | collective-permute-start | bytes 589832 | tf_op jit(solution)/shard_map/ppermute | solution.py:34
  54.3 2.2 %collective-permute-done.5 = bf16[1,256,384]{2,1,0:T(8,128)(2,1)S(1)} collective-permute-done((bf16[1,256,384]{2,1,0:T(8,128)(2,1)S(1)}, bf16[1,256,384]{2,1,0:T(8,128)(2,1)S(1)}, u32[]{:S(2)}, u32[]{:S(2)}) %collective-permute-start.5) | collective-permute-done | bytes 196640 | tf_op jit(solution)/shard_map/ppermute | solution.py:33
  56.5 0.9 collective-permute-start.7
  57.5 1.1 %collective-permute-start.8 = (bf16[1,256,384]{2,1,0:T(8,128)(2,1)S(1)}, bf16[1,256,384]{2,1,0:T(8,128)(2,1)S(1)}, u32[]{:S(2)}, u32[]{:S(2)}) collective-permute-start(bf16[1,256,384]{2,1,0:T(8,128)(2,1)S(1)} %collective-permute-done.6), channel_id=1, source_target_pairs={{0,1},{2,0},{4,2},{6,4},{7,6},{5,7},{3,5},{1,3},{8,9},{10,8},{12,1... | collective-permute-start | bytes 589832 | tf_op jit(solution)/shard_map/ppermute | solution.py:34
  58.7 0.7 constant_dynamic-update-slice_fusion.4
  59.4 0.7 constant_dynamic-update-slice_fusion.3
  60.1 0.8 collective-permute-done.12
  60.8 0.9 collective-permute-start.14
  61.8 1.1 %collective-permute-start.15 = (bf16[1,256,384]{2,1,0:T(8,128)(2,1)}, bf16[1,256,384]{2,1,0:T(8,128)(2,1)}, u32[]{:S(2)}, u32[]{:S(2)}) collective-permute-start(bf16[1,256,384]{2,1,0:T(8,128)(2,1)} %collective-permute-done.13), channel_id=1, source_target_pairs={{0,1},{2,0},{4,2},{6,4},{7,6},{5,7},{3,5},{1,3},{8,9},{10,8},{12,1... | collective-permute-start | bytes 589832 | tf_op jit(solution)/shard_map/ppermute | solution.py:34
  62.9 1.0 %constant_dynamic-update-slice_fusion.12 = bf16[1,2048,384]{2,1,0:T(8,128)(2,1)S(1)} fusion(bf16[1,2048,384]{2,1,0:T(8,128)(2,1)S(1)} %constant_dynamic-update-slice_fusion.13, bf16[1,256,384]{2,1,0:T(8,128)(2,1)} %collective-permute-done.12), kind=kLoop, calls=%fused_computation.118 | loop fusion | bytes 393216
  63.8 1.1 %collective-permute-done.7 = bf16[1,256,384]{2,1,0:T(8,128)(2,1)S(1)} collective-permute-done((bf16[1,256,384]{2,1,0:T(8,128)(2,1)S(1)}, bf16[1,256,384]{2,1,0:T(8,128)(2,1)S(1)}, u32[]{:S(2)}, u32[]{:S(2)}) %collective-permute-start.7) | collective-permute-done | bytes 196640 | tf_op jit(solution)/shard_map/ppermute | solution.py:33
  64.9 0.9 collective-permute-start.9
  65.9 1.0 %constant_dynamic-update-slice_fusion.11 = bf16[1,2048,384]{2,1,0:T(8,128)(2,1)S(1)} fusion(bf16[1,2048,384]{2,1,0:T(8,128)(2,1)S(1)} %constant_dynamic-update-slice_fusion.12, bf16[1,256,384]{2,1,0:T(8,128)(2,1)} %collective-permute-done.13), kind=kLoop, calls=%fused_computation.117 | loop fusion | bytes 393216
  66.8 0.8 constant_dynamic-update-slice_fusion.2
  67.6 0.7 constant_dynamic-update-slice_fusion.1
  68.3 3.7 %collective-permute-done.9 = bf16[1,256,384]{2,1,0:T(8,128)(2,1)S(1)} collective-permute-done((bf16[1,256,384]{2,1,0:T(8,128)(2,1)S(1)}, bf16[1,256,384]{2,1,0:T(8,128)(2,1)S(1)}, u32[]{:S(2)}, u32[]{:S(2)}) %collective-permute-start.9) | collective-permute-done | bytes 196640 | tf_op jit(solution)/shard_map/ppermute | solution.py:37
  72.0 0.7 constant_dynamic-update-slice_fusion
  72.7 3.2 %fusion.118 = (f32[256]{0:T(256)S(1)}, f32[256,2048]{1,0:T(8,128)S(1)}) fusion(bf16[256,384]{1,0:T(8,128)(2,1)S(1)} %convolution_convert_fusion.5, bf16[384,384]{1,0:T(8,128)(2,1)S(1)} %copy-done, bf16[1,2048,384]{2,1,0:T(8,128)(2,1)} %constant_dynamic-update-slice_fusion), kind=kOutput, calls=%fused_computation.165 | convolution fusion | flops 1008467712 | bytes 4162560 | tf_op jit(solution)/shard_map/fqc,fkc->fqk/dot_general | solution.py:120
  75.8 0.4 fusion.2
  76.3 3.2 %fusion.54 = bf16[256,384]{1,0:T(8,128)(2,1)S(1)} fusion(bf16[384,384]{1,0:T(8,128)(2,1)} %param.18, bf16[1,2048,384]{2,1,0:T(8,128)(2,1)} %constant_dynamic-update-slice_fusion, f32[256,2048]{1,0:T(8,128)S(1)} %get-tuple-element.26, f32[256]{0:T(256)S(1)} %get-tuple-element.25, f32[256]{0:T(256)S(1)} %fusion.2), kind=kOutput, calls=%fused_computation.54 | convolution fusion | flops 1008664576 | bytes 4163584 | tf_op jit(solution)/shard_map/fqk,fkc->fqc/dot_general | solution.py:126
  79.4 0.8 collective-permute-start.16
  80.3 1.7 %constant_dynamic-update-slice_fusion.10 = bf16[1,2048,384]{2,1,0:T(8,128)(2,1)} fusion(bf16[1,2048,384]{2,1,0:T(8,128)(2,1)} %copy-done.5, bf16[1,256,384]{2,1,0:T(8,128)(2,1)} %collective-permute-done.14), kind=kLoop, calls=%fused_computation.116 | loop fusion | bytes 393216
  82.0 1.6 %constant_dynamic-update-slice_fusion.9 = bf16[1,2048,384]{2,1,0:T(8,128)(2,1)} fusion(bf16[1,2048,384]{2,1,0:T(8,128)(2,1)} %constant_dynamic-update-slice_fusion.10, bf16[1,256,384]{2,1,0:T(8,128)(2,1)} %collective-permute-done.15), kind=kLoop, calls=%fused_computation.115 | loop fusion | bytes 393216
  83.6 0.3 fusion.44
  83.8 1.8 %collective-permute-done.16 = bf16[1,256,384]{2,1,0:T(8,128)(2,1)S(1)} collective-permute-done((bf16[1,256,384]{2,1,0:T(8,128)(2,1)}, bf16[1,256,384]{2,1,0:T(8,128)(2,1)S(1)}, u32[]{:S(2)}, u32[]{:S(2)}) %collective-permute-start.16) | collective-permute-done | bytes 196640 | tf_op jit(solution)/shard_map/ppermute | solution.py:37
  85.6 0.7 constant_dynamic-update-slice_fusion.8
  86.3 3.3 %fusion.115 = (f32[256]{0:T(256)S(1)}, f32[256,2048]{1,0:T(8,128)S(1)}) fusion(bf16[256,384]{1,0:T(8,128)(2,1)} %convolution_convert_fusion.4, bf16[384,384]{1,0:T(8,128)(2,1)S(1)} %copy-done, bf16[1,2048,384]{2,1,0:T(8,128)(2,1)} %constant_dynamic-update-slice_fusion.8), kind=kOutput, calls=%fused_computation.164 | convolution fusion | flops 1008467712 | bytes 4162560 | tf_op jit(solution)/shard_map/fqc,fkc->fqk/dot_general | solution.py:120
  89.6 0.4 fusion.4
  90.0 3.1 %fusion.48 = bf16[256,384]{1,0:T(8,128)(2,1)S(1)} fusion(bf16[384,384]{1,0:T(8,128)(2,1)} %param.18, bf16[1,2048,384]{2,1,0:T(8,128)(2,1)} %constant_dynamic-update-slice_fusion.8, f32[256,2048]{1,0:T(8,128)S(1)} %get-tuple-element.24, f32[256]{0:T(256)S(1)} %get-tuple-element.23, f32[256]{0:T(256)S(1)} %fusion.4), kind=kOutput, calls=%fused_computation.52 | convolution fusion | flops 1008664576 | bytes 4163584 | tf_op jit(solution)/shard_map/fqk,fkc->fqc/dot_general | solution.py:126
  93.1 0.3 fusion.43
  93.4 0.8 pad_maximum_fusion.1
  (65 shorter events, 3.3 us)
Async XLA Ops:
  0.0 72.7 %copy-start = (bf16[384,384]{1,0:T(8,128)(2,1)S(1)}, bf16[384,384]{1,0:T(8,128)(2,1)}, u32[]{:S(2)}) copy-start(bf16[384,384]{1,0:T(8,128)(2,1)} %param.17) | copy-start | bytes 884740
  0.0 15.4 %copy-start.1 = (bf16[2,2,128,384]{3,2,1,0:T(8,128)(2,1)S(1)}, bf16[2,2,128,384]{3,2,1,0:T(8,128)(2,1)}, u32[]{:S(2)}) copy-start(bf16[2,2,128,384]{3,2,1,0:T(8,128)(2,1)} %param.10) | copy-start | bytes 1179652
  0.0 15.5 %copy-start.9 = (f32[384]{0:T(512)S(1)}, f32[384]{0:T(512)}, u32[]{:S(2)}) copy-start(f32[384]{0:T(512)} %param.12) | copy-start | bytes 4612
  1.1 9.8 %collective-permute-start.1 = (bf16[2,1,128,384]{3,2,1,0:T(8,128)(2,1)S(1)}, bf16[2,1,128,384]{3,2,1,0:T(8,128)(2,1)S(1)}, u32[]{:S(2)}, u32[]{:S(2)}) collective-permute-start(bf16[2,1,128,384]{3,2,1,0:T(8,128)(2,1)S(1)} %get-tuple-element.18), channel_id=1, source_target_pairs={{1,0},{2,1},{3,2},{4,3},{5,4},{6,5},{7,6},{9,8},{10,9},{11,10},{12... | collective-permute-start | bytes 589832 | tf_op jit(solution)/shard_map/ppermute | solution.py:17
  2.4 12.8 %collective-permute-start = (bf16[2,1,128,384]{3,2,1,0:T(8,128)(2,1)S(1)}, bf16[2,1,128,384]{3,2,1,0:T(8,128)(2,1)S(1)}, u32[]{:S(2)}, u32[]{:S(2)}) collective-permute-start(bf16[2,1,128,384]{3,2,1,0:T(8,128)(2,1)S(1)} %get-tuple-element.17), channel_id=1, source_target_pairs={{0,1},{1,2},{2,3},{3,4},{4,5},{5,6},{6,7},{8,9},{9,10},{10,11},{11... | collective-permute-start | bytes 589832 | tf_op jit(solution)/shard_map/ppermute | solution.py:15
  16.0 0.7 copy-start.8
  16.3 0.9 copy-start.2
  16.3 2.6 %collective-permute-start.2 = (bf16[2,4,130,384]{3,2,1,0:T(8,128)(2,1)S(1)}, bf16[2,4,130,384]{3,2,1,0:T(8,128)(2,1)}, u32[]{:S(2)}, u32[]{:S(2)}) collective-permute-start(bf16[2,4,130,384]{3,2,1,0:T(8,128)(2,1)S(1)} %fusion.65), channel_id=1, source_target_pairs={{0,8},{8,0},{1,9},{9,1},{2,10},{10,2},{3,11},{11,3},{4,12},{12,4},... | collective-permute-start | bytes 2396168 | tf_op jit(solution)/shard_map/ppermute | solution.py:71
  23.1 3.7 %slice-start = ((s8[7962624]{0:T(1024)(128)(4,1)}), s8[4194304]{0:T(1024)(128)(4,1)S(1)}, s32[]{:S(2)}) async-start(s8[7962624]{0:T(1024)(128)(4,1)} %bitcast.122), calls=%async_computation | async-start | bytes 8388608
  25.3 2.3 %slice-start.1 = ((s8[7962624]{0:T(1024)(128)(4,1)}), s8[3768320]{0:T(1024)(128)(4,1)S(1)}, s32[]{:S(2)}) async-start(s8[7962624]{0:T(1024)(128)(4,1)} %bitcast.122), calls=%async_computation.1 | async-start | bytes 7536640
  26.5 1.0 %copy-start.10 = (pred[8,17]{0,1:T(8,128)(4,1)S(1)}, pred[8,17]{0,1:T(8,128)(4,1)}, u32[]{:S(2)}) copy-start(pred[8,17]{0,1:T(8,128)(4,1)} %constant.108) | copy-start | bytes 412
  30.7 0.7 copy-start.6
  30.8 0.8 copy-start.7
  30.8 4.2 %copy-start.4 = (bf16[384,384]{1,0:T(8,128)(2,1)S(1)}, bf16[384,384]{1,0:T(8,128)(2,1)}, u32[]{:S(2)}) copy-start(bf16[384,384]{1,0:T(8,128)(2,1)} %param.16) | copy-start | bytes 884740
  31.7 7.7 %collective-permute-start.3 = (bf16[1,256,384]{2,1,0:T(8,128)(2,1)S(1)}, bf16[1,256,384]{2,1,0:T(8,128)(2,1)S(1)}, u32[]{:S(2)}, u32[]{:S(2)}) collective-permute-start(bf16[1,256,384]{2,1,0:T(8,128)(2,1)S(1)} %bitcast.110), channel_id=1, source_target_pairs={{0,2},{2,4},{4,6},{6,7},{7,5},{5,3},{3,1},{1,0},{8,10},{10,12},{12... | collective-permute-start | bytes 589832 | tf_op jit(solution)/shard_map/ppermute | solution.py:33
  34.1 14.0 %collective-permute-start.4 = (bf16[1,256,384]{2,1,0:T(8,128)(2,1)S(1)}, bf16[1,256,384]{2,1,0:T(8,128)(2,1)S(1)}, u32[]{:S(2)}, u32[]{:S(2)}) collective-permute-start(bf16[1,256,384]{2,1,0:T(8,128)(2,1)S(1)} %bitcast.112), channel_id=1, source_target_pairs={{0,1},{2,0},{4,2},{6,4},{7,6},{5,7},{3,5},{1,3},{8,9},{10,8},{12,1... | collective-permute-start | bytes 589832 | tf_op jit(solution)/shard_map/ppermute | solution.py:34
  44.4 7.9 %collective-permute-start.10 = (bf16[1,256,384]{2,1,0:T(8,128)(2,1)S(1)}, bf16[1,256,384]{2,1,0:T(8,128)(2,1)S(1)}, u32[]{:S(2)}, u32[]{:S(2)}) collective-permute-start(bf16[1,256,384]{2,1,0:T(8,128)(2,1)S(1)} %bitcast.114), channel_id=1, source_target_pairs={{0,2},{2,4},{4,6},{6,7},{7,5},{5,3},{3,1},{1,0},{8,10},{10,12},{12... | collective-permute-start | bytes 589832 | tf_op jit(solution)/shard_map/ppermute | solution.py:33
  45.4 7.8 %collective-permute-start.11 = (bf16[1,256,384]{2,1,0:T(8,128)(2,1)S(1)}, bf16[1,256,384]{2,1,0:T(8,128)(2,1)S(1)}, u32[]{:S(2)}, u32[]{:S(2)}) collective-permute-start(bf16[1,256,384]{2,1,0:T(8,128)(2,1)S(1)} %bitcast.115), channel_id=1, source_target_pairs={{0,1},{2,0},{4,2},{6,4},{7,6},{5,7},{3,5},{1,3},{8,9},{10,8},{12,1... | collective-permute-start | bytes 589832 | tf_op jit(solution)/shard_map/ppermute | solution.py:34
  46.5 10.0 %collective-permute-start.5 = (bf16[1,256,384]{2,1,0:T(8,128)(2,1)S(1)}, bf16[1,256,384]{2,1,0:T(8,128)(2,1)S(1)}, u32[]{:S(2)}, u32[]{:S(2)}) collective-permute-start(bf16[1,256,384]{2,1,0:T(8,128)(2,1)S(1)} %collective-permute-done.3), channel_id=1, source_target_pairs={{0,2},{2,4},{4,6},{6,7},{7,5},{5,3},{3,1},{1,0},{8,10},{10,12},{12... | collective-permute-start | bytes 589832 | tf_op jit(solution)/shard_map/ppermute | solution.py:33
  48.1 9.4 %collective-permute-start.6 = (bf16[1,256,384]{2,1,0:T(8,128)(2,1)S(1)}, bf16[1,256,384]{2,1,0:T(8,128)(2,1)S(1)}, u32[]{:S(2)}, u32[]{:S(2)}) collective-permute-start(bf16[1,256,384]{2,1,0:T(8,128)(2,1)S(1)} %collective-permute-done.4), channel_id=1, source_target_pairs={{0,1},{2,0},{4,2},{6,4},{7,6},{5,7},{3,5},{1,3},{8,9},{10,8},{12,1... | collective-permute-start | bytes 589832 | tf_op jit(solution)/shard_map/ppermute | solution.py:34
  52.3 8.5 %collective-permute-start.12 = (bf16[1,256,384]{2,1,0:T(8,128)(2,1)S(1)}, bf16[1,256,384]{2,1,0:T(8,128)(2,1)}, u32[]{:S(2)}, u32[]{:S(2)}) collective-permute-start(bf16[1,256,384]{2,1,0:T(8,128)(2,1)S(1)} %collective-permute-done.10), channel_id=1, source_target_pairs={{0,2},{2,4},{4,6},{6,7},{7,5},{5,3},{3,1},{1,0},{8,10},{10,12},{12... | collective-permute-start | bytes 589832 | tf_op jit(solution)/shard_map/ppermute | solution.py:33
  53.2 8.5 %collective-permute-start.13 = (bf16[1,256,384]{2,1,0:T(8,128)(2,1)S(1)}, bf16[1,256,384]{2,1,0:T(8,128)(2,1)}, u32[]{:S(2)}, u32[]{:S(2)}) collective-permute-start(bf16[1,256,384]{2,1,0:T(8,128)(2,1)S(1)} %collective-permute-done.11), channel_id=1, source_target_pairs={{0,1},{2,0},{4,2},{6,4},{7,6},{5,7},{3,5},{1,3},{8,9},{10,8},{12,1... | collective-permute-start | bytes 589832 | tf_op jit(solution)/shard_map/ppermute | solution.py:34
  56.5 8.4 %collective-permute-start.7 = (bf16[1,256,384]{2,1,0:T(8,128)(2,1)S(1)}, bf16[1,256,384]{2,1,0:T(8,128)(2,1)S(1)}, u32[]{:S(2)}, u32[]{:S(2)}) collective-permute-start(bf16[1,256,384]{2,1,0:T(8,128)(2,1)S(1)} %collective-permute-done.5), channel_id=1, source_target_pairs={{0,2},{2,4},{4,6},{6,7},{7,5},{5,3},{3,1},{1,0},{8,10},{10,12},{12... | collective-permute-start | bytes 589832 | tf_op jit(solution)/shard_map/ppermute | solution.py:33
  57.5 10.1 %collective-permute-start.8 = (bf16[1,256,384]{2,1,0:T(8,128)(2,1)S(1)}, bf16[1,256,384]{2,1,0:T(8,128)(2,1)S(1)}, u32[]{:S(2)}, u32[]{:S(2)}) collective-permute-start(bf16[1,256,384]{2,1,0:T(8,128)(2,1)S(1)} %collective-permute-done.6), channel_id=1, source_target_pairs={{0,1},{2,0},{4,2},{6,4},{7,6},{5,7},{3,5},{1,3},{8,9},{10,8},{12,1... | collective-permute-start | bytes 589832 | tf_op jit(solution)/shard_map/ppermute | solution.py:34
  60.8 18.6 %collective-permute-start.14 = (bf16[1,256,384]{2,1,0:T(8,128)(2,1)}, bf16[1,256,384]{2,1,0:T(8,128)(2,1)}, u32[]{:S(2)}, u32[]{:S(2)}) collective-permute-start(bf16[1,256,384]{2,1,0:T(8,128)(2,1)} %collective-permute-done.12), channel_id=1, source_target_pairs={{0,2},{2,4},{4,6},{6,7},{7,5},{5,3},{3,1},{1,0},{8,10},{10,12},{12... | collective-permute-start | bytes 589832 | tf_op jit(solution)/shard_map/ppermute | solution.py:33
  61.8 20.2 %collective-permute-start.15 = (bf16[1,256,384]{2,1,0:T(8,128)(2,1)}, bf16[1,256,384]{2,1,0:T(8,128)(2,1)}, u32[]{:S(2)}, u32[]{:S(2)}) collective-permute-start(bf16[1,256,384]{2,1,0:T(8,128)(2,1)} %collective-permute-done.13), channel_id=1, source_target_pairs={{0,1},{2,0},{4,2},{6,4},{7,6},{5,7},{3,5},{1,3},{8,9},{10,8},{12,1... | collective-permute-start | bytes 589832 | tf_op jit(solution)/shard_map/ppermute | solution.py:34
  64.9 7.0 %collective-permute-start.9 = (bf16[1,256,384]{2,1,0:T(8,128)(2,1)S(1)}, bf16[1,256,384]{2,1,0:T(8,128)(2,1)S(1)}, u32[]{:S(2)}, u32[]{:S(2)}) collective-permute-start(bf16[1,256,384]{2,1,0:T(8,128)(2,1)S(1)} %collective-permute-done.7), channel_id=1, source_target_pairs={{0,2},{2,4},{4,6},{6,7},{7,5},{5,3},{3,1},{1,0},{8,10},{10,12},{12... | collective-permute-start | bytes 589832 | tf_op jit(solution)/shard_map/ppermute | solution.py:37
  66.8 5.2 %copy-start.5 = (bf16[1,2048,384]{2,1,0:T(8,128)(2,1)}, bf16[1,2048,384]{2,1,0:T(8,128)(2,1)S(1)}, u32[]{:S(2)}) copy-start(bf16[1,2048,384]{2,1,0:T(8,128)(2,1)S(1)} %constant_dynamic-update-slice_fusion.11) | copy-start | bytes 4718596
  76.3 7.3 %copy-start.3 = (bf16[384,384]{1,0:T(8,128)(2,1)S(1)}, bf16[384,384]{1,0:T(8,128)(2,1)}, u32[]{:S(2)}) copy-start(bf16[384,384]{1,0:T(8,128)(2,1)} %param.19) | copy-start | bytes 884740
  79.4 6.2 %collective-permute-start.16 = (bf16[1,256,384]{2,1,0:T(8,128)(2,1)}, bf16[1,256,384]{2,1,0:T(8,128)(2,1)S(1)}, u32[]{:S(2)}, u32[]{:S(2)}) collective-permute-start(bf16[1,256,384]{2,1,0:T(8,128)(2,1)} %collective-permute-done.14), channel_id=1, source_target_pairs={{0,2},{2,4},{4,6},{6,7},{7,5},{5,3},{3,1},{1,0},{8,10},{10,12},{12... | collective-permute-start | bytes 589832 | tf_op jit(solution)/shard_map/ppermute | solution.py:37

commit v23 on v21

--- a/solution.py
+++ b/solution.py
@@ -62,7 +62,6 @@
     activated = jax.nn.silu(rms_scaled(frames, gain_conv)).astype(jnp.bfloat16)
     rims = jax.nn.silu(rms_scaled(rims, gain_conv)).astype(jnp.bfloat16)
     rimmed = jnp.concatenate([rims[:, :1], activated, rims[:, 1:]], axis=1)
-    rimmed = jnp.pad(rimmed, ((0, 0), (0, 0), (1, 1), (0, 0)))
     ways = lax.axis_size("tm")
     mine = lax.axis_index("tm")
     pieces = [rimmed]
@@ -83,6 +82,7 @@
     window = jnp.take(pool, picks.reshape(-1), axis=0).reshape(
         (span_count, 3) + rimmed.shape[1:]
     )
+    window = jnp.pad(window, ((0, 0), (0, 0), (0, 0), (1, 1), (0, 0)))
     score_scale = 1.0 / channels**0.5
     outputs = []
     span_window = window[:1]

time: 94.4 us -> 95 us (level)
  local copies, waits for them, and re-layouts: 20.3 us -> 18.7 us
  other arithmetic: 8.4 us -> 9.65 us
    unnamed x42 -> x38, local copies, waits for them, and re-layouts: 12.7 us -> 10.6 us
    select_n x2, other arithmetic: 2.21 us -> 3.82 us  [shards(): jnp.take(pool, picks.reshape(-1), axis=0)]
  transfers between devices with their start and end apart: 17 -> 17, of which waited for: 10 -> 10; matrix products, arithmetic and copies ran while one was open for 27% -> 26% of each run, Pallas kernels for 0% -> 0%
where the time goes in v23:
time: 95 us; the launch traced here: 94.5 us
  waiting for transfers between devices  22.6 us (24%)
  starting transfers between devices  22.4 us (24%)
  matrix products  20.8 us (22%)
  local copies, waits for them, and re-layouts  18.7 us (20%)
  other arithmetic  9.65 us (10%)
    unnamed x38, local copies, waits for them, and re-layouts  10.6 us
    ppermute x6, starting transfers between devices, ring_gather(): backward = lax.ppermute(backward, axis, behind)  7.44 us
    dot_general x2, matrix products, shards(): jnp.einsum('fqc,fkc->fqk', queries, keys_all, preferred_element_type=jnp....  6.42 us
    conv_general_dilated x2, matrix products, shards(): lax.conv_general_dilated(span_window, conv_weight, window_strides=(1, 1,...  6.32 us
    dot_general x2, matrix products, shards(): jnp.einsum('fqk,fkc->fqc', weights_exp.astype(jnp.bfloat16), values_all,...  6.27 us
    ppermute x2, waiting for transfers between devices, ring_gather(): pieces.append(lax.ppermute(forward, axis, ahead))  6.18 us
    ppermute x6, starting transfers between devices, ring_gather(): forward = lax.ppermute(forward, axis, ahead)  5.85 us
    ppermute x1, starting transfers between devices, padded_2(): lax.ppermute(tail, axis, [(i, (i + 1) % count) for i in range(ends)])  5.52 us
  transfers between devices with their start and end apart: 17, of which 10 were waited for; matrix products, arithmetic and copies ran while one was open for 26% of the time, Pallas kernels for 0%

profile of v23, /device:TPU:0, one launch (start us, length us, event | category | flops | bytes accessed | tf_op | source)
XLA Modules:
  0.0 94.5 jit_solution(4095228665442281668)
XLA Ops:
  0.0 1.1 %fusion.109 = (bf16[2,1,128,384]{3,2,1,0:T(8,128)(2,1)S(1)}, bf16[2,1,128,384]{3,2,1,0:T(8,128)(2,1)S(1)}) fusion(bf16[2,2,128,384]{3,2,1,0:T(8,128)(2,1)} %param.10), kind=kLoop, calls=%fused_computation.157 | loop fusion | bytes 786432 | tf_op jit(solution)/shard_map/slice | solution.py:12
  1.1 1.3 %collective-permute-start.1 = (bf16[2,1,128,384]{3,2,1,0:T(8,128)(2,1)S(1)}, bf16[2,1,128,384]{3,2,1,0:T(8,128)(2,1)S(1)}, u32[]{:S(2)}, u32[]{:S(2)}) collective-permute-start(bf16[2,1,128,384]{3,2,1,0:T(8,128)(2,1)S(1)} %get-tuple-element.20), channel_id=1, source_target_pairs={{1,0},{2,1},{3,2},{4,3},{5,4},{6,5},{7,6},{9,8},{10,9},{11,10},{12... | collective-permute-start | bytes 589832 | tf_op jit(solution)/shard_map/ppermute | solution.py:17
  2.4 5.5 %collective-permute-start = (bf16[2,1,128,384]{3,2,1,0:T(8,128)(2,1)S(1)}, bf16[2,1,128,384]{3,2,1,0:T(8,128)(2,1)S(1)}, u32[]{:S(2)}, u32[]{:S(2)}) collective-permute-start(bf16[2,1,128,384]{3,2,1,0:T(8,128)(2,1)S(1)} %get-tuple-element.19), channel_id=1, source_target_pairs={{0,1},{1,2},{2,3},{3,4},{4,5},{5,6},{6,7},{8,9},{9,10},{10,11},{11... | collective-permute-start | bytes 589832 | tf_op jit(solution)/shard_map/ppermute | solution.py:15
  8.0 1.1 %fusion.69 = f32[2,2,128]{2,1,0:T(2,128)S(1)} fusion(bf16[2,2,128,384]{3,2,1,0:T(8,128)(2,1)} %param.10), kind=kLoop, calls=%fused_computation.67 | loop fusion | flops 589312 | bytes 395264 | tf_op jit(solution)/shard_map/reduce_sum | solution.py:43
  9.1 1.8 %collective-permute-done.1 = bf16[2,1,128,384]{3,2,1,0:T(8,128)(2,1)S(1)} collective-permute-done((bf16[2,1,128,384]{3,2,1,0:T(8,128)(2,1)S(1)}, bf16[2,1,128,384]{3,2,1,0:T(8,128)(2,1)S(1)}, u32[]{:S(2)}, u32[]{:S(2)}) %collective-permute-start.1) | collective-permute-done | bytes 196640 | tf_op jit(solution)/shard_map/ppermute | solution.py:17
  10.9 4.4 %collective-permute-done = bf16[2,1,128,384]{3,2,1,0:T(8,128)(2,1)S(1)} collective-permute-done((bf16[2,1,128,384]{3,2,1,0:T(8,128)(2,1)S(1)}, bf16[2,1,128,384]{3,2,1,0:T(8,128)(2,1)S(1)}, u32[]{:S(2)}, u32[]{:S(2)}) %collective-permute-start) | collective-permute-done | bytes 196640 | tf_op jit(solution)/shard_map/ppermute | solution.py:15
  15.5 0.5 fusion.76
  16.3 0.4 copy-done.7
  17.0 1.6 %collective-permute-done.2 = bf16[2,4,128,384]{3,2,1,0:T(8,128)(2,1)} collective-permute-done((bf16[2,4,128,384]{3,2,1,0:T(8,128)(2,1)S(1)}, bf16[2,4,128,384]{3,2,1,0:T(8,128)(2,1)}, u32[]{:S(2)}, u32[]{:S(2)}) %collective-permute-start.2) | collective-permute-done | bytes 786464 | tf_op jit(solution)/shard_map/ppermute | solution.py:70
  18.7 1.5 %maximum_maximum_fusion = bf16[5,4,128,384]{3,2,1,0:T(8,128)(2,1)S(1)} fusion(bf16[2,4,128,384]{3,2,1,0:T(8,128)(2,1)} %collective-permute-done.2, bf16[2,1,128,384]{3,2,1,0:T(8,128)(2,1)S(1)} %get-tuple-element.18, bf16[2,2,128,384]{3,2,1,0:T(8,128)(2,1)S(1)} %get-tuple-element.21, bf16[2,1,128,384]{3,2,1,0:T(8,128)(2,1)S(1)} %get-tuple-element.17, ...), kind=kLoop, calls=%fused_computation.13 | loop fusion | flops 3932160 | bytes 3538954 | tf_op jit(solution)/shard_map/concatenate | solution.py:73
  20.1 2.4 %gather_fusion = bf16[6,4,128,384]{3,2,1,0:T(8,128)(2,1)} fusion(bf16[5,4,128,384]{3,2,1,0:T(8,128)(2,1)S(1)} %maximum_maximum_fusion, s32[1024]{0:T(1024)S(1)} %pad_clamp_fusion), kind=kCustom, calls=%fused_computation | custom fusion | bytes 4718616 | tf_op jit(solution)/shard_map/jit(_take)/gather | solution.py:82
  22.6 3.8 %copy_select_fusion = bf16[2,3,4,128,384]{4,2,3,1,0:T(4,128)(2,1)S(1)} fusion(bf16[2,3,4,128,384]{4,3,2,1,0:T(8,128)(2,1)} %bitcast.106, pred[2,3]{1,0:T(4,128)(4,1)S(1)} %get-tuple-element.13), kind=kLoop, calls=%fused_computation.10 | loop fusion | flops 1179648 | bytes 4718598 | tf_op jit(solution)/shard_map/jit(_take)/select_n | solution.py:82
  26.4 1.0 %pad_slice_fusion = (bf16[1,3,4,130,384]{4,2,3,1,0:T(4,128)(2,1)S(1)}, bf16[3,4,1,130,384]{4,1,3,0,2:T(4,128)(2,1)S(1)}) fusion(bf16[2,3,4,128,384]{4,2,3,1,0:T(4,128)(2,1)S(1)} %copy_select_fusion), kind=kLoop, calls=%fused_computation.18 | loop fusion | bytes 4755456 | tf_op jit(solution)/shard_map/slice | solution.py:110
  27.4 0.5 pad.5
  28.2 0.3 slice-done.1
  28.6 3.2 %fusion.38 = f32[1,2,8,17,384]{4,2,3,1,0:T(8,128)S(1)} fusion(bf16[3,3,3,384,384]{4,3,2,1,0:T(8,128)(2,1)S(1)} %bitcast.123, bf16[3,4,1,7,2,384]{5,3,4,1,0,2:T(8,128)(2,1)S(1)} %slice.48, bf16[3,4,1,8,17,384]{5,3,4,1,0,2:T(8,128)(2,1)S(1)} %copy.13, pred[8,17]{0,1:T(8,128)(4,1)S(1)} %copy-done.9), kind=kOutput, calls=%fused_computation.42 | convolution fusion | flops 2170140672 | bytes 9762952 | tf_op jit(solution)/shard_map/conv_general_dilated | solution.py:90
  31.8 0.2 copy.14
  32.1 0.3 copy-done.5
  32.7 2.5 %collective-permute-start.4 = (bf16[1,256,384]{2,1,0:T(8,128)(2,1)S(1)}, bf16[1,256,384]{2,1,0:T(8,128)(2,1)S(1)}, u32[]{:S(2)}, u32[]{:S(2)}) collective-permute-start(bf16[1,256,384]{2,1,0:T(8,128)(2,1)S(1)} %bitcast.110), channel_id=1, source_target_pairs={{0,1},{2,0},{4,2},{6,4},{7,6},{5,7},{3,5},{1,3},{8,9},{10,8},{12,1... | collective-permute-start | bytes 589832 | tf_op jit(solution)/shard_map/ppermute | solution.py:34
  35.3 0.7 constant_dynamic-update-slice_fusion.7
  36.0 0.3 convolution_convert_fusion.5
  36.3 3.5 %collective-permute-done.4 = bf16[1,256,384]{2,1,0:T(8,128)(2,1)S(1)} collective-permute-done((bf16[1,256,384]{2,1,0:T(8,128)(2,1)S(1)}, bf16[1,256,384]{2,1,0:T(8,128)(2,1)S(1)}, u32[]{:S(2)}, u32[]{:S(2)}) %collective-permute-start.4) | collective-permute-done | bytes 196640 | tf_op jit(solution)/shard_map/ppermute | solution.py:34
  39.7 0.5 pad.7
  40.4 3.2 %fusion.35 = f32[1,2,8,17,384]{4,2,3,1,0:T(8,128)S(1)} fusion(bf16[3,3,3,384,384]{4,3,2,1,0:T(8,128)(2,1)S(1)} %bitcast.123, bf16[3,4,1,7,2,384]{5,3,4,1,0,2:T(8,128)(2,1)S(1)} %slice.50, bf16[3,4,1,8,17,384]{5,3,4,1,0,2:T(8,128)(2,1)S(1)} %copy.17, pred[8,17]{0,1:T(8,128)(4,1)S(1)} %copy-done.9), kind=kOutput, calls=%fused_computation.41 | convolution fusion | flops 2170140672 | bytes 9762952 | tf_op jit(solution)/shard_map/conv_general_dilated | solution.py:90
  43.6 0.2 copy.18
  44.2 1.7 %collective-permute-start.10 = (bf16[1,256,384]{2,1,0:T(8,128)(2,1)S(1)}, bf16[1,256,384]{2,1,0:T(8,128)(2,1)S(1)}, u32[]{:S(2)}, u32[]{:S(2)}) collective-permute-start(bf16[1,256,384]{2,1,0:T(8,128)(2,1)S(1)} %bitcast.114), channel_id=1, source_target_pairs={{0,2},{2,4},{4,6},{6,7},{7,5},{5,3},{3,1},{1,0},{8,10},{10,12},{12... | collective-permute-start | bytes 589832 | tf_op jit(solution)/shard_map/ppermute | solution.py:33
  45.9 0.9 collective-permute-start.11
  46.9 0.7 constant_dynamic-update-slice_fusion.6
  47.6 0.7 constant_dynamic-update-slice_fusion.5
  48.3 1.1 %collective-permute-start.5 = (bf16[1,256,384]{2,1,0:T(8,128)(2,1)S(1)}, bf16[1,256,384]{2,1,0:T(8,128)(2,1)S(1)}, u32[]{:S(2)}, u32[]{:S(2)}) collective-permute-start(bf16[1,256,384]{2,1,0:T(8,128)(2,1)S(1)} %collective-permute-done.3), channel_id=1, source_target_pairs={{0,2},{2,4},{4,6},{6,7},{7,5},{5,3},{3,1},{1,0},{8,10},{10,12},{12... | collective-permute-start | bytes 589832 | tf_op jit(solution)/shard_map/ppermute | solution.py:33
  49.4 0.9 collective-permute-start.6
  50.3 0.9 %convolution_convert_fusion.4 = bf16[256,384]{1,0:T(8,128)(2,1)} fusion(bf16[256,384]{1,0:T(8,128)(2,1)S(1)} %bitcast.117, bf16[384,384]{1,0:T(8,128)(2,1)S(1)} %copy-done.3), kind=kOutput, calls=%fused_computation.45 | convolution fusion | flops 75595776 | bytes 688128 | tf_op jit(solution)/shard_map/ftc,cd->ftd/dot_general | solution.py:103
  51.2 1.1 %collective-permute-done.10 = bf16[1,256,384]{2,1,0:T(8,128)(2,1)S(1)} collective-permute-done((bf16[1,256,384]{2,1,0:T(8,128)(2,1)S(1)}, bf16[1,256,384]{2,1,0:T(8,128)(2,1)S(1)}, u32[]{:S(2)}, u32[]{:S(2)}) %collective-permute-start.10) | collective-permute-done | bytes 196640 | tf_op jit(solution)/shard_map/ppermute | solution.py:33
  52.3 1.0 %collective-permute-start.12 = (bf16[1,256,384]{2,1,0:T(8,128)(2,1)S(1)}, bf16[1,256,384]{2,1,0:T(8,128)(2,1)}, u32[]{:S(2)}, u32[]{:S(2)}) collective-permute-start(bf16[1,256,384]{2,1,0:T(8,128)(2,1)S(1)} %collective-permute-done.10), channel_id=1, source_target_pairs={{0,2},{2,4},{4,6},{6,7},{7,5},{5,3},{3,1},{1,0},{8,10},{10,12},{12... | collective-permute-start | bytes 589832 | tf_op jit(solution)/shard_map/ppermute | solution.py:33
  53.3 1.0 %collective-permute-start.13 = (bf16[1,256,384]{2,1,0:T(8,128)(2,1)S(1)}, bf16[1,256,384]{2,1,0:T(8,128)(2,1)S(1)}, u32[]{:S(2)}, u32[]{:S(2)}) collective-permute-start(bf16[1,256,384]{2,1,0:T(8,128)(2,1)S(1)} %collective-permute-done.11), channel_id=1, source_target_pairs={{0,1},{2,0},{4,2},{6,4},{7,6},{5,7},{3,5},{1,3},{8,9},{10,8},{12,1... | collective-permute-start | bytes 589832 | tf_op jit(solution)/shard_map/ppermute | solution.py:34
  54.3 2.2 %collective-permute-done.5 = bf16[1,256,384]{2,1,0:T(8,128)(2,1)S(1)} collective-permute-done((bf16[1,256,384]{2,1,0:T(8,128)(2,1)S(1)}, bf16[1,256,384]{2,1,0:T(8,128)(2,1)S(1)}, u32[]{:S(2)}, u32[]{:S(2)}) %collective-permute-start.5) | collective-permute-done | bytes 196640 | tf_op jit(solution)/shard_map/ppermute | solution.py:33
  56.5 1.0 %collective-permute-start.7 = (bf16[1,256,384]{2,1,0:T(8,128)(2,1)S(1)}, bf16[1,256,384]{2,1,0:T(8,128)(2,1)S(1)}, u32[]{:S(2)}, u32[]{:S(2)}) collective-permute-start(bf16[1,256,384]{2,1,0:T(8,128)(2,1)S(1)} %collective-permute-done.5), channel_id=1, source_target_pairs={{0,2},{2,4},{4,6},{6,7},{7,5},{5,3},{3,1},{1,0},{8,10},{10,12},{12... | collective-permute-start | bytes 589832 | tf_op jit(solution)/shard_map/ppermute | solution.py:33
  57.6 1.1 %collective-permute-start.8 = (bf16[1,256,384]{2,1,0:T(8,128)(2,1)S(1)}, bf16[1,256,384]{2,1,0:T(8,128)(2,1)S(1)}, u32[]{:S(2)}, u32[]{:S(2)}) collective-permute-start(bf16[1,256,384]{2,1,0:T(8,128)(2,1)S(1)} %collective-permute-done.6), channel_id=1, source_target_pairs={{0,1},{2,0},{4,2},{6,4},{7,6},{5,7},{3,5},{1,3},{8,9},{10,8},{12,1... | collective-permute-start | bytes 589832 | tf_op jit(solution)/shard_map/ppermute | solution.py:34
  58.7 0.7 constant_dynamic-update-slice_fusion.4
  59.4 0.7 constant_dynamic-update-slice_fusion.3
  60.1 0.8 collective-permute-done.12
  60.8 1.0 %collective-permute-start.14 = (bf16[1,256,384]{2,1,0:T(8,128)(2,1)}, bf16[1,256,384]{2,1,0:T(8,128)(2,1)}, u32[]{:S(2)}, u32[]{:S(2)}) collective-permute-start(bf16[1,256,384]{2,1,0:T(8,128)(2,1)} %collective-permute-done.12), channel_id=1, source_target_pairs={{0,2},{2,4},{4,6},{6,7},{7,5},{5,3},{3,1},{1,0},{8,10},{10,12},{12... | collective-permute-start | bytes 589832 | tf_op jit(solution)/shard_map/ppermute | solution.py:33
  61.9 1.0 %collective-permute-start.15 = (bf16[1,256,384]{2,1,0:T(8,128)(2,1)S(1)}, bf16[1,256,384]{2,1,0:T(8,128)(2,1)}, u32[]{:S(2)}, u32[]{:S(2)}) collective-permute-start(bf16[1,256,384]{2,1,0:T(8,128)(2,1)S(1)} %collective-permute-done.13), channel_id=1, source_target_pairs={{0,1},{2,0},{4,2},{6,4},{7,6},{5,7},{3,5},{1,3},{8,9},{10,8},{12,1... | collective-permute-start | bytes 589832 | tf_op jit(solution)/shard_map/ppermute | solution.py:34
  62.9 1.0 %constant_dynamic-update-slice_fusion.12 = bf16[1,2048,384]{2,1,0:T(8,128)(2,1)S(1)} fusion(bf16[1,2048,384]{2,1,0:T(8,128)(2,1)S(1)} %constant_dynamic-update-slice_fusion.13, bf16[1,256,384]{2,1,0:T(8,128)(2,1)} %collective-permute-done.12), kind=kLoop, calls=%fused_computation.112 | loop fusion | bytes 393216
  63.8 1.1 %collective-permute-done.7 = bf16[1,256,384]{2,1,0:T(8,128)(2,1)S(1)} collective-permute-done((bf16[1,256,384]{2,1,0:T(8,128)(2,1)S(1)}, bf16[1,256,384]{2,1,0:T(8,128)(2,1)S(1)}, u32[]{:S(2)}, u32[]{:S(2)}) %collective-permute-start.7) | collective-permute-done | bytes 196640 | tf_op jit(solution)/shard_map/ppermute | solution.py:33
  64.9 1.0 %collective-permute-start.9 = (bf16[1,256,384]{2,1,0:T(8,128)(2,1)S(1)}, bf16[1,256,384]{2,1,0:T(8,128)(2,1)S(1)}, u32[]{:S(2)}, u32[]{:S(2)}) collective-permute-start(bf16[1,256,384]{2,1,0:T(8,128)(2,1)S(1)} %collective-permute-done.7), channel_id=1, source_target_pairs={{0,2},{2,4},{4,6},{6,7},{7,5},{5,3},{3,1},{1,0},{8,10},{10,12},{12... | collective-permute-start | bytes 589832 | tf_op jit(solution)/shard_map/ppermute | solution.py:37
  66.0 0.8 constant_dynamic-update-slice_fusion.2
  66.8 0.7 constant_dynamic-update-slice_fusion.1
  67.5 4.7 %collective-permute-done.9 = bf16[1,256,384]{2,1,0:T(8,128)(2,1)S(1)} collective-permute-done((bf16[1,256,384]{2,1,0:T(8,128)(2,1)S(1)}, bf16[1,256,384]{2,1,0:T(8,128)(2,1)S(1)}, u32[]{:S(2)}, u32[]{:S(2)}) %collective-permute-start.9) | collective-permute-done | bytes 196640 | tf_op jit(solution)/shard_map/ppermute | solution.py:37
  72.2 0.7 constant_dynamic-update-slice_fusion
  72.9 3.1 %fusion.113 = (f32[256]{0:T(256)S(1)}, f32[256,2048]{1,0:T(8,128)S(1)}) fusion(bf16[256,384]{1,0:T(8,128)(2,1)S(1)} %convolution_convert_fusion.5, bf16[384,384]{1,0:T(8,128)(2,1)S(1)} %copy-done, bf16[1,2048,384]{2,1,0:T(8,128)(2,1)} %constant_dynamic-update-slice_fusion), kind=kOutput, calls=%fused_computation.159 | convolution fusion | flops 1008467712 | bytes 4162560 | tf_op jit(solution)/shard_map/fqc,fkc->fqk/dot_general | solution.py:120
  76.0 0.4 fusion.2
  76.5 3.2 %fusion.54 = bf16[256,384]{1,0:T(8,128)(2,1)S(1)} fusion(bf16[384,384]{1,0:T(8,128)(2,1)} %param.18, bf16[1,2048,384]{2,1,0:T(8,128)(2,1)} %constant_dynamic-update-slice_fusion, f32[256,2048]{1,0:T(8,128)S(1)} %get-tuple-element.28, f32[256]{0:T(256)S(1)} %get-tuple-element.27, f32[256]{0:T(256)S(1)} %fusion.2), kind=kOutput, calls=%fused_computation.52 | convolution fusion | flops 1008664576 | bytes 4163584 | tf_op jit(solution)/shard_map/fqk,fkc->fqc/dot_general | solution.py:126
  79.7 1.2 %collective-permute-start.16 = (bf16[1,256,384]{2,1,0:T(8,128)(2,1)}, bf16[1,256,384]{2,1,0:T(8,128)(2,1)S(1)}, u32[]{:S(2)}, u32[]{:S(2)}) collective-permute-start(bf16[1,256,384]{2,1,0:T(8,128)(2,1)} %collective-permute-done.14), channel_id=1, source_target_pairs={{0,2},{2,4},{4,6},{6,7},{7,5},{5,3},{3,1},{1,0},{8,10},{10,12},{12... | collective-permute-start | bytes 589832 | tf_op jit(solution)/shard_map/ppermute | solution.py:37
  80.9 1.7 %constant_dynamic-update-slice_fusion.10 = bf16[1,2048,384]{2,1,0:T(8,128)(2,1)} fusion(bf16[1,2048,384]{2,1,0:T(8,128)(2,1)} %copy-done.4, bf16[1,256,384]{2,1,0:T(8,128)(2,1)} %collective-permute-done.14), kind=kLoop, calls=%fused_computation.110 | loop fusion | bytes 393216
  82.5 1.6 %constant_dynamic-update-slice_fusion.9 = bf16[1,2048,384]{2,1,0:T(8,128)(2,1)} fusion(bf16[1,2048,384]{2,1,0:T(8,128)(2,1)} %constant_dynamic-update-slice_fusion.10, bf16[1,256,384]{2,1,0:T(8,128)(2,1)} %collective-permute-done.15), kind=kLoop, calls=%fused_computation.109 | loop fusion | bytes 393216
  84.1 0.3 fusion.44
  84.4 1.5 %collective-permute-done.16 = bf16[1,256,384]{2,1,0:T(8,128)(2,1)S(1)} collective-permute-done((bf16[1,256,384]{2,1,0:T(8,128)(2,1)}, bf16[1,256,384]{2,1,0:T(8,128)(2,1)S(1)}, u32[]{:S(2)}, u32[]{:S(2)}) %collective-permute-start.16) | collective-permute-done | bytes 196640 | tf_op jit(solution)/shard_map/ppermute | solution.py:37
  85.9 0.7 constant_dynamic-update-slice_fusion.8
  86.6 3.3 %fusion.110 = (f32[256]{0:T(256)S(1)}, f32[256,2048]{1,0:T(8,128)S(1)}) fusion(bf16[256,384]{1,0:T(8,128)(2,1)} %convolution_convert_fusion.4, bf16[384,384]{1,0:T(8,128)(2,1)S(1)} %copy-done, bf16[1,2048,384]{2,1,0:T(8,128)(2,1)} %constant_dynamic-update-slice_fusion.8), kind=kOutput, calls=%fused_computation.158 | convolution fusion | flops 1008467712 | bytes 4162560 | tf_op jit(solution)/shard_map/fqc,fkc->fqk/dot_general | solution.py:120
  89.8 0.4 fusion.4
  90.3 3.1 %fusion.48 = bf16[256,384]{1,0:T(8,128)(2,1)S(1)} fusion(bf16[384,384]{1,0:T(8,128)(2,1)} %param.18, bf16[1,2048,384]{2,1,0:T(8,128)(2,1)} %constant_dynamic-update-slice_fusion.8, f32[256,2048]{1,0:T(8,128)S(1)} %get-tuple-element.26, f32[256]{0:T(256)S(1)} %get-tuple-element.25, f32[256]{0:T(256)S(1)} %fusion.4), kind=kOutput, calls=%fused_computation.50 | convolution fusion | flops 1008664576 | bytes 4163584 | tf_op jit(solution)/shard_map/fqk,fkc->fqc/dot_general | solution.py:126
  93.4 0.3 fusion.43
  93.7 0.8 pad_maximum_fusion.2
  (59 shorter events, 2.2 us)
Async XLA Ops:
  0.0 72.9 %copy-start = (bf16[384,384]{1,0:T(8,128)(2,1)S(1)}, bf16[384,384]{1,0:T(8,128)(2,1)}, u32[]{:S(2)}) copy-start(bf16[384,384]{1,0:T(8,128)(2,1)} %param.17) | copy-start | bytes 884740
  0.0 15.4 %copy-start.1 = (bf16[2,2,128,384]{3,2,1,0:T(8,128)(2,1)S(1)}, bf16[2,2,128,384]{3,2,1,0:T(8,128)(2,1)}, u32[]{:S(2)}) copy-start(bf16[2,2,128,384]{3,2,1,0:T(8,128)(2,1)} %param.10) | copy-start | bytes 1179652
  0.0 15.5 %copy-start.8 = (f32[384]{0:T(512)S(1)}, f32[384]{0:T(512)}, u32[]{:S(2)}) copy-start(f32[384]{0:T(512)} %param.12) | copy-start | bytes 4612
  1.1 9.8 %collective-permute-start.1 = (bf16[2,1,128,384]{3,2,1,0:T(8,128)(2,1)S(1)}, bf16[2,1,128,384]{3,2,1,0:T(8,128)(2,1)S(1)}, u32[]{:S(2)}, u32[]{:S(2)}) collective-permute-start(bf16[2,1,128,384]{3,2,1,0:T(8,128)(2,1)S(1)} %get-tuple-element.20), channel_id=1, source_target_pairs={{1,0},{2,1},{3,2},{4,3},{5,4},{6,5},{7,6},{9,8},{10,9},{11,10},{12... | collective-permute-start | bytes 589832 | tf_op jit(solution)/shard_map/ppermute | solution.py:17
  2.4 12.8 %collective-permute-start = (bf16[2,1,128,384]{3,2,1,0:T(8,128)(2,1)S(1)}, bf16[2,1,128,384]{3,2,1,0:T(8,128)(2,1)S(1)}, u32[]{:S(2)}, u32[]{:S(2)}) collective-permute-start(bf16[2,1,128,384]{3,2,1,0:T(8,128)(2,1)S(1)} %get-tuple-element.19), channel_id=1, source_target_pairs={{0,1},{1,2},{2,3},{3,4},{4,5},{5,6},{6,7},{8,9},{9,10},{10,11},{11... | collective-permute-start | bytes 589832 | tf_op jit(solution)/shard_map/ppermute | solution.py:15
  16.0 0.7 copy-start.7
  16.2 2.5 %collective-permute-start.2 = (bf16[2,4,128,384]{3,2,1,0:T(8,128)(2,1)S(1)}, bf16[2,4,128,384]{3,2,1,0:T(8,128)(2,1)}, u32[]{:S(2)}, u32[]{:S(2)}) collective-permute-start(bf16[2,4,128,384]{3,2,1,0:T(8,128)(2,1)S(1)} %pad_maximum_fusion), channel_id=1, source_target_pairs={{0,8},{8,0},{1,9},{9,1},{2,10},{10,2},{3,11},{11,3},{4,12},{12,4},... | collective-permute-start | bytes 2359304 | tf_op jit(solution)/shard_map/ppermute | solution.py:70
  22.6 5.6 %slice-start = ((s8[7962624]{0:T(1024)(128)(4,1)}), s8[4194304]{0:T(1024)(128)(4,1)S(1)}, s32[]{:S(2)}) async-start(s8[7962624]{0:T(1024)(128)(4,1)} %bitcast.122), calls=%async_computation | async-start | bytes 8388608
  26.4 2.1 %slice-start.1 = ((s8[7962624]{0:T(1024)(128)(4,1)}), s8[3768320]{0:T(1024)(128)(4,1)S(1)}, s32[]{:S(2)}) async-start(s8[7962624]{0:T(1024)(128)(4,1)} %bitcast.122), calls=%async_computation.1 | async-start | bytes 7536640
  27.9 0.7 copy-start.9
  31.8 0.7 copy-start.5
  31.8 0.8 copy-start.6
  31.8 4.2 %copy-start.3 = (bf16[384,384]{1,0:T(8,128)(2,1)S(1)}, bf16[384,384]{1,0:T(8,128)(2,1)}, u32[]{:S(2)}) copy-start(bf16[384,384]{1,0:T(8,128)(2,1)} %param.16) | copy-start | bytes 884740
  32.7 7.0 %collective-permute-start.4 = (bf16[1,256,384]{2,1,0:T(8,128)(2,1)S(1)}, bf16[1,256,384]{2,1,0:T(8,128)(2,1)S(1)}, u32[]{:S(2)}, u32[]{:S(2)}) collective-permute-start(bf16[1,256,384]{2,1,0:T(8,128)(2,1)S(1)} %bitcast.110), channel_id=1, source_target_pairs={{0,1},{2,0},{4,2},{6,4},{7,6},{5,7},{3,5},{1,3},{8,9},{10,8},{12,1... | collective-permute-start | bytes 589832 | tf_op jit(solution)/shard_map/ppermute | solution.py:34
  36.0 10.9 %collective-permute-start.3 = (bf16[1,256,384]{2,1,0:T(8,128)(2,1)S(1)}, bf16[1,256,384]{2,1,0:T(8,128)(2,1)S(1)}, u32[]{:S(2)}, u32[]{:S(2)}) collective-permute-start(bf16[1,256,384]{2,1,0:T(8,128)(2,1)S(1)} %bitcast.112), channel_id=1, source_target_pairs={{0,2},{2,4},{4,6},{6,7},{7,5},{5,3},{3,1},{1,0},{8,10},{10,12},{12... | collective-permute-start | bytes 589832 | tf_op jit(solution)/shard_map/ppermute | solution.py:33
  44.2 8.1 %collective-permute-start.10 = (bf16[1,256,384]{2,1,0:T(8,128)(2,1)S(1)}, bf16[1,256,384]{2,1,0:T(8,128)(2,1)S(1)}, u32[]{:S(2)}, u32[]{:S(2)}) collective-permute-start(bf16[1,256,384]{2,1,0:T(8,128)(2,1)S(1)} %bitcast.114), channel_id=1, source_target_pairs={{0,2},{2,4},{4,6},{6,7},{7,5},{5,3},{3,1},{1,0},{8,10},{10,12},{12... | collective-permute-start | bytes 589832 | tf_op jit(solution)/shard_map/ppermute | solution.py:33
  45.9 7.4 %collective-permute-start.11 = (bf16[1,256,384]{2,1,0:T(8,128)(2,1)S(1)}, bf16[1,256,384]{2,1,0:T(8,128)(2,1)S(1)}, u32[]{:S(2)}, u32[]{:S(2)}) collective-permute-start(bf16[1,256,384]{2,1,0:T(8,128)(2,1)S(1)} %bitcast.115), channel_id=1, source_target_pairs={{0,1},{2,0},{4,2},{6,4},{7,6},{5,7},{3,5},{1,3},{8,9},{10,8},{12,1... | collective-permute-start | bytes 589832 | tf_op jit(solution)/shard_map/ppermute | solution.py:34
  48.3 8.3 %collective-permute-start.5 = (bf16[1,256,384]{2,1,0:T(8,128)(2,1)S(1)}, bf16[1,256,384]{2,1,0:T(8,128)(2,1)S(1)}, u32[]{:S(2)}, u32[]{:S(2)}) collective-permute-start(bf16[1,256,384]{2,1,0:T(8,128)(2,1)S(1)} %collective-permute-done.3), channel_id=1, source_target_pairs={{0,2},{2,4},{4,6},{6,7},{7,5},{5,3},{3,1},{1,0},{8,10},{10,12},{12... | collective-permute-start | bytes 589832 | tf_op jit(solution)/shard_map/ppermute | solution.py:33
  49.4 8.2 %collective-permute-start.6 = (bf16[1,256,384]{2,1,0:T(8,128)(2,1)S(1)}, bf16[1,256,384]{2,1,0:T(8,128)(2,1)S(1)}, u32[]{:S(2)}, u32[]{:S(2)}) collective-permute-start(bf16[1,256,384]{2,1,0:T(8,128)(2,1)S(1)} %collective-permute-done.4), channel_id=1, source_target_pairs={{0,1},{2,0},{4,2},{6,4},{7,6},{5,7},{3,5},{1,3},{8,9},{10,8},{12,1... | collective-permute-start | bytes 589832 | tf_op jit(solution)/shard_map/ppermute | solution.py:34
  52.3 8.5 %collective-permute-start.12 = (bf16[1,256,384]{2,1,0:T(8,128)(2,1)S(1)}, bf16[1,256,384]{2,1,0:T(8,128)(2,1)}, u32[]{:S(2)}, u32[]{:S(2)}) collective-permute-start(bf16[1,256,384]{2,1,0:T(8,128)(2,1)S(1)} %collective-permute-done.10), channel_id=1, source_target_pairs={{0,2},{2,4},{4,6},{6,7},{7,5},{5,3},{3,1},{1,0},{8,10},{10,12},{12... | collective-permute-start | bytes 589832 | tf_op jit(solution)/shard_map/ppermute | solution.py:33
  53.3 8.5 %collective-permute-start.13 = (bf16[1,256,384]{2,1,0:T(8,128)(2,1)S(1)}, bf16[1,256,384]{2,1,0:T(8,128)(2,1)S(1)}, u32[]{:S(2)}, u32[]{:S(2)}) collective-permute-start(bf16[1,256,384]{2,1,0:T(8,128)(2,1)S(1)} %collective-permute-done.11), channel_id=1, source_target_pairs={{0,1},{2,0},{4,2},{6,4},{7,6},{5,7},{3,5},{1,3},{8,9},{10,8},{12,1... | collective-permute-start | bytes 589832 | tf_op jit(solution)/shard_map/ppermute | solution.py:34
  56.5 8.4 %collective-permute-start.7 = (bf16[1,256,384]{2,1,0:T(8,128)(2,1)S(1)}, bf16[1,256,384]{2,1,0:T(8,128)(2,1)S(1)}, u32[]{:S(2)}, u32[]{:S(2)}) collective-permute-start(bf16[1,256,384]{2,1,0:T(8,128)(2,1)S(1)} %collective-permute-done.5), channel_id=1, source_target_pairs={{0,2},{2,4},{4,6},{6,7},{7,5},{5,3},{3,1},{1,0},{8,10},{10,12},{12... | collective-permute-start | bytes 589832 | tf_op jit(solution)/shard_map/ppermute | solution.py:33
  57.6 9.2 %collective-permute-start.8 = (bf16[1,256,384]{2,1,0:T(8,128)(2,1)S(1)}, bf16[1,256,384]{2,1,0:T(8,128)(2,1)S(1)}, u32[]{:S(2)}, u32[]{:S(2)}) collective-permute-start(bf16[1,256,384]{2,1,0:T(8,128)(2,1)S(1)} %collective-permute-done.6), channel_id=1, source_target_pairs={{0,1},{2,0},{4,2},{6,4},{7,6},{5,7},{3,5},{1,3},{8,9},{10,8},{12,1... | collective-permute-start | bytes 589832 | tf_op jit(solution)/shard_map/ppermute | solution.py:34
  60.8 18.8 %collective-permute-start.14 = (bf16[1,256,384]{2,1,0:T(8,128)(2,1)}, bf16[1,256,384]{2,1,0:T(8,128)(2,1)}, u32[]{:S(2)}, u32[]{:S(2)}) collective-permute-start(bf16[1,256,384]{2,1,0:T(8,128)(2,1)} %collective-permute-done.12), channel_id=1, source_target_pairs={{0,2},{2,4},{4,6},{6,7},{7,5},{5,3},{3,1},{1,0},{8,10},{10,12},{12... | collective-permute-start | bytes 589832 | tf_op jit(solution)/shard_map/ppermute | solution.py:33
  61.9 20.7 %collective-permute-start.15 = (bf16[1,256,384]{2,1,0:T(8,128)(2,1)S(1)}, bf16[1,256,384]{2,1,0:T(8,128)(2,1)}, u32[]{:S(2)}, u32[]{:S(2)}) collective-permute-start(bf16[1,256,384]{2,1,0:T(8,128)(2,1)S(1)} %collective-permute-done.13), channel_id=1, source_target_pairs={{0,1},{2,0},{4,2},{6,4},{7,6},{5,7},{3,5},{1,3},{8,9},{10,8},{12,1... | collective-permute-start | bytes 589832 | tf_op jit(solution)/shard_map/ppermute | solution.py:34
  64.9 7.2 %collective-permute-start.9 = (bf16[1,256,384]{2,1,0:T(8,128)(2,1)S(1)}, bf16[1,256,384]{2,1,0:T(8,128)(2,1)S(1)}, u32[]{:S(2)}, u32[]{:S(2)}) collective-permute-start(bf16[1,256,384]{2,1,0:T(8,128)(2,1)S(1)} %collective-permute-done.7), channel_id=1, source_target_pairs={{0,2},{2,4},{4,6},{6,7},{7,5},{5,3},{3,1},{1,0},{8,10},{10,12},{12... | collective-permute-start | bytes 589832 | tf_op jit(solution)/shard_map/ppermute | solution.py:37
  66.0 6.2 %copy-start.4 = (bf16[1,2048,384]{2,1,0:T(8,128)(2,1)}, bf16[1,2048,384]{2,1,0:T(8,128)(2,1)S(1)}, u32[]{:S(2)}) copy-start(bf16[1,2048,384]{2,1,0:T(8,128)(2,1)S(1)} %constant_dynamic-update-slice_fusion.11) | copy-start | bytes 4718596
  76.5 7.7 %copy-start.2 = (bf16[384,384]{1,0:T(8,128)(2,1)S(1)}, bf16[384,384]{1,0:T(8,128)(2,1)}, u32[]{:S(2)}) copy-start(bf16[384,384]{1,0:T(8,128)(2,1)} %param.19) | copy-start | bytes 884740
  79.7 6.2 %collective-permute-start.16 = (bf16[1,256,384]{2,1,0:T(8,128)(2,1)}, bf16[1,256,384]{2,1,0:T(8,128)(2,1)S(1)}, u32[]{:S(2)}, u32[]{:S(2)}) collective-permute-start(bf16[1,256,384]{2,1,0:T(8,128)(2,1)} %collective-permute-done.14), channel_id=1, source_target_pairs={{0,2},{2,4},{4,6},{6,7},{7,5},{5,3},{3,1},{1,0},{8,10},{10,12},{12... | collective-permute-start | bytes 589832 | tf_op jit(solution)/shard_map/ppermute | solution.py:37
